TPU v7x, 32 devices: a whole 2x2x4 slice. The times are simulated.
32 devices in a mesh: groups: 2 (over y), bricks: 4 (over z), heads: 4 (over x, core).
Axes of the slice: x: 2, y: 2, z: 4, core: 2. Of those that a mesh axis runs over, the one named last changes fastest.
Arguments:
- voxel_feats: bfloat16 [4096, 1024], P(('groups', 'bricks'), 'heads'), parts along dimension 0, may hold values from -6 to 6
- face_open: int32 [8], P('groups'), parts along dimension 0, may hold values from 0 to 1
- pattern: int32 [8, 4], P('groups'), parts along dimension 0, may hold values from 0 to 1, as said below
- conv_weight: bfloat16 [27, 1024], P(None, 'heads'), may hold values from -1.25 to 1.25
- conv_bias: bfloat16 [1024], P('heads'), may hold values from -0.5 to 0.5
- gain_one: bfloat16 [1024], replicated, may hold values from 0.099609375 to 1.8984375
- query_weight: bfloat16 [1024, 1024], P(None, 'heads'), may hold values from -3 to 3
- key_weight: bfloat16 [1024, 1024], P(None, 'heads'), may hold values from -3 to 3
- value_weight: bfloat16 [1024, 1024], P(None, 'heads'), may hold values from -0.1875 to 0.1875
- out_weight: bfloat16 [1024, 1024], P('heads'), may hold values from -0.1875 to 0.1875
- gain_two: bfloat16 [1024], replicated, may hold values from 0.099609375 to 1.8984375
- up_weight: bfloat16 [1024, 4096], P(None, 'heads'), may hold values from -0.1875 to 0.1875
- down_weight: bfloat16 [4096, 1024], P('heads'), may hold values from -0.09375 to 0.09375
Outputs:
- block_out: bfloat16 [4096, 1024], P(('groups', 'bricks'), 'heads'), parts along dimension 0
There are 2 independent parts, one for each index of `groups`. A program takes and returns all parts, laid end to end along the dimension named above; an argument that names none is the same for every part. Nothing has to cross between parts.
Inputs may be any that keep to these rules, and one draw needn't show every extreme that they name: pattern is 0 or 1; every brick attends to itself; each query brick attends to 3 or more key bricks, and some query brick to all 4.
All inputs are finite; a program needn't handle non-finite values.
Results may differ from a plain program's by a relative error of at most 0.012.
Values may be sent and summed in bfloat16 or wider, within the bound.
No kernel may reach another device: no remote copies, remote signals or barrier semaphores. Data moves between devices by JAX's collectives and lax.ppermute only.
A program may use at most 64 MiB of HBM per device.

v0:
```python
import jax
import jax.numpy as jnp
from jax import lax
from jax.sharding import PartitionSpec as P

EDGE = 8
HEAD_DIM = 64


epsilon = 1e-05


def extended_2(value, sides, width):
    for axis, dim in sides:
        size, length = (lax.axis_size(axis), value.shape[dim])
        up = [(i, (i + 1) % size) for i in range(size - 1)]
        down = [(j, i) for i, j in up]
        last = lax.slice_in_dim(value, length - width, length, axis=dim)
        first = lax.slice_in_dim(value, 0, width, axis=dim)
        before = lax.ppermute(last, axis, up)
        after = lax.ppermute(first, axis, down)
        value = jnp.concatenate([before, value, after], axis=dim)
    return value


def layer_norm(inputs, gain_vec):
    values = inputs.astype(jnp.float32)
    center = values - jnp.mean(values, axis=-1, keepdims=True)
    spread = jnp.mean(center * center, axis=-1, keepdims=True)
    return center * lax.rsqrt(spread + epsilon) * gain_vec.astype(jnp.float32)


def depthwise(brick_vals, lower_face, upper_face, conv_weight, conv_bias):
    brick_count = brick_vals.shape[0]
    edge_len = brick_vals.shape[1]
    channels = brick_vals.shape[3]
    layers = jnp.concatenate([lower_face[:, None], brick_vals, upper_face[:, None]], axis=1)
    layers = layers.reshape(brick_count, edge_len + 2, edge_len, edge_len, channels)
    padded = jnp.pad(layers, ((0, 0), (0, 0), (1, 1), (1, 1), (0, 0)))
    weights = conv_weight.astype(jnp.float32)
    summed = jnp.zeros((brick_count, edge_len, edge_len, edge_len, channels), jnp.float32)
    for step_x in range(3):
        for step_y in range(3):
            for step_z in range(3):
                window = padded[
                    :,
                    step_x : step_x + edge_len,
                    step_y : step_y + edge_len,
                    step_z : step_z + edge_len,
                ]
                summed = summed + weights[step_x * 9 + step_y * 3 + step_z] * window
    return summed.reshape(brick_count * edge_len**3, channels) + conv_bias.astype(jnp.float32)


def shards(
    voxel_feats,
    face_open,
    pattern,
    conv_weight,
    conv_bias,
    gain_one,
    query_weight,
    key_weight,
    value_weight,
    out_weight,
    gain_two,
    up_weight,
    down_weight,
):
    row_count = voxel_feats.shape[0]
    local_width = voxel_feats.shape[1]
    face_rows = EDGE * EDGE
    brick_rows = EDGE * face_rows
    local_bricks = row_count // brick_rows
    brick_total = pattern.shape[0]
    first_brick = lax.axis_index("bricks") * local_bricks
    extended = extended_2(voxel_feats, (("bricks", 0),), face_rows)
    brick_vals = extended[face_rows : face_rows + row_count].astype(jnp.float32)
    brick_vals = brick_vals.reshape(local_bricks, EDGE, face_rows, local_width)
    lower_face = jnp.concatenate(
        [extended[:face_rows].astype(jnp.float32)[None], brick_vals[:-1, EDGE - 1]], axis=0
    )
    upper_face = jnp.concatenate(
        [brick_vals[1:, 0], extended[face_rows + row_count :].astype(jnp.float32)[None]], axis=0
    )
    brick_ids = first_brick + jnp.arange(local_bricks, dtype=jnp.int32)
    lower_open = jnp.where(brick_ids >= 1, jnp.take(face_open, brick_ids), 0)
    upper_open = jnp.where(
        brick_ids + 1 < brick_total,
        jnp.take(face_open, jnp.minimum(brick_ids + 1, brick_total - 1)),
        0,
    )
    lower_face = lower_face * lower_open.astype(jnp.float32)[:, None, None]
    upper_face = upper_face * upper_open.astype(jnp.float32)[:, None, None]
    conv_out = depthwise(brick_vals, lower_face, upper_face, conv_weight, conv_bias)
    stream = (voxel_feats.astype(jnp.float32) + conv_out).astype(jnp.bfloat16)
    stream_full = lax.all_gather(stream, "heads", axis=1, tiled=True)
    normed = layer_norm(stream_full, gain_one).astype(jnp.bfloat16)
    queries = jnp.dot(normed, query_weight, preferred_element_type=jnp.float32).astype(jnp.bfloat16)
    head_count = local_width // HEAD_DIM
    query_heads = queries.reshape(local_bricks, brick_rows, head_count, HEAD_DIM)
    score_scale = HEAD_DIM ** (-0.5)
    start_state = (
        jnp.full((local_bricks, head_count, brick_rows), -1e30, jnp.float32),
        jnp.zeros((local_bricks, head_count, brick_rows), jnp.float32),
        jnp.zeros((local_bricks, brick_rows, head_count, HEAD_DIM), jnp.float32),
    )

    def absorb(state_in, local_id, key_brick, fetch_pair):
        linked = pattern[first_brick + local_id, key_brick]

        def include(state_now):
            row_max, row_mass, weighted = state_now
            key_rows, value_rows = fetch_pair()
            keys_h = key_rows.reshape(brick_rows, head_count, HEAD_DIM)
            values_h = value_rows.reshape(brick_rows, head_count, HEAD_DIM)
            query_one = lax.dynamic_index_in_dim(query_heads, local_id, 0, keepdims=False)
            scores = (
                jnp.einsum("qhd,khd->hqk", query_one, keys_h, preferred_element_type=jnp.float32)
                * score_scale
            )
            max_old = lax.dynamic_index_in_dim(row_max, local_id, 0, keepdims=False)
            mass_old = lax.dynamic_index_in_dim(row_mass, local_id, 0, keepdims=False)
            sum_old = lax.dynamic_index_in_dim(weighted, local_id, 0, keepdims=False)
            max_new = jnp.maximum(max_old, jnp.max(scores, axis=-1))
            factor = jnp.exp(max_old - max_new)
            weights = jnp.exp(scores - max_new[:, :, None])
            mass_new = mass_old * factor + jnp.sum(weights, axis=-1)
            sum_new = sum_old * jnp.transpose(factor)[:, :, None] + jnp.einsum(
                "hqk,khd->qhd",
                weights.astype(jnp.bfloat16),
                values_h,
                preferred_element_type=jnp.float32,
            )
            return (
                lax.dynamic_update_index_in_dim(row_max, max_new, local_id, 0),
                lax.dynamic_update_index_in_dim(row_mass, mass_new, local_id, 0),
                lax.dynamic_update_index_in_dim(weighted, sum_new, local_id, 0),
            )

        return lax.cond(linked > 0, include, lambda state_now: state_now, state_in)

    keys_all = jnp.dot(normed, key_weight, preferred_element_type=jnp.float32).astype(jnp.bfloat16)
    values_all = jnp.dot(normed, value_weight, preferred_element_type=jnp.float32).astype(
        jnp.bfloat16
    )
    key_piece = lax.all_gather(keys_all, "bricks", axis=0, tiled=True)
    value_piece = lax.all_gather(values_all, "bricks", axis=0, tiled=True)
    piece_bricks = key_piece.shape[0] // brick_rows

    def visit(visit_idx, state_now):
        local_id = visit_idx // piece_bricks
        offset = visit_idx % piece_bricks

        def fetch_pair():
            return (
                lax.dynamic_slice_in_dim(key_piece, offset * brick_rows, brick_rows, 0),
                lax.dynamic_slice_in_dim(value_piece, offset * brick_rows, brick_rows, 0),
            )

        return absorb(state_now, local_id, offset, fetch_pair)

    result = lax.fori_loop(0, local_bricks * piece_bricks, visit, start_state)
    row_max, row_mass, weighted = result
    attended = (weighted / jnp.transpose(row_mass, (0, 2, 1))[:, :, :, None]).astype(jnp.bfloat16)
    attended = attended.reshape(row_count, local_width)
    partial_out = jnp.dot(attended, out_weight, preferred_element_type=jnp.float32)
    full_sum = lax.psum(partial_out.astype(jnp.bfloat16), "heads").astype(jnp.float32)
    stream_two_full = (stream_full.astype(jnp.float32) + full_sum).astype(jnp.bfloat16)
    stream_two = lax.dynamic_slice_in_dim(
        stream_two_full, lax.axis_index("heads") * local_width, local_width, 1
    )
    normed_two = layer_norm(stream_two_full, gain_two).astype(jnp.bfloat16)
    hidden = jax.nn.gelu(
        jnp.dot(normed_two, up_weight, preferred_element_type=jnp.float32), approximate=True
    ).astype(jnp.bfloat16)
    lowered = jnp.dot(hidden, down_weight, preferred_element_type=jnp.float32)
    mixed = lax.psum_scatter(
        lowered.astype(jnp.bfloat16), "heads", scatter_dimension=1, tiled=True
    ).astype(jnp.float32)
    return (stream_two.astype(jnp.float32) + mixed).astype(jnp.bfloat16)


def solution(mesh):
    return jax.shard_map(
        shards,
        mesh=mesh,
        in_specs=(
            P(("groups", "bricks"), "heads"),
            P("groups"),
            P("groups", None),
            P(None, "heads"),
            P("heads"),
            P(),
            P(None, "heads"),
            P(None, "heads"),
            P(None, "heads"),
            P("heads", None),
            P(),
            P(None, "heads"),
            P("heads", None),
        ),
        out_specs=P(("groups", "bricks"), "heads"),
        check_vma=False,
    )
```

profile of v0, /device:TPU:0, one launch (start us, length us, event | category | flops | bytes accessed | tf_op | source)
XLA Modules:
  0.0 208.5 jit_solution(12115050096938499187)
XLA Ops:
  6.5 0.9 fusion.95
  7.5 1.3 collective-permute-start.1
  8.8 5.6 %collective-permute-start = (bf16[64,256]{1,0:T(8,128)(2,1)S(1)}, bf16[64,256]{1,0:T(8,128)(2,1)S(1)}, u32[]{:S(2)}, u32[]{:S(2)}) collective-permute-start(bf16[64,256]{1,0:T(8,128)(2,1)S(1)} %get-tuple-element.350), channel_id=1, source_target_pairs={{0,4},{4,8},{8,12},{1,5},{5,9},{9,13},{2,6},{6,10},{10,14},{3,7},{... | collective-permute-start | bytes 98312 | tf_op jit(solution)/shard_map/ppermute | solution.py:20
  14.3 1.0 fusion.96
  15.3 0.9 fusion.97
  16.2 1.4 fusion.98
  18.3 1.0 convert.1
  19.9 0.7 convert_element_type.105
  20.6 0.3 select_maximum_fusion
  20.9 1.6 fusion.57
  22.5 0.8 fusion.86
  23.3 0.0 all-gather.4.cloned.1.call-update
  23.3 0.0 all-gather.6.cloned.1.call-start
  23.4 17.6 %all-gather.4.cloned.1.call-done = bf16[512,1024]{1,0:T(8,128)(2,1)} async-done(((bf16[512,256]{1,0:T(8,128)(2,1)}), bf16[512,1024]{1,0:T(8,128)(2,1)}) %all-gather.4.cloned.1.call-update) | async-done | bytes 1048592 | tf_op jit(solution)/shard_map/all_gather | solution.py:97
  41.0 1.5 convert_reduce_fusion
  42.5 1.6 fusion.25
  44.2 2.3 %convolution_convert_fusion.4 = bf16[512,256]{1,0:T(8,128)(2,1)} fusion(bf16[1024,256]{1,0:T(8,128)(2,1)} %param.24, bf16[512,1024]{1,0:T(8,128)(2,1)S(1)} %copy-done.1, f32[1024]{0:T(1024)S(1)} %convert_element_type.108, f32[512]{0:T(512)S(1)} %add_rsqrt_fusion.1, f32[512]{0:T(512)S(1)} %broadcast_multiply_fusion.1), kind=kOutput, calls=%fused_computation.61 | convolution fusion | flops 271187968 | bytes 1843200 | tf_op jit(solution)/shard_map/dot_general | solution.py:143
  46.4 0.0 all-gather.6.cloned.1.call-update
  46.4 0.0 all-gather.8.cloned.1.call-start
  46.5 2.3 %convolution_convert_fusion.2 = bf16[512,256]{1,0:T(8,128)(2,1)} fusion(bf16[1024,256]{1,0:T(8,128)(2,1)} %param.25, bf16[512,1024]{1,0:T(8,128)(2,1)S(1)} %copy-done.1, f32[1024]{0:T(1024)S(1)} %convert_element_type.108, f32[512]{0:T(512)S(1)} %add_rsqrt_fusion.1, f32[512]{0:T(512)S(1)} %broadcast_multiply_fusion.1), kind=kOutput, calls=%fused_computation.59 | convolution fusion | flops 271187968 | bytes 1843200 | tf_op jit(solution)/shard_map/dot_general | solution.py:144
  48.8 0.0 all-gather.8.cloned.1.call-update
  48.8 0.0 all-reduce.3.cloned.1.call-start
  48.8 1.7 convolution_convert_fusion.3
  50.6 24.0 %all-gather.6.cloned.1.call-done = bf16[2048,256]{1,0:T(8,128)(2,1)} async-done(((bf16[512,256]{1,0:T(8,128)(2,1)}), bf16[2048,256]{1,0:T(8,128)(2,1)}) %all-gather.6.cloned.1.call-update) | async-done | bytes 1048592 | tf_op jit(solution)/shard_map/all_gather | solution.py:147
  74.5 2.3 %copy.15 = bf16[2048,256]{0,1:T(8,128)(2,1)} copy(bf16[2048,256]{1,0:T(8,128)(2,1)} %all-gather.6.cloned.1.call-done) | data formatting | bytes 2097152 | tf_op jit(solution)/shard_map/while | solution.py:163
  76.8 26.8 %all-gather.8.cloned.1.call-done = bf16[2048,256]{1,0:T(8,128)(2,1)} async-done(((bf16[512,256]{1,0:T(8,128)(2,1)}), bf16[2048,256]{1,0:T(8,128)(2,1)}) %all-gather.8.cloned.1.call-update) | async-done | bytes 1048592 | tf_op jit(solution)/shard_map/all_gather | solution.py:148
  103.6 2.3 %copy.16 = bf16[2048,256]{0,1:T(8,128)(2,1)} copy(bf16[2048,256]{1,0:T(8,128)(2,1)} %all-gather.8.cloned.1.call-done) | data formatting | bytes 2097152 | tf_op jit(solution)/shard_map/while | solution.py:163
  105.9 22.0 %while.21 = (s32[]{:T(128)}, f32[1,4,512]{2,1,0:T(4,128)S(1)}, f32[1,4,512]{2,1,0:T(4,128)S(1)}, f32[1,512,4,64]{1,3,2,0:T(8,128)S(1)}, s32[]{:T(128)}, /*index=...) while((s32[]{:T(128)}, f32[1,4,512]{2,1,0:T(4,128)S(1)}, ...), condition=%wide.region_7.8_spmd, body=%wide.region_2.0_spmd.sunk | while | flops 277094432 | bytes 15589916 | solution.py:163
  106.0 1.3 dynamic_slice.33
  107.9 3.5 %conditional.2 = ((f32[1,4,512]{2,1,0:T(4,128)S(1)}, f32[1,4,512]{2,1,0:T(4,128)S(1)}, f32[1,512,4,64]{1,3,2,0:T(8,128)S(1)})) conditional(s32[]{:T(128)} %bitcast.111, (f32[1,4,512]{2,1,0:T(4,128)S(1)}, f32[1,4,512]{2,1,0:T(4,128)S(1)}, f32[1,512,4,64]{1,3,2,0:T(8,128)S(1)}) %tuple.92, (s32[]{:T(128)}, bf16[2048,256]{0,1:T(8,128)(2,1)}, ...), branch_computations={%region_3.3_spmd, %region_4.6_spmd} | conditional | flops 277094400 | bytes 15589458 | solution.py:141
  107.9 1.1 constant_dynamic-slice_fusion
  109.0 0.8 bitcast_reduce_fusion
  109.7 0.7 fusion.2
  110.5 0.9 fusion.13
  111.5 1.3 dynamic_slice.33
  113.4 3.5 %conditional.2 = ((f32[1,4,512]{2,1,0:T(4,128)S(1)}, f32[1,4,512]{2,1,0:T(4,128)S(1)}, f32[1,512,4,64]{1,3,2,0:T(8,128)S(1)})) conditional(s32[]{:T(128)} %bitcast.111, (f32[1,4,512]{2,1,0:T(4,128)S(1)}, f32[1,4,512]{2,1,0:T(4,128)S(1)}, f32[1,512,4,64]{1,3,2,0:T(8,128)S(1)}) %tuple.92, (s32[]{:T(128)}, bf16[2048,256]{0,1:T(8,128)(2,1)}, ...), branch_computations={%region_3.3_spmd, %region_4.6_spmd} | conditional | flops 277094400 | bytes 15589458 | solution.py:141
  113.4 1.1 constant_dynamic-slice_fusion
  114.5 0.8 bitcast_reduce_fusion
  115.3 0.7 fusion.2
  116.0 0.9 fusion.13
  117.0 1.3 dynamic_slice.33
  118.9 3.5 %conditional.2 = ((f32[1,4,512]{2,1,0:T(4,128)S(1)}, f32[1,4,512]{2,1,0:T(4,128)S(1)}, f32[1,512,4,64]{1,3,2,0:T(8,128)S(1)})) conditional(s32[]{:T(128)} %bitcast.111, (f32[1,4,512]{2,1,0:T(4,128)S(1)}, f32[1,4,512]{2,1,0:T(4,128)S(1)}, f32[1,512,4,64]{1,3,2,0:T(8,128)S(1)}) %tuple.92, (s32[]{:T(128)}, bf16[2048,256]{0,1:T(8,128)(2,1)}, ...), branch_computations={%region_3.3_spmd, %region_4.6_spmd} | conditional | flops 277094400 | bytes 15589458 | solution.py:141
  118.9 1.1 constant_dynamic-slice_fusion
  120.0 0.8 bitcast_reduce_fusion
  120.8 0.7 fusion.2
  121.5 0.9 fusion.13
  122.5 1.3 dynamic_slice.33
  124.4 3.5 %conditional.2 = ((f32[1,4,512]{2,1,0:T(4,128)S(1)}, f32[1,4,512]{2,1,0:T(4,128)S(1)}, f32[1,512,4,64]{1,3,2,0:T(8,128)S(1)})) conditional(s32[]{:T(128)} %bitcast.111, (f32[1,4,512]{2,1,0:T(4,128)S(1)}, f32[1,4,512]{2,1,0:T(4,128)S(1)}, f32[1,512,4,64]{1,3,2,0:T(8,128)S(1)}) %tuple.92, (s32[]{:T(128)}, bf16[2048,256]{0,1:T(8,128)(2,1)}, ...), branch_computations={%region_3.3_spmd, %region_4.6_spmd} | conditional | flops 277094400 | bytes 15589458 | solution.py:141
  124.4 1.1 constant_dynamic-slice_fusion
  125.5 0.8 bitcast_reduce_fusion
  126.3 0.7 fusion.2
  127.0 0.9 fusion.13
  127.9 0.1 divide_convert_fusion
  128.0 2.6 %convolution_convert_fusion.1 = bf16[512,1024]{1,0:T(8,128)(2,1)} fusion(bf16[512,256]{0,1:T(8,128)(2,1)S(1)} %bitcast.116, bf16[256,1024]{1,0:T(8,128)(2,1)} %param.26), kind=kOutput, calls=%fused_computation.58 | convolution fusion | flops 268959744 | bytes 1835008 | tf_op jit(solution)/shard_map/dot_general | solution.py:167
  130.6 0.0 all-reduce.3.cloned.1.call-update
  130.6 0.0 reduce-scatter.2.cloned.1.call-start
  130.7 35.7 %all-reduce.3.cloned.1.call-done = bf16[512,1024]{1,0:T(8,128)(2,1)} async-done(((bf16[512,1024]{1,0:T(8,128)(2,1)}), bf16[512,1024]{1,0:T(8,128)(2,1)}) %all-reduce.3.cloned.1.call-update) | async-done | bytes 1048592 | tf_op jit(solution)/shard_map/psum | solution.py:168
  166.4 1.6 convert_reduce_fusion.1
  168.0 1.0 copy-done.3
  168.9 0.4 fusion.28
  169.4 5.4 %convolution_convert_fusion = bf16[512,1024]{1,0:T(8,128)(2,1)} fusion(bf16[1024,1024]{1,0:T(8,128)(2,1)S(1)} %copy-done, bf16[1024,1024]{1,0:T(8,128)(2,1)} %param.28, bf16[512,1024]{1,0:T(8,128)(2,1)} %copy-done.3, f32[1024]{0:T(1024)S(1)} %convert_element_type.119, f32[512]{0:T(512)S(1)} %add_rsqrt_fusion, f32[512]{0:T(512)S(1)} %broadcast_multiply_fusion), kind=kOutput, calls=%fused_computation.57 | convolution fusion | flops 2155347968 | bytes 6299648 | tf_op jit(solution)/shard_map/dot_general | solution.py:177
  174.7 0.0 reduce-scatter.2.cloned.1.call-update
  174.8 25.4 %reduce-scatter.2.cloned.1.call-done = bf16[512,256]{1,0:T(8,128)(2,1)} async-done(((bf16[512,1024]{1,0:T(8,128)(2,1)}), bf16[512,256]{1,0:T(8,128)(2,1)}) %reduce-scatter.2.cloned.1.call-update) | async-done | bytes 262160 | tf_op jit(solution)/shard_map/reduce_scatter | solution.py:178
  200.2 1.8 add_convert_fusion
  (35 shorter events, 0.3 us)
Async XLA Ops:
  6.5 162.8 %copy-start = (bf16[1024,1024]{1,0:T(8,128)(2,1)S(1)}, bf16[1024,1024]{1,0:T(8,128)(2,1)}, u32[]{:S(2)}) copy-start(bf16[1024,1024]{1,0:T(8,128)(2,1)} %param.29) | copy-start | bytes 6291460
  6.5 34.4 %all-gather.4.cloned.1.call-start = ((), (), s32[]{:S(2)}) async-start(), calls=%async_computation.1 | async-start | bytes 1310720 | tf_op jit(solution)/shard_map/all_gather | solution.py:97
  7.5 13.1 %collective-permute-start.1 = (bf16[64,256]{1,0:T(8,128)(2,1)S(1)}, bf16[64,256]{1,0:T(8,128)(2,1)S(1)}, u32[]{:S(2)}, u32[]{:S(2)}) collective-permute-start(bf16[64,256]{1,0:T(8,128)(2,1)S(1)} %get-tuple-element.351), channel_id=1, source_target_pairs={{4,0},{8,4},{12,8},{5,1},{9,5},{13,9},{6,2},{10,6},{14,10},{7,3},{... | collective-permute-start | bytes 98312 | tf_op jit(solution)/shard_map/ppermute | solution.py:21
  8.8 11.8 %collective-permute-start = (bf16[64,256]{1,0:T(8,128)(2,1)S(1)}, bf16[64,256]{1,0:T(8,128)(2,1)S(1)}, u32[]{:S(2)}, u32[]{:S(2)}) collective-permute-start(bf16[64,256]{1,0:T(8,128)(2,1)S(1)} %get-tuple-element.350), channel_id=1, source_target_pairs={{0,4},{4,8},{8,12},{1,5},{5,9},{9,13},{2,6},{6,10},{10,14},{3,7},{... | collective-permute-start | bytes 98312 | tf_op jit(solution)/shard_map/ppermute | solution.py:20
  20.9 1.6 copy-start.4
  20.9 2.5 %copy-start.5 = (bf16[1024]{0:T(1024)(128)(2,1)S(1)}, bf16[1024]{0:T(1024)(128)(2,1)}, u32[]{:S(2)}) copy-start(bf16[1024]{0:T(1024)(128)(2,1)} %param.22) | copy-start | bytes 6148
  23.3 51.2 %all-gather.6.cloned.1.call-start = ((), (), s32[]{:S(2)}) async-start(), calls=%async_computation.2 | async-start | bytes 1310720 | tf_op jit(solution)/shard_map/all_gather | solution.py:147
  41.0 3.2 %copy-start.1 = (bf16[512,1024]{1,0:T(8,128)(2,1)S(1)}, bf16[512,1024]{1,0:T(8,128)(2,1)}, u32[]{:S(2)}) copy-start(bf16[512,1024]{1,0:T(8,128)(2,1)} %all-gather.4.cloned.1.call-done) | copy-start | bytes 3145732
  46.4 57.1 %all-gather.8.cloned.1.call-start = ((), (), s32[]{:S(2)}) async-start(), calls=%async_computation.3 | async-start | bytes 1310720 | tf_op jit(solution)/shard_map/all_gather | solution.py:148
  48.8 117.6 %all-reduce.3.cloned.1.call-start = ((), (), s32[]{:S(2)}) async-start(), calls=%async_computation.4 | async-start | bytes 2097152 | tf_op jit(solution)/shard_map/psum | solution.py:168
  127.9 2.7 %copy-start.6 = (bf16[1024]{0:T(1024)(128)(2,1)S(1)}, bf16[1024]{0:T(1024)(128)(2,1)}, u32[]{:S(2)}) copy-start(bf16[1024]{0:T(1024)(128)(2,1)} %param.27) | copy-start | bytes 6148
  128.0 38.3 %copy-start.2 = (bf16[512,1024]{1,0:T(8,128)(2,1)S(1)}, bf16[512,1024]{1,0:T(8,128)(2,1)}, u32[]{:S(2)}) copy-start(bf16[512,1024]{1,0:T(8,128)(2,1)} %all-gather.4.cloned.1.call-done) | copy-start | bytes 3145732
  130.6 69.5 %reduce-scatter.2.cloned.1.call-start = ((), (), s32[]{:S(2)}) async-start(), calls=%async_computation.5 | async-start | bytes 1310720 | tf_op jit(solution)/shard_map/reduce_scatter | solution.py:178
  168.0 1.0 copy-start.3
Sparse Core Ops, SparseCore 0:
  23.4 17.5 all-gather.3
  46.6 27.9 all-gather.5
  76.1 27.4 all-gather.7
  130.7 35.5 all-reduce.2
  174.9 25.2 reduce-scatter.1
where the time goes:
time: 209 us; the launch traced here: 208 us
  waiting for transfers between devices  129 us (62%)
  matrix products  21 us (10%)
  local copies, waits for them, and re-layouts  19.2 us (9%)
  between operations  14.6 us (7%)
  other arithmetic  14.3 us (7%)
  starting transfers between devices  7.01 us (3%)
  loops' own time  2.85 us (1%)
    psum x1, waiting for transfers between devices, shards(): lax.psum(partial_out.astype(jnp.bfloat16), 'heads').astype(jnp.float32)  35.7 us
    all_gather x1, waiting for transfers between devices, shards(): value_piece = lax.all_gather(values_all, 'bricks', axis=0, tiled=True)  26.8 us
    reduce_scatter x1, waiting for transfers between devices, shards(): lax.psum_scatter(lowered.astype(jnp.bfloat16), 'heads', scatter_dimension...  25.4 us
    all_gather x1, waiting for transfers between devices, shards(): key_piece = lax.all_gather(keys_all, 'bricks', axis=0, tiled=True)  24 us
    all_gather x1, waiting for transfers between devices, shards(): stream_full = lax.all_gather(stream, 'heads', axis=1, tiled=True)  17.6 us
    ppermute x1, starting transfers between devices, extended_2(): before = lax.ppermute(last, axis, up)  5.56 us
    dot_general x1, matrix products, shards(): lowered = jnp.dot(hidden, down_weight, preferred_element_type=jnp.float32)  5.37 us
    dynamic_slice x4, local copies, waits for them, and re-layouts, absorb(): linked = pattern[first_brick + local_id, key_brick]  5.15 us
  transfers between devices with their start and end apart: 7, of which 5 were waited for; matrix products, arithmetic and copies ran while one was open for 5% of the time, Pallas kernels for 0%

commit v1 on v0

--- a/solution.py
+++ b/solution.py
@@ -1,6 +1,10 @@
+import functools
+
 import jax
 import jax.numpy as jnp
 from jax import lax
+from jax.experimental import pallas as pl
+from jax.experimental.pallas import tpu as pltpu
 from jax.sharding import PartitionSpec as P
 
 EDGE = 8
@@ -50,6 +54,72 @@
                 ]
                 summed = summed + weights[step_x * 9 + step_y * 3 + step_z] * window
     return summed.reshape(brick_count * edge_len**3, channels) + conv_bias.astype(jnp.float32)
+
+
+def attention_body(linked_ref, query_ref, key_ref, value_ref, out_ref, max_ref, mass_ref, sum_ref,
+                   *, head_count, key_count):
+    key_id = pl.program_id(1)
+    score_scale = HEAD_DIM ** (-0.5)
+
+    @pl.when(key_id == 0)
+    def _start():
+        max_ref[...] = jnp.full(max_ref.shape, -1e30, jnp.float32)
+        mass_ref[...] = jnp.zeros(mass_ref.shape, jnp.float32)
+        sum_ref[...] = jnp.zeros(sum_ref.shape, jnp.float32)
+
+    linked = linked_ref[pl.program_id(0) * key_count + key_id]
+
+    @pl.when(linked > 0)
+    def _absorb():
+        for head in range(head_count):
+            cols = slice(head * HEAD_DIM, (head + 1) * HEAD_DIM)
+            query_h = query_ref[:, cols]
+            key_h = key_ref[:, cols]
+            value_h = value_ref[:, cols]
+            scores = lax.dot_general(
+                query_h, key_h, (((1,), (1,)), ((), ())), preferred_element_type=jnp.float32
+            ) * score_scale
+            max_old = max_ref[head]
+            max_new = jnp.maximum(max_old, jnp.max(scores, axis=-1, keepdims=True))
+            factor = jnp.exp(max_old - max_new)
+            weights = jnp.exp(scores - max_new)
+            mass_ref[head] = mass_ref[head] * factor + jnp.sum(weights, axis=-1, keepdims=True)
+            sum_ref[head] = sum_ref[head] * factor + jnp.dot(
+                weights.astype(jnp.bfloat16), value_h, preferred_element_type=jnp.float32
+            )
+            max_ref[head] = max_new
+
+    @pl.when(key_id == key_count - 1)
+    def _finish():
+        for head in range(head_count):
+            cols = slice(head * HEAD_DIM, (head + 1) * HEAD_DIM)
+            out_ref[:, cols] = (sum_ref[head] / mass_ref[head]).astype(out_ref.dtype)
+
+
+def brick_attention(linked_rows, queries, pair_piece, head_count, key_count, brick_rows):
+    row_count, width = queries.shape
+    body = functools.partial(attention_body, head_count=head_count, key_count=key_count)
+    grid_spec = pltpu.PrefetchScalarGridSpec(
+        num_scalar_prefetch=1,
+        grid=(row_count // brick_rows, key_count),
+        in_specs=[
+            pl.BlockSpec((brick_rows, width), lambda i, k, linked: (i, 0)),
+            pl.BlockSpec((brick_rows, width), lambda i, k, linked: (k, 0)),
+            pl.BlockSpec((brick_rows, width), lambda i, k, linked: (k, 1)),
+        ],
+        out_specs=pl.BlockSpec((brick_rows, width), lambda i, k, linked: (i, 0)),
+        scratch_shapes=[
+            pltpu.VMEM((head_count, brick_rows, 1), jnp.float32),
+            pltpu.VMEM((head_count, brick_rows, 1), jnp.float32),
+            pltpu.VMEM((head_count, brick_rows, HEAD_DIM), jnp.float32),
+        ],
+    )
+    return pl.pallas_call(
+        body,
+        grid_spec=grid_spec,
+        out_shape=jax.ShapeDtypeStruct((row_count, width), jnp.bfloat16),
+        compiler_params=pltpu.CompilerParams(dimension_semantics=("arbitrary", "arbitrary")),
+    )(linked_rows, queries, pair_piece, pair_piece)
 
 
 def shards(
@@ -98,71 +168,15 @@
     normed = layer_norm(stream_full, gain_one).astype(jnp.bfloat16)
     queries = jnp.dot(normed, query_weight, preferred_element_type=jnp.float32).astype(jnp.bfloat16)
     head_count = local_width // HEAD_DIM
-    query_heads = queries.reshape(local_bricks, brick_rows, head_count, HEAD_DIM)
-    score_scale = HEAD_DIM ** (-0.5)
-    start_state = (
-        jnp.full((local_bricks, head_count, brick_rows), -1e30, jnp.float32),
-        jnp.zeros((local_bricks, head_count, brick_rows), jnp.float32),
-        jnp.zeros((local_bricks, brick_rows, head_count, HEAD_DIM), jnp.float32),
-    )
-
-    def absorb(state_in, local_id, key_brick, fetch_pair):
-        linked = pattern[first_brick + local_id, key_brick]
-
-        def include(state_now):
-            row_max, row_mass, weighted = state_now
-            key_rows, value_rows = fetch_pair()
-            keys_h = key_rows.reshape(brick_rows, head_count, HEAD_DIM)
-            values_h = value_rows.reshape(brick_rows, head_count, HEAD_DIM)
-            query_one = lax.dynamic_index_in_dim(query_heads, local_id, 0, keepdims=False)
-            scores = (
-                jnp.einsum("qhd,khd->hqk", query_one, keys_h, preferred_element_type=jnp.float32)
-                * score_scale
-            )
-            max_old = lax.dynamic_index_in_dim(row_max, local_id, 0, keepdims=False)
-            mass_old = lax.dynamic_index_in_dim(row_mass, local_id, 0, keepdims=False)
-            sum_old = lax.dynamic_index_in_dim(weighted, local_id, 0, keepdims=False)
-            max_new = jnp.maximum(max_old, jnp.max(scores, axis=-1))
-            factor = jnp.exp(max_old - max_new)
-            weights = jnp.exp(scores - max_new[:, :, None])
-            mass_new = mass_old * factor + jnp.sum(weights, axis=-1)
-            sum_new = sum_old * jnp.transpose(factor)[:, :, None] + jnp.einsum(
-                "hqk,khd->qhd",
-                weights.astype(jnp.bfloat16),
-                values_h,
-                preferred_element_type=jnp.float32,
-            )
-            return (
-                lax.dynamic_update_index_in_dim(row_max, max_new, local_id, 0),
-                lax.dynamic_update_index_in_dim(row_mass, mass_new, local_id, 0),
-                lax.dynamic_update_index_in_dim(weighted, sum_new, local_id, 0),
-            )
-
-        return lax.cond(linked > 0, include, lambda state_now: state_now, state_in)
-
     keys_all = jnp.dot(normed, key_weight, preferred_element_type=jnp.float32).astype(jnp.bfloat16)
     values_all = jnp.dot(normed, value_weight, preferred_element_type=jnp.float32).astype(
         jnp.bfloat16
     )
-    key_piece = lax.all_gather(keys_all, "bricks", axis=0, tiled=True)
-    value_piece = lax.all_gather(values_all, "bricks", axis=0, tiled=True)
-    piece_bricks = key_piece.shape[0] // brick_rows
-
-    def visit(visit_idx, state_now):
-        local_id = visit_idx // piece_bricks
-        offset = visit_idx % piece_bricks
-
-        def fetch_pair():
-            return (
-                lax.dynamic_slice_in_dim(key_piece, offset * brick_rows, brick_rows, 0),
-                lax.dynamic_slice_in_dim(value_piece, offset * brick_rows, brick_rows, 0),
-            )
-
-        return absorb(state_now, local_id, offset, fetch_pair)
-
-    result = lax.fori_loop(0, local_bricks * piece_bricks, visit, start_state)
-    row_max, row_mass, weighted = result
-    attended = (weighted / jnp.transpose(row_mass, (0, 2, 1))[:, :, :, None]).astype(jnp.bfloat16)
+    pair_local = jnp.concatenate([keys_all, values_all], axis=1)
+    pair_piece = lax.all_gather(pair_local, "bricks", axis=0, tiled=True)
+    key_count = pair_piece.shape[0] // brick_rows
+    linked_rows = lax.dynamic_slice_in_dim(pattern, first_brick, local_bricks, 0).reshape(-1)
+    attended = brick_attention(linked_rows, queries, pair_piece, head_count, key_count, brick_rows)
     attended = attended.reshape(row_count, local_width)
     partial_out = jnp.dot(attended, out_weight, preferred_element_type=jnp.float32)
     full_sum = lax.psum(partial_out.astype(jnp.bfloat16), "heads").astype(jnp.float32)

time: 209 us -> 197 us (0.943)
  Pallas kernels: 0 us -> 24.3 us
  local copies, waits for them, and re-layouts: 19.2 us -> 6.39 us
  waiting for transfers between devices: 129 us -> 119 us
  matrix products: 21 us -> 12.3 us
  loops' own time: 2.85 us -> 0 us
  other arithmetic: 14.3 us -> 12.2 us
    pallas_call x0 -> x1, Pallas kernels: none -> 24.3 us  [brick_attention(): pl.pallas_call(body, grid_spec=grid_spec, out_shape=jax.ShapeDtypeStruct(...]
    dynamic_slice x8 -> x0, local copies, waits for them, and re-layouts: 9.43 us -> none  [the longest x4 5.15 us: absorb(): linked = pattern[first_brick + local_id, key_brick]]
    all_gather x2 -> x1, waiting for transfers between devices: 50.7 us -> 42.6 us  [shards(): pair_piece = lax.all_gather(pair_local, 'bricks', axis=0, tiled=True)]
    dot_general x8 -> x0, matrix products: 6.78 us -> none  [the longest x4 3.7 us: include(): jnp.einsum('hqk,khd->qhd', weights.astype(jnp.bfloat16), values_h, prefer...]
    while x2 -> x0, local copies, waits for them, and re-layouts: 4.55 us -> none  [shards(): result = lax.fori_loop(0, local_bricks * piece_bricks, visit, start_state)]
    another operation x5 -> x0, loops' own time: 2.85 us -> none  [the longest x1 2.68 us: shards(): result = lax.fori_loop(0, local_bricks * piece_bricks, visit, start_state)]
    reduce_sum x4 -> x0, other arithmetic: 2.82 us -> none  [include(): mass_new = mass_old * factor + jnp.sum(weights, axis=-1)]
  transfers between devices with their start and end apart: 7 -> 6, of which waited for: 5 -> 4; matrix products, arithmetic and copies ran while one was open for 5% -> 4% of each run, Pallas kernels for 0% -> 0%
where the time goes in v1:
time: 197 us; the launch traced here: 196 us
  waiting for transfers between devices  119 us (60%)
  Pallas kernels  24.3 us (12%)
  between operations  14.6 us (7%)
  matrix products  12.3 us (6%)
  other arithmetic  12.2 us (6%)
  starting transfers between devices  7.15 us (4%)
  local copies, waits for them, and re-layouts  6.39 us (3%)
    all_gather x1, waiting for transfers between devices, shards(): pair_piece = lax.all_gather(pair_local, 'bricks', axis=0, tiled=True)  42.6 us
    psum x1, waiting for transfers between devices, shards(): lax.psum(partial_out.astype(jnp.bfloat16), 'heads').astype(jnp.float32)  33.8 us
    reduce_scatter x1, waiting for transfers between devices, shards(): lax.psum_scatter(lowered.astype(jnp.bfloat16), 'heads', scatter_dimension...  25.4 us
    pallas_call x1, Pallas kernels, brick_attention(): pl.pallas_call(body, grid_spec=grid_spec, out_shape=jax.ShapeDtypeStruct(...  24.3 us
    all_gather x1, waiting for transfers between devices, shards(): stream_full = lax.all_gather(stream, 'heads', axis=1, tiled=True)  17.6 us
    ppermute x1, starting transfers between devices, extended_2(): before = lax.ppermute(last, axis, up)  5.56 us
    dot_general x1, matrix products, shards(): lowered = jnp.dot(hidden, down_weight, preferred_element_type=jnp.float32)  5.39 us
  transfers between devices with their start and end apart: 6, of which 4 were waited for; matrix products, arithmetic and copies ran while one was open for 4% of the time, Pallas kernels for 0%

profile of v1, /device:TPU:0, one launch (start us, length us, event | category | flops | bytes accessed | tf_op | source)
XLA Modules:
  0.0 196.4 jit_solution(15413551960294845472)
XLA Ops:
  6.5 0.0 copy-start
  6.5 0.0 all-gather.3.cloned.1.call-start
  6.5 0.9 fusion.74
  7.5 1.3 collective-permute-start.1
  8.8 5.6 %collective-permute-start = (bf16[64,256]{1,0:T(8,128)(2,1)S(1)}, bf16[64,256]{1,0:T(8,128)(2,1)S(1)}, u32[]{:S(2)}, u32[]{:S(2)}) collective-permute-start(bf16[64,256]{1,0:T(8,128)(2,1)S(1)} %get-tuple-element.29), channel_id=1, source_target_pairs={{0,4},{4,8},{8,12},{1,5},{5,9},{9,13},{2,6},{6,10},{10,14},{3,7},{... | collective-permute-start | bytes 98312 | tf_op jit(solution)/shard_map/ppermute | solution.py:24
  14.3 1.0 fusion.75
  15.3 0.9 fusion.76
  16.2 1.4 fusion.77
  18.9 1.0 convert
  19.9 0.7 convert_element_type.85
  20.6 0.0 collective-permute-done.1
  20.6 0.0 collective-permute-done
  20.6 0.3 select_maximum_fusion
  20.9 0.0 copy-start.3
  20.9 0.0 copy-start.4
  20.9 1.6 fusion.36
  22.5 0.0 copy-done.3
  22.5 0.8 fusion.65
  23.3 0.0 all-gather.3.cloned.1.call-update
  23.3 0.0 all-gather.5.cloned.1.call-start
  23.3 0.0 copy-done.4
  23.4 17.6 %all-gather.3.cloned.1.call-done = bf16[512,1024]{1,0:T(8,128)(2,1)} async-done(((bf16[512,256]{1,0:T(8,128)(2,1)}), bf16[512,1024]{1,0:T(8,128)(2,1)}) %all-gather.3.cloned.1.call-update) | async-done | bytes 1048592 | tf_op jit(solution)/shard_map/all_gather | solution.py:167
  41.0 0.0 copy-start.1
  41.0 1.5 convert_reduce_fusion
  42.5 0.0 copy-start.6
  42.5 1.7 fusion.4
  44.2 0.0 copy-done.1
  44.2 1.6 convolution_convert_fusion.3
  45.8 0.0 copy-done.6
  45.8 0.5 convolution_convert_fusion.2
  46.3 0.9 pad_maximum_fusion.2
  47.2 0.0 all-gather.5.cloned.1.call-update
  47.2 0.0 all-reduce.3.cloned.1.call-start
  47.2 1.2 dynamic-slice_bitcast_fusion.linked_ref
  48.4 2.3 %convolution_convert_fusion.4.query_ref = bf16[512,256]{1,0:T(8,128)(2,1)} fusion(bf16[1024,256]{1,0:T(8,128)(2,1)} %param.19, bf16[512,1024]{1,0:T(8,128)(2,1)S(1)} %copy-done.1, f32[1024]{0:T(1024)S(1)} %convert_element_type.88, f32[512]{0:T(512)S(1)} %add_rsqrt_fusion.1, f32[512]{0:T(512)S(1)} %broadcast_multiply_fusion.1), kind=kOutput, calls=%fused_computation.38 | convolution fusion | flops 271187968 | bytes 1843200 | tf_op jit(solution)/shard_map/dot_general | solution.py:169
  50.7 42.6 %all-gather.5.cloned.1.call-done.key_ref.value_ref = bf16[2048,512]{1,0:T(8,128)(2,1)} async-done(((bf16[512,512]{1,0:T(8,128)(2,1)}), bf16[2048,512]{1,0:T(8,128)(2,1)}) %all-gather.5.cloned.1.call-update) | async-done | bytes 2097168 | tf_op jit(solution)/shard_map/all_gather | solution.py:176
  93.3 24.3 %shard_map.127 = bf16[512,256]{1,0:T(8,128)(2,1)} custom-call(s32[4]{0:T(128)} %dynamic-slice_bitcast_fusion.linked_ref, bf16[512,256]{1,0:T(8,128)(2,1)} %convolution_convert_fusion.4.query_ref, bf16[2048,512]{1,0:T(8,128)(2,1)} %all-gather.5.cloned.1.call-done.key_ref.value_ref, bf16[2048,512]{1,0:T(8,128)(2,1)} %all-gather.5.cloned.1.call-done.key_ref.value_ref), custom_call_target="tpu_custom_call" | custom-call | tf_op jit(solution)/shard_map/pallas_call | solution.py:117
  117.6 0.0 copy-start.5
  117.6 2.5 %convolution_convert_fusion.1 = bf16[512,1024]{1,0:T(8,128)(2,1)} fusion(bf16[512,256]{1,0:T(8,128)(2,1)} %shard_map.127, bf16[256,1024]{1,0:T(8,128)(2,1)} %param.22), kind=kOutput, calls=%fused_computation.35 | convolution fusion | flops 268959744 | bytes 1835008 | tf_op jit(solution)/shard_map/dot_general | solution.py:181
  120.1 0.0 all-reduce.3.cloned.1.call-update
  120.2 0.2 reduce-scatter.2.cloned.1.call-start
  120.4 0.0 copy-done.5
  120.4 33.8 %all-reduce.3.cloned.1.call-done = bf16[512,1024]{1,0:T(8,128)(2,1)} async-done(((bf16[512,1024]{1,0:T(8,128)(2,1)}), bf16[512,1024]{1,0:T(8,128)(2,1)}) %all-reduce.3.cloned.1.call-update) | async-done | bytes 1048592 | tf_op jit(solution)/shard_map/psum | solution.py:182
  154.2 1.6 convert_reduce_fusion.1
  155.8 0.0 copy-start.2
  155.8 1.0 copy-done.2
  156.8 0.4 fusion.7
  157.2 0.0 copy-done
  157.2 5.4 %convolution_convert_fusion = bf16[512,1024]{1,0:T(8,128)(2,1)} fusion(bf16[1024,1024]{1,0:T(8,128)(2,1)S(1)} %copy-done, bf16[1024,1024]{1,0:T(8,128)(2,1)} %param.24, bf16[512,1024]{1,0:T(8,128)(2,1)} %copy-done.2, f32[1024]{0:T(1024)S(1)} %convert_element_type.98, f32[512]{0:T(512)S(1)} %add_rsqrt_fusion, f32[512]{0:T(512)S(1)} %broadcast_multiply_fusion), kind=kOutput, calls=%fused_computation.34 | convolution fusion | flops 2155347968 | bytes 6299648 | tf_op jit(solution)/shard_map/dot_general | solution.py:191
  162.6 0.0 reduce-scatter.2.cloned.1.call-update
  162.6 25.4 %reduce-scatter.2.cloned.1.call-done = bf16[512,256]{1,0:T(8,128)(2,1)} async-done(((bf16[512,1024]{1,0:T(8,128)(2,1)}), bf16[512,256]{1,0:T(8,128)(2,1)}) %reduce-scatter.2.cloned.1.call-update) | async-done | bytes 262160 | tf_op jit(solution)/shard_map/reduce_scatter | solution.py:192
  188.1 1.8 add_convert_fusion
  (8 shorter events, 0.1 us)
Async XLA Ops:
  6.5 150.7 %copy-start = (bf16[1024,1024]{1,0:T(8,128)(2,1)S(1)}, bf16[1024,1024]{1,0:T(8,128)(2,1)}, u32[]{:S(2)}) copy-start(bf16[1024,1024]{1,0:T(8,128)(2,1)} %param.25) | copy-start | bytes 6291460
  6.5 34.4 %all-gather.3.cloned.1.call-start = ((), (), s32[]{:S(2)}) async-start(), calls=%async_computation.1 | async-start | bytes 1310720 | tf_op jit(solution)/shard_map/all_gather | solution.py:167
  7.5 13.1 %collective-permute-start.1 = (bf16[64,256]{1,0:T(8,128)(2,1)S(1)}, bf16[64,256]{1,0:T(8,128)(2,1)S(1)}, u32[]{:S(2)}, u32[]{:S(2)}) collective-permute-start(bf16[64,256]{1,0:T(8,128)(2,1)S(1)} %get-tuple-element.30), channel_id=1, source_target_pairs={{4,0},{8,4},{12,8},{5,1},{9,5},{13,9},{6,2},{10,6},{14,10},{7,3},{... | collective-permute-start | bytes 98312 | tf_op jit(solution)/shard_map/ppermute | solution.py:25
  8.8 11.8 %collective-permute-start = (bf16[64,256]{1,0:T(8,128)(2,1)S(1)}, bf16[64,256]{1,0:T(8,128)(2,1)S(1)}, u32[]{:S(2)}, u32[]{:S(2)}) collective-permute-start(bf16[64,256]{1,0:T(8,128)(2,1)S(1)} %get-tuple-element.29), channel_id=1, source_target_pairs={{0,4},{4,8},{8,12},{1,5},{5,9},{9,13},{2,6},{6,10},{10,14},{3,7},{... | collective-permute-start | bytes 98312 | tf_op jit(solution)/shard_map/ppermute | solution.py:24
  20.9 1.6 copy-start.3
  20.9 2.5 %copy-start.4 = (bf16[1024]{0:T(1024)(128)(2,1)S(1)}, bf16[1024]{0:T(1024)(128)(2,1)}, u32[]{:S(2)}) copy-start(bf16[1024]{0:T(1024)(128)(2,1)} %param.18) | copy-start | bytes 6148
  23.3 70.0 %all-gather.5.cloned.1.call-start = ((), (), s32[]{:S(2)}) async-start(), calls=%async_computation.2 | async-start | bytes 2621440 | tf_op jit(solution)/shard_map/all_gather | solution.py:176
  41.0 3.2 %copy-start.1 = (bf16[512,1024]{1,0:T(8,128)(2,1)S(1)}, bf16[512,1024]{1,0:T(8,128)(2,1)}, u32[]{:S(2)}) copy-start(bf16[512,1024]{1,0:T(8,128)(2,1)} %all-gather.3.cloned.1.call-done) | copy-start | bytes 3145732
  42.5 3.3 %copy-start.6 = (bf16[1024,256]{1,0:T(8,128)(2,1)S(1)}, bf16[1024,256]{1,0:T(8,128)(2,1)}, u32[]{:S(2)}) copy-start(bf16[1024,256]{1,0:T(8,128)(2,1)} %param.21) | copy-start | bytes 1572868
  47.2 107.0 %all-reduce.3.cloned.1.call-start = ((), (), s32[]{:S(2)}) async-start(), calls=%async_computation.3 | async-start | bytes 2097152 | tf_op jit(solution)/shard_map/psum | solution.py:182
  117.6 2.8 %copy-start.5 = (bf16[1024]{0:T(1024)(128)(2,1)S(1)}, bf16[1024]{0:T(1024)(128)(2,1)}, u32[]{:S(2)}) copy-start(bf16[1024]{0:T(1024)(128)(2,1)} %param.23) | copy-start | bytes 6148
  120.2 67.9 %reduce-scatter.2.cloned.1.call-start = ((), (), s32[]{:S(2)}) async-start(), calls=%async_computation.4 | async-start | bytes 1310720 | tf_op jit(solution)/shard_map/reduce_scatter | solution.py:192
  155.8 1.0 copy-start.2
Sparse Core Ops, SparseCore 0:
  23.4 17.5 all-gather.2
  47.3 45.9 all-gather.4
  120.3 33.8 all-reduce.2
  162.7 25.2 reduce-scatter.1

commit v2 on v0

--- a/solution.py
+++ b/solution.py
@@ -50,6 +50,65 @@
                 ]
                 summed = summed + weights[step_x * 9 + step_y * 3 + step_z] * window
     return summed.reshape(brick_count * edge_len**3, channels) + conv_bias.astype(jnp.float32)
+
+
+def level_count(total):
+    levels = total.bit_length() - 1
+    assert 1 << levels == total
+    return levels
+
+
+def scatter_heads(partial, head_id, head_total):
+    levels = level_count(head_total)
+    rows = partial.shape[0]
+    width = partial.shape[1] // head_total
+    current = partial.reshape((rows,) + (2,) * levels + (width,))
+    for level in range(levels):
+        bit = 1 << level
+        axis = levels - level
+        mine = (head_id >> level) & 1
+        keep = lax.dynamic_index_in_dim(current, mine, axis, keepdims=False)
+        give = lax.dynamic_index_in_dim(current, 1 - mine, axis, keepdims=False)
+        got = lax.ppermute(
+            give.astype(jnp.bfloat16), "heads", [(i, i ^ bit) for i in range(head_total)]
+        )
+        current = keep + got.astype(jnp.float32)
+    return current.reshape(rows, width)
+
+
+def gather_heads(piece, head_id, head_total):
+    levels = level_count(head_total)
+    rows, width = piece.shape
+    current = piece
+    for level in reversed(range(levels)):
+        bit = 1 << level
+        mine = (head_id >> level) & 1
+        got = lax.ppermute(current, "heads", [(i, i ^ bit) for i in range(head_total)])
+        low = jnp.where(mine == 0, current, got)
+        high = jnp.where(mine == 0, got, current)
+        current = jnp.stack([low, high], axis=current.ndim - 1)
+    return current.reshape(rows, head_total * width)
+
+
+def absorb_block(state, query_heads, block, linked, head_count, brick_rows, local_width):
+    row_max, row_mass, weighted = state
+    key_rows = block[:, :local_width].reshape(-1, head_count, HEAD_DIM)
+    value_rows = block[:, local_width:].reshape(-1, head_count, HEAD_DIM)
+    scores = (
+        jnp.einsum("bqhd,khd->bhqk", query_heads, key_rows, preferred_element_type=jnp.float32)
+        * HEAD_DIM ** (-0.5)
+    )
+    keep = jnp.repeat(linked, brick_rows, axis=1, total_repeat_length=key_rows.shape[0])
+    scores = jnp.where(keep[:, None, None, :], scores, -1e30)
+    max_new = jnp.maximum(row_max, jnp.max(scores, axis=-1))
+    factor = jnp.exp(row_max - max_new)
+    weights = jnp.exp(scores - max_new[..., None])
+    mass_new = row_mass * factor + jnp.sum(weights, axis=-1)
+    sum_new = weighted * jnp.transpose(factor, (0, 2, 1))[..., None] + jnp.einsum(
+        "bhqk,khd->bqhd", weights.astype(jnp.bfloat16), value_rows,
+        preferred_element_type=jnp.float32,
+    )
+    return max_new, mass_new, sum_new
 
 
 def shards(
@@ -94,90 +153,49 @@
     upper_face = upper_face * upper_open.astype(jnp.float32)[:, None, None]
     conv_out = depthwise(brick_vals, lower_face, upper_face, conv_weight, conv_bias)
     stream = (voxel_feats.astype(jnp.float32) + conv_out).astype(jnp.bfloat16)
-    stream_full = lax.all_gather(stream, "heads", axis=1, tiled=True)
+    head_total = lax.axis_size("heads")
+    head_id = lax.axis_index("heads")
+    stream_full = gather_heads(stream, head_id, head_total)
     normed = layer_norm(stream_full, gain_one).astype(jnp.bfloat16)
     queries = jnp.dot(normed, query_weight, preferred_element_type=jnp.float32).astype(jnp.bfloat16)
     head_count = local_width // HEAD_DIM
+    keys_all = jnp.dot(normed, key_weight, preferred_element_type=jnp.float32).astype(jnp.bfloat16)
+    values_all = jnp.dot(normed, value_weight, preferred_element_type=jnp.float32).astype(
+        jnp.bfloat16
+    )
+    pair_local = jnp.concatenate([keys_all, values_all], axis=1)
+    brick_dev = lax.axis_index("bricks")
+    dev_total = lax.axis_size("bricks")
+    key_total = pattern.shape[1]
     query_heads = queries.reshape(local_bricks, brick_rows, head_count, HEAD_DIM)
-    score_scale = HEAD_DIM ** (-0.5)
-    start_state = (
+    linked_rows = lax.dynamic_slice_in_dim(pattern, first_brick, local_bricks, 0)
+    state = (
         jnp.full((local_bricks, head_count, brick_rows), -1e30, jnp.float32),
         jnp.zeros((local_bricks, head_count, brick_rows), jnp.float32),
         jnp.zeros((local_bricks, brick_rows, head_count, HEAD_DIM), jnp.float32),
     )
-
-    def absorb(state_in, local_id, key_brick, fetch_pair):
-        linked = pattern[first_brick + local_id, key_brick]
-
-        def include(state_now):
-            row_max, row_mass, weighted = state_now
-            key_rows, value_rows = fetch_pair()
-            keys_h = key_rows.reshape(brick_rows, head_count, HEAD_DIM)
-            values_h = value_rows.reshape(brick_rows, head_count, HEAD_DIM)
-            query_one = lax.dynamic_index_in_dim(query_heads, local_id, 0, keepdims=False)
-            scores = (
-                jnp.einsum("qhd,khd->hqk", query_one, keys_h, preferred_element_type=jnp.float32)
-                * score_scale
-            )
-            max_old = lax.dynamic_index_in_dim(row_max, local_id, 0, keepdims=False)
-            mass_old = lax.dynamic_index_in_dim(row_mass, local_id, 0, keepdims=False)
-            sum_old = lax.dynamic_index_in_dim(weighted, local_id, 0, keepdims=False)
-            max_new = jnp.maximum(max_old, jnp.max(scores, axis=-1))
-            factor = jnp.exp(max_old - max_new)
-            weights = jnp.exp(scores - max_new[:, :, None])
-            mass_new = mass_old * factor + jnp.sum(weights, axis=-1)
-            sum_new = sum_old * jnp.transpose(factor)[:, :, None] + jnp.einsum(
-                "hqk,khd->qhd",
-                weights.astype(jnp.bfloat16),
-                values_h,
-                preferred_element_type=jnp.float32,
-            )
-            return (
-                lax.dynamic_update_index_in_dim(row_max, max_new, local_id, 0),
-                lax.dynamic_update_index_in_dim(row_mass, mass_new, local_id, 0),
-                lax.dynamic_update_index_in_dim(weighted, sum_new, local_id, 0),
-            )
-
-        return lax.cond(linked > 0, include, lambda state_now: state_now, state_in)
-
-    keys_all = jnp.dot(normed, key_weight, preferred_element_type=jnp.float32).astype(jnp.bfloat16)
-    values_all = jnp.dot(normed, value_weight, preferred_element_type=jnp.float32).astype(
-        jnp.bfloat16
-    )
-    key_piece = lax.all_gather(keys_all, "bricks", axis=0, tiled=True)
-    value_piece = lax.all_gather(values_all, "bricks", axis=0, tiled=True)
-    piece_bricks = key_piece.shape[0] // brick_rows
-
-    def visit(visit_idx, state_now):
-        local_id = visit_idx // piece_bricks
-        offset = visit_idx % piece_bricks
-
-        def fetch_pair():
-            return (
-                lax.dynamic_slice_in_dim(key_piece, offset * brick_rows, brick_rows, 0),
-                lax.dynamic_slice_in_dim(value_piece, offset * brick_rows, brick_rows, 0),
-            )
-
-        return absorb(state_now, local_id, offset, fetch_pair)
-
-    result = lax.fori_loop(0, local_bricks * piece_bricks, visit, start_state)
-    row_max, row_mass, weighted = result
+    ring = [(i, (i + 1) % dev_total) for i in range(dev_total)]
+    block = pair_local
+    for step in range(dev_total):
+        if step > 0:
+            block = lax.ppermute(block, "bricks", ring)
+        source = (brick_dev - step) % dev_total
+        key_ids = source * local_bricks + jnp.arange(local_bricks, dtype=jnp.int32)
+        linked = jnp.take(linked_rows, key_ids, axis=1) > 0
+        state = absorb_block(state, query_heads, block, linked, head_count, brick_rows, local_width)
+    row_max, row_mass, weighted = state
     attended = (weighted / jnp.transpose(row_mass, (0, 2, 1))[:, :, :, None]).astype(jnp.bfloat16)
     attended = attended.reshape(row_count, local_width)
     partial_out = jnp.dot(attended, out_weight, preferred_element_type=jnp.float32)
-    full_sum = lax.psum(partial_out.astype(jnp.bfloat16), "heads").astype(jnp.float32)
-    stream_two_full = (stream_full.astype(jnp.float32) + full_sum).astype(jnp.bfloat16)
-    stream_two = lax.dynamic_slice_in_dim(
-        stream_two_full, lax.axis_index("heads") * local_width, local_width, 1
-    )
+    out_sum = scatter_heads(partial_out, head_id, head_total)
+    stream_two = (stream.astype(jnp.float32) + out_sum).astype(jnp.bfloat16)
+    stream_two_full = gather_heads(stream_two, head_id, head_total)
     normed_two = layer_norm(stream_two_full, gain_two).astype(jnp.bfloat16)
     hidden = jax.nn.gelu(
         jnp.dot(normed_two, up_weight, preferred_element_type=jnp.float32), approximate=True
     ).astype(jnp.bfloat16)
     lowered = jnp.dot(hidden, down_weight, preferred_element_type=jnp.float32)
-    mixed = lax.psum_scatter(
-        lowered.astype(jnp.bfloat16), "heads", scatter_dimension=1, tiled=True
-    ).astype(jnp.float32)
+    mixed = scatter_heads(lowered, head_id, head_total)
     return (stream_two.astype(jnp.float32) + mixed).astype(jnp.bfloat16)
 
 

time: 209 us -> 135 us (0.65)
  waiting for transfers between devices: 129 us -> 72.4 us
  between operations: 14.6 us -> 4.16 us
  starting transfers between devices: 7.01 us -> 16 us
  matrix products: 21 us -> 14.4 us
  local copies, waits for them, and re-layouts: 19.2 us -> 13.1 us
  loops' own time: 2.85 us -> 0 us
    ppermute x0 -> x11, waiting for transfers between devices: none -> 72.4 us  [the longest x3 41.2 us: shards(): block = lax.ppermute(block, 'bricks', ring)]
    all_gather x3 -> x0, waiting for transfers between devices: 68.3 us -> none  [the longest x1 26.8 us: shards(): value_piece = lax.all_gather(values_all, 'bricks', axis=0, tiled=True)]
    psum x1 -> x0, waiting for transfers between devices: 35.7 us -> none  [shards(): lax.psum(partial_out.astype(jnp.bfloat16), 'heads').astype(jnp.float32)]
    reduce_scatter x1 -> x0, waiting for transfers between devices: 25.4 us -> none  [shards(): lax.psum_scatter(lowered.astype(jnp.bfloat16), 'heads', scatter_dimension...]
    dynamic_slice x8 -> x0, local copies, waits for them, and re-layouts: 9.43 us -> none  [the longest x4 5.15 us: absorb(): linked = pattern[first_brick + local_id, key_brick]]
    ppermute x0 -> x11, starting transfers between devices: none -> 9.12 us  [the longest x4 3.75 us: gather_heads(): lax.ppermute(current, 'heads', [(i, i ^ bit) for i in range(head_total)])]
    while x2 -> x0, local copies, waits for them, and re-layouts: 4.55 us -> none  [shards(): result = lax.fori_loop(0, local_bricks * piece_bricks, visit, start_state)]
    convert_element_type x0 -> x8, local copies, waits for them, and re-layouts: none -> 3.5 us  [the longest x4 2.19 us: scatter_heads(): give.astype(jnp.bfloat16)]
  transfers between devices with their start and end apart: 7 -> 13, of which waited for: 5 -> 10; matrix products, arithmetic and copies ran while one was open for 5% -> 7% of each run, Pallas kernels for 0% -> 0%
where the time goes in v2:
time: 135 us; the launch traced here: 134 us
  waiting for transfers between devices  72.4 us (54%)
  starting transfers between devices  16 us (12%)
  other arithmetic  14.4 us (11%)
  matrix products  14.4 us (11%)
  local copies, waits for them, and re-layouts  13.1 us (10%)
  between operations  4.16 us (3%)
    ppermute x3, waiting for transfers between devices, shards(): block = lax.ppermute(block, 'bricks', ring)  41.2 us
    ppermute x4, waiting for transfers between devices, scatter_heads(): lax.ppermute(give.astype(jnp.bfloat16), 'heads', [(i, i ^ bit) for i in r...  17.6 us
    ppermute x4, waiting for transfers between devices, gather_heads(): lax.ppermute(current, 'heads', [(i, i ^ bit) for i in range(head_total)])  13.6 us
    ppermute x1, starting transfers between devices, extended_2(): before = lax.ppermute(last, axis, up)  5.56 us
    dot_general x1, matrix products, shards(): lowered = jnp.dot(hidden, down_weight, preferred_element_type=jnp.float32)  5.49 us
    dot_general x4, matrix products, absorb_block(): jnp.einsum('bhqk,khd->bqhd', weights.astype(jnp.bfloat16), value_rows, pr...  3.98 us
    ppermute x4, starting transfers between devices, gather_heads(): lax.ppermute(current, 'heads', [(i, i ^ bit) for i in range(head_total)])  3.75 us
    ppermute x4, starting transfers between devices, scatter_heads(): lax.ppermute(give.astype(jnp.bfloat16), 'heads', [(i, i ^ bit) for i in r...  3.57 us
  transfers between devices with their start and end apart: 13, of which 10 were waited for; matrix products, arithmetic and copies ran while one was open for 7% of the time, Pallas kernels for 0%

profile of v2, /device:TPU:0, one launch (start us, length us, event | category | flops | bytes accessed | tf_op | source)
XLA Modules:
  0.0 134.5 jit_solution(11454134670906255574)
XLA Ops:
  0.0 0.9 fusion.158
  0.9 1.3 collective-permute-start.1
  2.2 5.6 %collective-permute-start = (bf16[64,256]{1,0:T(8,128)(2,1)S(1)}, bf16[64,256]{1,0:T(8,128)(2,1)S(1)}, u32[]{:S(2)}, u32[]{:S(2)}) collective-permute-start(bf16[64,256]{1,0:T(8,128)(2,1)S(1)} %get-tuple-element.161), channel_id=1, source_target_pairs={{0,4},{4,8},{8,12},{1,5},{5,9},{9,13},{2,6},{6,10},{10,14},{3,7},{... | collective-permute-start | bytes 98312 | tf_op jit(solution)/shard_map/ppermute | solution.py:20
  7.8 1.0 fusion.159
  8.8 0.9 fusion.160
  9.7 1.1 copy.26
  10.8 1.4 %fusion.162 = (s32[1]{0:T(128)}, s32[1]{0:T(128)}) fusion(s32[4]{0:T(128)} %param.32, s32[]{:T(128)} %bitcast.2, s32[]{:T(128)} %bitcast.6), kind=kLoop, calls=%fused_computation.221 | loop fusion | bytes 24 | tf_op jit(solution)/shard_map/jit(_take)/gather | solution.py:146
  13.5 0.7 convert_element_type.140
  14.2 0.3 select_maximum_fusion
  14.5 1.7 %fusion.92 = f32[1,8,8,8,256]{4,3,2,1,0:T(8,128)S(1)} fusion(f32[1,10,10,10,256]{4,3,2,1,0:T(8,128)S(1)} %select_maximum_fusion, f32[1,1,8,8,256]{4,3,2,1,0:T(8,128)S(1)} %multiply_bitcast_fusion, f32[1,8,8,8,256]{4,3,2,1,0:T(8,128)S(1)} %bitcast.475, f32[1,1,8,8,256]{4,3,2,1,0:T(8,128)S(1)} %multiply_bitcast_fusion.1, f32[256]{0:T(256)S(1)} %bitcast.520, ...), kind=kLoop, calls=%fused_computation.94 | loop fusion | flops 7208960 | bytes 13790208 | tf_op jit(solution)/shard_map/add | solution.py:51
  16.2 0.2 copy.28
  16.5 2.0 %collective-permute-start.2 = (bf16[512,256]{0,1:T(8,128)(2,1)S(1)}, bf16[512,256]{0,1:T(8,128)(2,1)S(1)}, u32[]{:S(2)}, u32[]{:S(2)}) collective-permute-start(bf16[512,256]{0,1:T(8,128)(2,1)S(1)} %add_convert_fusion), channel_id=1, source_target_pairs={{0,2},{1,3},{2,0},{3,1},{4,6},{5,7},{6,4},{7,5},{8,10},{9,11},{10,... | collective-permute-start | bytes 786440 | tf_op jit(solution)/shard_map/ppermute | solution.py:86
  18.5 5.8 %collective-permute-done.2 = bf16[512,256]{0,1:T(8,128)(2,1)S(1)} collective-permute-done((bf16[512,256]{0,1:T(8,128)(2,1)S(1)}, bf16[512,256]{0,1:T(8,128)(2,1)S(1)}, u32[]{:S(2)}, u32[]{:S(2)}) %collective-permute-start.2) | collective-permute-done | bytes 262176 | tf_op jit(solution)/shard_map/ppermute | solution.py:86
  24.4 0.8 pad_maximum_fusion.2
  25.3 0.7 fusion.161
  28.4 1.2 copy.47
  29.7 1.1 select_bitcast_fusion.3
  30.8 0.2 fusion.125
  31.0 0.1 maximum_convert_fusion
  31.1 0.3 multiply_reduce_fusion.1
  31.5 0.2 copy.29
  31.7 0.3 fusion.29
  32.0 0.7 copy-done.7
  32.7 0.5 convolution_convert_fusion
  33.2 0.5 convolution_convert_fusion.2
  33.8 1.8 %collective-permute-start.4 = (bf16[512,512]{0,1:T(8,128)(2,1)S(1)}, bf16[512,512]{0,1:T(8,128)(2,1)S(1)}, u32[]{:S(2)}, u32[]{:S(2)}) collective-permute-start(bf16[512,512]{0,1:T(8,128)(2,1)S(1)} %pad_maximum_fusion.3), channel_id=1, source_target_pairs={{0,4},{4,8},{8,12},{12,0},{1,5},{5,9},{9,13},{13,1},{2,6},{6,10},{... | collective-permute-start | bytes 1572872 | tf_op jit(solution)/shard_map/ppermute | solution.py:181
  35.5 0.5 convolution_convert_fusion.1
  36.0 0.8 bitcast_reduce_fusion.3
  36.8 13.1 %collective-permute-done.4 = bf16[512,512]{0,1:T(8,128)(2,1)S(1)} collective-permute-done((bf16[512,512]{0,1:T(8,128)(2,1)S(1)}, bf16[512,512]{0,1:T(8,128)(2,1)S(1)}, u32[]{:S(2)}, u32[]{:S(2)}) %collective-permute-start.4) | collective-permute-done | bytes 524320 | tf_op jit(solution)/shard_map/ppermute | solution.py:181
  50.0 0.8 bitcast_reduce_fusion.2
  50.7 14.5 %collective-permute-done.5 = bf16[512,512]{0,1:T(8,128)(2,1)S(1)} collective-permute-done((bf16[512,512]{0,1:T(8,128)(2,1)S(1)}, bf16[512,512]{0,1:T(8,128)(2,1)S(1)}, u32[]{:S(2)}, u32[]{:S(2)}) %collective-permute-start.5) | collective-permute-done | bytes 524320 | tf_op jit(solution)/shard_map/ppermute | solution.py:181
  65.3 0.8 bitcast_reduce_fusion.1
  66.1 13.6 %collective-permute-done.6 = bf16[512,512]{0,1:T(8,128)(2,1)S(1)} collective-permute-done((bf16[512,512]{0,1:T(8,128)(2,1)S(1)}, bf16[512,512]{0,1:T(8,128)(2,1)S(1)}, u32[]{:S(2)}, u32[]{:S(2)}) %collective-permute-start.6) | collective-permute-done | bytes 524320 | tf_op jit(solution)/shard_map/ppermute | solution.py:181
  79.7 0.8 bitcast_reduce_fusion
  80.5 1.7 %fusion.4 = (f32[4,512]{1,0:T(4,128)S(1)}, f32[4,512]{1,0:T(4,128)S(1)}) fusion(f32[4,512,512]{2,1,0:T(8,128)S(1)} %get-tuple-element.209, f32[4,512]{1,0:T(4,128)S(1)} %get-tuple-element.195, pred[]{:T(512)} %bitcast.39, f32[4,512]{1,0:T(4,128)S(1)} %get-tuple-element.146, f32[4,512,512]{2,1,0:T(8,128)S(1)} %get-tuple-element.207, pred[]{:T(512)} %bitcast.59), kind=kLoop, calls=%fused_computation.16 | loop fusion | flops 8384512 | bytes 8421378 | tf_op jit(solution)/shard_map/reduce_sum | solution.py:106
  82.2 1.7 %fusion.8 = (f32[4,512]{1,0:T(4,128)S(1)}, f32[4,512]{1,0:T(4,128)S(1)}) fusion(f32[4,512,512]{2,1,0:T(8,128)S(1)} %get-tuple-element.205, f32[4,512]{1,0:T(4,128)S(1)} %get-tuple-element.145, pred[]{:T(512)} %bitcast.73, f32[4,512]{1,0:T(4,128)S(1)} %get-tuple-element.144, f32[4,512,512]{2,1,0:T(8,128)S(1)} %get-tuple-element.203, pred[]{:T(512)} %bitcast.87), kind=kLoop, calls=%fused_computation.20 | loop fusion | flops 8384512 | bytes 8421378 | tf_op jit(solution)/shard_map/reduce_sum | solution.py:106
  83.9 1.0 fusion.75
  84.9 1.0 fusion.72
  85.9 1.0 fusion.69
  86.9 1.0 fusion.87
  87.9 0.4 fusion.165
  88.3 1.3 copy-done.1
  89.8 2.0 %collective-permute-done.7 = bf16[512,2,256]{0,2,1:T(8,128)(2,1)} collective-permute-done((bf16[512,2,256]{0,2,1:T(8,128)(2,1)S(1)}, bf16[512,2,256]{0,2,1:T(8,128)(2,1)}, u32[]{:S(2)}, u32[]{:S(2)}) %collective-permute-start.7) | collective-permute-done | bytes 524320 | tf_op jit(solution)/shard_map/ppermute | solution.py:72
  91.9 1.6 %bitcast_add_fusion.1 = f32[512,2,256]{0,2,1:T(8,128)S(1)} fusion(bf16[512,2,256]{0,2,1:T(8,128)(2,1)} %collective-permute-done.7, f32[512,2,2,256]{0,3,2,1:T(8,128)} %copy-done.1, s32[]{:T(128)S(6)} %select_n.199), kind=kLoop, calls=%fused_computation.83 | loop fusion | flops 524288 | bytes 2621444 | tf_op jit(solution)/shard_map/add | solution.py:75
  93.4 0.7 fusion.126
  94.2 1.6 %collective-permute-start.8 = (bf16[512,256]{0,1:T(8,128)(2,1)}, bf16[512,256]{0,1:T(8,128)(2,1)}, u32[]{:S(2)}, u32[]{:S(2)}) collective-permute-start(bf16[512,256]{0,1:T(8,128)(2,1)} %fusion.126), channel_id=1, source_target_pairs={{0,2},{1,3},{2,0},{3,1},{4,6},{5,7},{6,4},{7,5},{8,10},{9,11},{10,... | collective-permute-start | bytes 786440 | tf_op jit(solution)/shard_map/ppermute | solution.py:72
  95.8 7.0 %collective-permute-done.8 = bf16[512,256]{0,1:T(8,128)(2,1)} collective-permute-done((bf16[512,256]{0,1:T(8,128)(2,1)}, bf16[512,256]{0,1:T(8,128)(2,1)}, u32[]{:S(2)}, u32[]{:S(2)}) %collective-permute-start.8) | collective-permute-done | bytes 262176 | tf_op jit(solution)/shard_map/ppermute | solution.py:72
  102.8 1.1 fusion.123
  103.9 1.7 %collective-permute-start.9 = (bf16[512,256]{0,1:T(8,128)(2,1)S(1)}, bf16[512,256]{0,1:T(8,128)(2,1)S(1)}, u32[]{:S(2)}, u32[]{:S(2)}) collective-permute-start(bf16[512,256]{0,1:T(8,128)(2,1)S(1)} %fusion.123), channel_id=1, source_target_pairs={{0,2},{1,3},{2,0},{3,1},{4,6},{5,7},{6,4},{7,5},{8,10},{9,11},{10,... | collective-permute-start | bytes 786440 | tf_op jit(solution)/shard_map/ppermute | solution.py:86
  105.6 5.9 %collective-permute-done.9 = bf16[512,256]{0,1:T(8,128)(2,1)S(1)} collective-permute-done((bf16[512,256]{0,1:T(8,128)(2,1)S(1)}, bf16[512,256]{0,1:T(8,128)(2,1)S(1)}, u32[]{:S(2)}, u32[]{:S(2)}) %collective-permute-start.9) | collective-permute-done | bytes 262176 | tf_op jit(solution)/shard_map/ppermute | solution.py:86
  111.7 1.9 %collective-permute-done.10 = bf16[512,2,256]{0,2,1:T(8,128)(2,1)S(1)} collective-permute-done((bf16[512,2,256]{0,2,1:T(8,128)(2,1)S(1)}, bf16[512,2,256]{0,2,1:T(8,128)(2,1)S(1)}, u32[]{:S(2)}, u32[]{:S(2)}) %collective-permute-start.10) | collective-permute-done | bytes 524320 | tf_op jit(solution)/shard_map/ppermute | solution.py:86
  113.7 0.2 fusion.124
  113.9 0.1 maximum_convert_fusion.1
  114.0 0.3 multiply_reduce_fusion
  114.4 0.2 copy.36
  114.5 0.3 fusion.26
  114.8 5.5 %fusion.78 = f32[512,1024]{0,1:T(8,128)} fusion(bf16[1024,1024]{1,0:T(8,128)(2,1)S(1)} %copy-done, bf16[512,1024]{0,1:T(8,128)(2,1)S(1)} %fusion.26, bf16[1024,1024]{1,0:T(8,128)(2,1)} %param.42), kind=kOutput, calls=%fused_computation.78 | convolution fusion | flops 2152202240 | bytes 7340032 | tf_op jit(solution)/shard_map/dot_general | solution.py:197
  120.3 1.3 fusion.91
  121.7 0.2 collective-permute-start.11
  121.9 1.8 %collective-permute-done.11 = bf16[512,2,256]{0,2,1:T(8,128)(2,1)S(1)} collective-permute-done((bf16[512,2,256]{0,2,1:T(8,128)(2,1)S(1)}, bf16[512,2,256]{0,2,1:T(8,128)(2,1)S(1)}, u32[]{:S(2)}, u32[]{:S(2)}) %collective-permute-start.11) | collective-permute-done | bytes 524320 | tf_op jit(solution)/shard_map/ppermute | solution.py:72
  123.6 1.4 %bitcast_add_fusion = f32[512,2,256]{0,2,1:T(8,128)S(1)} fusion(bf16[512,2,256]{0,2,1:T(8,128)(2,1)S(1)} %collective-permute-done.11, f32[512,2,2,256]{0,3,2,1:T(8,128)} %bitcast.483, s32[]{:T(128)S(6)} %select_n.199), kind=kLoop, calls=%fused_computation.82 | loop fusion | flops 524288 | bytes 2621444 | tf_op jit(solution)/shard_map/add | solution.py:75
  125.1 1.7 %collective-permute-start.12 = (bf16[512,256]{0,1:T(8,128)(2,1)S(1)}, bf16[512,256]{0,1:T(8,128)(2,1)S(1)}, u32[]{:S(2)}, u32[]{:S(2)}) collective-permute-start(bf16[512,256]{0,1:T(8,128)(2,1)S(1)} %fusion.127), channel_id=1, source_target_pairs={{0,2},{1,3},{2,0},{3,1},{4,6},{5,7},{6,4},{7,5},{8,10},{9,11},{10,... | collective-permute-start | bytes 786440 | tf_op jit(solution)/shard_map/ppermute | solution.py:72
  126.8 6.7 %collective-permute-done.12 = bf16[512,256]{0,1:T(8,128)(2,1)S(1)} collective-permute-done((bf16[512,256]{0,1:T(8,128)(2,1)S(1)}, bf16[512,256]{0,1:T(8,128)(2,1)S(1)}, u32[]{:S(2)}, u32[]{:S(2)}) %collective-permute-start.12) | collective-permute-done | bytes 262176 | tf_op jit(solution)/shard_map/ppermute | solution.py:72
  133.6 0.8 copy.39
  (49 shorter events, 1.1 us)
Async XLA Ops:
  0.0 114.8 %copy-start = (bf16[1024,1024]{1,0:T(8,128)(2,1)S(1)}, bf16[1024,1024]{1,0:T(8,128)(2,1)}, u32[]{:S(2)}) copy-start(bf16[1024,1024]{1,0:T(8,128)(2,1)} %param.43) | copy-start | bytes 6291460
  0.9 13.2 %collective-permute-start.1 = (bf16[64,256]{1,0:T(8,128)(2,1)S(1)}, bf16[64,256]{1,0:T(8,128)(2,1)S(1)}, u32[]{:S(2)}, u32[]{:S(2)}) collective-permute-start(bf16[64,256]{1,0:T(8,128)(2,1)S(1)} %get-tuple-element.162), channel_id=1, source_target_pairs={{4,0},{8,4},{12,8},{5,1},{9,5},{13,9},{6,2},{10,6},{14,10},{7,3},{... | collective-permute-start | bytes 98312 | tf_op jit(solution)/shard_map/ppermute | solution.py:21
  2.2 12.0 %collective-permute-start = (bf16[64,256]{1,0:T(8,128)(2,1)S(1)}, bf16[64,256]{1,0:T(8,128)(2,1)S(1)}, u32[]{:S(2)}, u32[]{:S(2)}) collective-permute-start(bf16[64,256]{1,0:T(8,128)(2,1)S(1)} %get-tuple-element.161), channel_id=1, source_target_pairs={{0,4},{4,8},{8,12},{1,5},{5,9},{9,13},{2,6},{6,10},{10,14},{3,7},{... | collective-permute-start | bytes 98312 | tf_op jit(solution)/shard_map/ppermute | solution.py:20
  16.1 9.1 %copy-start.4 = (bf16[1024]{0:T(1024)(128)(2,1)S(1)}, bf16[1024]{0:T(1024)(128)(2,1)}, u32[]{:S(2)}) copy-start(bf16[1024]{0:T(1024)(128)(2,1)} %param.36) | copy-start | bytes 6148
  16.2 9.1 %copy-start.6 = (s32[4,4]{1,0:T(4,128)S(1)}, s32[4,4]{1,0:T(4,128)}, u32[]{:S(2)}) copy-start(s32[4,4]{1,0:T(4,128)} %param.33) | copy-start | bytes 196
  16.5 7.8 %collective-permute-start.2 = (bf16[512,256]{0,1:T(8,128)(2,1)S(1)}, bf16[512,256]{0,1:T(8,128)(2,1)S(1)}, u32[]{:S(2)}, u32[]{:S(2)}) collective-permute-start(bf16[512,256]{0,1:T(8,128)(2,1)S(1)} %add_convert_fusion), channel_id=1, source_target_pairs={{0,2},{1,3},{2,0},{3,1},{4,6},{5,7},{6,4},{7,5},{8,10},{9,11},{10,... | collective-permute-start | bytes 786440 | tf_op jit(solution)/shard_map/ppermute | solution.py:86
  25.2 4.4 %collective-permute-start.3 = (bf16[512,2,256]{0,2,1:T(8,128)(2,1)}, bf16[512,2,256]{0,2,1:T(8,128)(2,1)}, u32[]{:S(2)}, u32[]{:S(2)}) collective-permute-start(bf16[512,2,256]{0,2,1:T(8,128)(2,1)} %pad_maximum_fusion.2), channel_id=1, source_target_pairs={{0,1},{1,0},{2,3},{3,2},{4,5},{5,4},{6,7},{7,6},{8,9},{9,8},{10,11... | collective-permute-start | bytes 1572872 | tf_op jit(solution)/shard_map/ppermute | solution.py:86
  31.7 1.0 copy-start.7
  31.7 1.5 %copy-start.8 = (bf16[1024,256]{1,0:T(8,128)(2,1)S(1)}, bf16[1024,256]{1,0:T(8,128)(2,1)}, u32[]{:S(2)}) copy-start(bf16[1024,256]{1,0:T(8,128)(2,1)} %param.38) | copy-start | bytes 1572868
  32.7 2.8 %copy-start.9 = (bf16[1024,256]{1,0:T(8,128)(2,1)S(1)}, bf16[1024,256]{1,0:T(8,128)(2,1)}, u32[]{:S(2)}) copy-start(bf16[1024,256]{1,0:T(8,128)(2,1)} %param.37) | copy-start | bytes 1572868
  33.8 16.2 %collective-permute-start.4 = (bf16[512,512]{0,1:T(8,128)(2,1)S(1)}, bf16[512,512]{0,1:T(8,128)(2,1)S(1)}, u32[]{:S(2)}, u32[]{:S(2)}) collective-permute-start(bf16[512,512]{0,1:T(8,128)(2,1)S(1)} %pad_maximum_fusion.3), channel_id=1, source_target_pairs={{0,4},{4,8},{8,12},{12,0},{1,5},{5,9},{9,13},{13,1},{2,6},{6,10},{... | collective-permute-start | bytes 1572872 | tf_op jit(solution)/shard_map/ppermute | solution.py:181
  49.9 15.3 %collective-permute-start.5 = (bf16[512,512]{0,1:T(8,128)(2,1)S(1)}, bf16[512,512]{0,1:T(8,128)(2,1)S(1)}, u32[]{:S(2)}, u32[]{:S(2)}) collective-permute-start(bf16[512,512]{0,1:T(8,128)(2,1)S(1)} %collective-permute-done.4), channel_id=1, source_target_pairs={{0,4},{4,8},{8,12},{12,0},{1,5},{5,9},{9,13},{13,1},{2,6},{6,10},{... | collective-permute-start | bytes 1572872 | tf_op jit(solution)/shard_map/ppermute | solution.py:181
  65.2 14.4 %collective-permute-start.6 = (bf16[512,512]{0,1:T(8,128)(2,1)S(1)}, bf16[512,512]{0,1:T(8,128)(2,1)S(1)}, u32[]{:S(2)}, u32[]{:S(2)}) collective-permute-start(bf16[512,512]{0,1:T(8,128)(2,1)S(1)} %collective-permute-done.5), channel_id=1, source_target_pairs={{0,4},{4,8},{8,12},{12,0},{1,5},{5,9},{9,13},{13,1},{2,6},{6,10},{... | collective-permute-start | bytes 1572872 | tf_op jit(solution)/shard_map/ppermute | solution.py:181
  88.3 1.3 %copy-start.1 = (f32[512,2,2,256]{0,3,2,1:T(8,128)}, f32[512,2,2,256]{0,3,2,1:T(8,128)S(1)}, u32[]{:S(2)}) copy-start(f32[512,2,2,256]{0,3,2,1:T(8,128)S(1)} %fusion.165) | copy-start | bytes 6291460
  89.7 2.1 %collective-permute-start.7 = (bf16[512,2,256]{0,2,1:T(8,128)(2,1)S(1)}, bf16[512,2,256]{0,2,1:T(8,128)(2,1)}, u32[]{:S(2)}, u32[]{:S(2)}) collective-permute-start(bf16[512,2,256]{0,2,1:T(8,128)(2,1)S(1)} %fusion.90), channel_id=1, source_target_pairs={{0,1},{1,0},{2,3},{3,2},{4,5},{5,4},{6,7},{7,6},{8,9},{9,8},{10,11... | collective-permute-start | bytes 1572872 | tf_op jit(solution)/shard_map/ppermute | solution.py:72
  93.4 18.3 %copy-start.5 = (bf16[1024]{0:T(1024)(128)(2,1)S(1)}, bf16[1024]{0:T(1024)(128)(2,1)}, u32[]{:S(2)}) copy-start(bf16[1024]{0:T(1024)(128)(2,1)} %param.41) | copy-start | bytes 6148
  94.2 8.7 %collective-permute-start.8 = (bf16[512,256]{0,1:T(8,128)(2,1)}, bf16[512,256]{0,1:T(8,128)(2,1)}, u32[]{:S(2)}, u32[]{:S(2)}) collective-permute-start(bf16[512,256]{0,1:T(8,128)(2,1)} %fusion.126), channel_id=1, source_target_pairs={{0,2},{1,3},{2,0},{3,1},{4,6},{5,7},{6,4},{7,5},{8,10},{9,11},{10,... | collective-permute-start | bytes 786440 | tf_op jit(solution)/shard_map/ppermute | solution.py:72
  103.9 7.8 %copy-start.2 = (bf16[512,256]{0,1:T(8,128)(2,1)}, bf16[512,256]{0,1:T(8,128)(2,1)S(1)}, u32[]{:S(2)}) copy-start(bf16[512,256]{0,1:T(8,128)(2,1)S(1)} %fusion.123) | copy-start | bytes 786436
  103.9 7.6 %collective-permute-start.9 = (bf16[512,256]{0,1:T(8,128)(2,1)S(1)}, bf16[512,256]{0,1:T(8,128)(2,1)S(1)}, u32[]{:S(2)}, u32[]{:S(2)}) collective-permute-start(bf16[512,256]{0,1:T(8,128)(2,1)S(1)} %fusion.123), channel_id=1, source_target_pairs={{0,2},{1,3},{2,0},{3,1},{4,6},{5,7},{6,4},{7,5},{8,10},{9,11},{10,... | collective-permute-start | bytes 786440 | tf_op jit(solution)/shard_map/ppermute | solution.py:86
  111.6 2.0 %collective-permute-start.10 = (bf16[512,2,256]{0,2,1:T(8,128)(2,1)S(1)}, bf16[512,2,256]{0,2,1:T(8,128)(2,1)S(1)}, u32[]{:S(2)}, u32[]{:S(2)}) collective-permute-start(bf16[512,2,256]{0,2,1:T(8,128)(2,1)S(1)} %pad_maximum_fusion.4), channel_id=1, source_target_pairs={{0,1},{1,0},{2,3},{3,2},{4,5},{5,4},{6,7},{7,6},{8,9},{9,8},{10,11... | collective-permute-start | bytes 1572872 | tf_op jit(solution)/shard_map/ppermute | solution.py:86
  120.3 13.2 %copy-start.3 = (bf16[512,256]{0,1:T(8,128)(2,1)S(1)}, bf16[512,256]{0,1:T(8,128)(2,1)}, u32[]{:S(2)}) copy-start(bf16[512,256]{0,1:T(8,128)(2,1)} %copy-done.2) | copy-start | bytes 786436
  121.7 2.0 %collective-permute-start.11 = (bf16[512,2,256]{0,2,1:T(8,128)(2,1)S(1)}, bf16[512,2,256]{0,2,1:T(8,128)(2,1)S(1)}, u32[]{:S(2)}, u32[]{:S(2)}) collective-permute-start(bf16[512,2,256]{0,2,1:T(8,128)(2,1)S(1)} %fusion.91), channel_id=1, source_target_pairs={{0,1},{1,0},{2,3},{3,2},{4,5},{5,4},{6,7},{7,6},{8,9},{9,8},{10,11... | collective-permute-start | bytes 1572872 | tf_op jit(solution)/shard_map/ppermute | solution.py:72
  125.1 8.4 %collective-permute-start.12 = (bf16[512,256]{0,1:T(8,128)(2,1)S(1)}, bf16[512,256]{0,1:T(8,128)(2,1)S(1)}, u32[]{:S(2)}, u32[]{:S(2)}) collective-permute-start(bf16[512,256]{0,1:T(8,128)(2,1)S(1)} %fusion.127), channel_id=1, source_target_pairs={{0,2},{1,3},{2,0},{3,1},{4,6},{5,7},{6,4},{7,5},{8,10},{9,11},{10,... | collective-permute-start | bytes 786440 | tf_op jit(solution)/shard_map/ppermute | solution.py:72

commit v3 on v2

--- a/solution.py
+++ b/solution.py
@@ -177,12 +177,14 @@
     ring = [(i, (i + 1) % dev_total) for i in range(dev_total)]
     block = pair_local
     for step in range(dev_total):
-        if step > 0:
-            block = lax.ppermute(block, "bricks", ring)
+        if step + 1 < dev_total:
+            arriving = lax.ppermute(block, "bricks", ring)
         source = (brick_dev - step) % dev_total
         key_ids = source * local_bricks + jnp.arange(local_bricks, dtype=jnp.int32)
         linked = jnp.take(linked_rows, key_ids, axis=1) > 0
         state = absorb_block(state, query_heads, block, linked, head_count, brick_rows, local_width)
+        if step + 1 < dev_total:
+            state, block = lax.optimization_barrier((state, arriving))
     row_max, row_mass, weighted = state
     attended = (weighted / jnp.transpose(row_mass, (0, 2, 1))[:, :, :, None]).astype(jnp.bfloat16)
     attended = attended.reshape(row_count, local_width)

time: 135 us -> 131 us (0.970)
  waiting for transfers between devices: 72.4 us -> 67.9 us
    ppermute x3, waiting for transfers between devices: 41.2 us -> 36.8 us  [shards(): arriving = lax.ppermute(block, 'bricks', ring)]
    reduce_sum x2 -> x4, other arithmetic: 3.34 us -> 3.36 us  [absorb_block(): mass_new = row_mass * factor + jnp.sum(weights, axis=-1)]
  transfers between devices with their start and end apart: 13 -> 13, of which waited for: 10 -> 10; matrix products, arithmetic and copies ran while one was open for 7% -> 11% of each run, Pallas kernels for 0% -> 0%
where the time goes in v3:
time: 131 us; the launch traced here: 130 us
  waiting for transfers between devices  67.9 us (52%)
  starting transfers between devices  16.3 us (12%)
  other arithmetic  14.7 us (11%)
  matrix products  14.4 us (11%)
  local copies, waits for them, and re-layouts  12.6 us (10%)
  between operations  4.46 us (3%)
    ppermute x3, waiting for transfers between devices, shards(): arriving = lax.ppermute(block, 'bricks', ring)  36.8 us
    ppermute x4, waiting for transfers between devices, scatter_heads(): lax.ppermute(give.astype(jnp.bfloat16), 'heads', [(i, i ^ bit) for i in r...  17.5 us
    ppermute x4, waiting for transfers between devices, gather_heads(): lax.ppermute(current, 'heads', [(i, i ^ bit) for i in range(head_total)])  13.6 us
    ppermute x1, starting transfers between devices, extended_2(): before = lax.ppermute(last, axis, up)  5.56 us
    dot_general x1, matrix products, shards(): lowered = jnp.dot(hidden, down_weight, preferred_element_type=jnp.float32)  5.49 us
    dot_general x4, matrix products, absorb_block(): jnp.einsum('bhqk,khd->bqhd', weights.astype(jnp.bfloat16), value_rows, pr...  3.95 us
    ppermute x4, starting transfers between devices, gather_heads(): lax.ppermute(current, 'heads', [(i, i ^ bit) for i in range(head_total)])  3.78 us
    ppermute x4, starting transfers between devices, scatter_heads(): lax.ppermute(give.astype(jnp.bfloat16), 'heads', [(i, i ^ bit) for i in r...  3.64 us
  transfers between devices with their start and end apart: 13, of which 10 were waited for; matrix products, arithmetic and copies ran while one was open for 11% of the time, Pallas kernels for 0%

profile of v3, /device:TPU:0, one launch (start us, length us, event | category | flops | bytes accessed | tf_op | source)
XLA Modules:
  0.0 130.4 jit_solution(4365535214535680547)
XLA Ops:
  0.0 0.9 fusion.128
  0.9 1.3 collective-permute-start.1
  2.2 5.6 %collective-permute-start = (bf16[64,256]{1,0:T(8,128)(2,1)S(1)}, bf16[64,256]{1,0:T(8,128)(2,1)S(1)}, u32[]{:S(2)}, u32[]{:S(2)}) collective-permute-start(bf16[64,256]{1,0:T(8,128)(2,1)S(1)} %get-tuple-element.186), channel_id=1, source_target_pairs={{0,4},{4,8},{8,12},{1,5},{5,9},{9,13},{2,6},{6,10},{10,14},{3,7},{... | collective-permute-start | bytes 98312 | tf_op jit(solution)/shard_map/ppermute | solution.py:20
  7.8 1.0 fusion.129
  8.8 0.9 fusion.130
  9.7 1.1 copy.26
  10.8 1.4 %fusion.132 = (s32[1]{0:T(128)}, s32[1]{0:T(128)}) fusion(s32[4]{0:T(128)} %param.32, s32[]{:T(128)} %bitcast.2, s32[]{:T(128)} %bitcast.6), kind=kLoop, calls=%fused_computation.210 | loop fusion | bytes 24 | tf_op jit(solution)/shard_map/jit(_take)/gather | solution.py:146
  13.7 0.7 convert_element_type.140
  14.4 0.3 select_maximum_fusion
  14.6 1.7 %fusion.68 = f32[1,8,8,8,256]{4,3,2,1,0:T(8,128)S(1)} fusion(f32[1,10,10,10,256]{4,3,2,1,0:T(8,128)S(1)} %select_maximum_fusion, f32[1,1,8,8,256]{4,3,2,1,0:T(8,128)S(1)} %multiply_bitcast_fusion, f32[1,8,8,8,256]{4,3,2,1,0:T(8,128)S(1)} %bitcast.375, f32[1,1,8,8,256]{4,3,2,1,0:T(8,128)S(1)} %multiply_bitcast_fusion.1, f32[256]{0:T(256)S(1)} %bitcast.424, ...), kind=kLoop, calls=%fused_computation.86 | loop fusion | flops 7208960 | bytes 13790208 | tf_op jit(solution)/shard_map/add | solution.py:51
  16.3 0.2 copy.28
  16.7 2.0 %collective-permute-start.2 = (bf16[512,256]{0,1:T(8,128)(2,1)S(1)}, bf16[512,256]{0,1:T(8,128)(2,1)S(1)}, u32[]{:S(2)}, u32[]{:S(2)}) collective-permute-start(bf16[512,256]{0,1:T(8,128)(2,1)S(1)} %add_convert_fusion), channel_id=1, source_target_pairs={{0,2},{1,3},{2,0},{3,1},{4,6},{5,7},{6,4},{7,5},{8,10},{9,11},{10,... | collective-permute-start | bytes 786440 | tf_op jit(solution)/shard_map/ppermute | solution.py:86
  18.7 5.8 %collective-permute-done.2 = bf16[512,256]{0,1:T(8,128)(2,1)S(1)} collective-permute-done((bf16[512,256]{0,1:T(8,128)(2,1)S(1)}, bf16[512,256]{0,1:T(8,128)(2,1)S(1)}, u32[]{:S(2)}, u32[]{:S(2)}) %collective-permute-start.2) | collective-permute-done | bytes 262176 | tf_op jit(solution)/shard_map/ppermute | solution.py:86
  24.5 0.9 pad_maximum_fusion.2
  25.4 0.7 fusion.131
  28.7 1.2 copy.47
  30.0 1.1 select_bitcast_fusion.3
  31.2 0.2 fusion.101
  31.4 0.2 copy.29
  31.6 0.3 multiply_reduce_fusion.1
  32.0 0.3 fusion.29
  32.3 0.2 copy-done.7
  32.5 0.5 convolution_convert_fusion.2
  33.0 0.5 convolution_convert_fusion.1
  33.5 0.8 bitcast_reduce_fusion.3
  34.3 0.5 convolution_convert_fusion
  34.8 1.8 %collective-permute-start.4 = (bf16[512,512]{0,1:T(8,128)(2,1)S(1)}, bf16[512,512]{0,1:T(8,128)(2,1)S(1)}, u32[]{:S(2)}, u32[]{:S(2)}) collective-permute-start(bf16[512,512]{0,1:T(8,128)(2,1)S(1)} %pad_maximum_fusion.3), channel_id=1, source_target_pairs={{0,4},{4,8},{8,12},{12,0},{1,5},{5,9},{9,13},{13,1},{2,6},{6,10},{... | collective-permute-start | bytes 1572872 | tf_op jit(solution)/shard_map/ppermute | solution.py:181
  36.6 0.8 fusion.5
  37.5 1.0 fusion.57
  38.4 12.5 %collective-permute-done.4 = bf16[512,512]{0,1:T(8,128)(2,1)S(1)} collective-permute-done((bf16[512,512]{0,1:T(8,128)(2,1)S(1)}, bf16[512,512]{0,1:T(8,128)(2,1)S(1)}, u32[]{:S(2)}, u32[]{:S(2)}) %collective-permute-start.4) | collective-permute-done | bytes 524320 | tf_op jit(solution)/shard_map/ppermute | solution.py:181
  51.1 0.8 bitcast_reduce_fusion.2
  51.9 0.8 fusion.7
  52.7 1.0 fusion.51
  53.8 12.6 %collective-permute-done.5 = bf16[512,512]{0,1:T(8,128)(2,1)S(1)} collective-permute-done((bf16[512,512]{0,1:T(8,128)(2,1)S(1)}, bf16[512,512]{0,1:T(8,128)(2,1)S(1)}, u32[]{:S(2)}, u32[]{:S(2)}) %collective-permute-start.5) | collective-permute-done | bytes 524320 | tf_op jit(solution)/shard_map/ppermute | solution.py:181
  66.4 0.2 collective-permute-start.6
  66.7 0.8 bitcast_reduce_fusion.1
  67.5 0.8 fusion.9
  68.3 1.0 fusion.48
  69.4 11.7 %collective-permute-done.6 = bf16[512,512]{0,1:T(8,128)(2,1)S(1)} collective-permute-done((bf16[512,512]{0,1:T(8,128)(2,1)S(1)}, bf16[512,512]{0,1:T(8,128)(2,1)S(1)}, u32[]{:S(2)}, u32[]{:S(2)}) %collective-permute-start.6) | collective-permute-done | bytes 524320 | tf_op jit(solution)/shard_map/ppermute | solution.py:181
  81.2 0.8 bitcast_reduce_fusion
  82.0 0.8 fusion.10
  82.8 1.0 divide_convert_fusion
  83.8 0.4 fusion.135
  84.3 1.3 %copy-done.1 = f32[512,2,2,256]{0,3,2,1:T(8,128)} copy-done((f32[512,2,2,256]{0,3,2,1:T(8,128)}, f32[512,2,2,256]{0,3,2,1:T(8,128)S(1)}, u32[]{:S(2)}) %copy-start.1) | copy-done | bytes 2097176
  85.8 2.0 %collective-permute-done.7 = bf16[512,2,256]{0,2,1:T(8,128)(2,1)} collective-permute-done((bf16[512,2,256]{0,2,1:T(8,128)(2,1)S(1)}, bf16[512,2,256]{0,2,1:T(8,128)(2,1)}, u32[]{:S(2)}, u32[]{:S(2)}) %collective-permute-start.7) | collective-permute-done | bytes 524320 | tf_op jit(solution)/shard_map/ppermute | solution.py:72
  87.8 1.6 %bitcast_add_fusion.1 = f32[512,2,256]{0,2,1:T(8,128)S(1)} fusion(bf16[512,2,256]{0,2,1:T(8,128)(2,1)} %collective-permute-done.7, f32[512,2,2,256]{0,3,2,1:T(8,128)} %copy-done.1, s32[]{:T(128)S(6)} %select_n.199), kind=kLoop, calls=%fused_computation.77 | loop fusion | flops 524288 | bytes 2621444 | tf_op jit(solution)/shard_map/add | solution.py:75
  89.4 0.7 fusion.102
  90.1 1.6 %collective-permute-start.8 = (bf16[512,256]{0,1:T(8,128)(2,1)}, bf16[512,256]{0,1:T(8,128)(2,1)}, u32[]{:S(2)}, u32[]{:S(2)}) collective-permute-start(bf16[512,256]{0,1:T(8,128)(2,1)} %fusion.102), channel_id=1, source_target_pairs={{0,2},{1,3},{2,0},{3,1},{4,6},{5,7},{6,4},{7,5},{8,10},{9,11},{10,... | collective-permute-start | bytes 786440 | tf_op jit(solution)/shard_map/ppermute | solution.py:72
  91.8 7.0 %collective-permute-done.8 = bf16[512,256]{0,1:T(8,128)(2,1)} collective-permute-done((bf16[512,256]{0,1:T(8,128)(2,1)}, bf16[512,256]{0,1:T(8,128)(2,1)}, u32[]{:S(2)}, u32[]{:S(2)}) %collective-permute-start.8) | collective-permute-done | bytes 262176 | tf_op jit(solution)/shard_map/ppermute | solution.py:72
  98.8 1.1 fusion.99
  99.9 1.7 %collective-permute-start.9 = (bf16[512,256]{0,1:T(8,128)(2,1)S(1)}, bf16[512,256]{0,1:T(8,128)(2,1)S(1)}, u32[]{:S(2)}, u32[]{:S(2)}) collective-permute-start(bf16[512,256]{0,1:T(8,128)(2,1)S(1)} %fusion.99), channel_id=1, source_target_pairs={{0,2},{1,3},{2,0},{3,1},{4,6},{5,7},{6,4},{7,5},{8,10},{9,11},{10,... | collective-permute-start | bytes 786440 | tf_op jit(solution)/shard_map/ppermute | solution.py:86
  101.6 5.9 %collective-permute-done.9 = bf16[512,256]{0,1:T(8,128)(2,1)S(1)} collective-permute-done((bf16[512,256]{0,1:T(8,128)(2,1)S(1)}, bf16[512,256]{0,1:T(8,128)(2,1)S(1)}, u32[]{:S(2)}, u32[]{:S(2)}) %collective-permute-start.9) | collective-permute-done | bytes 262176 | tf_op jit(solution)/shard_map/ppermute | solution.py:86
  107.7 1.9 %collective-permute-done.10 = bf16[512,2,256]{0,2,1:T(8,128)(2,1)S(1)} collective-permute-done((bf16[512,2,256]{0,2,1:T(8,128)(2,1)S(1)}, bf16[512,2,256]{0,2,1:T(8,128)(2,1)S(1)}, u32[]{:S(2)}, u32[]{:S(2)}) %collective-permute-start.10) | collective-permute-done | bytes 524320 | tf_op jit(solution)/shard_map/ppermute | solution.py:86
  109.7 0.2 fusion.100
  110.1 0.3 multiply_reduce_fusion
  110.5 0.3 fusion.26
  110.8 5.5 %fusion.60 = f32[512,1024]{0,1:T(8,128)} fusion(bf16[1024,1024]{1,0:T(8,128)(2,1)S(1)} %copy-done, bf16[512,1024]{0,1:T(8,128)(2,1)S(1)} %fusion.26, bf16[1024,1024]{1,0:T(8,128)(2,1)} %param.42), kind=kOutput, calls=%fused_computation.72 | convolution fusion | flops 2152202240 | bytes 7340032 | tf_op jit(solution)/shard_map/dot_general | solution.py:199
  116.3 1.3 %fusion.67 = bf16[512,2,256]{0,2,1:T(8,128)(2,1)S(1)} fusion(f32[512,2,2,256]{0,3,2,1:T(8,128)} %bitcast.382, s32[]{:T(128)S(6)} %select_n.200), kind=kLoop, calls=%fused_computation.84 | loop fusion | bytes 1048580 | tf_op jit(solution)/shard_map/convert_element_type | solution.py:73
  117.6 0.2 collective-permute-start.11
  117.8 1.8 %collective-permute-done.11 = bf16[512,2,256]{0,2,1:T(8,128)(2,1)S(1)} collective-permute-done((bf16[512,2,256]{0,2,1:T(8,128)(2,1)S(1)}, bf16[512,2,256]{0,2,1:T(8,128)(2,1)S(1)}, u32[]{:S(2)}, u32[]{:S(2)}) %collective-permute-start.11) | collective-permute-done | bytes 524320 | tf_op jit(solution)/shard_map/ppermute | solution.py:72
  119.6 1.4 %bitcast_add_fusion = f32[512,2,256]{0,2,1:T(8,128)S(1)} fusion(bf16[512,2,256]{0,2,1:T(8,128)(2,1)S(1)} %collective-permute-done.11, f32[512,2,2,256]{0,3,2,1:T(8,128)} %bitcast.383, s32[]{:T(128)S(6)} %select_n.199), kind=kLoop, calls=%fused_computation.76 | loop fusion | flops 524288 | bytes 2621444 | tf_op jit(solution)/shard_map/add | solution.py:75
  121.1 1.7 %collective-permute-start.12 = (bf16[512,256]{0,1:T(8,128)(2,1)S(1)}, bf16[512,256]{0,1:T(8,128)(2,1)S(1)}, u32[]{:S(2)}, u32[]{:S(2)}) collective-permute-start(bf16[512,256]{0,1:T(8,128)(2,1)S(1)} %fusion.103), channel_id=1, source_target_pairs={{0,2},{1,3},{2,0},{3,1},{4,6},{5,7},{6,4},{7,5},{8,10},{9,11},{10,... | collective-permute-start | bytes 786440 | tf_op jit(solution)/shard_map/ppermute | solution.py:72
  122.8 6.7 %collective-permute-done.12 = bf16[512,256]{0,1:T(8,128)(2,1)S(1)} collective-permute-done((bf16[512,256]{0,1:T(8,128)(2,1)S(1)}, bf16[512,256]{0,1:T(8,128)(2,1)S(1)}, u32[]{:S(2)}, u32[]{:S(2)}) %collective-permute-start.12) | collective-permute-done | bytes 262176 | tf_op jit(solution)/shard_map/ppermute | solution.py:72
  129.6 0.8 copy.39
  (59 shorter events, 1.9 us)
Async XLA Ops:
  0.0 110.8 %copy-start = (bf16[1024,1024]{1,0:T(8,128)(2,1)S(1)}, bf16[1024,1024]{1,0:T(8,128)(2,1)}, u32[]{:S(2)}) copy-start(bf16[1024,1024]{1,0:T(8,128)(2,1)} %param.43) | copy-start | bytes 6291460
  0.9 13.4 %collective-permute-start.1 = (bf16[64,256]{1,0:T(8,128)(2,1)S(1)}, bf16[64,256]{1,0:T(8,128)(2,1)S(1)}, u32[]{:S(2)}, u32[]{:S(2)}) collective-permute-start(bf16[64,256]{1,0:T(8,128)(2,1)S(1)} %get-tuple-element.187), channel_id=1, source_target_pairs={{4,0},{8,4},{12,8},{5,1},{9,5},{13,9},{6,2},{10,6},{14,10},{7,3},{... | collective-permute-start | bytes 98312 | tf_op jit(solution)/shard_map/ppermute | solution.py:21
  2.2 12.1 %collective-permute-start = (bf16[64,256]{1,0:T(8,128)(2,1)S(1)}, bf16[64,256]{1,0:T(8,128)(2,1)S(1)}, u32[]{:S(2)}, u32[]{:S(2)}) collective-permute-start(bf16[64,256]{1,0:T(8,128)(2,1)S(1)} %get-tuple-element.186), channel_id=1, source_target_pairs={{0,4},{4,8},{8,12},{1,5},{5,9},{9,13},{2,6},{6,10},{10,14},{3,7},{... | collective-permute-start | bytes 98312 | tf_op jit(solution)/shard_map/ppermute | solution.py:20
  16.3 9.1 %copy-start.4 = (bf16[1024]{0:T(1024)(128)(2,1)S(1)}, bf16[1024]{0:T(1024)(128)(2,1)}, u32[]{:S(2)}) copy-start(bf16[1024]{0:T(1024)(128)(2,1)} %param.36) | copy-start | bytes 6148
  16.3 9.1 %copy-start.6 = (s32[4,4]{1,0:T(4,128)S(1)}, s32[4,4]{1,0:T(4,128)}, u32[]{:S(2)}) copy-start(s32[4,4]{1,0:T(4,128)} %param.33) | copy-start | bytes 196
  16.7 7.8 %collective-permute-start.2 = (bf16[512,256]{0,1:T(8,128)(2,1)S(1)}, bf16[512,256]{0,1:T(8,128)(2,1)S(1)}, u32[]{:S(2)}, u32[]{:S(2)}) collective-permute-start(bf16[512,256]{0,1:T(8,128)(2,1)S(1)} %add_convert_fusion), channel_id=1, source_target_pairs={{0,2},{1,3},{2,0},{3,1},{4,6},{5,7},{6,4},{7,5},{8,10},{9,11},{10,... | collective-permute-start | bytes 786440 | tf_op jit(solution)/shard_map/ppermute | solution.py:86
  25.4 4.6 %collective-permute-start.3 = (bf16[512,2,256]{0,2,1:T(8,128)(2,1)}, bf16[512,2,256]{0,2,1:T(8,128)(2,1)}, u32[]{:S(2)}, u32[]{:S(2)}) collective-permute-start(bf16[512,2,256]{0,2,1:T(8,128)(2,1)} %pad_maximum_fusion.2), channel_id=1, source_target_pairs={{0,1},{1,0},{2,3},{3,2},{4,5},{5,4},{6,7},{7,6},{8,9},{9,8},{10,11... | collective-permute-start | bytes 1572872 | tf_op jit(solution)/shard_map/ppermute | solution.py:86
  31.4 1.0 copy-start.7
  31.4 1.5 %copy-start.8 = (bf16[1024,256]{1,0:T(8,128)(2,1)S(1)}, bf16[1024,256]{1,0:T(8,128)(2,1)}, u32[]{:S(2)}) copy-start(bf16[1024,256]{1,0:T(8,128)(2,1)} %param.37) | copy-start | bytes 1572868
  32.5 1.8 %copy-start.9 = (bf16[1024,256]{1,0:T(8,128)(2,1)S(1)}, bf16[1024,256]{1,0:T(8,128)(2,1)}, u32[]{:S(2)}) copy-start(bf16[1024,256]{1,0:T(8,128)(2,1)} %param.39) | copy-start | bytes 1572868
  34.8 16.2 %collective-permute-start.4 = (bf16[512,512]{0,1:T(8,128)(2,1)S(1)}, bf16[512,512]{0,1:T(8,128)(2,1)S(1)}, u32[]{:S(2)}, u32[]{:S(2)}) collective-permute-start(bf16[512,512]{0,1:T(8,128)(2,1)S(1)} %pad_maximum_fusion.3), channel_id=1, source_target_pairs={{0,4},{4,8},{8,12},{12,0},{1,5},{5,9},{9,13},{13,1},{2,6},{6,10},{... | collective-permute-start | bytes 1572872 | tf_op jit(solution)/shard_map/ppermute | solution.py:181
  51.0 15.4 %collective-permute-start.5 = (bf16[512,512]{0,1:T(8,128)(2,1)S(1)}, bf16[512,512]{0,1:T(8,128)(2,1)S(1)}, u32[]{:S(2)}, u32[]{:S(2)}) collective-permute-start(bf16[512,512]{0,1:T(8,128)(2,1)S(1)} %collective-permute-done.4), channel_id=1, source_target_pairs={{0,4},{4,8},{8,12},{12,0},{1,5},{5,9},{9,13},{13,1},{2,6},{6,10},{... | collective-permute-start | bytes 1572872 | tf_op jit(solution)/shard_map/ppermute | solution.py:181
  66.4 14.7 %collective-permute-start.6 = (bf16[512,512]{0,1:T(8,128)(2,1)S(1)}, bf16[512,512]{0,1:T(8,128)(2,1)S(1)}, u32[]{:S(2)}, u32[]{:S(2)}) collective-permute-start(bf16[512,512]{0,1:T(8,128)(2,1)S(1)} %collective-permute-done.5), channel_id=1, source_target_pairs={{0,4},{4,8},{8,12},{12,0},{1,5},{5,9},{9,13},{13,1},{2,6},{6,10},{... | collective-permute-start | bytes 1572872 | tf_op jit(solution)/shard_map/ppermute | solution.py:181
  84.3 1.3 %copy-start.1 = (f32[512,2,2,256]{0,3,2,1:T(8,128)}, f32[512,2,2,256]{0,3,2,1:T(8,128)S(1)}, u32[]{:S(2)}) copy-start(f32[512,2,2,256]{0,3,2,1:T(8,128)S(1)} %fusion.135) | copy-start | bytes 6291460
  85.6 22.0 %copy-start.5 = (bf16[1024]{0:T(1024)(128)(2,1)S(1)}, bf16[1024]{0:T(1024)(128)(2,1)}, u32[]{:S(2)}) copy-start(bf16[1024]{0:T(1024)(128)(2,1)} %param.41) | copy-start | bytes 6148
  85.7 2.1 %collective-permute-start.7 = (bf16[512,2,256]{0,2,1:T(8,128)(2,1)S(1)}, bf16[512,2,256]{0,2,1:T(8,128)(2,1)}, u32[]{:S(2)}, u32[]{:S(2)}) collective-permute-start(bf16[512,2,256]{0,2,1:T(8,128)(2,1)S(1)} %fusion.66), channel_id=1, source_target_pairs={{0,1},{1,0},{2,3},{3,2},{4,5},{5,4},{6,7},{7,6},{8,9},{9,8},{10,11... | collective-permute-start | bytes 1572872 | tf_op jit(solution)/shard_map/ppermute | solution.py:72
  90.1 8.7 %collective-permute-start.8 = (bf16[512,256]{0,1:T(8,128)(2,1)}, bf16[512,256]{0,1:T(8,128)(2,1)}, u32[]{:S(2)}, u32[]{:S(2)}) collective-permute-start(bf16[512,256]{0,1:T(8,128)(2,1)} %fusion.102), channel_id=1, source_target_pairs={{0,2},{1,3},{2,0},{3,1},{4,6},{5,7},{6,4},{7,5},{8,10},{9,11},{10,... | collective-permute-start | bytes 786440 | tf_op jit(solution)/shard_map/ppermute | solution.py:72
  99.8 7.8 %copy-start.2 = (bf16[512,256]{0,1:T(8,128)(2,1)}, bf16[512,256]{0,1:T(8,128)(2,1)S(1)}, u32[]{:S(2)}) copy-start(bf16[512,256]{0,1:T(8,128)(2,1)S(1)} %fusion.99) | copy-start | bytes 786436
  99.9 7.6 %collective-permute-start.9 = (bf16[512,256]{0,1:T(8,128)(2,1)S(1)}, bf16[512,256]{0,1:T(8,128)(2,1)S(1)}, u32[]{:S(2)}, u32[]{:S(2)}) collective-permute-start(bf16[512,256]{0,1:T(8,128)(2,1)S(1)} %fusion.99), channel_id=1, source_target_pairs={{0,2},{1,3},{2,0},{3,1},{4,6},{5,7},{6,4},{7,5},{8,10},{9,11},{10,... | collective-permute-start | bytes 786440 | tf_op jit(solution)/shard_map/ppermute | solution.py:86
  107.5 2.0 %collective-permute-start.10 = (bf16[512,2,256]{0,2,1:T(8,128)(2,1)S(1)}, bf16[512,2,256]{0,2,1:T(8,128)(2,1)S(1)}, u32[]{:S(2)}, u32[]{:S(2)}) collective-permute-start(bf16[512,2,256]{0,2,1:T(8,128)(2,1)S(1)} %pad_maximum_fusion.4), channel_id=1, source_target_pairs={{0,1},{1,0},{2,3},{3,2},{4,5},{5,4},{6,7},{7,6},{8,9},{9,8},{10,11... | collective-permute-start | bytes 1572872 | tf_op jit(solution)/shard_map/ppermute | solution.py:86
  116.3 13.2 %copy-start.3 = (bf16[512,256]{0,1:T(8,128)(2,1)S(1)}, bf16[512,256]{0,1:T(8,128)(2,1)}, u32[]{:S(2)}) copy-start(bf16[512,256]{0,1:T(8,128)(2,1)} %copy-done.2) | copy-start | bytes 786436
  117.6 2.0 %collective-permute-start.11 = (bf16[512,2,256]{0,2,1:T(8,128)(2,1)S(1)}, bf16[512,2,256]{0,2,1:T(8,128)(2,1)S(1)}, u32[]{:S(2)}, u32[]{:S(2)}) collective-permute-start(bf16[512,2,256]{0,2,1:T(8,128)(2,1)S(1)} %fusion.67), channel_id=1, source_target_pairs={{0,1},{1,0},{2,3},{3,2},{4,5},{5,4},{6,7},{7,6},{8,9},{9,8},{10,11... | collective-permute-start | bytes 1572872 | tf_op jit(solution)/shard_map/ppermute | solution.py:72
  121.1 8.4 %collective-permute-start.12 = (bf16[512,256]{0,1:T(8,128)(2,1)S(1)}, bf16[512,256]{0,1:T(8,128)(2,1)S(1)}, u32[]{:S(2)}, u32[]{:S(2)}) collective-permute-start(bf16[512,256]{0,1:T(8,128)(2,1)S(1)} %fusion.103), channel_id=1, source_target_pairs={{0,2},{1,3},{2,0},{3,1},{4,6},{5,7},{6,4},{7,5},{8,10},{9,11},{10,... | collective-permute-start | bytes 786440 | tf_op jit(solution)/shard_map/ppermute | solution.py:72

commit v4 on v2

--- a/solution.py
+++ b/solution.py
@@ -174,15 +174,40 @@
         jnp.zeros((local_bricks, head_count, brick_rows), jnp.float32),
         jnp.zeros((local_bricks, brick_rows, head_count, HEAD_DIM), jnp.float32),
     )
-    ring = [(i, (i + 1) % dev_total) for i in range(dev_total)]
-    block = pair_local
-    for step in range(dev_total):
-        if step > 0:
-            block = lax.ppermute(block, "bricks", ring)
-        source = (brick_dev - step) % dev_total
-        key_ids = source * local_bricks + jnp.arange(local_bricks, dtype=jnp.int32)
-        linked = jnp.take(linked_rows, key_ids, axis=1) > 0
-        state = absorb_block(state, query_heads, block, linked, head_count, brick_rows, local_width)
+    def take_block(state_now, block, source, valid):
+        key_ids = jnp.clip(source, 0, dev_total - 1) * local_bricks + jnp.arange(
+            local_bricks, dtype=jnp.int32
+        )
+        linked = (jnp.take(linked_rows, key_ids, axis=1) > 0) & valid
+        return absorb_block(
+            state_now, query_heads, block, linked, head_count, brick_rows, local_width
+        )
+
+    upward, downward = pair_local, pair_local
+    pending = [(pair_local, brick_dev, jnp.bool_(True))]
+    for step in range(1, dev_total):
+        up_pairs = [(i, i + 1) for i in range(step - 1, dev_total - 1)]
+        down_pairs = [(i, i - 1) for i in range(1, dev_total - step + 1)]
+        upward_next = lax.ppermute(upward, "bricks", up_pairs)
+        downward_next = lax.ppermute(downward, "bricks", down_pairs)
+        for block, source, valid in pending:
+            state = take_block(state, block, source, valid)
+        state, upward, downward = lax.optimization_barrier((state, upward_next, downward_next))
+        from_below = brick_dev >= step
+        from_above = brick_dev + step <= dev_total - 1
+        if 2 * step > dev_total - 1:
+            pending = [(
+                jnp.where(from_below, upward, downward),
+                jnp.where(from_below, brick_dev - step, brick_dev + step),
+                from_below | from_above,
+            )]
+        else:
+            pending = [
+                (upward, brick_dev - step, from_below),
+                (downward, brick_dev + step, from_above),
+            ]
+    for block, source, valid in pending:
+        state = take_block(state, block, source, valid)
     row_max, row_mass, weighted = state
     attended = (weighted / jnp.transpose(row_mass, (0, 2, 1))[:, :, :, None]).astype(jnp.bfloat16)
     attended = attended.reshape(row_count, local_width)

time: 135 us -> 136 us (level)
  waiting for transfers between devices: 72.4 us -> 63 us
  starting transfers between devices: 16 us -> 23.1 us
  matrix products: 14.4 us -> 16.2 us
    ppermute x3 -> x6, waiting for transfers between devices: 41.2 us -> 31.5 us  [the longest x3 24.1 us: shards(): downward_next = lax.ppermute(downward, 'bricks', down_pairs)]
    ppermute x3 -> x6, starting transfers between devices: 1.79 us -> 9.32 us  [the longest x3 5.04 us: shards(): upward_next = lax.ppermute(upward, 'bricks', up_pairs)]
    dot_general x4 -> x5, matrix products: 3.98 us -> 4.97 us  [absorb_block(): jnp.einsum('bhqk,khd->bqhd', weights.astype(jnp.bfloat16), value_rows, pr...]
    reduce_sum x2 -> x5, other arithmetic: 3.34 us -> 4.19 us  [absorb_block(): mass_new = row_mass * factor + jnp.sum(weights, axis=-1)]
    dot_general x4 -> x5, matrix products: 3.09 us -> 3.87 us  [absorb_block(): jnp.einsum('bqhd,khd->bhqk', query_heads, key_rows, preferred_element_typ...]
  transfers between devices with their start and end apart: 13 -> 16, of which waited for: 10 -> 11; matrix products, arithmetic and copies ran while one was open for 7% -> 14% of each run, Pallas kernels for 0% -> 0%
where the time goes in v4:
time: 136 us
  waiting for transfers between devices  63 us (46%)
  starting transfers between devices  23.1 us (17%)
  matrix products  16.2 us (12%)
  other arithmetic  15.5 us (11%)
  local copies, waits for them, and re-layouts  12.6 us (9%)
  between operations  5.02 us (4%)
    ppermute x3, waiting for transfers between devices, shards(): downward_next = lax.ppermute(downward, 'bricks', down_pairs)  24.1 us
    ppermute x4, waiting for transfers between devices, scatter_heads(): lax.ppermute(give.astype(jnp.bfloat16), 'heads', [(i, i ^ bit) for i in r...  17.8 us
    ppermute x4, waiting for transfers between devices, gather_heads(): lax.ppermute(current, 'heads', [(i, i ^ bit) for i in range(head_total)])  13.7 us
    ppermute x3, waiting for transfers between devices, shards(): upward_next = lax.ppermute(upward, 'bricks', up_pairs)  7.36 us
    ppermute x1, starting transfers between devices, extended_2(): before = lax.ppermute(last, axis, up)  5.56 us
    dot_general x1, matrix products, shards(): lowered = jnp.dot(hidden, down_weight, preferred_element_type=jnp.float32)  5.5 us
    ppermute x3, starting transfers between devices, shards(): upward_next = lax.ppermute(upward, 'bricks', up_pairs)  5.04 us
    dot_general x5, matrix products, absorb_block(): jnp.einsum('bhqk,khd->bqhd', weights.astype(jnp.bfloat16), value_rows, pr...  4.97 us
  transfers between devices with their start and end apart: 16, of which 11 were waited for; matrix products, arithmetic and copies ran while one was open for 14% of the time, Pallas kernels for 0%

profile of v4, /device:TPU:0, one launch (start us, length us, event | category | flops | bytes accessed | tf_op | source)
XLA Modules:
  0.0 135.5 jit_solution(16063936035298824252)
XLA Ops:
  0.0 0.9 fusion.147
  0.9 1.3 collective-permute-start.1
  2.2 5.6 %collective-permute-start = (bf16[64,256]{1,0:T(8,128)(2,1)S(1)}, bf16[64,256]{1,0:T(8,128)(2,1)S(1)}, u32[]{:S(2)}, u32[]{:S(2)}) collective-permute-start(bf16[64,256]{1,0:T(8,128)(2,1)S(1)} %get-tuple-element.221), channel_id=1, source_target_pairs={{0,4},{4,8},{8,12},{1,5},{5,9},{9,13},{2,6},{6,10},{10,14},{3,7},{... | collective-permute-start | bytes 98312 | tf_op jit(solution)/shard_map/ppermute | solution.py:20
  7.8 1.0 fusion.148
  8.8 0.9 fusion.149
  9.7 1.1 copy.27
  10.8 1.4 %fusion.151 = (s32[1]{0:T(128)}, s32[1]{0:T(128)}) fusion(s32[4]{0:T(128)} %param.36, s32[]{:T(128)} %bitcast.2, s32[]{:T(128)} %bitcast.6), kind=kLoop, calls=%fused_computation.231 | loop fusion | bytes 24 | tf_op jit(solution)/shard_map/jit(_take)/gather | solution.py:146
  13.7 0.7 convert_element_type.143
  14.7 1.7 %fusion.81 = f32[1,8,8,8,256]{4,3,2,1,0:T(8,128)S(1)} fusion(f32[1,10,10,10,256]{4,3,2,1,0:T(8,128)S(1)} %select_maximum_fusion, f32[1,1,8,8,256]{4,3,2,1,0:T(8,128)S(1)} %multiply_bitcast_fusion, f32[1,8,8,8,256]{4,3,2,1,0:T(8,128)S(1)} %bitcast.464, f32[1,1,8,8,256]{4,3,2,1,0:T(8,128)S(1)} %multiply_bitcast_fusion.1, f32[256]{0:T(256)S(1)} %bitcast.511, ...), kind=kLoop, calls=%fused_computation.97 | loop fusion | flops 7208960 | bytes 13790208 | tf_op jit(solution)/shard_map/add | solution.py:51
  16.7 2.0 %collective-permute-start.2 = (bf16[512,256]{0,1:T(8,128)(2,1)S(1)}, bf16[512,256]{0,1:T(8,128)(2,1)S(1)}, u32[]{:S(2)}, u32[]{:S(2)}) collective-permute-start(bf16[512,256]{0,1:T(8,128)(2,1)S(1)} %add_convert_fusion), channel_id=1, source_target_pairs={{0,2},{1,3},{2,0},{3,1},{4,6},{5,7},{6,4},{7,5},{8,10},{9,11},{10,... | collective-permute-start | bytes 786440 | tf_op jit(solution)/shard_map/ppermute | solution.py:86
  18.7 5.8 %collective-permute-done.2 = bf16[512,256]{0,1:T(8,128)(2,1)S(1)} collective-permute-done((bf16[512,256]{0,1:T(8,128)(2,1)S(1)}, bf16[512,256]{0,1:T(8,128)(2,1)S(1)}, u32[]{:S(2)}, u32[]{:S(2)}) %collective-permute-start.2) | collective-permute-done | bytes 262176 | tf_op jit(solution)/shard_map/ppermute | solution.py:86
  24.6 0.8 pad_maximum_fusion.2
  25.4 0.6 fusion.150
  29.1 1.2 copy.50
  30.4 1.1 select_bitcast_fusion.3
  32.1 0.3 multiply_reduce_fusion.1
  32.9 0.5 convolution_convert_fusion.2
  33.4 0.5 convolution_convert_fusion
  34.0 3.7 %collective-permute-start.4 = (bf16[512,512]{0,1:T(8,128)(2,1)S(1)}, bf16[512,512]{0,1:T(8,128)(2,1)S(1)}, u32[]{:S(2)}, u32[]{:S(2)}) collective-permute-start(bf16[512,512]{0,1:T(8,128)(2,1)S(1)} %pad_maximum_fusion.3), channel_id=1, source_target_pairs={{0,4},{4,8},{8,12},{1,5},{5,9},{9,13},{2,6},{6,10},{10,14},{3,7},{... | collective-permute-start | bytes 1572872 | tf_op jit(solution)/shard_map/ppermute | solution.py:191
  37.6 1.3 collective-permute-start.5
  38.9 0.5 convolution_convert_fusion.1
  39.4 0.8 bitcast_reduce_fusion.4
  40.2 0.8 fusion.6
  41.1 1.0 fusion.67
  42.1 7.3 %collective-permute-done.4 = bf16[512,512]{0,1:T(8,128)(2,1)S(1)} collective-permute-done((bf16[512,512]{0,1:T(8,128)(2,1)S(1)}, bf16[512,512]{0,1:T(8,128)(2,1)S(1)}, u32[]{:S(2)}, u32[]{:S(2)}) %collective-permute-start.4) | collective-permute-done | bytes 524320 | tf_op jit(solution)/shard_map/ppermute | solution.py:191
  49.4 4.1 %collective-permute-done.5 = bf16[512,512]{0,1:T(8,128)(2,1)S(1)} collective-permute-done((bf16[512,512]{0,1:T(8,128)(2,1)S(1)}, bf16[512,512]{0,1:T(8,128)(2,1)S(1)}, u32[]{:S(2)}, u32[]{:S(2)}) %collective-permute-start.5) | collective-permute-done | bytes 524320 | tf_op jit(solution)/shard_map/ppermute | solution.py:192
  53.6 0.7 collective-permute-start.6
  54.3 1.5 %collective-permute-start.7 = (bf16[512,512]{0,1:T(8,128)(2,1)S(1)}, bf16[512,512]{0,1:T(8,128)(2,1)S(1)}, u32[]{:S(2)}, u32[]{:S(2)}) collective-permute-start(bf16[512,512]{0,1:T(8,128)(2,1)S(1)} %collective-permute-done.5), channel_id=1, source_target_pairs={{4,0},{8,4},{5,1},{9,5},{6,2},{10,6},{7,3},{11,7},{20,16},{24,20},... | collective-permute-start | bytes 1572872 | tf_op jit(solution)/shard_map/ppermute | solution.py:192
  55.8 0.8 bitcast_reduce_fusion.3
  56.6 0.8 bitcast_reduce_fusion.2
  57.4 0.8 fusion.8
  58.2 1.0 fusion.61
  59.2 0.8 fusion.10
  60.1 1.0 fusion.70
  61.1 9.7 %collective-permute-done.7 = bf16[512,512]{0,1:T(8,128)(2,1)S(1)} collective-permute-done((bf16[512,512]{0,1:T(8,128)(2,1)S(1)}, bf16[512,512]{0,1:T(8,128)(2,1)S(1)}, u32[]{:S(2)}, u32[]{:S(2)}) %collective-permute-start.7) | collective-permute-done | bytes 524320 | tf_op jit(solution)/shard_map/ppermute | solution.py:192
  70.8 0.7 collective-permute-start.8
  71.6 1.5 %collective-permute-start.9 = (bf16[512,512]{0,1:T(8,128)(2,1)S(1)}, bf16[512,512]{0,1:T(8,128)(2,1)S(1)}, u32[]{:S(2)}, u32[]{:S(2)}) collective-permute-start(bf16[512,512]{0,1:T(8,128)(2,1)S(1)} %collective-permute-done.7), channel_id=1, source_target_pairs={{4,0},{5,1},{6,2},{7,3},{20,16},{21,17},{22,18},{23,19}} | collective-permute-start | bytes 1572872 | tf_op jit(solution)/shard_map/ppermute | solution.py:192
  73.2 0.8 bitcast_reduce_fusion.1
  74.0 0.8 fusion.12
  74.8 1.0 fusion.55
  75.9 10.2 %collective-permute-done.9 = bf16[512,512]{0,1:T(8,128)(2,1)S(1)} collective-permute-done((bf16[512,512]{0,1:T(8,128)(2,1)S(1)}, bf16[512,512]{0,1:T(8,128)(2,1)S(1)}, u32[]{:S(2)}, u32[]{:S(2)}) %collective-permute-start.9) | collective-permute-done | bytes 524320 | tf_op jit(solution)/shard_map/ppermute | solution.py:192
  86.2 0.8 bitcast_reduce_fusion
  87.0 0.8 fusion.13
  87.9 1.0 divide_convert_fusion
  88.9 0.4 fusion.154
  89.4 1.3 copy-done.1
  90.9 2.0 %collective-permute-done.10 = bf16[512,2,256]{0,2,1:T(8,128)(2,1)} collective-permute-done((bf16[512,2,256]{0,2,1:T(8,128)(2,1)S(1)}, bf16[512,2,256]{0,2,1:T(8,128)(2,1)}, u32[]{:S(2)}, u32[]{:S(2)}) %collective-permute-start.10) | collective-permute-done | bytes 524320 | tf_op jit(solution)/shard_map/ppermute | solution.py:72
  92.9 1.6 %bitcast_add_fusion.1 = f32[512,2,256]{0,2,1:T(8,128)S(1)} fusion(bf16[512,2,256]{0,2,1:T(8,128)(2,1)} %collective-permute-done.10, f32[512,2,2,256]{0,3,2,1:T(8,128)} %copy-done.1, s32[]{:T(128)S(6)} %select_n.220), kind=kLoop, calls=%fused_computation.88 | loop fusion | flops 524288 | bytes 2621444 | tf_op jit(solution)/shard_map/add | solution.py:75
  94.5 0.7 fusion.115
  95.2 1.5 %collective-permute-start.11 = (bf16[512,256]{0,1:T(8,128)(2,1)}, bf16[512,256]{0,1:T(8,128)(2,1)}, u32[]{:S(2)}, u32[]{:S(2)}) collective-permute-start(bf16[512,256]{0,1:T(8,128)(2,1)} %fusion.115), channel_id=1, source_target_pairs={{0,2},{1,3},{2,0},{3,1},{4,6},{5,7},{6,4},{7,5},{8,10},{9,11},{10,... | collective-permute-start | bytes 786440 | tf_op jit(solution)/shard_map/ppermute | solution.py:72
  96.7 7.2 %collective-permute-done.11 = bf16[512,256]{0,1:T(8,128)(2,1)} collective-permute-done((bf16[512,256]{0,1:T(8,128)(2,1)}, bf16[512,256]{0,1:T(8,128)(2,1)}, u32[]{:S(2)}, u32[]{:S(2)}) %collective-permute-start.11) | collective-permute-done | bytes 262176 | tf_op jit(solution)/shard_map/ppermute | solution.py:72
  103.9 1.1 fusion.112
  104.9 1.6 %collective-permute-start.12 = (bf16[512,256]{0,1:T(8,128)(2,1)S(1)}, bf16[512,256]{0,1:T(8,128)(2,1)S(1)}, u32[]{:S(2)}, u32[]{:S(2)}) collective-permute-start(bf16[512,256]{0,1:T(8,128)(2,1)S(1)} %fusion.112), channel_id=1, source_target_pairs={{0,2},{1,3},{2,0},{3,1},{4,6},{5,7},{6,4},{7,5},{8,10},{9,11},{10,... | collective-permute-start | bytes 786440 | tf_op jit(solution)/shard_map/ppermute | solution.py:86
  106.5 6.0 %collective-permute-done.12 = bf16[512,256]{0,1:T(8,128)(2,1)S(1)} collective-permute-done((bf16[512,256]{0,1:T(8,128)(2,1)S(1)}, bf16[512,256]{0,1:T(8,128)(2,1)S(1)}, u32[]{:S(2)}, u32[]{:S(2)}) %collective-permute-start.12) | collective-permute-done | bytes 262176 | tf_op jit(solution)/shard_map/ppermute | solution.py:86
  112.7 1.9 %collective-permute-done.13 = bf16[512,2,256]{0,2,1:T(8,128)(2,1)S(1)} collective-permute-done((bf16[512,2,256]{0,2,1:T(8,128)(2,1)S(1)}, bf16[512,2,256]{0,2,1:T(8,128)(2,1)S(1)}, u32[]{:S(2)}, u32[]{:S(2)}) %collective-permute-start.13) | collective-permute-done | bytes 524320 | tf_op jit(solution)/shard_map/ppermute | solution.py:86
  115.2 0.3 multiply_reduce_fusion
  115.6 0.3 fusion.30
  115.9 5.5 %fusion.73 = f32[512,1024]{0,1:T(8,128)} fusion(bf16[1024,1024]{1,0:T(8,128)(2,1)S(1)} %copy-done, bf16[512,1024]{0,1:T(8,128)(2,1)S(1)} %fusion.30, bf16[1024,1024]{1,0:T(8,128)(2,1)} %param.46), kind=kOutput, calls=%fused_computation.83 | convolution fusion | flops 2152202240 | bytes 7340032 | tf_op jit(solution)/shard_map/dot_general | solution.py:222
  121.4 1.3 fusion.80
  122.9 1.8 %collective-permute-done.14 = bf16[512,2,256]{0,2,1:T(8,128)(2,1)S(1)} collective-permute-done((bf16[512,2,256]{0,2,1:T(8,128)(2,1)S(1)}, bf16[512,2,256]{0,2,1:T(8,128)(2,1)S(1)}, u32[]{:S(2)}, u32[]{:S(2)}) %collective-permute-start.14) | collective-permute-done | bytes 524320 | tf_op jit(solution)/shard_map/ppermute | solution.py:72
  124.7 1.4 %bitcast_add_fusion = f32[512,2,256]{0,2,1:T(8,128)S(1)} fusion(bf16[512,2,256]{0,2,1:T(8,128)(2,1)S(1)} %collective-permute-done.14, f32[512,2,2,256]{0,3,2,1:T(8,128)} %bitcast.468, s32[]{:T(128)S(6)} %select_n.220), kind=kLoop, calls=%fused_computation.87 | loop fusion | flops 524288 | bytes 2621444 | tf_op jit(solution)/shard_map/add | solution.py:75
  126.1 1.6 %collective-permute-start.15 = (bf16[512,256]{0,1:T(8,128)(2,1)S(1)}, bf16[512,256]{0,1:T(8,128)(2,1)S(1)}, u32[]{:S(2)}, u32[]{:S(2)}) collective-permute-start(bf16[512,256]{0,1:T(8,128)(2,1)S(1)} %fusion.116), channel_id=1, source_target_pairs={{0,2},{1,3},{2,0},{3,1},{4,6},{5,7},{6,4},{7,5},{8,10},{9,11},{10,... | collective-permute-start | bytes 786440 | tf_op jit(solution)/shard_map/ppermute | solution.py:72
  127.7 6.9 %collective-permute-done.15 = bf16[512,256]{0,1:T(8,128)(2,1)S(1)} collective-permute-done((bf16[512,256]{0,1:T(8,128)(2,1)S(1)}, bf16[512,256]{0,1:T(8,128)(2,1)S(1)}, u32[]{:S(2)}, u32[]{:S(2)}) %collective-permute-start.15) | collective-permute-done | bytes 262176 | tf_op jit(solution)/shard_map/ppermute | solution.py:72
  134.7 0.8 copy.41
  (69 shorter events, 3.6 us)
Async XLA Ops:
  0.0 115.9 %copy-start = (bf16[1024,1024]{1,0:T(8,128)(2,1)S(1)}, bf16[1024,1024]{1,0:T(8,128)(2,1)}, u32[]{:S(2)}) copy-start(bf16[1024,1024]{1,0:T(8,128)(2,1)} %param.47) | copy-start | bytes 6291460
  0.9 13.4 %collective-permute-start.1 = (bf16[64,256]{1,0:T(8,128)(2,1)S(1)}, bf16[64,256]{1,0:T(8,128)(2,1)S(1)}, u32[]{:S(2)}, u32[]{:S(2)}) collective-permute-start(bf16[64,256]{1,0:T(8,128)(2,1)S(1)} %get-tuple-element.222), channel_id=1, source_target_pairs={{4,0},{8,4},{12,8},{5,1},{9,5},{13,9},{6,2},{10,6},{14,10},{7,3},{... | collective-permute-start | bytes 98312 | tf_op jit(solution)/shard_map/ppermute | solution.py:21
  2.2 12.2 %collective-permute-start = (bf16[64,256]{1,0:T(8,128)(2,1)S(1)}, bf16[64,256]{1,0:T(8,128)(2,1)S(1)}, u32[]{:S(2)}, u32[]{:S(2)}) collective-permute-start(bf16[64,256]{1,0:T(8,128)(2,1)S(1)} %get-tuple-element.221), channel_id=1, source_target_pairs={{0,4},{4,8},{8,12},{1,5},{5,9},{9,13},{2,6},{6,10},{10,14},{3,7},{... | collective-permute-start | bytes 98312 | tf_op jit(solution)/shard_map/ppermute | solution.py:20
  16.3 9.1 %copy-start.5 = (bf16[1024]{0:T(1024)(128)(2,1)S(1)}, bf16[1024]{0:T(1024)(128)(2,1)}, u32[]{:S(2)}) copy-start(bf16[1024]{0:T(1024)(128)(2,1)} %param.40) | copy-start | bytes 6148
  16.3 9.1 %copy-start.4 = (s32[4,4]{1,0:T(4,128)S(1)}, s32[4,4]{1,0:T(4,128)}, u32[]{:S(2)}) copy-start(s32[4,4]{1,0:T(4,128)} %param.37) | copy-start | bytes 196
  16.7 7.8 %collective-permute-start.2 = (bf16[512,256]{0,1:T(8,128)(2,1)S(1)}, bf16[512,256]{0,1:T(8,128)(2,1)S(1)}, u32[]{:S(2)}, u32[]{:S(2)}) collective-permute-start(bf16[512,256]{0,1:T(8,128)(2,1)S(1)} %add_convert_fusion), channel_id=1, source_target_pairs={{0,2},{1,3},{2,0},{3,1},{4,6},{5,7},{6,4},{7,5},{8,10},{9,11},{10,... | collective-permute-start | bytes 786440 | tf_op jit(solution)/shard_map/ppermute | solution.py:86
  25.4 5.0 %collective-permute-start.3 = (bf16[512,2,256]{0,2,1:T(8,128)(2,1)}, bf16[512,2,256]{0,2,1:T(8,128)(2,1)}, u32[]{:S(2)}, u32[]{:S(2)}) collective-permute-start(bf16[512,2,256]{0,2,1:T(8,128)(2,1)} %pad_maximum_fusion.2), channel_id=1, source_target_pairs={{0,1},{1,0},{2,3},{3,2},{4,5},{5,4},{6,7},{7,6},{8,9},{9,8},{10,11... | collective-permute-start | bytes 1572872 | tf_op jit(solution)/shard_map/ppermute | solution.py:86
  31.9 1.0 copy-start.7
  31.9 1.5 %copy-start.8 = (bf16[1024,256]{1,0:T(8,128)(2,1)S(1)}, bf16[1024,256]{1,0:T(8,128)(2,1)}, u32[]{:S(2)}) copy-start(bf16[1024,256]{1,0:T(8,128)(2,1)} %param.43) | copy-start | bytes 1572868
  32.4 6.5 %copy-start.9 = (bf16[1024,256]{1,0:T(8,128)(2,1)S(1)}, bf16[1024,256]{1,0:T(8,128)(2,1)}, u32[]{:S(2)}) copy-start(bf16[1024,256]{1,0:T(8,128)(2,1)} %param.41) | copy-start | bytes 1572868
  34.0 15.5 %collective-permute-start.4 = (bf16[512,512]{0,1:T(8,128)(2,1)S(1)}, bf16[512,512]{0,1:T(8,128)(2,1)S(1)}, u32[]{:S(2)}, u32[]{:S(2)}) collective-permute-start(bf16[512,512]{0,1:T(8,128)(2,1)S(1)} %pad_maximum_fusion.3), channel_id=1, source_target_pairs={{0,4},{4,8},{8,12},{1,5},{5,9},{9,13},{2,6},{6,10},{10,14},{3,7},{... | collective-permute-start | bytes 1572872 | tf_op jit(solution)/shard_map/ppermute | solution.py:191
  37.6 15.9 %collective-permute-start.5 = (bf16[512,512]{0,1:T(8,128)(2,1)S(1)}, bf16[512,512]{0,1:T(8,128)(2,1)S(1)}, u32[]{:S(2)}, u32[]{:S(2)}) collective-permute-start(bf16[512,512]{0,1:T(8,128)(2,1)S(1)} %pad_maximum_fusion.3), channel_id=1, source_target_pairs={{4,0},{8,4},{12,8},{5,1},{9,5},{13,9},{6,2},{10,6},{14,10},{7,3},{... | collective-permute-start | bytes 1572872 | tf_op jit(solution)/shard_map/ppermute | solution.py:192
  53.6 7.5 %collective-permute-start.6 = (bf16[512,512]{0,1:T(8,128)(2,1)S(1)}, bf16[512,512]{0,1:T(8,128)(2,1)S(1)}, u32[]{:S(2)}, u32[]{:S(2)}) collective-permute-start(bf16[512,512]{0,1:T(8,128)(2,1)S(1)} %collective-permute-done.4), channel_id=1, source_target_pairs={{4,8},{8,12},{5,9},{9,13},{6,10},{10,14},{7,11},{11,15},{20,24},{2... | collective-permute-start | bytes 1572872 | tf_op jit(solution)/shard_map/ppermute | solution.py:191
  54.3 16.5 %collective-permute-start.7 = (bf16[512,512]{0,1:T(8,128)(2,1)S(1)}, bf16[512,512]{0,1:T(8,128)(2,1)S(1)}, u32[]{:S(2)}, u32[]{:S(2)}) collective-permute-start(bf16[512,512]{0,1:T(8,128)(2,1)S(1)} %collective-permute-done.5), channel_id=1, source_target_pairs={{4,0},{8,4},{5,1},{9,5},{6,2},{10,6},{7,3},{11,7},{20,16},{24,20},... | collective-permute-start | bytes 1572872 | tf_op jit(solution)/shard_map/ppermute | solution.py:192
  70.8 5.1 %collective-permute-start.8 = (bf16[512,512]{0,1:T(8,128)(2,1)S(1)}, bf16[512,512]{0,1:T(8,128)(2,1)S(1)}, u32[]{:S(2)}, u32[]{:S(2)}) collective-permute-start(bf16[512,512]{0,1:T(8,128)(2,1)S(1)} %collective-permute-done.6), channel_id=1, source_target_pairs={{8,12},{9,13},{10,14},{11,15},{24,28},{25,29},{26,30},{27,31}} | collective-permute-start | bytes 1572872 | tf_op jit(solution)/shard_map/ppermute | solution.py:191
  71.6 14.5 %collective-permute-start.9 = (bf16[512,512]{0,1:T(8,128)(2,1)S(1)}, bf16[512,512]{0,1:T(8,128)(2,1)S(1)}, u32[]{:S(2)}, u32[]{:S(2)}) collective-permute-start(bf16[512,512]{0,1:T(8,128)(2,1)S(1)} %collective-permute-done.7), channel_id=1, source_target_pairs={{4,0},{5,1},{6,2},{7,3},{20,16},{21,17},{22,18},{23,19}} | collective-permute-start | bytes 1572872 | tf_op jit(solution)/shard_map/ppermute | solution.py:192
  89.4 1.4 copy-start.1
  90.7 22.0 %copy-start.6 = (bf16[1024]{0:T(1024)(128)(2,1)S(1)}, bf16[1024]{0:T(1024)(128)(2,1)}, u32[]{:S(2)}) copy-start(bf16[1024]{0:T(1024)(128)(2,1)} %param.45) | copy-start | bytes 6148
  90.8 2.1 %collective-permute-start.10 = (bf16[512,2,256]{0,2,1:T(8,128)(2,1)S(1)}, bf16[512,2,256]{0,2,1:T(8,128)(2,1)}, u32[]{:S(2)}, u32[]{:S(2)}) collective-permute-start(bf16[512,2,256]{0,2,1:T(8,128)(2,1)S(1)} %fusion.79), channel_id=1, source_target_pairs={{0,1},{1,0},{2,3},{3,2},{4,5},{5,4},{6,7},{7,6},{8,9},{9,8},{10,11... | collective-permute-start | bytes 1572872 | tf_op jit(solution)/shard_map/ppermute | solution.py:72
  95.2 8.7 %collective-permute-start.11 = (bf16[512,256]{0,1:T(8,128)(2,1)}, bf16[512,256]{0,1:T(8,128)(2,1)}, u32[]{:S(2)}, u32[]{:S(2)}) collective-permute-start(bf16[512,256]{0,1:T(8,128)(2,1)} %fusion.115), channel_id=1, source_target_pairs={{0,2},{1,3},{2,0},{3,1},{4,6},{5,7},{6,4},{7,5},{8,10},{9,11},{10,... | collective-permute-start | bytes 786440 | tf_op jit(solution)/shard_map/ppermute | solution.py:72
  104.9 7.8 %copy-start.2 = (bf16[512,256]{0,1:T(8,128)(2,1)}, bf16[512,256]{0,1:T(8,128)(2,1)S(1)}, u32[]{:S(2)}) copy-start(bf16[512,256]{0,1:T(8,128)(2,1)S(1)} %fusion.112) | copy-start | bytes 786436
  104.9 7.6 %collective-permute-start.12 = (bf16[512,256]{0,1:T(8,128)(2,1)S(1)}, bf16[512,256]{0,1:T(8,128)(2,1)S(1)}, u32[]{:S(2)}, u32[]{:S(2)}) collective-permute-start(bf16[512,256]{0,1:T(8,128)(2,1)S(1)} %fusion.112), channel_id=1, source_target_pairs={{0,2},{1,3},{2,0},{3,1},{4,6},{5,7},{6,4},{7,5},{8,10},{9,11},{10,... | collective-permute-start | bytes 786440 | tf_op jit(solution)/shard_map/ppermute | solution.py:86
  112.6 2.0 %collective-permute-start.13 = (bf16[512,2,256]{0,2,1:T(8,128)(2,1)S(1)}, bf16[512,2,256]{0,2,1:T(8,128)(2,1)S(1)}, u32[]{:S(2)}, u32[]{:S(2)}) collective-permute-start(bf16[512,2,256]{0,2,1:T(8,128)(2,1)S(1)} %pad_maximum_fusion.4), channel_id=1, source_target_pairs={{0,1},{1,0},{2,3},{3,2},{4,5},{5,4},{6,7},{7,6},{8,9},{9,8},{10,11... | collective-permute-start | bytes 1572872 | tf_op jit(solution)/shard_map/ppermute | solution.py:86
  121.4 13.2 %copy-start.3 = (bf16[512,256]{0,1:T(8,128)(2,1)S(1)}, bf16[512,256]{0,1:T(8,128)(2,1)}, u32[]{:S(2)}) copy-start(bf16[512,256]{0,1:T(8,128)(2,1)} %copy-done.2) | copy-start | bytes 786436
  122.7 2.0 %collective-permute-start.14 = (bf16[512,2,256]{0,2,1:T(8,128)(2,1)S(1)}, bf16[512,2,256]{0,2,1:T(8,128)(2,1)S(1)}, u32[]{:S(2)}, u32[]{:S(2)}) collective-permute-start(bf16[512,2,256]{0,2,1:T(8,128)(2,1)S(1)} %fusion.80), channel_id=1, source_target_pairs={{0,1},{1,0},{2,3},{3,2},{4,5},{5,4},{6,7},{7,6},{8,9},{9,8},{10,11... | collective-permute-start | bytes 1572872 | tf_op jit(solution)/shard_map/ppermute | solution.py:72
  126.1 8.4 %collective-permute-start.15 = (bf16[512,256]{0,1:T(8,128)(2,1)S(1)}, bf16[512,256]{0,1:T(8,128)(2,1)S(1)}, u32[]{:S(2)}, u32[]{:S(2)}) collective-permute-start(bf16[512,256]{0,1:T(8,128)(2,1)S(1)} %fusion.116), channel_id=1, source_target_pairs={{0,2},{1,3},{2,0},{3,1},{4,6},{5,7},{6,4},{7,5},{8,10},{9,11},{10,... | collective-permute-start | bytes 786440 | tf_op jit(solution)/shard_map/ppermute | solution.py:72

commit v5 on v3

--- a/solution.py
+++ b/solution.py
@@ -188,18 +188,23 @@
     row_max, row_mass, weighted = state
     attended = (weighted / jnp.transpose(row_mass, (0, 2, 1))[:, :, :, None]).astype(jnp.bfloat16)
     attended = attended.reshape(row_count, local_width)
-    partial_out = jnp.dot(attended, out_weight, preferred_element_type=jnp.float32)
-    out_sum = scatter_heads(partial_out, head_id, head_total)
-    stream_two = (stream.astype(jnp.float32) + out_sum).astype(jnp.bfloat16)
-    stream_two_full = gather_heads(stream_two, head_id, head_total)
-    normed_two = layer_norm(stream_two_full, gain_two).astype(jnp.bfloat16)
-    hidden = jax.nn.gelu(
-        jnp.dot(normed_two, up_weight, preferred_element_type=jnp.float32), approximate=True
-    ).astype(jnp.bfloat16)
-    lowered = jnp.dot(hidden, down_weight, preferred_element_type=jnp.float32)
-    mixed = scatter_heads(lowered, head_id, head_total)
-    return (stream_two.astype(jnp.float32) + mixed).astype(jnp.bfloat16)
-
+    chunk_count = 2 if row_count % 16 == 0 else 1
+    chunk_rows = row_count // chunk_count
+    outputs = []
+    for chunk in range(chunk_count):
+        rows = slice(chunk * chunk_rows, (chunk + 1) * chunk_rows)
+        partial_out = jnp.dot(attended[rows], out_weight, preferred_element_type=jnp.float32)
+        out_sum = scatter_heads(partial_out, head_id, head_total)
+        stream_two = (stream[rows].astype(jnp.float32) + out_sum).astype(jnp.bfloat16)
+        stream_two_full = gather_heads(stream_two, head_id, head_total)
+        normed_two = layer_norm(stream_two_full, gain_two).astype(jnp.bfloat16)
+        hidden = jax.nn.gelu(
+            jnp.dot(normed_two, up_weight, preferred_element_type=jnp.float32), approximate=True
+        ).astype(jnp.bfloat16)
+        lowered = jnp.dot(hidden, down_weight, preferred_element_type=jnp.float32)
+        mixed = scatter_heads(lowered, head_id, head_total)
+        outputs.append((stream_two.astype(jnp.float32) + mixed).astype(jnp.bfloat16))
+    return jnp.concatenate(outputs, axis=0)
 
 def solution(mesh):
     return jax.shard_map(

time: 131 us -> 129 us (0.985)
  waiting for transfers between devices: 67.9 us -> 60 us
  matrix products: 14.4 us -> 17.5 us
  starting transfers between devices: 16.3 us -> 18.8 us
    ppermute x4 -> x8, waiting for transfers between devices: 17.5 us -> 10.5 us  [scatter_heads(): lax.ppermute(give.astype(jnp.bfloat16), 'heads', [(i, i ^ bit) for i in r...]
    dot_general x1 -> x2, matrix products: 5.49 us -> 8.38 us  [shards(): lowered = jnp.dot(hidden, down_weight, preferred_element_type=jnp.float32)]
    ppermute x4 -> x8, starting transfers between devices: 3.64 us -> 5.6 us  [scatter_heads(): lax.ppermute(give.astype(jnp.bfloat16), 'heads', [(i, i ^ bit) for i in r...]
    unnamed x21 -> x15, local copies, waits for them, and re-layouts: 2.67 us -> 1.32 us
    convert_element_type x4 -> x8, local copies, waits for them, and re-layouts: 2.19 us -> 3.24 us  [scatter_heads(): give.astype(jnp.bfloat16)]
    ppermute x4 -> x6, waiting for transfers between devices: 13.6 us -> 12.7 us  [gather_heads(): lax.ppermute(current, 'heads', [(i, i ^ bit) for i in range(head_total)])]
    ppermute x4 -> x6, starting transfers between devices: 3.78 us -> 4.23 us  [gather_heads(): lax.ppermute(current, 'heads', [(i, i ^ bit) for i in range(head_total)])]
    add x2 -> x4, other arithmetic: 2.96 us -> 3.11 us  [scatter_heads(): current = keep + got.astype(jnp.float32)]
  transfers between devices with their start and end apart: 13 -> 19, of which waited for: 10 -> 13; matrix products, arithmetic and copies ran while one was open for 11% -> 19% of each run, Pallas kernels for 0% -> 0%
where the time goes in v5:
time: 129 us; the launch traced here: 128 us
  waiting for transfers between devices  60 us (47%)
  starting transfers between devices  18.8 us (15%)
  matrix products  17.5 us (14%)
  other arithmetic  15 us (12%)
  local copies, waits for them, and re-layouts  12.3 us (10%)
  between operations  4.44 us (3%)
    ppermute x3, waiting for transfers between devices, shards(): arriving = lax.ppermute(block, 'bricks', ring)  36.8 us
    ppermute x6, waiting for transfers between devices, gather_heads(): lax.ppermute(current, 'heads', [(i, i ^ bit) for i in range(head_total)])  12.7 us
    ppermute x8, waiting for transfers between devices, scatter_heads(): lax.ppermute(give.astype(jnp.bfloat16), 'heads', [(i, i ^ bit) for i in r...  10.5 us
    dot_general x2, matrix products, shards(): lowered = jnp.dot(hidden, down_weight, preferred_element_type=jnp.float32)  8.38 us
    ppermute x8, starting transfers between devices, scatter_heads(): lax.ppermute(give.astype(jnp.bfloat16), 'heads', [(i, i ^ bit) for i in r...  5.6 us
    ppermute x1, starting transfers between devices, extended_2(): before = lax.ppermute(last, axis, up)  5.56 us
    ppermute x6, starting transfers between devices, gather_heads(): lax.ppermute(current, 'heads', [(i, i ^ bit) for i in range(head_total)])  4.23 us
    dot_general x4, matrix products, absorb_block(): jnp.einsum('bhqk,khd->bqhd', weights.astype(jnp.bfloat16), value_rows, pr...  3.95 us
  transfers between devices with their start and end apart: 19, of which 13 were waited for; matrix products, arithmetic and copies ran while one was open for 19% of the time, Pallas kernels for 0%

profile of v5, /device:TPU:0, one launch (start us, length us, event | category | flops | bytes accessed | tf_op | source)
XLA Modules:
  0.0 128.0 jit_solution(5209106092133280510)
XLA Ops:
  0.0 0.9 fusion.159
  0.9 1.3 %collective-permute-start.1 = (bf16[64,256]{1,0:T(8,128)(2,1)S(1)}, bf16[64,256]{1,0:T(8,128)(2,1)S(1)}, u32[]{:S(2)}, u32[]{:S(2)}) collective-permute-start(bf16[64,256]{1,0:T(8,128)(2,1)S(1)} %get-tuple-element.195), channel_id=1, source_target_pairs={{4,0},{8,4},{12,8},{5,1},{9,5},{13,9},{6,2},{10,6},{14,10},{7,3},{... | collective-permute-start | bytes 98312 | tf_op jit(solution)/shard_map/ppermute | solution.py:21
  2.2 5.6 %collective-permute-start = (bf16[64,256]{1,0:T(8,128)(2,1)S(1)}, bf16[64,256]{1,0:T(8,128)(2,1)S(1)}, u32[]{:S(2)}, u32[]{:S(2)}) collective-permute-start(bf16[64,256]{1,0:T(8,128)(2,1)S(1)} %get-tuple-element.194), channel_id=1, source_target_pairs={{0,4},{4,8},{8,12},{1,5},{5,9},{9,13},{2,6},{6,10},{10,14},{3,7},{... | collective-permute-start | bytes 98312 | tf_op jit(solution)/shard_map/ppermute | solution.py:20
  7.8 1.0 fusion.160
  8.8 0.9 fusion.161
  9.7 1.1 copy.29
  10.8 1.4 %fusion.163 = (s32[1]{0:T(128)}, s32[1]{0:T(128)}) fusion(s32[4]{0:T(128)} %param.32, s32[]{:T(128)} %bitcast.2, s32[]{:T(128)} %bitcast.6), kind=kLoop, calls=%fused_computation.260 | loop fusion | bytes 24 | tf_op jit(solution)/shard_map/jit(_take)/gather | solution.py:146
  13.6 0.7 convert_element_type.205
  14.6 1.7 %fusion.75 = f32[1,8,8,8,256]{4,3,2,1,0:T(8,128)S(1)} fusion(f32[1,10,10,10,256]{4,3,2,1,0:T(8,128)S(1)} %select_maximum_fusion, f32[1,1,8,8,256]{4,3,2,1,0:T(8,128)S(1)} %multiply_bitcast_fusion, f32[1,8,8,8,256]{4,3,2,1,0:T(8,128)S(1)} %bitcast.434, f32[1,1,8,8,256]{4,3,2,1,0:T(8,128)S(1)} %multiply_bitcast_fusion.1, f32[256]{0:T(256)S(1)} %bitcast.485, ...), kind=kLoop, calls=%fused_computation.90 | loop fusion | flops 7208960 | bytes 13790208 | tf_op jit(solution)/shard_map/add | solution.py:51
  16.6 2.0 %collective-permute-start.2 = (bf16[512,256]{0,1:T(8,128)(2,1)S(1)}, bf16[512,256]{0,1:T(8,128)(2,1)S(1)}, u32[]{:S(2)}, u32[]{:S(2)}) collective-permute-start(bf16[512,256]{0,1:T(8,128)(2,1)S(1)} %add_convert_fusion), channel_id=1, source_target_pairs={{0,2},{1,3},{2,0},{3,1},{4,6},{5,7},{6,4},{7,5},{8,10},{9,11},{10,... | collective-permute-start | bytes 786440 | tf_op jit(solution)/shard_map/ppermute | solution.py:86
  18.6 5.8 %collective-permute-done.2 = bf16[512,256]{0,1:T(8,128)(2,1)S(1)} collective-permute-done((bf16[512,256]{0,1:T(8,128)(2,1)S(1)}, bf16[512,256]{0,1:T(8,128)(2,1)S(1)}, u32[]{:S(2)}, u32[]{:S(2)}) %collective-permute-start.2) | collective-permute-done | bytes 262176 | tf_op jit(solution)/shard_map/ppermute | solution.py:86
  24.5 0.8 pad_maximum_fusion.2
  25.4 0.6 fusion.162
  28.5 1.2 copy.59
  29.8 1.1 select_bitcast_fusion.1
  31.5 0.3 multiply_reduce_fusion
  32.3 0.5 convolution_convert_fusion.2
  32.8 0.5 convolution_convert_fusion.1
  33.3 0.8 bitcast_reduce_fusion.3
  34.1 0.5 convolution_convert_fusion
  34.6 1.8 %collective-permute-start.4 = (bf16[512,512]{0,1:T(8,128)(2,1)S(1)}, bf16[512,512]{0,1:T(8,128)(2,1)S(1)}, u32[]{:S(2)}, u32[]{:S(2)}) collective-permute-start(bf16[512,512]{0,1:T(8,128)(2,1)S(1)} %pad_maximum_fusion.3), channel_id=1, source_target_pairs={{0,4},{4,8},{8,12},{12,0},{1,5},{5,9},{9,13},{13,1},{2,6},{6,10},{... | collective-permute-start | bytes 1572872 | tf_op jit(solution)/shard_map/ppermute | solution.py:181
  36.4 0.8 fusion.5
  37.3 1.0 fusion.46
  38.3 12.5 %collective-permute-done.4 = bf16[512,512]{0,1:T(8,128)(2,1)S(1)} collective-permute-done((bf16[512,512]{0,1:T(8,128)(2,1)S(1)}, bf16[512,512]{0,1:T(8,128)(2,1)S(1)}, u32[]{:S(2)}, u32[]{:S(2)}) %collective-permute-start.4) | collective-permute-done | bytes 524320 | tf_op jit(solution)/shard_map/ppermute | solution.py:181
  50.9 0.8 bitcast_reduce_fusion.2
  51.7 0.8 fusion.7
  52.6 1.0 fusion.40
  53.7 12.6 %collective-permute-done.5 = bf16[512,512]{0,1:T(8,128)(2,1)S(1)} collective-permute-done((bf16[512,512]{0,1:T(8,128)(2,1)S(1)}, bf16[512,512]{0,1:T(8,128)(2,1)S(1)}, u32[]{:S(2)}, u32[]{:S(2)}) %collective-permute-start.5) | collective-permute-done | bytes 524320 | tf_op jit(solution)/shard_map/ppermute | solution.py:181
  66.5 0.8 bitcast_reduce_fusion.1
  67.3 0.8 fusion.9
  68.2 1.0 fusion.37
  69.3 11.7 %collective-permute-done.6 = bf16[512,512]{0,1:T(8,128)(2,1)S(1)} collective-permute-done((bf16[512,512]{0,1:T(8,128)(2,1)S(1)}, bf16[512,512]{0,1:T(8,128)(2,1)S(1)}, u32[]{:S(2)}, u32[]{:S(2)}) %collective-permute-start.6) | collective-permute-done | bytes 524320 | tf_op jit(solution)/shard_map/ppermute | solution.py:181
  81.0 0.8 bitcast_reduce_fusion
  81.8 0.8 fusion.10
  82.7 1.0 divide_convert_fusion
  83.7 0.3 fusion.168
  84.1 0.3 fusion.169
  84.5 0.6 collective-permute-start.13
  85.0 0.6 collective-permute-done.7
  85.7 1.7 %collective-permute-start.8 = (bf16[256,256]{0,1:T(8,128)(2,1)S(1)}, bf16[256,256]{0,1:T(8,128)(2,1)S(1)}, u32[]{:S(2)}, u32[]{:S(2)}) collective-permute-start(bf16[256,256]{0,1:T(8,128)(2,1)S(1)} %fusion.126), channel_id=1, source_target_pairs={{0,2},{1,3},{2,0},{3,1},{4,6},{5,7},{6,4},{7,5},{8,10},{9,11},{10,... | collective-permute-start | bytes 393224 | tf_op jit(solution)/shard_map/ppermute | solution.py:72
  87.5 0.9 bitcast_add_fusion.1
  88.3 1.0 fusion.128
  89.3 0.5 collective-permute-start.14
  89.8 1.6 %collective-permute-done.8 = bf16[256,256]{0,1:T(8,128)(2,1)S(1)} collective-permute-done((bf16[256,256]{0,1:T(8,128)(2,1)S(1)}, bf16[256,256]{0,1:T(8,128)(2,1)S(1)}, u32[]{:S(2)}, u32[]{:S(2)}) %collective-permute-start.8) | collective-permute-done | bytes 131104 | tf_op jit(solution)/shard_map/ppermute | solution.py:72
  91.3 3.3 %collective-permute-done.14 = bf16[256,256]{0,1:T(8,128)(2,1)S(1)} collective-permute-done((bf16[256,256]{0,1:T(8,128)(2,1)S(1)}, bf16[256,256]{0,1:T(8,128)(2,1)S(1)}, u32[]{:S(2)}, u32[]{:S(2)}) %collective-permute-start.14) | collective-permute-done | bytes 131104 | tf_op jit(solution)/shard_map/ppermute | solution.py:72
  94.6 1.0 fusion.123
  95.6 1.3 collective-permute-start.15
  96.9 0.8 collective-permute-start.9
  97.7 4.1 %collective-permute-done.15 = bf16[256,256]{0,1:T(8,128)(2,1)S(1)} collective-permute-done((bf16[256,256]{0,1:T(8,128)(2,1)S(1)}, bf16[256,256]{0,1:T(8,128)(2,1)S(1)}, u32[]{:S(2)}, u32[]{:S(2)}) %collective-permute-start.15) | collective-permute-done | bytes 131104 | tf_op jit(solution)/shard_map/ppermute | solution.py:86
  101.9 1.3 collective-permute-done.9
  103.5 1.4 %collective-permute-done.10 = bf16[256,2,256]{0,2,1:T(8,128)(2,1)S(1)} collective-permute-done((bf16[256,2,256]{0,2,1:T(8,128)(2,1)S(1)}, bf16[256,2,256]{0,2,1:T(8,128)(2,1)S(1)}, u32[]{:S(2)}, u32[]{:S(2)}) %collective-permute-start.10) | collective-permute-done | bytes 262176 | tf_op jit(solution)/shard_map/ppermute | solution.py:86
  106.0 0.3 fusion.70
  106.3 4.2 %fusion.71 = f32[256,1024]{0,1:T(8,128)} fusion(bf16[1024,1024]{1,0:T(8,128)(2,1)S(1)} %copy-done, bf16[256,1024]{0,1:T(8,128)(2,1)S(1)} %get-tuple-element.230, bf16[1024,1024]{1,0:T(8,128)(2,1)} %param.42), kind=kOutput, calls=%fused_computation.87 | convolution fusion | flops 1076101120 | bytes 5767168 | tf_op jit(solution)/shard_map/dot_general | solution.py:204
  110.5 1.1 fusion.115
  111.8 4.2 %fusion.73 = f32[256,1024]{0,1:T(8,128)} fusion(bf16[1024,1024]{1,0:T(8,128)(2,1)S(1)} %copy-done, bf16[256,1024]{0,1:T(8,128)(2,1)S(1)} %get-tuple-element.229, bf16[1024,1024]{1,0:T(8,128)(2,1)} %param.42), kind=kOutput, calls=%fused_computation.88 | convolution fusion | flops 1076101120 | bytes 5767168 | tf_op jit(solution)/shard_map/dot_general | solution.py:204
  116.0 1.1 fusion.114
  117.1 0.4 collective-permute-start.11
  117.5 1.1 bitcast_add_fusion
  118.6 1.7 %collective-permute-start.18 = (bf16[256,256]{0,1:T(8,128)(2,1)S(1)}, bf16[256,256]{0,1:T(8,128)(2,1)S(1)}, u32[]{:S(2)}, u32[]{:S(2)}) collective-permute-start(bf16[256,256]{0,1:T(8,128)(2,1)S(1)} %fusion.129), channel_id=1, source_target_pairs={{0,2},{1,3},{2,0},{3,1},{4,6},{5,7},{6,4},{7,5},{8,10},{9,11},{10,... | collective-permute-start | bytes 393224 | tf_op jit(solution)/shard_map/ppermute | solution.py:72
  120.4 1.1 bitcast_add_fusion.2
  121.5 0.4 collective-permute-start.12
  121.9 2.5 %collective-permute-done.18 = bf16[256,256]{0,1:T(8,128)(2,1)S(1)} collective-permute-done((bf16[256,256]{0,1:T(8,128)(2,1)S(1)}, bf16[256,256]{0,1:T(8,128)(2,1)S(1)}, u32[]{:S(2)}, u32[]{:S(2)}) %collective-permute-start.18) | collective-permute-done | bytes 131104 | tf_op jit(solution)/shard_map/ppermute | solution.py:72
  124.4 2.6 %collective-permute-done.12 = bf16[256,256]{0,1:T(8,128)(2,1)S(1)} collective-permute-done((bf16[256,256]{0,1:T(8,128)(2,1)S(1)}, bf16[256,256]{0,1:T(8,128)(2,1)S(1)}, u32[]{:S(2)}, u32[]{:S(2)}) %collective-permute-start.12) | collective-permute-done | bytes 131104 | tf_op jit(solution)/shard_map/ppermute | solution.py:72
  127.1 0.8 copy.48
  (84 shorter events, 4.6 us)
Async XLA Ops:
  0.0 106.3 %copy-start = (bf16[1024,1024]{1,0:T(8,128)(2,1)S(1)}, bf16[1024,1024]{1,0:T(8,128)(2,1)}, u32[]{:S(2)}) copy-start(bf16[1024,1024]{1,0:T(8,128)(2,1)} %param.43) | copy-start | bytes 6291460
  0.9 13.3 %collective-permute-start.1 = (bf16[64,256]{1,0:T(8,128)(2,1)S(1)}, bf16[64,256]{1,0:T(8,128)(2,1)S(1)}, u32[]{:S(2)}, u32[]{:S(2)}) collective-permute-start(bf16[64,256]{1,0:T(8,128)(2,1)S(1)} %get-tuple-element.195), channel_id=1, source_target_pairs={{4,0},{8,4},{12,8},{5,1},{9,5},{13,9},{6,2},{10,6},{14,10},{7,3},{... | collective-permute-start | bytes 98312 | tf_op jit(solution)/shard_map/ppermute | solution.py:21
  2.2 12.1 %collective-permute-start = (bf16[64,256]{1,0:T(8,128)(2,1)S(1)}, bf16[64,256]{1,0:T(8,128)(2,1)S(1)}, u32[]{:S(2)}, u32[]{:S(2)}) collective-permute-start(bf16[64,256]{1,0:T(8,128)(2,1)S(1)} %get-tuple-element.194), channel_id=1, source_target_pairs={{0,4},{4,8},{8,12},{1,5},{5,9},{9,13},{2,6},{6,10},{10,14},{3,7},{... | collective-permute-start | bytes 98312 | tf_op jit(solution)/shard_map/ppermute | solution.py:20
  16.2 9.1 %copy-start.1 = (bf16[1024]{0:T(1024)(128)(2,1)S(1)}, bf16[1024]{0:T(1024)(128)(2,1)}, u32[]{:S(2)}) copy-start(bf16[1024]{0:T(1024)(128)(2,1)} %param.36) | copy-start | bytes 6148
  16.3 9.1 %copy-start.3 = (s32[4,4]{1,0:T(4,128)S(1)}, s32[4,4]{1,0:T(4,128)}, u32[]{:S(2)}) copy-start(s32[4,4]{1,0:T(4,128)} %param.33) | copy-start | bytes 196
  16.6 7.8 %collective-permute-start.2 = (bf16[512,256]{0,1:T(8,128)(2,1)S(1)}, bf16[512,256]{0,1:T(8,128)(2,1)S(1)}, u32[]{:S(2)}, u32[]{:S(2)}) collective-permute-start(bf16[512,256]{0,1:T(8,128)(2,1)S(1)} %add_convert_fusion), channel_id=1, source_target_pairs={{0,2},{1,3},{2,0},{3,1},{4,6},{5,7},{6,4},{7,5},{8,10},{9,11},{10,... | collective-permute-start | bytes 786440 | tf_op jit(solution)/shard_map/ppermute | solution.py:86
  25.3 4.5 %collective-permute-start.3 = (bf16[512,2,256]{0,2,1:T(8,128)(2,1)}, bf16[512,2,256]{0,2,1:T(8,128)(2,1)}, u32[]{:S(2)}, u32[]{:S(2)}) collective-permute-start(bf16[512,2,256]{0,2,1:T(8,128)(2,1)} %pad_maximum_fusion.2), channel_id=1, source_target_pairs={{0,1},{1,0},{2,3},{3,2},{4,5},{5,4},{6,7},{7,6},{8,9},{9,8},{10,11... | collective-permute-start | bytes 1572872 | tf_op jit(solution)/shard_map/ppermute | solution.py:86
  31.3 1.0 copy-start.4
  31.3 1.5 %copy-start.5 = (bf16[1024,256]{1,0:T(8,128)(2,1)S(1)}, bf16[1024,256]{1,0:T(8,128)(2,1)}, u32[]{:S(2)}) copy-start(bf16[1024,256]{1,0:T(8,128)(2,1)} %param.37) | copy-start | bytes 1572868
  32.3 1.8 %copy-start.6 = (bf16[1024,256]{1,0:T(8,128)(2,1)S(1)}, bf16[1024,256]{1,0:T(8,128)(2,1)}, u32[]{:S(2)}) copy-start(bf16[1024,256]{1,0:T(8,128)(2,1)} %param.39) | copy-start | bytes 1572868
  34.6 16.2 %collective-permute-start.4 = (bf16[512,512]{0,1:T(8,128)(2,1)S(1)}, bf16[512,512]{0,1:T(8,128)(2,1)S(1)}, u32[]{:S(2)}, u32[]{:S(2)}) collective-permute-start(bf16[512,512]{0,1:T(8,128)(2,1)S(1)} %pad_maximum_fusion.3), channel_id=1, source_target_pairs={{0,4},{4,8},{8,12},{12,0},{1,5},{5,9},{9,13},{13,1},{2,6},{6,10},{... | collective-permute-start | bytes 1572872 | tf_op jit(solution)/shard_map/ppermute | solution.py:181
  50.9 15.4 %collective-permute-start.5 = (bf16[512,512]{0,1:T(8,128)(2,1)S(1)}, bf16[512,512]{0,1:T(8,128)(2,1)S(1)}, u32[]{:S(2)}, u32[]{:S(2)}) collective-permute-start(bf16[512,512]{0,1:T(8,128)(2,1)S(1)} %collective-permute-done.4), channel_id=1, source_target_pairs={{0,4},{4,8},{8,12},{12,0},{1,5},{5,9},{9,13},{13,1},{2,6},{6,10},{... | collective-permute-start | bytes 1572872 | tf_op jit(solution)/shard_map/ppermute | solution.py:181
  66.3 14.7 %collective-permute-start.6 = (bf16[512,512]{0,1:T(8,128)(2,1)S(1)}, bf16[512,512]{0,1:T(8,128)(2,1)S(1)}, u32[]{:S(2)}, u32[]{:S(2)}) collective-permute-start(bf16[512,512]{0,1:T(8,128)(2,1)S(1)} %collective-permute-done.5), channel_id=1, source_target_pairs={{0,4},{4,8},{8,12},{12,0},{1,5},{5,9},{9,13},{13,1},{2,6},{6,10},{... | collective-permute-start | bytes 1572872 | tf_op jit(solution)/shard_map/ppermute | solution.py:181
  84.0 1.6 %collective-permute-start.7 = (bf16[256,2,256]{0,2,1:T(8,128)(2,1)S(1)}, bf16[256,2,256]{0,2,1:T(8,128)(2,1)S(1)}, u32[]{:S(2)}, u32[]{:S(2)}) collective-permute-start(bf16[256,2,256]{0,2,1:T(8,128)(2,1)S(1)} %fusion.112), channel_id=1, source_target_pairs={{0,1},{1,0},{2,3},{3,2},{4,5},{5,4},{6,7},{7,6},{8,9},{9,8},{10,11... | collective-permute-start | bytes 786440 | tf_op jit(solution)/shard_map/ppermute | solution.py:72
  84.1 19.2 %copy-start.2 = (bf16[1024]{0:T(1024)(128)(2,1)S(1)}, bf16[1024]{0:T(1024)(128)(2,1)}, u32[]{:S(2)}) copy-start(bf16[1024]{0:T(1024)(128)(2,1)} %param.41) | copy-start | bytes 6148
  84.5 3.0 %collective-permute-start.13 = (bf16[256,2,256]{0,2,1:T(8,128)(2,1)S(1)}, bf16[256,2,256]{0,2,1:T(8,128)(2,1)S(1)}, u32[]{:S(2)}, u32[]{:S(2)}) collective-permute-start(bf16[256,2,256]{0,2,1:T(8,128)(2,1)S(1)} %fusion.113), channel_id=1, source_target_pairs={{0,1},{1,0},{2,3},{3,2},{4,5},{5,4},{6,7},{7,6},{8,9},{9,8},{10,11... | collective-permute-start | bytes 786440 | tf_op jit(solution)/shard_map/ppermute | solution.py:72
  85.7 5.6 %collective-permute-start.8 = (bf16[256,256]{0,1:T(8,128)(2,1)S(1)}, bf16[256,256]{0,1:T(8,128)(2,1)S(1)}, u32[]{:S(2)}, u32[]{:S(2)}) collective-permute-start(bf16[256,256]{0,1:T(8,128)(2,1)S(1)} %fusion.126), channel_id=1, source_target_pairs={{0,2},{1,3},{2,0},{3,1},{4,6},{5,7},{6,4},{7,5},{8,10},{9,11},{10,... | collective-permute-start | bytes 393224 | tf_op jit(solution)/shard_map/ppermute | solution.py:72
  89.3 5.3 %collective-permute-start.14 = (bf16[256,256]{0,1:T(8,128)(2,1)S(1)}, bf16[256,256]{0,1:T(8,128)(2,1)S(1)}, u32[]{:S(2)}, u32[]{:S(2)}) collective-permute-start(bf16[256,256]{0,1:T(8,128)(2,1)S(1)} %fusion.128), channel_id=1, source_target_pairs={{0,2},{1,3},{2,0},{3,1},{4,6},{5,7},{6,4},{7,5},{8,10},{9,11},{10,... | collective-permute-start | bytes 393224 | tf_op jit(solution)/shard_map/ppermute | solution.py:72
  95.6 6.2 %collective-permute-start.15 = (bf16[256,256]{0,1:T(8,128)(2,1)S(1)}, bf16[256,256]{0,1:T(8,128)(2,1)S(1)}, u32[]{:S(2)}, u32[]{:S(2)}) collective-permute-start(bf16[256,256]{0,1:T(8,128)(2,1)S(1)} %get-tuple-element.189), channel_id=1, source_target_pairs={{0,2},{1,3},{2,0},{3,1},{4,6},{5,7},{6,4},{7,5},{8,10},{9,11},{10,... | collective-permute-start | bytes 393224 | tf_op jit(solution)/shard_map/ppermute | solution.py:86
  96.9 6.3 %collective-permute-start.9 = (bf16[256,256]{0,1:T(8,128)(2,1)S(1)}, bf16[256,256]{0,1:T(8,128)(2,1)S(1)}, u32[]{:S(2)}, u32[]{:S(2)}) collective-permute-start(bf16[256,256]{0,1:T(8,128)(2,1)S(1)} %get-tuple-element.188), channel_id=1, source_target_pairs={{0,2},{1,3},{2,0},{3,1},{4,6},{5,7},{6,4},{7,5},{8,10},{9,11},{10,... | collective-permute-start | bytes 393224 | tf_op jit(solution)/shard_map/ppermute | solution.py:86
  101.9 1.6 %collective-permute-start.16 = (bf16[256,2,256]{0,2,1:T(8,128)(2,1)S(1)}, bf16[256,2,256]{0,2,1:T(8,128)(2,1)S(1)}, u32[]{:S(2)}, u32[]{:S(2)}) collective-permute-start(bf16[256,2,256]{0,2,1:T(8,128)(2,1)S(1)} %pad_maximum_fusion.5), channel_id=1, source_target_pairs={{0,1},{1,0},{2,3},{3,2},{4,5},{5,4},{6,7},{7,6},{8,9},{9,8},{10,11... | collective-permute-start | bytes 786440 | tf_op jit(solution)/shard_map/ppermute | solution.py:86
  103.3 1.6 %collective-permute-start.10 = (bf16[256,2,256]{0,2,1:T(8,128)(2,1)S(1)}, bf16[256,2,256]{0,2,1:T(8,128)(2,1)S(1)}, u32[]{:S(2)}, u32[]{:S(2)}) collective-permute-start(bf16[256,2,256]{0,2,1:T(8,128)(2,1)S(1)} %pad_maximum_fusion.4), channel_id=1, source_target_pairs={{0,1},{1,0},{2,3},{3,2},{4,5},{5,4},{6,7},{7,6},{8,9},{9,8},{10,11... | collective-permute-start | bytes 786440 | tf_op jit(solution)/shard_map/ppermute | solution.py:86
  111.6 5.9 %collective-permute-start.17 = (bf16[256,2,256]{0,2,1:T(8,128)(2,1)S(1)}, bf16[256,2,256]{0,2,1:T(8,128)(2,1)S(1)}, u32[]{:S(2)}, u32[]{:S(2)}) collective-permute-start(bf16[256,2,256]{0,2,1:T(8,128)(2,1)S(1)} %fusion.115), channel_id=1, source_target_pairs={{0,1},{1,0},{2,3},{3,2},{4,5},{5,4},{6,7},{7,6},{8,9},{9,8},{10,11... | collective-permute-start | bytes 786440 | tf_op jit(solution)/shard_map/ppermute | solution.py:72
  117.1 3.3 %collective-permute-start.11 = (bf16[256,2,256]{0,2,1:T(8,128)(2,1)S(1)}, bf16[256,2,256]{0,2,1:T(8,128)(2,1)S(1)}, u32[]{:S(2)}, u32[]{:S(2)}) collective-permute-start(bf16[256,2,256]{0,2,1:T(8,128)(2,1)S(1)} %fusion.114), channel_id=1, source_target_pairs={{0,1},{1,0},{2,3},{3,2},{4,5},{5,4},{6,7},{7,6},{8,9},{9,8},{10,11... | collective-permute-start | bytes 786440 | tf_op jit(solution)/shard_map/ppermute | solution.py:72
  118.6 5.7 %collective-permute-start.18 = (bf16[256,256]{0,1:T(8,128)(2,1)S(1)}, bf16[256,256]{0,1:T(8,128)(2,1)S(1)}, u32[]{:S(2)}, u32[]{:S(2)}) collective-permute-start(bf16[256,256]{0,1:T(8,128)(2,1)S(1)} %fusion.129), channel_id=1, source_target_pairs={{0,2},{1,3},{2,0},{3,1},{4,6},{5,7},{6,4},{7,5},{8,10},{9,11},{10,... | collective-permute-start | bytes 393224 | tf_op jit(solution)/shard_map/ppermute | solution.py:72
  121.5 5.5 %collective-permute-start.12 = (bf16[256,256]{0,1:T(8,128)(2,1)S(1)}, bf16[256,256]{0,1:T(8,128)(2,1)S(1)}, u32[]{:S(2)}, u32[]{:S(2)}) collective-permute-start(bf16[256,256]{0,1:T(8,128)(2,1)S(1)} %fusion.127), channel_id=1, source_target_pairs={{0,2},{1,3},{2,0},{3,1},{4,6},{5,7},{6,4},{7,5},{8,10},{9,11},{10,... | collective-permute-start | bytes 393224 | tf_op jit(solution)/shard_map/ppermute | solution.py:72

commit v6 on v5

--- a/solution.py
+++ b/solution.py
@@ -155,36 +155,48 @@
     stream = (voxel_feats.astype(jnp.float32) + conv_out).astype(jnp.bfloat16)
     head_total = lax.axis_size("heads")
     head_id = lax.axis_index("heads")
-    stream_full = gather_heads(stream, head_id, head_total)
-    normed = layer_norm(stream_full, gain_one).astype(jnp.bfloat16)
-    queries = jnp.dot(normed, query_weight, preferred_element_type=jnp.float32).astype(jnp.bfloat16)
     head_count = local_width // HEAD_DIM
-    keys_all = jnp.dot(normed, key_weight, preferred_element_type=jnp.float32).astype(jnp.bfloat16)
-    values_all = jnp.dot(normed, value_weight, preferred_element_type=jnp.float32).astype(
-        jnp.bfloat16
-    )
-    pair_local = jnp.concatenate([keys_all, values_all], axis=1)
     brick_dev = lax.axis_index("bricks")
     dev_total = lax.axis_size("bricks")
-    key_total = pattern.shape[1]
-    query_heads = queries.reshape(local_bricks, brick_rows, head_count, HEAD_DIM)
+    ring = [(i, (i + 1) % dev_total) for i in range(dev_total)]
+    pair_weight = jnp.concatenate([key_weight, value_weight], axis=1)
     linked_rows = lax.dynamic_slice_in_dim(pattern, first_brick, local_bricks, 0)
     state = (
         jnp.full((local_bricks, head_count, brick_rows), -1e30, jnp.float32),
         jnp.zeros((local_bricks, head_count, brick_rows), jnp.float32),
         jnp.zeros((local_bricks, brick_rows, head_count, HEAD_DIM), jnp.float32),
     )
-    ring = [(i, (i + 1) % dev_total) for i in range(dev_total)]
-    block = pair_local
+    if dev_total > 1:
+        ring_block = lax.ppermute(stream, "bricks", ring)
+    full_now = gather_heads(stream, head_id, head_total)
+    query_heads = None
     for step in range(dev_total):
-        if step + 1 < dev_total:
-            arriving = lax.ppermute(block, "bricks", ring)
+        normed_now = layer_norm(full_now, gain_one).astype(jnp.bfloat16)
+        if step == 0:
+            queries = jnp.dot(normed_now, query_weight, preferred_element_type=jnp.float32).astype(
+                jnp.bfloat16
+            )
+            query_heads = queries.reshape(local_bricks, brick_rows, head_count, HEAD_DIM)
+        pair_block = jnp.dot(normed_now, pair_weight, preferred_element_type=jnp.float32).astype(
+            jnp.bfloat16
+        )
         source = (brick_dev - step) % dev_total
         key_ids = source * local_bricks + jnp.arange(local_bricks, dtype=jnp.int32)
         linked = jnp.take(linked_rows, key_ids, axis=1) > 0
-        state = absorb_block(state, query_heads, block, linked, head_count, brick_rows, local_width)
+        state = absorb_block(
+            state, query_heads, pair_block, linked, head_count, brick_rows, local_width
+        )
         if step + 1 < dev_total:
-            state, block = lax.optimization_barrier((state, arriving))
+            arrived = ring_block
+            if step + 2 < dev_total:
+                ring_block = lax.ppermute(arrived, "bricks", ring)
+            full_next = gather_heads(arrived, head_id, head_total)
+            if step + 2 < dev_total:
+                state, full_now, ring_block = lax.optimization_barrier(
+                    (state, full_next, ring_block)
+                )
+            else:
+                state, full_now = lax.optimization_barrier((state, full_next))
     row_max, row_mass, weighted = state
     attended = (weighted / jnp.transpose(row_mass, (0, 2, 1))[:, :, :, None]).astype(jnp.bfloat16)
     attended = attended.reshape(row_count, local_width)

time: 129 us -> 124 us (0.961)
  waiting for transfers between devices: 60 us -> 42.3 us
  other arithmetic: 15 us -> 18.5 us
  starting transfers between devices: 18.8 us -> 22.3 us
  matrix products: 17.5 us -> 20.3 us
  local copies, waits for them, and re-layouts: 12.3 us -> 14.9 us
    ppermute x3, waiting for transfers between devices: 36.8 us -> 10.1 us  [the longest x1 6.05 us: shards(): ring_block = lax.ppermute(stream, 'bricks', ring)]
    ppermute x6 -> x12, waiting for transfers between devices: 12.7 us -> 20.9 us  [gather_heads(): lax.ppermute(current, 'heads', [(i, i ^ bit) for i in range(head_total)])]
    ppermute x6 -> x12, starting transfers between devices: 4.23 us -> 7.77 us  [gather_heads(): lax.ppermute(current, 'heads', [(i, i ^ bit) for i in range(head_total)])]
    another operation x8 -> x20, other arithmetic: 2.19 us -> 5.08 us  [gather_heads(): current = jnp.stack([low, high], axis=current.ndim - 1)]
    dot_general x3 -> x5, matrix products: 1.45 us -> 4.04 us  [the longest x4 3.56 us: shards(): jnp.dot(normed_now, pair_weight, preferred_element_type=jnp.float32)]
  transfers between devices with their start and end apart: 19 -> 25, of which waited for: 13 -> 17; matrix products, arithmetic and copies ran while one was open for 19% -> 29% of each run, Pallas kernels for 0% -> 0%
where the time goes in v6:
time: 124 us; the launch traced here: 123 us
  waiting for transfers between devices  42.3 us (34%)
  starting transfers between devices  22.3 us (18%)
  matrix products  20.3 us (16%)
  other arithmetic  18.5 us (15%)
  local copies, waits for them, and re-layouts  14.9 us (12%)
  between operations  4.61 us (4%)
    ppermute x12, waiting for transfers between devices, gather_heads(): lax.ppermute(current, 'heads', [(i, i ^ bit) for i in range(head_total)])  20.9 us
    ppermute x8, waiting for transfers between devices, scatter_heads(): lax.ppermute(give.astype(jnp.bfloat16), 'heads', [(i, i ^ bit) for i in r...  11.3 us
    dot_general x2, matrix products, shards(): lowered = jnp.dot(hidden, down_weight, preferred_element_type=jnp.float32)  8.38 us
    ppermute x12, starting transfers between devices, gather_heads(): lax.ppermute(current, 'heads', [(i, i ^ bit) for i in range(head_total)])  7.77 us
    ppermute x1, waiting for transfers between devices, shards(): ring_block = lax.ppermute(stream, 'bricks', ring)  6.05 us
    ppermute x8, starting transfers between devices, scatter_heads(): lax.ppermute(give.astype(jnp.bfloat16), 'heads', [(i, i ^ bit) for i in r...  5.6 us
    ppermute x1, starting transfers between devices, extended_2(): before = lax.ppermute(last, axis, up)  5.56 us
    another operation x20, other arithmetic, gather_heads(): current = jnp.stack([low, high], axis=current.ndim - 1)  5.08 us
  transfers between devices with their start and end apart: 25, of which 17 were waited for; matrix products, arithmetic and copies ran while one was open for 29% of the time, Pallas kernels for 0%

profile of v6, /device:TPU:0, one launch (start us, length us, event | category | flops | bytes accessed | tf_op | source)
XLA Modules:
  0.0 123.0 jit_solution(12751846469516198201)
XLA Ops:
  0.0 0.9 fusion.194
  0.9 1.3 %collective-permute-start.1 = (bf16[64,256]{1,0:T(8,128)(2,1)S(1)}, bf16[64,256]{1,0:T(8,128)(2,1)S(1)}, u32[]{:S(2)}, u32[]{:S(2)}) collective-permute-start(bf16[64,256]{1,0:T(8,128)(2,1)S(1)} %get-tuple-element.213), channel_id=1, source_target_pairs={{4,0},{8,4},{12,8},{5,1},{9,5},{13,9},{6,2},{10,6},{14,10},{7,3},{... | collective-permute-start | bytes 98312 | tf_op jit(solution)/shard_map/ppermute | solution.py:21
  2.2 5.6 %collective-permute-start = (bf16[64,256]{1,0:T(8,128)(2,1)S(1)}, bf16[64,256]{1,0:T(8,128)(2,1)S(1)}, u32[]{:S(2)}, u32[]{:S(2)}) collective-permute-start(bf16[64,256]{1,0:T(8,128)(2,1)S(1)} %get-tuple-element.212), channel_id=1, source_target_pairs={{0,4},{4,8},{8,12},{1,5},{5,9},{9,13},{2,6},{6,10},{10,14},{3,7},{... | collective-permute-start | bytes 98312 | tf_op jit(solution)/shard_map/ppermute | solution.py:20
  7.8 1.0 fusion.195
  8.8 0.9 fusion.196
  9.7 1.1 copy.29
  10.8 1.4 %fusion.198 = (s32[1]{0:T(128)}, s32[1]{0:T(128)}) fusion(s32[4]{0:T(128)} %param.32, s32[]{:T(128)} %bitcast.2, s32[]{:T(128)} %bitcast.6), kind=kLoop, calls=%fused_computation.320 | loop fusion | bytes 24 | tf_op jit(solution)/shard_map/jit(_take)/gather | solution.py:146
  14.6 1.7 %fusion.111 = f32[1,8,8,8,256]{4,3,2,1,0:T(8,128)S(1)} fusion(f32[1,10,10,10,256]{4,3,2,1,0:T(8,128)S(1)} %select_maximum_fusion, f32[1,1,8,8,256]{4,3,2,1,0:T(8,128)S(1)} %multiply_bitcast_fusion, f32[1,8,8,8,256]{4,3,2,1,0:T(8,128)S(1)} %bitcast.487, f32[1,1,8,8,256]{4,3,2,1,0:T(8,128)S(1)} %multiply_bitcast_fusion.1, f32[256]{0:T(256)S(1)} %bitcast.538, ...), kind=kLoop, calls=%fused_computation.128 | loop fusion | flops 7208960 | bytes 13790208 | tf_op jit(solution)/shard_map/add | solution.py:51
  16.6 2.1 %collective-permute-start.4 = (bf16[512,256]{0,1:T(8,128)(2,1)S(1)}, bf16[512,256]{0,1:T(8,128)(2,1)S(1)}, u32[]{:S(2)}, u32[]{:S(2)}) collective-permute-start(bf16[512,256]{0,1:T(8,128)(2,1)S(1)} %add_convert_fusion), channel_id=1, source_target_pairs={{0,4},{4,8},{8,12},{12,0},{1,5},{5,9},{9,13},{13,1},{2,6},{6,10},{... | collective-permute-start | bytes 786440 | tf_op jit(solution)/shard_map/ppermute | solution.py:170
  18.7 1.5 %collective-permute-start.2 = (bf16[512,256]{0,1:T(8,128)(2,1)S(1)}, bf16[512,256]{0,1:T(8,128)(2,1)S(1)}, u32[]{:S(2)}, u32[]{:S(2)}) collective-permute-start(bf16[512,256]{0,1:T(8,128)(2,1)S(1)} %add_convert_fusion), channel_id=1, source_target_pairs={{0,2},{1,3},{2,0},{3,1},{4,6},{5,7},{6,4},{7,5},{8,10},{9,11},{10,... | collective-permute-start | bytes 786440 | tf_op jit(solution)/shard_map/ppermute | solution.py:86
  20.2 6.1 %collective-permute-done.4 = bf16[512,256]{0,1:T(8,128)(2,1)S(1)} collective-permute-done((bf16[512,256]{0,1:T(8,128)(2,1)S(1)}, bf16[512,256]{0,1:T(8,128)(2,1)S(1)}, u32[]{:S(2)}, u32[]{:S(2)}) %collective-permute-start.4) | collective-permute-done | bytes 262176 | tf_op jit(solution)/shard_map/ppermute | solution.py:170
  26.2 1.6 %collective-permute-start.5 = (bf16[512,256]{0,1:T(8,128)(2,1)S(1)}, bf16[512,256]{0,1:T(8,128)(2,1)S(1)}, u32[]{:S(2)}, u32[]{:S(2)}) collective-permute-start(bf16[512,256]{0,1:T(8,128)(2,1)S(1)} %collective-permute-done.4), channel_id=1, source_target_pairs={{0,2},{1,3},{2,0},{3,1},{4,6},{5,7},{6,4},{7,5},{8,10},{9,11},{10,... | collective-permute-start | bytes 786440 | tf_op jit(solution)/shard_map/ppermute | solution.py:86
  27.9 0.9 pad_maximum_fusion.5
  28.8 4.3 %collective-permute-done.5 = bf16[512,256]{0,1:T(8,128)(2,1)S(1)} collective-permute-done((bf16[512,256]{0,1:T(8,128)(2,1)S(1)}, bf16[512,256]{0,1:T(8,128)(2,1)S(1)}, u32[]{:S(2)}, u32[]{:S(2)}) %collective-permute-start.5) | collective-permute-done | bytes 262176 | tf_op jit(solution)/shard_map/ppermute | solution.py:86
  33.1 1.0 select_bitcast_fusion.17
  34.1 0.9 pad_maximum_fusion.6
  38.3 1.2 %copy.62 = bf16[1024,256]{1,0:T(8,128)(2,1)S(1)} copy(bf16[1024,256]{0,1:T(8,128)(2,1)} %bitcast.501) | data formatting | bytes 1048576 | tf_op jit(solution)/shard_map/dot_general | solution.py:208
  39.6 1.1 constant_dynamic-update-slice_fusion.1
  40.7 1.1 constant_dynamic-update-slice_fusion
  41.9 1.4 %select_bitcast_fusion.5 = (bf16[512,2,1,256]{0,3,1,2:T(8,128)(2,1)S(1)}, bf16[512,2,1,256]{0,3,1,2:T(8,128)(2,1)S(1)}, bf16[512,2,1,256]{0,3,1,2:T(8,128)(2,1)S(1)}, bf16[512,2,1,256]{0,3,1,2:T(8,128)(2,1)S(1)}) fusion(bf16[512,2,256]{0,2,1:T(8,128)(2,1)} %collective-permute-done.6, pred[]{:T(512)S(6)} %eq.9, bf16[512,1,256]{0,2,1:T(8,128)(2,1)S(1)} %copy-done.4, ...), kind=kLoop, calls=%fused_computation.210 | loop fusion | flops 1572864 | bytes 4194305 | tf_op jit(solution)/shard_map/stack | solution.py:89
  44.5 0.8 convolution_convert_fusion.3
  46.1 0.8 bitcast_reduce_fusion.3
  46.9 0.8 fusion.5
  47.9 1.0 fusion.61
  48.9 3.5 %collective-permute-done.7 = bf16[512,256]{0,1:T(8,128)(2,1)S(1)} collective-permute-done((bf16[512,256]{0,1:T(8,128)(2,1)S(1)}, bf16[512,256]{0,1:T(8,128)(2,1)S(1)}, u32[]{:S(2)}, u32[]{:S(2)}) %collective-permute-start.7) | collective-permute-done | bytes 262176 | tf_op jit(solution)/shard_map/ppermute | solution.py:192
  52.4 1.4 %collective-permute-start.8 = (bf16[512,256]{0,1:T(8,128)(2,1)S(1)}, bf16[512,256]{0,1:T(8,128)(2,1)S(1)}, u32[]{:S(2)}, u32[]{:S(2)}) collective-permute-start(bf16[512,256]{0,1:T(8,128)(2,1)S(1)} %collective-permute-done.7), channel_id=1, source_target_pairs={{0,2},{1,3},{2,0},{3,1},{4,6},{5,7},{6,4},{7,5},{8,10},{9,11},{10,... | collective-permute-start | bytes 786440 | tf_op jit(solution)/shard_map/ppermute | solution.py:86
  54.3 0.9 convolution_convert_fusion.2
  55.3 0.8 bitcast_reduce_fusion.2
  56.1 0.8 fusion.7
  56.9 3.4 %collective-permute-done.8 = bf16[512,256]{0,1:T(8,128)(2,1)S(1)} collective-permute-done((bf16[512,256]{0,1:T(8,128)(2,1)S(1)}, bf16[512,256]{0,1:T(8,128)(2,1)S(1)}, u32[]{:S(2)}, u32[]{:S(2)}) %collective-permute-start.8) | collective-permute-done | bytes 262176 | tf_op jit(solution)/shard_map/ppermute | solution.py:86
  60.5 1.0 fusion.55
  61.6 0.8 collective-permute-done.9
  63.7 0.9 convolution_convert_fusion.1
  64.7 0.9 collective-permute-start.11
  65.6 0.8 bitcast_reduce_fusion.1
  66.4 0.8 fusion.9
  67.2 5.4 %collective-permute-done.11 = bf16[512,256]{0,1:T(8,128)(2,1)S(1)} collective-permute-done((bf16[512,256]{0,1:T(8,128)(2,1)S(1)}, bf16[512,256]{0,1:T(8,128)(2,1)S(1)}, u32[]{:S(2)}, u32[]{:S(2)}) %collective-permute-start.11) | collective-permute-done | bytes 262176 | tf_op jit(solution)/shard_map/ppermute | solution.py:86
  72.8 1.0 fusion.52
  73.9 0.8 collective-permute-done.12
  75.5 0.9 convolution_convert_fusion
  76.5 0.8 bitcast_reduce_fusion
  77.3 0.8 fusion.10
  78.2 1.2 %fusion.104 = bf16[1,512,4,64]{1,3,2,0:T(8,128)(2,1)S(1)} fusion(bf16[512,4,64]{0,2,1:T(8,128)(2,1)S(1)} %bitcast.507, f32[4,512,512]{2,1,0:T(8,128)S(1)} %get-tuple-element.262, f32[4,512]{1,0:T(4,128)S(1)} %fusion.167, pred[]{:T(512)} %bitcast.107, f32[1,512,4,64]{1,3,2,0:T(8,128)S(1)} %multiply_add_fusion, f32[512,4]{0,1:T(4,128)S(1)} %get-tuple-element.215, ...), kind=kOutput, calls=%fused_computation.124 | convolution fusion | flops 138936320 | bytes 5267457 | tf_op jit(solution)/shard_map/bhqk,khd->bqhd/dot_general | solution.py:107
  81.5 1.4 %collective-permute-start.14 = (bf16[256,256]{0,1:T(8,128)(2,1)S(1)}, bf16[256,256]{0,1:T(8,128)(2,1)S(1)}, u32[]{:S(2)}, u32[]{:S(2)}) collective-permute-start(bf16[256,256]{0,1:T(8,128)(2,1)S(1)} %fusion.162), channel_id=1, source_target_pairs={{0,2},{1,3},{2,0},{3,1},{4,6},{5,7},{6,4},{7,5},{8,10},{9,11},{10,... | collective-permute-start | bytes 393224 | tf_op jit(solution)/shard_map/ppermute | solution.py:72
  82.9 0.9 bitcast_add_fusion.1
  83.7 1.0 fusion.164
  84.7 0.7 collective-permute-start.20
  85.5 1.6 %collective-permute-done.14 = bf16[256,256]{0,1:T(8,128)(2,1)S(1)} collective-permute-done((bf16[256,256]{0,1:T(8,128)(2,1)S(1)}, bf16[256,256]{0,1:T(8,128)(2,1)S(1)}, u32[]{:S(2)}, u32[]{:S(2)}) %collective-permute-start.14) | collective-permute-done | bytes 131104 | tf_op jit(solution)/shard_map/ppermute | solution.py:72
  87.1 3.0 %collective-permute-done.20 = bf16[256,256]{0,1:T(8,128)(2,1)S(1)} collective-permute-done((bf16[256,256]{0,1:T(8,128)(2,1)S(1)}, bf16[256,256]{0,1:T(8,128)(2,1)S(1)}, u32[]{:S(2)}, u32[]{:S(2)}) %collective-permute-start.20) | collective-permute-done | bytes 131104 | tf_op jit(solution)/shard_map/ppermute | solution.py:72
  90.0 1.0 fusion.159
  91.1 1.3 %collective-permute-start.15 = (bf16[256,256]{0,1:T(8,128)(2,1)S(1)}, bf16[256,256]{0,1:T(8,128)(2,1)S(1)}, u32[]{:S(2)}, u32[]{:S(2)}) collective-permute-start(bf16[256,256]{0,1:T(8,128)(2,1)S(1)} %get-tuple-element.206), channel_id=1, source_target_pairs={{0,2},{1,3},{2,0},{3,1},{4,6},{5,7},{6,4},{7,5},{8,10},{9,11},{10,... | collective-permute-start | bytes 393224 | tf_op jit(solution)/shard_map/ppermute | solution.py:86
  92.3 0.8 collective-permute-start.21
  93.2 3.8 %collective-permute-done.15 = bf16[256,256]{0,1:T(8,128)(2,1)S(1)} collective-permute-done((bf16[256,256]{0,1:T(8,128)(2,1)S(1)}, bf16[256,256]{0,1:T(8,128)(2,1)S(1)}, u32[]{:S(2)}, u32[]{:S(2)}) %collective-permute-start.15) | collective-permute-done | bytes 131104 | tf_op jit(solution)/shard_map/ppermute | solution.py:86
  97.1 1.3 %collective-permute-done.21 = bf16[256,256]{0,1:T(8,128)(2,1)S(1)} collective-permute-done((bf16[256,256]{0,1:T(8,128)(2,1)S(1)}, bf16[256,256]{0,1:T(8,128)(2,1)S(1)}, u32[]{:S(2)}, u32[]{:S(2)}) %collective-permute-start.21) | collective-permute-done | bytes 131104 | tf_op jit(solution)/shard_map/ppermute | solution.py:86
  98.9 1.1 collective-permute-done.22
  101.3 4.2 %fusion.107 = f32[256,1024]{0,1:T(8,128)} fusion(bf16[1024,1024]{1,0:T(8,128)(2,1)S(1)} %copy-done, bf16[256,1024]{0,1:T(8,128)(2,1)S(1)} %get-tuple-element.248, bf16[1024,1024]{1,0:T(8,128)(2,1)} %param.42), kind=kOutput, calls=%fused_computation.125 | convolution fusion | flops 1076101120 | bytes 5767168 | tf_op jit(solution)/shard_map/dot_general | solution.py:216
  105.4 1.1 fusion.151
  106.7 4.2 %fusion.109 = f32[256,1024]{0,1:T(8,128)} fusion(bf16[1024,1024]{1,0:T(8,128)(2,1)S(1)} %copy-done, bf16[256,1024]{0,1:T(8,128)(2,1)S(1)} %get-tuple-element.247, bf16[1024,1024]{1,0:T(8,128)(2,1)} %param.42), kind=kOutput, calls=%fused_computation.126 | convolution fusion | flops 1076101120 | bytes 5767168 | tf_op jit(solution)/shard_map/dot_general | solution.py:216
  110.9 1.2 fusion.150
  112.5 1.1 bitcast_add_fusion
  113.6 1.7 %collective-permute-start.24 = (bf16[256,256]{0,1:T(8,128)(2,1)S(1)}, bf16[256,256]{0,1:T(8,128)(2,1)S(1)}, u32[]{:S(2)}, u32[]{:S(2)}) collective-permute-start(bf16[256,256]{0,1:T(8,128)(2,1)S(1)} %fusion.165), channel_id=1, source_target_pairs={{0,2},{1,3},{2,0},{3,1},{4,6},{5,7},{6,4},{7,5},{8,10},{9,11},{10,... | collective-permute-start | bytes 393224 | tf_op jit(solution)/shard_map/ppermute | solution.py:72
  115.9 4.1 %collective-permute-done.24 = bf16[256,256]{0,1:T(8,128)(2,1)S(1)} collective-permute-done((bf16[256,256]{0,1:T(8,128)(2,1)S(1)}, bf16[256,256]{0,1:T(8,128)(2,1)S(1)}, u32[]{:S(2)}, u32[]{:S(2)}) %collective-permute-start.24) | collective-permute-done | bytes 131104 | tf_op jit(solution)/shard_map/ppermute | solution.py:72
  120.1 2.0 %collective-permute-done.18 = bf16[256,256]{0,1:T(8,128)(2,1)S(1)} collective-permute-done((bf16[256,256]{0,1:T(8,128)(2,1)S(1)}, bf16[256,256]{0,1:T(8,128)(2,1)S(1)}, u32[]{:S(2)}, u32[]{:S(2)}) %collective-permute-start.18) | collective-permute-done | bytes 131104 | tf_op jit(solution)/shard_map/ppermute | solution.py:72
  122.1 0.8 copy.51
  (137 shorter events, 12.8 us)
Async XLA Ops:
  0.0 101.2 %copy-start = (bf16[1024,1024]{1,0:T(8,128)(2,1)S(1)}, bf16[1024,1024]{1,0:T(8,128)(2,1)}, u32[]{:S(2)}) copy-start(bf16[1024,1024]{1,0:T(8,128)(2,1)} %param.43) | copy-start | bytes 6291460
  0.9 13.4 %collective-permute-start.1 = (bf16[64,256]{1,0:T(8,128)(2,1)S(1)}, bf16[64,256]{1,0:T(8,128)(2,1)S(1)}, u32[]{:S(2)}, u32[]{:S(2)}) collective-permute-start(bf16[64,256]{1,0:T(8,128)(2,1)S(1)} %get-tuple-element.213), channel_id=1, source_target_pairs={{4,0},{8,4},{12,8},{5,1},{9,5},{13,9},{6,2},{10,6},{14,10},{7,3},{... | collective-permute-start | bytes 98312 | tf_op jit(solution)/shard_map/ppermute | solution.py:21
  2.2 12.1 %collective-permute-start = (bf16[64,256]{1,0:T(8,128)(2,1)S(1)}, bf16[64,256]{1,0:T(8,128)(2,1)S(1)}, u32[]{:S(2)}, u32[]{:S(2)}) collective-permute-start(bf16[64,256]{1,0:T(8,128)(2,1)S(1)} %get-tuple-element.212), channel_id=1, source_target_pairs={{0,4},{4,8},{8,12},{1,5},{5,9},{9,13},{2,6},{6,10},{10,14},{3,7},{... | collective-permute-start | bytes 98312 | tf_op jit(solution)/shard_map/ppermute | solution.py:20
  16.6 9.6 %collective-permute-start.4 = (bf16[512,256]{0,1:T(8,128)(2,1)S(1)}, bf16[512,256]{0,1:T(8,128)(2,1)S(1)}, u32[]{:S(2)}, u32[]{:S(2)}) collective-permute-start(bf16[512,256]{0,1:T(8,128)(2,1)S(1)} %add_convert_fusion), channel_id=1, source_target_pairs={{0,4},{4,8},{8,12},{12,0},{1,5},{5,9},{9,13},{13,1},{2,6},{6,10},{... | collective-permute-start | bytes 786440 | tf_op jit(solution)/shard_map/ppermute | solution.py:170
  18.7 9.2 %collective-permute-start.2 = (bf16[512,256]{0,1:T(8,128)(2,1)S(1)}, bf16[512,256]{0,1:T(8,128)(2,1)S(1)}, u32[]{:S(2)}, u32[]{:S(2)}) collective-permute-start(bf16[512,256]{0,1:T(8,128)(2,1)S(1)} %add_convert_fusion), channel_id=1, source_target_pairs={{0,2},{1,3},{2,0},{3,1},{4,6},{5,7},{6,4},{7,5},{8,10},{9,11},{10,... | collective-permute-start | bytes 786440 | tf_op jit(solution)/shard_map/ppermute | solution.py:86
  20.2 14.9 %copy-start.8 = (bf16[1024]{0:T(1024)(128)(2,1)S(1)}, bf16[1024]{0:T(1024)(128)(2,1)}, u32[]{:S(2)}) copy-start(bf16[1024]{0:T(1024)(128)(2,1)} %param.36) | copy-start | bytes 6148
  20.2 14.9 %copy-start.10 = (s32[4,4]{1,0:T(4,128)S(1)}, s32[4,4]{1,0:T(4,128)}, u32[]{:S(2)}) copy-start(s32[4,4]{1,0:T(4,128)} %param.33) | copy-start | bytes 196
  26.2 2.6 %copy-start.6 = (bf16[512,256]{0,1:T(8,128)(2,1)}, bf16[512,256]{0,1:T(8,128)(2,1)S(1)}, u32[]{:S(2)}) copy-start(bf16[512,256]{0,1:T(8,128)(2,1)S(1)} %collective-permute-done.4) | copy-start | bytes 786436
  26.2 6.9 %collective-permute-start.5 = (bf16[512,256]{0,1:T(8,128)(2,1)S(1)}, bf16[512,256]{0,1:T(8,128)(2,1)S(1)}, u32[]{:S(2)}, u32[]{:S(2)}) collective-permute-start(bf16[512,256]{0,1:T(8,128)(2,1)S(1)} %collective-permute-done.4), channel_id=1, source_target_pairs={{0,2},{1,3},{2,0},{3,1},{4,6},{5,7},{6,4},{7,5},{8,10},{9,11},{10,... | collective-permute-start | bytes 786440 | tf_op jit(solution)/shard_map/ppermute | solution.py:86
  28.8 13.1 %collective-permute-start.3 = (bf16[512,2,256]{0,2,1:T(8,128)(2,1)}, bf16[512,2,256]{0,2,1:T(8,128)(2,1)}, u32[]{:S(2)}, u32[]{:S(2)}) collective-permute-start(bf16[512,2,256]{0,2,1:T(8,128)(2,1)} %pad_maximum_fusion.5), channel_id=1, source_target_pairs={{0,1},{1,0},{2,3},{3,2},{4,5},{5,4},{6,7},{7,6},{8,9},{9,8},{10,11... | collective-permute-start | bytes 1572872 | tf_op jit(solution)/shard_map/ppermute | solution.py:86
  34.1 4.2 %copy-start.1 = (bf16[512,1,256]{0,2,1:T(8,128)(2,1)}, bf16[512,1,256]{0,2,1:T(8,128)(2,1)S(1)}, u32[]{:S(2)}) copy-start(bf16[512,1,256]{0,2,1:T(8,128)(2,1)S(1)} %get-tuple-element.198) | copy-start | bytes 786436
  34.1 4.2 %copy-start.3 = (bf16[512,1,256]{0,2,1:T(8,128)(2,1)}, bf16[512,1,256]{0,2,1:T(8,128)(2,1)S(1)}, u32[]{:S(2)}) copy-start(bf16[512,1,256]{0,2,1:T(8,128)(2,1)S(1)} %get-tuple-element.199) | copy-start | bytes 786436
  35.0 6.9 %collective-permute-start.6 = (bf16[512,2,256]{0,2,1:T(8,128)(2,1)}, bf16[512,2,256]{0,2,1:T(8,128)(2,1)}, u32[]{:S(2)}, u32[]{:S(2)}) collective-permute-start(bf16[512,2,256]{0,2,1:T(8,128)(2,1)} %pad_maximum_fusion.6), channel_id=1, source_target_pairs={{0,1},{1,0},{2,3},{3,2},{4,5},{5,4},{6,7},{7,6},{8,9},{9,8},{10,11... | collective-permute-start | bytes 1572872 | tf_op jit(solution)/shard_map/ppermute | solution.py:86
  39.5 2.3 %copy-start.7 = (bf16[512,256]{0,1:T(8,128)(2,1)S(1)}, bf16[512,256]{0,1:T(8,128)(2,1)}, u32[]{:S(2)}) copy-start(bf16[512,256]{0,1:T(8,128)(2,1)} %copy-done.6) | copy-start | bytes 786436
  39.5 2.4 %copy-start.2 = (bf16[512,1,256]{0,2,1:T(8,128)(2,1)S(1)}, bf16[512,1,256]{0,2,1:T(8,128)(2,1)}, u32[]{:S(2)}) copy-start(bf16[512,1,256]{0,2,1:T(8,128)(2,1)} %copy-done.1) | copy-start | bytes 786436
  39.6 2.4 %copy-start.4 = (bf16[512,1,256]{0,2,1:T(8,128)(2,1)S(1)}, bf16[512,1,256]{0,2,1:T(8,128)(2,1)}, u32[]{:S(2)}) copy-start(bf16[512,1,256]{0,2,1:T(8,128)(2,1)} %copy-done.3) | copy-start | bytes 786436
  41.8 10.5 %collective-permute-start.7 = (bf16[512,256]{0,1:T(8,128)(2,1)S(1)}, bf16[512,256]{0,1:T(8,128)(2,1)S(1)}, u32[]{:S(2)}, u32[]{:S(2)}) collective-permute-start(bf16[512,256]{0,1:T(8,128)(2,1)S(1)} %copy-done.7), channel_id=1, source_target_pairs={{0,4},{4,8},{8,12},{12,0},{1,5},{5,9},{9,13},{13,1},{2,6},{6,10},{... | collective-permute-start | bytes 786440 | tf_op jit(solution)/shard_map/ppermute | solution.py:192
  44.5 1.0 copy-start.11
  52.4 7.9 %collective-permute-start.8 = (bf16[512,256]{0,1:T(8,128)(2,1)S(1)}, bf16[512,256]{0,1:T(8,128)(2,1)S(1)}, u32[]{:S(2)}, u32[]{:S(2)}) collective-permute-start(bf16[512,256]{0,1:T(8,128)(2,1)S(1)} %collective-permute-done.7), channel_id=1, source_target_pairs={{0,2},{1,3},{2,0},{3,1},{4,6},{5,7},{6,4},{7,5},{8,10},{9,11},{10,... | collective-permute-start | bytes 786440 | tf_op jit(solution)/shard_map/ppermute | solution.py:86
  53.7 9.4 %collective-permute-start.10 = (bf16[512,256]{0,1:T(8,128)(2,1)S(1)}, bf16[512,256]{0,1:T(8,128)(2,1)S(1)}, u32[]{:S(2)}, u32[]{:S(2)}) collective-permute-start(bf16[512,256]{0,1:T(8,128)(2,1)S(1)} %collective-permute-done.7), channel_id=1, source_target_pairs={{0,4},{4,8},{8,12},{12,0},{1,5},{5,9},{9,13},{13,1},{2,6},{6,10},{... | collective-permute-start | bytes 786440 | tf_op jit(solution)/shard_map/ppermute | solution.py:192
  60.4 2.0 %collective-permute-start.9 = (bf16[512,2,256]{0,2,1:T(8,128)(2,1)S(1)}, bf16[512,2,256]{0,2,1:T(8,128)(2,1)S(1)}, u32[]{:S(2)}, u32[]{:S(2)}) collective-permute-start(bf16[512,2,256]{0,2,1:T(8,128)(2,1)S(1)} %pad_maximum_fusion.7), channel_id=1, source_target_pairs={{0,1},{1,0},{2,3},{3,2},{4,5},{5,4},{6,7},{7,6},{8,9},{9,8},{10,11... | collective-permute-start | bytes 1572872 | tf_op jit(solution)/shard_map/ppermute | solution.py:86
  64.7 7.9 %collective-permute-start.11 = (bf16[512,256]{0,1:T(8,128)(2,1)S(1)}, bf16[512,256]{0,1:T(8,128)(2,1)S(1)}, u32[]{:S(2)}, u32[]{:S(2)}) collective-permute-start(bf16[512,256]{0,1:T(8,128)(2,1)S(1)} %collective-permute-done.10), channel_id=1, source_target_pairs={{0,2},{1,3},{2,0},{3,1},{4,6},{5,7},{6,4},{7,5},{8,10},{9,11},{10,... | collective-permute-start | bytes 786440 | tf_op jit(solution)/shard_map/ppermute | solution.py:86
  72.7 2.0 %collective-permute-start.12 = (bf16[512,2,256]{0,2,1:T(8,128)(2,1)S(1)}, bf16[512,2,256]{0,2,1:T(8,128)(2,1)S(1)}, u32[]{:S(2)}, u32[]{:S(2)}) collective-permute-start(bf16[512,2,256]{0,2,1:T(8,128)(2,1)S(1)} %pad_maximum_fusion.8), channel_id=1, source_target_pairs={{0,1},{1,0},{2,3},{3,2},{4,5},{5,4},{6,7},{7,6},{8,9},{9,8},{10,11... | collective-permute-start | bytes 1572872 | tf_op jit(solution)/shard_map/ppermute | solution.py:86
  79.8 1.6 %collective-permute-start.13 = (bf16[256,2,256]{0,2,1:T(8,128)(2,1)S(1)}, bf16[256,2,256]{0,2,1:T(8,128)(2,1)S(1)}, u32[]{:S(2)}, u32[]{:S(2)}) collective-permute-start(bf16[256,2,256]{0,2,1:T(8,128)(2,1)S(1)} %fusion.148), channel_id=1, source_target_pairs={{0,1},{1,0},{2,3},{3,2},{4,5},{5,4},{6,7},{7,6},{8,9},{9,8},{10,11... | collective-permute-start | bytes 786440 | tf_op jit(solution)/shard_map/ppermute | solution.py:72
  80.3 12.0 %copy-start.9 = (bf16[1024]{0:T(1024)(128)(2,1)S(1)}, bf16[1024]{0:T(1024)(128)(2,1)}, u32[]{:S(2)}) copy-start(bf16[1024]{0:T(1024)(128)(2,1)} %param.41) | copy-start | bytes 6148
  80.3 2.6 %collective-permute-start.19 = (bf16[256,2,256]{0,2,1:T(8,128)(2,1)S(1)}, bf16[256,2,256]{0,2,1:T(8,128)(2,1)S(1)}, u32[]{:S(2)}, u32[]{:S(2)}) collective-permute-start(bf16[256,2,256]{0,2,1:T(8,128)(2,1)S(1)} %fusion.149), channel_id=1, source_target_pairs={{0,1},{1,0},{2,3},{3,2},{4,5},{5,4},{6,7},{7,6},{8,9},{9,8},{10,11... | collective-permute-start | bytes 786440 | tf_op jit(solution)/shard_map/ppermute | solution.py:72
  81.5 5.6 %collective-permute-start.14 = (bf16[256,256]{0,1:T(8,128)(2,1)S(1)}, bf16[256,256]{0,1:T(8,128)(2,1)S(1)}, u32[]{:S(2)}, u32[]{:S(2)}) collective-permute-start(bf16[256,256]{0,1:T(8,128)(2,1)S(1)} %fusion.162), channel_id=1, source_target_pairs={{0,2},{1,3},{2,0},{3,1},{4,6},{5,7},{6,4},{7,5},{8,10},{9,11},{10,... | collective-permute-start | bytes 393224 | tf_op jit(solution)/shard_map/ppermute | solution.py:72
  84.7 5.3 %collective-permute-start.20 = (bf16[256,256]{0,1:T(8,128)(2,1)S(1)}, bf16[256,256]{0,1:T(8,128)(2,1)S(1)}, u32[]{:S(2)}, u32[]{:S(2)}) collective-permute-start(bf16[256,256]{0,1:T(8,128)(2,1)S(1)} %fusion.164), channel_id=1, source_target_pairs={{0,2},{1,3},{2,0},{3,1},{4,6},{5,7},{6,4},{7,5},{8,10},{9,11},{10,... | collective-permute-start | bytes 393224 | tf_op jit(solution)/shard_map/ppermute | solution.py:72
  91.1 5.9 %collective-permute-start.15 = (bf16[256,256]{0,1:T(8,128)(2,1)S(1)}, bf16[256,256]{0,1:T(8,128)(2,1)S(1)}, u32[]{:S(2)}, u32[]{:S(2)}) collective-permute-start(bf16[256,256]{0,1:T(8,128)(2,1)S(1)} %get-tuple-element.206), channel_id=1, source_target_pairs={{0,2},{1,3},{2,0},{3,1},{4,6},{5,7},{6,4},{7,5},{8,10},{9,11},{10,... | collective-permute-start | bytes 393224 | tf_op jit(solution)/shard_map/ppermute | solution.py:86
  92.3 6.1 %collective-permute-start.21 = (bf16[256,256]{0,1:T(8,128)(2,1)S(1)}, bf16[256,256]{0,1:T(8,128)(2,1)S(1)}, u32[]{:S(2)}, u32[]{:S(2)}) collective-permute-start(bf16[256,256]{0,1:T(8,128)(2,1)S(1)} %get-tuple-element.207), channel_id=1, source_target_pairs={{0,2},{1,3},{2,0},{3,1},{4,6},{5,7},{6,4},{7,5},{8,10},{9,11},{10,... | collective-permute-start | bytes 393224 | tf_op jit(solution)/shard_map/ppermute | solution.py:86
  97.1 1.6 %collective-permute-start.16 = (bf16[256,2,256]{0,2,1:T(8,128)(2,1)S(1)}, bf16[256,2,256]{0,2,1:T(8,128)(2,1)S(1)}, u32[]{:S(2)}, u32[]{:S(2)}) collective-permute-start(bf16[256,2,256]{0,2,1:T(8,128)(2,1)S(1)} %pad_maximum_fusion.9), channel_id=1, source_target_pairs={{0,1},{1,0},{2,3},{3,2},{4,5},{5,4},{6,7},{7,6},{8,9},{9,8},{10,11... | collective-permute-start | bytes 786440 | tf_op jit(solution)/shard_map/ppermute | solution.py:86
  98.5 1.6 %collective-permute-start.22 = (bf16[256,2,256]{0,2,1:T(8,128)(2,1)S(1)}, bf16[256,2,256]{0,2,1:T(8,128)(2,1)S(1)}, u32[]{:S(2)}, u32[]{:S(2)}) collective-permute-start(bf16[256,2,256]{0,2,1:T(8,128)(2,1)S(1)} %pad_maximum_fusion.10), channel_id=1, source_target_pairs={{0,1},{1,0},{2,3},{3,2},{4,5},{5,4},{6,7},{7,6},{8,9},{9,8},{10,11... | collective-permute-start | bytes 786440 | tf_op jit(solution)/shard_map/ppermute | solution.py:86
  106.5 6.0 %collective-permute-start.23 = (bf16[256,2,256]{0,2,1:T(8,128)(2,1)S(1)}, bf16[256,2,256]{0,2,1:T(8,128)(2,1)S(1)}, u32[]{:S(2)}, u32[]{:S(2)}) collective-permute-start(bf16[256,2,256]{0,2,1:T(8,128)(2,1)S(1)} %fusion.151), channel_id=1, source_target_pairs={{0,1},{1,0},{2,3},{3,2},{4,5},{5,4},{6,7},{7,6},{8,9},{9,8},{10,11... | collective-permute-start | bytes 786440 | tf_op jit(solution)/shard_map/ppermute | solution.py:72
  110.9 4.5 %copy-start.5 = (f32[256,1024]{0,1:T(8,128)S(1)}, f32[256,1024]{0,1:T(8,128)}, u32[]{:S(2)}) copy-start(f32[256,1024]{0,1:T(8,128)} %fusion.109) | copy-start | bytes 3145732
  112.1 3.3 %collective-permute-start.17 = (bf16[256,2,256]{0,2,1:T(8,128)(2,1)S(1)}, bf16[256,2,256]{0,2,1:T(8,128)(2,1)S(1)}, u32[]{:S(2)}, u32[]{:S(2)}) collective-permute-start(bf16[256,2,256]{0,2,1:T(8,128)(2,1)S(1)} %fusion.150), channel_id=1, source_target_pairs={{0,1},{1,0},{2,3},{3,2},{4,5},{5,4},{6,7},{7,6},{8,9},{9,8},{10,11... | collective-permute-start | bytes 786440 | tf_op jit(solution)/shard_map/ppermute | solution.py:72
  113.6 6.4 %collective-permute-start.24 = (bf16[256,256]{0,1:T(8,128)(2,1)S(1)}, bf16[256,256]{0,1:T(8,128)(2,1)S(1)}, u32[]{:S(2)}, u32[]{:S(2)}) collective-permute-start(bf16[256,256]{0,1:T(8,128)(2,1)S(1)} %fusion.165), channel_id=1, source_target_pairs={{0,2},{1,3},{2,0},{3,1},{4,6},{5,7},{6,4},{7,5},{8,10},{9,11},{10,... | collective-permute-start | bytes 393224 | tf_op jit(solution)/shard_map/ppermute | solution.py:72
  115.5 6.6 %collective-permute-start.18 = (bf16[256,256]{0,1:T(8,128)(2,1)S(1)}, bf16[256,256]{0,1:T(8,128)(2,1)S(1)}, u32[]{:S(2)}, u32[]{:S(2)}) collective-permute-start(bf16[256,256]{0,1:T(8,128)(2,1)S(1)} %fusion.163), channel_id=1, source_target_pairs={{0,2},{1,3},{2,0},{3,1},{4,6},{5,7},{6,4},{7,5},{8,10},{9,11},{10,... | collective-permute-start | bytes 393224 | tf_op jit(solution)/shard_map/ppermute | solution.py:72

commit v7 on v6

--- a/solution.py
+++ b/solution.py
@@ -109,6 +109,35 @@
         preferred_element_type=jnp.float32,
     )
     return max_new, mass_new, sum_new
+
+
+def shifted_depthwise(brick_vals, lower_face, upper_face, conv_weight, conv_bias):
+    brick_count, edge_len, face_rows, channels = brick_vals.shape
+    brick_rows = edge_len * face_rows
+    layers = jnp.concatenate([lower_face[:, None], brick_vals, upper_face[:, None]], axis=1)
+    flat = layers.reshape(brick_count, (edge_len + 2) * face_rows, channels)
+    reach = face_rows + edge_len + 1
+    flat = jnp.pad(flat, ((0, 0), (reach, reach), (0, 0)))
+    row_ids = jnp.arange(brick_rows, dtype=jnp.int32)[:, None]
+    y_ids = (row_ids // edge_len) % edge_len
+    z_ids = row_ids % edge_len
+    weights = conv_weight.astype(jnp.float32)
+    summed = jnp.zeros((brick_count, brick_rows, channels), jnp.float32)
+    for step_x in range(3):
+        for step_y in range(3):
+            for step_z in range(3):
+                offset = (step_x - 1) * face_rows + (step_y - 1) * edge_len + (step_z - 1)
+                begin = reach + face_rows + offset
+                window = flat[:, begin : begin + brick_rows]
+                inside = (
+                    (y_ids + step_y - 1 >= 0)
+                    & (y_ids + step_y - 1 < edge_len)
+                    & (z_ids + step_z - 1 >= 0)
+                    & (z_ids + step_z - 1 < edge_len)
+                )
+                window = jnp.where(inside[None], window, 0.0)
+                summed = summed + weights[step_x * 9 + step_y * 3 + step_z] * window
+    return summed.reshape(brick_count * brick_rows, channels) + conv_bias.astype(jnp.float32)
 
 
 def shards(
@@ -151,7 +180,7 @@
     )
     lower_face = lower_face * lower_open.astype(jnp.float32)[:, None, None]
     upper_face = upper_face * upper_open.astype(jnp.float32)[:, None, None]
-    conv_out = depthwise(brick_vals, lower_face, upper_face, conv_weight, conv_bias)
+    conv_out = shifted_depthwise(brick_vals, lower_face, upper_face, conv_weight, conv_bias)
     stream = (voxel_feats.astype(jnp.float32) + conv_out).astype(jnp.bfloat16)
     head_total = lax.axis_size("heads")
     head_id = lax.axis_index("heads")

time: 124 us -> 128 us (1.032)
  other arithmetic: 18.5 us -> 23.6 us
  waiting for transfers between devices: 42.3 us -> 37.2 us
  local copies, waits for them, and re-layouts: 14.9 us -> 19.1 us
    convert_element_type x1, other arithmetic: 0.13 us -> 5.72 us  [shards(): stream = (voxel_feats.astype(jnp.float32) + conv_out).astype(jnp.bfloat16)]
    ppermute x12, waiting for transfers between devices: 20.9 us -> 18 us  [gather_heads(): lax.ppermute(current, 'heads', [(i, i ^ bit) for i in range(head_total)])]
    ppermute x2, waiting for transfers between devices: 4.01 us -> 2.09 us  [shards(): ring_block = lax.ppermute(arrived, 'bricks', ring)]
    add x1 -> x0, other arithmetic: 1.66 us -> none  [depthwise(): summed = summed + weights[step_x * 9 + step_y * 3 + step_z] * window]
    unnamed x26 -> x22, local copies, waits for them, and re-layouts: 2.52 us -> 4.06 us
    another operation x20 -> x21, other arithmetic: 5.08 us -> 4.02 us  [gather_heads(): current = jnp.stack([low, high], axis=current.ndim - 1)]
  transfers between devices with their start and end apart: 25 -> 25, of which waited for: 17 -> 15; matrix products, arithmetic and copies ran while one was open for 29% -> 30% of each run, Pallas kernels for 0% -> 0%
where the time goes in v7:
time: 128 us; the launch traced here: 127 us
  waiting for transfers between devices  37.2 us (29%)
  other arithmetic  23.6 us (18%)
  starting transfers between devices  22 us (17%)
  matrix products  20.3 us (16%)
  local copies, waits for them, and re-layouts  19.1 us (15%)
  between operations  4.42 us (3%)
    ppermute x12, waiting for transfers between devices, gather_heads(): lax.ppermute(current, 'heads', [(i, i ^ bit) for i in range(head_total)])  18 us
    ppermute x8, waiting for transfers between devices, scatter_heads(): lax.ppermute(give.astype(jnp.bfloat16), 'heads', [(i, i ^ bit) for i in r...  10.9 us
    dot_general x2, matrix products, shards(): lowered = jnp.dot(hidden, down_weight, preferred_element_type=jnp.float32)  8.4 us
    ppermute x12, starting transfers between devices, gather_heads(): lax.ppermute(current, 'heads', [(i, i ^ bit) for i in range(head_total)])  7.73 us
    ppermute x1, waiting for transfers between devices, shards(): ring_block = lax.ppermute(stream, 'bricks', ring)  6.16 us
    convert_element_type x1, other arithmetic, shards(): stream = (voxel_feats.astype(jnp.float32) + conv_out).astype(jnp.bfloat16)  5.72 us
    ppermute x1, starting transfers between devices, extended_2(): before = lax.ppermute(last, axis, up)  5.56 us
    ppermute x8, starting transfers between devices, scatter_heads(): lax.ppermute(give.astype(jnp.bfloat16), 'heads', [(i, i ^ bit) for i in r...  5.4 us
  transfers between devices with their start and end apart: 25, of which 15 were waited for; matrix products, arithmetic and copies ran while one was open for 30% of the time, Pallas kernels for 0%

profile of v7, /device:TPU:0, one launch (start us, length us, event | category | flops | bytes accessed | tf_op | source)
XLA Modules:
  0.0 126.7 jit_solution(4898734455590396877)
XLA Ops:
  0.0 0.9 fusion.236
  0.9 1.3 %collective-permute-start.1 = (bf16[64,256]{1,0:T(8,128)(2,1)S(1)}, bf16[64,256]{1,0:T(8,128)(2,1)S(1)}, u32[]{:S(2)}, u32[]{:S(2)}) collective-permute-start(bf16[64,256]{1,0:T(8,128)(2,1)S(1)} %get-tuple-element.213), channel_id=1, source_target_pairs={{4,0},{8,4},{12,8},{5,1},{9,5},{13,9},{6,2},{10,6},{14,10},{7,3},{... | collective-permute-start | bytes 98312 | tf_op jit(solution)/shard_map/ppermute | solution.py:21
  2.2 5.6 %collective-permute-start = (bf16[64,256]{1,0:T(8,128)(2,1)S(1)}, bf16[64,256]{1,0:T(8,128)(2,1)S(1)}, u32[]{:S(2)}, u32[]{:S(2)}) collective-permute-start(bf16[64,256]{1,0:T(8,128)(2,1)S(1)} %get-tuple-element.212), channel_id=1, source_target_pairs={{0,4},{4,8},{8,12},{1,5},{5,9},{9,13},{2,6},{6,10},{10,14},{3,7},{... | collective-permute-start | bytes 98312 | tf_op jit(solution)/shard_map/ppermute | solution.py:20
  7.8 0.9 fusion.238
  8.7 1.0 fusion.237
  10.8 1.1 copy.27
  11.9 1.4 %fusion.240 = (s32[1]{0:T(128)}, s32[1]{0:T(128)}) fusion(s32[4]{0:T(128)} %param.32, s32[]{:T(128)} %bitcast.2, s32[]{:T(128)} %bitcast.6), kind=kLoop, calls=%fused_computation.382 | loop fusion | bytes 24 | tf_op jit(solution)/shard_map/jit(_take)/gather | solution.py:175
  14.0 0.9 copy.28
  15.6 0.7 convert_element_type.232
  16.3 1.1 pad_maximum_fusion.3
  17.7 5.7 %fusion.146 = bf16[512,256]{0,1:T(8,128)(2,1)S(1)} fusion(f32[1,640,256]{1,2,0:T(8,128)S(1)} %copy.29, f32[256]{0:T(256)S(1)} %convert_element_type.232, f32[256]{0:T(256)S(1)} %bitcast.526, f32[256]{0:T(256)S(1)} %bitcast.525, f32[256]{0:T(256)S(1)} %bitcast.524, f32[256]{0:T(256)S(1)} %bitcast.523, f32[256]{0:T(256)S(1)} %bitcast.522, ...), kind=kLoop, calls=%fused_computation.165 | loop fusion | flops 11010048 | bytes 11174400 | tf_op jit(solution)/shard_map/convert_element_type | solution.py:184
  23.4 2.1 %collective-permute-start.4 = (bf16[512,256]{0,1:T(8,128)(2,1)S(1)}, bf16[512,256]{0,1:T(8,128)(2,1)}, u32[]{:S(2)}, u32[]{:S(2)}) collective-permute-start(bf16[512,256]{0,1:T(8,128)(2,1)S(1)} %fusion.146), channel_id=1, source_target_pairs={{0,4},{4,8},{8,12},{12,0},{1,5},{5,9},{9,13},{13,1},{2,6},{6,10},{... | collective-permute-start | bytes 786440 | tf_op jit(solution)/shard_map/ppermute | solution.py:199
  25.5 1.5 %collective-permute-start.2 = (bf16[512,256]{0,1:T(8,128)(2,1)S(1)}, bf16[512,256]{0,1:T(8,128)(2,1)S(1)}, u32[]{:S(2)}, u32[]{:S(2)}) collective-permute-start(bf16[512,256]{0,1:T(8,128)(2,1)S(1)} %fusion.146), channel_id=1, source_target_pairs={{0,2},{1,3},{2,0},{3,1},{4,6},{5,7},{6,4},{7,5},{8,10},{9,11},{10,... | collective-permute-start | bytes 786440 | tf_op jit(solution)/shard_map/ppermute | solution.py:86
  26.9 6.2 %collective-permute-done.4 = bf16[512,256]{0,1:T(8,128)(2,1)} collective-permute-done((bf16[512,256]{0,1:T(8,128)(2,1)S(1)}, bf16[512,256]{0,1:T(8,128)(2,1)}, u32[]{:S(2)}, u32[]{:S(2)}) %collective-permute-start.4) | collective-permute-done | bytes 262176 | tf_op jit(solution)/shard_map/ppermute | solution.py:199
  33.1 1.6 %collective-permute-start.5 = (bf16[512,256]{0,1:T(8,128)(2,1)}, bf16[512,256]{0,1:T(8,128)(2,1)}, u32[]{:S(2)}, u32[]{:S(2)}) collective-permute-start(bf16[512,256]{0,1:T(8,128)(2,1)} %collective-permute-done.4), channel_id=1, source_target_pairs={{0,2},{1,3},{2,0},{3,1},{4,6},{5,7},{6,4},{7,5},{8,10},{9,11},{10,... | collective-permute-start | bytes 786440 | tf_op jit(solution)/shard_map/ppermute | solution.py:86
  34.8 0.9 pad_maximum_fusion.4
  35.7 1.9 %constant_dynamic-update-slice_fusion.1 = bf16[1024,512]{1,0:T(8,128)(2,1)} fusion(bf16[1024,256]{1,0:T(8,128)(2,1)} %param.38), kind=kLoop, calls=%fused_computation.305 | loop fusion | bytes 1048576
  40.6 1.2 copy.79
  41.8 1.9 %constant_dynamic-update-slice_fusion = bf16[1024,512]{1,0:T(8,128)(2,1)} fusion(bf16[1024,512]{1,0:T(8,128)(2,1)} %constant_dynamic-update-slice_fusion.1, bf16[1024,256]{1,0:T(8,128)(2,1)} %param.39), kind=kLoop, calls=%fused_computation.304 | loop fusion | bytes 1048576 | tf_op jit(solution)/shard_map/concatenate | solution.py:191
  43.7 1.1 select_bitcast_fusion.17
  45.5 1.1 select_bitcast_fusion.7
  48.2 0.8 convolution_convert_fusion.3
  49.5 0.8 bitcast_reduce_fusion.3
  50.2 0.8 fusion.5
  51.1 1.0 fusion.58
  52.4 2.1 %collective-permute-done.7 = bf16[512,256]{0,1:T(8,128)(2,1)S(1)} collective-permute-done((bf16[512,256]{0,1:T(8,128)(2,1)}, bf16[512,256]{0,1:T(8,128)(2,1)S(1)}, u32[]{:S(2)}, u32[]{:S(2)}) %collective-permute-start.7) | collective-permute-done | bytes 262176 | tf_op jit(solution)/shard_map/ppermute | solution.py:221
  55.4 0.9 convolution_convert_fusion.2
  56.4 0.8 bitcast_reduce_fusion.2
  57.2 0.8 fusion.7
  58.0 4.4 %collective-permute-done.8 = bf16[512,256]{0,1:T(8,128)(2,1)S(1)} collective-permute-done((bf16[512,256]{0,1:T(8,128)(2,1)S(1)}, bf16[512,256]{0,1:T(8,128)(2,1)S(1)}, u32[]{:S(2)}, u32[]{:S(2)}) %collective-permute-start.8) | collective-permute-done | bytes 262176 | tf_op jit(solution)/shard_map/ppermute | solution.py:86
  62.6 1.0 fusion.52
  63.7 0.8 collective-permute-done.9
  65.3 0.9 convolution_convert_fusion.1
  66.3 1.3 collective-permute-start.11
  67.6 0.8 bitcast_reduce_fusion.1
  68.4 0.8 fusion.9
  69.2 5.5 %collective-permute-done.11 = bf16[512,256]{0,1:T(8,128)(2,1)S(1)} collective-permute-done((bf16[512,256]{0,1:T(8,128)(2,1)S(1)}, bf16[512,256]{0,1:T(8,128)(2,1)S(1)}, u32[]{:S(2)}, u32[]{:S(2)}) %collective-permute-start.11) | collective-permute-done | bytes 262176 | tf_op jit(solution)/shard_map/ppermute | solution.py:86
  74.9 1.0 fusion.49
  76.0 0.8 collective-permute-done.12
  77.6 0.9 convolution_convert_fusion
  78.6 0.8 bitcast_reduce_fusion
  79.4 0.8 fusion.10
  80.3 1.2 fusion.101
  83.6 0.7 fusion.196
  84.7 0.7 fusion.198
  85.3 1.6 %collective-permute-start.20 = (bf16[256,256]{0,1:T(8,128)(2,1)}, bf16[256,256]{0,1:T(8,128)(2,1)}, u32[]{:S(2)}, u32[]{:S(2)}) collective-permute-start(bf16[256,256]{0,1:T(8,128)(2,1)} %fusion.198), channel_id=1, source_target_pairs={{0,2},{1,3},{2,0},{3,1},{4,6},{5,7},{6,4},{7,5},{8,10},{9,11},{10,... | collective-permute-start | bytes 393224 | tf_op jit(solution)/shard_map/ppermute | solution.py:72
  87.0 3.8 %collective-permute-done.14 = bf16[256,256]{0,1:T(8,128)(2,1)S(1)} collective-permute-done((bf16[256,256]{0,1:T(8,128)(2,1)}, bf16[256,256]{0,1:T(8,128)(2,1)S(1)}, u32[]{:S(2)}, u32[]{:S(2)}) %collective-permute-start.14) | collective-permute-done | bytes 131104 | tf_op jit(solution)/shard_map/ppermute | solution.py:72
  90.8 0.7 copy-done.5
  91.4 1.5 %collective-permute-done.20 = bf16[256,256]{0,1:T(8,128)(2,1)} collective-permute-done((bf16[256,256]{0,1:T(8,128)(2,1)}, bf16[256,256]{0,1:T(8,128)(2,1)}, u32[]{:S(2)}, u32[]{:S(2)}) %collective-permute-start.20) | collective-permute-done | bytes 131104 | tf_op jit(solution)/shard_map/ppermute | solution.py:72
  92.9 1.0 fusion.193
  94.4 1.6 %collective-permute-start.21 = (bf16[256,256]{0,1:T(8,128)(2,1)S(1)}, bf16[256,256]{0,1:T(8,128)(2,1)S(1)}, u32[]{:S(2)}, u32[]{:S(2)}) collective-permute-start(bf16[256,256]{0,1:T(8,128)(2,1)S(1)} %get-tuple-element.207), channel_id=1, source_target_pairs={{0,2},{1,3},{2,0},{3,1},{4,6},{5,7},{6,4},{7,5},{8,10},{9,11},{10,... | collective-permute-start | bytes 393224 | tf_op jit(solution)/shard_map/ppermute | solution.py:86
  96.1 4.1 %collective-permute-done.15 = bf16[256,256]{0,1:T(8,128)(2,1)S(1)} collective-permute-done((bf16[256,256]{0,1:T(8,128)(2,1)S(1)}, bf16[256,256]{0,1:T(8,128)(2,1)S(1)}, u32[]{:S(2)}, u32[]{:S(2)}) %collective-permute-start.15) | collective-permute-done | bytes 131104 | tf_op jit(solution)/shard_map/ppermute | solution.py:86
  100.3 1.3 collective-permute-done.21
  102.1 1.1 collective-permute-done.22
  104.4 4.2 %fusion.104 = f32[256,1024]{0,1:T(8,128)} fusion(bf16[1024,1024]{1,0:T(8,128)(2,1)S(1)} %copy-done, bf16[256,1024]{0,1:T(8,128)(2,1)S(1)} %get-tuple-element.248, bf16[1024,1024]{1,0:T(8,128)(2,1)} %param.42), kind=kOutput, calls=%fused_computation.125 | convolution fusion | flops 1076101120 | bytes 5767168 | tf_op jit(solution)/shard_map/dot_general | solution.py:245
  108.6 1.8 %fusion.185 = bf16[256,2,256]{0,2,1:T(8,128)(2,1)} fusion(f32[256,2,2,256]{0,3,2,1:T(8,128)} %bitcast.506, s32[]{:T(128)S(6)} %select_n.689), kind=kLoop, calls=%fused_computation.247 | loop fusion | bytes 524292 | tf_op jit(solution)/shard_map/convert_element_type | solution.py:73
  110.5 4.2 %fusion.106 = f32[256,1024]{0,1:T(8,128)} fusion(bf16[1024,1024]{1,0:T(8,128)(2,1)S(1)} %copy-done, bf16[256,1024]{0,1:T(8,128)(2,1)S(1)} %get-tuple-element.247, bf16[1024,1024]{1,0:T(8,128)(2,1)} %param.42), kind=kOutput, calls=%fused_computation.126 | convolution fusion | flops 1076101120 | bytes 5767168 | tf_op jit(solution)/shard_map/dot_general | solution.py:245
  114.7 1.1 fusion.184
  116.2 1.1 bitcast_add_fusion
  117.9 1.1 bitcast_add_fusion.2
  119.1 1.6 %collective-permute-start.18 = (bf16[256,256]{0,1:T(8,128)(2,1)S(1)}, bf16[256,256]{0,1:T(8,128)(2,1)S(1)}, u32[]{:S(2)}, u32[]{:S(2)}) collective-permute-start(bf16[256,256]{0,1:T(8,128)(2,1)S(1)} %fusion.197), channel_id=1, source_target_pairs={{0,2},{1,3},{2,0},{3,1},{4,6},{5,7},{6,4},{7,5},{8,10},{9,11},{10,... | collective-permute-start | bytes 393224 | tf_op jit(solution)/shard_map/ppermute | solution.py:72
  120.7 3.1 %collective-permute-done.24 = bf16[256,256]{0,1:T(8,128)(2,1)S(1)} collective-permute-done((bf16[256,256]{0,1:T(8,128)(2,1)S(1)}, bf16[256,256]{0,1:T(8,128)(2,1)S(1)}, u32[]{:S(2)}, u32[]{:S(2)}) %collective-permute-start.24) | collective-permute-done | bytes 131104 | tf_op jit(solution)/shard_map/ppermute | solution.py:72
  123.8 2.0 %collective-permute-done.18 = bf16[256,256]{0,1:T(8,128)(2,1)S(1)} collective-permute-done((bf16[256,256]{0,1:T(8,128)(2,1)S(1)}, bf16[256,256]{0,1:T(8,128)(2,1)S(1)}, u32[]{:S(2)}, u32[]{:S(2)}) %collective-permute-start.18) | collective-permute-done | bytes 131104 | tf_op jit(solution)/shard_map/ppermute | solution.py:72
  125.9 0.8 copy.68
  (138 shorter events, 14.3 us)
Async XLA Ops:
  0.0 104.4 %copy-start = (bf16[1024,1024]{1,0:T(8,128)(2,1)S(1)}, bf16[1024,1024]{1,0:T(8,128)(2,1)}, u32[]{:S(2)}) copy-start(bf16[1024,1024]{1,0:T(8,128)(2,1)} %param.43) | copy-start | bytes 6291460
  0.9 15.3 %collective-permute-start.1 = (bf16[64,256]{1,0:T(8,128)(2,1)S(1)}, bf16[64,256]{1,0:T(8,128)(2,1)S(1)}, u32[]{:S(2)}, u32[]{:S(2)}) collective-permute-start(bf16[64,256]{1,0:T(8,128)(2,1)S(1)} %get-tuple-element.213), channel_id=1, source_target_pairs={{4,0},{8,4},{12,8},{5,1},{9,5},{13,9},{6,2},{10,6},{14,10},{7,3},{... | collective-permute-start | bytes 98312 | tf_op jit(solution)/shard_map/ppermute | solution.py:21
  2.2 14.0 %collective-permute-start = (bf16[64,256]{1,0:T(8,128)(2,1)S(1)}, bf16[64,256]{1,0:T(8,128)(2,1)S(1)}, u32[]{:S(2)}, u32[]{:S(2)}) collective-permute-start(bf16[64,256]{1,0:T(8,128)(2,1)S(1)} %get-tuple-element.212), channel_id=1, source_target_pairs={{0,4},{4,8},{8,12},{1,5},{5,9},{9,13},{2,6},{6,10},{10,14},{3,7},{... | collective-permute-start | bytes 98312 | tf_op jit(solution)/shard_map/ppermute | solution.py:20
  11.9 5.5 %copy-start.1 = (bf16[512,256]{0,1:T(8,128)(2,1)}, bf16[512,256]{0,1:T(8,128)(2,1)S(1)}, u32[]{:S(2)}) copy-start(bf16[512,256]{0,1:T(8,128)(2,1)S(1)} %copy.27) | copy-start | bytes 786436
  17.6 19.9 %copy-start.6 = (bf16[1024]{0:T(1024)(128)(2,1)S(1)}, bf16[1024]{0:T(1024)(128)(2,1)}, u32[]{:S(2)}) copy-start(bf16[1024]{0:T(1024)(128)(2,1)} %param.36) | copy-start | bytes 6148
  17.6 19.9 %copy-start.8 = (s32[4,4]{1,0:T(4,128)S(1)}, s32[4,4]{1,0:T(4,128)}, u32[]{:S(2)}) copy-start(s32[4,4]{1,0:T(4,128)} %param.33) | copy-start | bytes 196
  23.4 9.7 %collective-permute-start.4 = (bf16[512,256]{0,1:T(8,128)(2,1)S(1)}, bf16[512,256]{0,1:T(8,128)(2,1)}, u32[]{:S(2)}, u32[]{:S(2)}) collective-permute-start(bf16[512,256]{0,1:T(8,128)(2,1)S(1)} %fusion.146), channel_id=1, source_target_pairs={{0,4},{4,8},{8,12},{12,0},{1,5},{5,9},{9,13},{13,1},{2,6},{6,10},{... | collective-permute-start | bytes 786440 | tf_op jit(solution)/shard_map/ppermute | solution.py:199
  25.5 9.3 %collective-permute-start.2 = (bf16[512,256]{0,1:T(8,128)(2,1)S(1)}, bf16[512,256]{0,1:T(8,128)(2,1)S(1)}, u32[]{:S(2)}, u32[]{:S(2)}) collective-permute-start(bf16[512,256]{0,1:T(8,128)(2,1)S(1)} %fusion.146), channel_id=1, source_target_pairs={{0,2},{1,3},{2,0},{3,1},{4,6},{5,7},{6,4},{7,5},{8,10},{9,11},{10,... | collective-permute-start | bytes 786440 | tf_op jit(solution)/shard_map/ppermute | solution.py:86
  33.1 10.6 %collective-permute-start.5 = (bf16[512,256]{0,1:T(8,128)(2,1)}, bf16[512,256]{0,1:T(8,128)(2,1)}, u32[]{:S(2)}, u32[]{:S(2)}) collective-permute-start(bf16[512,256]{0,1:T(8,128)(2,1)} %collective-permute-done.4), channel_id=1, source_target_pairs={{0,2},{1,3},{2,0},{3,1},{4,6},{5,7},{6,4},{7,5},{8,10},{9,11},{10,... | collective-permute-start | bytes 786440 | tf_op jit(solution)/shard_map/ppermute | solution.py:86
  35.7 9.8 %collective-permute-start.3 = (bf16[512,2,256]{0,2,1:T(8,128)(2,1)}, bf16[512,2,256]{0,2,1:T(8,128)(2,1)}, u32[]{:S(2)}, u32[]{:S(2)}) collective-permute-start(bf16[512,2,256]{0,2,1:T(8,128)(2,1)} %pad_maximum_fusion.4), channel_id=1, source_target_pairs={{0,1},{1,0},{2,3},{3,2},{4,5},{5,4},{6,7},{7,6},{8,9},{9,8},{10,11... | collective-permute-start | bytes 1572872 | tf_op jit(solution)/shard_map/ppermute | solution.py:86
  43.7 10.7 %collective-permute-start.7 = (bf16[512,256]{0,1:T(8,128)(2,1)}, bf16[512,256]{0,1:T(8,128)(2,1)S(1)}, u32[]{:S(2)}, u32[]{:S(2)}) collective-permute-start(bf16[512,256]{0,1:T(8,128)(2,1)} %collective-permute-done.4), channel_id=1, source_target_pairs={{0,4},{4,8},{8,12},{12,0},{1,5},{5,9},{9,13},{13,1},{2,6},{6,10},{... | collective-permute-start | bytes 786440 | tf_op jit(solution)/shard_map/ppermute | solution.py:221
  44.9 7.2 %collective-permute-start.6 = (bf16[512,2,256]{0,2,1:T(8,128)(2,1)S(1)}, bf16[512,2,256]{0,2,1:T(8,128)(2,1)S(1)}, u32[]{:S(2)}, u32[]{:S(2)}) collective-permute-start(bf16[512,2,256]{0,2,1:T(8,128)(2,1)S(1)} %pad_maximum_fusion.5), channel_id=1, source_target_pairs={{0,1},{1,0},{2,3},{3,2},{4,5},{5,4},{6,7},{7,6},{8,9},{9,8},{10,11... | collective-permute-start | bytes 1572872 | tf_op jit(solution)/shard_map/ppermute | solution.py:86
  46.9 1.2 copy-start.4
  47.5 1.5 %copy-start.9 = (bf16[1024,256]{1,0:T(8,128)(2,1)S(1)}, bf16[1024,256]{1,0:T(8,128)(2,1)}, u32[]{:S(2)}) copy-start(bf16[1024,256]{1,0:T(8,128)(2,1)} %param.37) | copy-start | bytes 1572868
  54.5 7.9 %collective-permute-start.8 = (bf16[512,256]{0,1:T(8,128)(2,1)S(1)}, bf16[512,256]{0,1:T(8,128)(2,1)S(1)}, u32[]{:S(2)}, u32[]{:S(2)}) collective-permute-start(bf16[512,256]{0,1:T(8,128)(2,1)S(1)} %collective-permute-done.7), channel_id=1, source_target_pairs={{0,2},{1,3},{2,0},{3,1},{4,6},{5,7},{6,4},{7,5},{8,10},{9,11},{10,... | collective-permute-start | bytes 786440 | tf_op jit(solution)/shard_map/ppermute | solution.py:86
  54.8 9.9 %collective-permute-start.10 = (bf16[512,256]{0,1:T(8,128)(2,1)S(1)}, bf16[512,256]{0,1:T(8,128)(2,1)S(1)}, u32[]{:S(2)}, u32[]{:S(2)}) collective-permute-start(bf16[512,256]{0,1:T(8,128)(2,1)S(1)} %collective-permute-done.7), channel_id=1, source_target_pairs={{0,4},{4,8},{8,12},{12,0},{1,5},{5,9},{9,13},{13,1},{2,6},{6,10},{... | collective-permute-start | bytes 786440 | tf_op jit(solution)/shard_map/ppermute | solution.py:221
  62.5 2.0 %collective-permute-start.9 = (bf16[512,2,256]{0,2,1:T(8,128)(2,1)S(1)}, bf16[512,2,256]{0,2,1:T(8,128)(2,1)S(1)}, u32[]{:S(2)}, u32[]{:S(2)}) collective-permute-start(bf16[512,2,256]{0,2,1:T(8,128)(2,1)S(1)} %pad_maximum_fusion.6), channel_id=1, source_target_pairs={{0,1},{1,0},{2,3},{3,2},{4,5},{5,4},{6,7},{7,6},{8,9},{9,8},{10,11... | collective-permute-start | bytes 1572872 | tf_op jit(solution)/shard_map/ppermute | solution.py:86
  66.3 8.4 %collective-permute-start.11 = (bf16[512,256]{0,1:T(8,128)(2,1)S(1)}, bf16[512,256]{0,1:T(8,128)(2,1)S(1)}, u32[]{:S(2)}, u32[]{:S(2)}) collective-permute-start(bf16[512,256]{0,1:T(8,128)(2,1)S(1)} %collective-permute-done.10), channel_id=1, source_target_pairs={{0,2},{1,3},{2,0},{3,1},{4,6},{5,7},{6,4},{7,5},{8,10},{9,11},{10,... | collective-permute-start | bytes 786440 | tf_op jit(solution)/shard_map/ppermute | solution.py:86
  74.8 2.0 %collective-permute-start.12 = (bf16[512,2,256]{0,2,1:T(8,128)(2,1)S(1)}, bf16[512,2,256]{0,2,1:T(8,128)(2,1)S(1)}, u32[]{:S(2)}, u32[]{:S(2)}) collective-permute-start(bf16[512,2,256]{0,2,1:T(8,128)(2,1)S(1)} %pad_maximum_fusion.7), channel_id=1, source_target_pairs={{0,1},{1,0},{2,3},{3,2},{4,5},{5,4},{6,7},{7,6},{8,9},{9,8},{10,11... | collective-permute-start | bytes 1572872 | tf_op jit(solution)/shard_map/ppermute | solution.py:86
  81.5 12.9 %copy-start.7 = (bf16[1024]{0:T(1024)(128)(2,1)S(1)}, bf16[1024]{0:T(1024)(128)(2,1)}, u32[]{:S(2)}) copy-start(bf16[1024]{0:T(1024)(128)(2,1)} %param.41) | copy-start | bytes 6148
  81.9 1.6 %collective-permute-start.13 = (bf16[256,2,256]{0,2,1:T(8,128)(2,1)S(1)}, bf16[256,2,256]{0,2,1:T(8,128)(2,1)S(1)}, u32[]{:S(2)}, u32[]{:S(2)}) collective-permute-start(bf16[256,2,256]{0,2,1:T(8,128)(2,1)S(1)} %fusion.182), channel_id=1, source_target_pairs={{0,1},{1,0},{2,3},{3,2},{4,5},{5,4},{6,7},{7,6},{8,9},{9,8},{10,11... | collective-permute-start | bytes 786440 | tf_op jit(solution)/shard_map/ppermute | solution.py:72
  82.4 2.2 %collective-permute-start.19 = (bf16[256,2,256]{0,2,1:T(8,128)(2,1)S(1)}, bf16[256,2,256]{0,2,1:T(8,128)(2,1)S(1)}, u32[]{:S(2)}, u32[]{:S(2)}) collective-permute-start(bf16[256,2,256]{0,2,1:T(8,128)(2,1)S(1)} %fusion.183), channel_id=1, source_target_pairs={{0,1},{1,0},{2,3},{3,2},{4,5},{5,4},{6,7},{7,6},{8,9},{9,8},{10,11... | collective-permute-start | bytes 786440 | tf_op jit(solution)/shard_map/ppermute | solution.py:72
  84.2 6.5 %collective-permute-start.14 = (bf16[256,256]{0,1:T(8,128)(2,1)}, bf16[256,256]{0,1:T(8,128)(2,1)S(1)}, u32[]{:S(2)}, u32[]{:S(2)}) collective-permute-start(bf16[256,256]{0,1:T(8,128)(2,1)} %fusion.196), channel_id=1, source_target_pairs={{0,2},{1,3},{2,0},{3,1},{4,6},{5,7},{6,4},{7,5},{8,10},{9,11},{10,... | collective-permute-start | bytes 393224 | tf_op jit(solution)/shard_map/ppermute | solution.py:72
  85.3 7.6 %collective-permute-start.20 = (bf16[256,256]{0,1:T(8,128)(2,1)}, bf16[256,256]{0,1:T(8,128)(2,1)}, u32[]{:S(2)}, u32[]{:S(2)}) collective-permute-start(bf16[256,256]{0,1:T(8,128)(2,1)} %fusion.198), channel_id=1, source_target_pairs={{0,2},{1,3},{2,0},{3,1},{4,6},{5,7},{6,4},{7,5},{8,10},{9,11},{10,... | collective-permute-start | bytes 393224 | tf_op jit(solution)/shard_map/ppermute | solution.py:72
  90.8 0.7 copy-start.5
  94.0 9.5 %copy-start.2 = (bf16[256,256]{0,1:T(8,128)(2,1)}, bf16[256,256]{0,1:T(8,128)(2,1)S(1)}, u32[]{:S(2)}) copy-start(bf16[256,256]{0,1:T(8,128)(2,1)S(1)} %get-tuple-element.207) | copy-start | bytes 393220
  94.0 6.2 %collective-permute-start.15 = (bf16[256,256]{0,1:T(8,128)(2,1)S(1)}, bf16[256,256]{0,1:T(8,128)(2,1)S(1)}, u32[]{:S(2)}, u32[]{:S(2)}) collective-permute-start(bf16[256,256]{0,1:T(8,128)(2,1)S(1)} %get-tuple-element.206), channel_id=1, source_target_pairs={{0,2},{1,3},{2,0},{3,1},{4,6},{5,7},{6,4},{7,5},{8,10},{9,11},{10,... | collective-permute-start | bytes 393224 | tf_op jit(solution)/shard_map/ppermute | solution.py:86
  94.4 7.1 %collective-permute-start.21 = (bf16[256,256]{0,1:T(8,128)(2,1)S(1)}, bf16[256,256]{0,1:T(8,128)(2,1)S(1)}, u32[]{:S(2)}, u32[]{:S(2)}) collective-permute-start(bf16[256,256]{0,1:T(8,128)(2,1)S(1)} %get-tuple-element.207), channel_id=1, source_target_pairs={{0,2},{1,3},{2,0},{3,1},{4,6},{5,7},{6,4},{7,5},{8,10},{9,11},{10,... | collective-permute-start | bytes 393224 | tf_op jit(solution)/shard_map/ppermute | solution.py:86
  100.2 1.6 %collective-permute-start.16 = (bf16[256,2,256]{0,2,1:T(8,128)(2,1)S(1)}, bf16[256,2,256]{0,2,1:T(8,128)(2,1)S(1)}, u32[]{:S(2)}, u32[]{:S(2)}) collective-permute-start(bf16[256,2,256]{0,2,1:T(8,128)(2,1)S(1)} %pad_maximum_fusion.8), channel_id=1, source_target_pairs={{0,1},{1,0},{2,3},{3,2},{4,5},{5,4},{6,7},{7,6},{8,9},{9,8},{10,11... | collective-permute-start | bytes 786440 | tf_op jit(solution)/shard_map/ppermute | solution.py:86
  101.6 1.6 %collective-permute-start.22 = (bf16[256,2,256]{0,2,1:T(8,128)(2,1)S(1)}, bf16[256,2,256]{0,2,1:T(8,128)(2,1)S(1)}, u32[]{:S(2)}, u32[]{:S(2)}) collective-permute-start(bf16[256,2,256]{0,2,1:T(8,128)(2,1)S(1)} %pad_maximum_fusion.9), channel_id=1, source_target_pairs={{0,1},{1,0},{2,3},{3,2},{4,5},{5,4},{6,7},{7,6},{8,9},{9,8},{10,11... | collective-permute-start | bytes 786440 | tf_op jit(solution)/shard_map/ppermute | solution.py:86
  110.4 5.9 %collective-permute-start.23 = (bf16[256,2,256]{0,2,1:T(8,128)(2,1)}, bf16[256,2,256]{0,2,1:T(8,128)(2,1)S(1)}, u32[]{:S(2)}, u32[]{:S(2)}) collective-permute-start(bf16[256,2,256]{0,2,1:T(8,128)(2,1)} %fusion.185), channel_id=1, source_target_pairs={{0,1},{1,0},{2,3},{3,2},{4,5},{5,4},{6,7},{7,6},{8,9},{9,8},{10,11... | collective-permute-start | bytes 786440 | tf_op jit(solution)/shard_map/ppermute | solution.py:72
  110.5 13.3 %copy-start.3 = (bf16[256,256]{0,1:T(8,128)(2,1)S(1)}, bf16[256,256]{0,1:T(8,128)(2,1)}, u32[]{:S(2)}) copy-start(bf16[256,256]{0,1:T(8,128)(2,1)} %copy-done.2) | copy-start | bytes 393220
  115.8 2.1 %collective-permute-start.17 = (bf16[256,2,256]{0,2,1:T(8,128)(2,1)S(1)}, bf16[256,2,256]{0,2,1:T(8,128)(2,1)S(1)}, u32[]{:S(2)}, u32[]{:S(2)}) collective-permute-start(bf16[256,2,256]{0,2,1:T(8,128)(2,1)S(1)} %fusion.184), channel_id=1, source_target_pairs={{0,1},{1,0},{2,3},{3,2},{4,5},{5,4},{6,7},{7,6},{8,9},{9,8},{10,11... | collective-permute-start | bytes 786440 | tf_op jit(solution)/shard_map/ppermute | solution.py:72
  117.4 6.4 %collective-permute-start.24 = (bf16[256,256]{0,1:T(8,128)(2,1)S(1)}, bf16[256,256]{0,1:T(8,128)(2,1)S(1)}, u32[]{:S(2)}, u32[]{:S(2)}) collective-permute-start(bf16[256,256]{0,1:T(8,128)(2,1)S(1)} %fusion.199), channel_id=1, source_target_pairs={{0,2},{1,3},{2,0},{3,1},{4,6},{5,7},{6,4},{7,5},{8,10},{9,11},{10,... | collective-permute-start | bytes 393224 | tf_op jit(solution)/shard_map/ppermute | solution.py:72
  119.1 6.7 %collective-permute-start.18 = (bf16[256,256]{0,1:T(8,128)(2,1)S(1)}, bf16[256,256]{0,1:T(8,128)(2,1)S(1)}, u32[]{:S(2)}, u32[]{:S(2)}) collective-permute-start(bf16[256,256]{0,1:T(8,128)(2,1)S(1)} %fusion.197), channel_id=1, source_target_pairs={{0,2},{1,3},{2,0},{3,1},{4,6},{5,7},{6,4},{7,5},{8,10},{9,11},{10,... | collective-permute-start | bytes 393224 | tf_op jit(solution)/shard_map/ppermute | solution.py:72

commit v8 on v6

--- a/solution.py
+++ b/solution.py
@@ -200,7 +200,7 @@
     row_max, row_mass, weighted = state
     attended = (weighted / jnp.transpose(row_mass, (0, 2, 1))[:, :, :, None]).astype(jnp.bfloat16)
     attended = attended.reshape(row_count, local_width)
-    chunk_count = 2 if row_count % 16 == 0 else 1
+    chunk_count = 4 if row_count % 32 == 0 else 1
     chunk_rows = row_count // chunk_count
     outputs = []
     for chunk in range(chunk_count):

time: 124 us -> 181 us (1.46)
  other arithmetic: 18.5 us -> 47.3 us
  local copies, waits for them, and re-layouts: 14.9 us -> 40.5 us
  waiting for transfers between devices: 42.3 us -> 29.7 us
  starting transfers between devices: 22.3 us -> 30.6 us
  matrix products: 20.3 us -> 26.3 us
    unnamed x26 -> x105, local copies, waits for them, and re-layouts: 2.52 us -> 11.1 us
    convert_element_type x3 -> x5, local copies, waits for them, and re-layouts: 0.33 us -> 7.17 us  [layer_norm(): values = inputs.astype(jnp.float32)]
    another operation x3, local copies, waits for them, and re-layouts: 0.21 us -> 6.86 us  [gather_heads(): current = jnp.stack([low, high], axis=current.ndim - 1)]
    reduce_sum x6 -> x8, other arithmetic: 1.77 us -> 7.75 us  [layer_norm(): spread = jnp.mean(center * center, axis=-1, keepdims=True)]
    another operation x20 -> x26, other arithmetic: 5.08 us -> 11 us  [gather_heads(): current = jnp.stack([low, high], axis=current.ndim - 1)]
    ppermute x8 -> x16, starting transfers between devices: 5.6 us -> 10.7 us  [scatter_heads(): lax.ppermute(give.astype(jnp.bfloat16), 'heads', [(i, i ^ bit) for i in r...]
    dynamic_slice x0 -> x12, local copies, waits for them, and re-layouts: none -> 5.06 us  [the longest x8 3.67 us: scatter_heads(): keep = lax.dynamic_index_in_dim(current, mine, axis, keepdims=False)]
    ppermute x8 -> x16, waiting for transfers between devices: 11.3 us -> 6.88 us  [scatter_heads(): lax.ppermute(give.astype(jnp.bfloat16), 'heads', [(i, i ^ bit) for i in r...]
  transfers between devices with their start and end apart: 25 -> 37, of which waited for: 17 -> 14; matrix products, arithmetic and copies ran while one was open for 29% -> 34% of each run, Pallas kernels for 0% -> 0%
where the time goes in v8:
time: 181 us; the launch traced here: 179 us
  other arithmetic  47.3 us (26%)
  local copies, waits for them, and re-layouts  40.5 us (22%)
  starting transfers between devices  30.6 us (17%)
  waiting for transfers between devices  29.7 us (16%)
  matrix products  26.3 us (15%)
  between operations  5.05 us (3%)
    ppermute x16, waiting for transfers between devices, gather_heads(): lax.ppermute(current, 'heads', [(i, i ^ bit) for i in range(head_total)])  16.6 us
    dot_general x4, matrix products, shards(): lowered = jnp.dot(hidden, down_weight, preferred_element_type=jnp.float32)  11.8 us
    unnamed x105, local copies, waits for them, and re-layouts  11.1 us
    another operation x26, other arithmetic, gather_heads(): current = jnp.stack([low, high], axis=current.ndim - 1)  11 us
    ppermute x16, starting transfers between devices, scatter_heads(): lax.ppermute(give.astype(jnp.bfloat16), 'heads', [(i, i ^ bit) for i in r...  10.7 us
    ppermute x16, starting transfers between devices, gather_heads(): lax.ppermute(current, 'heads', [(i, i ^ bit) for i in range(head_total)])  10.5 us
    reduce_sum x8, other arithmetic, layer_norm(): spread = jnp.mean(center * center, axis=-1, keepdims=True)  7.75 us
    convert_element_type x5, local copies, waits for them, and re-layouts, layer_norm(): values = inputs.astype(jnp.float32)  7.17 us
  transfers between devices with their start and end apart: 37, of which 14 were waited for; matrix products, arithmetic and copies ran while one was open for 34% of the time, Pallas kernels for 0%

profile of v8, /device:TPU:0, one launch (start us, length us, event | category | flops | bytes accessed | tf_op | source)
XLA Modules:
  0.0 179.5 jit_solution(16887818579430427809)
XLA Ops:
  0.9 1.3 collective-permute-start.1
  2.2 5.6 %collective-permute-start = (bf16[64,256]{1,0:T(8,128)(2,1)S(1)}, bf16[64,256]{1,0:T(8,128)(2,1)S(1)}, u32[]{:S(2)}, u32[]{:S(2)}) collective-permute-start(bf16[64,256]{1,0:T(8,128)(2,1)S(1)} %get-tuple-element.216), channel_id=1, source_target_pairs={{0,4},{4,8},{8,12},{1,5},{5,9},{9,13},{2,6},{6,10},{10,14},{3,7},{... | collective-permute-start | bytes 98312 | tf_op jit(solution)/shard_map/ppermute | solution.py:20
  7.8 1.0 fusion.253
  9.7 1.4 fusion.256
  14.3 1.6 fusion.117
  15.9 2.1 %collective-permute-start.4 = (bf16[512,256]{1,0:T(8,128)(2,1)S(1)}, bf16[512,256]{1,0:T(8,128)(2,1)}, u32[]{:S(2)}, u32[]{:S(2)}) collective-permute-start(bf16[512,256]{1,0:T(8,128)(2,1)S(1)} %fusion.158), channel_id=1, source_target_pairs={{0,4},{4,8},{8,12},{12,0},{1,5},{5,9},{9,13},{13,1},{2,6},{6,10},{... | collective-permute-start | bytes 786440 | tf_op jit(solution)/shard_map/ppermute | solution.py:170
  18.0 1.5 collective-permute-start.2
  19.5 6.2 %collective-permute-done.4 = bf16[512,256]{1,0:T(8,128)(2,1)} collective-permute-done((bf16[512,256]{1,0:T(8,128)(2,1)S(1)}, bf16[512,256]{1,0:T(8,128)(2,1)}, u32[]{:S(2)}, u32[]{:S(2)}) %collective-permute-start.4) | collective-permute-done | bytes 262176 | tf_op jit(solution)/shard_map/ppermute | solution.py:170
  25.7 1.6 collective-permute-start.5
  28.9 3.8 %collective-permute-done.5 = bf16[512,256]{1,0:T(8,128)(2,1)S(1)} collective-permute-done((bf16[512,256]{1,0:T(8,128)(2,1)}, bf16[512,256]{1,0:T(8,128)(2,1)S(1)}, u32[]{:S(2)}, u32[]{:S(2)}) %collective-permute-start.5) | collective-permute-done | bytes 262176 | tf_op jit(solution)/shard_map/ppermute | solution.py:86
  38.7 1.2 copy.80
  39.9 1.1 constant_dynamic-update-slice_fusion.1
  41.1 1.1 constant_dynamic-update-slice_fusion
  44.0 2.5 %select_bitcast_fusion.5 = (bf16[512,2,1,256]{3,0,1,2:T(8,128)(2,1)}, bf16[512,2,1,256]{3,0,1,2:T(8,128)(2,1)}, bf16[512,2,1,256]{3,0,1,2:T(8,128)(2,1)S(1)}, bf16[512,2,1,256]{3,0,1,2:T(8,128)(2,1)S(1)}) fusion(bf16[512,2,256]{2,0,1:T(8,128)(2,1)} %collective-permute-done.6, pred[]{:T(512)S(6)} %eq.9, bf16[512,1,256]{2,0,1:T(8,128)(2,1)S(1)} %copy-done.11, ...), kind=kLoop, calls=%fused_computation.221 | loop fusion | flops 1572864 | bytes 4194305 | tf_op jit(solution)/shard_map/stack | solution.py:89
  46.5 1.5 maximum_convert_fusion
  48.3 2.9 %copy.29 = f32[512,2,2,256]{0,3,2,1:T(8,128)} copy(f32[512,2,2,256]{3,0,1,2:T(8,128)} %maximum_convert_fusion) | data formatting | bytes 4194304 | tf_op jit(solution)/shard_map/convert_element_type | solution.py:27
  51.2 1.5 multiply_reduce_fusion
  52.7 1.9 %fusion.33 = bf16[512,1024]{0,1:T(8,128)(2,1)S(1)} fusion(f32[512,2,2,256]{0,3,2,1:T(8,128)} %copy.29, f32[1024]{0:T(1024)S(1)} %convert_element_type.368, f32[512]{0:T(512)S(1)} %add_rsqrt_fusion.3, f32[512]{0:T(512)S(1)} %broadcast_multiply_fusion.3), kind=kLoop, calls=%fused_computation.56 | loop fusion | flops 2097152 | bytes 3153920 | tf_op jit(solution)/shard_map/convert_element_type | solution.py:174
  58.3 1.1 copy-done.1
  59.4 1.1 pad_maximum_fusion
  60.5 2.3 %copy.31 = bf16[512,2,2,256]{0,3,2,1:T(8,128)(2,1)} copy(bf16[512,2,2,256]{3,0,1,2:T(8,128)(2,1)} %pad_maximum_fusion) | data formatting | bytes 2097152 | tf_op jit(solution)/shard_map/stack | solution.py:89
  62.8 3.3 %fusion.61 = f32[1,512,4,64]{1,3,2,0:T(8,128)S(1)} fusion(bf16[512,4,64]{0,2,1:T(8,128)(2,1)S(1)} %bitcast.616, f32[4,512,512]{2,1,0:T(8,128)} %copy-done.1, f32[4,512]{1,0:T(4,128)S(1)} %get-tuple-element.257, pred[]{:T(512)} %bitcast.39, f32[512,4]{0,1:T(4,128)S(1)} %get-tuple-element.255), kind=kOutput, calls=%fused_computation.79 | convolution fusion | flops 138543104 | bytes 4997121 | tf_op jit(solution)/shard_map/bhqk,khd->bqhd/dot_general | solution.py:107
  66.1 1.4 collective-permute-start.8
  71.1 3.9 %collective-permute-done.8 = bf16[512,256]{1,0:T(8,128)(2,1)S(1)} collective-permute-done((bf16[512,256]{1,0:T(8,128)(2,1)}, bf16[512,256]{1,0:T(8,128)(2,1)S(1)}, u32[]{:S(2)}, u32[]{:S(2)}) %collective-permute-start.8) | collective-permute-done | bytes 262176 | tf_op jit(solution)/shard_map/ppermute | solution.py:86
  75.0 1.0 select_bitcast_fusion.11
  78.2 1.1 pad_maximum_fusion.1
  79.2 2.3 %copy.33 = bf16[512,2,2,256]{0,3,2,1:T(8,128)(2,1)} copy(bf16[512,2,2,256]{3,0,1,2:T(8,128)(2,1)} %pad_maximum_fusion.1) | data formatting | bytes 2097152 | tf_op jit(solution)/shard_map/stack | solution.py:89
  81.5 1.6 convert_reduce_fusion.1
  83.1 1.6 fusion.21
  85.7 1.4 collective-permute-start.11
  88.8 5.9 %collective-permute-done.11 = bf16[512,256]{1,0:T(8,128)(2,1)S(1)} collective-permute-done((bf16[512,256]{1,0:T(8,128)(2,1)}, bf16[512,256]{1,0:T(8,128)(2,1)S(1)}, u32[]{:S(2)}, u32[]{:S(2)}) %collective-permute-start.11) | collective-permute-done | bytes 262176 | tf_op jit(solution)/shard_map/ppermute | solution.py:86
  94.7 1.0 select_bitcast_fusion.9
  97.9 1.1 pad_maximum_fusion.2
  99.0 2.3 %copy.35 = bf16[512,2,2,256]{0,3,2,1:T(8,128)(2,1)} copy(bf16[512,2,2,256]{3,0,1,2:T(8,128)(2,1)} %pad_maximum_fusion.2) | data formatting | bytes 2097152 | tf_op jit(solution)/shard_map/stack | solution.py:89
  101.2 1.6 convert_reduce_fusion
  102.8 1.6 fusion.18
  107.2 1.0 fusion.82
  111.6 1.4 collective-permute-start.14
  115.1 1.4 collective-permute-start.26
  118.6 1.3 collective-permute-done.26
  119.9 1.6 collective-permute-done.20
  121.4 1.1 fusion.203
  123.4 1.3 collective-permute-start.21
  125.4 1.3 collective-permute-start.33
  134.3 1.0 copy.39
  136.1 1.1 multiply_reduce_fusion.3
  137.2 1.0 copy.46
  138.9 1.2 multiply_reduce_fusion.2
  142.0 1.2 copy.60
  143.3 2.5 %fusion.156 = (bf16[128,1024]{0,1:T(8,128)(2,1)S(1)}, bf16[128,1024]{0,1:T(8,128)(2,1)}, bf16[128,1024]{0,1:T(8,128)(2,1)}, bf16[128,1024]{0,1:T(8,128)(2,1)}) fusion(f32[128,2,2,256]{0,3,2,1:T(8,128)S(1)} %copy-done.23, f32[1024]{0:T(1024)S(1)} %convert_element_type.397, f32[128]{0:T(128)S(1)} %copy-done.48, f32[128]{0:T(128)S(1)} %broadcast_multiply_fusion.7, ...), kind=kLoop, calls=%fused_computation.206 | loop fusion | flops 2097152 | bytes 3153920 | tf_op jit(solution)/shard_map/convert_element_type | solution.py:212
  145.7 3.0 %fusion.160 = f32[128,1024]{0,1:T(8,128)S(1)} fusion(bf16[1024,1024]{1,0:T(8,128)(2,1)S(1)} %copy-done, bf16[128,1024]{0,1:T(8,128)(2,1)} %get-tuple-element.262, bf16[1024,1024]{1,0:T(8,128)(2,1)} %param.42), kind=kOutput, calls=%fused_computation.225 | convolution fusion | flops 538050560 | bytes 4980736 | tf_op jit(solution)/shard_map/dot_general | solution.py:216
  150.1 2.9 %fusion.162 = f32[128,1024]{0,1:T(8,128)S(1)} fusion(bf16[1024,1024]{1,0:T(8,128)(2,1)S(1)} %copy-done, bf16[128,1024]{0,1:T(8,128)(2,1)S(1)} %copy-done.26, bf16[1024,1024]{1,0:T(8,128)(2,1)} %param.42), kind=kOutput, calls=%fused_computation.226 | convolution fusion | flops 538050560 | bytes 4980736 | tf_op jit(solution)/shard_map/dot_general | solution.py:216
  153.7 3.1 %fusion.164 = f32[128,1024]{0,1:T(8,128)S(1)} fusion(bf16[1024,1024]{1,0:T(8,128)(2,1)S(1)} %copy-done, bf16[128,1024]{0,1:T(8,128)(2,1)S(1)} %copy-done.25, bf16[1024,1024]{1,0:T(8,128)(2,1)} %param.42), kind=kOutput, calls=%fused_computation.227 | convolution fusion | flops 538050560 | bytes 4980736 | tf_op jit(solution)/shard_map/dot_general | solution.py:216
  156.8 1.8 copy.62
  158.6 1.7 copy.87
  161.6 1.7 copy.85
  164.7 2.8 %fusion.166 = f32[128,1024]{0,1:T(8,128)S(1)} fusion(bf16[1024,1024]{1,0:T(8,128)(2,1)S(1)} %copy-done, bf16[128,1024]{0,1:T(8,128)(2,1)S(1)} %get-tuple-element.259, bf16[1024,1024]{1,0:T(8,128)(2,1)} %param.42), kind=kOutput, calls=%fused_computation.228 | convolution fusion | flops 538050560 | bytes 4980736 | tf_op jit(solution)/shard_map/dot_general | solution.py:216
  168.0 1.0 bitcast_add_fusion.1
  169.0 1.1 collective-permute-start.36
  170.1 1.0 bitcast_add_fusion.3
  171.1 1.0 collective-permute-start.30
  173.1 1.1 collective-permute-start.24
  174.3 1.0 collective-permute-start.18
  175.5 2.5 %collective-permute-done.24 = bf16[128,256]{1,0:T(8,128)(2,1)S(1)} collective-permute-done((bf16[128,256]{1,0:T(8,128)(2,1)S(1)}, bf16[128,256]{1,0:T(8,128)(2,1)S(1)}, u32[]{:S(2)}, u32[]{:S(2)}) %collective-permute-start.24) | collective-permute-done | bytes 65568 | tf_op jit(solution)/shard_map/ppermute | solution.py:72
  (282 shorter events, 55.2 us)
Async XLA Ops:
  0.0 145.7 %copy-start = (bf16[1024,1024]{1,0:T(8,128)(2,1)S(1)}, bf16[1024,1024]{1,0:T(8,128)(2,1)}, u32[]{:S(2)}) copy-start(bf16[1024,1024]{1,0:T(8,128)(2,1)} %param.43) | copy-start | bytes 6291460
  0.9 13.0 %collective-permute-start.1 = (bf16[64,256]{1,0:T(8,128)(2,1)S(1)}, bf16[64,256]{1,0:T(8,128)(2,1)S(1)}, u32[]{:S(2)}, u32[]{:S(2)}) collective-permute-start(bf16[64,256]{1,0:T(8,128)(2,1)S(1)} %get-tuple-element.217), channel_id=1, source_target_pairs={{4,0},{8,4},{12,8},{5,1},{9,5},{13,9},{6,2},{10,6},{14,10},{7,3},{... | collective-permute-start | bytes 98312 | tf_op jit(solution)/shard_map/ppermute | solution.py:21
  2.2 11.7 %collective-permute-start = (bf16[64,256]{1,0:T(8,128)(2,1)S(1)}, bf16[64,256]{1,0:T(8,128)(2,1)S(1)}, u32[]{:S(2)}, u32[]{:S(2)}) collective-permute-start(bf16[64,256]{1,0:T(8,128)(2,1)S(1)} %get-tuple-element.216), channel_id=1, source_target_pairs={{0,4},{4,8},{8,12},{1,5},{5,9},{9,13},{2,6},{6,10},{10,14},{3,7},{... | collective-permute-start | bytes 98312 | tf_op jit(solution)/shard_map/ppermute | solution.py:20
  15.9 9.7 %collective-permute-start.4 = (bf16[512,256]{1,0:T(8,128)(2,1)S(1)}, bf16[512,256]{1,0:T(8,128)(2,1)}, u32[]{:S(2)}, u32[]{:S(2)}) collective-permute-start(bf16[512,256]{1,0:T(8,128)(2,1)S(1)} %fusion.158), channel_id=1, source_target_pairs={{0,4},{4,8},{8,12},{12,0},{1,5},{5,9},{9,13},{13,1},{2,6},{6,10},{... | collective-permute-start | bytes 786440 | tf_op jit(solution)/shard_map/ppermute | solution.py:170
  18.0 9.3 %collective-permute-start.2 = (bf16[512,256]{1,0:T(8,128)(2,1)S(1)}, bf16[512,256]{1,0:T(8,128)(2,1)S(1)}, u32[]{:S(2)}, u32[]{:S(2)}) collective-permute-start(bf16[512,256]{1,0:T(8,128)(2,1)S(1)} %fusion.158), channel_id=1, source_target_pairs={{0,2},{1,3},{2,0},{3,1},{4,6},{5,7},{6,4},{7,5},{8,10},{9,11},{10,... | collective-permute-start | bytes 786440 | tf_op jit(solution)/shard_map/ppermute | solution.py:86
  19.5 15.8 %copy-start.45 = (bf16[1024]{0:T(1024)(128)(2,1)S(1)}, bf16[1024]{0:T(1024)(128)(2,1)}, u32[]{:S(2)}) copy-start(bf16[1024]{0:T(1024)(128)(2,1)} %param.36) | copy-start | bytes 6148
  19.5 15.8 %copy-start.47 = (s32[4,4]{1,0:T(4,128)S(1)}, s32[4,4]{1,0:T(4,128)}, u32[]{:S(2)}) copy-start(s32[4,4]{1,0:T(4,128)} %param.33) | copy-start | bytes 196
  25.7 7.1 %collective-permute-start.5 = (bf16[512,256]{1,0:T(8,128)(2,1)}, bf16[512,256]{1,0:T(8,128)(2,1)S(1)}, u32[]{:S(2)}, u32[]{:S(2)}) collective-permute-start(bf16[512,256]{1,0:T(8,128)(2,1)} %collective-permute-done.4), channel_id=1, source_target_pairs={{0,2},{1,3},{2,0},{3,1},{4,6},{5,7},{6,4},{7,5},{8,10},{9,11},{10,... | collective-permute-start | bytes 786440 | tf_op jit(solution)/shard_map/ppermute | solution.py:86
  28.9 13.3 %collective-permute-start.3 = (bf16[512,2,256]{2,0,1:T(8,128)(2,1)}, bf16[512,2,256]{2,0,1:T(8,128)(2,1)S(1)}, u32[]{:S(2)}, u32[]{:S(2)}) collective-permute-start(bf16[512,2,256]{2,0,1:T(8,128)(2,1)} %pad_maximum_fusion.5), channel_id=1, source_target_pairs={{0,1},{1,0},{2,3},{3,2},{4,5},{5,4},{6,7},{7,6},{8,9},{9,8},{10,11... | collective-permute-start | bytes 1572872 | tf_op jit(solution)/shard_map/ppermute | solution.py:86
  35.3 8.7 %collective-permute-start.6 = (bf16[512,2,256]{2,0,1:T(8,128)(2,1)}, bf16[512,2,256]{2,0,1:T(8,128)(2,1)}, u32[]{:S(2)}, u32[]{:S(2)}) collective-permute-start(bf16[512,2,256]{2,0,1:T(8,128)(2,1)} %pad_maximum_fusion.6), channel_id=1, source_target_pairs={{0,1},{1,0},{2,3},{3,2},{4,5},{5,4},{6,7},{7,6},{8,9},{9,8},{10,11... | collective-permute-start | bytes 1572872 | tf_op jit(solution)/shard_map/ppermute | solution.py:86
  39.9 4.1 %copy-start.9 = (bf16[512,1,256]{2,0,1:T(8,128)(2,1)S(1)}, bf16[512,1,256]{2,0,1:T(8,128)(2,1)}, u32[]{:S(2)}) copy-start(bf16[512,1,256]{2,0,1:T(8,128)(2,1)} %copy-done.8) | copy-start | bytes 786436
  39.9 4.1 %copy-start.11 = (bf16[512,1,256]{2,0,1:T(8,128)(2,1)S(1)}, bf16[512,1,256]{2,0,1:T(8,128)(2,1)}, u32[]{:S(2)}) copy-start(bf16[512,1,256]{2,0,1:T(8,128)(2,1)} %copy-done.10) | copy-start | bytes 786436
  42.2 23.9 %collective-permute-start.7 = (bf16[512,256]{1,0:T(8,128)(2,1)}, bf16[512,256]{1,0:T(8,128)(2,1)}, u32[]{:S(2)}, u32[]{:S(2)}) collective-permute-start(bf16[512,256]{1,0:T(8,128)(2,1)} %collective-permute-done.4), channel_id=1, source_target_pairs={{0,4},{4,8},{8,12},{12,0},{1,5},{5,9},{9,13},{13,1},{2,6},{6,10},{... | collective-permute-start | bytes 786440 | tf_op jit(solution)/shard_map/ppermute | solution.py:192
  51.2 3.4 %copy-start.40 = (bf16[1024,512]{1,0:T(8,128)(2,1)S(1)}, bf16[1024,512]{1,0:T(8,128)(2,1)}, u32[]{:S(2)}) copy-start(bf16[1024,512]{1,0:T(8,128)(2,1)} %copy-done.39) | copy-start | bytes 3145732
  59.4 3.4 %copy-start.44 = (bf16[512,256]{0,1:T(8,128)(2,1)S(1)}, bf16[512,256]{0,1:T(8,128)(2,1)}, u32[]{:S(2)}) copy-start(bf16[512,256]{0,1:T(8,128)(2,1)} %get-tuple-element.196) | copy-start | bytes 786436
  62.8 5.1 %copy-start.2 = (bf16[512,2,2,256]{0,3,2,1:T(8,128)(2,1)S(1)}, bf16[512,2,2,256]{0,3,2,1:T(8,128)(2,1)}, u32[]{:S(2)}) copy-start(bf16[512,2,2,256]{0,3,2,1:T(8,128)(2,1)} %copy.31) | copy-start | bytes 3145732
  66.1 9.0 %collective-permute-start.8 = (bf16[512,256]{1,0:T(8,128)(2,1)}, bf16[512,256]{1,0:T(8,128)(2,1)S(1)}, u32[]{:S(2)}, u32[]{:S(2)}) collective-permute-start(bf16[512,256]{1,0:T(8,128)(2,1)} %collective-permute-done.7), channel_id=1, source_target_pairs={{0,2},{1,3},{2,0},{3,1},{4,6},{5,7},{6,4},{7,5},{8,10},{9,11},{10,... | collective-permute-start | bytes 786440 | tf_op jit(solution)/shard_map/ppermute | solution.py:86
  67.5 14.1 %collective-permute-start.10 = (bf16[512,256]{1,0:T(8,128)(2,1)}, bf16[512,256]{1,0:T(8,128)(2,1)}, u32[]{:S(2)}, u32[]{:S(2)}) collective-permute-start(bf16[512,256]{1,0:T(8,128)(2,1)} %collective-permute-done.7), channel_id=1, source_target_pairs={{0,4},{4,8},{8,12},{12,0},{1,5},{5,9},{9,13},{13,1},{2,6},{6,10},{... | collective-permute-start | bytes 786440 | tf_op jit(solution)/shard_map/ppermute | solution.py:192
  76.1 2.0 %collective-permute-start.9 = (bf16[512,2,256]{2,0,1:T(8,128)(2,1)S(1)}, bf16[512,2,256]{2,0,1:T(8,128)(2,1)S(1)}, u32[]{:S(2)}, u32[]{:S(2)}) collective-permute-start(bf16[512,2,256]{2,0,1:T(8,128)(2,1)S(1)} %pad_maximum_fusion.7), channel_id=1, source_target_pairs={{0,1},{1,0},{2,3},{3,2},{4,5},{5,4},{6,7},{7,6},{8,9},{9,8},{10,11... | collective-permute-start | bytes 1572872 | tf_op jit(solution)/shard_map/ppermute | solution.py:86
  81.5 3.2 %copy-start.3 = (bf16[512,2,2,256]{0,3,2,1:T(8,128)(2,1)S(1)}, bf16[512,2,2,256]{0,3,2,1:T(8,128)(2,1)}, u32[]{:S(2)}) copy-start(bf16[512,2,2,256]{0,3,2,1:T(8,128)(2,1)} %copy.33) | copy-start | bytes 3145732
  81.5 3.2 %copy-start.42 = (bf16[1024,512]{1,0:T(8,128)(2,1)S(1)}, bf16[1024,512]{1,0:T(8,128)(2,1)}, u32[]{:S(2)}) copy-start(bf16[1024,512]{1,0:T(8,128)(2,1)} %copy-done.39) | copy-start | bytes 3145732
  85.7 9.0 %collective-permute-start.11 = (bf16[512,256]{1,0:T(8,128)(2,1)}, bf16[512,256]{1,0:T(8,128)(2,1)S(1)}, u32[]{:S(2)}, u32[]{:S(2)}) collective-permute-start(bf16[512,256]{1,0:T(8,128)(2,1)} %collective-permute-done.10), channel_id=1, source_target_pairs={{0,2},{1,3},{2,0},{3,1},{4,6},{5,7},{6,4},{7,5},{8,10},{9,11},{10,... | collective-permute-start | bytes 786440 | tf_op jit(solution)/shard_map/ppermute | solution.py:86
  95.8 2.0 %collective-permute-start.12 = (bf16[512,2,256]{2,0,1:T(8,128)(2,1)S(1)}, bf16[512,2,256]{2,0,1:T(8,128)(2,1)S(1)}, u32[]{:S(2)}, u32[]{:S(2)}) collective-permute-start(bf16[512,2,256]{2,0,1:T(8,128)(2,1)S(1)} %pad_maximum_fusion.8), channel_id=1, source_target_pairs={{0,1},{1,0},{2,3},{3,2},{4,5},{5,4},{6,7},{7,6},{8,9},{9,8},{10,11... | collective-permute-start | bytes 1572872 | tf_op jit(solution)/shard_map/ppermute | solution.py:86
  101.2 3.2 %copy-start.43 = (bf16[1024,512]{1,0:T(8,128)(2,1)S(1)}, bf16[1024,512]{1,0:T(8,128)(2,1)}, u32[]{:S(2)}) copy-start(bf16[1024,512]{1,0:T(8,128)(2,1)} %copy-done.39) | copy-start | bytes 3145732
  108.6 2.3 %collective-permute-start.13 = (bf16[128,2,256]{2,0,1:T(8,128)(2,1)S(1)}, bf16[128,2,256]{2,0,1:T(8,128)(2,1)S(1)}, u32[]{:S(2)}, u32[]{:S(2)}) collective-permute-start(bf16[128,2,256]{2,0,1:T(8,128)(2,1)S(1)} %fusion.184), channel_id=1, source_target_pairs={{0,1},{1,0},{2,3},{3,2},{4,5},{5,4},{6,7},{7,6},{8,9},{9,8},{10,11... | collective-permute-start | bytes 393224 | tf_op jit(solution)/shard_map/ppermute | solution.py:72
  109.5 3.4 %collective-permute-start.31 = (bf16[128,2,256]{2,0,1:T(8,128)(2,1)S(1)}, bf16[128,2,256]{2,0,1:T(8,128)(2,1)S(1)}, u32[]{:S(2)}, u32[]{:S(2)}) collective-permute-start(bf16[128,2,256]{2,0,1:T(8,128)(2,1)S(1)} %fusion.187), channel_id=1, source_target_pairs={{0,1},{1,0},{2,3},{3,2},{4,5},{5,4},{6,7},{7,6},{8,9},{9,8},{10,11... | collective-permute-start | bytes 393224 | tf_op jit(solution)/shard_map/ppermute | solution.py:72
  110.0 4.4 %collective-permute-start.25 = (bf16[128,2,256]{2,0,1:T(8,128)(2,1)S(1)}, bf16[128,2,256]{2,0,1:T(8,128)(2,1)S(1)}, u32[]{:S(2)}, u32[]{:S(2)}) collective-permute-start(bf16[128,2,256]{2,0,1:T(8,128)(2,1)S(1)} %fusion.186), channel_id=1, source_target_pairs={{0,1},{1,0},{2,3},{3,2},{4,5},{5,4},{6,7},{7,6},{8,9},{9,8},{10,11... | collective-permute-start | bytes 393224 | tf_op jit(solution)/shard_map/ppermute | solution.py:72
  110.9 12.5 %copy-start.46 = (bf16[1024]{0:T(1024)(128)(2,1)S(1)}, bf16[1024]{0:T(1024)(128)(2,1)}, u32[]{:S(2)}) copy-start(bf16[1024]{0:T(1024)(128)(2,1)} %param.41) | copy-start | bytes 6148
  110.9 5.6 %collective-permute-start.19 = (bf16[128,2,256]{2,0,1:T(8,128)(2,1)S(1)}, bf16[128,2,256]{2,0,1:T(8,128)(2,1)S(1)}, u32[]{:S(2)}, u32[]{:S(2)}) collective-permute-start(bf16[128,2,256]{2,0,1:T(8,128)(2,1)S(1)} %fusion.185), channel_id=1, source_target_pairs={{0,1},{1,0},{2,3},{3,2},{4,5},{5,4},{6,7},{7,6},{8,9},{9,8},{10,11... | collective-permute-start | bytes 393224 | tf_op jit(solution)/shard_map/ppermute | solution.py:72
  111.6 6.2 %collective-permute-start.14 = (bf16[128,256]{1,0:T(8,128)(2,1)}, bf16[128,256]{1,0:T(8,128)(2,1)S(1)}, u32[]{:S(2)}, u32[]{:S(2)}) collective-permute-start(bf16[128,256]{1,0:T(8,128)(2,1)} %fusion.208), channel_id=1, source_target_pairs={{0,2},{1,3},{2,0},{3,1},{4,6},{5,7},{6,4},{7,5},{8,10},{9,11},{10,... | collective-permute-start | bytes 196616 | tf_op jit(solution)/shard_map/ppermute | solution.py:72
  113.7 4.9 %collective-permute-start.32 = (bf16[128,256]{1,0:T(8,128)(2,1)}, bf16[128,256]{1,0:T(8,128)(2,1)S(1)}, u32[]{:S(2)}, u32[]{:S(2)}) collective-permute-start(bf16[128,256]{1,0:T(8,128)(2,1)} %fusion.214), channel_id=1, source_target_pairs={{0,2},{1,3},{2,0},{3,1},{4,6},{5,7},{6,4},{7,5},{8,10},{9,11},{10,... | collective-permute-start | bytes 196616 | tf_op jit(solution)/shard_map/ppermute | solution.py:72
  115.1 4.8 %collective-permute-start.26 = (bf16[128,256]{1,0:T(8,128)(2,1)}, bf16[128,256]{1,0:T(8,128)(2,1)}, u32[]{:S(2)}, u32[]{:S(2)}) collective-permute-start(bf16[128,256]{1,0:T(8,128)(2,1)} %fusion.212), channel_id=1, source_target_pairs={{0,2},{1,3},{2,0},{3,1},{4,6},{5,7},{6,4},{7,5},{8,10},{9,11},{10,... | collective-permute-start | bytes 196616 | tf_op jit(solution)/shard_map/ppermute | solution.py:72
  117.2 4.3 %collective-permute-start.20 = (bf16[128,256]{1,0:T(8,128)(2,1)S(1)}, bf16[128,256]{1,0:T(8,128)(2,1)S(1)}, u32[]{:S(2)}, u32[]{:S(2)}) collective-permute-start(bf16[128,256]{1,0:T(8,128)(2,1)S(1)} %fusion.210), channel_id=1, source_target_pairs={{0,2},{1,3},{2,0},{3,1},{4,6},{5,7},{6,4},{7,5},{8,10},{9,11},{10,... | collective-permute-start | bytes 196616 | tf_op jit(solution)/shard_map/ppermute | solution.py:72
  122.5 7.6 %copy-start.29 = (bf16[128,256]{1,0:T(8,128)(2,1)}, bf16[128,256]{1,0:T(8,128)(2,1)S(1)}, u32[]{:S(2)}) copy-start(bf16[128,256]{1,0:T(8,128)(2,1)S(1)} %get-tuple-element.202) | copy-start | bytes 196612
  122.5 7.6 %copy-start.31 = (bf16[128,256]{1,0:T(8,128)(2,1)}, bf16[128,256]{1,0:T(8,128)(2,1)S(1)}, u32[]{:S(2)}) copy-start(bf16[128,256]{1,0:T(8,128)(2,1)S(1)} %get-tuple-element.205) | copy-start | bytes 196612
  122.5 7.6 %copy-start.33 = (bf16[128,256]{1,0:T(8,128)(2,1)}, bf16[128,256]{1,0:T(8,128)(2,1)S(1)}, u32[]{:S(2)}) copy-start(bf16[128,256]{1,0:T(8,128)(2,1)S(1)} %get-tuple-element.204) | copy-start | bytes 196612
  122.5 7.6 %copy-start.35 = (bf16[128,256]{1,0:T(8,128)(2,1)}, bf16[128,256]{1,0:T(8,128)(2,1)S(1)}, u32[]{:S(2)}) copy-start(bf16[128,256]{1,0:T(8,128)(2,1)S(1)} %get-tuple-element.203) | copy-start | bytes 196612
  122.6 5.0 %collective-permute-start.15 = (bf16[128,256]{1,0:T(8,128)(2,1)S(1)}, bf16[128,256]{1,0:T(8,128)(2,1)S(1)}, u32[]{:S(2)}, u32[]{:S(2)}) collective-permute-start(bf16[128,256]{1,0:T(8,128)(2,1)S(1)} %get-tuple-element.202), channel_id=1, source_target_pairs={{0,2},{1,3},{2,0},{3,1},{4,6},{5,7},{6,4},{7,5},{8,10},{9,11},{10,... | collective-permute-start | bytes 196616 | tf_op jit(solution)/shard_map/ppermute | solution.py:86
  123.4 5.2 %collective-permute-start.21 = (bf16[128,256]{1,0:T(8,128)(2,1)S(1)}, bf16[128,256]{1,0:T(8,128)(2,1)S(1)}, u32[]{:S(2)}, u32[]{:S(2)}) collective-permute-start(bf16[128,256]{1,0:T(8,128)(2,1)S(1)} %get-tuple-element.205), channel_id=1, source_target_pairs={{0,2},{1,3},{2,0},{3,1},{4,6},{5,7},{6,4},{7,5},{8,10},{9,11},{10,... | collective-permute-start | bytes 196616 | tf_op jit(solution)/shard_map/ppermute | solution.py:86
  124.7 4.6 %collective-permute-start.27 = (bf16[128,256]{1,0:T(8,128)(2,1)S(1)}, bf16[128,256]{1,0:T(8,128)(2,1)S(1)}, u32[]{:S(2)}, u32[]{:S(2)}) collective-permute-start(bf16[128,256]{1,0:T(8,128)(2,1)S(1)} %get-tuple-element.204), channel_id=1, source_target_pairs={{0,2},{1,3},{2,0},{3,1},{4,6},{5,7},{6,4},{7,5},{8,10},{9,11},{10,... | collective-permute-start | bytes 196616 | tf_op jit(solution)/shard_map/ppermute | solution.py:86
  125.4 4.6 %collective-permute-start.33 = (bf16[128,256]{1,0:T(8,128)(2,1)S(1)}, bf16[128,256]{1,0:T(8,128)(2,1)S(1)}, u32[]{:S(2)}, u32[]{:S(2)}) collective-permute-start(bf16[128,256]{1,0:T(8,128)(2,1)S(1)} %get-tuple-element.203), channel_id=1, source_target_pairs={{0,2},{1,3},{2,0},{3,1},{4,6},{5,7},{6,4},{7,5},{8,10},{9,11},{10,... | collective-permute-start | bytes 196616 | tf_op jit(solution)/shard_map/ppermute | solution.py:86
  127.6 2.5 %collective-permute-start.16 = (bf16[128,2,256]{2,0,1:T(8,128)(2,1)S(1)}, bf16[128,2,256]{2,0,1:T(8,128)(2,1)S(1)}, u32[]{:S(2)}, u32[]{:S(2)}) collective-permute-start(bf16[128,2,256]{2,0,1:T(8,128)(2,1)S(1)} %pad_maximum_fusion.10), channel_id=1, source_target_pairs={{0,1},{1,0},{2,3},{3,2},{4,5},{5,4},{6,7},{7,6},{8,9},{9,8},{10,11... | collective-permute-start | bytes 393224 | tf_op jit(solution)/shard_map/ppermute | solution.py:86
  128.6 1.7 collective-permute-start.22
  129.3 1.8 collective-permute-start.28
  130.0 2.6 %collective-permute-start.34 = (bf16[128,2,256]{2,0,1:T(8,128)(2,1)S(1)}, bf16[128,2,256]{2,0,1:T(8,128)(2,1)S(1)}, u32[]{:S(2)}, u32[]{:S(2)}) collective-permute-start(bf16[128,2,256]{2,0,1:T(8,128)(2,1)S(1)} %pad_maximum_fusion.13), channel_id=1, source_target_pairs={{0,1},{1,0},{2,3},{3,2},{4,5},{5,4},{6,7},{7,6},{8,9},{9,8},{10,11... | collective-permute-start | bytes 393224 | tf_op jit(solution)/shard_map/ppermute | solution.py:86
  135.3 4.8 %copy-start.15 = (f32[128,2,2,256]{3,0,1,2:T(8,128)S(1)}, f32[128,2,2,256]{3,0,1,2:T(8,128)}, u32[]{:S(2)}) copy-start(f32[128,2,2,256]{3,0,1,2:T(8,128)} %maximum_convert_fusion.3) | copy-start | bytes 1572868
  135.5 6.3 %copy-start.20 = (bf16[128,2,1,256]{3,0,1,2:T(8,128)(2,1)S(1)}, bf16[128,2,1,256]{3,0,1,2:T(8,128)(2,1)}, u32[]{:S(2)}) copy-start(bf16[128,2,1,256]{3,0,1,2:T(8,128)(2,1)} %copy-done.19) | copy-start | bytes 393220
  135.5 6.3 %copy-start.22 = (bf16[128,2,1,256]{3,0,1,2:T(8,128)(2,1)S(1)}, bf16[128,2,1,256]{3,0,1,2:T(8,128)(2,1)}, u32[]{:S(2)}) copy-start(bf16[128,2,1,256]{3,0,1,2:T(8,128)(2,1)} %copy-done.21) | copy-start | bytes 393220
  136.1 7.1 %copy-start.48 = (f32[128]{0:T(128)S(1)}, f32[128]{0:T(128)}, u32[]{:S(2)}) copy-start(f32[128]{0:T(128)} %add_rsqrt_fusion.7) | copy-start | bytes 1540
  138.2 5.0 %copy-start.23 = (f32[128,2,2,256]{0,3,2,1:T(8,128)S(1)}, f32[128,2,2,256]{0,3,2,1:T(8,128)}, u32[]{:S(2)}) copy-start(f32[128,2,2,256]{0,3,2,1:T(8,128)} %copy.39) | copy-start | bytes 1572868
  145.7 4.3 %copy-start.26 = (bf16[128,1024]{0,1:T(8,128)(2,1)S(1)}, bf16[128,1024]{0,1:T(8,128)(2,1)}, u32[]{:S(2)}) copy-start(bf16[128,1024]{0,1:T(8,128)(2,1)} %get-tuple-element.261) | copy-start | bytes 786436
  150.1 3.6 %copy-start.25 = (bf16[128,1024]{0,1:T(8,128)(2,1)S(1)}, bf16[128,1024]{0,1:T(8,128)(2,1)}, u32[]{:S(2)}) copy-start(bf16[128,1024]{0,1:T(8,128)(2,1)} %get-tuple-element.260) | copy-start | bytes 786436
  160.3 7.7 %collective-permute-start.35 = (bf16[128,2,256]{2,0,1:T(8,128)(2,1)}, bf16[128,2,256]{2,0,1:T(8,128)(2,1)}, u32[]{:S(2)}, u32[]{:S(2)}) collective-permute-start(bf16[128,2,256]{2,0,1:T(8,128)(2,1)} %bitcast.538), channel_id=1, source_target_pairs={{0,1},{1,0},{2,3},{3,2},{4,5},{5,4},{6,7},{7,6},{8,9},{9,8},{10,11... | collective-permute-start | bytes 393224 | tf_op jit(solution)/shard_map/ppermute | solution.py:72
  163.3 6.9 %collective-permute-start.29 = (bf16[128,2,256]{2,0,1:T(8,128)(2,1)}, bf16[128,2,256]{2,0,1:T(8,128)(2,1)}, u32[]{:S(2)}, u32[]{:S(2)}) collective-permute-start(bf16[128,2,256]{2,0,1:T(8,128)(2,1)} %bitcast.539), channel_id=1, source_target_pairs={{0,1},{1,0},{2,3},{3,2},{4,5},{5,4},{6,7},{7,6},{8,9},{9,8},{10,11... | collective-permute-start | bytes 393224 | tf_op jit(solution)/shard_map/ppermute | solution.py:72
  164.2 8.0 %collective-permute-start.23 = (bf16[128,2,256]{2,0,1:T(8,128)(2,1)}, bf16[128,2,256]{2,0,1:T(8,128)(2,1)}, u32[]{:S(2)}, u32[]{:S(2)}) collective-permute-start(bf16[128,2,256]{2,0,1:T(8,128)(2,1)} %bitcast.540), channel_id=1, source_target_pairs={{0,1},{1,0},{2,3},{3,2},{4,5},{5,4},{6,7},{7,6},{8,9},{9,8},{10,11... | collective-permute-start | bytes 393224 | tf_op jit(solution)/shard_map/ppermute | solution.py:72
  167.5 7.8 %copy-start.36 = (bf16[128,256]{1,0:T(8,128)(2,1)S(1)}, bf16[128,256]{1,0:T(8,128)(2,1)}, u32[]{:S(2)}) copy-start(bf16[128,256]{1,0:T(8,128)(2,1)} %copy-done.35) | copy-start | bytes 196612
  167.7 7.8 %copy-start.34 = (bf16[128,256]{1,0:T(8,128)(2,1)S(1)}, bf16[128,256]{1,0:T(8,128)(2,1)}, u32[]{:S(2)}) copy-start(bf16[128,256]{1,0:T(8,128)(2,1)} %copy-done.33) | copy-start | bytes 196612
  167.7 10.3 %copy-start.32 = (bf16[128,256]{1,0:T(8,128)(2,1)S(1)}, bf16[128,256]{1,0:T(8,128)(2,1)}, u32[]{:S(2)}) copy-start(bf16[128,256]{1,0:T(8,128)(2,1)} %copy-done.31) | copy-start | bytes 196612
  167.8 10.9 %copy-start.30 = (bf16[128,256]{1,0:T(8,128)(2,1)S(1)}, bf16[128,256]{1,0:T(8,128)(2,1)}, u32[]{:S(2)}) copy-start(bf16[128,256]{1,0:T(8,128)(2,1)} %copy-done.29) | copy-start | bytes 196612
  167.9 6.4 %collective-permute-start.17 = (bf16[128,2,256]{2,0,1:T(8,128)(2,1)S(1)}, bf16[128,2,256]{2,0,1:T(8,128)(2,1)S(1)}, u32[]{:S(2)}, u32[]{:S(2)}) collective-permute-start(bf16[128,2,256]{2,0,1:T(8,128)(2,1)S(1)} %bitcast.626), channel_id=1, source_target_pairs={{0,1},{1,0},{2,3},{3,2},{4,5},{5,4},{6,7},{7,6},{8,9},{9,8},{10,11... | collective-permute-start | bytes 393224 | tf_op jit(solution)/shard_map/ppermute | solution.py:72
  169.0 6.4 %collective-permute-start.36 = (bf16[128,256]{1,0:T(8,128)(2,1)S(1)}, bf16[128,256]{1,0:T(8,128)(2,1)S(1)}, u32[]{:S(2)}, u32[]{:S(2)}) collective-permute-start(bf16[128,256]{1,0:T(8,128)(2,1)S(1)} %fusion.215), channel_id=1, source_target_pairs={{0,2},{1,3},{2,0},{3,1},{4,6},{5,7},{6,4},{7,5},{8,10},{9,11},{10,... | collective-permute-start | bytes 196616 | tf_op jit(solution)/shard_map/ppermute | solution.py:72
  171.1 4.3 %collective-permute-start.30 = (bf16[128,256]{1,0:T(8,128)(2,1)S(1)}, bf16[128,256]{1,0:T(8,128)(2,1)S(1)}, u32[]{:S(2)}, u32[]{:S(2)}) collective-permute-start(bf16[128,256]{1,0:T(8,128)(2,1)S(1)} %fusion.213), channel_id=1, source_target_pairs={{0,2},{1,3},{2,0},{3,1},{4,6},{5,7},{6,4},{7,5},{8,10},{9,11},{10,... | collective-permute-start | bytes 196616 | tf_op jit(solution)/shard_map/ppermute | solution.py:72
  173.1 4.9 %collective-permute-start.24 = (bf16[128,256]{1,0:T(8,128)(2,1)S(1)}, bf16[128,256]{1,0:T(8,128)(2,1)S(1)}, u32[]{:S(2)}, u32[]{:S(2)}) collective-permute-start(bf16[128,256]{1,0:T(8,128)(2,1)S(1)} %fusion.211), channel_id=1, source_target_pairs={{0,2},{1,3},{2,0},{3,1},{4,6},{5,7},{6,4},{7,5},{8,10},{9,11},{10,... | collective-permute-start | bytes 196616 | tf_op jit(solution)/shard_map/ppermute | solution.py:72
  174.3 4.4 %collective-permute-start.18 = (bf16[128,256]{1,0:T(8,128)(2,1)S(1)}, bf16[128,256]{1,0:T(8,128)(2,1)S(1)}, u32[]{:S(2)}, u32[]{:S(2)}) collective-permute-start(bf16[128,256]{1,0:T(8,128)(2,1)S(1)} %fusion.209), channel_id=1, source_target_pairs={{0,2},{1,3},{2,0},{3,1},{4,6},{5,7},{6,4},{7,5},{8,10},{9,11},{10,... | collective-permute-start | bytes 196616 | tf_op jit(solution)/shard_map/ppermute | solution.py:72
  (23 other events, 31.6 us)

commit v9 on v5

--- a/solution.py
+++ b/solution.py
@@ -88,6 +88,17 @@
         high = jnp.where(mine == 0, got, current)
         current = jnp.stack([low, high], axis=current.ndim - 1)
     return current.reshape(rows, head_total * width)
+
+
+def gather_levels(current, head_id, head_total, level_list):
+    for level in level_list:
+        bit = 1 << level
+        mine = (head_id >> level) & 1
+        got = lax.ppermute(current, "heads", [(i, i ^ bit) for i in range(head_total)])
+        low = jnp.where(mine == 0, current, got)
+        high = jnp.where(mine == 0, got, current)
+        current = jnp.stack([low, high], axis=current.ndim - 1)
+    return current
 
 
 def absorb_block(state, query_heads, block, linked, head_count, brick_rows, local_width):
@@ -155,36 +166,59 @@
     stream = (voxel_feats.astype(jnp.float32) + conv_out).astype(jnp.bfloat16)
     head_total = lax.axis_size("heads")
     head_id = lax.axis_index("heads")
-    stream_full = gather_heads(stream, head_id, head_total)
-    normed = layer_norm(stream_full, gain_one).astype(jnp.bfloat16)
-    queries = jnp.dot(normed, query_weight, preferred_element_type=jnp.float32).astype(jnp.bfloat16)
     head_count = local_width // HEAD_DIM
-    keys_all = jnp.dot(normed, key_weight, preferred_element_type=jnp.float32).astype(jnp.bfloat16)
-    values_all = jnp.dot(normed, value_weight, preferred_element_type=jnp.float32).astype(
-        jnp.bfloat16
-    )
-    pair_local = jnp.concatenate([keys_all, values_all], axis=1)
     brick_dev = lax.axis_index("bricks")
     dev_total = lax.axis_size("bricks")
-    key_total = pattern.shape[1]
-    query_heads = queries.reshape(local_bricks, brick_rows, head_count, HEAD_DIM)
+    ring = [(i, (i + 1) % dev_total) for i in range(dev_total)]
+    pair_weight = jnp.concatenate([key_weight, value_weight], axis=1)
     linked_rows = lax.dynamic_slice_in_dim(pattern, first_brick, local_bricks, 0)
     state = (
         jnp.full((local_bricks, head_count, brick_rows), -1e30, jnp.float32),
         jnp.zeros((local_bricks, head_count, brick_rows), jnp.float32),
         jnp.zeros((local_bricks, brick_rows, head_count, HEAD_DIM), jnp.float32),
     )
-    ring = [(i, (i + 1) % dev_total) for i in range(dev_total)]
-    block = pair_local
-    for step in range(dev_total):
-        if step + 1 < dev_total:
-            arriving = lax.ppermute(block, "bricks", ring)
-        source = (brick_dev - step) % dev_total
-        key_ids = source * local_bricks + jnp.arange(local_bricks, dtype=jnp.int32)
-        linked = jnp.take(linked_rows, key_ids, axis=1) > 0
-        state = absorb_block(state, query_heads, block, linked, head_count, brick_rows, local_width)
-        if step + 1 < dev_total:
-            state, block = lax.optimization_barrier((state, arriving))
+    levels = level_count(head_total)
+    cross_levels = list(reversed(range(1, levels)))
+    chip_levels = list(range(min(levels, 1)))
+    ringed = {0: stream}
+    crossed = {}
+    gathered = {}
+    query_heads = None
+    for slot in range(dev_total + 2):
+        made = []
+        if 1 <= slot + 1 < dev_total:
+            ringed[slot + 1] = lax.ppermute(ringed[slot], "bricks", ring)
+            made.append((ringed, slot + 1))
+        if slot < dev_total:
+            crossed[slot] = gather_levels(ringed[slot], head_id, head_total, cross_levels)
+            made.append((crossed, slot))
+        if 0 <= slot - 1 < dev_total:
+            gathered[slot - 1] = gather_levels(
+                crossed[slot - 1], head_id, head_total, chip_levels
+            ).reshape(row_count, head_total * local_width)
+            made.append((gathered, slot - 1))
+        step = slot - 2
+        if 0 <= step < dev_total:
+            normed_now = layer_norm(gathered[step], gain_one).astype(jnp.bfloat16)
+            if step == 0:
+                queries = jnp.dot(
+                    normed_now, query_weight, preferred_element_type=jnp.float32
+                ).astype(jnp.bfloat16)
+                query_heads = queries.reshape(local_bricks, brick_rows, head_count, HEAD_DIM)
+            pair_block = jnp.dot(
+                normed_now, pair_weight, preferred_element_type=jnp.float32
+            ).astype(jnp.bfloat16)
+            source = (brick_dev - step) % dev_total
+            key_ids = source * local_bricks + jnp.arange(local_bricks, dtype=jnp.int32)
+            linked = jnp.take(linked_rows, key_ids, axis=1) > 0
+            state = absorb_block(
+                state, query_heads, pair_block, linked, head_count, brick_rows, local_width
+            )
+        if slot < dev_total + 1:
+            packed = lax.optimization_barrier((state, [table[key] for table, key in made]))
+            state = packed[0]
+            for (table, key), value in zip(made, packed[1]):
+                table[key] = value
     row_max, row_mass, weighted = state
     attended = (weighted / jnp.transpose(row_mass, (0, 2, 1))[:, :, :, None]).astype(jnp.bfloat16)
     attended = attended.reshape(row_count, local_width)

time: 129 us -> 121 us (0.938)
  waiting for transfers between devices: 60 us -> 40.5 us
  starting transfers between devices: 18.8 us -> 22.7 us
  matrix products: 17.5 us -> 20.4 us
  local copies, waits for them, and re-layouts: 12.3 us -> 15.2 us
  other arithmetic: 15 us -> 17.5 us
    ppermute x3 -> x11, waiting for transfers between devices: 36.8 us -> 22.1 us  [the longest x8 11.5 us: gather_levels(): lax.ppermute(current, 'heads', [(i, i ^ bit) for i in range(head_total)])]
    ppermute x3 -> x11, starting transfers between devices: 2.09 us -> 8.04 us  [the longest x8 5.87 us: gather_levels(): lax.ppermute(current, 'heads', [(i, i ^ bit) for i in range(head_total)])]
    ppermute x6 -> x4, waiting for transfers between devices: 12.7 us -> 6.78 us  [gather_heads(): lax.ppermute(current, 'heads', [(i, i ^ bit) for i in range(head_total)])]
    another operation x2 -> x16, other arithmetic: 0.02 us -> 4.01 us  [gather_levels(): current = jnp.stack([low, high], axis=current.ndim - 1)]
    dot_general x3 -> x5, matrix products: 1.45 us -> 4.38 us  [the longest x4 3.74 us: shards(): jnp.dot(normed_now, pair_weight, preferred_element_type=jnp.float32)]
    another operation x8 -> x5, other arithmetic: 2.19 us -> 0.19 us  [gather_heads(): current = jnp.stack([low, high], axis=current.ndim - 1)]
    ppermute x6 -> x4, starting transfers between devices: 4.23 us -> 2.23 us  [gather_heads(): lax.ppermute(current, 'heads', [(i, i ^ bit) for i in range(head_total)])]
    concatenate x0 -> x1, local copies, waits for them, and re-layouts: none -> 1.91 us  [shards(): pair_weight = jnp.concatenate([key_weight, value_weight], axis=1)]
  transfers between devices with their start and end apart: 19 -> 25, of which waited for: 13 -> 16; matrix products, arithmetic and copies ran while one was open for 19% -> 25% of each run, Pallas kernels for 0% -> 0%
where the time goes in v9:
time: 121 us
  waiting for transfers between devices  40.5 us (33%)
  starting transfers between devices  22.7 us (19%)
  matrix products  20.4 us (17%)
  other arithmetic  17.5 us (14%)
  local copies, waits for them, and re-layouts  15.2 us (13%)
  between operations  4.46 us (4%)
    ppermute x8, waiting for transfers between devices, scatter_heads(): lax.ppermute(give.astype(jnp.bfloat16), 'heads', [(i, i ^ bit) for i in r...  11.6 us
    ppermute x8, waiting for transfers between devices, gather_levels(): lax.ppermute(current, 'heads', [(i, i ^ bit) for i in range(head_total)])  11.5 us
    ppermute x3, waiting for transfers between devices, shards(): ringed[slot + 1] = lax.ppermute(ringed[slot], 'bricks', ring)  10.6 us
    dot_general x2, matrix products, shards(): lowered = jnp.dot(hidden, down_weight, preferred_element_type=jnp.float32)  8.37 us
    ppermute x4, waiting for transfers between devices, gather_heads(): lax.ppermute(current, 'heads', [(i, i ^ bit) for i in range(head_total)])  6.78 us
    ppermute x8, starting transfers between devices, gather_levels(): lax.ppermute(current, 'heads', [(i, i ^ bit) for i in range(head_total)])  5.87 us
    ppermute x8, starting transfers between devices, scatter_heads(): lax.ppermute(give.astype(jnp.bfloat16), 'heads', [(i, i ^ bit) for i in r...  5.61 us
    ppermute x1, starting transfers between devices, extended_2(): before = lax.ppermute(last, axis, up)  5.56 us
  transfers between devices with their start and end apart: 25, of which 16 were waited for; matrix products, arithmetic and copies ran while one was open for 25% of the time, Pallas kernels for 0%

profile of v9, /device:TPU:0, one launch (start us, length us, event | category | flops | bytes accessed | tf_op | source)
XLA Modules:
  0.0 120.7 jit_solution(15777303262157229044)
XLA Ops:
  0.0 0.9 fusion.196
  0.9 1.3 %collective-permute-start.1 = (bf16[64,256]{1,0:T(8,128)(2,1)S(1)}, bf16[64,256]{1,0:T(8,128)(2,1)S(1)}, u32[]{:S(2)}, u32[]{:S(2)}) collective-permute-start(bf16[64,256]{1,0:T(8,128)(2,1)S(1)} %get-tuple-element.239), channel_id=1, source_target_pairs={{4,0},{8,4},{12,8},{5,1},{9,5},{13,9},{6,2},{10,6},{14,10},{7,3},{... | collective-permute-start | bytes 98312 | tf_op jit(solution)/shard_map/ppermute | solution.py:21
  2.2 5.6 %collective-permute-start = (bf16[64,256]{1,0:T(8,128)(2,1)S(1)}, bf16[64,256]{1,0:T(8,128)(2,1)S(1)}, u32[]{:S(2)}, u32[]{:S(2)}) collective-permute-start(bf16[64,256]{1,0:T(8,128)(2,1)S(1)} %get-tuple-element.238), channel_id=1, source_target_pairs={{0,4},{4,8},{8,12},{1,5},{5,9},{9,13},{2,6},{6,10},{10,14},{3,7},{... | collective-permute-start | bytes 98312 | tf_op jit(solution)/shard_map/ppermute | solution.py:20
  7.8 1.0 fusion.197
  8.8 0.9 fusion.198
  9.7 1.1 copy.29
  10.8 1.3 %fusion.200 = (s32[1]{0:T(128)}, s32[1]{0:T(128)}) fusion(s32[4]{0:T(128)} %param.32, s32[]{:T(128)} %bitcast.2, s32[]{:T(128)} %bitcast.6), kind=kLoop, calls=%fused_computation.320 | loop fusion | bytes 24 | tf_op jit(solution)/shard_map/jit(_take)/gather | solution.py:157
  13.5 0.7 convert_element_type.225
  14.5 1.7 %fusion.113 = f32[1,8,8,8,256]{4,3,2,1,0:T(8,128)S(1)} fusion(f32[1,10,10,10,256]{4,3,2,1,0:T(8,128)S(1)} %select_maximum_fusion, f32[1,1,8,8,256]{4,3,2,1,0:T(8,128)S(1)} %multiply_bitcast_fusion, f32[1,8,8,8,256]{4,3,2,1,0:T(8,128)S(1)} %bitcast.482, f32[1,1,8,8,256]{4,3,2,1,0:T(8,128)S(1)} %multiply_bitcast_fusion.1, f32[256]{0:T(256)S(1)} %bitcast.535, ...), kind=kLoop, calls=%fused_computation.130 | loop fusion | flops 7208960 | bytes 13790208 | tf_op jit(solution)/shard_map/add | solution.py:51
  16.5 2.0 %collective-permute-start.3 = (bf16[512,256]{0,1:T(8,128)(2,1)S(1)}, bf16[512,256]{0,1:T(8,128)(2,1)S(1)}, u32[]{:S(2)}, u32[]{:S(2)}) collective-permute-start(bf16[512,256]{0,1:T(8,128)(2,1)S(1)} %add_convert_fusion), channel_id=1, source_target_pairs={{0,2},{1,3},{2,0},{3,1},{4,6},{5,7},{6,4},{7,5},{8,10},{9,11},{10,... | collective-permute-start | bytes 786440 | tf_op jit(solution)/shard_map/ppermute | solution.py:97
  18.5 1.6 %collective-permute-start.2 = (bf16[512,256]{0,1:T(8,128)(2,1)S(1)}, bf16[512,256]{0,1:T(8,128)(2,1)S(1)}, u32[]{:S(2)}, u32[]{:S(2)}) collective-permute-start(bf16[512,256]{0,1:T(8,128)(2,1)S(1)} %add_convert_fusion), channel_id=1, source_target_pairs={{0,4},{4,8},{8,12},{12,0},{1,5},{5,9},{9,13},{13,1},{2,6},{6,10},{... | collective-permute-start | bytes 786440 | tf_op jit(solution)/shard_map/ppermute | solution.py:190
  20.1 4.3 %collective-permute-done.3 = bf16[512,256]{0,1:T(8,128)(2,1)S(1)} collective-permute-done((bf16[512,256]{0,1:T(8,128)(2,1)S(1)}, bf16[512,256]{0,1:T(8,128)(2,1)S(1)}, u32[]{:S(2)}, u32[]{:S(2)}) %collective-permute-start.3) | collective-permute-done | bytes 262176 | tf_op jit(solution)/shard_map/ppermute | solution.py:97
  24.4 0.9 pad_maximum_fusion.6
  25.2 2.3 %collective-permute-done.2 = bf16[512,256]{0,1:T(8,128)(2,1)S(1)} collective-permute-done((bf16[512,256]{0,1:T(8,128)(2,1)S(1)}, bf16[512,256]{0,1:T(8,128)(2,1)S(1)}, u32[]{:S(2)}, u32[]{:S(2)}) %collective-permute-start.2) | collective-permute-done | bytes 262176 | tf_op jit(solution)/shard_map/ppermute | solution.py:190
  27.9 0.8 constant_dynamic-update-slice_fusion.1
  28.7 0.6 fusion.199
  31.9 1.2 %copy.62 = bf16[1024,256]{1,0:T(8,128)(2,1)S(1)} copy(bf16[1024,256]{0,1:T(8,128)(2,1)} %bitcast.496) | data formatting | bytes 1048576 | tf_op jit(solution)/shard_map/dot_general | solution.py:230
  33.1 1.9 %constant_dynamic-update-slice_fusion = bf16[1024,512]{1,0:T(8,128)(2,1)} fusion(bf16[1024,512]{1,0:T(8,128)(2,1)} %constant_dynamic-update-slice_fusion.1, bf16[1024,256]{1,0:T(8,128)(2,1)} %param.39), kind=kLoop, calls=%fused_computation.277 | loop fusion | bytes 1048576 | tf_op jit(solution)/shard_map/concatenate | solution.py:173
  35.6 1.0 select_bitcast_fusion.17
  36.7 1.3 %select_bitcast_fusion.7 = (bf16[512,2,1,256]{0,3,1,2:T(8,128)(2,1)S(1)}, bf16[512,2,1,256]{0,3,1,2:T(8,128)(2,1)S(1)}) fusion(bf16[512,2,256]{0,2,1:T(8,128)(2,1)} %pad_maximum_fusion.6, bf16[512,2,256]{0,2,1:T(8,128)(2,1)} %collective-permute-done.6, pred[]{:T(512)S(6)} %eq.9), kind=kLoop, calls=%fused_computation.214 | loop fusion | flops 524288 | bytes 2097153 | tf_op jit(solution)/shard_map/stack | solution.py:100
  38.1 7.4 %collective-permute-done.4 = bf16[512,256]{0,1:T(8,128)(2,1)S(1)} collective-permute-done((bf16[512,256]{0,1:T(8,128)(2,1)S(1)}, bf16[512,256]{0,1:T(8,128)(2,1)S(1)}, u32[]{:S(2)}, u32[]{:S(2)}) %collective-permute-start.4) | collective-permute-done | bytes 262176 | tf_op jit(solution)/shard_map/ppermute | solution.py:190
  45.5 1.6 %collective-permute-start.8 = (bf16[512,256]{0,1:T(8,128)(2,1)S(1)}, bf16[512,256]{0,1:T(8,128)(2,1)S(1)}, u32[]{:S(2)}, u32[]{:S(2)}) collective-permute-start(bf16[512,256]{0,1:T(8,128)(2,1)S(1)} %collective-permute-done.4), channel_id=1, source_target_pairs={{0,2},{1,3},{2,0},{3,1},{4,6},{5,7},{6,4},{7,5},{8,10},{9,11},{10,... | collective-permute-start | bytes 786440 | tf_op jit(solution)/shard_map/ppermute | solution.py:97
  47.8 0.9 convolution_convert_fusion.3
  49.5 0.8 bitcast_reduce_fusion.3
  50.3 0.8 fusion.5
  51.1 1.0 fusion.60
  52.4 1.1 collective-permute-done.8
  54.3 1.0 collective-permute-done.7
  55.8 0.9 convolution_convert_fusion.2
  56.8 0.8 bitcast_reduce_fusion.2
  57.6 0.8 fusion.7
  58.5 1.0 fusion.57
  59.5 1.7 %collective-permute-start.10 = (bf16[512,256]{0,1:T(8,128)(2,1)S(1)}, bf16[512,256]{0,1:T(8,128)(2,1)S(1)}, u32[]{:S(2)}, u32[]{:S(2)}) collective-permute-start(bf16[512,256]{0,1:T(8,128)(2,1)S(1)} %collective-permute-done.7), channel_id=1, source_target_pairs={{0,2},{1,3},{2,0},{3,1},{4,6},{5,7},{6,4},{7,5},{8,10},{9,11},{10,... | collective-permute-start | bytes 786440 | tf_op jit(solution)/shard_map/ppermute | solution.py:97
  61.3 5.6 %collective-permute-done.10 = bf16[512,256]{0,1:T(8,128)(2,1)S(1)} collective-permute-done((bf16[512,256]{0,1:T(8,128)(2,1)S(1)}, bf16[512,256]{0,1:T(8,128)(2,1)S(1)}, u32[]{:S(2)}, u32[]{:S(2)}) %collective-permute-start.10) | collective-permute-done | bytes 262176 | tf_op jit(solution)/shard_map/ppermute | solution.py:97
  67.9 0.9 convolution_convert_fusion.1
  68.9 0.8 bitcast_reduce_fusion.1
  69.7 1.1 fusion.9
  70.8 1.0 fusion.63
  72.6 0.9 convolution_convert_fusion
  73.6 0.8 bitcast_reduce_fusion
  74.4 0.8 fusion.10
  75.3 1.0 fusion.106
  77.7 0.7 collective-permute-done.13
  78.5 1.4 %collective-permute-start.14 = (bf16[256,256]{0,1:T(8,128)(2,1)S(1)}, bf16[256,256]{0,1:T(8,128)(2,1)S(1)}, u32[]{:S(2)}, u32[]{:S(2)}) collective-permute-start(bf16[256,256]{0,1:T(8,128)(2,1)S(1)} %fusion.165), channel_id=1, source_target_pairs={{0,2},{1,3},{2,0},{3,1},{4,6},{5,7},{6,4},{7,5},{8,10},{9,11},{10,... | collective-permute-start | bytes 393224 | tf_op jit(solution)/shard_map/ppermute | solution.py:72
  79.9 0.9 bitcast_add_fusion.1
  80.7 1.0 fusion.167
  81.7 0.8 collective-permute-start.20
  82.5 1.8 %collective-permute-done.14 = bf16[256,256]{0,1:T(8,128)(2,1)S(1)} collective-permute-done((bf16[256,256]{0,1:T(8,128)(2,1)S(1)}, bf16[256,256]{0,1:T(8,128)(2,1)S(1)}, u32[]{:S(2)}, u32[]{:S(2)}) %collective-permute-start.14) | collective-permute-done | bytes 131104 | tf_op jit(solution)/shard_map/ppermute | solution.py:72
  84.3 2.9 %collective-permute-done.20 = bf16[256,256]{0,1:T(8,128)(2,1)S(1)} collective-permute-done((bf16[256,256]{0,1:T(8,128)(2,1)S(1)}, bf16[256,256]{0,1:T(8,128)(2,1)S(1)}, u32[]{:S(2)}, u32[]{:S(2)}) %collective-permute-start.20) | collective-permute-done | bytes 131104 | tf_op jit(solution)/shard_map/ppermute | solution.py:72
  87.3 1.0 fusion.160
  88.3 1.2 %collective-permute-start.21 = (bf16[256,256]{0,1:T(8,128)(2,1)S(1)}, bf16[256,256]{0,1:T(8,128)(2,1)S(1)}, u32[]{:S(2)}, u32[]{:S(2)}) collective-permute-start(bf16[256,256]{0,1:T(8,128)(2,1)S(1)} %get-tuple-element.233), channel_id=1, source_target_pairs={{0,2},{1,3},{2,0},{3,1},{4,6},{5,7},{6,4},{7,5},{8,10},{9,11},{10,... | collective-permute-start | bytes 393224 | tf_op jit(solution)/shard_map/ppermute | solution.py:86
  89.5 0.9 collective-permute-start.15
  90.4 4.0 %collective-permute-done.21 = bf16[256,256]{0,1:T(8,128)(2,1)S(1)} collective-permute-done((bf16[256,256]{0,1:T(8,128)(2,1)S(1)}, bf16[256,256]{0,1:T(8,128)(2,1)S(1)}, u32[]{:S(2)}, u32[]{:S(2)}) %collective-permute-start.21) | collective-permute-done | bytes 131104 | tf_op jit(solution)/shard_map/ppermute | solution.py:86
  94.6 1.3 %collective-permute-done.15 = bf16[256,256]{0,1:T(8,128)(2,1)S(1)} collective-permute-done((bf16[256,256]{0,1:T(8,128)(2,1)S(1)}, bf16[256,256]{0,1:T(8,128)(2,1)S(1)}, u32[]{:S(2)}, u32[]{:S(2)}) %collective-permute-start.15) | collective-permute-done | bytes 131104 | tf_op jit(solution)/shard_map/ppermute | solution.py:86
  96.1 1.4 %collective-permute-done.16 = bf16[256,2,256]{0,2,1:T(8,128)(2,1)S(1)} collective-permute-done((bf16[256,2,256]{0,2,1:T(8,128)(2,1)S(1)}, bf16[256,2,256]{0,2,1:T(8,128)(2,1)S(1)}, u32[]{:S(2)}, u32[]{:S(2)}) %collective-permute-start.16) | collective-permute-done | bytes 262176 | tf_op jit(solution)/shard_map/ppermute | solution.py:86
  98.9 4.2 %fusion.109 = f32[256,1024]{0,1:T(8,128)} fusion(bf16[1024,1024]{1,0:T(8,128)(2,1)S(1)} %copy-done, bf16[256,1024]{0,1:T(8,128)(2,1)S(1)} %get-tuple-element.270, bf16[1024,1024]{1,0:T(8,128)(2,1)} %param.42), kind=kOutput, calls=%fused_computation.127 | convolution fusion | flops 1076101120 | bytes 5767168 | tf_op jit(solution)/shard_map/dot_general | solution.py:238
  103.1 1.1 fusion.152
  104.4 4.2 %fusion.111 = f32[256,1024]{0,1:T(8,128)} fusion(bf16[1024,1024]{1,0:T(8,128)(2,1)S(1)} %copy-done, bf16[256,1024]{0,1:T(8,128)(2,1)S(1)} %get-tuple-element.269, bf16[1024,1024]{1,0:T(8,128)(2,1)} %param.42), kind=kOutput, calls=%fused_computation.128 | convolution fusion | flops 1076101120 | bytes 5767168 | tf_op jit(solution)/shard_map/dot_general | solution.py:238
  108.6 1.2 fusion.151
  110.2 1.1 bitcast_add_fusion
  111.3 1.7 %collective-permute-start.24 = (bf16[256,256]{0,1:T(8,128)(2,1)S(1)}, bf16[256,256]{0,1:T(8,128)(2,1)S(1)}, u32[]{:S(2)}, u32[]{:S(2)}) collective-permute-start(bf16[256,256]{0,1:T(8,128)(2,1)S(1)} %fusion.168), channel_id=1, source_target_pairs={{0,2},{1,3},{2,0},{3,1},{4,6},{5,7},{6,4},{7,5},{8,10},{9,11},{10,... | collective-permute-start | bytes 393224 | tf_op jit(solution)/shard_map/ppermute | solution.py:72
  113.6 4.1 %collective-permute-done.24 = bf16[256,256]{0,1:T(8,128)(2,1)S(1)} collective-permute-done((bf16[256,256]{0,1:T(8,128)(2,1)S(1)}, bf16[256,256]{0,1:T(8,128)(2,1)S(1)}, u32[]{:S(2)}, u32[]{:S(2)}) %collective-permute-start.24) | collective-permute-done | bytes 131104 | tf_op jit(solution)/shard_map/ppermute | solution.py:72
  117.8 2.0 %collective-permute-done.18 = bf16[256,256]{0,1:T(8,128)(2,1)S(1)} collective-permute-done((bf16[256,256]{0,1:T(8,128)(2,1)S(1)}, bf16[256,256]{0,1:T(8,128)(2,1)S(1)}, u32[]{:S(2)}, u32[]{:S(2)}) %collective-permute-start.18) | collective-permute-done | bytes 131104 | tf_op jit(solution)/shard_map/ppermute | solution.py:72
  119.8 0.8 copy.51
  (131 shorter events, 11.5 us)
Async XLA Ops:
  0.0 98.9 %copy-start = (bf16[1024,1024]{1,0:T(8,128)(2,1)S(1)}, bf16[1024,1024]{1,0:T(8,128)(2,1)}, u32[]{:S(2)}) copy-start(bf16[1024,1024]{1,0:T(8,128)(2,1)} %param.43) | copy-start | bytes 6291460
  0.9 13.2 %collective-permute-start.1 = (bf16[64,256]{1,0:T(8,128)(2,1)S(1)}, bf16[64,256]{1,0:T(8,128)(2,1)S(1)}, u32[]{:S(2)}, u32[]{:S(2)}) collective-permute-start(bf16[64,256]{1,0:T(8,128)(2,1)S(1)} %get-tuple-element.239), channel_id=1, source_target_pairs={{4,0},{8,4},{12,8},{5,1},{9,5},{13,9},{6,2},{10,6},{14,10},{7,3},{... | collective-permute-start | bytes 98312 | tf_op jit(solution)/shard_map/ppermute | solution.py:21
  2.2 11.9 %collective-permute-start = (bf16[64,256]{1,0:T(8,128)(2,1)S(1)}, bf16[64,256]{1,0:T(8,128)(2,1)S(1)}, u32[]{:S(2)}, u32[]{:S(2)}) collective-permute-start(bf16[64,256]{1,0:T(8,128)(2,1)S(1)} %get-tuple-element.238), channel_id=1, source_target_pairs={{0,4},{4,8},{8,12},{1,5},{5,9},{9,13},{2,6},{6,10},{10,14},{3,7},{... | collective-permute-start | bytes 98312 | tf_op jit(solution)/shard_map/ppermute | solution.py:20
  16.3 12.4 %copy-start.4 = (bf16[1024]{0:T(1024)(128)(2,1)S(1)}, bf16[1024]{0:T(1024)(128)(2,1)}, u32[]{:S(2)}) copy-start(bf16[1024]{0:T(1024)(128)(2,1)} %param.36) | copy-start | bytes 6148
  16.3 12.4 %copy-start.6 = (s32[4,4]{1,0:T(4,128)S(1)}, s32[4,4]{1,0:T(4,128)}, u32[]{:S(2)}) copy-start(s32[4,4]{1,0:T(4,128)} %param.33) | copy-start | bytes 196
  16.5 7.8 %collective-permute-start.3 = (bf16[512,256]{0,1:T(8,128)(2,1)S(1)}, bf16[512,256]{0,1:T(8,128)(2,1)S(1)}, u32[]{:S(2)}, u32[]{:S(2)}) collective-permute-start(bf16[512,256]{0,1:T(8,128)(2,1)S(1)} %add_convert_fusion), channel_id=1, source_target_pairs={{0,2},{1,3},{2,0},{3,1},{4,6},{5,7},{6,4},{7,5},{8,10},{9,11},{10,... | collective-permute-start | bytes 786440 | tf_op jit(solution)/shard_map/ppermute | solution.py:97
  18.5 9.4 %copy-start.2 = (bf16[1024,256]{1,0:T(8,128)(2,1)S(1)}, bf16[1024,256]{1,0:T(8,128)(2,1)}, u32[]{:S(2)}) copy-start(bf16[1024,256]{1,0:T(8,128)(2,1)} %param.38) | copy-start | bytes 1572868
  18.5 9.0 %collective-permute-start.2 = (bf16[512,256]{0,1:T(8,128)(2,1)S(1)}, bf16[512,256]{0,1:T(8,128)(2,1)S(1)}, u32[]{:S(2)}, u32[]{:S(2)}) collective-permute-start(bf16[512,256]{0,1:T(8,128)(2,1)S(1)} %add_convert_fusion), channel_id=1, source_target_pairs={{0,4},{4,8},{8,12},{12,0},{1,5},{5,9},{9,13},{13,1},{2,6},{6,10},{... | collective-permute-start | bytes 786440 | tf_op jit(solution)/shard_map/ppermute | solution.py:190
  27.5 8.1 %collective-permute-start.5 = (bf16[512,256]{0,1:T(8,128)(2,1)S(1)}, bf16[512,256]{0,1:T(8,128)(2,1)}, u32[]{:S(2)}, u32[]{:S(2)}) collective-permute-start(bf16[512,256]{0,1:T(8,128)(2,1)S(1)} %collective-permute-done.2), channel_id=1, source_target_pairs={{0,2},{1,3},{2,0},{3,1},{4,6},{5,7},{6,4},{7,5},{8,10},{9,11},{10,... | collective-permute-start | bytes 786440 | tf_op jit(solution)/shard_map/ppermute | solution.py:97
  27.9 8.8 %collective-permute-start.6 = (bf16[512,2,256]{0,2,1:T(8,128)(2,1)}, bf16[512,2,256]{0,2,1:T(8,128)(2,1)}, u32[]{:S(2)}, u32[]{:S(2)}) collective-permute-start(bf16[512,2,256]{0,2,1:T(8,128)(2,1)} %pad_maximum_fusion.6), channel_id=1, source_target_pairs={{0,1},{1,0},{2,3},{3,2},{4,5},{5,4},{6,7},{7,6},{8,9},{9,8},{10,11... | collective-permute-start | bytes 1572872 | tf_op jit(solution)/shard_map/ppermute | solution.py:97
  35.0 10.5 %collective-permute-start.4 = (bf16[512,256]{0,1:T(8,128)(2,1)S(1)}, bf16[512,256]{0,1:T(8,128)(2,1)S(1)}, u32[]{:S(2)}, u32[]{:S(2)}) collective-permute-start(bf16[512,256]{0,1:T(8,128)(2,1)S(1)} %collective-permute-done.2), channel_id=1, source_target_pairs={{0,4},{4,8},{8,12},{12,0},{1,5},{5,9},{9,13},{13,1},{2,6},{6,10},{... | collective-permute-start | bytes 786440 | tf_op jit(solution)/shard_map/ppermute | solution.py:190
  38.1 9.7 %copy-start.3 = (bf16[1024,512]{1,0:T(8,128)(2,1)S(1)}, bf16[1024,512]{1,0:T(8,128)(2,1)}, u32[]{:S(2)}) copy-start(bf16[1024,512]{1,0:T(8,128)(2,1)} %constant_dynamic-update-slice_fusion) | copy-start | bytes 3145732
  45.5 9.7 %collective-permute-start.7 = (bf16[512,256]{0,1:T(8,128)(2,1)S(1)}, bf16[512,256]{0,1:T(8,128)(2,1)S(1)}, u32[]{:S(2)}, u32[]{:S(2)}) collective-permute-start(bf16[512,256]{0,1:T(8,128)(2,1)S(1)} %collective-permute-done.4), channel_id=1, source_target_pairs={{0,4},{4,8},{8,12},{12,0},{1,5},{5,9},{9,13},{13,1},{2,6},{6,10},{... | collective-permute-start | bytes 786440 | tf_op jit(solution)/shard_map/ppermute | solution.py:190
  45.5 7.9 %collective-permute-start.8 = (bf16[512,256]{0,1:T(8,128)(2,1)S(1)}, bf16[512,256]{0,1:T(8,128)(2,1)S(1)}, u32[]{:S(2)}, u32[]{:S(2)}) collective-permute-start(bf16[512,256]{0,1:T(8,128)(2,1)S(1)} %collective-permute-done.4), channel_id=1, source_target_pairs={{0,2},{1,3},{2,0},{3,1},{4,6},{5,7},{6,4},{7,5},{8,10},{9,11},{10,... | collective-permute-start | bytes 786440 | tf_op jit(solution)/shard_map/ppermute | solution.py:97
  47.8 1.0 copy-start.7
  52.1 2.0 %collective-permute-start.9 = (bf16[512,2,256]{0,2,1:T(8,128)(2,1)S(1)}, bf16[512,2,256]{0,2,1:T(8,128)(2,1)S(1)}, u32[]{:S(2)}, u32[]{:S(2)}) collective-permute-start(bf16[512,2,256]{0,2,1:T(8,128)(2,1)S(1)} %pad_maximum_fusion.7), channel_id=1, source_target_pairs={{0,1},{1,0},{2,3},{3,2},{4,5},{5,4},{6,7},{7,6},{8,9},{9,8},{10,11... | collective-permute-start | bytes 1572872 | tf_op jit(solution)/shard_map/ppermute | solution.py:97
  59.5 7.5 %collective-permute-start.10 = (bf16[512,256]{0,1:T(8,128)(2,1)S(1)}, bf16[512,256]{0,1:T(8,128)(2,1)S(1)}, u32[]{:S(2)}, u32[]{:S(2)}) collective-permute-start(bf16[512,256]{0,1:T(8,128)(2,1)S(1)} %collective-permute-done.7), channel_id=1, source_target_pairs={{0,2},{1,3},{2,0},{3,1},{4,6},{5,7},{6,4},{7,5},{8,10},{9,11},{10,... | collective-permute-start | bytes 786440 | tf_op jit(solution)/shard_map/ppermute | solution.py:97
  61.2 5.9 %collective-permute-start.11 = (bf16[512,2,256]{0,2,1:T(8,128)(2,1)S(1)}, bf16[512,2,256]{0,2,1:T(8,128)(2,1)S(1)}, u32[]{:S(2)}, u32[]{:S(2)}) collective-permute-start(bf16[512,2,256]{0,2,1:T(8,128)(2,1)S(1)} %pad_maximum_fusion.8), channel_id=1, source_target_pairs={{0,1},{1,0},{2,3},{3,2},{4,5},{5,4},{6,7},{7,6},{8,9},{9,8},{10,11... | collective-permute-start | bytes 1572872 | tf_op jit(solution)/shard_map/ppermute | solution.py:97
  68.9 3.0 %collective-permute-start.12 = (bf16[512,2,256]{0,2,1:T(8,128)(2,1)S(1)}, bf16[512,2,256]{0,2,1:T(8,128)(2,1)S(1)}, u32[]{:S(2)}, u32[]{:S(2)}) collective-permute-start(bf16[512,2,256]{0,2,1:T(8,128)(2,1)S(1)} %pad_maximum_fusion.9), channel_id=1, source_target_pairs={{0,1},{1,0},{2,3},{3,2},{4,5},{5,4},{6,7},{7,6},{8,9},{9,8},{10,11... | collective-permute-start | bytes 1572872 | tf_op jit(solution)/shard_map/ppermute | solution.py:97
  76.7 1.7 %collective-permute-start.13 = (bf16[256,2,256]{0,2,1:T(8,128)(2,1)S(1)}, bf16[256,2,256]{0,2,1:T(8,128)(2,1)S(1)}, u32[]{:S(2)}, u32[]{:S(2)}) collective-permute-start(bf16[256,2,256]{0,2,1:T(8,128)(2,1)S(1)} %fusion.149), channel_id=1, source_target_pairs={{0,1},{1,0},{2,3},{3,2},{4,5},{5,4},{6,7},{7,6},{8,9},{9,8},{10,11... | collective-permute-start | bytes 786440 | tf_op jit(solution)/shard_map/ppermute | solution.py:72
  77.6 2.3 %collective-permute-start.19 = (bf16[256,2,256]{0,2,1:T(8,128)(2,1)S(1)}, bf16[256,2,256]{0,2,1:T(8,128)(2,1)S(1)}, u32[]{:S(2)}, u32[]{:S(2)}) collective-permute-start(bf16[256,2,256]{0,2,1:T(8,128)(2,1)S(1)} %fusion.150), channel_id=1, source_target_pairs={{0,1},{1,0},{2,3},{3,2},{4,5},{5,4},{6,7},{7,6},{8,9},{9,8},{10,11... | collective-permute-start | bytes 786440 | tf_op jit(solution)/shard_map/ppermute | solution.py:72
  78.5 5.8 %collective-permute-start.14 = (bf16[256,256]{0,1:T(8,128)(2,1)S(1)}, bf16[256,256]{0,1:T(8,128)(2,1)S(1)}, u32[]{:S(2)}, u32[]{:S(2)}) collective-permute-start(bf16[256,256]{0,1:T(8,128)(2,1)S(1)} %fusion.165), channel_id=1, source_target_pairs={{0,2},{1,3},{2,0},{3,1},{4,6},{5,7},{6,4},{7,5},{8,10},{9,11},{10,... | collective-permute-start | bytes 393224 | tf_op jit(solution)/shard_map/ppermute | solution.py:72
  80.7 15.2 %copy-start.5 = (bf16[1024]{0:T(1024)(128)(2,1)S(1)}, bf16[1024]{0:T(1024)(128)(2,1)}, u32[]{:S(2)}) copy-start(bf16[1024]{0:T(1024)(128)(2,1)} %param.41) | copy-start | bytes 6148
  81.7 5.5 %collective-permute-start.20 = (bf16[256,256]{0,1:T(8,128)(2,1)S(1)}, bf16[256,256]{0,1:T(8,128)(2,1)S(1)}, u32[]{:S(2)}, u32[]{:S(2)}) collective-permute-start(bf16[256,256]{0,1:T(8,128)(2,1)S(1)} %fusion.167), channel_id=1, source_target_pairs={{0,2},{1,3},{2,0},{3,1},{4,6},{5,7},{6,4},{7,5},{8,10},{9,11},{10,... | collective-permute-start | bytes 393224 | tf_op jit(solution)/shard_map/ppermute | solution.py:72
  88.3 6.1 %collective-permute-start.21 = (bf16[256,256]{0,1:T(8,128)(2,1)S(1)}, bf16[256,256]{0,1:T(8,128)(2,1)S(1)}, u32[]{:S(2)}, u32[]{:S(2)}) collective-permute-start(bf16[256,256]{0,1:T(8,128)(2,1)S(1)} %get-tuple-element.233), channel_id=1, source_target_pairs={{0,2},{1,3},{2,0},{3,1},{4,6},{5,7},{6,4},{7,5},{8,10},{9,11},{10,... | collective-permute-start | bytes 393224 | tf_op jit(solution)/shard_map/ppermute | solution.py:86
  89.5 6.3 %collective-permute-start.15 = (bf16[256,256]{0,1:T(8,128)(2,1)S(1)}, bf16[256,256]{0,1:T(8,128)(2,1)S(1)}, u32[]{:S(2)}, u32[]{:S(2)}) collective-permute-start(bf16[256,256]{0,1:T(8,128)(2,1)S(1)} %get-tuple-element.232), channel_id=1, source_target_pairs={{0,2},{1,3},{2,0},{3,1},{4,6},{5,7},{6,4},{7,5},{8,10},{9,11},{10,... | collective-permute-start | bytes 393224 | tf_op jit(solution)/shard_map/ppermute | solution.py:86
  94.5 1.6 %collective-permute-start.22 = (bf16[256,2,256]{0,2,1:T(8,128)(2,1)S(1)}, bf16[256,2,256]{0,2,1:T(8,128)(2,1)S(1)}, u32[]{:S(2)}, u32[]{:S(2)}) collective-permute-start(bf16[256,2,256]{0,2,1:T(8,128)(2,1)S(1)} %pad_maximum_fusion.11), channel_id=1, source_target_pairs={{0,1},{1,0},{2,3},{3,2},{4,5},{5,4},{6,7},{7,6},{8,9},{9,8},{10,11... | collective-permute-start | bytes 786440 | tf_op jit(solution)/shard_map/ppermute | solution.py:86
  95.9 1.6 %collective-permute-start.16 = (bf16[256,2,256]{0,2,1:T(8,128)(2,1)S(1)}, bf16[256,2,256]{0,2,1:T(8,128)(2,1)S(1)}, u32[]{:S(2)}, u32[]{:S(2)}) collective-permute-start(bf16[256,2,256]{0,2,1:T(8,128)(2,1)S(1)} %pad_maximum_fusion.10), channel_id=1, source_target_pairs={{0,1},{1,0},{2,3},{3,2},{4,5},{5,4},{6,7},{7,6},{8,9},{9,8},{10,11... | collective-permute-start | bytes 786440 | tf_op jit(solution)/shard_map/ppermute | solution.py:86
  104.2 6.0 %collective-permute-start.23 = (bf16[256,2,256]{0,2,1:T(8,128)(2,1)S(1)}, bf16[256,2,256]{0,2,1:T(8,128)(2,1)S(1)}, u32[]{:S(2)}, u32[]{:S(2)}) collective-permute-start(bf16[256,2,256]{0,2,1:T(8,128)(2,1)S(1)} %fusion.152), channel_id=1, source_target_pairs={{0,1},{1,0},{2,3},{3,2},{4,5},{5,4},{6,7},{7,6},{8,9},{9,8},{10,11... | collective-permute-start | bytes 786440 | tf_op jit(solution)/shard_map/ppermute | solution.py:72
  108.6 4.4 %copy-start.1 = (f32[256,1024]{0,1:T(8,128)S(1)}, f32[256,1024]{0,1:T(8,128)}, u32[]{:S(2)}) copy-start(f32[256,1024]{0,1:T(8,128)} %fusion.111) | copy-start | bytes 3145732
  109.8 3.3 %collective-permute-start.17 = (bf16[256,2,256]{0,2,1:T(8,128)(2,1)S(1)}, bf16[256,2,256]{0,2,1:T(8,128)(2,1)S(1)}, u32[]{:S(2)}, u32[]{:S(2)}) collective-permute-start(bf16[256,2,256]{0,2,1:T(8,128)(2,1)S(1)} %fusion.151), channel_id=1, source_target_pairs={{0,1},{1,0},{2,3},{3,2},{4,5},{5,4},{6,7},{7,6},{8,9},{9,8},{10,11... | collective-permute-start | bytes 786440 | tf_op jit(solution)/shard_map/ppermute | solution.py:72
  111.3 6.4 %collective-permute-start.24 = (bf16[256,256]{0,1:T(8,128)(2,1)S(1)}, bf16[256,256]{0,1:T(8,128)(2,1)S(1)}, u32[]{:S(2)}, u32[]{:S(2)}) collective-permute-start(bf16[256,256]{0,1:T(8,128)(2,1)S(1)} %fusion.168), channel_id=1, source_target_pairs={{0,2},{1,3},{2,0},{3,1},{4,6},{5,7},{6,4},{7,5},{8,10},{9,11},{10,... | collective-permute-start | bytes 393224 | tf_op jit(solution)/shard_map/ppermute | solution.py:72
  113.1 6.6 %collective-permute-start.18 = (bf16[256,256]{0,1:T(8,128)(2,1)S(1)}, bf16[256,256]{0,1:T(8,128)(2,1)S(1)}, u32[]{:S(2)}, u32[]{:S(2)}) collective-permute-start(bf16[256,256]{0,1:T(8,128)(2,1)S(1)} %fusion.166), channel_id=1, source_target_pairs={{0,2},{1,3},{2,0},{3,1},{4,6},{5,7},{6,4},{7,5},{8,10},{9,11},{10,... | collective-permute-start | bytes 393224 | tf_op jit(solution)/shard_map/ppermute | solution.py:72

commit v10 on v9

--- a/solution.py
+++ b/solution.py
@@ -101,10 +101,10 @@
     return current
 
 
-def absorb_block(state, query_heads, block, linked, head_count, brick_rows, local_width):
+def absorb_block(state, query_heads, key_block, value_block, linked, head_count, brick_rows):
     row_max, row_mass, weighted = state
-    key_rows = block[:, :local_width].reshape(-1, head_count, HEAD_DIM)
-    value_rows = block[:, local_width:].reshape(-1, head_count, HEAD_DIM)
+    key_rows = key_block.reshape(-1, head_count, HEAD_DIM)
+    value_rows = value_block.reshape(-1, head_count, HEAD_DIM)
     scores = (
         jnp.einsum("bqhd,khd->bhqk", query_heads, key_rows, preferred_element_type=jnp.float32)
         * HEAD_DIM ** (-0.5)
@@ -170,7 +170,6 @@
     brick_dev = lax.axis_index("bricks")
     dev_total = lax.axis_size("bricks")
     ring = [(i, (i + 1) % dev_total) for i in range(dev_total)]
-    pair_weight = jnp.concatenate([key_weight, value_weight], axis=1)
     linked_rows = lax.dynamic_slice_in_dim(pattern, first_brick, local_bricks, 0)
     state = (
         jnp.full((local_bricks, head_count, brick_rows), -1e30, jnp.float32),
@@ -205,14 +204,17 @@
                     normed_now, query_weight, preferred_element_type=jnp.float32
                 ).astype(jnp.bfloat16)
                 query_heads = queries.reshape(local_bricks, brick_rows, head_count, HEAD_DIM)
-            pair_block = jnp.dot(
-                normed_now, pair_weight, preferred_element_type=jnp.float32
+            key_block = jnp.dot(
+                normed_now, key_weight, preferred_element_type=jnp.float32
+            ).astype(jnp.bfloat16)
+            value_block = jnp.dot(
+                normed_now, value_weight, preferred_element_type=jnp.float32
             ).astype(jnp.bfloat16)
             source = (brick_dev - step) % dev_total
             key_ids = source * local_bricks + jnp.arange(local_bricks, dtype=jnp.int32)
             linked = jnp.take(linked_rows, key_ids, axis=1) > 0
             state = absorb_block(
-                state, query_heads, pair_block, linked, head_count, brick_rows, local_width
+                state, query_heads, key_block, value_block, linked, head_count, brick_rows
             )
         if slot < dev_total + 1:
             packed = lax.optimization_barrier((state, [table[key] for table, key in made]))

time: 121 us -> 121 us (level)
  local copies, waits for them, and re-layouts: 15.2 us -> 12.7 us
  matrix products: 20.4 us -> 22.1 us
    concatenate x1 -> x0, local copies, waits for them, and re-layouts: 1.91 us -> none  [shards(): pair_weight = jnp.concatenate([key_weight, value_weight], axis=1)]
    ppermute x8, waiting for transfers between devices: 11.5 us -> 13.1 us  [gather_levels(): lax.ppermute(current, 'heads', [(i, i ^ bit) for i in range(head_total)])]
    ppermute x3, waiting for transfers between devices: 10.6 us -> 9.02 us  [shards(): ringed[slot + 1] = lax.ppermute(ringed[slot], 'bricks', ring)]
    dot_general x4 -> x8, matrix products: 3.74 us -> 5.13 us  [the longest x4 2.56 us: shards(): jnp.dot(normed_now, key_weight, preferred_element_type=jnp.float32)]
  transfers between devices with their start and end apart: 25 -> 25, of which waited for: 16 -> 16; matrix products, arithmetic and copies ran while one was open for 25% -> 23% of each run, Pallas kernels for 0% -> 0%
where the time goes in v10:
time: 121 us; the launch traced here: 120 us
  waiting for transfers between devices  40.8 us (34%)
  starting transfers between devices  22.7 us (19%)
  matrix products  22.1 us (18%)
  other arithmetic  17.2 us (14%)
  local copies, waits for them, and re-layouts  12.7 us (10%)
  between operations  4.56 us (4%)
    ppermute x8, waiting for transfers between devices, gather_levels(): lax.ppermute(current, 'heads', [(i, i ^ bit) for i in range(head_total)])  13.1 us
    ppermute x8, waiting for transfers between devices, scatter_heads(): lax.ppermute(give.astype(jnp.bfloat16), 'heads', [(i, i ^ bit) for i in r...  11.5 us
    ppermute x3, waiting for transfers between devices, shards(): ringed[slot + 1] = lax.ppermute(ringed[slot], 'bricks', ring)  9.02 us
    dot_general x2, matrix products, shards(): lowered = jnp.dot(hidden, down_weight, preferred_element_type=jnp.float32)  8.41 us
    ppermute x4, waiting for transfers between devices, gather_heads(): lax.ppermute(current, 'heads', [(i, i ^ bit) for i in range(head_total)])  7.2 us
    ppermute x8, starting transfers between devices, gather_levels(): lax.ppermute(current, 'heads', [(i, i ^ bit) for i in range(head_total)])  5.88 us
    ppermute x8, starting transfers between devices, scatter_heads(): lax.ppermute(give.astype(jnp.bfloat16), 'heads', [(i, i ^ bit) for i in r...  5.58 us
    ppermute x1, starting transfers between devices, extended_2(): before = lax.ppermute(last, axis, up)  5.56 us
  transfers between devices with their start and end apart: 25, of which 16 were waited for; matrix products, arithmetic and copies ran while one was open for 23% of the time, Pallas kernels for 0%

profile of v10, /device:TPU:0, one launch (start us, length us, event | category | flops | bytes accessed | tf_op | source)
XLA Modules:
  0.0 120.1 jit_solution(12904023276750405028)
XLA Ops:
  0.0 0.9 fusion.187
  0.9 1.3 %collective-permute-start.1 = (bf16[64,256]{1,0:T(8,128)(2,1)S(1)}, bf16[64,256]{1,0:T(8,128)(2,1)S(1)}, u32[]{:S(2)}, u32[]{:S(2)}) collective-permute-start(bf16[64,256]{1,0:T(8,128)(2,1)S(1)} %get-tuple-element.231), channel_id=1, source_target_pairs={{4,0},{8,4},{12,8},{5,1},{9,5},{13,9},{6,2},{10,6},{14,10},{7,3},{... | collective-permute-start | bytes 98312 | tf_op jit(solution)/shard_map/ppermute | solution.py:21
  2.2 5.6 %collective-permute-start = (bf16[64,256]{1,0:T(8,128)(2,1)S(1)}, bf16[64,256]{1,0:T(8,128)(2,1)S(1)}, u32[]{:S(2)}, u32[]{:S(2)}) collective-permute-start(bf16[64,256]{1,0:T(8,128)(2,1)S(1)} %get-tuple-element.230), channel_id=1, source_target_pairs={{0,4},{4,8},{8,12},{1,5},{5,9},{9,13},{2,6},{6,10},{10,14},{3,7},{... | collective-permute-start | bytes 98312 | tf_op jit(solution)/shard_map/ppermute | solution.py:20
  7.8 1.0 fusion.188
  8.8 0.9 fusion.189
  9.7 1.1 copy.29
  10.8 1.4 %fusion.191 = (s32[1]{0:T(128)}, s32[1]{0:T(128)}) fusion(s32[4]{0:T(128)} %param.32, s32[]{:T(128)} %bitcast.2, s32[]{:T(128)} %bitcast.6), kind=kLoop, calls=%fused_computation.309 | loop fusion | bytes 24 | tf_op jit(solution)/shard_map/jit(_take)/gather | solution.py:157
  13.5 0.7 convert_element_type.237
  14.5 1.7 %fusion.101 = f32[1,8,8,8,256]{4,3,2,1,0:T(8,128)S(1)} fusion(f32[1,10,10,10,256]{4,3,2,1,0:T(8,128)S(1)} %select_maximum_fusion, f32[1,1,8,8,256]{4,3,2,1,0:T(8,128)S(1)} %multiply_bitcast_fusion, f32[1,8,8,8,256]{4,3,2,1,0:T(8,128)S(1)} %bitcast.490, f32[1,1,8,8,256]{4,3,2,1,0:T(8,128)S(1)} %multiply_bitcast_fusion.1, f32[256]{0:T(256)S(1)} %bitcast.539, ...), kind=kLoop, calls=%fused_computation.125 | loop fusion | flops 7208960 | bytes 13790208 | tf_op jit(solution)/shard_map/add | solution.py:51
  16.5 2.0 %collective-permute-start.3 = (bf16[512,256]{0,1:T(8,128)(2,1)S(1)}, bf16[512,256]{0,1:T(8,128)(2,1)S(1)}, u32[]{:S(2)}, u32[]{:S(2)}) collective-permute-start(bf16[512,256]{0,1:T(8,128)(2,1)S(1)} %add_convert_fusion), channel_id=1, source_target_pairs={{0,2},{1,3},{2,0},{3,1},{4,6},{5,7},{6,4},{7,5},{8,10},{9,11},{10,... | collective-permute-start | bytes 786440 | tf_op jit(solution)/shard_map/ppermute | solution.py:97
  18.5 1.6 %collective-permute-start.2 = (bf16[512,256]{0,1:T(8,128)(2,1)S(1)}, bf16[512,256]{0,1:T(8,128)(2,1)S(1)}, u32[]{:S(2)}, u32[]{:S(2)}) collective-permute-start(bf16[512,256]{0,1:T(8,128)(2,1)S(1)} %add_convert_fusion), channel_id=1, source_target_pairs={{0,4},{4,8},{8,12},{12,0},{1,5},{5,9},{9,13},{13,1},{2,6},{6,10},{... | collective-permute-start | bytes 786440 | tf_op jit(solution)/shard_map/ppermute | solution.py:189
  20.1 4.3 %collective-permute-done.3 = bf16[512,256]{0,1:T(8,128)(2,1)S(1)} collective-permute-done((bf16[512,256]{0,1:T(8,128)(2,1)S(1)}, bf16[512,256]{0,1:T(8,128)(2,1)S(1)}, u32[]{:S(2)}, u32[]{:S(2)}) %collective-permute-start.3) | collective-permute-done | bytes 262176 | tf_op jit(solution)/shard_map/ppermute | solution.py:97
  24.4 0.8 pad_maximum_fusion.6
  25.2 2.3 %collective-permute-done.2 = bf16[512,256]{0,1:T(8,128)(2,1)S(1)} collective-permute-done((bf16[512,256]{0,1:T(8,128)(2,1)S(1)}, bf16[512,256]{0,1:T(8,128)(2,1)S(1)}, u32[]{:S(2)}, u32[]{:S(2)}) %collective-permute-start.2) | collective-permute-done | bytes 262176 | tf_op jit(solution)/shard_map/ppermute | solution.py:189
  27.9 0.7 fusion.190
  31.2 1.2 %copy.62 = bf16[1024,256]{1,0:T(8,128)(2,1)S(1)} copy(bf16[1024,256]{0,1:T(8,128)(2,1)} %bitcast.500) | data formatting | bytes 1048576 | tf_op jit(solution)/shard_map/dot_general | solution.py:232
  33.0 0.9 collective-permute-done.5
  34.0 1.0 select_bitcast_fusion.17
  35.0 1.3 %select_bitcast_fusion.7 = (bf16[512,2,1,256]{0,3,1,2:T(8,128)(2,1)S(1)}, bf16[512,2,1,256]{0,3,1,2:T(8,128)(2,1)S(1)}) fusion(bf16[512,2,256]{0,2,1:T(8,128)(2,1)} %pad_maximum_fusion.6, bf16[512,2,256]{0,2,1:T(8,128)(2,1)} %collective-permute-done.6, pred[]{:T(512)S(6)} %eq.9), kind=kLoop, calls=%fused_computation.209 | loop fusion | flops 524288 | bytes 2097153 | tf_op jit(solution)/shard_map/stack | solution.py:100
  36.5 6.5 %collective-permute-done.4 = bf16[512,256]{0,1:T(8,128)(2,1)S(1)} collective-permute-done((bf16[512,256]{0,1:T(8,128)(2,1)S(1)}, bf16[512,256]{0,1:T(8,128)(2,1)S(1)}, u32[]{:S(2)}, u32[]{:S(2)}) %collective-permute-start.4) | collective-permute-done | bytes 262176 | tf_op jit(solution)/shard_map/ppermute | solution.py:189
  43.0 1.6 %collective-permute-start.8 = (bf16[512,256]{0,1:T(8,128)(2,1)S(1)}, bf16[512,256]{0,1:T(8,128)(2,1)S(1)}, u32[]{:S(2)}, u32[]{:S(2)}) collective-permute-start(bf16[512,256]{0,1:T(8,128)(2,1)S(1)} %collective-permute-done.4), channel_id=1, source_target_pairs={{0,2},{1,3},{2,0},{3,1},{4,6},{5,7},{6,4},{7,5},{8,10},{9,11},{10,... | collective-permute-start | bytes 786440 | tf_op jit(solution)/shard_map/ppermute | solution.py:97
  45.2 0.6 convolution_convert_fusion.8
  45.9 0.6 convolution_convert_fusion.7
  47.6 0.8 bitcast_reduce_fusion.3
  48.4 0.8 fusion.5
  49.2 1.0 fusion.60
  51.0 1.2 collective-permute-done.9
  53.3 0.6 convolution_convert_fusion.5
  54.6 0.8 bitcast_reduce_fusion.2
  55.4 0.8 fusion.7
  56.2 1.0 fusion.57
  57.2 1.7 %collective-permute-start.10 = (bf16[512,256]{0,1:T(8,128)(2,1)S(1)}, bf16[512,256]{0,1:T(8,128)(2,1)S(1)}, u32[]{:S(2)}, u32[]{:S(2)}) collective-permute-start(bf16[512,256]{0,1:T(8,128)(2,1)S(1)} %collective-permute-done.7), channel_id=1, source_target_pairs={{0,2},{1,3},{2,0},{3,1},{4,6},{5,7},{6,4},{7,5},{8,10},{9,11},{10,... | collective-permute-start | bytes 786440 | tf_op jit(solution)/shard_map/ppermute | solution.py:97
  59.0 6.3 %collective-permute-done.10 = bf16[512,256]{0,1:T(8,128)(2,1)S(1)} collective-permute-done((bf16[512,256]{0,1:T(8,128)(2,1)S(1)}, bf16[512,256]{0,1:T(8,128)(2,1)S(1)}, u32[]{:S(2)}, u32[]{:S(2)}) %collective-permute-start.10) | collective-permute-done | bytes 262176 | tf_op jit(solution)/shard_map/ppermute | solution.py:97
  66.3 0.6 convolution_convert_fusion.3
  66.9 0.6 convolution_convert_fusion.2
  67.7 1.0 bitcast_reduce_fusion.1
  68.7 0.8 fusion.9
  69.6 1.0 fusion.63
  71.4 0.6 convolution_convert_fusion
  72.7 0.8 bitcast_reduce_fusion
  73.5 0.8 fusion.10
  74.4 1.0 fusion.94
  76.7 0.7 collective-permute-done.13
  77.6 0.7 collective-permute-start.14
  78.3 0.9 bitcast_add_fusion.1
  79.1 1.0 fusion.159
  80.1 1.5 %collective-permute-start.20 = (bf16[256,256]{0,1:T(8,128)(2,1)S(1)}, bf16[256,256]{0,1:T(8,128)(2,1)S(1)}, u32[]{:S(2)}, u32[]{:S(2)}) collective-permute-start(bf16[256,256]{0,1:T(8,128)(2,1)S(1)} %fusion.159), channel_id=1, source_target_pairs={{0,2},{1,3},{2,0},{3,1},{4,6},{5,7},{6,4},{7,5},{8,10},{9,11},{10,... | collective-permute-start | bytes 393224 | tf_op jit(solution)/shard_map/ppermute | solution.py:72
  81.6 2.3 %collective-permute-done.14 = bf16[256,256]{0,1:T(8,128)(2,1)S(1)} collective-permute-done((bf16[256,256]{0,1:T(8,128)(2,1)S(1)}, bf16[256,256]{0,1:T(8,128)(2,1)S(1)}, u32[]{:S(2)}, u32[]{:S(2)}) %collective-permute-start.14) | collective-permute-done | bytes 131104 | tf_op jit(solution)/shard_map/ppermute | solution.py:72
  83.9 2.4 %collective-permute-done.20 = bf16[256,256]{0,1:T(8,128)(2,1)S(1)} collective-permute-done((bf16[256,256]{0,1:T(8,128)(2,1)S(1)}, bf16[256,256]{0,1:T(8,128)(2,1)S(1)}, u32[]{:S(2)}, u32[]{:S(2)}) %collective-permute-start.20) | collective-permute-done | bytes 131104 | tf_op jit(solution)/shard_map/ppermute | solution.py:72
  86.2 1.0 fusion.148
  87.2 0.9 collective-permute-start.21
  88.2 1.2 collective-permute-start.15
  89.3 4.4 %collective-permute-done.21 = bf16[256,256]{0,1:T(8,128)(2,1)S(1)} collective-permute-done((bf16[256,256]{0,1:T(8,128)(2,1)S(1)}, bf16[256,256]{0,1:T(8,128)(2,1)S(1)}, u32[]{:S(2)}, u32[]{:S(2)}) %collective-permute-start.21) | collective-permute-done | bytes 131104 | tf_op jit(solution)/shard_map/ppermute | solution.py:86
  93.9 1.3 %collective-permute-done.15 = bf16[256,256]{0,1:T(8,128)(2,1)S(1)} collective-permute-done((bf16[256,256]{0,1:T(8,128)(2,1)S(1)}, bf16[256,256]{0,1:T(8,128)(2,1)S(1)}, u32[]{:S(2)}, u32[]{:S(2)}) %collective-permute-start.15) | collective-permute-done | bytes 131104 | tf_op jit(solution)/shard_map/ppermute | solution.py:86
  95.4 1.5 %collective-permute-done.16 = bf16[256,2,256]{0,2,1:T(8,128)(2,1)S(1)} collective-permute-done((bf16[256,2,256]{0,2,1:T(8,128)(2,1)S(1)}, bf16[256,2,256]{0,2,1:T(8,128)(2,1)S(1)}, u32[]{:S(2)}, u32[]{:S(2)}) %collective-permute-start.16) | collective-permute-done | bytes 262176 | tf_op jit(solution)/shard_map/ppermute | solution.py:86
  98.3 4.2 %fusion.97 = f32[256,1024]{0,1:T(8,128)} fusion(bf16[1024,1024]{1,0:T(8,128)(2,1)S(1)} %copy-done, bf16[256,1024]{0,1:T(8,128)(2,1)S(1)} %get-tuple-element.262, bf16[1024,1024]{1,0:T(8,128)(2,1)} %param.42), kind=kOutput, calls=%fused_computation.122 | convolution fusion | flops 1076101120 | bytes 5767168 | tf_op jit(solution)/shard_map/dot_general | solution.py:240
  102.5 1.1 fusion.140
  103.8 4.2 %fusion.99 = f32[256,1024]{0,1:T(8,128)} fusion(bf16[1024,1024]{1,0:T(8,128)(2,1)S(1)} %copy-done, bf16[256,1024]{0,1:T(8,128)(2,1)S(1)} %get-tuple-element.261, bf16[1024,1024]{1,0:T(8,128)(2,1)} %param.42), kind=kOutput, calls=%fused_computation.123 | convolution fusion | flops 1076101120 | bytes 5767168 | tf_op jit(solution)/shard_map/dot_general | solution.py:240
  108.0 1.2 fusion.139
  109.6 1.1 bitcast_add_fusion
  111.3 1.7 %collective-permute-start.18 = (bf16[256,256]{0,1:T(8,128)(2,1)S(1)}, bf16[256,256]{0,1:T(8,128)(2,1)S(1)}, u32[]{:S(2)}, u32[]{:S(2)}) collective-permute-start(bf16[256,256]{0,1:T(8,128)(2,1)S(1)} %fusion.158), channel_id=1, source_target_pairs={{0,2},{1,3},{2,0},{3,1},{4,6},{5,7},{6,4},{7,5},{8,10},{9,11},{10,... | collective-permute-start | bytes 393224 | tf_op jit(solution)/shard_map/ppermute | solution.py:72
  113.0 4.1 %collective-permute-done.24 = bf16[256,256]{0,1:T(8,128)(2,1)S(1)} collective-permute-done((bf16[256,256]{0,1:T(8,128)(2,1)S(1)}, bf16[256,256]{0,1:T(8,128)(2,1)S(1)}, u32[]{:S(2)}, u32[]{:S(2)}) %collective-permute-start.24) | collective-permute-done | bytes 131104 | tf_op jit(solution)/shard_map/ppermute | solution.py:72
  117.2 2.0 %collective-permute-done.18 = bf16[256,256]{0,1:T(8,128)(2,1)S(1)} collective-permute-done((bf16[256,256]{0,1:T(8,128)(2,1)S(1)}, bf16[256,256]{0,1:T(8,128)(2,1)S(1)}, u32[]{:S(2)}, u32[]{:S(2)}) %collective-permute-start.18) | collective-permute-done | bytes 131104 | tf_op jit(solution)/shard_map/ppermute | solution.py:72
  119.2 0.8 copy.51
  (129 shorter events, 13.2 us)
Async XLA Ops:
  0.0 98.3 %copy-start = (bf16[1024,1024]{1,0:T(8,128)(2,1)S(1)}, bf16[1024,1024]{1,0:T(8,128)(2,1)}, u32[]{:S(2)}) copy-start(bf16[1024,1024]{1,0:T(8,128)(2,1)} %param.43) | copy-start | bytes 6291460
  0.9 13.2 %collective-permute-start.1 = (bf16[64,256]{1,0:T(8,128)(2,1)S(1)}, bf16[64,256]{1,0:T(8,128)(2,1)S(1)}, u32[]{:S(2)}, u32[]{:S(2)}) collective-permute-start(bf16[64,256]{1,0:T(8,128)(2,1)S(1)} %get-tuple-element.231), channel_id=1, source_target_pairs={{4,0},{8,4},{12,8},{5,1},{9,5},{13,9},{6,2},{10,6},{14,10},{7,3},{... | collective-permute-start | bytes 98312 | tf_op jit(solution)/shard_map/ppermute | solution.py:21
  2.2 12.0 %collective-permute-start = (bf16[64,256]{1,0:T(8,128)(2,1)S(1)}, bf16[64,256]{1,0:T(8,128)(2,1)S(1)}, u32[]{:S(2)}, u32[]{:S(2)}) collective-permute-start(bf16[64,256]{1,0:T(8,128)(2,1)S(1)} %get-tuple-element.230), channel_id=1, source_target_pairs={{0,4},{4,8},{8,12},{1,5},{5,9},{9,13},{2,6},{6,10},{10,14},{3,7},{... | collective-permute-start | bytes 98312 | tf_op jit(solution)/shard_map/ppermute | solution.py:20
  16.1 11.7 %copy-start.2 = (bf16[1024]{0:T(1024)(128)(2,1)S(1)}, bf16[1024]{0:T(1024)(128)(2,1)}, u32[]{:S(2)}) copy-start(bf16[1024]{0:T(1024)(128)(2,1)} %param.36) | copy-start | bytes 6148
  16.1 11.7 %copy-start.4 = (s32[4,4]{1,0:T(4,128)S(1)}, s32[4,4]{1,0:T(4,128)}, u32[]{:S(2)}) copy-start(s32[4,4]{1,0:T(4,128)} %param.33) | copy-start | bytes 196
  16.5 7.8 %collective-permute-start.3 = (bf16[512,256]{0,1:T(8,128)(2,1)S(1)}, bf16[512,256]{0,1:T(8,128)(2,1)S(1)}, u32[]{:S(2)}, u32[]{:S(2)}) collective-permute-start(bf16[512,256]{0,1:T(8,128)(2,1)S(1)} %add_convert_fusion), channel_id=1, source_target_pairs={{0,2},{1,3},{2,0},{3,1},{4,6},{5,7},{6,4},{7,5},{8,10},{9,11},{10,... | collective-permute-start | bytes 786440 | tf_op jit(solution)/shard_map/ppermute | solution.py:97
  18.5 9.0 %collective-permute-start.2 = (bf16[512,256]{0,1:T(8,128)(2,1)S(1)}, bf16[512,256]{0,1:T(8,128)(2,1)S(1)}, u32[]{:S(2)}, u32[]{:S(2)}) collective-permute-start(bf16[512,256]{0,1:T(8,128)(2,1)S(1)} %add_convert_fusion), channel_id=1, source_target_pairs={{0,4},{4,8},{8,12},{12,0},{1,5},{5,9},{9,13},{13,1},{2,6},{6,10},{... | collective-permute-start | bytes 786440 | tf_op jit(solution)/shard_map/ppermute | solution.py:189
  27.5 6.5 %collective-permute-start.5 = (bf16[512,256]{0,1:T(8,128)(2,1)S(1)}, bf16[512,256]{0,1:T(8,128)(2,1)}, u32[]{:S(2)}, u32[]{:S(2)}) collective-permute-start(bf16[512,256]{0,1:T(8,128)(2,1)S(1)} %collective-permute-done.2), channel_id=1, source_target_pairs={{0,2},{1,3},{2,0},{3,1},{4,6},{5,7},{6,4},{7,5},{8,10},{9,11},{10,... | collective-permute-start | bytes 786440 | tf_op jit(solution)/shard_map/ppermute | solution.py:97
  27.9 7.2 %collective-permute-start.6 = (bf16[512,2,256]{0,2,1:T(8,128)(2,1)}, bf16[512,2,256]{0,2,1:T(8,128)(2,1)}, u32[]{:S(2)}, u32[]{:S(2)}) collective-permute-start(bf16[512,2,256]{0,2,1:T(8,128)(2,1)} %pad_maximum_fusion.6), channel_id=1, source_target_pairs={{0,1},{1,0},{2,3},{3,2},{4,5},{5,4},{6,7},{7,6},{8,9},{9,8},{10,11... | collective-permute-start | bytes 1572872 | tf_op jit(solution)/shard_map/ppermute | solution.py:97
  32.4 10.5 %collective-permute-start.4 = (bf16[512,256]{0,1:T(8,128)(2,1)S(1)}, bf16[512,256]{0,1:T(8,128)(2,1)S(1)}, u32[]{:S(2)}, u32[]{:S(2)}) collective-permute-start(bf16[512,256]{0,1:T(8,128)(2,1)S(1)} %collective-permute-done.2), channel_id=1, source_target_pairs={{0,4},{4,8},{8,12},{12,0},{1,5},{5,9},{9,13},{13,1},{2,6},{6,10},{... | collective-permute-start | bytes 786440 | tf_op jit(solution)/shard_map/ppermute | solution.py:189
  36.4 8.8 %copy-start.7 = (bf16[1024,256]{1,0:T(8,128)(2,1)S(1)}, bf16[1024,256]{1,0:T(8,128)(2,1)}, u32[]{:S(2)}) copy-start(bf16[1024,256]{1,0:T(8,128)(2,1)} %param.38) | copy-start | bytes 1572868
  43.0 9.7 %collective-permute-start.7 = (bf16[512,256]{0,1:T(8,128)(2,1)S(1)}, bf16[512,256]{0,1:T(8,128)(2,1)S(1)}, u32[]{:S(2)}, u32[]{:S(2)}) collective-permute-start(bf16[512,256]{0,1:T(8,128)(2,1)S(1)} %collective-permute-done.4), channel_id=1, source_target_pairs={{0,4},{4,8},{8,12},{12,0},{1,5},{5,9},{9,13},{13,1},{2,6},{6,10},{... | collective-permute-start | bytes 786440 | tf_op jit(solution)/shard_map/ppermute | solution.py:189
  43.0 7.9 %collective-permute-start.8 = (bf16[512,256]{0,1:T(8,128)(2,1)S(1)}, bf16[512,256]{0,1:T(8,128)(2,1)S(1)}, u32[]{:S(2)}, u32[]{:S(2)}) collective-permute-start(bf16[512,256]{0,1:T(8,128)(2,1)S(1)} %collective-permute-done.4), channel_id=1, source_target_pairs={{0,2},{1,3},{2,0},{3,1},{4,6},{5,7},{6,4},{7,5},{8,10},{9,11},{10,... | collective-permute-start | bytes 786440 | tf_op jit(solution)/shard_map/ppermute | solution.py:97
  44.8 1.0 copy-start.5
  45.9 1.0 copy-start.6
  50.2 2.0 %collective-permute-start.9 = (bf16[512,2,256]{0,2,1:T(8,128)(2,1)S(1)}, bf16[512,2,256]{0,2,1:T(8,128)(2,1)S(1)}, u32[]{:S(2)}, u32[]{:S(2)}) collective-permute-start(bf16[512,2,256]{0,2,1:T(8,128)(2,1)S(1)} %pad_maximum_fusion.7), channel_id=1, source_target_pairs={{0,1},{1,0},{2,3},{3,2},{4,5},{5,4},{6,7},{7,6},{8,9},{9,8},{10,11... | collective-permute-start | bytes 1572872 | tf_op jit(solution)/shard_map/ppermute | solution.py:97
  57.2 8.2 %collective-permute-start.10 = (bf16[512,256]{0,1:T(8,128)(2,1)S(1)}, bf16[512,256]{0,1:T(8,128)(2,1)S(1)}, u32[]{:S(2)}, u32[]{:S(2)}) collective-permute-start(bf16[512,256]{0,1:T(8,128)(2,1)S(1)} %collective-permute-done.7), channel_id=1, source_target_pairs={{0,2},{1,3},{2,0},{3,1},{4,6},{5,7},{6,4},{7,5},{8,10},{9,11},{10,... | collective-permute-start | bytes 786440 | tf_op jit(solution)/shard_map/ppermute | solution.py:97
  58.9 6.6 %collective-permute-start.11 = (bf16[512,2,256]{0,2,1:T(8,128)(2,1)S(1)}, bf16[512,2,256]{0,2,1:T(8,128)(2,1)S(1)}, u32[]{:S(2)}, u32[]{:S(2)}) collective-permute-start(bf16[512,2,256]{0,2,1:T(8,128)(2,1)S(1)} %pad_maximum_fusion.8), channel_id=1, source_target_pairs={{0,1},{1,0},{2,3},{3,2},{4,5},{5,4},{6,7},{7,6},{8,9},{9,8},{10,11... | collective-permute-start | bytes 1572872 | tf_op jit(solution)/shard_map/ppermute | solution.py:97
  67.6 3.0 %collective-permute-start.12 = (bf16[512,2,256]{0,2,1:T(8,128)(2,1)S(1)}, bf16[512,2,256]{0,2,1:T(8,128)(2,1)S(1)}, u32[]{:S(2)}, u32[]{:S(2)}) collective-permute-start(bf16[512,2,256]{0,2,1:T(8,128)(2,1)S(1)} %pad_maximum_fusion.9), channel_id=1, source_target_pairs={{0,1},{1,0},{2,3},{3,2},{4,5},{5,4},{6,7},{7,6},{8,9},{9,8},{10,11... | collective-permute-start | bytes 1572872 | tf_op jit(solution)/shard_map/ppermute | solution.py:97
  75.8 1.7 %collective-permute-start.13 = (bf16[256,2,256]{0,2,1:T(8,128)(2,1)S(1)}, bf16[256,2,256]{0,2,1:T(8,128)(2,1)S(1)}, u32[]{:S(2)}, u32[]{:S(2)}) collective-permute-start(bf16[256,2,256]{0,2,1:T(8,128)(2,1)S(1)} %fusion.137), channel_id=1, source_target_pairs={{0,1},{1,0},{2,3},{3,2},{4,5},{5,4},{6,7},{7,6},{8,9},{9,8},{10,11... | collective-permute-start | bytes 786440 | tf_op jit(solution)/shard_map/ppermute | solution.py:72
  76.7 1.6 %collective-permute-start.19 = (bf16[256,2,256]{0,2,1:T(8,128)(2,1)S(1)}, bf16[256,2,256]{0,2,1:T(8,128)(2,1)S(1)}, u32[]{:S(2)}, u32[]{:S(2)}) collective-permute-start(bf16[256,2,256]{0,2,1:T(8,128)(2,1)S(1)} %fusion.138), channel_id=1, source_target_pairs={{0,1},{1,0},{2,3},{3,2},{4,5},{5,4},{6,7},{7,6},{8,9},{9,8},{10,11... | collective-permute-start | bytes 786440 | tf_op jit(solution)/shard_map/ppermute | solution.py:72
  77.6 6.3 %collective-permute-start.14 = (bf16[256,256]{0,1:T(8,128)(2,1)S(1)}, bf16[256,256]{0,1:T(8,128)(2,1)S(1)}, u32[]{:S(2)}, u32[]{:S(2)}) collective-permute-start(bf16[256,256]{0,1:T(8,128)(2,1)S(1)} %fusion.157), channel_id=1, source_target_pairs={{0,2},{1,3},{2,0},{3,1},{4,6},{5,7},{6,4},{7,5},{8,10},{9,11},{10,... | collective-permute-start | bytes 393224 | tf_op jit(solution)/shard_map/ppermute | solution.py:72
  79.1 16.2 %copy-start.3 = (bf16[1024]{0:T(1024)(128)(2,1)S(1)}, bf16[1024]{0:T(1024)(128)(2,1)}, u32[]{:S(2)}) copy-start(bf16[1024]{0:T(1024)(128)(2,1)} %param.41) | copy-start | bytes 6148
  80.1 6.1 %collective-permute-start.20 = (bf16[256,256]{0,1:T(8,128)(2,1)S(1)}, bf16[256,256]{0,1:T(8,128)(2,1)S(1)}, u32[]{:S(2)}, u32[]{:S(2)}) collective-permute-start(bf16[256,256]{0,1:T(8,128)(2,1)S(1)} %fusion.159), channel_id=1, source_target_pairs={{0,2},{1,3},{2,0},{3,1},{4,6},{5,7},{6,4},{7,5},{8,10},{9,11},{10,... | collective-permute-start | bytes 393224 | tf_op jit(solution)/shard_map/ppermute | solution.py:72
  87.2 6.5 %collective-permute-start.21 = (bf16[256,256]{0,1:T(8,128)(2,1)S(1)}, bf16[256,256]{0,1:T(8,128)(2,1)S(1)}, u32[]{:S(2)}, u32[]{:S(2)}) collective-permute-start(bf16[256,256]{0,1:T(8,128)(2,1)S(1)} %get-tuple-element.225), channel_id=1, source_target_pairs={{0,2},{1,3},{2,0},{3,1},{4,6},{5,7},{6,4},{7,5},{8,10},{9,11},{10,... | collective-permute-start | bytes 393224 | tf_op jit(solution)/shard_map/ppermute | solution.py:86
  88.2 7.0 %collective-permute-start.15 = (bf16[256,256]{0,1:T(8,128)(2,1)S(1)}, bf16[256,256]{0,1:T(8,128)(2,1)S(1)}, u32[]{:S(2)}, u32[]{:S(2)}) collective-permute-start(bf16[256,256]{0,1:T(8,128)(2,1)S(1)} %get-tuple-element.224), channel_id=1, source_target_pairs={{0,2},{1,3},{2,0},{3,1},{4,6},{5,7},{6,4},{7,5},{8,10},{9,11},{10,... | collective-permute-start | bytes 393224 | tf_op jit(solution)/shard_map/ppermute | solution.py:86
  93.8 1.6 %collective-permute-start.22 = (bf16[256,2,256]{0,2,1:T(8,128)(2,1)S(1)}, bf16[256,2,256]{0,2,1:T(8,128)(2,1)S(1)}, u32[]{:S(2)}, u32[]{:S(2)}) collective-permute-start(bf16[256,2,256]{0,2,1:T(8,128)(2,1)S(1)} %pad_maximum_fusion.11), channel_id=1, source_target_pairs={{0,1},{1,0},{2,3},{3,2},{4,5},{5,4},{6,7},{7,6},{8,9},{9,8},{10,11... | collective-permute-start | bytes 786440 | tf_op jit(solution)/shard_map/ppermute | solution.py:86
  95.3 1.6 %collective-permute-start.16 = (bf16[256,2,256]{0,2,1:T(8,128)(2,1)S(1)}, bf16[256,2,256]{0,2,1:T(8,128)(2,1)S(1)}, u32[]{:S(2)}, u32[]{:S(2)}) collective-permute-start(bf16[256,2,256]{0,2,1:T(8,128)(2,1)S(1)} %pad_maximum_fusion.10), channel_id=1, source_target_pairs={{0,1},{1,0},{2,3},{3,2},{4,5},{5,4},{6,7},{7,6},{8,9},{9,8},{10,11... | collective-permute-start | bytes 786440 | tf_op jit(solution)/shard_map/ppermute | solution.py:86
  103.6 6.0 %collective-permute-start.23 = (bf16[256,2,256]{0,2,1:T(8,128)(2,1)S(1)}, bf16[256,2,256]{0,2,1:T(8,128)(2,1)S(1)}, u32[]{:S(2)}, u32[]{:S(2)}) collective-permute-start(bf16[256,2,256]{0,2,1:T(8,128)(2,1)S(1)} %fusion.140), channel_id=1, source_target_pairs={{0,1},{1,0},{2,3},{3,2},{4,5},{5,4},{6,7},{7,6},{8,9},{9,8},{10,11... | collective-permute-start | bytes 786440 | tf_op jit(solution)/shard_map/ppermute | solution.py:72
  108.0 3.2 %copy-start.1 = (f32[256,1024]{0,1:T(8,128)S(1)}, f32[256,1024]{0,1:T(8,128)}, u32[]{:S(2)}) copy-start(f32[256,1024]{0,1:T(8,128)} %fusion.99) | copy-start | bytes 3145732
  109.2 2.1 %collective-permute-start.17 = (bf16[256,2,256]{0,2,1:T(8,128)(2,1)S(1)}, bf16[256,2,256]{0,2,1:T(8,128)(2,1)S(1)}, u32[]{:S(2)}, u32[]{:S(2)}) collective-permute-start(bf16[256,2,256]{0,2,1:T(8,128)(2,1)S(1)} %fusion.139), channel_id=1, source_target_pairs={{0,1},{1,0},{2,3},{3,2},{4,5},{5,4},{6,7},{7,6},{8,9},{9,8},{10,11... | collective-permute-start | bytes 786440 | tf_op jit(solution)/shard_map/ppermute | solution.py:72
  110.7 6.4 %collective-permute-start.24 = (bf16[256,256]{0,1:T(8,128)(2,1)S(1)}, bf16[256,256]{0,1:T(8,128)(2,1)S(1)}, u32[]{:S(2)}, u32[]{:S(2)}) collective-permute-start(bf16[256,256]{0,1:T(8,128)(2,1)S(1)} %fusion.160), channel_id=1, source_target_pairs={{0,2},{1,3},{2,0},{3,1},{4,6},{5,7},{6,4},{7,5},{8,10},{9,11},{10,... | collective-permute-start | bytes 393224 | tf_op jit(solution)/shard_map/ppermute | solution.py:72
  111.3 7.8 %collective-permute-start.18 = (bf16[256,256]{0,1:T(8,128)(2,1)S(1)}, bf16[256,256]{0,1:T(8,128)(2,1)S(1)}, u32[]{:S(2)}, u32[]{:S(2)}) collective-permute-start(bf16[256,256]{0,1:T(8,128)(2,1)S(1)} %fusion.158), channel_id=1, source_target_pairs={{0,2},{1,3},{2,0},{3,1},{4,6},{5,7},{6,4},{7,5},{8,10},{9,11},{10,... | collective-permute-start | bytes 393224 | tf_op jit(solution)/shard_map/ppermute | solution.py:72

commit v11 on v10

--- a/solution.py
+++ b/solution.py
@@ -90,14 +90,14 @@
     return current.reshape(rows, head_total * width)
 
 
-def gather_levels(current, head_id, head_total, level_list):
-    for level in level_list:
+def gather_levels(current, head_id, head_total, level_list, by_rows=False, first_axis=0):
+    for done, level in enumerate(level_list, first_axis):
         bit = 1 << level
         mine = (head_id >> level) & 1
         got = lax.ppermute(current, "heads", [(i, i ^ bit) for i in range(head_total)])
         low = jnp.where(mine == 0, current, got)
         high = jnp.where(mine == 0, got, current)
-        current = jnp.stack([low, high], axis=current.ndim - 1)
+        current = jnp.stack([low, high], axis=done if by_rows else current.ndim - 1)
     return current
 
 
@@ -137,6 +137,8 @@
     up_weight,
     down_weight,
 ):
+    head_total = lax.axis_size("heads")
+    head_id = lax.axis_index("heads")
     row_count = voxel_feats.shape[0]
     local_width = voxel_feats.shape[1]
     face_rows = EDGE * EDGE
@@ -164,8 +166,6 @@
     upper_face = upper_face * upper_open.astype(jnp.float32)[:, None, None]
     conv_out = depthwise(brick_vals, lower_face, upper_face, conv_weight, conv_bias)
     stream = (voxel_feats.astype(jnp.float32) + conv_out).astype(jnp.bfloat16)
-    head_total = lax.axis_size("heads")
-    head_id = lax.axis_index("heads")
     head_count = local_width // HEAD_DIM
     brick_dev = lax.axis_index("bricks")
     dev_total = lax.axis_size("bricks")
@@ -183,8 +183,17 @@
     crossed = {}
     gathered = {}
     query_heads = None
+    weights = {"out": out_weight}
     for slot in range(dev_total + 2):
         made = []
+        if slot == dev_total - 1:
+            made.append((weights, "out"))
+        if slot == dev_total:
+            weights["out"] = gather_levels(
+                weights["out"], head_id, head_total, cross_levels, True
+            )
+        if slot == dev_total + 1:
+            made.append((weights, "out"))
         if 1 <= slot + 1 < dev_total:
             ringed[slot + 1] = lax.ppermute(ringed[slot], "bricks", ring)
             made.append((ringed, slot + 1))
@@ -216,11 +225,14 @@
             state = absorb_block(
                 state, query_heads, key_block, value_block, linked, head_count, brick_rows
             )
-        if slot < dev_total + 1:
+        if made:
             packed = lax.optimization_barrier((state, [table[key] for table, key in made]))
             state = packed[0]
             for (table, key), value in zip(made, packed[1]):
                 table[key] = value
+    out_weight_full = gather_levels(
+        weights["out"], head_id, head_total, chip_levels, True, len(cross_levels)
+    ).reshape(head_total * out_weight.shape[0], out_weight.shape[1])
     row_max, row_mass, weighted = state
     attended = (weighted / jnp.transpose(row_mass, (0, 2, 1))[:, :, :, None]).astype(jnp.bfloat16)
     attended = attended.reshape(row_count, local_width)
@@ -229,10 +241,12 @@
     outputs = []
     for chunk in range(chunk_count):
         rows = slice(chunk * chunk_rows, (chunk + 1) * chunk_rows)
-        partial_out = jnp.dot(attended[rows], out_weight, preferred_element_type=jnp.float32)
-        out_sum = scatter_heads(partial_out, head_id, head_total)
-        stream_two = (stream[rows].astype(jnp.float32) + out_sum).astype(jnp.bfloat16)
-        stream_two_full = gather_heads(stream_two, head_id, head_total)
+        attended_full = gather_heads(attended[rows], head_id, head_total)
+        projected = jnp.dot(attended_full, out_weight_full, preferred_element_type=jnp.float32)
+        stream_two_full = (gathered[0][rows].astype(jnp.float32) + projected).astype(jnp.bfloat16)
+        stream_two = lax.dynamic_slice_in_dim(
+            stream_two_full, head_id * local_width, local_width, 1
+        )
         normed_two = layer_norm(stream_two_full, gain_two).astype(jnp.bfloat16)
         hidden = jax.nn.gelu(
             jnp.dot(normed_two, up_weight, preferred_element_type=jnp.float32), approximate=True

time: 121 us -> 151 us (1.25)
  other arithmetic: 17.2 us -> 39.3 us
  local copies, waits for them, and re-layouts: 12.7 us -> 32.9 us
  waiting for transfers between devices: 40.8 us -> 29.1 us
  starting transfers between devices: 22.7 us -> 19.2 us
  matrix products: 22.1 us -> 24.3 us
    reshape x1 -> x4, local copies, waits for them, and re-layouts: 0.2 us -> 9.54 us  [shards(): gathered[slot - 1] = gather_levels(crossed[slot - 1], head_id, head_total...]
    another operation x4, local copies, waits for them, and re-layouts: 0.28 us -> 8.26 us  [gather_levels(): current = jnp.stack([low, high], axis=done if by_rows else current.ndim - 1)]
    ppermute x8 -> x4, waiting for transfers between devices: 11.5 us -> 5.24 us  [scatter_heads(): lax.ppermute(give.astype(jnp.bfloat16), 'heads', [(i, i ^ bit) for i in r...]
    another operation x16 -> x19, other arithmetic: 3.98 us -> 10.2 us  [gather_levels(): current = jnp.stack([low, high], axis=done if by_rows else current.ndim - 1)]
    dynamic_slice x0 -> x5, local copies, waits for them, and re-layouts: none -> 5.64 us  [the longest x4 4.38 us: scatter_heads(): keep = lax.dynamic_index_in_dim(current, mine, axis, keepdims=False)]
    another operation x5 -> x6, other arithmetic: 0.19 us -> 5.49 us  [gather_heads(): current = jnp.stack([low, high], axis=current.ndim - 1)]
    reduce_sum x6, other arithmetic: 1.78 us -> 6 us  [layer_norm(): spread = jnp.mean(center * center, axis=-1, keepdims=True)]
    ppermute x3, waiting for transfers between devices: 9.02 us -> 4.89 us  [shards(): ringed[slot + 1] = lax.ppermute(ringed[slot], 'bricks', ring)]
  transfers between devices with their start and end apart: 25 -> 23, of which waited for: 16 -> 10; matrix products, arithmetic and copies ran while one was open for 23% -> 37% of each run, Pallas kernels for 0% -> 0%
where the time goes in v11:
time: 151 us; the launch traced here: 149 us
  other arithmetic  39.3 us (26%)
  local copies, waits for them, and re-layouts  32.9 us (22%)
  waiting for transfers between devices  29.1 us (19%)
  matrix products  24.3 us (16%)
  starting transfers between devices  19.2 us (13%)
  between operations  4.63 us (3%)
    ppermute x10, waiting for transfers between devices, gather_levels(): lax.ppermute(current, 'heads', [(i, i ^ bit) for i in range(head_total)])  13.8 us
    another operation x19, other arithmetic, gather_levels(): current = jnp.stack([low, high], axis=done if by_rows else current.ndim - 1)  10.2 us
    reshape x4, local copies, waits for them, and re-layouts, shards(): gathered[slot - 1] = gather_levels(crossed[slot - 1], head_id, head_total...  9.54 us
    dot_general x2, matrix products, shards(): lowered = jnp.dot(hidden, down_weight, preferred_element_type=jnp.float32)  8.59 us
    another operation x4, local copies, waits for them, and re-layouts, gather_levels(): current = jnp.stack([low, high], axis=done if by_rows else current.ndim - 1)  8.26 us
    reduce_sum x6, other arithmetic, layer_norm(): spread = jnp.mean(center * center, axis=-1, keepdims=True)  6 us
    ppermute x10, starting transfers between devices, gather_levels(): lax.ppermute(current, 'heads', [(i, i ^ bit) for i in range(head_total)])  5.76 us
    ppermute x1, starting transfers between devices, extended_2(): before = lax.ppermute(last, axis, up)  5.56 us
  transfers between devices with their start and end apart: 23, of which 10 were waited for; matrix products, arithmetic and copies ran while one was open for 37% of the time, Pallas kernels for 0%

profile of v11, /device:TPU:0, one launch (start us, length us, event | category | flops | bytes accessed | tf_op | source)
XLA Modules:
  0.0 149.5 jit_solution(10956244250286723889)
XLA Ops:
  0.0 0.9 fusion.207
  0.9 1.3 collective-permute-start.1
  2.2 5.6 %collective-permute-start = (bf16[64,256]{1,0:T(8,128)(2,1)S(1)}, bf16[64,256]{1,0:T(8,128)(2,1)S(1)}, u32[]{:S(2)}, u32[]{:S(2)}) collective-permute-start(bf16[64,256]{1,0:T(8,128)(2,1)S(1)} %get-tuple-element.242), channel_id=1, source_target_pairs={{0,4},{4,8},{8,12},{1,5},{5,9},{9,13},{2,6},{6,10},{10,14},{3,7},{... | collective-permute-start | bytes 98312 | tf_op jit(solution)/shard_map/ppermute | solution.py:20
  7.8 1.0 fusion.208
  8.8 0.9 fusion.209
  9.7 1.4 fusion.211
  11.8 1.0 convert
  14.4 1.6 %fusion.111 = f32[1,8,8,8,256]{4,3,2,1,0:T(8,128)S(1)} fusion(f32[1,10,10,10,256]{4,3,2,1,0:T(8,128)S(1)} %select_maximum_fusion, f32[1,1,8,8,256]{4,3,2,1,0:T(8,128)S(1)} %multiply_bitcast_fusion, f32[1,8,8,8,256]{4,3,2,1,0:T(8,128)S(1)} %convert, f32[1,1,8,8,256]{4,3,2,1,0:T(8,128)S(1)} %multiply_bitcast_fusion.1, f32[256]{0:T(256)S(1)} %bitcast.458, ...), kind=kLoop, calls=%fused_computation.137 | loop fusion | flops 7208960 | bytes 13790208 | tf_op jit(solution)/shard_map/add | solution.py:51
  16.1 2.0 %collective-permute-start.3 = (bf16[512,256]{1,0:T(8,128)(2,1)S(1)}, bf16[512,256]{1,0:T(8,128)(2,1)S(1)}, u32[]{:S(2)}, u32[]{:S(2)}) collective-permute-start(bf16[512,256]{1,0:T(8,128)(2,1)S(1)} %fusion.145), channel_id=1, source_target_pairs={{0,2},{1,3},{2,0},{3,1},{4,6},{5,7},{6,4},{7,5},{8,10},{9,11},{10,... | collective-permute-start | bytes 786440 | tf_op jit(solution)/shard_map/ppermute | solution.py:97
  18.1 1.6 %collective-permute-start.2 = (bf16[512,256]{1,0:T(8,128)(2,1)S(1)}, bf16[512,256]{1,0:T(8,128)(2,1)S(1)}, u32[]{:S(2)}, u32[]{:S(2)}) collective-permute-start(bf16[512,256]{1,0:T(8,128)(2,1)S(1)} %fusion.145), channel_id=1, source_target_pairs={{0,4},{4,8},{8,12},{12,0},{1,5},{5,9},{9,13},{13,1},{2,6},{6,10},{... | collective-permute-start | bytes 786440 | tf_op jit(solution)/shard_map/ppermute | solution.py:198
  19.7 4.3 %collective-permute-done.3 = bf16[512,256]{1,0:T(8,128)(2,1)S(1)} collective-permute-done((bf16[512,256]{1,0:T(8,128)(2,1)S(1)}, bf16[512,256]{1,0:T(8,128)(2,1)S(1)}, u32[]{:S(2)}, u32[]{:S(2)}) %collective-permute-start.3) | collective-permute-done | bytes 262176 | tf_op jit(solution)/shard_map/ppermute | solution.py:97
  24.0 3.1 %collective-permute-done.2 = bf16[512,256]{1,0:T(8,128)(2,1)S(1)} collective-permute-done((bf16[512,256]{1,0:T(8,128)(2,1)S(1)}, bf16[512,256]{1,0:T(8,128)(2,1)S(1)}, u32[]{:S(2)}, u32[]{:S(2)}) %collective-permute-start.2) | collective-permute-done | bytes 262176 | tf_op jit(solution)/shard_map/ppermute | solution.py:198
  30.7 2.9 %collective-permute-done.5 = bf16[512,256]{1,0:T(8,128)(2,1)} collective-permute-done((bf16[512,256]{1,0:T(8,128)(2,1)S(1)}, bf16[512,256]{1,0:T(8,128)(2,1)}, u32[]{:S(2)}, u32[]{:S(2)}) %collective-permute-start.5) | collective-permute-done | bytes 262176 | tf_op jit(solution)/shard_map/ppermute | solution.py:97
  33.6 1.0 select_bitcast_fusion.21
  35.6 2.1 %copy.31 = bf16[512,2,2,256]{3,2,1,0:T(2,128)(2,1)} copy(bf16[512,2,2,256]{3,0,1,2:T(8,128)(2,1)S(1)} %pad_maximum_fusion.3) | data formatting | bytes 2097152 | tf_op jit(solution)/shard_map/stack | solution.py:100
  37.7 1.8 %reshape.457 = bf16[512,1024]{1,0:T(8,128)(2,1)S(1)} reshape(bf16[512,2,2,256]{3,2,1,0:T(2,128)(2,1)} %copy.31) | data formatting | bytes 2097152 | tf_op jit(solution)/shard_map/reshape | solution.py:206
  39.5 1.8 %collective-permute-done.4 = bf16[512,256]{1,0:T(8,128)(2,1)} collective-permute-done((bf16[512,256]{1,0:T(8,128)(2,1)S(1)}, bf16[512,256]{1,0:T(8,128)(2,1)}, u32[]{:S(2)}, u32[]{:S(2)}) %collective-permute-start.4) | collective-permute-done | bytes 262176 | tf_op jit(solution)/shard_map/ppermute | solution.py:198
  41.3 1.6 %collective-permute-start.8 = (bf16[512,256]{1,0:T(8,128)(2,1)}, bf16[512,256]{1,0:T(8,128)(2,1)S(1)}, u32[]{:S(2)}, u32[]{:S(2)}) collective-permute-start(bf16[512,256]{1,0:T(8,128)(2,1)} %collective-permute-done.4), channel_id=1, source_target_pairs={{0,2},{1,3},{2,0},{3,1},{4,6},{5,7},{6,4},{7,5},{8,10},{9,11},{10,... | collective-permute-start | bytes 786440 | tf_op jit(solution)/shard_map/ppermute | solution.py:97
  47.7 1.0 fusion.64
  48.9 0.9 multiply_add_fusion.1
  49.8 1.0 select_bitcast_fusion.19
  51.9 2.1 %copy.33 = bf16[512,2,2,256]{3,2,1,0:T(2,128)(2,1)} copy(bf16[512,2,2,256]{3,0,1,2:T(8,128)(2,1)S(1)} %pad_maximum_fusion.4) | data formatting | bytes 2097152 | tf_op jit(solution)/shard_map/stack | solution.py:100
  54.0 2.6 %reshape.462 = bf16[512,1024]{1,0:T(8,128)(2,1)} reshape(bf16[512,2,2,256]{3,2,1,0:T(2,128)(2,1)} %copy.33) | data formatting | bytes 2097152 | tf_op jit(solution)/shard_map/reshape | solution.py:206
  56.6 1.6 %convert_reduce_fusion.2 = f32[512]{0:T(512)S(1)} fusion(bf16[512,1024]{1,0:T(8,128)(2,1)} %reshape.462), kind=kLoop, calls=%fused_computation.29 | loop fusion | flops 1048064 | bytes 1050624 | tf_op jit(solution)/shard_map/reduce_sum | solution.py:28
  58.1 1.7 %fusion.26 = f32[512]{0:T(512)S(1)} fusion(bf16[512,1024]{1,0:T(8,128)(2,1)} %reshape.462, f32[512]{0:T(512)S(1)} %broadcast_multiply_fusion.2), kind=kLoop, calls=%fused_computation.50 | loop fusion | flops 2096640 | bytes 1052672 | tf_op jit(solution)/shard_map/reduce_sum | solution.py:29
  62.0 0.8 fusion.7
  62.9 1.0 fusion.61
  63.9 1.3 collective-permute-start.10
  65.2 0.9 multiply_add_fusion
  66.2 6.7 %collective-permute-done.10 = bf16[512,256]{1,0:T(8,128)(2,1)S(1)} collective-permute-done((bf16[512,256]{1,0:T(8,128)(2,1)}, bf16[512,256]{1,0:T(8,128)(2,1)S(1)}, u32[]{:S(2)}, u32[]{:S(2)}) %collective-permute-start.10) | collective-permute-done | bytes 262176 | tf_op jit(solution)/shard_map/ppermute | solution.py:97
  72.9 1.0 select_bitcast_fusion.17
  73.9 0.8 pad_maximum_fusion.13
  75.0 2.1 %copy.35 = bf16[512,2,2,256]{3,2,1,0:T(2,128)(2,1)} copy(bf16[512,2,2,256]{3,0,1,2:T(8,128)(2,1)S(1)} %pad_maximum_fusion.5) | data formatting | bytes 2097152 | tf_op jit(solution)/shard_map/stack | solution.py:100
  77.0 2.6 %reshape.466 = bf16[512,1024]{1,0:T(8,128)(2,1)} reshape(bf16[512,2,2,256]{3,2,1,0:T(2,128)(2,1)} %copy.35) | data formatting | bytes 2097152 | tf_op jit(solution)/shard_map/reshape | solution.py:206
  79.6 1.6 %convert_reduce_fusion.1 = f32[512]{0:T(512)S(1)} fusion(bf16[512,1024]{1,0:T(8,128)(2,1)} %reshape.466), kind=kLoop, calls=%fused_computation.27 | loop fusion | flops 1048064 | bytes 1050624 | tf_op jit(solution)/shard_map/reduce_sum | solution.py:28
  81.2 1.7 %fusion.23 = f32[512]{0:T(512)S(1)} fusion(bf16[512,1024]{1,0:T(8,128)(2,1)} %reshape.466, f32[512]{0:T(512)S(1)} %broadcast_multiply_fusion.1), kind=kLoop, calls=%fused_computation.47 | loop fusion | flops 2096640 | bytes 1052672 | tf_op jit(solution)/shard_map/reduce_sum | solution.py:29
  86.9 1.8 %fusion.67 = f32[1,512,4,64]{1,3,2,0:T(8,128)} fusion(bf16[512,4,64]{0,2,1:T(8,128)(2,1)S(1)} %bitcast.459, f32[4,512,512]{2,1,0:T(8,128)S(1)} %get-tuple-element.282, f32[4,512]{1,0:T(4,128)S(1)} %bitcast.428, pred[]{:T(512)} %bitcast.86, f32[1,512,4,64]{1,3,2,0:T(8,128)S(1)} %copy-done.14, f32[512,4]{0,1:T(4,128)S(1)} %get-tuple-element.206), kind=kOutput, calls=%fused_computation.90 | convolution fusion | flops 138674176 | bytes 5521409 | tf_op jit(solution)/shard_map/bhqk,khd->bqhd/dot_general | solution.py:118
  88.9 2.1 %copy.37 = bf16[512,2,2,256]{3,2,1,0:T(2,128)(2,1)} copy(bf16[512,2,2,256]{3,0,1,2:T(8,128)(2,1)S(1)} %pad_maximum_fusion.6) | data formatting | bytes 2097152 | tf_op jit(solution)/shard_map/stack | solution.py:100
  90.9 2.6 %reshape.470 = bf16[512,1024]{1,0:T(8,128)(2,1)} reshape(bf16[512,2,2,256]{3,2,1,0:T(2,128)(2,1)} %copy.37) | data formatting | bytes 2097152 | tf_op jit(solution)/shard_map/reshape | solution.py:206
  93.5 1.6 %convert_reduce_fusion = f32[512]{0:T(512)S(1)} fusion(bf16[512,1024]{1,0:T(8,128)(2,1)} %reshape.470), kind=kLoop, calls=%fused_computation.25 | loop fusion | flops 1048064 | bytes 1050624 | tf_op jit(solution)/shard_map/reduce_sum | solution.py:28
  95.1 1.6 %fusion.20 = f32[512]{0:T(512)S(1)} fusion(bf16[512,1024]{1,0:T(8,128)(2,1)} %reshape.470, f32[512]{0:T(512)S(1)} %broadcast_multiply_fusion), kind=kLoop, calls=%fused_computation.44 | loop fusion | flops 2096640 | bytes 1052672 | tf_op jit(solution)/shard_map/reduce_sum | solution.py:29
  100.0 1.3 select_bitcast_fusion.3
  101.3 1.1 pad_maximum_fusion.7
  102.4 1.0 fusion.70
  103.6 1.7 %collective-permute-start.19 = (bf16[256,256]{1,0:T(8,128)(2,1)S(1)}, bf16[256,256]{1,0:T(8,128)(2,1)}, u32[]{:S(2)}, u32[]{:S(2)}) collective-permute-start(bf16[256,256]{1,0:T(8,128)(2,1)S(1)} %copy.48), channel_id=1, source_target_pairs={{0,2},{1,3},{2,0},{3,1},{4,6},{5,7},{6,4},{7,5},{8,10},{9,11},{10,... | collective-permute-start | bytes 393224 | tf_op jit(solution)/shard_map/ppermute | solution.py:86
  105.9 4.2 %collective-permute-done.19 = bf16[256,256]{1,0:T(8,128)(2,1)} collective-permute-done((bf16[256,256]{1,0:T(8,128)(2,1)S(1)}, bf16[256,256]{1,0:T(8,128)(2,1)}, u32[]{:S(2)}, u32[]{:S(2)}) %collective-permute-start.19) | collective-permute-done | bytes 131104 | tf_op jit(solution)/shard_map/ppermute | solution.py:86
  110.1 1.0 select_bitcast_fusion.25
  112.1 0.9 select_bitcast_fusion.27
  114.7 1.1 select_bitcast_fusion.13
  116.3 1.0 select_bitcast_fusion.15
  117.4 1.4 select_bitcast_fusion.1
  121.8 4.4 %fusion.95 = f32[256,1024]{0,1:T(8,128)} fusion(bf16[1024,1024]{1,0:T(8,128)(2,1)S(1)} %copy-done, bf16[1024,1024]{1,0:T(8,128)(2,1)} %param.42, bf16[256,1024]{1,0:T(8,128)(2,1)} %copy-done.11, f32[256]{0:T(256)S(1)} %add_rsqrt_fusion.4, f32[256]{0:T(256)S(1)} %broadcast_multiply_fusion.4, f32[1024]{0:T(1024)S(1)} %convert_element_type.216), kind=kOutput, calls=%fused_computation.132 | convolution fusion | flops 1077411840 | bytes 5773312 | tf_op jit(solution)/shard_map/dot_general | solution.py:254
  126.2 4.2 %fusion.97 = f32[256,1024]{0,1:T(8,128)} fusion(bf16[1024,1024]{1,0:T(8,128)(2,1)S(1)} %copy-done, bf16[1024,1024]{1,0:T(8,128)(2,1)} %param.42, bf16[256,1024]{1,0:T(8,128)(2,1)S(1)} %copy-done.13, f32[1024]{0:T(1024)S(1)} %convert_element_type.216, f32[256]{0:T(256)S(1)} %add_rsqrt_fusion.5, f32[256]{0:T(256)S(1)} %broadcast_multiply_fusion.5), kind=kOutput, calls=%fused_computation.133 | convolution fusion | flops 1077411840 | bytes 5773312 | tf_op jit(solution)/shard_map/dot_general | solution.py:254
  130.4 1.3 constant_dynamic-slice_fusion.1
  132.7 1.1 constant_dynamic-slice_fusion
  134.0 1.9 %constant_dynamic-slice_fusion.2 = f32[256,2,1,256]{0,3,2,1:T(8,128)} fusion(f32[256,2,2,256]{0,3,2,1:T(8,128)} %bitcast.413, s32[]{:T(128)S(6)} %select_n.324), kind=kLoop, calls=%fused_computation.278 | loop fusion | bytes 1048580 | tf_op jit(solution)/shard_map/jit(dynamic_index_in_dim)/dynamic_slice | solution.py:70
  135.9 1.2 copy.45
  137.1 0.9 copy.62
  138.3 1.0 bitcast_add_fusion
  139.3 1.7 %collective-permute-start.22 = (bf16[256,256]{1,0:T(8,128)(2,1)S(1)}, bf16[256,256]{1,0:T(8,128)(2,1)S(1)}, u32[]{:S(2)}, u32[]{:S(2)}) collective-permute-start(bf16[256,256]{1,0:T(8,128)(2,1)S(1)} %fusion.174), channel_id=1, source_target_pairs={{0,2},{1,3},{2,0},{3,1},{4,6},{5,7},{6,4},{7,5},{8,10},{9,11},{10,... | collective-permute-start | bytes 393224 | tf_op jit(solution)/shard_map/ppermute | solution.py:72
  141.6 4.1 %collective-permute-done.22 = bf16[256,256]{1,0:T(8,128)(2,1)S(1)} collective-permute-done((bf16[256,256]{1,0:T(8,128)(2,1)S(1)}, bf16[256,256]{1,0:T(8,128)(2,1)S(1)}, u32[]{:S(2)}, u32[]{:S(2)}) %collective-permute-start.22) | collective-permute-done | bytes 131104 | tf_op jit(solution)/shard_map/ppermute | solution.py:72
  145.7 1.0 fusion.170
  146.7 1.1 collective-permute-done.18
  147.8 1.0 fusion.172
  (167 shorter events, 28.7 us)
Async XLA Ops:
  0.0 121.8 %copy-start = (bf16[1024,1024]{1,0:T(8,128)(2,1)S(1)}, bf16[1024,1024]{1,0:T(8,128)(2,1)}, u32[]{:S(2)}) copy-start(bf16[1024,1024]{1,0:T(8,128)(2,1)} %param.43) | copy-start | bytes 6291460
  0.9 13.1 %collective-permute-start.1 = (bf16[64,256]{1,0:T(8,128)(2,1)S(1)}, bf16[64,256]{1,0:T(8,128)(2,1)S(1)}, u32[]{:S(2)}, u32[]{:S(2)}) collective-permute-start(bf16[64,256]{1,0:T(8,128)(2,1)S(1)} %get-tuple-element.243), channel_id=1, source_target_pairs={{4,0},{8,4},{12,8},{5,1},{9,5},{13,9},{6,2},{10,6},{14,10},{7,3},{... | collective-permute-start | bytes 98312 | tf_op jit(solution)/shard_map/ppermute | solution.py:21
  2.2 11.9 %collective-permute-start = (bf16[64,256]{1,0:T(8,128)(2,1)S(1)}, bf16[64,256]{1,0:T(8,128)(2,1)S(1)}, u32[]{:S(2)}, u32[]{:S(2)}) collective-permute-start(bf16[64,256]{1,0:T(8,128)(2,1)S(1)} %get-tuple-element.242), channel_id=1, source_target_pairs={{0,4},{4,8},{8,12},{1,5},{5,9},{9,13},{2,6},{6,10},{10,14},{3,7},{... | collective-permute-start | bytes 98312 | tf_op jit(solution)/shard_map/ppermute | solution.py:20
  14.4 1.6 %copy-start.9 = (bf16[512,256]{1,0:T(8,128)(2,1)S(1)}, bf16[512,256]{1,0:T(8,128)(2,1)}, u32[]{:S(2)}) copy-start(bf16[512,256]{1,0:T(8,128)(2,1)} %param.31) | copy-start | bytes 786436
  16.0 11.5 %copy-start.17 = (bf16[1024]{0:T(1024)(128)(2,1)S(1)}, bf16[1024]{0:T(1024)(128)(2,1)}, u32[]{:S(2)}) copy-start(bf16[1024]{0:T(1024)(128)(2,1)} %param.36) | copy-start | bytes 6148
  16.0 11.5 %copy-start.19 = (s32[4,4]{1,0:T(4,128)S(1)}, s32[4,4]{1,0:T(4,128)}, u32[]{:S(2)}) copy-start(s32[4,4]{1,0:T(4,128)} %param.33) | copy-start | bytes 196
  16.1 7.8 %collective-permute-start.3 = (bf16[512,256]{1,0:T(8,128)(2,1)S(1)}, bf16[512,256]{1,0:T(8,128)(2,1)S(1)}, u32[]{:S(2)}, u32[]{:S(2)}) collective-permute-start(bf16[512,256]{1,0:T(8,128)(2,1)S(1)} %fusion.145), channel_id=1, source_target_pairs={{0,2},{1,3},{2,0},{3,1},{4,6},{5,7},{6,4},{7,5},{8,10},{9,11},{10,... | collective-permute-start | bytes 786440 | tf_op jit(solution)/shard_map/ppermute | solution.py:97
  18.1 9.0 %collective-permute-start.2 = (bf16[512,256]{1,0:T(8,128)(2,1)S(1)}, bf16[512,256]{1,0:T(8,128)(2,1)S(1)}, u32[]{:S(2)}, u32[]{:S(2)}) collective-permute-start(bf16[512,256]{1,0:T(8,128)(2,1)S(1)} %fusion.145), channel_id=1, source_target_pairs={{0,4},{4,8},{8,12},{12,0},{1,5},{5,9},{9,13},{13,1},{2,6},{6,10},{... | collective-permute-start | bytes 786440 | tf_op jit(solution)/shard_map/ppermute | solution.py:198
  27.1 6.5 %collective-permute-start.5 = (bf16[512,256]{1,0:T(8,128)(2,1)S(1)}, bf16[512,256]{1,0:T(8,128)(2,1)}, u32[]{:S(2)}, u32[]{:S(2)}) collective-permute-start(bf16[512,256]{1,0:T(8,128)(2,1)S(1)} %collective-permute-done.2), channel_id=1, source_target_pairs={{0,2},{1,3},{2,0},{3,1},{4,6},{5,7},{6,4},{7,5},{8,10},{9,11},{10,... | collective-permute-start | bytes 786440 | tf_op jit(solution)/shard_map/ppermute | solution.py:97
  27.5 7.9 %collective-permute-start.6 = (bf16[512,2,256]{2,0,1:T(8,128)(2,1)S(1)}, bf16[512,2,256]{2,0,1:T(8,128)(2,1)S(1)}, u32[]{:S(2)}, u32[]{:S(2)}) collective-permute-start(bf16[512,2,256]{2,0,1:T(8,128)(2,1)S(1)} %pad_maximum_fusion.10), channel_id=1, source_target_pairs={{0,1},{1,0},{2,3},{3,2},{4,5},{5,4},{6,7},{7,6},{8,9},{9,8},{10,11... | collective-permute-start | bytes 1572872 | tf_op jit(solution)/shard_map/ppermute | solution.py:97
  30.6 10.7 %collective-permute-start.4 = (bf16[512,256]{1,0:T(8,128)(2,1)S(1)}, bf16[512,256]{1,0:T(8,128)(2,1)}, u32[]{:S(2)}, u32[]{:S(2)}) collective-permute-start(bf16[512,256]{1,0:T(8,128)(2,1)S(1)} %collective-permute-done.2), channel_id=1, source_target_pairs={{0,4},{4,8},{8,12},{12,0},{1,5},{5,9},{9,13},{13,1},{2,6},{6,10},{... | collective-permute-start | bytes 786440 | tf_op jit(solution)/shard_map/ppermute | solution.py:198
  39.5 4.1 %copy-start.21 = (bf16[1024,256]{1,0:T(8,128)(2,1)S(1)}, bf16[1024,256]{1,0:T(8,128)(2,1)}, u32[]{:S(2)}) copy-start(bf16[1024,256]{1,0:T(8,128)(2,1)} %param.38) | copy-start | bytes 1572868
  41.3 15.3 %collective-permute-start.7 = (bf16[512,256]{1,0:T(8,128)(2,1)}, bf16[512,256]{1,0:T(8,128)(2,1)}, u32[]{:S(2)}, u32[]{:S(2)}) collective-permute-start(bf16[512,256]{1,0:T(8,128)(2,1)} %collective-permute-done.4), channel_id=1, source_target_pairs={{0,4},{4,8},{8,12},{12,0},{1,5},{5,9},{9,13},{13,1},{2,6},{6,10},{... | collective-permute-start | bytes 786440 | tf_op jit(solution)/shard_map/ppermute | solution.py:198
  41.3 8.5 %collective-permute-start.8 = (bf16[512,256]{1,0:T(8,128)(2,1)}, bf16[512,256]{1,0:T(8,128)(2,1)S(1)}, u32[]{:S(2)}, u32[]{:S(2)}) collective-permute-start(bf16[512,256]{1,0:T(8,128)(2,1)} %collective-permute-done.4), channel_id=1, source_target_pairs={{0,2},{1,3},{2,0},{3,1},{4,6},{5,7},{6,4},{7,5},{8,10},{9,11},{10,... | collective-permute-start | bytes 786440 | tf_op jit(solution)/shard_map/ppermute | solution.py:97
  43.2 1.2 copy-start.20
  44.3 1.0 copy-start.25
  47.7 1.0 copy-start.6
  48.8 2.9 %collective-permute-start.9 = (bf16[512,2,256]{2,0,1:T(8,128)(2,1)S(1)}, bf16[512,2,256]{2,0,1:T(8,128)(2,1)S(1)}, u32[]{:S(2)}, u32[]{:S(2)}) collective-permute-start(bf16[512,2,256]{2,0,1:T(8,128)(2,1)S(1)} %copy-done.6), channel_id=1, source_target_pairs={{0,1},{1,0},{2,3},{3,2},{4,5},{5,4},{6,7},{7,6},{8,9},{9,8},{10,11... | collective-permute-start | bytes 1572872 | tf_op jit(solution)/shard_map/ppermute | solution.py:97
  56.6 3.3 %copy-start.2 = (bf16[512,1024]{1,0:T(8,128)(2,1)S(1)}, bf16[512,1024]{1,0:T(8,128)(2,1)}, u32[]{:S(2)}) copy-start(bf16[512,1024]{1,0:T(8,128)(2,1)} %reshape.462) | copy-start | bytes 3145732
  56.6 3.3 %copy-start.22 = (bf16[1024,256]{1,0:T(8,128)(2,1)S(1)}, bf16[1024,256]{1,0:T(8,128)(2,1)}, u32[]{:S(2)}) copy-start(bf16[1024,256]{1,0:T(8,128)(2,1)} %param.38) | copy-start | bytes 1572868
  58.1 2.4 %copy-start.26 = (bf16[1024,256]{1,0:T(8,128)(2,1)S(1)}, bf16[1024,256]{1,0:T(8,128)(2,1)}, u32[]{:S(2)}) copy-start(bf16[1024,256]{1,0:T(8,128)(2,1)} %param.39) | copy-start | bytes 1572868
  62.9 2.3 %copy-start.7 = (bf16[512,2,256]{2,0,1:T(8,128)(2,1)S(1)}, bf16[512,2,256]{2,0,1:T(8,128)(2,1)}, u32[]{:S(2)}) copy-start(bf16[512,2,256]{2,0,1:T(8,128)(2,1)} %pad_maximum_fusion.12) | copy-start | bytes 1572868
  62.9 2.3 %copy-start.5 = (f32[1,512,4,64]{1,3,2,0:T(8,128)S(1)}, f32[1,512,4,64]{1,3,2,0:T(8,128)}, u32[]{:S(2)}) copy-start(f32[1,512,4,64]{1,3,2,0:T(8,128)} %multiply_add_fusion.1) | copy-start | bytes 1572868
  63.9 9.0 %collective-permute-start.10 = (bf16[512,256]{1,0:T(8,128)(2,1)}, bf16[512,256]{1,0:T(8,128)(2,1)S(1)}, u32[]{:S(2)}, u32[]{:S(2)}) collective-permute-start(bf16[512,256]{1,0:T(8,128)(2,1)} %collective-permute-done.7), channel_id=1, source_target_pairs={{0,2},{1,3},{2,0},{3,1},{4,6},{5,7},{6,4},{7,5},{8,10},{9,11},{10,... | collective-permute-start | bytes 786440 | tf_op jit(solution)/shard_map/ppermute | solution.py:97
  65.2 9.5 %collective-permute-start.11 = (bf16[512,2,256]{2,0,1:T(8,128)(2,1)S(1)}, bf16[512,2,256]{2,0,1:T(8,128)(2,1)S(1)}, u32[]{:S(2)}, u32[]{:S(2)}) collective-permute-start(bf16[512,2,256]{2,0,1:T(8,128)(2,1)S(1)} %copy-done.7), channel_id=1, source_target_pairs={{0,1},{1,0},{2,3},{3,2},{4,5},{5,4},{6,7},{7,6},{8,9},{9,8},{10,11... | collective-permute-start | bytes 1572872 | tf_op jit(solution)/shard_map/ppermute | solution.py:97
  79.6 3.3 %copy-start.3 = (bf16[512,1024]{1,0:T(8,128)(2,1)S(1)}, bf16[512,1024]{1,0:T(8,128)(2,1)}, u32[]{:S(2)}) copy-start(bf16[512,1024]{1,0:T(8,128)(2,1)} %reshape.466) | copy-start | bytes 3145732
  79.6 3.3 %copy-start.23 = (bf16[1024,256]{1,0:T(8,128)(2,1)S(1)}, bf16[1024,256]{1,0:T(8,128)(2,1)}, u32[]{:S(2)}) copy-start(bf16[1024,256]{1,0:T(8,128)(2,1)} %param.38) | copy-start | bytes 1572868
  81.2 2.4 %copy-start.27 = (bf16[1024,256]{1,0:T(8,128)(2,1)S(1)}, bf16[1024,256]{1,0:T(8,128)(2,1)}, u32[]{:S(2)}) copy-start(bf16[1024,256]{1,0:T(8,128)(2,1)} %param.39) | copy-start | bytes 1572868
  83.6 1.0 copy-start.8
  84.6 4.0 %collective-permute-start.12 = (bf16[512,2,256]{2,0,1:T(8,128)(2,1)S(1)}, bf16[512,2,256]{2,0,1:T(8,128)(2,1)S(1)}, u32[]{:S(2)}, u32[]{:S(2)}) collective-permute-start(bf16[512,2,256]{2,0,1:T(8,128)(2,1)S(1)} %copy-done.8), channel_id=1, source_target_pairs={{0,1},{1,0},{2,3},{3,2},{4,5},{5,4},{6,7},{7,6},{8,9},{9,8},{10,11... | collective-permute-start | bytes 1572872 | tf_op jit(solution)/shard_map/ppermute | solution.py:97
  84.7 15.3 %collective-permute-start.13 = (bf16[256,1024]{1,0:T(8,128)(2,1)}, bf16[256,1024]{1,0:T(8,128)(2,1)}, u32[]{:S(2)}, u32[]{:S(2)}) collective-permute-start(bf16[256,1024]{1,0:T(8,128)(2,1)} %param.40), channel_id=1, source_target_pairs={{0,2},{1,3},{2,0},{3,1},{4,6},{5,7},{6,4},{7,5},{8,10},{9,11},{10,... | collective-permute-start | bytes 1572872 | tf_op jit(solution)/shard_map/ppermute | solution.py:97
  85.8 1.0 copy-start.14
  93.5 3.2 %copy-start.1 = (bf16[512,1024]{1,0:T(8,128)(2,1)S(1)}, bf16[512,1024]{1,0:T(8,128)(2,1)}, u32[]{:S(2)}) copy-start(bf16[512,1024]{1,0:T(8,128)(2,1)} %reshape.470) | copy-start | bytes 3145732
  93.5 3.2 %copy-start.24 = (bf16[1024,256]{1,0:T(8,128)(2,1)S(1)}, bf16[1024,256]{1,0:T(8,128)(2,1)}, u32[]{:S(2)}) copy-start(bf16[1024,256]{1,0:T(8,128)(2,1)} %param.38) | copy-start | bytes 1572868
  98.2 1.0 copy-start.28
  100.0 2.4 %copy-start.29 = (f32[1,512,4,64]{1,3,2,0:T(8,128)S(1)}, f32[1,512,4,64]{1,3,2,0:T(8,128)}, u32[]{:S(2)}) copy-start(f32[1,512,4,64]{1,3,2,0:T(8,128)} %fusion.67) | copy-start | bytes 1572868
  103.4 11.2 %copy-start.18 = (bf16[1024]{0:T(1024)(128)(2,1)S(1)}, bf16[1024]{0:T(1024)(128)(2,1)}, u32[]{:S(2)}) copy-start(bf16[1024]{0:T(1024)(128)(2,1)} %param.41) | copy-start | bytes 6148
  103.6 2.3 %copy-start.16 = (bf16[256,256]{1,0:T(8,128)(2,1)}, bf16[256,256]{1,0:T(8,128)(2,1)S(1)}, u32[]{:S(2)}) copy-start(bf16[256,256]{1,0:T(8,128)(2,1)S(1)} %copy.48) | copy-start | bytes 393220
  103.6 6.4 %collective-permute-start.19 = (bf16[256,256]{1,0:T(8,128)(2,1)S(1)}, bf16[256,256]{1,0:T(8,128)(2,1)}, u32[]{:S(2)}, u32[]{:S(2)}) collective-permute-start(bf16[256,256]{1,0:T(8,128)(2,1)S(1)} %copy.48), channel_id=1, source_target_pairs={{0,2},{1,3},{2,0},{3,1},{4,6},{5,7},{6,4},{7,5},{8,10},{9,11},{10,... | collective-permute-start | bytes 393224 | tf_op jit(solution)/shard_map/ppermute | solution.py:86
  105.4 12.0 %collective-permute-start.16 = (bf16[2,256,1024]{2,1,0:T(8,128)(2,1)}, bf16[2,256,1024]{2,1,0:T(8,128)(2,1)}, u32[]{:S(2)}, u32[]{:S(2)}) collective-permute-start(bf16[2,256,1024]{2,1,0:T(8,128)(2,1)} %pad_maximum_fusion.7), channel_id=1, source_target_pairs={{0,1},{1,0},{2,3},{3,2},{4,5},{5,4},{6,7},{7,6},{8,9},{9,8},{10,11... | collective-permute-start | bytes 3145736 | tf_op jit(solution)/shard_map/ppermute | solution.py:97
  105.5 6.3 %copy-start.15 = (bf16[256,256]{1,0:T(8,128)(2,1)}, bf16[256,256]{1,0:T(8,128)(2,1)S(1)}, u32[]{:S(2)}) copy-start(bf16[256,256]{1,0:T(8,128)(2,1)S(1)} %copy.40) | copy-start | bytes 393220
  105.5 6.7 %collective-permute-start.14 = (bf16[256,256]{1,0:T(8,128)(2,1)S(1)}, bf16[256,256]{1,0:T(8,128)(2,1)S(1)}, u32[]{:S(2)}, u32[]{:S(2)}) collective-permute-start(bf16[256,256]{1,0:T(8,128)(2,1)S(1)} %copy.40), channel_id=1, source_target_pairs={{0,2},{1,3},{2,0},{3,1},{4,6},{5,7},{6,4},{7,5},{8,10},{9,11},{10,... | collective-permute-start | bytes 393224 | tf_op jit(solution)/shard_map/ppermute | solution.py:86
  111.8 2.9 %collective-permute-start.20 = (bf16[256,2,256]{2,0,1:T(8,128)(2,1)}, bf16[256,2,256]{2,0,1:T(8,128)(2,1)}, u32[]{:S(2)}, u32[]{:S(2)}) collective-permute-start(bf16[256,2,256]{2,0,1:T(8,128)(2,1)} %pad_maximum_fusion.20), channel_id=1, source_target_pairs={{0,1},{1,0},{2,3},{3,2},{4,5},{5,4},{6,7},{7,6},{8,9},{9,8},{10,11... | collective-permute-start | bytes 786440 | tf_op jit(solution)/shard_map/ppermute | solution.py:86
  113.1 0.6 copy-start.10
  114.5 1.9 %collective-permute-start.15 = (bf16[256,2,256]{2,0,1:T(8,128)(2,1)}, bf16[256,2,256]{2,0,1:T(8,128)(2,1)}, u32[]{:S(2)}, u32[]{:S(2)}) collective-permute-start(bf16[256,2,256]{2,0,1:T(8,128)(2,1)} %pad_maximum_fusion.19), channel_id=1, source_target_pairs={{0,1},{1,0},{2,3},{3,2},{4,5},{5,4},{6,7},{7,6},{8,9},{9,8},{10,11... | collective-permute-start | bytes 786440 | tf_op jit(solution)/shard_map/ppermute | solution.py:86
  114.7 2.7 %copy-start.4 = (bf16[2,256,1024]{2,1,0:T(8,128)(2,1)S(1)}, bf16[2,256,1024]{2,1,0:T(8,128)(2,1)}, u32[]{:S(2)}) copy-start(bf16[2,256,1024]{2,1,0:T(8,128)(2,1)} %pad_maximum_fusion.7) | copy-start | bytes 3145732
  119.6 1.1 copy-start.11
  120.7 0.8 copy-start.12
  121.8 4.4 %copy-start.13 = (bf16[256,1024]{1,0:T(8,128)(2,1)S(1)}, bf16[256,1024]{1,0:T(8,128)(2,1)}, u32[]{:S(2)}) copy-start(bf16[256,1024]{1,0:T(8,128)(2,1)} %copy-done.12) | copy-start | bytes 1572868
  132.5 5.8 %collective-permute-start.21 = (bf16[256,2,256]{2,0,1:T(8,128)(2,1)}, bf16[256,2,256]{2,0,1:T(8,128)(2,1)}, u32[]{:S(2)}, u32[]{:S(2)}) collective-permute-start(bf16[256,2,256]{2,0,1:T(8,128)(2,1)} %bitcast.376), channel_id=1, source_target_pairs={{0,1},{1,0},{2,3},{3,2},{4,5},{5,4},{6,7},{7,6},{8,9},{9,8},{10,11... | collective-permute-start | bytes 786440 | tf_op jit(solution)/shard_map/ppermute | solution.py:72
  138.0 3.1 %collective-permute-start.17 = (bf16[256,2,256]{2,0,1:T(8,128)(2,1)}, bf16[256,2,256]{2,0,1:T(8,128)(2,1)S(1)}, u32[]{:S(2)}, u32[]{:S(2)}) collective-permute-start(bf16[256,2,256]{2,0,1:T(8,128)(2,1)} %bitcast.422), channel_id=1, source_target_pairs={{0,1},{1,0},{2,3},{3,2},{4,5},{5,4},{6,7},{7,6},{8,9},{9,8},{10,11... | collective-permute-start | bytes 786440 | tf_op jit(solution)/shard_map/ppermute | solution.py:72
  139.3 6.4 %collective-permute-start.22 = (bf16[256,256]{1,0:T(8,128)(2,1)S(1)}, bf16[256,256]{1,0:T(8,128)(2,1)S(1)}, u32[]{:S(2)}, u32[]{:S(2)}) collective-permute-start(bf16[256,256]{1,0:T(8,128)(2,1)S(1)} %fusion.174), channel_id=1, source_target_pairs={{0,2},{1,3},{2,0},{3,1},{4,6},{5,7},{6,4},{7,5},{8,10},{9,11},{10,... | collective-permute-start | bytes 393224 | tf_op jit(solution)/shard_map/ppermute | solution.py:72
  141.2 6.6 %collective-permute-start.18 = (bf16[256,256]{1,0:T(8,128)(2,1)S(1)}, bf16[256,256]{1,0:T(8,128)(2,1)S(1)}, u32[]{:S(2)}, u32[]{:S(2)}) collective-permute-start(bf16[256,256]{1,0:T(8,128)(2,1)S(1)} %fusion.173), channel_id=1, source_target_pairs={{0,2},{1,3},{2,0},{3,1},{4,6},{5,7},{6,4},{7,5},{8,10},{9,11},{10,... | collective-permute-start | bytes 393224 | tf_op jit(solution)/shard_map/ppermute | solution.py:72

commit v12 on v11

--- a/solution.py
+++ b/solution.py
@@ -77,17 +77,8 @@
 
 
 def gather_heads(piece, head_id, head_total):
-    levels = level_count(head_total)
-    rows, width = piece.shape
-    current = piece
-    for level in reversed(range(levels)):
-        bit = 1 << level
-        mine = (head_id >> level) & 1
-        got = lax.ppermute(current, "heads", [(i, i ^ bit) for i in range(head_total)])
-        low = jnp.where(mine == 0, current, got)
-        high = jnp.where(mine == 0, got, current)
-        current = jnp.stack([low, high], axis=current.ndim - 1)
-    return current.reshape(rows, head_total * width)
+    order = list(reversed(range(level_count(head_total))))
+    return join_parts(gather_parts([piece], head_id, head_total, order), order)
 
 
 def gather_levels(current, head_id, head_total, level_list, by_rows=False, first_axis=0):
@@ -99,6 +90,28 @@
         high = jnp.where(mine == 0, got, current)
         current = jnp.stack([low, high], axis=done if by_rows else current.ndim - 1)
     return current
+
+
+def gather_parts(parts, head_id, head_total, level_list):
+    width = parts[0].shape[-1]
+    for level in level_list:
+        bit = 1 << level
+        mine = (head_id >> level) & 1
+        sent = parts[0] if len(parts) == 1 else jnp.concatenate(parts, axis=-1)
+        got = lax.ppermute(sent, "heads", [(i, i ^ bit) for i in range(head_total)])
+        got_parts = [got[..., k * width : (k + 1) * width] for k in range(len(parts))]
+        low = [jnp.where(mine == 0, a, b) for a, b in zip(parts, got_parts)]
+        high = [jnp.where(mine == 0, b, a) for a, b in zip(parts, got_parts)]
+        parts = low + high
+    return parts
+
+
+def join_parts(parts, level_order):
+    ordered = []
+    for head in range(len(parts)):
+        slot = sum(((head >> level) & 1) << t for t, level in enumerate(level_order))
+        ordered.append(parts[slot])
+    return ordered[0] if len(ordered) == 1 else jnp.concatenate(ordered, axis=-1)
 
 
 def absorb_block(state, query_heads, key_block, value_block, linked, head_count, brick_rows):
@@ -198,12 +211,13 @@
             ringed[slot + 1] = lax.ppermute(ringed[slot], "bricks", ring)
             made.append((ringed, slot + 1))
         if slot < dev_total:
-            crossed[slot] = gather_levels(ringed[slot], head_id, head_total, cross_levels)
+            crossed[slot] = gather_parts([ringed[slot]], head_id, head_total, cross_levels)
             made.append((crossed, slot))
         if 0 <= slot - 1 < dev_total:
-            gathered[slot - 1] = gather_levels(
-                crossed[slot - 1], head_id, head_total, chip_levels
-            ).reshape(row_count, head_total * local_width)
+            gathered[slot - 1] = join_parts(
+                gather_parts(crossed[slot - 1], head_id, head_total, chip_levels),
+                cross_levels + chip_levels,
+            )
             made.append((gathered, slot - 1))
         step = slot - 2
         if 0 <= step < dev_total:

time: 151 us -> 134 us (0.89)
  local copies, waits for them, and re-layouts: 32.9 us -> 14.9 us
  waiting for transfers between devices: 29.1 us -> 46 us
  other arithmetic: 39.3 us -> 24 us
    ppermute x4 -> x12, waiting for transfers between devices: 5.1 us -> 23.8 us  [gather_parts(): got = lax.ppermute(sent, 'heads', [(i, i ^ bit) for i in range(head_total)])]
    reshape x4 -> x0, local copies, waits for them, and re-layouts: 9.54 us -> none  [shards(): gathered[slot - 1] = gather_levels(crossed[slot - 1], head_id, head_total...]
    another operation x4 -> x0, local copies, waits for them, and re-layouts: 8.26 us -> none  [gather_levels(): current = jnp.stack([low, high], axis=done if by_rows else current.ndim - 1)]
    another operation x19 -> x4, other arithmetic: 10.2 us -> 3.01 us  [gather_levels(): current = jnp.stack([low, high], axis=done if by_rows else current.ndim - 1)]
    another operation x6 -> x0, other arithmetic: 5.49 us -> none  [gather_heads(): current = jnp.stack([low, high], axis=current.ndim - 1)]
    ppermute x4 -> x12, starting transfers between devices: 2.34 us -> 7.77 us  [gather_parts(): got = lax.ppermute(sent, 'heads', [(i, i ^ bit) for i in range(head_total)])]
    ppermute x10 -> x2, starting transfers between devices: 5.76 us -> 0.4 us  [gather_levels(): lax.ppermute(current, 'heads', [(i, i ^ bit) for i in range(head_total)])]
    ppermute x10 -> x2, waiting for transfers between devices: 13.8 us -> 9.81 us  [gather_levels(): lax.ppermute(current, 'heads', [(i, i ^ bit) for i in range(head_total)])]
  transfers between devices with their start and end apart: 23 -> 23, of which waited for: 10 -> 12; matrix products, arithmetic and copies ran while one was open for 37% -> 23% of each run, Pallas kernels for 0% -> 0%
where the time goes in v12:
time: 134 us; the launch traced here: 133 us
  waiting for transfers between devices  46 us (34%)
  other arithmetic  24 us (18%)
  matrix products  24 us (18%)
  starting transfers between devices  19.3 us (14%)
  local copies, waits for them, and re-layouts  14.9 us (11%)
  between operations  4.63 us (3%)
    ppermute x12, waiting for transfers between devices, gather_parts(): got = lax.ppermute(sent, 'heads', [(i, i ^ bit) for i in range(head_total)])  23.8 us
    ppermute x2, waiting for transfers between devices, gather_levels(): lax.ppermute(current, 'heads', [(i, i ^ bit) for i in range(head_total)])  9.81 us
    dot_general x2, matrix products, shards(): lowered = jnp.dot(hidden, down_weight, preferred_element_type=jnp.float32)  8.92 us
    ppermute x12, starting transfers between devices, gather_parts(): got = lax.ppermute(sent, 'heads', [(i, i ^ bit) for i in range(head_total)])  7.77 us
    ppermute x3, waiting for transfers between devices, shards(): ringed[slot + 1] = lax.ppermute(ringed[slot], 'bricks', ring)  7.1 us
    ppermute x1, starting transfers between devices, extended_2(): before = lax.ppermute(last, axis, up)  5.56 us
    ppermute x4, waiting for transfers between devices, scatter_heads(): lax.ppermute(give.astype(jnp.bfloat16), 'heads', [(i, i ^ bit) for i in r...  5.2 us
    dynamic_slice x4, local copies, waits for them, and re-layouts, scatter_heads(): keep = lax.dynamic_index_in_dim(current, mine, axis, keepdims=False)  4.4 us
  transfers between devices with their start and end apart: 23, of which 12 were waited for; matrix products, arithmetic and copies ran while one was open for 23% of the time, Pallas kernels for 0%

profile of v12, /device:TPU:0, one launch (start us, length us, event | category | flops | bytes accessed | tf_op | source)
XLA Modules:
  0.0 132.8 jit_solution(4669418021351660389)
XLA Ops:
  0.0 0.9 fusion.216
  0.9 1.3 collective-permute-start.1
  2.2 5.6 %collective-permute-start = (bf16[64,256]{1,0:T(8,128)(2,1)S(1)}, bf16[64,256]{1,0:T(8,128)(2,1)S(1)}, u32[]{:S(2)}, u32[]{:S(2)}) collective-permute-start(bf16[64,256]{1,0:T(8,128)(2,1)S(1)} %get-tuple-element.274), channel_id=1, source_target_pairs={{0,4},{4,8},{8,12},{1,5},{5,9},{9,13},{2,6},{6,10},{10,14},{3,7},{... | collective-permute-start | bytes 98312 | tf_op jit(solution)/shard_map/ppermute | solution.py:20
  7.8 1.0 fusion.217
  8.8 0.9 fusion.218
  9.7 1.4 %fusion.220 = (s32[1]{0:T(128)}, s32[1]{0:T(128)}) fusion(s32[4]{0:T(128)} %param.32, s32[]{:T(128)} %bitcast.2, s32[]{:T(128)} %bitcast.6), kind=kLoop, calls=%fused_computation.340 | loop fusion | bytes 24 | tf_op jit(solution)/shard_map/jit(_take)/gather | solution.py:172
  11.7 1.0 convert
  14.3 1.7 %fusion.108 = f32[1,8,8,8,256]{4,3,2,1,0:T(8,128)S(1)} fusion(f32[1,10,10,10,256]{4,3,2,1,0:T(8,128)S(1)} %select_maximum_fusion, f32[1,1,8,8,256]{4,3,2,1,0:T(8,128)S(1)} %multiply_bitcast_fusion, f32[1,8,8,8,256]{4,3,2,1,0:T(8,128)S(1)} %convert, f32[1,1,8,8,256]{4,3,2,1,0:T(8,128)S(1)} %multiply_bitcast_fusion.1, f32[256]{0:T(256)S(1)} %bitcast.397, ...), kind=kLoop, calls=%fused_computation.134 | loop fusion | flops 7208960 | bytes 13790208 | tf_op jit(solution)/shard_map/add | solution.py:51
  16.1 2.0 %collective-permute-start.3 = (bf16[512,256]{1,0:T(8,128)(2,1)S(1)}, bf16[512,256]{1,0:T(8,128)(2,1)S(1)}, u32[]{:S(2)}, u32[]{:S(2)}) collective-permute-start(bf16[512,256]{1,0:T(8,128)(2,1)S(1)} %fusion.157), channel_id=1, source_target_pairs={{0,2},{1,3},{2,0},{3,1},{4,6},{5,7},{6,4},{7,5},{8,10},{9,11},{10,... | collective-permute-start | bytes 786440 | tf_op jit(solution)/shard_map/ppermute | solution.py:101
  18.1 1.6 %collective-permute-start.2 = (bf16[512,256]{1,0:T(8,128)(2,1)S(1)}, bf16[512,256]{1,0:T(8,128)(2,1)S(1)}, u32[]{:S(2)}, u32[]{:S(2)}) collective-permute-start(bf16[512,256]{1,0:T(8,128)(2,1)S(1)} %fusion.157), channel_id=1, source_target_pairs={{0,4},{4,8},{8,12},{12,0},{1,5},{5,9},{9,13},{13,1},{2,6},{6,10},{... | collective-permute-start | bytes 786440 | tf_op jit(solution)/shard_map/ppermute | solution.py:211
  19.7 4.3 %collective-permute-done.3 = bf16[512,256]{1,0:T(8,128)(2,1)S(1)} collective-permute-done((bf16[512,256]{1,0:T(8,128)(2,1)S(1)}, bf16[512,256]{1,0:T(8,128)(2,1)S(1)}, u32[]{:S(2)}, u32[]{:S(2)}) %collective-permute-start.3) | collective-permute-done | bytes 262176 | tf_op jit(solution)/shard_map/ppermute | solution.py:101
  24.0 3.1 %collective-permute-done.2 = bf16[512,256]{1,0:T(8,128)(2,1)S(1)} collective-permute-done((bf16[512,256]{1,0:T(8,128)(2,1)S(1)}, bf16[512,256]{1,0:T(8,128)(2,1)S(1)}, u32[]{:S(2)}, u32[]{:S(2)}) %collective-permute-start.2) | collective-permute-done | bytes 262176 | tf_op jit(solution)/shard_map/ppermute | solution.py:211
  27.8 0.8 pad_maximum_fusion.8
  32.4 5.2 %collective-permute-done.5 = bf16[512,256]{1,0:T(8,128)(2,1)S(1)} collective-permute-done((bf16[512,256]{1,0:T(8,128)(2,1)}, bf16[512,256]{1,0:T(8,128)(2,1)S(1)}, u32[]{:S(2)}, u32[]{:S(2)}) %collective-permute-start.5) | collective-permute-done | bytes 262176 | tf_op jit(solution)/shard_map/ppermute | solution.py:101
  37.6 1.0 broadcast_select_fusion.20
  38.8 4.0 %collective-permute-done.4 = bf16[512,256]{1,0:T(8,128)(2,1)S(1)} collective-permute-done((bf16[512,256]{1,0:T(8,128)(2,1)}, bf16[512,256]{1,0:T(8,128)(2,1)S(1)}, u32[]{:S(2)}, u32[]{:S(2)}) %collective-permute-start.4) | collective-permute-done | bytes 262176 | tf_op jit(solution)/shard_map/ppermute | solution.py:211
  42.8 1.6 %collective-permute-start.8 = (bf16[512,256]{1,0:T(8,128)(2,1)S(1)}, bf16[512,256]{1,0:T(8,128)(2,1)S(1)}, u32[]{:S(2)}, u32[]{:S(2)}) collective-permute-start(bf16[512,256]{1,0:T(8,128)(2,1)S(1)} %collective-permute-done.4), channel_id=1, source_target_pairs={{0,2},{1,3},{2,0},{3,1},{4,6},{5,7},{6,4},{7,5},{8,10},{9,11},{10,... | collective-permute-start | bytes 786440 | tf_op jit(solution)/shard_map/ppermute | solution.py:101
  47.6 0.8 bitcast_reduce_fusion.3
  48.4 0.8 fusion.5
  49.3 1.0 fusion.64
  50.6 1.6 %collective-permute-done.9 = bf16[512,512]{1,0:T(8,128)(2,1)S(1)} collective-permute-done((bf16[512,512]{1,0:T(8,128)(2,1)S(1)}, bf16[512,512]{1,0:T(8,128)(2,1)S(1)}, u32[]{:S(2)}, u32[]{:S(2)}) %collective-permute-start.9) | collective-permute-done | bytes 524320 | tf_op jit(solution)/shard_map/ppermute | solution.py:101
  53.1 0.7 convolution_convert_fusion.5
  54.6 0.8 bitcast_reduce_fusion.2
  55.4 0.8 fusion.7
  56.2 1.0 fusion.61
  57.2 1.4 %collective-permute-start.10 = (bf16[512,256]{1,0:T(8,128)(2,1)S(1)}, bf16[512,256]{1,0:T(8,128)(2,1)S(1)}, u32[]{:S(2)}, u32[]{:S(2)}) collective-permute-start(bf16[512,256]{1,0:T(8,128)(2,1)S(1)} %collective-permute-done.7), channel_id=1, source_target_pairs={{0,2},{1,3},{2,0},{3,1},{4,6},{5,7},{6,4},{7,5},{8,10},{9,11},{10,... | collective-permute-start | bytes 786440 | tf_op jit(solution)/shard_map/ppermute | solution.py:101
  58.9 6.7 %collective-permute-done.10 = bf16[512,256]{1,0:T(8,128)(2,1)S(1)} collective-permute-done((bf16[512,256]{1,0:T(8,128)(2,1)S(1)}, bf16[512,256]{1,0:T(8,128)(2,1)S(1)}, u32[]{:S(2)}, u32[]{:S(2)}) %collective-permute-start.10) | collective-permute-done | bytes 262176 | tf_op jit(solution)/shard_map/ppermute | solution.py:101
  66.5 0.7 convolution_convert_fusion.3
  68.3 0.8 bitcast_reduce_fusion.1
  69.1 0.8 fusion.9
  70.0 1.0 fusion.58
  72.4 0.7 convolution_convert_fusion.1
  73.2 0.8 bitcast_reduce_fusion
  74.0 0.8 fusion.11
  74.8 0.7 convolution_convert_fusion
  75.6 9.8 %collective-permute-done.13 = bf16[256,1024]{1,0:T(8,128)(2,1)S(1)} collective-permute-done((bf16[256,1024]{1,0:T(8,128)(2,1)S(1)}, bf16[256,1024]{1,0:T(8,128)(2,1)S(1)}, u32[]{:S(2)}, u32[]{:S(2)}) %collective-permute-start.13) | collective-permute-done | bytes 524320 | tf_op jit(solution)/shard_map/ppermute | solution.py:88
  85.4 1.1 pad_maximum_fusion.5
  86.5 1.0 fusion.67
  88.0 1.6 %collective-permute-start.14 = (bf16[256,256]{0,1:T(8,128)(2,1)S(1)}, bf16[256,256]{0,1:T(8,128)(2,1)S(1)}, u32[]{:S(2)}, u32[]{:S(2)}) collective-permute-start(bf16[256,256]{0,1:T(8,128)(2,1)S(1)} %bitcast.355), channel_id=1, source_target_pairs={{0,2},{1,3},{2,0},{3,1},{4,6},{5,7},{6,4},{7,5},{8,10},{9,11},{10,... | collective-permute-start | bytes 393224 | tf_op jit(solution)/shard_map/ppermute | solution.py:101
  89.7 4.4 %collective-permute-done.19 = bf16[256,256]{0,1:T(8,128)(2,1)S(1)} collective-permute-done((bf16[256,256]{0,1:T(8,128)(2,1)S(1)}, bf16[256,256]{0,1:T(8,128)(2,1)S(1)}, u32[]{:S(2)}, u32[]{:S(2)}) %collective-permute-start.19) | collective-permute-done | bytes 131104 | tf_op jit(solution)/shard_map/ppermute | solution.py:101
  94.1 0.7 pad_maximum_fusion.13
  94.8 0.8 collective-permute-done.14
  97.0 1.0 broadcast_select_fusion.31
  98.0 0.8 collective-permute-done.15
  98.9 1.1 broadcast_select_fusion.35
  100.0 1.7 %select_bitcast_fusion.1 = (bf16[2,1,256,1024]{3,2,1,0:T(8,128)(2,1)S(1)}, bf16[2,1,256,1024]{3,2,1,0:T(8,128)(2,1)S(1)}) fusion(bf16[2,256,1024]{2,1,0:T(8,128)(2,1)} %pad_maximum_fusion.5, bf16[2,256,1024]{2,1,0:T(8,128)(2,1)} %collective-permute-done.16, pred[]{:T(512)S(6)} %eq.9), kind=kLoop, calls=%fused_computation.128 | loop fusion | flops 1048576 | bytes 4194305 | tf_op jit(solution)/shard_map/stack | solution.py:91
  101.9 0.8 convert_reduce_fusion.4
  103.0 0.8 convert_reduce_fusion.5
  103.8 0.8 copy-done.4
  104.9 4.5 %fusion.92 = f32[256,1024]{0,1:T(8,128)} fusion(bf16[1024,1024]{1,0:T(8,128)(2,1)S(1)} %copy-done, bf16[1024,1024]{1,0:T(8,128)(2,1)} %param.42, bf16[256,1024]{1,0:T(8,128)(2,1)} %copy-done.3, f32[256]{0:T(256)S(1)} %add_rsqrt_fusion.4, f32[256]{0:T(256)S(1)} %broadcast_multiply_fusion.4, f32[1024]{0:T(1024)S(1)} %convert_element_type.216), kind=kOutput, calls=%fused_computation.129 | convolution fusion | flops 1077411840 | bytes 5773312 | tf_op jit(solution)/shard_map/dot_general | solution.py:268
  109.4 4.5 %fusion.94 = f32[256,1024]{0,1:T(8,128)} fusion(bf16[1024,1024]{1,0:T(8,128)(2,1)S(1)} %copy-done, bf16[1024,1024]{1,0:T(8,128)(2,1)} %param.42, bf16[256,1024]{1,0:T(8,128)(2,1)S(1)} %copy-done.5, f32[1024]{0:T(1024)S(1)} %convert_element_type.216, f32[256]{0:T(256)S(1)} %add_rsqrt_fusion.5, f32[256]{0:T(256)S(1)} %broadcast_multiply_fusion.5), kind=kOutput, calls=%fused_computation.130 | convolution fusion | flops 1077411840 | bytes 5773312 | tf_op jit(solution)/shard_map/dot_general | solution.py:268
  113.8 1.3 constant_dynamic-slice_fusion.1
  115.1 0.8 copy.36
  116.1 1.1 constant_dynamic-slice_fusion
  117.4 1.9 %constant_dynamic-slice_fusion.2 = f32[256,2,1,256]{0,3,2,1:T(8,128)} fusion(f32[256,2,2,256]{0,3,2,1:T(8,128)} %bitcast.352, s32[]{:T(128)S(6)} %select_n.378), kind=kLoop, calls=%fused_computation.299 | loop fusion | bytes 1048580 | tf_op jit(solution)/shard_map/jit(dynamic_index_in_dim)/dynamic_slice | solution.py:70
  119.3 1.2 copy.24
  120.5 0.8 copy.35
  121.7 1.0 bitcast_add_fusion
  123.3 1.7 %collective-permute-start.18 = (bf16[256,256]{1,0:T(8,128)(2,1)S(1)}, bf16[256,256]{1,0:T(8,128)(2,1)S(1)}, u32[]{:S(2)}, u32[]{:S(2)}) collective-permute-start(bf16[256,256]{1,0:T(8,128)(2,1)S(1)} %fusion.182), channel_id=1, source_target_pairs={{0,2},{1,3},{2,0},{3,1},{4,6},{5,7},{6,4},{7,5},{8,10},{9,11},{10,... | collective-permute-start | bytes 393224 | tf_op jit(solution)/shard_map/ppermute | solution.py:72
  125.0 4.2 %collective-permute-done.22 = bf16[256,256]{1,0:T(8,128)(2,1)S(1)} collective-permute-done((bf16[256,256]{1,0:T(8,128)(2,1)S(1)}, bf16[256,256]{1,0:T(8,128)(2,1)S(1)}, u32[]{:S(2)}, u32[]{:S(2)}) %collective-permute-start.22) | collective-permute-done | bytes 131104 | tf_op jit(solution)/shard_map/ppermute | solution.py:72
  129.2 1.0 fusion.179
  130.1 1.0 collective-permute-done.18
  131.2 0.9 fusion.181
  132.1 0.7 pad_maximum_fusion.14
  (127 shorter events, 15.9 us)
Async XLA Ops:
  0.0 104.9 %copy-start = (bf16[1024,1024]{1,0:T(8,128)(2,1)S(1)}, bf16[1024,1024]{1,0:T(8,128)(2,1)}, u32[]{:S(2)}) copy-start(bf16[1024,1024]{1,0:T(8,128)(2,1)} %param.43) | copy-start | bytes 6291460
  0.9 13.1 %collective-permute-start.1 = (bf16[64,256]{1,0:T(8,128)(2,1)S(1)}, bf16[64,256]{1,0:T(8,128)(2,1)S(1)}, u32[]{:S(2)}, u32[]{:S(2)}) collective-permute-start(bf16[64,256]{1,0:T(8,128)(2,1)S(1)} %get-tuple-element.275), channel_id=1, source_target_pairs={{4,0},{8,4},{12,8},{5,1},{9,5},{13,9},{6,2},{10,6},{14,10},{7,3},{... | collective-permute-start | bytes 98312 | tf_op jit(solution)/shard_map/ppermute | solution.py:21
  2.2 11.8 %collective-permute-start = (bf16[64,256]{1,0:T(8,128)(2,1)S(1)}, bf16[64,256]{1,0:T(8,128)(2,1)S(1)}, u32[]{:S(2)}, u32[]{:S(2)}) collective-permute-start(bf16[64,256]{1,0:T(8,128)(2,1)S(1)} %get-tuple-element.274), channel_id=1, source_target_pairs={{0,4},{4,8},{8,12},{1,5},{5,9},{9,13},{2,6},{6,10},{10,14},{3,7},{... | collective-permute-start | bytes 98312 | tf_op jit(solution)/shard_map/ppermute | solution.py:20
  14.3 1.7 %copy-start.1 = (bf16[512,256]{1,0:T(8,128)(2,1)S(1)}, bf16[512,256]{1,0:T(8,128)(2,1)}, u32[]{:S(2)}) copy-start(bf16[512,256]{1,0:T(8,128)(2,1)} %param.31) | copy-start | bytes 786436
  16.0 13.0 %copy-start.8 = (bf16[1024]{0:T(1024)(128)(2,1)S(1)}, bf16[1024]{0:T(1024)(128)(2,1)}, u32[]{:S(2)}) copy-start(bf16[1024]{0:T(1024)(128)(2,1)} %param.36) | copy-start | bytes 6148
  16.0 13.0 %copy-start.10 = (s32[4,4]{1,0:T(4,128)S(1)}, s32[4,4]{1,0:T(4,128)}, u32[]{:S(2)}) copy-start(s32[4,4]{1,0:T(4,128)} %param.33) | copy-start | bytes 196
  16.1 7.8 %collective-permute-start.3 = (bf16[512,256]{1,0:T(8,128)(2,1)S(1)}, bf16[512,256]{1,0:T(8,128)(2,1)S(1)}, u32[]{:S(2)}, u32[]{:S(2)}) collective-permute-start(bf16[512,256]{1,0:T(8,128)(2,1)S(1)} %fusion.157), channel_id=1, source_target_pairs={{0,2},{1,3},{2,0},{3,1},{4,6},{5,7},{6,4},{7,5},{8,10},{9,11},{10,... | collective-permute-start | bytes 786440 | tf_op jit(solution)/shard_map/ppermute | solution.py:101
  18.1 9.0 %collective-permute-start.2 = (bf16[512,256]{1,0:T(8,128)(2,1)S(1)}, bf16[512,256]{1,0:T(8,128)(2,1)S(1)}, u32[]{:S(2)}, u32[]{:S(2)}) collective-permute-start(bf16[512,256]{1,0:T(8,128)(2,1)S(1)} %fusion.157), channel_id=1, source_target_pairs={{0,4},{4,8},{8,12},{12,0},{1,5},{5,9},{9,13},{13,1},{2,6},{6,10},{... | collective-permute-start | bytes 786440 | tf_op jit(solution)/shard_map/ppermute | solution.py:211
  27.1 0.7 copy-start.7
  28.7 9.9 %collective-permute-start.6 = (bf16[512,512]{1,0:T(8,128)(2,1)}, bf16[512,512]{1,0:T(8,128)(2,1)S(1)}, u32[]{:S(2)}, u32[]{:S(2)}) collective-permute-start(bf16[512,512]{1,0:T(8,128)(2,1)} %pad_maximum_fusion.8), channel_id=1, source_target_pairs={{0,1},{1,0},{2,3},{3,2},{4,5},{5,4},{6,7},{7,6},{8,9},{9,8},{10,11... | collective-permute-start | bytes 1572872 | tf_op jit(solution)/shard_map/ppermute | solution.py:101
  28.7 8.9 %collective-permute-start.5 = (bf16[512,256]{1,0:T(8,128)(2,1)}, bf16[512,256]{1,0:T(8,128)(2,1)S(1)}, u32[]{:S(2)}, u32[]{:S(2)}) collective-permute-start(bf16[512,256]{1,0:T(8,128)(2,1)} %copy-done.7), channel_id=1, source_target_pairs={{0,2},{1,3},{2,0},{3,1},{4,6},{5,7},{6,4},{7,5},{8,10},{9,11},{10,... | collective-permute-start | bytes 786440 | tf_op jit(solution)/shard_map/ppermute | solution.py:101
  32.3 10.5 %collective-permute-start.4 = (bf16[512,256]{1,0:T(8,128)(2,1)}, bf16[512,256]{1,0:T(8,128)(2,1)S(1)}, u32[]{:S(2)}, u32[]{:S(2)}) collective-permute-start(bf16[512,256]{1,0:T(8,128)(2,1)} %copy-done.7), channel_id=1, source_target_pairs={{0,4},{4,8},{8,12},{12,0},{1,5},{5,9},{9,13},{13,1},{2,6},{6,10},{... | collective-permute-start | bytes 786440 | tf_op jit(solution)/shard_map/ppermute | solution.py:211
  38.7 6.4 %copy-start.12 = (bf16[1024,256]{1,0:T(8,128)(2,1)S(1)}, bf16[1024,256]{1,0:T(8,128)(2,1)}, u32[]{:S(2)}) copy-start(bf16[1024,256]{1,0:T(8,128)(2,1)} %param.38) | copy-start | bytes 1572868
  42.8 9.7 %collective-permute-start.7 = (bf16[512,256]{1,0:T(8,128)(2,1)S(1)}, bf16[512,256]{1,0:T(8,128)(2,1)S(1)}, u32[]{:S(2)}, u32[]{:S(2)}) collective-permute-start(bf16[512,256]{1,0:T(8,128)(2,1)S(1)} %collective-permute-done.4), channel_id=1, source_target_pairs={{0,4},{4,8},{8,12},{12,0},{1,5},{5,9},{9,13},{13,1},{2,6},{6,10},{... | collective-permute-start | bytes 786440 | tf_op jit(solution)/shard_map/ppermute | solution.py:211
  42.8 7.7 %collective-permute-start.8 = (bf16[512,256]{1,0:T(8,128)(2,1)S(1)}, bf16[512,256]{1,0:T(8,128)(2,1)S(1)}, u32[]{:S(2)}, u32[]{:S(2)}) collective-permute-start(bf16[512,256]{1,0:T(8,128)(2,1)S(1)} %collective-permute-done.4), channel_id=1, source_target_pairs={{0,2},{1,3},{2,0},{3,1},{4,6},{5,7},{6,4},{7,5},{8,10},{9,11},{10,... | collective-permute-start | bytes 786440 | tf_op jit(solution)/shard_map/ppermute | solution.py:101
  44.7 1.2 copy-start.11
  45.8 1.0 copy-start.13
  50.3 2.0 %collective-permute-start.9 = (bf16[512,512]{1,0:T(8,128)(2,1)S(1)}, bf16[512,512]{1,0:T(8,128)(2,1)S(1)}, u32[]{:S(2)}, u32[]{:S(2)}) collective-permute-start(bf16[512,512]{1,0:T(8,128)(2,1)S(1)} %pad_maximum_fusion.9), channel_id=1, source_target_pairs={{0,1},{1,0},{2,3},{3,2},{4,5},{5,4},{6,7},{7,6},{8,9},{9,8},{10,11... | collective-permute-start | bytes 1572872 | tf_op jit(solution)/shard_map/ppermute | solution.py:101
  57.2 8.4 %collective-permute-start.10 = (bf16[512,256]{1,0:T(8,128)(2,1)S(1)}, bf16[512,256]{1,0:T(8,128)(2,1)S(1)}, u32[]{:S(2)}, u32[]{:S(2)}) collective-permute-start(bf16[512,256]{1,0:T(8,128)(2,1)S(1)} %collective-permute-done.7), channel_id=1, source_target_pairs={{0,2},{1,3},{2,0},{3,1},{4,6},{5,7},{6,4},{7,5},{8,10},{9,11},{10,... | collective-permute-start | bytes 786440 | tf_op jit(solution)/shard_map/ppermute | solution.py:101
  58.7 7.0 %collective-permute-start.11 = (bf16[512,512]{1,0:T(8,128)(2,1)S(1)}, bf16[512,512]{1,0:T(8,128)(2,1)S(1)}, u32[]{:S(2)}, u32[]{:S(2)}) collective-permute-start(bf16[512,512]{1,0:T(8,128)(2,1)S(1)} %pad_maximum_fusion.10), channel_id=1, source_target_pairs={{0,1},{1,0},{2,3},{3,2},{4,5},{5,4},{6,7},{7,6},{8,9},{9,8},{10,11... | collective-permute-start | bytes 1572872 | tf_op jit(solution)/shard_map/ppermute | solution.py:101
  68.3 3.3 %collective-permute-start.12 = (bf16[512,512]{1,0:T(8,128)(2,1)S(1)}, bf16[512,512]{1,0:T(8,128)(2,1)S(1)}, u32[]{:S(2)}, u32[]{:S(2)}) collective-permute-start(bf16[512,512]{1,0:T(8,128)(2,1)S(1)} %pad_maximum_fusion.11), channel_id=1, source_target_pairs={{0,1},{1,0},{2,3},{3,2},{4,5},{5,4},{6,7},{7,6},{8,9},{9,8},{10,11... | collective-permute-start | bytes 1572872 | tf_op jit(solution)/shard_map/ppermute | solution.py:101
  70.0 1.0 copy-start.6
  71.0 14.3 %collective-permute-start.13 = (bf16[256,1024]{1,0:T(8,128)(2,1)S(1)}, bf16[256,1024]{1,0:T(8,128)(2,1)S(1)}, u32[]{:S(2)}, u32[]{:S(2)}) collective-permute-start(bf16[256,1024]{1,0:T(8,128)(2,1)S(1)} %copy-done.6), channel_id=1, source_target_pairs={{0,2},{1,3},{2,0},{3,1},{4,6},{5,7},{6,4},{7,5},{8,10},{9,11},{10,... | collective-permute-start | bytes 1572872 | tf_op jit(solution)/shard_map/ppermute | solution.py:88
  87.5 9.5 %copy-start.9 = (bf16[1024]{0:T(1024)(128)(2,1)S(1)}, bf16[1024]{0:T(1024)(128)(2,1)}, u32[]{:S(2)}) copy-start(bf16[1024]{0:T(1024)(128)(2,1)} %param.41) | copy-start | bytes 6148
  87.6 6.5 %collective-permute-start.19 = (bf16[256,256]{0,1:T(8,128)(2,1)S(1)}, bf16[256,256]{0,1:T(8,128)(2,1)S(1)}, u32[]{:S(2)}, u32[]{:S(2)}) collective-permute-start(bf16[256,256]{0,1:T(8,128)(2,1)S(1)} %bitcast.356), channel_id=1, source_target_pairs={{0,2},{1,3},{2,0},{3,1},{4,6},{5,7},{6,4},{7,5},{8,10},{9,11},{10,... | collective-permute-start | bytes 393224 | tf_op jit(solution)/shard_map/ppermute | solution.py:101
  88.0 11.9 %collective-permute-start.16 = (bf16[2,256,1024]{2,1,0:T(8,128)(2,1)}, bf16[2,256,1024]{2,1,0:T(8,128)(2,1)}, u32[]{:S(2)}, u32[]{:S(2)}) collective-permute-start(bf16[2,256,1024]{2,1,0:T(8,128)(2,1)} %pad_maximum_fusion.5), channel_id=1, source_target_pairs={{0,1},{1,0},{2,3},{3,2},{4,5},{5,4},{6,7},{7,6},{8,9},{9,8},{10,11... | collective-permute-start | bytes 3145736 | tf_op jit(solution)/shard_map/ppermute | solution.py:88
  88.0 7.5 %collective-permute-start.14 = (bf16[256,256]{0,1:T(8,128)(2,1)S(1)}, bf16[256,256]{0,1:T(8,128)(2,1)S(1)}, u32[]{:S(2)}, u32[]{:S(2)}) collective-permute-start(bf16[256,256]{0,1:T(8,128)(2,1)S(1)} %bitcast.355), channel_id=1, source_target_pairs={{0,2},{1,3},{2,0},{3,1},{4,6},{5,7},{6,4},{7,5},{8,10},{9,11},{10,... | collective-permute-start | bytes 393224 | tf_op jit(solution)/shard_map/ppermute | solution.py:101
  94.8 2.2 %collective-permute-start.20 = (bf16[256,512]{0,1:T(8,128)(2,1)}, bf16[256,512]{0,1:T(8,128)(2,1)}, u32[]{:S(2)}, u32[]{:S(2)}) collective-permute-start(bf16[256,512]{0,1:T(8,128)(2,1)} %pad_maximum_fusion.13), channel_id=1, source_target_pairs={{0,1},{1,0},{2,3},{3,2},{4,5},{5,4},{6,7},{7,6},{8,9},{9,8},{10,11... | collective-permute-start | bytes 786440 | tf_op jit(solution)/shard_map/ppermute | solution.py:101
  95.6 0.7 copy-start.2
  97.0 1.9 %collective-permute-start.15 = (bf16[256,512]{0,1:T(8,128)(2,1)}, bf16[256,512]{0,1:T(8,128)(2,1)}, u32[]{:S(2)}, u32[]{:S(2)}) collective-permute-start(bf16[256,512]{0,1:T(8,128)(2,1)} %pad_maximum_fusion.12), channel_id=1, source_target_pairs={{0,1},{1,0},{2,3},{3,2},{4,5},{5,4},{6,7},{7,6},{8,9},{9,8},{10,11... | collective-permute-start | bytes 786440 | tf_op jit(solution)/shard_map/ppermute | solution.py:101
  102.7 1.1 copy-start.3
  103.8 0.8 copy-start.4
  104.9 4.5 %copy-start.5 = (bf16[256,1024]{1,0:T(8,128)(2,1)S(1)}, bf16[256,1024]{1,0:T(8,128)(2,1)}, u32[]{:S(2)}) copy-start(bf16[256,1024]{1,0:T(8,128)(2,1)} %copy-done.4) | copy-start | bytes 1572868
  115.9 5.8 %collective-permute-start.21 = (bf16[256,2,256]{2,0,1:T(8,128)(2,1)}, bf16[256,2,256]{2,0,1:T(8,128)(2,1)}, u32[]{:S(2)}, u32[]{:S(2)}) collective-permute-start(bf16[256,2,256]{2,0,1:T(8,128)(2,1)} %bitcast.311), channel_id=1, source_target_pairs={{0,1},{1,0},{2,3},{3,2},{4,5},{5,4},{6,7},{7,6},{8,9},{9,8},{10,11... | collective-permute-start | bytes 786440 | tf_op jit(solution)/shard_map/ppermute | solution.py:72
  121.3 1.9 %collective-permute-start.17 = (bf16[256,2,256]{2,0,1:T(8,128)(2,1)}, bf16[256,2,256]{2,0,1:T(8,128)(2,1)S(1)}, u32[]{:S(2)}, u32[]{:S(2)}) collective-permute-start(bf16[256,2,256]{2,0,1:T(8,128)(2,1)} %bitcast.361), channel_id=1, source_target_pairs={{0,1},{1,0},{2,3},{3,2},{4,5},{5,4},{6,7},{7,6},{8,9},{9,8},{10,11... | collective-permute-start | bytes 786440 | tf_op jit(solution)/shard_map/ppermute | solution.py:72
  122.8 6.4 %collective-permute-start.22 = (bf16[256,256]{1,0:T(8,128)(2,1)S(1)}, bf16[256,256]{1,0:T(8,128)(2,1)S(1)}, u32[]{:S(2)}, u32[]{:S(2)}) collective-permute-start(bf16[256,256]{1,0:T(8,128)(2,1)S(1)} %fusion.183), channel_id=1, source_target_pairs={{0,2},{1,3},{2,0},{3,1},{4,6},{5,7},{6,4},{7,5},{8,10},{9,11},{10,... | collective-permute-start | bytes 393224 | tf_op jit(solution)/shard_map/ppermute | solution.py:72
  123.3 7.9 %collective-permute-start.18 = (bf16[256,256]{1,0:T(8,128)(2,1)S(1)}, bf16[256,256]{1,0:T(8,128)(2,1)S(1)}, u32[]{:S(2)}, u32[]{:S(2)}) collective-permute-start(bf16[256,256]{1,0:T(8,128)(2,1)S(1)} %fusion.182), channel_id=1, source_target_pairs={{0,2},{1,3},{2,0},{3,1},{4,6},{5,7},{6,4},{7,5},{8,10},{9,11},{10,... | collective-permute-start | bytes 393224 | tf_op jit(solution)/shard_map/ppermute | solution.py:72

commit v13 on v12

--- a/solution.py
+++ b/solution.py
@@ -81,17 +81,6 @@
     return join_parts(gather_parts([piece], head_id, head_total, order), order)
 
 
-def gather_levels(current, head_id, head_total, level_list, by_rows=False, first_axis=0):
-    for done, level in enumerate(level_list, first_axis):
-        bit = 1 << level
-        mine = (head_id >> level) & 1
-        got = lax.ppermute(current, "heads", [(i, i ^ bit) for i in range(head_total)])
-        low = jnp.where(mine == 0, current, got)
-        high = jnp.where(mine == 0, got, current)
-        current = jnp.stack([low, high], axis=done if by_rows else current.ndim - 1)
-    return current
-
-
 def gather_parts(parts, head_id, head_total, level_list):
     width = parts[0].shape[-1]
     for level in level_list:
@@ -150,8 +139,6 @@
     up_weight,
     down_weight,
 ):
-    head_total = lax.axis_size("heads")
-    head_id = lax.axis_index("heads")
     row_count = voxel_feats.shape[0]
     local_width = voxel_feats.shape[1]
     face_rows = EDGE * EDGE
@@ -179,6 +166,8 @@
     upper_face = upper_face * upper_open.astype(jnp.float32)[:, None, None]
     conv_out = depthwise(brick_vals, lower_face, upper_face, conv_weight, conv_bias)
     stream = (voxel_feats.astype(jnp.float32) + conv_out).astype(jnp.bfloat16)
+    head_total = lax.axis_size("heads")
+    head_id = lax.axis_index("heads")
     head_count = local_width // HEAD_DIM
     brick_dev = lax.axis_index("bricks")
     dev_total = lax.axis_size("bricks")
@@ -196,17 +185,8 @@
     crossed = {}
     gathered = {}
     query_heads = None
-    weights = {"out": out_weight}
     for slot in range(dev_total + 2):
         made = []
-        if slot == dev_total - 1:
-            made.append((weights, "out"))
-        if slot == dev_total:
-            weights["out"] = gather_levels(
-                weights["out"], head_id, head_total, cross_levels, True
-            )
-        if slot == dev_total + 1:
-            made.append((weights, "out"))
         if 1 <= slot + 1 < dev_total:
             ringed[slot + 1] = lax.ppermute(ringed[slot], "bricks", ring)
             made.append((ringed, slot + 1))
@@ -239,14 +219,11 @@
             state = absorb_block(
                 state, query_heads, key_block, value_block, linked, head_count, brick_rows
             )
-        if made:
+        if slot < dev_total + 1:
             packed = lax.optimization_barrier((state, [table[key] for table, key in made]))
             state = packed[0]
             for (table, key), value in zip(made, packed[1]):
                 table[key] = value
-    out_weight_full = gather_levels(
-        weights["out"], head_id, head_total, chip_levels, True, len(cross_levels)
-    ).reshape(head_total * out_weight.shape[0], out_weight.shape[1])
     row_max, row_mass, weighted = state
     attended = (weighted / jnp.transpose(row_mass, (0, 2, 1))[:, :, :, None]).astype(jnp.bfloat16)
     attended = attended.reshape(row_count, local_width)
@@ -255,12 +232,10 @@
     outputs = []
     for chunk in range(chunk_count):
         rows = slice(chunk * chunk_rows, (chunk + 1) * chunk_rows)
-        attended_full = gather_heads(attended[rows], head_id, head_total)
-        projected = jnp.dot(attended_full, out_weight_full, preferred_element_type=jnp.float32)
-        stream_two_full = (gathered[0][rows].astype(jnp.float32) + projected).astype(jnp.bfloat16)
-        stream_two = lax.dynamic_slice_in_dim(
-            stream_two_full, head_id * local_width, local_width, 1
-        )
+        partial_out = jnp.dot(attended[rows], out_weight, preferred_element_type=jnp.float32)
+        out_sum = scatter_heads(partial_out, head_id, head_total)
+        stream_two = (stream[rows].astype(jnp.float32) + out_sum).astype(jnp.bfloat16)
+        stream_two_full = gather_heads(stream_two, head_id, head_total)
         normed_two = layer_norm(stream_two_full, gain_two).astype(jnp.bfloat16)
         hidden = jax.nn.gelu(
             jnp.dot(normed_two, up_weight, preferred_element_type=jnp.float32), approximate=True

time: 134 us -> 122 us (0.910)
  other arithmetic: 24 us -> 18.4 us
  waiting for transfers between devices: 46 us -> 41.6 us
  starting transfers between devices: 19.3 us -> 21.8 us
  local copies, waits for them, and re-layouts: 14.9 us -> 12.9 us
  matrix products: 24 us -> 22.4 us
    ppermute x2 -> x0, waiting for transfers between devices: 9.81 us -> none  [gather_levels(): lax.ppermute(current, 'heads', [(i, i ^ bit) for i in range(head_total)])]
    ppermute x4 -> x8, waiting for transfers between devices: 5.2 us -> 12.1 us  [scatter_heads(): lax.ppermute(give.astype(jnp.bfloat16), 'heads', [(i, i ^ bit) for i in r...]
    dynamic_slice x5 -> x0, local copies, waits for them, and re-layouts: 5.66 us -> none  [the longest x4 4.4 us: scatter_heads(): keep = lax.dynamic_index_in_dim(current, mine, axis, keepdims=False)]
    convert_element_type x2 -> x8, local copies, waits for them, and re-layouts: 0.05 us -> 4.03 us  [scatter_heads(): give.astype(jnp.bfloat16)]
    another operation x4 -> x0, other arithmetic: 3.01 us -> none  [gather_levels(): current = jnp.stack([low, high], axis=done if by_rows else current.ndim - 1)]
    unnamed x30 -> x17, local copies, waits for them, and re-layouts: 4.25 us -> 1.52 us
    ppermute x4 -> x8, starting transfers between devices: 2.67 us -> 5.29 us  [scatter_heads(): lax.ppermute(give.astype(jnp.bfloat16), 'heads', [(i, i ^ bit) for i in r...]
    convert_element_type x2, other arithmetic: 1.9 us -> 0.1 us  [shards(): (stream_two.astype(jnp.float32) + mixed).astype(jnp.bfloat16)]
  transfers between devices with their start and end apart: 23 -> 25, of which waited for: 12 -> 15; matrix products, arithmetic and copies ran while one was open for 23% -> 29% of each run, Pallas kernels for 0% -> 0%
where the time goes in v13:
time: 122 us; the launch traced here: 121 us
  waiting for transfers between devices  41.6 us (34%)
  matrix products  22.4 us (18%)
  starting transfers between devices  21.8 us (18%)
  other arithmetic  18.4 us (15%)
  local copies, waits for them, and re-layouts  12.9 us (11%)
  between operations  4.38 us (4%)
    ppermute x12, waiting for transfers between devices, gather_parts(): got = lax.ppermute(sent, 'heads', [(i, i ^ bit) for i in range(head_total)])  22.3 us
    ppermute x8, waiting for transfers between devices, scatter_heads(): lax.ppermute(give.astype(jnp.bfloat16), 'heads', [(i, i ^ bit) for i in r...  12.1 us
    dot_general x2, matrix products, shards(): lowered = jnp.dot(hidden, down_weight, preferred_element_type=jnp.float32)  8.61 us
    ppermute x12, starting transfers between devices, gather_parts(): got = lax.ppermute(sent, 'heads', [(i, i ^ bit) for i in range(head_total)])  8.07 us
    ppermute x3, waiting for transfers between devices, shards(): ringed[slot + 1] = lax.ppermute(ringed[slot], 'bricks', ring)  7.22 us
    ppermute x1, starting transfers between devices, extended_2(): before = lax.ppermute(last, axis, up)  5.56 us
    ppermute x8, starting transfers between devices, scatter_heads(): lax.ppermute(give.astype(jnp.bfloat16), 'heads', [(i, i ^ bit) for i in r...  5.29 us
    convert_element_type x8, local copies, waits for them, and re-layouts, scatter_heads(): give.astype(jnp.bfloat16)  4.03 us
  transfers between devices with their start and end apart: 25, of which 15 were waited for; matrix products, arithmetic and copies ran while one was open for 29% of the time, Pallas kernels for 0%

profile of v13, /device:TPU:0, one launch (start us, length us, event | category | flops | bytes accessed | tf_op | source)
XLA Modules:
  0.0 121.4 jit_solution(16021718817270055989)
XLA Ops:
  0.0 0.9 fusion.210
  0.9 1.3 %collective-permute-start.1 = (bf16[64,256]{1,0:T(8,128)(2,1)S(1)}, bf16[64,256]{1,0:T(8,128)(2,1)S(1)}, u32[]{:S(2)}, u32[]{:S(2)}) collective-permute-start(bf16[64,256]{1,0:T(8,128)(2,1)S(1)} %get-tuple-element.263), channel_id=1, source_target_pairs={{4,0},{8,4},{12,8},{5,1},{9,5},{13,9},{6,2},{10,6},{14,10},{7,3},{... | collective-permute-start | bytes 98312 | tf_op jit(solution)/shard_map/ppermute | solution.py:21
  2.2 5.6 %collective-permute-start = (bf16[64,256]{1,0:T(8,128)(2,1)S(1)}, bf16[64,256]{1,0:T(8,128)(2,1)S(1)}, u32[]{:S(2)}, u32[]{:S(2)}) collective-permute-start(bf16[64,256]{1,0:T(8,128)(2,1)S(1)} %get-tuple-element.262), channel_id=1, source_target_pairs={{0,4},{4,8},{8,12},{1,5},{5,9},{9,13},{2,6},{6,10},{10,14},{3,7},{... | collective-permute-start | bytes 98312 | tf_op jit(solution)/shard_map/ppermute | solution.py:20
  7.8 1.0 fusion.211
  8.8 0.9 fusion.212
  9.7 1.1 copy.29
  10.8 1.4 %fusion.214 = (s32[1]{0:T(128)}, s32[1]{0:T(128)}) fusion(s32[4]{0:T(128)} %param.32, s32[]{:T(128)} %bitcast.2, s32[]{:T(128)} %bitcast.6), kind=kLoop, calls=%fused_computation.331 | loop fusion | bytes 24 | tf_op jit(solution)/shard_map/jit(_take)/gather | solution.py:159
  13.5 0.7 convert_element_type.223
  14.5 1.7 %fusion.114 = f32[1,8,8,8,256]{4,3,2,1,0:T(8,128)S(1)} fusion(f32[1,10,10,10,256]{4,3,2,1,0:T(8,128)S(1)} %select_maximum_fusion, f32[1,1,8,8,256]{4,3,2,1,0:T(8,128)S(1)} %multiply_bitcast_fusion, f32[1,8,8,8,256]{4,3,2,1,0:T(8,128)S(1)} %bitcast.395, f32[1,1,8,8,256]{4,3,2,1,0:T(8,128)S(1)} %multiply_bitcast_fusion.1, f32[256]{0:T(256)S(1)} %bitcast.444, ...), kind=kLoop, calls=%fused_computation.130 | loop fusion | flops 7208960 | bytes 13790208 | tf_op jit(solution)/shard_map/add | solution.py:51
  16.5 2.0 %collective-permute-start.3 = (bf16[512,256]{0,1:T(8,128)(2,1)S(1)}, bf16[512,256]{0,1:T(8,128)(2,1)S(1)}, u32[]{:S(2)}, u32[]{:S(2)}) collective-permute-start(bf16[512,256]{0,1:T(8,128)(2,1)S(1)} %add_convert_fusion), channel_id=1, source_target_pairs={{0,2},{1,3},{2,0},{3,1},{4,6},{5,7},{6,4},{7,5},{8,10},{9,11},{10,... | collective-permute-start | bytes 786440 | tf_op jit(solution)/shard_map/ppermute | solution.py:90
  18.5 1.6 %collective-permute-start.2 = (bf16[512,256]{0,1:T(8,128)(2,1)S(1)}, bf16[512,256]{0,1:T(8,128)(2,1)}, u32[]{:S(2)}, u32[]{:S(2)}) collective-permute-start(bf16[512,256]{0,1:T(8,128)(2,1)S(1)} %add_convert_fusion), channel_id=1, source_target_pairs={{0,4},{4,8},{8,12},{12,0},{1,5},{5,9},{9,13},{13,1},{2,6},{6,10},{... | collective-permute-start | bytes 786440 | tf_op jit(solution)/shard_map/ppermute | solution.py:191
  20.1 4.3 %collective-permute-done.3 = bf16[512,256]{0,1:T(8,128)(2,1)S(1)} collective-permute-done((bf16[512,256]{0,1:T(8,128)(2,1)S(1)}, bf16[512,256]{0,1:T(8,128)(2,1)S(1)}, u32[]{:S(2)}, u32[]{:S(2)}) %collective-permute-start.3) | collective-permute-done | bytes 262176 | tf_op jit(solution)/shard_map/ppermute | solution.py:90
  24.4 3.2 %collective-permute-done.2 = bf16[512,256]{0,1:T(8,128)(2,1)} collective-permute-done((bf16[512,256]{0,1:T(8,128)(2,1)S(1)}, bf16[512,256]{0,1:T(8,128)(2,1)}, u32[]{:S(2)}, u32[]{:S(2)}) %collective-permute-start.2) | collective-permute-done | bytes 262176 | tf_op jit(solution)/shard_map/ppermute | solution.py:191
  27.6 0.8 pad_maximum_fusion.6
  28.8 0.7 fusion.213
  32.0 1.2 %copy.56 = bf16[1024,256]{1,0:T(8,128)(2,1)S(1)} copy(bf16[1024,256]{0,1:T(8,128)(2,1)} %bitcast.405) | data formatting | bytes 1048576 | tf_op jit(solution)/shard_map/dot_general | solution.py:235
  33.3 4.2 %collective-permute-done.5 = bf16[512,256]{0,1:T(8,128)(2,1)} collective-permute-done((bf16[512,256]{0,1:T(8,128)(2,1)}, bf16[512,256]{0,1:T(8,128)(2,1)}, u32[]{:S(2)}, u32[]{:S(2)}) %collective-permute-start.5) | collective-permute-done | bytes 262176 | tf_op jit(solution)/shard_map/ppermute | solution.py:90
  37.5 1.1 broadcast_select_fusion.20
  38.5 1.1 broadcast_select_fusion.15
  39.7 4.0 %collective-permute-done.4 = bf16[512,256]{0,1:T(8,128)(2,1)S(1)} collective-permute-done((bf16[512,256]{0,1:T(8,128)(2,1)}, bf16[512,256]{0,1:T(8,128)(2,1)S(1)}, u32[]{:S(2)}, u32[]{:S(2)}) %collective-permute-start.4) | collective-permute-done | bytes 262176 | tf_op jit(solution)/shard_map/ppermute | solution.py:191
  43.7 1.6 %collective-permute-start.8 = (bf16[512,256]{0,1:T(8,128)(2,1)S(1)}, bf16[512,256]{0,1:T(8,128)(2,1)S(1)}, u32[]{:S(2)}, u32[]{:S(2)}) collective-permute-start(bf16[512,256]{0,1:T(8,128)(2,1)S(1)} %collective-permute-done.4), channel_id=1, source_target_pairs={{0,2},{1,3},{2,0},{3,1},{4,6},{5,7},{6,4},{7,5},{8,10},{9,11},{10,... | collective-permute-start | bytes 786440 | tf_op jit(solution)/shard_map/ppermute | solution.py:90
  46.0 0.7 convolution_convert_fusion.8
  46.6 0.7 convolution_convert_fusion.7
  47.7 0.7 convolution_convert_fusion.6
  48.3 0.8 bitcast_reduce_fusion.3
  49.1 0.8 fusion.5
  50.0 1.0 fusion.64
  51.4 1.6 %collective-permute-done.9 = bf16[512,512]{0,1:T(8,128)(2,1)S(1)} collective-permute-done((bf16[512,512]{0,1:T(8,128)(2,1)S(1)}, bf16[512,512]{0,1:T(8,128)(2,1)S(1)}, u32[]{:S(2)}, u32[]{:S(2)}) %collective-permute-start.9) | collective-permute-done | bytes 524320 | tf_op jit(solution)/shard_map/ppermute | solution.py:90
  53.8 0.7 convolution_convert_fusion.5
  55.1 0.8 bitcast_reduce_fusion.2
  55.9 0.8 fusion.7
  56.7 1.0 fusion.61
  57.7 1.7 %collective-permute-start.10 = (bf16[512,256]{0,1:T(8,128)(2,1)S(1)}, bf16[512,256]{0,1:T(8,128)(2,1)S(1)}, u32[]{:S(2)}, u32[]{:S(2)}) collective-permute-start(bf16[512,256]{0,1:T(8,128)(2,1)S(1)} %collective-permute-done.7), channel_id=1, source_target_pairs={{0,2},{1,3},{2,0},{3,1},{4,6},{5,7},{6,4},{7,5},{8,10},{9,11},{10,... | collective-permute-start | bytes 786440 | tf_op jit(solution)/shard_map/ppermute | solution.py:90
  59.6 6.5 %collective-permute-done.10 = bf16[512,256]{0,1:T(8,128)(2,1)S(1)} collective-permute-done((bf16[512,256]{0,1:T(8,128)(2,1)S(1)}, bf16[512,256]{0,1:T(8,128)(2,1)S(1)}, u32[]{:S(2)}, u32[]{:S(2)}) %collective-permute-start.10) | collective-permute-done | bytes 262176 | tf_op jit(solution)/shard_map/ppermute | solution.py:90
  66.9 0.7 convolution_convert_fusion.3
  68.4 1.0 bitcast_reduce_fusion.1
  69.4 0.8 fusion.9
  70.2 1.0 fusion.58
  72.1 0.7 convolution_convert_fusion
  73.4 0.8 bitcast_reduce_fusion
  74.2 0.8 fusion.10
  75.1 1.0 fusion.95
  77.5 0.7 collective-permute-done.13
  79.0 0.9 bitcast_add_fusion.1
  79.8 1.0 fusion.182
  80.8 1.5 %collective-permute-start.20 = (bf16[256,256]{0,1:T(8,128)(2,1)S(1)}, bf16[256,256]{0,1:T(8,128)(2,1)S(1)}, u32[]{:S(2)}, u32[]{:S(2)}) collective-permute-start(bf16[256,256]{0,1:T(8,128)(2,1)S(1)} %fusion.182), channel_id=1, source_target_pairs={{0,2},{1,3},{2,0},{3,1},{4,6},{5,7},{6,4},{7,5},{8,10},{9,11},{10,... | collective-permute-start | bytes 393224 | tf_op jit(solution)/shard_map/ppermute | solution.py:72
  82.3 2.3 %collective-permute-done.14 = bf16[256,256]{0,1:T(8,128)(2,1)S(1)} collective-permute-done((bf16[256,256]{0,1:T(8,128)(2,1)S(1)}, bf16[256,256]{0,1:T(8,128)(2,1)S(1)}, u32[]{:S(2)}, u32[]{:S(2)}) %collective-permute-start.14) | collective-permute-done | bytes 131104 | tf_op jit(solution)/shard_map/ppermute | solution.py:72
  84.6 2.4 %collective-permute-done.20 = bf16[256,256]{0,1:T(8,128)(2,1)S(1)} collective-permute-done((bf16[256,256]{0,1:T(8,128)(2,1)S(1)}, bf16[256,256]{0,1:T(8,128)(2,1)S(1)}, u32[]{:S(2)}, u32[]{:S(2)}) %collective-permute-start.20) | collective-permute-done | bytes 131104 | tf_op jit(solution)/shard_map/ppermute | solution.py:72
  86.9 1.0 fusion.173
  88.0 0.9 collective-permute-start.21
  88.8 1.2 collective-permute-start.15
  90.0 4.4 %collective-permute-done.21 = bf16[256,256]{0,1:T(8,128)(2,1)S(1)} collective-permute-done((bf16[256,256]{0,1:T(8,128)(2,1)S(1)}, bf16[256,256]{0,1:T(8,128)(2,1)S(1)}, u32[]{:S(2)}, u32[]{:S(2)}) %collective-permute-start.21) | collective-permute-done | bytes 131104 | tf_op jit(solution)/shard_map/ppermute | solution.py:90
  94.6 1.3 %collective-permute-done.15 = bf16[256,256]{0,1:T(8,128)(2,1)S(1)} collective-permute-done((bf16[256,256]{0,1:T(8,128)(2,1)S(1)}, bf16[256,256]{0,1:T(8,128)(2,1)S(1)}, u32[]{:S(2)}, u32[]{:S(2)}) %collective-permute-start.15) | collective-permute-done | bytes 131104 | tf_op jit(solution)/shard_map/ppermute | solution.py:90
  95.9 0.7 pad_maximum_fusion.12
  97.1 4.3 %fusion.98 = f32[256,1024]{0,1:T(8,128)} fusion(bf16[1024,1024]{1,0:T(8,128)(2,1)S(1)} %copy-done, bf16[1024,1024]{1,0:T(8,128)(2,1)} %param.42, f32[256]{0:T(256)S(1)} %add_rsqrt_fusion.4, f32[256]{0:T(256)S(1)} %broadcast_multiply_fusion.4, f32[1024]{0:T(1024)S(1)} %convert_element_type.258, bf16[256,256]{0,1:T(8,128)(2,1)S(1)} %get-tuple-element.258, ...), kind=kOutput, calls=%fused_computation.125 | convolution fusion | flops 1079246848 | bytes 5773312 | tf_op jit(solution)/shard_map/dot_general | solution.py:243
  101.4 1.8 %fusion.165 = bf16[256,2,256]{0,2,1:T(8,128)(2,1)} fusion(f32[256,2,2,256]{0,3,2,1:T(8,128)} %bitcast.401, s32[]{:T(128)S(6)} %select_n.344), kind=kLoop, calls=%fused_computation.218 | loop fusion | bytes 524292 | tf_op jit(solution)/shard_map/convert_element_type | solution.py:73
  103.6 1.0 broadcast_select_fusion.35
  105.0 4.3 %fusion.100 = f32[256,1024]{0,1:T(8,128)} fusion(bf16[1024,1024]{1,0:T(8,128)(2,1)S(1)} %copy-done, bf16[1024,1024]{1,0:T(8,128)(2,1)} %param.42, f32[1024]{0:T(1024)S(1)} %convert_element_type.258, f32[256]{0:T(256)S(1)} %add_rsqrt_fusion.5, f32[256]{0:T(256)S(1)} %broadcast_multiply_fusion.5, bf16[256,256]{0,1:T(8,128)(2,1)S(1)} %get-tuple-element.250, ...), kind=kOutput, calls=%fused_computation.126 | convolution fusion | flops 1079246848 | bytes 5773312 | tf_op jit(solution)/shard_map/dot_general | solution.py:243
  109.4 1.2 fusion.164
  110.6 1.1 bitcast_add_fusion
  112.3 1.7 %collective-permute-start.18 = (bf16[256,256]{0,1:T(8,128)(2,1)S(1)}, bf16[256,256]{0,1:T(8,128)(2,1)S(1)}, u32[]{:S(2)}, u32[]{:S(2)}) collective-permute-start(bf16[256,256]{0,1:T(8,128)(2,1)S(1)} %fusion.181), channel_id=1, source_target_pairs={{0,2},{1,3},{2,0},{3,1},{4,6},{5,7},{6,4},{7,5},{8,10},{9,11},{10,... | collective-permute-start | bytes 393224 | tf_op jit(solution)/shard_map/ppermute | solution.py:72
  114.0 4.1 %collective-permute-done.24 = bf16[256,256]{0,1:T(8,128)(2,1)S(1)} collective-permute-done((bf16[256,256]{0,1:T(8,128)(2,1)S(1)}, bf16[256,256]{0,1:T(8,128)(2,1)S(1)}, u32[]{:S(2)}, u32[]{:S(2)}) %collective-permute-start.24) | collective-permute-done | bytes 131104 | tf_op jit(solution)/shard_map/ppermute | solution.py:72
  118.2 2.3 %collective-permute-done.18 = bf16[256,256]{0,1:T(8,128)(2,1)S(1)} collective-permute-done((bf16[256,256]{0,1:T(8,128)(2,1)S(1)}, bf16[256,256]{0,1:T(8,128)(2,1)S(1)}, u32[]{:S(2)}, u32[]{:S(2)}) %collective-permute-start.18) | collective-permute-done | bytes 131104 | tf_op jit(solution)/shard_map/ppermute | solution.py:72
  120.6 0.8 copy.45
  (122 shorter events, 11.7 us)
Async XLA Ops:
  0.0 97.1 %copy-start = (bf16[1024,1024]{1,0:T(8,128)(2,1)S(1)}, bf16[1024,1024]{1,0:T(8,128)(2,1)}, u32[]{:S(2)}) copy-start(bf16[1024,1024]{1,0:T(8,128)(2,1)} %param.43) | copy-start | bytes 6291460
  0.9 13.2 %collective-permute-start.1 = (bf16[64,256]{1,0:T(8,128)(2,1)S(1)}, bf16[64,256]{1,0:T(8,128)(2,1)S(1)}, u32[]{:S(2)}, u32[]{:S(2)}) collective-permute-start(bf16[64,256]{1,0:T(8,128)(2,1)S(1)} %get-tuple-element.263), channel_id=1, source_target_pairs={{4,0},{8,4},{12,8},{5,1},{9,5},{13,9},{6,2},{10,6},{14,10},{7,3},{... | collective-permute-start | bytes 98312 | tf_op jit(solution)/shard_map/ppermute | solution.py:21
  2.2 12.0 %collective-permute-start = (bf16[64,256]{1,0:T(8,128)(2,1)S(1)}, bf16[64,256]{1,0:T(8,128)(2,1)S(1)}, u32[]{:S(2)}, u32[]{:S(2)}) collective-permute-start(bf16[64,256]{1,0:T(8,128)(2,1)S(1)} %get-tuple-element.262), channel_id=1, source_target_pairs={{0,4},{4,8},{8,12},{1,5},{5,9},{9,13},{2,6},{6,10},{10,14},{3,7},{... | collective-permute-start | bytes 98312 | tf_op jit(solution)/shard_map/ppermute | solution.py:20
  16.1 12.7 %copy-start.2 = (bf16[1024]{0:T(1024)(128)(2,1)S(1)}, bf16[1024]{0:T(1024)(128)(2,1)}, u32[]{:S(2)}) copy-start(bf16[1024]{0:T(1024)(128)(2,1)} %param.36) | copy-start | bytes 6148
  16.1 12.7 %copy-start.4 = (s32[4,4]{1,0:T(4,128)S(1)}, s32[4,4]{1,0:T(4,128)}, u32[]{:S(2)}) copy-start(s32[4,4]{1,0:T(4,128)} %param.33) | copy-start | bytes 196
  16.5 7.8 %collective-permute-start.3 = (bf16[512,256]{0,1:T(8,128)(2,1)S(1)}, bf16[512,256]{0,1:T(8,128)(2,1)S(1)}, u32[]{:S(2)}, u32[]{:S(2)}) collective-permute-start(bf16[512,256]{0,1:T(8,128)(2,1)S(1)} %add_convert_fusion), channel_id=1, source_target_pairs={{0,2},{1,3},{2,0},{3,1},{4,6},{5,7},{6,4},{7,5},{8,10},{9,11},{10,... | collective-permute-start | bytes 786440 | tf_op jit(solution)/shard_map/ppermute | solution.py:90
  18.5 9.1 %collective-permute-start.2 = (bf16[512,256]{0,1:T(8,128)(2,1)S(1)}, bf16[512,256]{0,1:T(8,128)(2,1)}, u32[]{:S(2)}, u32[]{:S(2)}) collective-permute-start(bf16[512,256]{0,1:T(8,128)(2,1)S(1)} %add_convert_fusion), channel_id=1, source_target_pairs={{0,4},{4,8},{8,12},{12,0},{1,5},{5,9},{9,13},{13,1},{2,6},{6,10},{... | collective-permute-start | bytes 786440 | tf_op jit(solution)/shard_map/ppermute | solution.py:191
  28.4 10.1 %collective-permute-start.6 = (bf16[512,512]{0,1:T(8,128)(2,1)}, bf16[512,512]{0,1:T(8,128)(2,1)}, u32[]{:S(2)}, u32[]{:S(2)}) collective-permute-start(bf16[512,512]{0,1:T(8,128)(2,1)} %pad_maximum_fusion.6), channel_id=1, source_target_pairs={{0,1},{1,0},{2,3},{3,2},{4,5},{5,4},{6,7},{7,6},{8,9},{9,8},{10,11... | collective-permute-start | bytes 1572872 | tf_op jit(solution)/shard_map/ppermute | solution.py:90
  28.4 9.0 %collective-permute-start.5 = (bf16[512,256]{0,1:T(8,128)(2,1)}, bf16[512,256]{0,1:T(8,128)(2,1)}, u32[]{:S(2)}, u32[]{:S(2)}) collective-permute-start(bf16[512,256]{0,1:T(8,128)(2,1)} %collective-permute-done.2), channel_id=1, source_target_pairs={{0,2},{1,3},{2,0},{3,1},{4,6},{5,7},{6,4},{7,5},{8,10},{9,11},{10,... | collective-permute-start | bytes 786440 | tf_op jit(solution)/shard_map/ppermute | solution.py:90
  33.2 10.5 %collective-permute-start.4 = (bf16[512,256]{0,1:T(8,128)(2,1)}, bf16[512,256]{0,1:T(8,128)(2,1)S(1)}, u32[]{:S(2)}, u32[]{:S(2)}) collective-permute-start(bf16[512,256]{0,1:T(8,128)(2,1)} %collective-permute-done.2), channel_id=1, source_target_pairs={{0,4},{4,8},{8,12},{12,0},{1,5},{5,9},{9,13},{13,1},{2,6},{6,10},{... | collective-permute-start | bytes 786440 | tf_op jit(solution)/shard_map/ppermute | solution.py:191
  39.6 6.3 %copy-start.7 = (bf16[1024,256]{1,0:T(8,128)(2,1)S(1)}, bf16[1024,256]{1,0:T(8,128)(2,1)}, u32[]{:S(2)}) copy-start(bf16[1024,256]{1,0:T(8,128)(2,1)} %param.38) | copy-start | bytes 1572868
  43.7 9.5 %collective-permute-start.7 = (bf16[512,256]{0,1:T(8,128)(2,1)S(1)}, bf16[512,256]{0,1:T(8,128)(2,1)S(1)}, u32[]{:S(2)}, u32[]{:S(2)}) collective-permute-start(bf16[512,256]{0,1:T(8,128)(2,1)S(1)} %collective-permute-done.4), channel_id=1, source_target_pairs={{0,4},{4,8},{8,12},{12,0},{1,5},{5,9},{9,13},{13,1},{2,6},{6,10},{... | collective-permute-start | bytes 786440 | tf_op jit(solution)/shard_map/ppermute | solution.py:191
  43.7 7.6 %collective-permute-start.8 = (bf16[512,256]{0,1:T(8,128)(2,1)S(1)}, bf16[512,256]{0,1:T(8,128)(2,1)S(1)}, u32[]{:S(2)}, u32[]{:S(2)}) collective-permute-start(bf16[512,256]{0,1:T(8,128)(2,1)S(1)} %collective-permute-done.4), channel_id=1, source_target_pairs={{0,2},{1,3},{2,0},{3,1},{4,6},{5,7},{6,4},{7,5},{8,10},{9,11},{10,... | collective-permute-start | bytes 786440 | tf_op jit(solution)/shard_map/ppermute | solution.py:90
  45.6 1.0 copy-start.5
  46.6 1.0 copy-start.6
  51.0 2.0 %collective-permute-start.9 = (bf16[512,512]{0,1:T(8,128)(2,1)S(1)}, bf16[512,512]{0,1:T(8,128)(2,1)S(1)}, u32[]{:S(2)}, u32[]{:S(2)}) collective-permute-start(bf16[512,512]{0,1:T(8,128)(2,1)S(1)} %pad_maximum_fusion.7), channel_id=1, source_target_pairs={{0,1},{1,0},{2,3},{3,2},{4,5},{5,4},{6,7},{7,6},{8,9},{9,8},{10,11... | collective-permute-start | bytes 1572872 | tf_op jit(solution)/shard_map/ppermute | solution.py:90
  57.7 8.4 %collective-permute-start.10 = (bf16[512,256]{0,1:T(8,128)(2,1)S(1)}, bf16[512,256]{0,1:T(8,128)(2,1)S(1)}, u32[]{:S(2)}, u32[]{:S(2)}) collective-permute-start(bf16[512,256]{0,1:T(8,128)(2,1)S(1)} %collective-permute-done.7), channel_id=1, source_target_pairs={{0,2},{1,3},{2,0},{3,1},{4,6},{5,7},{6,4},{7,5},{8,10},{9,11},{10,... | collective-permute-start | bytes 786440 | tf_op jit(solution)/shard_map/ppermute | solution.py:90
  59.4 6.8 %collective-permute-start.11 = (bf16[512,512]{0,1:T(8,128)(2,1)S(1)}, bf16[512,512]{0,1:T(8,128)(2,1)S(1)}, u32[]{:S(2)}, u32[]{:S(2)}) collective-permute-start(bf16[512,512]{0,1:T(8,128)(2,1)S(1)} %pad_maximum_fusion.8), channel_id=1, source_target_pairs={{0,1},{1,0},{2,3},{3,2},{4,5},{5,4},{6,7},{7,6},{8,9},{9,8},{10,11... | collective-permute-start | bytes 1572872 | tf_op jit(solution)/shard_map/ppermute | solution.py:90
  68.3 3.1 %collective-permute-start.12 = (bf16[512,512]{0,1:T(8,128)(2,1)S(1)}, bf16[512,512]{0,1:T(8,128)(2,1)S(1)}, u32[]{:S(2)}, u32[]{:S(2)}) collective-permute-start(bf16[512,512]{0,1:T(8,128)(2,1)S(1)} %pad_maximum_fusion.9), channel_id=1, source_target_pairs={{0,1},{1,0},{2,3},{3,2},{4,5},{5,4},{6,7},{7,6},{8,9},{9,8},{10,11... | collective-permute-start | bytes 1572872 | tf_op jit(solution)/shard_map/ppermute | solution.py:90
  76.5 1.7 %collective-permute-start.13 = (bf16[256,2,256]{0,2,1:T(8,128)(2,1)S(1)}, bf16[256,2,256]{0,2,1:T(8,128)(2,1)S(1)}, u32[]{:S(2)}, u32[]{:S(2)}) collective-permute-start(bf16[256,2,256]{0,2,1:T(8,128)(2,1)S(1)} %fusion.162), channel_id=1, source_target_pairs={{0,1},{1,0},{2,3},{3,2},{4,5},{5,4},{6,7},{7,6},{8,9},{9,8},{10,11... | collective-permute-start | bytes 786440 | tf_op jit(solution)/shard_map/ppermute | solution.py:72
  77.4 11.5 %copy-start.3 = (bf16[1024]{0:T(1024)(128)(2,1)S(1)}, bf16[1024]{0:T(1024)(128)(2,1)}, u32[]{:S(2)}) copy-start(bf16[1024]{0:T(1024)(128)(2,1)} %param.41) | copy-start | bytes 6148
  77.4 1.6 %collective-permute-start.19 = (bf16[256,2,256]{0,2,1:T(8,128)(2,1)S(1)}, bf16[256,2,256]{0,2,1:T(8,128)(2,1)S(1)}, u32[]{:S(2)}, u32[]{:S(2)}) collective-permute-start(bf16[256,2,256]{0,2,1:T(8,128)(2,1)S(1)} %fusion.163), channel_id=1, source_target_pairs={{0,1},{1,0},{2,3},{3,2},{4,5},{5,4},{6,7},{7,6},{8,9},{9,8},{10,11... | collective-permute-start | bytes 786440 | tf_op jit(solution)/shard_map/ppermute | solution.py:72
  78.3 6.3 %collective-permute-start.14 = (bf16[256,256]{0,1:T(8,128)(2,1)S(1)}, bf16[256,256]{0,1:T(8,128)(2,1)S(1)}, u32[]{:S(2)}, u32[]{:S(2)}) collective-permute-start(bf16[256,256]{0,1:T(8,128)(2,1)S(1)} %fusion.180), channel_id=1, source_target_pairs={{0,2},{1,3},{2,0},{3,1},{4,6},{5,7},{6,4},{7,5},{8,10},{9,11},{10,... | collective-permute-start | bytes 393224 | tf_op jit(solution)/shard_map/ppermute | solution.py:72
  80.8 6.1 %collective-permute-start.20 = (bf16[256,256]{0,1:T(8,128)(2,1)S(1)}, bf16[256,256]{0,1:T(8,128)(2,1)S(1)}, u32[]{:S(2)}, u32[]{:S(2)}) collective-permute-start(bf16[256,256]{0,1:T(8,128)(2,1)S(1)} %fusion.182), channel_id=1, source_target_pairs={{0,2},{1,3},{2,0},{3,1},{4,6},{5,7},{6,4},{7,5},{8,10},{9,11},{10,... | collective-permute-start | bytes 393224 | tf_op jit(solution)/shard_map/ppermute | solution.py:72
  88.0 6.5 %collective-permute-start.21 = (bf16[256,256]{0,1:T(8,128)(2,1)S(1)}, bf16[256,256]{0,1:T(8,128)(2,1)S(1)}, u32[]{:S(2)}, u32[]{:S(2)}) collective-permute-start(bf16[256,256]{0,1:T(8,128)(2,1)S(1)} %get-tuple-element.255), channel_id=1, source_target_pairs={{0,2},{1,3},{2,0},{3,1},{4,6},{5,7},{6,4},{7,5},{8,10},{9,11},{10,... | collective-permute-start | bytes 393224 | tf_op jit(solution)/shard_map/ppermute | solution.py:90
  88.8 7.0 %collective-permute-start.15 = (bf16[256,256]{0,1:T(8,128)(2,1)S(1)}, bf16[256,256]{0,1:T(8,128)(2,1)S(1)}, u32[]{:S(2)}, u32[]{:S(2)}) collective-permute-start(bf16[256,256]{0,1:T(8,128)(2,1)S(1)} %get-tuple-element.254), channel_id=1, source_target_pairs={{0,2},{1,3},{2,0},{3,1},{4,6},{5,7},{6,4},{7,5},{8,10},{9,11},{10,... | collective-permute-start | bytes 393224 | tf_op jit(solution)/shard_map/ppermute | solution.py:90
  94.5 2.2 %collective-permute-start.22 = (bf16[256,512]{0,1:T(8,128)(2,1)S(1)}, bf16[256,512]{0,1:T(8,128)(2,1)S(1)}, u32[]{:S(2)}, u32[]{:S(2)}) collective-permute-start(bf16[256,512]{0,1:T(8,128)(2,1)S(1)} %pad_maximum_fusion.13), channel_id=1, source_target_pairs={{0,1},{1,0},{2,3},{3,2},{4,5},{5,4},{6,7},{7,6},{8,9},{9,8},{10,11... | collective-permute-start | bytes 786440 | tf_op jit(solution)/shard_map/ppermute | solution.py:90
  96.6 7.0 %collective-permute-start.16 = (bf16[256,512]{0,1:T(8,128)(2,1)}, bf16[256,512]{0,1:T(8,128)(2,1)}, u32[]{:S(2)}, u32[]{:S(2)}) collective-permute-start(bf16[256,512]{0,1:T(8,128)(2,1)} %pad_maximum_fusion.12), channel_id=1, source_target_pairs={{0,1},{1,0},{2,3},{3,2},{4,5},{5,4},{6,7},{7,6},{8,9},{9,8},{10,11... | collective-permute-start | bytes 786440 | tf_op jit(solution)/shard_map/ppermute | solution.py:90
  103.1 7.5 %collective-permute-start.23 = (bf16[256,2,256]{0,2,1:T(8,128)(2,1)}, bf16[256,2,256]{0,2,1:T(8,128)(2,1)S(1)}, u32[]{:S(2)}, u32[]{:S(2)}) collective-permute-start(bf16[256,2,256]{0,2,1:T(8,128)(2,1)} %fusion.165), channel_id=1, source_target_pairs={{0,1},{1,0},{2,3},{3,2},{4,5},{5,4},{6,7},{7,6},{8,9},{9,8},{10,11... | collective-permute-start | bytes 786440 | tf_op jit(solution)/shard_map/ppermute | solution.py:72
  109.4 2.9 %copy-start.1 = (f32[256,1024]{0,1:T(8,128)S(1)}, f32[256,1024]{0,1:T(8,128)}, u32[]{:S(2)}) copy-start(f32[256,1024]{0,1:T(8,128)} %fusion.100) | copy-start | bytes 3145732
  110.5 1.7 %collective-permute-start.17 = (bf16[256,2,256]{0,2,1:T(8,128)(2,1)S(1)}, bf16[256,2,256]{0,2,1:T(8,128)(2,1)S(1)}, u32[]{:S(2)}, u32[]{:S(2)}) collective-permute-start(bf16[256,2,256]{0,2,1:T(8,128)(2,1)S(1)} %fusion.164), channel_id=1, source_target_pairs={{0,1},{1,0},{2,3},{3,2},{4,5},{5,4},{6,7},{7,6},{8,9},{9,8},{10,11... | collective-permute-start | bytes 786440 | tf_op jit(solution)/shard_map/ppermute | solution.py:72
  111.7 6.4 %collective-permute-start.24 = (bf16[256,256]{0,1:T(8,128)(2,1)S(1)}, bf16[256,256]{0,1:T(8,128)(2,1)S(1)}, u32[]{:S(2)}, u32[]{:S(2)}) collective-permute-start(bf16[256,256]{0,1:T(8,128)(2,1)S(1)} %fusion.183), channel_id=1, source_target_pairs={{0,2},{1,3},{2,0},{3,1},{4,6},{5,7},{6,4},{7,5},{8,10},{9,11},{10,... | collective-permute-start | bytes 393224 | tf_op jit(solution)/shard_map/ppermute | solution.py:72
  112.3 8.2 %collective-permute-start.18 = (bf16[256,256]{0,1:T(8,128)(2,1)S(1)}, bf16[256,256]{0,1:T(8,128)(2,1)S(1)}, u32[]{:S(2)}, u32[]{:S(2)}) collective-permute-start(bf16[256,256]{0,1:T(8,128)(2,1)S(1)} %fusion.181), channel_id=1, source_target_pairs={{0,2},{1,3},{2,0},{3,1},{4,6},{5,7},{6,4},{7,5},{8,10},{9,11},{10,... | collective-permute-start | bytes 393224 | tf_op jit(solution)/shard_map/ppermute | solution.py:72

commit v14 on v10

--- a/solution.py
+++ b/solution.py
@@ -99,6 +99,27 @@
         high = jnp.where(mine == 0, got, current)
         current = jnp.stack([low, high], axis=current.ndim - 1)
     return current
+
+
+def reduce_all_heads(partial, head_id, head_total):
+    levels = level_count(head_total)
+    rows, cols = partial.shape
+    halves = partial.reshape(rows, 2, cols // 2)
+    mine = head_id & 1
+    keep = lax.dynamic_index_in_dim(halves, mine, 1, keepdims=False)
+    give = lax.dynamic_index_in_dim(halves, 1 - mine, 1, keepdims=False)
+    got = lax.ppermute(give.astype(jnp.bfloat16), "heads", [(i, i ^ 1) for i in range(head_total)])
+    current = keep + got.astype(jnp.float32)
+    for level in range(1, levels):
+        bit = 1 << level
+        sent = current.astype(jnp.bfloat16)
+        got = lax.ppermute(sent, "heads", [(i, i ^ bit) for i in range(head_total)])
+        current = sent.astype(jnp.float32) + got.astype(jnp.float32)
+    own = current.astype(jnp.bfloat16)
+    other = lax.ppermute(own, "heads", [(i, i ^ 1) for i in range(head_total)])
+    low = jnp.where(mine == 0, own, other)
+    high = jnp.where(mine == 0, other, own)
+    return jnp.concatenate([low, high], axis=1)
 
 
 def absorb_block(state, query_heads, key_block, value_block, linked, head_count, brick_rows):
@@ -230,9 +251,16 @@
     for chunk in range(chunk_count):
         rows = slice(chunk * chunk_rows, (chunk + 1) * chunk_rows)
         partial_out = jnp.dot(attended[rows], out_weight, preferred_element_type=jnp.float32)
-        out_sum = scatter_heads(partial_out, head_id, head_total)
-        stream_two = (stream[rows].astype(jnp.float32) + out_sum).astype(jnp.bfloat16)
-        stream_two_full = gather_heads(stream_two, head_id, head_total)
+        own_cols = head_id * local_width
+        partial_out = lax.dynamic_update_slice_in_dim(
+            partial_out,
+            lax.dynamic_slice_in_dim(partial_out, own_cols, local_width, 1)
+            + stream[rows].astype(jnp.float32),
+            own_cols,
+            1,
+        )
+        stream_two_full = reduce_all_heads(partial_out, head_id, head_total)
+        stream_two = lax.dynamic_slice_in_dim(stream_two_full, own_cols, local_width, 1)
         normed_two = layer_norm(stream_two_full, gain_two).astype(jnp.bfloat16)
         hidden = jax.nn.gelu(
             jnp.dot(normed_two, up_weight, preferred_element_type=jnp.float32), approximate=True

time: 121 us -> 150 us (1.24)
  local copies, waits for them, and re-layouts: 12.7 us -> 36.3 us
  other arithmetic: 17.2 us -> 27.8 us
  starting transfers between devices: 22.7 us -> 19.7 us
  waiting for transfers between devices: 40.8 us -> 38.1 us
    reshape x1 -> x4, local copies, waits for them, and re-layouts: 0.2 us -> 11.4 us  [the longest x2 6.44 us: scatter_heads(): current = partial.reshape((rows,) + (2,) * levels + (width,))]
    dynamic_slice x0 -> x8, local copies, waits for them, and re-layouts: none -> 8.9 us  [the longest x2 3.54 us: reduce_all_heads(): give = lax.dynamic_index_in_dim(halves, 1 - mine, 1, keepdims=False)]
    another operation x16, other arithmetic: 3.98 us -> 10.5 us  [gather_levels(): current = jnp.stack([low, high], axis=current.ndim - 1)]
    another operation x4, local copies, waits for them, and re-layouts: 0.28 us -> 6.22 us  [gather_levels(): current = jnp.stack([low, high], axis=current.ndim - 1)]
    ppermute x8 -> x4, waiting for transfers between devices: 11.5 us -> 6.42 us  [scatter_heads(): lax.ppermute(give.astype(jnp.bfloat16), 'heads', [(i, i ^ bit) for i in r...]
    ppermute x4 -> x6, waiting for transfers between devices: 7.2 us -> 11.5 us  [the longest x2 11.5 us: reduce_all_heads(): got = lax.ppermute(sent, 'heads', [(i, i ^ bit) for i in range(head_total)])]
    convert_element_type x8 -> x2, local copies, waits for them, and re-layouts: 3.34 us -> 0.05 us  [scatter_heads(): give.astype(jnp.bfloat16)]
    unnamed x17 -> x60, local copies, waits for them, and re-layouts: 1.54 us -> 4.77 us
  transfers between devices with their start and end apart: 25 -> 23, of which waited for: 16 -> 9; matrix products, arithmetic and copies ran while one was open for 23% -> 38% of each run, Pallas kernels for 0% -> 0%
where the time goes in v14:
time: 150 us; the launch traced here: 149 us
  waiting for transfers between devices  38.1 us (25%)
  local copies, waits for them, and re-layouts  36.3 us (24%)
  other arithmetic  27.8 us (19%)
  matrix products  22.5 us (15%)
  starting transfers between devices  19.7 us (13%)
  between operations  4.53 us (3%)
    ppermute x8, waiting for transfers between devices, gather_levels(): lax.ppermute(current, 'heads', [(i, i ^ bit) for i in range(head_total)])  13.9 us
    ppermute x2, waiting for transfers between devices, reduce_all_heads(): got = lax.ppermute(sent, 'heads', [(i, i ^ bit) for i in range(head_total)])  11.5 us
    another operation x16, other arithmetic, gather_levels(): current = jnp.stack([low, high], axis=current.ndim - 1)  10.5 us
    dot_general x2, matrix products, shards(): lowered = jnp.dot(hidden, down_weight, preferred_element_type=jnp.float32)  8.18 us
    reshape x2, local copies, waits for them, and re-layouts, scatter_heads(): current = partial.reshape((rows,) + (2,) * levels + (width,))  6.44 us
    ppermute x4, waiting for transfers between devices, scatter_heads(): lax.ppermute(give.astype(jnp.bfloat16), 'heads', [(i, i ^ bit) for i in r...  6.42 us
    ppermute x3, waiting for transfers between devices, shards(): ringed[slot + 1] = lax.ppermute(ringed[slot], 'bricks', ring)  6.24 us
    another operation x4, local copies, waits for them, and re-layouts, gather_levels(): current = jnp.stack([low, high], axis=current.ndim - 1)  6.22 us
  transfers between devices with their start and end apart: 23, of which 9 were waited for; matrix products, arithmetic and copies ran while one was open for 38% of the time, Pallas kernels for 0%

profile of v14, /device:TPU:0, one launch (start us, length us, event | category | flops | bytes accessed | tf_op | source)
XLA Modules:
  0.0 148.9 jit_solution(2344488953531184083)
XLA Ops:
  0.0 0.9 fusion.217
  0.9 1.3 collective-permute-start.1
  2.2 5.6 %collective-permute-start = (bf16[64,256]{1,0:T(8,128)(2,1)S(1)}, bf16[64,256]{1,0:T(8,128)(2,1)S(1)}, u32[]{:S(2)}, u32[]{:S(2)}) collective-permute-start(bf16[64,256]{1,0:T(8,128)(2,1)S(1)} %get-tuple-element.226), channel_id=1, source_target_pairs={{0,4},{4,8},{8,12},{1,5},{5,9},{9,13},{2,6},{6,10},{10,14},{3,7},{... | collective-permute-start | bytes 98312 | tf_op jit(solution)/shard_map/ppermute | solution.py:20
  7.8 1.0 fusion.218
  8.8 0.9 fusion.219
  9.7 1.4 fusion.221
  11.8 1.0 convert
  14.3 1.6 %fusion.117 = f32[1,8,8,8,256]{4,3,2,1,0:T(8,128)S(1)} fusion(f32[1,10,10,10,256]{4,3,2,1,0:T(8,128)S(1)} %select_maximum_fusion, f32[1,1,8,8,256]{4,3,2,1,0:T(8,128)S(1)} %multiply_bitcast_fusion, f32[1,8,8,8,256]{4,3,2,1,0:T(8,128)S(1)} %convert, f32[1,1,8,8,256]{4,3,2,1,0:T(8,128)S(1)} %multiply_bitcast_fusion.1, f32[256]{0:T(256)S(1)} %bitcast.477, ...), kind=kLoop, calls=%fused_computation.137 | loop fusion | flops 7208960 | bytes 13790208 | tf_op jit(solution)/shard_map/add | solution.py:51
  16.1 2.0 %collective-permute-start.3 = (bf16[512,256]{1,0:T(8,128)(2,1)S(1)}, bf16[512,256]{1,0:T(8,128)(2,1)S(1)}, u32[]{:S(2)}, u32[]{:S(2)}) collective-permute-start(bf16[512,256]{1,0:T(8,128)(2,1)S(1)} %fusion.148), channel_id=1, source_target_pairs={{0,2},{1,3},{2,0},{3,1},{4,6},{5,7},{6,4},{7,5},{8,10},{9,11},{10,... | collective-permute-start | bytes 786440 | tf_op jit(solution)/shard_map/ppermute | solution.py:97
  18.1 1.6 %collective-permute-start.2 = (bf16[512,256]{1,0:T(8,128)(2,1)S(1)}, bf16[512,256]{1,0:T(8,128)(2,1)}, u32[]{:S(2)}, u32[]{:S(2)}) collective-permute-start(bf16[512,256]{1,0:T(8,128)(2,1)S(1)} %fusion.148), channel_id=1, source_target_pairs={{0,4},{4,8},{8,12},{12,0},{1,5},{5,9},{9,13},{13,1},{2,6},{6,10},{... | collective-permute-start | bytes 786440 | tf_op jit(solution)/shard_map/ppermute | solution.py:210
  19.6 4.3 %collective-permute-done.3 = bf16[512,256]{1,0:T(8,128)(2,1)S(1)} collective-permute-done((bf16[512,256]{1,0:T(8,128)(2,1)S(1)}, bf16[512,256]{1,0:T(8,128)(2,1)S(1)}, u32[]{:S(2)}, u32[]{:S(2)}) %collective-permute-start.3) | collective-permute-done | bytes 262176 | tf_op jit(solution)/shard_map/ppermute | solution.py:97
  24.0 3.2 %collective-permute-done.2 = bf16[512,256]{1,0:T(8,128)(2,1)} collective-permute-done((bf16[512,256]{1,0:T(8,128)(2,1)S(1)}, bf16[512,256]{1,0:T(8,128)(2,1)}, u32[]{:S(2)}, u32[]{:S(2)}) %collective-permute-start.2) | collective-permute-done | bytes 262176 | tf_op jit(solution)/shard_map/ppermute | solution.py:210
  30.7 3.1 %collective-permute-done.5 = bf16[512,256]{1,0:T(8,128)(2,1)} collective-permute-done((bf16[512,256]{1,0:T(8,128)(2,1)}, bf16[512,256]{1,0:T(8,128)(2,1)}, u32[]{:S(2)}, u32[]{:S(2)}) %collective-permute-start.5) | collective-permute-done | bytes 262176 | tf_op jit(solution)/shard_map/ppermute | solution.py:97
  33.9 1.1 select_bitcast_fusion.13
  34.9 0.9 pad_maximum_fusion.9
  35.9 1.1 pad_maximum_fusion
  36.9 1.5 %copy.24 = bf16[512,2,2,256]{0,3,2,1:T(8,128)(2,1)S(1)} copy(bf16[512,2,2,256]{3,0,1,2:T(8,128)(2,1)} %pad_maximum_fusion) | data formatting | bytes 2097152 | tf_op jit(solution)/shard_map/stack | solution.py:100
  38.5 3.1 %collective-permute-done.4 = bf16[512,256]{1,0:T(8,128)(2,1)} collective-permute-done((bf16[512,256]{1,0:T(8,128)(2,1)}, bf16[512,256]{1,0:T(8,128)(2,1)}, u32[]{:S(2)}, u32[]{:S(2)}) %collective-permute-start.4) | collective-permute-done | bytes 262176 | tf_op jit(solution)/shard_map/ppermute | solution.py:210
  41.5 1.6 %collective-permute-start.8 = (bf16[512,256]{1,0:T(8,128)(2,1)}, bf16[512,256]{1,0:T(8,128)(2,1)S(1)}, u32[]{:S(2)}, u32[]{:S(2)}) collective-permute-start(bf16[512,256]{1,0:T(8,128)(2,1)} %collective-permute-done.4), channel_id=1, source_target_pairs={{0,2},{1,3},{2,0},{3,1},{4,6},{5,7},{6,4},{7,5},{8,10},{9,11},{10,... | collective-permute-start | bytes 786440 | tf_op jit(solution)/shard_map/ppermute | solution.py:97
  46.9 0.8 fusion.5
  47.8 1.0 fusion.64
  48.9 0.9 multiply_add_fusion.1
  49.9 1.0 select_bitcast_fusion.11
  50.9 0.9 pad_maximum_fusion.10
  51.9 1.1 pad_maximum_fusion.1
  53.0 1.5 %copy.26 = bf16[512,2,2,256]{0,3,2,1:T(8,128)(2,1)S(1)} copy(bf16[512,2,2,256]{3,0,1,2:T(8,128)(2,1)} %pad_maximum_fusion.1) | data formatting | bytes 2097152 | tf_op jit(solution)/shard_map/stack | solution.py:100
  56.8 0.8 bitcast_reduce_fusion.2
  57.6 0.8 fusion.7
  58.5 1.0 fusion.61
  59.5 1.5 %collective-permute-start.10 = (bf16[512,256]{1,0:T(8,128)(2,1)}, bf16[512,256]{1,0:T(8,128)(2,1)S(1)}, u32[]{:S(2)}, u32[]{:S(2)}) collective-permute-start(bf16[512,256]{1,0:T(8,128)(2,1)} %collective-permute-done.7), channel_id=1, source_target_pairs={{0,2},{1,3},{2,0},{3,1},{4,6},{5,7},{6,4},{7,5},{8,10},{9,11},{10,... | collective-permute-start | bytes 786440 | tf_op jit(solution)/shard_map/ppermute | solution.py:97
  61.0 0.9 multiply_add_fusion
  61.9 6.5 %collective-permute-done.10 = bf16[512,256]{1,0:T(8,128)(2,1)S(1)} collective-permute-done((bf16[512,256]{1,0:T(8,128)(2,1)}, bf16[512,256]{1,0:T(8,128)(2,1)S(1)}, u32[]{:S(2)}, u32[]{:S(2)}) %collective-permute-start.10) | collective-permute-done | bytes 262176 | tf_op jit(solution)/shard_map/ppermute | solution.py:97
  68.5 1.0 select_bitcast_fusion.9
  69.5 0.9 pad_maximum_fusion.11
  70.5 1.1 pad_maximum_fusion.2
  71.5 1.5 %copy.28 = bf16[512,2,2,256]{0,3,2,1:T(8,128)(2,1)S(1)} copy(bf16[512,2,2,256]{3,0,1,2:T(8,128)(2,1)} %pad_maximum_fusion.2) | data formatting | bytes 2097152 | tf_op jit(solution)/shard_map/stack | solution.py:100
  75.8 0.8 bitcast_reduce_fusion.1
  76.6 0.8 fusion.9
  77.6 1.8 %fusion.67 = f32[1,512,4,64]{1,3,2,0:T(8,128)} fusion(bf16[512,4,64]{0,2,1:T(8,128)(2,1)S(1)} %bitcast.478, f32[4,512,512]{2,1,0:T(8,128)S(1)} %get-tuple-element.268, f32[4,512]{1,0:T(4,128)S(1)} %bitcast.450, pred[]{:T(512)} %bitcast.89, f32[1,512,4,64]{1,3,2,0:T(8,128)S(1)} %copy-done.14, f32[512,4]{0,1:T(4,128)S(1)} %get-tuple-element.196), kind=kOutput, calls=%fused_computation.87 | convolution fusion | flops 138674176 | bytes 5521409 | tf_op jit(solution)/shard_map/bhqk,khd->bqhd/dot_general | solution.py:139
  79.5 1.1 pad_maximum_fusion.3
  80.6 1.7 %copy.30 = bf16[512,2,2,256]{0,3,2,1:T(8,128)(2,1)S(1)} copy(bf16[512,2,2,256]{3,0,1,2:T(8,128)(2,1)} %pad_maximum_fusion.3) | data formatting | bytes 2097152 | tf_op jit(solution)/shard_map/stack | solution.py:100
  85.5 0.8 fusion.10
  86.5 1.0 fusion.98
  88.6 1.0 copy-done.1
  89.6 3.1 %reshape.481 = f32[256,2,512]{2,1,0:T(2,128)} reshape(f32[256,1024]{1,0:T(8,128)} %copy-done.1) | data formatting | bytes 2097152 | tf_op jit(solution)/shard_map/reshape | solution.py:107
  92.7 1.7 %constant_dynamic-slice_fusion = bf16[256,1,512]{2,1,0:T(2,128)(2,1)S(1)} fusion(f32[256,2,512]{2,1,0:T(2,128)} %reshape.481, s32[]{:T(128)S(6)} %select_n.283), kind=kLoop, calls=%fused_computation.280 | loop fusion | bytes 524292 | tf_op jit(solution)/shard_map/jit(dynamic_index_in_dim)/dynamic_slice | solution.py:110
  95.0 1.9 %reshape.479 = f32[256,2,512]{2,1,0:T(2,128)} reshape(f32[256,1024]{1,0:T(8,128)S(1)} %get-tuple-element.222) | data formatting | bytes 2097152 | tf_op jit(solution)/shard_map/reshape | solution.py:107
  96.9 1.8 %constant_dynamic-slice_fusion.5 = bf16[256,1,512]{2,1,0:T(2,128)(2,1)S(1)} fusion(f32[256,2,512]{2,1,0:T(2,128)} %reshape.479, s32[]{:T(128)S(6)} %select_n.283), kind=kLoop, calls=%fused_computation.285 | loop fusion | bytes 524292 | tf_op jit(solution)/shard_map/jit(dynamic_index_in_dim)/dynamic_slice | solution.py:110
  99.4 1.0 fusion.145
  101.4 1.7 %collective-permute-start.14 = (bf16[256,512]{1,0:T(8,128)(2,1)S(1)}, bf16[256,512]{1,0:T(8,128)(2,1)S(1)}, u32[]{:S(2)}, u32[]{:S(2)}) collective-permute-start(bf16[256,512]{1,0:T(8,128)(2,1)S(1)} %fusion.146), channel_id=1, source_target_pairs={{0,2},{1,3},{2,0},{3,1},{4,6},{5,7},{6,4},{7,5},{8,10},{9,11},{10,... | collective-permute-start | bytes 786440 | tf_op jit(solution)/shard_map/ppermute | solution.py:116
  103.1 6.5 %collective-permute-done.19 = bf16[256,512]{1,0:T(8,128)(2,1)S(1)} collective-permute-done((bf16[256,512]{1,0:T(8,128)(2,1)S(1)}, bf16[256,512]{1,0:T(8,128)(2,1)S(1)}, u32[]{:S(2)}, u32[]{:S(2)}) %collective-permute-start.19) | collective-permute-done | bytes 262176 | tf_op jit(solution)/shard_map/ppermute | solution.py:116
  109.7 5.0 %collective-permute-done.14 = bf16[256,512]{1,0:T(8,128)(2,1)S(1)} collective-permute-done((bf16[256,512]{1,0:T(8,128)(2,1)S(1)}, bf16[256,512]{1,0:T(8,128)(2,1)S(1)}, u32[]{:S(2)}, u32[]{:S(2)}) %collective-permute-start.14) | collective-permute-done | bytes 262176 | tf_op jit(solution)/shard_map/ppermute | solution.py:116
  114.9 1.0 broadcast_select_fusion.1
  116.4 4.1 %fusion.101 = f32[256,1024]{1,0:T(8,128)} fusion(bf16[1024,1024]{1,0:T(8,128)(2,1)S(1)} %copy-done, bf16[1024,1024]{1,0:T(8,128)(2,1)} %param.42, f32[256]{0:T(256)S(1)} %add_rsqrt_fusion.4, f32[256]{0:T(256)S(1)} %broadcast_multiply_fusion.4, f32[1024]{0:T(1024)S(1)} %convert_element_type.258, bf16[256,512]{1,0:T(8,128)(2,1)S(1)} %get-tuple-element.213, ...), kind=kOutput, calls=%fused_computation.132 | convolution fusion | flops 1078198272 | bytes 5773312 | tf_op jit(solution)/shard_map/dot_general | solution.py:268
  120.5 3.3 %reshape.482 = f32[256,2,2,256]{3,2,1,0:T(2,128)} reshape(f32[256,1024]{1,0:T(8,128)} %fusion.101) | data formatting | bytes 2097152 | tf_op jit(solution)/shard_map/reshape | solution.py:65
  123.8 1.7 %constant_dynamic-slice_fusion.4 = bf16[256,2,1,256]{3,2,1,0:T(2,128)(2,1)S(1)} fusion(f32[256,2,2,256]{3,2,1,0:T(2,128)} %reshape.482, s32[]{:T(128)S(6)} %select_n.287), kind=kLoop, calls=%fused_computation.284 | loop fusion | bytes 524292 | tf_op jit(solution)/shard_map/jit(dynamic_index_in_dim)/dynamic_slice | solution.py:71
  126.8 1.0 broadcast_select_fusion.3
  128.2 4.1 %fusion.103 = f32[256,1024]{1,0:T(8,128)} fusion(bf16[1024,1024]{1,0:T(8,128)(2,1)S(1)} %copy-done, bf16[1024,1024]{1,0:T(8,128)(2,1)} %param.42, f32[1024]{0:T(1024)S(1)} %convert_element_type.258, f32[256]{0:T(256)S(1)} %add_rsqrt_fusion.5, f32[256]{0:T(256)S(1)} %broadcast_multiply_fusion.5, bf16[256,512]{1,0:T(8,128)(2,1)S(1)} %get-tuple-element.211, ...), kind=kOutput, calls=%fused_computation.133 | convolution fusion | flops 1078198272 | bytes 5773312 | tf_op jit(solution)/shard_map/dot_general | solution.py:268
  132.3 3.1 %reshape.480 = f32[256,2,2,256]{3,2,1,0:T(2,128)} reshape(f32[256,1024]{1,0:T(8,128)} %fusion.103) | data formatting | bytes 2097152 | tf_op jit(solution)/shard_map/reshape | solution.py:65
  135.4 1.8 %constant_dynamic-slice_fusion.2 = bf16[256,2,1,256]{3,2,1,0:T(2,128)(2,1)S(1)} fusion(f32[256,2,2,256]{3,2,1,0:T(2,128)} %reshape.480, s32[]{:T(128)S(6)} %select_n.287), kind=kLoop, calls=%fused_computation.282 | loop fusion | bytes 524292 | tf_op jit(solution)/shard_map/jit(dynamic_index_in_dim)/dynamic_slice | solution.py:71
  138.3 1.0 bitcast_add_fusion.2
  139.9 1.7 %collective-permute-start.17 = (bf16[256,256]{1,0:T(8,128)(2,1)S(1)}, bf16[256,256]{1,0:T(8,128)(2,1)S(1)}, u32[]{:S(2)}, u32[]{:S(2)}) collective-permute-start(bf16[256,256]{1,0:T(8,128)(2,1)S(1)} %fusion.183), channel_id=1, source_target_pairs={{0,2},{1,3},{2,0},{3,1},{4,6},{5,7},{6,4},{7,5},{8,10},{9,11},{10,... | collective-permute-start | bytes 393224 | tf_op jit(solution)/shard_map/ppermute | solution.py:72
  141.6 4.1 %collective-permute-done.22 = bf16[256,256]{1,0:T(8,128)(2,1)S(1)} collective-permute-done((bf16[256,256]{1,0:T(8,128)(2,1)S(1)}, bf16[256,256]{1,0:T(8,128)(2,1)S(1)}, u32[]{:S(2)}, u32[]{:S(2)}) %collective-permute-start.22) | collective-permute-done | bytes 131104 | tf_op jit(solution)/shard_map/ppermute | solution.py:72
  145.8 2.3 %collective-permute-done.17 = bf16[256,256]{1,0:T(8,128)(2,1)S(1)} collective-permute-done((bf16[256,256]{1,0:T(8,128)(2,1)S(1)}, bf16[256,256]{1,0:T(8,128)(2,1)S(1)}, u32[]{:S(2)}, u32[]{:S(2)}) %collective-permute-start.17) | collective-permute-done | bytes 131104 | tf_op jit(solution)/shard_map/ppermute | solution.py:72
  (165 shorter events, 23.1 us)
Async XLA Ops:
  0.0 116.4 %copy-start = (bf16[1024,1024]{1,0:T(8,128)(2,1)S(1)}, bf16[1024,1024]{1,0:T(8,128)(2,1)}, u32[]{:S(2)}) copy-start(bf16[1024,1024]{1,0:T(8,128)(2,1)} %param.43) | copy-start | bytes 6291460
  0.9 13.1 %collective-permute-start.1 = (bf16[64,256]{1,0:T(8,128)(2,1)S(1)}, bf16[64,256]{1,0:T(8,128)(2,1)S(1)}, u32[]{:S(2)}, u32[]{:S(2)}) collective-permute-start(bf16[64,256]{1,0:T(8,128)(2,1)S(1)} %get-tuple-element.227), channel_id=1, source_target_pairs={{4,0},{8,4},{12,8},{5,1},{9,5},{13,9},{6,2},{10,6},{14,10},{7,3},{... | collective-permute-start | bytes 98312 | tf_op jit(solution)/shard_map/ppermute | solution.py:21
  2.2 11.8 %collective-permute-start = (bf16[64,256]{1,0:T(8,128)(2,1)S(1)}, bf16[64,256]{1,0:T(8,128)(2,1)S(1)}, u32[]{:S(2)}, u32[]{:S(2)}) collective-permute-start(bf16[64,256]{1,0:T(8,128)(2,1)S(1)} %get-tuple-element.226), channel_id=1, source_target_pairs={{0,4},{4,8},{8,12},{1,5},{5,9},{9,13},{2,6},{6,10},{10,14},{3,7},{... | collective-permute-start | bytes 98312 | tf_op jit(solution)/shard_map/ppermute | solution.py:20
  14.3 1.6 %copy-start.13 = (bf16[512,256]{1,0:T(8,128)(2,1)S(1)}, bf16[512,256]{1,0:T(8,128)(2,1)}, u32[]{:S(2)}) copy-start(bf16[512,256]{1,0:T(8,128)(2,1)} %param.31) | copy-start | bytes 786436
  16.0 11.6 %copy-start.15 = (bf16[1024]{0:T(1024)(128)(2,1)S(1)}, bf16[1024]{0:T(1024)(128)(2,1)}, u32[]{:S(2)}) copy-start(bf16[1024]{0:T(1024)(128)(2,1)} %param.36) | copy-start | bytes 6148
  16.0 11.6 %copy-start.17 = (s32[4,4]{1,0:T(4,128)S(1)}, s32[4,4]{1,0:T(4,128)}, u32[]{:S(2)}) copy-start(s32[4,4]{1,0:T(4,128)} %param.33) | copy-start | bytes 196
  16.0 19.7 %copy-start.6 = (bf16[512,256]{1,0:T(8,128)(2,1)}, bf16[512,256]{1,0:T(8,128)(2,1)S(1)}, u32[]{:S(2)}) copy-start(bf16[512,256]{1,0:T(8,128)(2,1)S(1)} %fusion.148) | copy-start | bytes 786436
  16.1 7.8 %collective-permute-start.3 = (bf16[512,256]{1,0:T(8,128)(2,1)S(1)}, bf16[512,256]{1,0:T(8,128)(2,1)S(1)}, u32[]{:S(2)}, u32[]{:S(2)}) collective-permute-start(bf16[512,256]{1,0:T(8,128)(2,1)S(1)} %fusion.148), channel_id=1, source_target_pairs={{0,2},{1,3},{2,0},{3,1},{4,6},{5,7},{6,4},{7,5},{8,10},{9,11},{10,... | collective-permute-start | bytes 786440 | tf_op jit(solution)/shard_map/ppermute | solution.py:97
  18.1 9.1 %collective-permute-start.2 = (bf16[512,256]{1,0:T(8,128)(2,1)S(1)}, bf16[512,256]{1,0:T(8,128)(2,1)}, u32[]{:S(2)}, u32[]{:S(2)}) collective-permute-start(bf16[512,256]{1,0:T(8,128)(2,1)S(1)} %fusion.148), channel_id=1, source_target_pairs={{0,4},{4,8},{8,12},{12,0},{1,5},{5,9},{9,13},{13,1},{2,6},{6,10},{... | collective-permute-start | bytes 786440 | tf_op jit(solution)/shard_map/ppermute | solution.py:210
  27.2 6.7 %collective-permute-start.5 = (bf16[512,256]{1,0:T(8,128)(2,1)}, bf16[512,256]{1,0:T(8,128)(2,1)}, u32[]{:S(2)}, u32[]{:S(2)}) collective-permute-start(bf16[512,256]{1,0:T(8,128)(2,1)} %collective-permute-done.2), channel_id=1, source_target_pairs={{0,2},{1,3},{2,0},{3,1},{4,6},{5,7},{6,4},{7,5},{8,10},{9,11},{10,... | collective-permute-start | bytes 786440 | tf_op jit(solution)/shard_map/ppermute | solution.py:97
  27.5 8.3 %collective-permute-start.6 = (bf16[512,2,256]{2,0,1:T(8,128)(2,1)S(1)}, bf16[512,2,256]{2,0,1:T(8,128)(2,1)S(1)}, u32[]{:S(2)}, u32[]{:S(2)}) collective-permute-start(bf16[512,2,256]{2,0,1:T(8,128)(2,1)S(1)} %pad_maximum_fusion.8), channel_id=1, source_target_pairs={{0,1},{1,0},{2,3},{3,2},{4,5},{5,4},{6,7},{7,6},{8,9},{9,8},{10,11... | collective-permute-start | bytes 1572872 | tf_op jit(solution)/shard_map/ppermute | solution.py:97
  30.7 10.9 %collective-permute-start.4 = (bf16[512,256]{1,0:T(8,128)(2,1)}, bf16[512,256]{1,0:T(8,128)(2,1)}, u32[]{:S(2)}, u32[]{:S(2)}) collective-permute-start(bf16[512,256]{1,0:T(8,128)(2,1)} %collective-permute-done.2), channel_id=1, source_target_pairs={{0,4},{4,8},{8,12},{12,0},{1,5},{5,9},{9,13},{13,1},{2,6},{6,10},{... | collective-permute-start | bytes 786440 | tf_op jit(solution)/shard_map/ppermute | solution.py:210
  38.5 5.3 %copy-start.23 = (bf16[1024,256]{1,0:T(8,128)(2,1)S(1)}, bf16[1024,256]{1,0:T(8,128)(2,1)}, u32[]{:S(2)}) copy-start(bf16[1024,256]{1,0:T(8,128)(2,1)} %param.38) | copy-start | bytes 1572868
  41.5 13.0 %collective-permute-start.7 = (bf16[512,256]{1,0:T(8,128)(2,1)}, bf16[512,256]{1,0:T(8,128)(2,1)}, u32[]{:S(2)}, u32[]{:S(2)}) collective-permute-start(bf16[512,256]{1,0:T(8,128)(2,1)} %collective-permute-done.4), channel_id=1, source_target_pairs={{0,4},{4,8},{8,12},{12,0},{1,5},{5,9},{9,13},{13,1},{2,6},{6,10},{... | collective-permute-start | bytes 786440 | tf_op jit(solution)/shard_map/ppermute | solution.py:210
  41.5 8.3 %collective-permute-start.8 = (bf16[512,256]{1,0:T(8,128)(2,1)}, bf16[512,256]{1,0:T(8,128)(2,1)S(1)}, u32[]{:S(2)}, u32[]{:S(2)}) collective-permute-start(bf16[512,256]{1,0:T(8,128)(2,1)} %collective-permute-done.4), channel_id=1, source_target_pairs={{0,2},{1,3},{2,0},{3,1},{4,6},{5,7},{6,4},{7,5},{8,10},{9,11},{10,... | collective-permute-start | bytes 786440 | tf_op jit(solution)/shard_map/ppermute | solution.py:97
  43.4 1.0 copy-start.18
  44.4 1.0 copy-start.19
  47.8 1.0 copy-start.9
  48.8 3.0 %collective-permute-start.9 = (bf16[512,2,256]{2,0,1:T(8,128)(2,1)S(1)}, bf16[512,2,256]{2,0,1:T(8,128)(2,1)S(1)}, u32[]{:S(2)}, u32[]{:S(2)}) collective-permute-start(bf16[512,2,256]{2,0,1:T(8,128)(2,1)S(1)} %copy-done.9), channel_id=1, source_target_pairs={{0,1},{1,0},{2,3},{3,2},{4,5},{5,4},{6,7},{7,6},{8,9},{9,8},{10,11... | collective-permute-start | bytes 1572872 | tf_op jit(solution)/shard_map/ppermute | solution.py:97
  54.5 1.0 copy-start.24
  54.7 1.5 copy-start.20
  58.5 2.5 %copy-start.10 = (bf16[512,2,256]{2,0,1:T(8,128)(2,1)S(1)}, bf16[512,2,256]{2,0,1:T(8,128)(2,1)}, u32[]{:S(2)}) copy-start(bf16[512,2,256]{2,0,1:T(8,128)(2,1)} %pad_maximum_fusion.10) | copy-start | bytes 1572868
  58.5 2.5 %copy-start.8 = (f32[1,512,4,64]{1,3,2,0:T(8,128)S(1)}, f32[1,512,4,64]{1,3,2,0:T(8,128)}, u32[]{:S(2)}) copy-start(f32[1,512,4,64]{1,3,2,0:T(8,128)} %multiply_add_fusion.1) | copy-start | bytes 1572868
  59.5 9.0 %collective-permute-start.10 = (bf16[512,256]{1,0:T(8,128)(2,1)}, bf16[512,256]{1,0:T(8,128)(2,1)S(1)}, u32[]{:S(2)}, u32[]{:S(2)}) collective-permute-start(bf16[512,256]{1,0:T(8,128)(2,1)} %collective-permute-done.7), channel_id=1, source_target_pairs={{0,2},{1,3},{2,0},{3,1},{4,6},{5,7},{6,4},{7,5},{8,10},{9,11},{10,... | collective-permute-start | bytes 786440 | tf_op jit(solution)/shard_map/ppermute | solution.py:97
  61.0 9.3 %collective-permute-start.11 = (bf16[512,2,256]{2,0,1:T(8,128)(2,1)S(1)}, bf16[512,2,256]{2,0,1:T(8,128)(2,1)S(1)}, u32[]{:S(2)}, u32[]{:S(2)}) collective-permute-start(bf16[512,2,256]{2,0,1:T(8,128)(2,1)S(1)} %copy-done.10), channel_id=1, source_target_pairs={{0,1},{1,0},{2,3},{3,2},{4,5},{5,4},{6,7},{7,6},{8,9},{9,8},{10,11... | collective-permute-start | bytes 1572872 | tf_op jit(solution)/shard_map/ppermute | solution.py:97
  73.0 1.0 copy-start.25
  73.3 1.5 copy-start.21
  74.7 1.0 copy-start.11
  75.8 3.7 %collective-permute-start.12 = (bf16[512,2,256]{2,0,1:T(8,128)(2,1)S(1)}, bf16[512,2,256]{2,0,1:T(8,128)(2,1)S(1)}, u32[]{:S(2)}, u32[]{:S(2)}) collective-permute-start(bf16[512,2,256]{2,0,1:T(8,128)(2,1)S(1)} %copy-done.11), channel_id=1, source_target_pairs={{0,1},{1,0},{2,3},{3,2},{4,5},{5,4},{6,7},{7,6},{8,9},{9,8},{10,11... | collective-permute-start | bytes 1572872 | tf_op jit(solution)/shard_map/ppermute | solution.py:97
  76.6 1.0 copy-start.14
  82.3 1.0 copy-start.22
  82.6 1.5 copy-start.26
  85.5 1.0 copy-start.27
  86.5 1.1 copy-start.12
  87.5 1.0 copy-start.7
  88.6 1.0 copy-start.1
  94.4 4.9 %collective-permute-start.18 = (bf16[256,512]{1,0:T(8,128)(2,1)S(1)}, bf16[256,512]{1,0:T(8,128)(2,1)}, u32[]{:S(2)}, u32[]{:S(2)}) collective-permute-start(bf16[256,512]{1,0:T(8,128)(2,1)S(1)} %bitcast.438), channel_id=1, source_target_pairs={{0,1},{1,0},{2,3},{3,2},{4,5},{5,4},{6,7},{7,6},{8,9},{9,8},{10,11... | collective-permute-start | bytes 786440 | tf_op jit(solution)/shard_map/ppermute | solution.py:111
  96.9 2.0 %copy-start.3 = (f32[256,2,512]{2,1,0:T(2,128)S(1)}, f32[256,2,512]{2,1,0:T(2,128)}, u32[]{:S(2)}) copy-start(f32[256,2,512]{2,1,0:T(2,128)} %reshape.481) | copy-start | bytes 3145732
  96.9 4.0 %copy-start.4 = (f32[256,2,512]{2,1,0:T(2,128)S(1)}, f32[256,2,512]{2,1,0:T(2,128)}, u32[]{:S(2)}) copy-start(f32[256,2,512]{2,1,0:T(2,128)} %reshape.479) | copy-start | bytes 3145732
  98.8 2.5 %collective-permute-start.13 = (bf16[256,512]{1,0:T(8,128)(2,1)S(1)}, bf16[256,512]{1,0:T(8,128)(2,1)S(1)}, u32[]{:S(2)}, u32[]{:S(2)}) collective-permute-start(bf16[256,512]{1,0:T(8,128)(2,1)S(1)} %bitcast.440), channel_id=1, source_target_pairs={{0,1},{1,0},{2,3},{3,2},{4,5},{5,4},{6,7},{7,6},{8,9},{9,8},{10,11... | collective-permute-start | bytes 786440 | tf_op jit(solution)/shard_map/ppermute | solution.py:111
  99.3 10.4 %copy-start.16 = (bf16[1024]{0:T(1024)(128)(2,1)S(1)}, bf16[1024]{0:T(1024)(128)(2,1)}, u32[]{:S(2)}) copy-start(bf16[1024]{0:T(1024)(128)(2,1)} %param.41) | copy-start | bytes 6148
  100.4 9.2 %collective-permute-start.19 = (bf16[256,512]{1,0:T(8,128)(2,1)S(1)}, bf16[256,512]{1,0:T(8,128)(2,1)S(1)}, u32[]{:S(2)}, u32[]{:S(2)}) collective-permute-start(bf16[256,512]{1,0:T(8,128)(2,1)S(1)} %fusion.145), channel_id=1, source_target_pairs={{0,2},{1,3},{2,0},{3,1},{4,6},{5,7},{6,4},{7,5},{8,10},{9,11},{10,... | collective-permute-start | bytes 786440 | tf_op jit(solution)/shard_map/ppermute | solution.py:116
  101.4 13.4 %collective-permute-start.14 = (bf16[256,512]{1,0:T(8,128)(2,1)S(1)}, bf16[256,512]{1,0:T(8,128)(2,1)S(1)}, u32[]{:S(2)}, u32[]{:S(2)}) collective-permute-start(bf16[256,512]{1,0:T(8,128)(2,1)S(1)} %fusion.146), channel_id=1, source_target_pairs={{0,2},{1,3},{2,0},{3,1},{4,6},{5,7},{6,4},{7,5},{8,10},{9,11},{10,... | collective-permute-start | bytes 786440 | tf_op jit(solution)/shard_map/ppermute | solution.py:116
  109.6 5.3 %collective-permute-start.20 = (bf16[256,512]{1,0:T(8,128)(2,1)S(1)}, bf16[256,512]{1,0:T(8,128)(2,1)}, u32[]{:S(2)}, u32[]{:S(2)}) collective-permute-start(bf16[256,512]{1,0:T(8,128)(2,1)S(1)} %add_convert_fusion), channel_id=1, source_target_pairs={{0,1},{1,0},{2,3},{3,2},{4,5},{5,4},{6,7},{7,6},{8,9},{9,8},{10,11... | collective-permute-start | bytes 786440 | tf_op jit(solution)/shard_map/ppermute | solution.py:119
  114.8 11.9 %collective-permute-start.15 = (bf16[256,512]{1,0:T(8,128)(2,1)S(1)}, bf16[256,512]{1,0:T(8,128)(2,1)}, u32[]{:S(2)}, u32[]{:S(2)}) collective-permute-start(bf16[256,512]{1,0:T(8,128)(2,1)S(1)} %add_convert_fusion.1), channel_id=1, source_target_pairs={{0,1},{1,0},{2,3},{3,2},{4,5},{5,4},{6,7},{7,6},{8,9},{9,8},{10,11... | collective-permute-start | bytes 786440 | tf_op jit(solution)/shard_map/ppermute | solution.py:119
  126.3 12.0 %collective-permute-start.21 = (bf16[256,2,256]{2,0,1:T(8,128)(2,1)}, bf16[256,2,256]{2,0,1:T(8,128)(2,1)}, u32[]{:S(2)}, u32[]{:S(2)}) collective-permute-start(bf16[256,2,256]{2,0,1:T(8,128)(2,1)} %bitcast.413), channel_id=1, source_target_pairs={{0,1},{1,0},{2,3},{3,2},{4,5},{5,4},{6,7},{7,6},{8,9},{9,8},{10,11... | collective-permute-start | bytes 786440 | tf_op jit(solution)/shard_map/ppermute | solution.py:72
  135.4 2.0 %copy-start.2 = (f32[256,2,2,256]{3,2,1,0:T(2,128)S(1)}, f32[256,2,2,256]{3,2,1,0:T(2,128)}, u32[]{:S(2)}) copy-start(f32[256,2,2,256]{3,2,1,0:T(2,128)} %reshape.482) | copy-start | bytes 3145732
  135.4 2.5 %copy-start.5 = (f32[256,2,2,256]{3,2,1,0:T(2,128)S(1)}, f32[256,2,2,256]{3,2,1,0:T(2,128)}, u32[]{:S(2)}) copy-start(f32[256,2,2,256]{3,2,1,0:T(2,128)} %reshape.480) | copy-start | bytes 3145732
  137.3 2.5 %collective-permute-start.16 = (bf16[256,2,256]{2,0,1:T(8,128)(2,1)S(1)}, bf16[256,2,256]{2,0,1:T(8,128)(2,1)S(1)}, u32[]{:S(2)}, u32[]{:S(2)}) collective-permute-start(bf16[256,2,256]{2,0,1:T(8,128)(2,1)S(1)} %bitcast.439), channel_id=1, source_target_pairs={{0,1},{1,0},{2,3},{3,2},{4,5},{5,4},{6,7},{7,6},{8,9},{9,8},{10,11... | collective-permute-start | bytes 786440 | tf_op jit(solution)/shard_map/ppermute | solution.py:72
  139.4 6.4 %collective-permute-start.22 = (bf16[256,256]{1,0:T(8,128)(2,1)S(1)}, bf16[256,256]{1,0:T(8,128)(2,1)S(1)}, u32[]{:S(2)}, u32[]{:S(2)}) collective-permute-start(bf16[256,256]{1,0:T(8,128)(2,1)S(1)} %fusion.184), channel_id=1, source_target_pairs={{0,2},{1,3},{2,0},{3,1},{4,6},{5,7},{6,4},{7,5},{8,10},{9,11},{10,... | collective-permute-start | bytes 393224 | tf_op jit(solution)/shard_map/ppermute | solution.py:72
  139.9 8.2 %collective-permute-start.17 = (bf16[256,256]{1,0:T(8,128)(2,1)S(1)}, bf16[256,256]{1,0:T(8,128)(2,1)S(1)}, u32[]{:S(2)}, u32[]{:S(2)}) collective-permute-start(bf16[256,256]{1,0:T(8,128)(2,1)S(1)} %fusion.183), channel_id=1, source_target_pairs={{0,2},{1,3},{2,0},{3,1},{4,6},{5,7},{6,4},{7,5},{8,10},{9,11},{10,... | collective-permute-start | bytes 393224 | tf_op jit(solution)/shard_map/ppermute | solution.py:72

commit v15 on v10

--- a/solution.py
+++ b/solution.py
@@ -176,6 +176,9 @@
         jnp.zeros((local_bricks, head_count, brick_rows), jnp.float32),
         jnp.zeros((local_bricks, brick_rows, head_count, HEAD_DIM), jnp.float32),
     )
+    chunk_count = 2 if row_count % 16 == 0 else 1
+    chunk_rows = row_count // chunk_count
+    split_last = local_bricks == 1 and chunk_count == 2
     levels = level_count(head_total)
     cross_levels = list(reversed(range(1, levels)))
     chip_levels = list(range(min(levels, 1)))
@@ -213,23 +216,37 @@
             source = (brick_dev - step) % dev_total
             key_ids = source * local_bricks + jnp.arange(local_bricks, dtype=jnp.int32)
             linked = jnp.take(linked_rows, key_ids, axis=1) > 0
-            state = absorb_block(
-                state, query_heads, key_block, value_block, linked, head_count, brick_rows
-            )
+            if step == dev_total - 1 and split_last:
+                parts = []
+                for half in range(chunk_count):
+                    cut = slice(half * chunk_rows, (half + 1) * chunk_rows)
+                    part = (state[0][:, :, cut], state[1][:, :, cut], state[2][:, cut])
+                    parts.append(absorb_block(
+                        part, query_heads[:, cut], key_block, value_block, linked, head_count,
+                        brick_rows,
+                    ))
+                state = parts
+            else:
+                state = absorb_block(
+                    state, query_heads, key_block, value_block, linked, head_count, brick_rows
+                )
         if slot < dev_total + 1:
             packed = lax.optimization_barrier((state, [table[key] for table, key in made]))
             state = packed[0]
             for (table, key), value in zip(made, packed[1]):
                 table[key] = value
-    row_max, row_mass, weighted = state
-    attended = (weighted / jnp.transpose(row_mass, (0, 2, 1))[:, :, :, None]).astype(jnp.bfloat16)
-    attended = attended.reshape(row_count, local_width)
-    chunk_count = 2 if row_count % 16 == 0 else 1
-    chunk_rows = row_count // chunk_count
+    if not split_last:
+        state = [state]
+    attended_parts = []
+    for row_max, row_mass, weighted in state:
+        attended = weighted / jnp.transpose(row_mass, (0, 2, 1))[:, :, :, None]
+        attended_parts.append(attended.astype(jnp.bfloat16).reshape(-1, local_width))
+    attended = jnp.concatenate(attended_parts, axis=0) if not split_last else None
     outputs = []
     for chunk in range(chunk_count):
         rows = slice(chunk * chunk_rows, (chunk + 1) * chunk_rows)
-        partial_out = jnp.dot(attended[rows], out_weight, preferred_element_type=jnp.float32)
+        attended_rows = attended_parts[chunk] if split_last else attended[rows]
+        partial_out = jnp.dot(attended_rows, out_weight, preferred_element_type=jnp.float32)
         out_sum = scatter_heads(partial_out, head_id, head_total)
         stream_two = (stream[rows].astype(jnp.float32) + out_sum).astype(jnp.bfloat16)
         stream_two_full = gather_heads(stream_two, head_id, head_total)

time: 121 us -> 120 us (level)
    dot_general x4 -> x5, matrix products: 3.34 us -> 3.57 us  [absorb_block(): jnp.einsum('bqhd,khd->bhqk', query_heads, key_rows, preferred_element_typ...]
    dot_general x4 -> x5, matrix products: 3.96 us -> 4.05 us  [absorb_block(): jnp.einsum('bhqk,khd->bqhd', weights.astype(jnp.bfloat16), value_rows, pr...]
    reduce_sum x4 -> x5, other arithmetic: 3.36 us -> 3.38 us  [absorb_block(): mass_new = row_mass * factor + jnp.sum(weights, axis=-1)]
  transfers between devices with their start and end apart: 25 -> 25, of which waited for: 16 -> 18; matrix products, arithmetic and copies ran while one was open for 23% -> 24% of each run, Pallas kernels for 0% -> 0%
where the time goes in v15:
time: 120 us
  waiting for transfers between devices  40.5 us (34%)
  matrix products  22.4 us (19%)
  starting transfers between devices  22.2 us (18%)
  other arithmetic  17.2 us (14%)
  local copies, waits for them, and re-layouts  12.7 us (11%)
  between operations  4.53 us (4%)
    ppermute x8, waiting for transfers between devices, gather_levels(): lax.ppermute(current, 'heads', [(i, i ^ bit) for i in range(head_total)])  13.3 us
    ppermute x8, waiting for transfers between devices, scatter_heads(): lax.ppermute(give.astype(jnp.bfloat16), 'heads', [(i, i ^ bit) for i in r...  11.5 us
    ppermute x3, waiting for transfers between devices, shards(): ringed[slot + 1] = lax.ppermute(ringed[slot], 'bricks', ring)  8.81 us
    dot_general x2, matrix products, shards(): lowered = jnp.dot(hidden, down_weight, preferred_element_type=jnp.float32)  8.42 us
    ppermute x4, waiting for transfers between devices, gather_heads(): lax.ppermute(current, 'heads', [(i, i ^ bit) for i in range(head_total)])  6.85 us
    ppermute x8, starting transfers between devices, gather_levels(): lax.ppermute(current, 'heads', [(i, i ^ bit) for i in range(head_total)])  5.88 us
    ppermute x1, starting transfers between devices, extended_2(): before = lax.ppermute(last, axis, up)  5.56 us
    ppermute x8, starting transfers between devices, scatter_heads(): lax.ppermute(give.astype(jnp.bfloat16), 'heads', [(i, i ^ bit) for i in r...  5.03 us
  transfers between devices with their start and end apart: 25, of which 18 were waited for; matrix products, arithmetic and copies ran while one was open for 24% of the time, Pallas kernels for 0%

profile of v15, /device:TPU:0, one launch (start us, length us, event | category | flops | bytes accessed | tf_op | source)
XLA Modules:
  0.0 119.5 jit_solution(5006009417765164819)
XLA Ops:
  0.0 0.9 fusion.198
  0.9 1.3 %collective-permute-start.1 = (bf16[64,256]{1,0:T(8,128)(2,1)S(1)}, bf16[64,256]{1,0:T(8,128)(2,1)S(1)}, u32[]{:S(2)}, u32[]{:S(2)}) collective-permute-start(bf16[64,256]{1,0:T(8,128)(2,1)S(1)} %get-tuple-element.245), channel_id=1, source_target_pairs={{4,0},{8,4},{12,8},{5,1},{9,5},{13,9},{6,2},{10,6},{14,10},{7,3},{... | collective-permute-start | bytes 98312 | tf_op jit(solution)/shard_map/ppermute | solution.py:21
  2.2 5.6 %collective-permute-start = (bf16[64,256]{1,0:T(8,128)(2,1)S(1)}, bf16[64,256]{1,0:T(8,128)(2,1)S(1)}, u32[]{:S(2)}, u32[]{:S(2)}) collective-permute-start(bf16[64,256]{1,0:T(8,128)(2,1)S(1)} %get-tuple-element.244), channel_id=1, source_target_pairs={{0,4},{4,8},{8,12},{1,5},{5,9},{9,13},{2,6},{6,10},{10,14},{3,7},{... | collective-permute-start | bytes 98312 | tf_op jit(solution)/shard_map/ppermute | solution.py:20
  7.8 1.0 fusion.199
  8.8 0.9 fusion.200
  9.7 1.1 copy.30
  10.8 1.4 %fusion.202 = (s32[1]{0:T(128)}, s32[1]{0:T(128)}) fusion(s32[4]{0:T(128)} %param.36, s32[]{:T(128)} %bitcast.2, s32[]{:T(128)} %bitcast.6), kind=kLoop, calls=%fused_computation.337 | loop fusion | bytes 24 | tf_op jit(solution)/shard_map/jit(_take)/gather | solution.py:157
  13.7 0.7 convert_element_type.243
  14.7 1.7 %fusion.106 = f32[1,8,8,8,256]{4,3,2,1,0:T(8,128)S(1)} fusion(f32[1,10,10,10,256]{4,3,2,1,0:T(8,128)S(1)} %select_maximum_fusion, f32[1,1,8,8,256]{4,3,2,1,0:T(8,128)S(1)} %multiply_bitcast_fusion, f32[1,8,8,8,256]{4,3,2,1,0:T(8,128)S(1)} %bitcast.540, f32[1,1,8,8,256]{4,3,2,1,0:T(8,128)S(1)} %multiply_bitcast_fusion.1, f32[256]{0:T(256)S(1)} %bitcast.591, ...), kind=kLoop, calls=%fused_computation.142 | loop fusion | flops 7208960 | bytes 13790208 | tf_op jit(solution)/shard_map/add | solution.py:51
  16.7 2.0 %collective-permute-start.3 = (bf16[512,256]{0,1:T(8,128)(2,1)S(1)}, bf16[512,256]{0,1:T(8,128)(2,1)S(1)}, u32[]{:S(2)}, u32[]{:S(2)}) collective-permute-start(bf16[512,256]{0,1:T(8,128)(2,1)S(1)} %add_convert_fusion), channel_id=1, source_target_pairs={{0,2},{1,3},{2,0},{3,1},{4,6},{5,7},{6,4},{7,5},{8,10},{9,11},{10,... | collective-permute-start | bytes 786440 | tf_op jit(solution)/shard_map/ppermute | solution.py:97
  18.7 1.6 %collective-permute-start.2 = (bf16[512,256]{0,1:T(8,128)(2,1)S(1)}, bf16[512,256]{0,1:T(8,128)(2,1)S(1)}, u32[]{:S(2)}, u32[]{:S(2)}) collective-permute-start(bf16[512,256]{0,1:T(8,128)(2,1)S(1)} %add_convert_fusion), channel_id=1, source_target_pairs={{0,4},{4,8},{8,12},{12,0},{1,5},{5,9},{9,13},{13,1},{2,6},{6,10},{... | collective-permute-start | bytes 786440 | tf_op jit(solution)/shard_map/ppermute | solution.py:192
  20.3 4.3 %collective-permute-done.3 = bf16[512,256]{0,1:T(8,128)(2,1)S(1)} collective-permute-done((bf16[512,256]{0,1:T(8,128)(2,1)S(1)}, bf16[512,256]{0,1:T(8,128)(2,1)S(1)}, u32[]{:S(2)}, u32[]{:S(2)}) %collective-permute-start.3) | collective-permute-done | bytes 262176 | tf_op jit(solution)/shard_map/ppermute | solution.py:97
  24.6 0.8 pad_maximum_fusion.6
  25.4 2.3 %collective-permute-done.2 = bf16[512,256]{0,1:T(8,128)(2,1)S(1)} collective-permute-done((bf16[512,256]{0,1:T(8,128)(2,1)S(1)}, bf16[512,256]{0,1:T(8,128)(2,1)S(1)}, u32[]{:S(2)}, u32[]{:S(2)}) %collective-permute-start.2) | collective-permute-done | bytes 262176 | tf_op jit(solution)/shard_map/ppermute | solution.py:192
  28.1 0.6 fusion.201
  31.2 1.2 %copy.65 = bf16[1024,256]{1,0:T(8,128)(2,1)S(1)} copy(bf16[1024,256]{0,1:T(8,128)(2,1)} %bitcast.553) | data formatting | bytes 1048576 | tf_op jit(solution)/shard_map/dot_general | solution.py:249
  33.0 1.1 collective-permute-done.5
  34.2 1.0 select_bitcast_fusion.17
  35.2 1.3 %select_bitcast_fusion.7 = (bf16[512,2,1,256]{0,3,1,2:T(8,128)(2,1)S(1)}, bf16[512,2,1,256]{0,3,1,2:T(8,128)(2,1)S(1)}) fusion(bf16[512,2,256]{0,2,1:T(8,128)(2,1)} %pad_maximum_fusion.6, bf16[512,2,256]{0,2,1:T(8,128)(2,1)} %collective-permute-done.6, pred[]{:T(512)S(6)} %eq.9), kind=kLoop, calls=%fused_computation.226 | loop fusion | flops 524288 | bytes 2097153 | tf_op jit(solution)/shard_map/stack | solution.py:100
  36.7 6.3 %collective-permute-done.4 = bf16[512,256]{0,1:T(8,128)(2,1)S(1)} collective-permute-done((bf16[512,256]{0,1:T(8,128)(2,1)S(1)}, bf16[512,256]{0,1:T(8,128)(2,1)S(1)}, u32[]{:S(2)}, u32[]{:S(2)}) %collective-permute-start.4) | collective-permute-done | bytes 262176 | tf_op jit(solution)/shard_map/ppermute | solution.py:192
  43.0 1.6 %collective-permute-start.8 = (bf16[512,256]{0,1:T(8,128)(2,1)S(1)}, bf16[512,256]{0,1:T(8,128)(2,1)S(1)}, u32[]{:S(2)}, u32[]{:S(2)}) collective-permute-start(bf16[512,256]{0,1:T(8,128)(2,1)S(1)} %collective-permute-done.4), channel_id=1, source_target_pairs={{0,2},{1,3},{2,0},{3,1},{4,6},{5,7},{6,4},{7,5},{8,10},{9,11},{10,... | collective-permute-start | bytes 786440 | tf_op jit(solution)/shard_map/ppermute | solution.py:97
  45.2 0.6 convolution_convert_fusion.8
  45.9 0.6 convolution_convert_fusion.7
  46.9 0.6 convolution_convert_fusion.6
  47.6 0.8 bitcast_reduce_fusion.2
  48.4 0.8 fusion.4
  49.2 1.0 fusion.56
  51.0 1.2 collective-permute-done.9
  53.3 0.6 convolution_convert_fusion.5
  53.9 0.6 convolution_convert_fusion.4
  54.6 0.8 bitcast_reduce_fusion.1
  55.4 0.8 fusion.6
  56.2 1.0 fusion.53
  57.2 1.7 %collective-permute-start.10 = (bf16[512,256]{0,1:T(8,128)(2,1)S(1)}, bf16[512,256]{0,1:T(8,128)(2,1)S(1)}, u32[]{:S(2)}, u32[]{:S(2)}) collective-permute-start(bf16[512,256]{0,1:T(8,128)(2,1)S(1)} %collective-permute-done.7), channel_id=1, source_target_pairs={{0,2},{1,3},{2,0},{3,1},{4,6},{5,7},{6,4},{7,5},{8,10},{9,11},{10,... | collective-permute-start | bytes 786440 | tf_op jit(solution)/shard_map/ppermute | solution.py:97
  59.0 6.3 %collective-permute-done.10 = bf16[512,256]{0,1:T(8,128)(2,1)S(1)} collective-permute-done((bf16[512,256]{0,1:T(8,128)(2,1)S(1)}, bf16[512,256]{0,1:T(8,128)(2,1)S(1)}, u32[]{:S(2)}, u32[]{:S(2)}) %collective-permute-start.10) | collective-permute-done | bytes 262176 | tf_op jit(solution)/shard_map/ppermute | solution.py:97
  66.3 0.6 convolution_convert_fusion.3
  66.9 0.6 convolution_convert_fusion.2
  67.7 1.0 bitcast_reduce_fusion
  68.7 0.8 fusion.8
  69.6 1.0 fusion.59
  71.4 0.6 convolution_convert_fusion
  72.1 0.6 convolution_convert_fusion.1
  77.3 0.7 collective-permute-start.14
  78.6 0.8 bitcast_add_fusion.1
  79.4 1.0 fusion.164
  80.4 0.9 collective-permute-start.20
  81.3 1.8 %collective-permute-done.14 = bf16[256,256]{0,1:T(8,128)(2,1)S(1)} collective-permute-done((bf16[256,256]{0,1:T(8,128)(2,1)S(1)}, bf16[256,256]{0,1:T(8,128)(2,1)S(1)}, u32[]{:S(2)}, u32[]{:S(2)}) %collective-permute-start.14) | collective-permute-done | bytes 131104 | tf_op jit(solution)/shard_map/ppermute | solution.py:72
  83.2 2.8 %collective-permute-done.20 = bf16[256,256]{0,1:T(8,128)(2,1)S(1)} collective-permute-done((bf16[256,256]{0,1:T(8,128)(2,1)S(1)}, bf16[256,256]{0,1:T(8,128)(2,1)S(1)}, u32[]{:S(2)}, u32[]{:S(2)}) %collective-permute-start.20) | collective-permute-done | bytes 131104 | tf_op jit(solution)/shard_map/ppermute | solution.py:72
  86.0 1.0 fusion.153
  87.1 0.9 collective-permute-start.21
  87.9 1.2 %collective-permute-start.15 = (bf16[256,256]{0,1:T(8,128)(2,1)S(1)}, bf16[256,256]{0,1:T(8,128)(2,1)S(1)}, u32[]{:S(2)}, u32[]{:S(2)}) collective-permute-start(bf16[256,256]{0,1:T(8,128)(2,1)S(1)} %get-tuple-element.240), channel_id=1, source_target_pairs={{0,2},{1,3},{2,0},{3,1},{4,6},{5,7},{6,4},{7,5},{8,10},{9,11},{10,... | collective-permute-start | bytes 393224 | tf_op jit(solution)/shard_map/ppermute | solution.py:86
  89.1 4.1 %collective-permute-done.21 = bf16[256,256]{0,1:T(8,128)(2,1)S(1)} collective-permute-done((bf16[256,256]{0,1:T(8,128)(2,1)S(1)}, bf16[256,256]{0,1:T(8,128)(2,1)S(1)}, u32[]{:S(2)}, u32[]{:S(2)}) %collective-permute-start.21) | collective-permute-done | bytes 131104 | tf_op jit(solution)/shard_map/ppermute | solution.py:86
  93.4 1.3 %collective-permute-done.15 = bf16[256,256]{0,1:T(8,128)(2,1)S(1)} collective-permute-done((bf16[256,256]{0,1:T(8,128)(2,1)S(1)}, bf16[256,256]{0,1:T(8,128)(2,1)S(1)}, u32[]{:S(2)}, u32[]{:S(2)}) %collective-permute-start.15) | collective-permute-done | bytes 131104 | tf_op jit(solution)/shard_map/ppermute | solution.py:86
  94.9 1.4 %collective-permute-done.16 = bf16[256,2,256]{0,2,1:T(8,128)(2,1)S(1)} collective-permute-done((bf16[256,2,256]{0,2,1:T(8,128)(2,1)S(1)}, bf16[256,2,256]{0,2,1:T(8,128)(2,1)S(1)}, u32[]{:S(2)}, u32[]{:S(2)}) %collective-permute-start.16) | collective-permute-done | bytes 262176 | tf_op jit(solution)/shard_map/ppermute | solution.py:86
  97.8 4.2 %fusion.102 = f32[256,1024]{0,1:T(8,128)} fusion(bf16[1024,1024]{1,0:T(8,128)(2,1)S(1)} %copy-done, bf16[256,1024]{0,1:T(8,128)(2,1)S(1)} %get-tuple-element.280, bf16[1024,1024]{1,0:T(8,128)(2,1)} %param.46), kind=kOutput, calls=%fused_computation.139 | convolution fusion | flops 1076101120 | bytes 5767168 | tf_op jit(solution)/shard_map/dot_general | solution.py:257
  102.0 1.1 fusion.145
  103.2 4.2 %fusion.104 = f32[256,1024]{0,1:T(8,128)} fusion(bf16[1024,1024]{1,0:T(8,128)(2,1)S(1)} %copy-done, bf16[256,1024]{0,1:T(8,128)(2,1)S(1)} %get-tuple-element.279, bf16[1024,1024]{1,0:T(8,128)(2,1)} %param.46), kind=kOutput, calls=%fused_computation.140 | convolution fusion | flops 1076101120 | bytes 5767168 | tf_op jit(solution)/shard_map/dot_general | solution.py:257
  107.5 1.2 fusion.144
  109.1 1.1 bitcast_add_fusion
  110.2 0.8 collective-permute-start.24
  111.1 1.4 %collective-permute-start.18 = (bf16[256,256]{0,1:T(8,128)(2,1)S(1)}, bf16[256,256]{0,1:T(8,128)(2,1)S(1)}, u32[]{:S(2)}, u32[]{:S(2)}) collective-permute-start(bf16[256,256]{0,1:T(8,128)(2,1)S(1)} %fusion.163), channel_id=1, source_target_pairs={{0,2},{1,3},{2,0},{3,1},{4,6},{5,7},{6,4},{7,5},{8,10},{9,11},{10,... | collective-permute-start | bytes 393224 | tf_op jit(solution)/shard_map/ppermute | solution.py:72
  112.5 4.1 %collective-permute-done.24 = bf16[256,256]{0,1:T(8,128)(2,1)S(1)} collective-permute-done((bf16[256,256]{0,1:T(8,128)(2,1)S(1)}, bf16[256,256]{0,1:T(8,128)(2,1)S(1)}, u32[]{:S(2)}, u32[]{:S(2)}) %collective-permute-start.24) | collective-permute-done | bytes 131104 | tf_op jit(solution)/shard_map/ppermute | solution.py:72
  116.7 1.9 %collective-permute-done.18 = bf16[256,256]{0,1:T(8,128)(2,1)S(1)} collective-permute-done((bf16[256,256]{0,1:T(8,128)(2,1)S(1)}, bf16[256,256]{0,1:T(8,128)(2,1)S(1)}, u32[]{:S(2)}, u32[]{:S(2)}) %collective-permute-start.18) | collective-permute-done | bytes 131104 | tf_op jit(solution)/shard_map/ppermute | solution.py:72
  118.7 0.8 copy.53
  (131 shorter events, 14.6 us)
Async XLA Ops:
  0.0 97.8 %copy-start = (bf16[1024,1024]{1,0:T(8,128)(2,1)S(1)}, bf16[1024,1024]{1,0:T(8,128)(2,1)}, u32[]{:S(2)}) copy-start(bf16[1024,1024]{1,0:T(8,128)(2,1)} %param.47) | copy-start | bytes 6291460
  0.9 13.4 %collective-permute-start.1 = (bf16[64,256]{1,0:T(8,128)(2,1)S(1)}, bf16[64,256]{1,0:T(8,128)(2,1)S(1)}, u32[]{:S(2)}, u32[]{:S(2)}) collective-permute-start(bf16[64,256]{1,0:T(8,128)(2,1)S(1)} %get-tuple-element.245), channel_id=1, source_target_pairs={{4,0},{8,4},{12,8},{5,1},{9,5},{13,9},{6,2},{10,6},{14,10},{7,3},{... | collective-permute-start | bytes 98312 | tf_op jit(solution)/shard_map/ppermute | solution.py:21
  2.2 12.2 %collective-permute-start = (bf16[64,256]{1,0:T(8,128)(2,1)S(1)}, bf16[64,256]{1,0:T(8,128)(2,1)S(1)}, u32[]{:S(2)}, u32[]{:S(2)}) collective-permute-start(bf16[64,256]{1,0:T(8,128)(2,1)S(1)} %get-tuple-element.244), channel_id=1, source_target_pairs={{0,4},{4,8},{8,12},{1,5},{5,9},{9,13},{2,6},{6,10},{10,14},{3,7},{... | collective-permute-start | bytes 98312 | tf_op jit(solution)/shard_map/ppermute | solution.py:20
  16.3 11.7 %copy-start.2 = (bf16[1024]{0:T(1024)(128)(2,1)S(1)}, bf16[1024]{0:T(1024)(128)(2,1)}, u32[]{:S(2)}) copy-start(bf16[1024]{0:T(1024)(128)(2,1)} %param.40) | copy-start | bytes 6148
  16.3 11.7 %copy-start.4 = (s32[4,4]{1,0:T(4,128)S(1)}, s32[4,4]{1,0:T(4,128)}, u32[]{:S(2)}) copy-start(s32[4,4]{1,0:T(4,128)} %param.37) | copy-start | bytes 196
  16.7 7.8 %collective-permute-start.3 = (bf16[512,256]{0,1:T(8,128)(2,1)S(1)}, bf16[512,256]{0,1:T(8,128)(2,1)S(1)}, u32[]{:S(2)}, u32[]{:S(2)}) collective-permute-start(bf16[512,256]{0,1:T(8,128)(2,1)S(1)} %add_convert_fusion), channel_id=1, source_target_pairs={{0,2},{1,3},{2,0},{3,1},{4,6},{5,7},{6,4},{7,5},{8,10},{9,11},{10,... | collective-permute-start | bytes 786440 | tf_op jit(solution)/shard_map/ppermute | solution.py:97
  18.7 9.0 %collective-permute-start.2 = (bf16[512,256]{0,1:T(8,128)(2,1)S(1)}, bf16[512,256]{0,1:T(8,128)(2,1)S(1)}, u32[]{:S(2)}, u32[]{:S(2)}) collective-permute-start(bf16[512,256]{0,1:T(8,128)(2,1)S(1)} %add_convert_fusion), channel_id=1, source_target_pairs={{0,4},{4,8},{8,12},{12,0},{1,5},{5,9},{9,13},{13,1},{2,6},{6,10},{... | collective-permute-start | bytes 786440 | tf_op jit(solution)/shard_map/ppermute | solution.py:192
  27.7 6.5 %collective-permute-start.5 = (bf16[512,256]{0,1:T(8,128)(2,1)S(1)}, bf16[512,256]{0,1:T(8,128)(2,1)}, u32[]{:S(2)}, u32[]{:S(2)}) collective-permute-start(bf16[512,256]{0,1:T(8,128)(2,1)S(1)} %collective-permute-done.2), channel_id=1, source_target_pairs={{0,2},{1,3},{2,0},{3,1},{4,6},{5,7},{6,4},{7,5},{8,10},{9,11},{10,... | collective-permute-start | bytes 786440 | tf_op jit(solution)/shard_map/ppermute | solution.py:97
  28.1 7.2 %collective-permute-start.6 = (bf16[512,2,256]{0,2,1:T(8,128)(2,1)}, bf16[512,2,256]{0,2,1:T(8,128)(2,1)}, u32[]{:S(2)}, u32[]{:S(2)}) collective-permute-start(bf16[512,2,256]{0,2,1:T(8,128)(2,1)} %pad_maximum_fusion.6), channel_id=1, source_target_pairs={{0,1},{1,0},{2,3},{3,2},{4,5},{5,4},{6,7},{7,6},{8,9},{9,8},{10,11... | collective-permute-start | bytes 1572872 | tf_op jit(solution)/shard_map/ppermute | solution.py:97
  32.4 10.5 %collective-permute-start.4 = (bf16[512,256]{0,1:T(8,128)(2,1)S(1)}, bf16[512,256]{0,1:T(8,128)(2,1)S(1)}, u32[]{:S(2)}, u32[]{:S(2)}) collective-permute-start(bf16[512,256]{0,1:T(8,128)(2,1)S(1)} %collective-permute-done.2), channel_id=1, source_target_pairs={{0,4},{4,8},{8,12},{12,0},{1,5},{5,9},{9,13},{13,1},{2,6},{6,10},{... | collective-permute-start | bytes 786440 | tf_op jit(solution)/shard_map/ppermute | solution.py:192
  36.6 8.6 %copy-start.7 = (bf16[1024,256]{1,0:T(8,128)(2,1)S(1)}, bf16[1024,256]{1,0:T(8,128)(2,1)}, u32[]{:S(2)}) copy-start(bf16[1024,256]{1,0:T(8,128)(2,1)} %param.42) | copy-start | bytes 1572868
  43.0 9.7 %collective-permute-start.7 = (bf16[512,256]{0,1:T(8,128)(2,1)S(1)}, bf16[512,256]{0,1:T(8,128)(2,1)S(1)}, u32[]{:S(2)}, u32[]{:S(2)}) collective-permute-start(bf16[512,256]{0,1:T(8,128)(2,1)S(1)} %collective-permute-done.4), channel_id=1, source_target_pairs={{0,4},{4,8},{8,12},{12,0},{1,5},{5,9},{9,13},{13,1},{2,6},{6,10},{... | collective-permute-start | bytes 786440 | tf_op jit(solution)/shard_map/ppermute | solution.py:192
  43.0 7.9 %collective-permute-start.8 = (bf16[512,256]{0,1:T(8,128)(2,1)S(1)}, bf16[512,256]{0,1:T(8,128)(2,1)S(1)}, u32[]{:S(2)}, u32[]{:S(2)}) collective-permute-start(bf16[512,256]{0,1:T(8,128)(2,1)S(1)} %collective-permute-done.4), channel_id=1, source_target_pairs={{0,2},{1,3},{2,0},{3,1},{4,6},{5,7},{6,4},{7,5},{8,10},{9,11},{10,... | collective-permute-start | bytes 786440 | tf_op jit(solution)/shard_map/ppermute | solution.py:97
  44.8 1.0 copy-start.5
  45.9 1.0 copy-start.6
  50.2 2.0 %collective-permute-start.9 = (bf16[512,2,256]{0,2,1:T(8,128)(2,1)S(1)}, bf16[512,2,256]{0,2,1:T(8,128)(2,1)S(1)}, u32[]{:S(2)}, u32[]{:S(2)}) collective-permute-start(bf16[512,2,256]{0,2,1:T(8,128)(2,1)S(1)} %pad_maximum_fusion.7), channel_id=1, source_target_pairs={{0,1},{1,0},{2,3},{3,2},{4,5},{5,4},{6,7},{7,6},{8,9},{9,8},{10,11... | collective-permute-start | bytes 1572872 | tf_op jit(solution)/shard_map/ppermute | solution.py:97
  57.2 8.2 %collective-permute-start.10 = (bf16[512,256]{0,1:T(8,128)(2,1)S(1)}, bf16[512,256]{0,1:T(8,128)(2,1)S(1)}, u32[]{:S(2)}, u32[]{:S(2)}) collective-permute-start(bf16[512,256]{0,1:T(8,128)(2,1)S(1)} %collective-permute-done.7), channel_id=1, source_target_pairs={{0,2},{1,3},{2,0},{3,1},{4,6},{5,7},{6,4},{7,5},{8,10},{9,11},{10,... | collective-permute-start | bytes 786440 | tf_op jit(solution)/shard_map/ppermute | solution.py:97
  58.9 6.6 %collective-permute-start.11 = (bf16[512,2,256]{0,2,1:T(8,128)(2,1)S(1)}, bf16[512,2,256]{0,2,1:T(8,128)(2,1)S(1)}, u32[]{:S(2)}, u32[]{:S(2)}) collective-permute-start(bf16[512,2,256]{0,2,1:T(8,128)(2,1)S(1)} %pad_maximum_fusion.8), channel_id=1, source_target_pairs={{0,1},{1,0},{2,3},{3,2},{4,5},{5,4},{6,7},{7,6},{8,9},{9,8},{10,11... | collective-permute-start | bytes 1572872 | tf_op jit(solution)/shard_map/ppermute | solution.py:97
  67.6 3.0 %collective-permute-start.12 = (bf16[512,2,256]{0,2,1:T(8,128)(2,1)S(1)}, bf16[512,2,256]{0,2,1:T(8,128)(2,1)S(1)}, u32[]{:S(2)}, u32[]{:S(2)}) collective-permute-start(bf16[512,2,256]{0,2,1:T(8,128)(2,1)S(1)} %pad_maximum_fusion.9), channel_id=1, source_target_pairs={{0,1},{1,0},{2,3},{3,2},{4,5},{5,4},{6,7},{7,6},{8,9},{9,8},{10,11... | collective-permute-start | bytes 1572872 | tf_op jit(solution)/shard_map/ppermute | solution.py:97
  75.5 1.7 %collective-permute-start.13 = (bf16[256,2,256]{0,2,1:T(8,128)(2,1)S(1)}, bf16[256,2,256]{0,2,1:T(8,128)(2,1)S(1)}, u32[]{:S(2)}, u32[]{:S(2)}) collective-permute-start(bf16[256,2,256]{0,2,1:T(8,128)(2,1)S(1)} %fusion.142), channel_id=1, source_target_pairs={{0,1},{1,0},{2,3},{3,2},{4,5},{5,4},{6,7},{7,6},{8,9},{9,8},{10,11... | collective-permute-start | bytes 786440 | tf_op jit(solution)/shard_map/ppermute | solution.py:72
  77.0 1.6 %collective-permute-start.19 = (bf16[256,2,256]{0,2,1:T(8,128)(2,1)S(1)}, bf16[256,2,256]{0,2,1:T(8,128)(2,1)S(1)}, u32[]{:S(2)}, u32[]{:S(2)}) collective-permute-start(bf16[256,2,256]{0,2,1:T(8,128)(2,1)S(1)} %fusion.143), channel_id=1, source_target_pairs={{0,1},{1,0},{2,3},{3,2},{4,5},{5,4},{6,7},{7,6},{8,9},{9,8},{10,11... | collective-permute-start | bytes 786440 | tf_op jit(solution)/shard_map/ppermute | solution.py:72
  77.3 5.8 %collective-permute-start.14 = (bf16[256,256]{0,1:T(8,128)(2,1)S(1)}, bf16[256,256]{0,1:T(8,128)(2,1)S(1)}, u32[]{:S(2)}, u32[]{:S(2)}) collective-permute-start(bf16[256,256]{0,1:T(8,128)(2,1)S(1)} %fusion.162), channel_id=1, source_target_pairs={{0,2},{1,3},{2,0},{3,1},{4,6},{5,7},{6,4},{7,5},{8,10},{9,11},{10,... | collective-permute-start | bytes 393224 | tf_op jit(solution)/shard_map/ppermute | solution.py:72
  79.4 15.4 %copy-start.3 = (bf16[1024]{0:T(1024)(128)(2,1)S(1)}, bf16[1024]{0:T(1024)(128)(2,1)}, u32[]{:S(2)}) copy-start(bf16[1024]{0:T(1024)(128)(2,1)} %param.45) | copy-start | bytes 6148
  80.4 5.6 %collective-permute-start.20 = (bf16[256,256]{0,1:T(8,128)(2,1)S(1)}, bf16[256,256]{0,1:T(8,128)(2,1)S(1)}, u32[]{:S(2)}, u32[]{:S(2)}) collective-permute-start(bf16[256,256]{0,1:T(8,128)(2,1)S(1)} %fusion.164), channel_id=1, source_target_pairs={{0,2},{1,3},{2,0},{3,1},{4,6},{5,7},{6,4},{7,5},{8,10},{9,11},{10,... | collective-permute-start | bytes 393224 | tf_op jit(solution)/shard_map/ppermute | solution.py:72
  87.1 6.2 %collective-permute-start.21 = (bf16[256,256]{0,1:T(8,128)(2,1)S(1)}, bf16[256,256]{0,1:T(8,128)(2,1)S(1)}, u32[]{:S(2)}, u32[]{:S(2)}) collective-permute-start(bf16[256,256]{0,1:T(8,128)(2,1)S(1)} %get-tuple-element.241), channel_id=1, source_target_pairs={{0,2},{1,3},{2,0},{3,1},{4,6},{5,7},{6,4},{7,5},{8,10},{9,11},{10,... | collective-permute-start | bytes 393224 | tf_op jit(solution)/shard_map/ppermute | solution.py:86
  87.9 6.7 %collective-permute-start.15 = (bf16[256,256]{0,1:T(8,128)(2,1)S(1)}, bf16[256,256]{0,1:T(8,128)(2,1)S(1)}, u32[]{:S(2)}, u32[]{:S(2)}) collective-permute-start(bf16[256,256]{0,1:T(8,128)(2,1)S(1)} %get-tuple-element.240), channel_id=1, source_target_pairs={{0,2},{1,3},{2,0},{3,1},{4,6},{5,7},{6,4},{7,5},{8,10},{9,11},{10,... | collective-permute-start | bytes 393224 | tf_op jit(solution)/shard_map/ppermute | solution.py:86
  93.3 1.6 %collective-permute-start.22 = (bf16[256,2,256]{0,2,1:T(8,128)(2,1)S(1)}, bf16[256,2,256]{0,2,1:T(8,128)(2,1)S(1)}, u32[]{:S(2)}, u32[]{:S(2)}) collective-permute-start(bf16[256,2,256]{0,2,1:T(8,128)(2,1)S(1)} %pad_maximum_fusion.11), channel_id=1, source_target_pairs={{0,1},{1,0},{2,3},{3,2},{4,5},{5,4},{6,7},{7,6},{8,9},{9,8},{10,11... | collective-permute-start | bytes 786440 | tf_op jit(solution)/shard_map/ppermute | solution.py:86
  94.7 1.6 %collective-permute-start.16 = (bf16[256,2,256]{0,2,1:T(8,128)(2,1)S(1)}, bf16[256,2,256]{0,2,1:T(8,128)(2,1)S(1)}, u32[]{:S(2)}, u32[]{:S(2)}) collective-permute-start(bf16[256,2,256]{0,2,1:T(8,128)(2,1)S(1)} %pad_maximum_fusion.10), channel_id=1, source_target_pairs={{0,1},{1,0},{2,3},{3,2},{4,5},{5,4},{6,7},{7,6},{8,9},{9,8},{10,11... | collective-permute-start | bytes 786440 | tf_op jit(solution)/shard_map/ppermute | solution.py:86
  103.0 6.0 %collective-permute-start.23 = (bf16[256,2,256]{0,2,1:T(8,128)(2,1)S(1)}, bf16[256,2,256]{0,2,1:T(8,128)(2,1)S(1)}, u32[]{:S(2)}, u32[]{:S(2)}) collective-permute-start(bf16[256,2,256]{0,2,1:T(8,128)(2,1)S(1)} %fusion.145), channel_id=1, source_target_pairs={{0,1},{1,0},{2,3},{3,2},{4,5},{5,4},{6,7},{7,6},{8,9},{9,8},{10,11... | collective-permute-start | bytes 786440 | tf_op jit(solution)/shard_map/ppermute | solution.py:72
  107.5 3.5 %copy-start.1 = (f32[256,1024]{0,1:T(8,128)S(1)}, f32[256,1024]{0,1:T(8,128)}, u32[]{:S(2)}) copy-start(f32[256,1024]{0,1:T(8,128)} %fusion.104) | copy-start | bytes 3145732
  108.6 2.4 %collective-permute-start.17 = (bf16[256,2,256]{0,2,1:T(8,128)(2,1)S(1)}, bf16[256,2,256]{0,2,1:T(8,128)(2,1)S(1)}, u32[]{:S(2)}, u32[]{:S(2)}) collective-permute-start(bf16[256,2,256]{0,2,1:T(8,128)(2,1)S(1)} %fusion.144), channel_id=1, source_target_pairs={{0,1},{1,0},{2,3},{3,2},{4,5},{5,4},{6,7},{7,6},{8,9},{9,8},{10,11... | collective-permute-start | bytes 786440 | tf_op jit(solution)/shard_map/ppermute | solution.py:72
  110.2 6.4 %collective-permute-start.24 = (bf16[256,256]{0,1:T(8,128)(2,1)S(1)}, bf16[256,256]{0,1:T(8,128)(2,1)S(1)}, u32[]{:S(2)}, u32[]{:S(2)}) collective-permute-start(bf16[256,256]{0,1:T(8,128)(2,1)S(1)} %fusion.165), channel_id=1, source_target_pairs={{0,2},{1,3},{2,0},{3,1},{4,6},{5,7},{6,4},{7,5},{8,10},{9,11},{10,... | collective-permute-start | bytes 393224 | tf_op jit(solution)/shard_map/ppermute | solution.py:72
  111.1 7.5 %collective-permute-start.18 = (bf16[256,256]{0,1:T(8,128)(2,1)S(1)}, bf16[256,256]{0,1:T(8,128)(2,1)S(1)}, u32[]{:S(2)}, u32[]{:S(2)}) collective-permute-start(bf16[256,256]{0,1:T(8,128)(2,1)S(1)} %fusion.163), channel_id=1, source_target_pairs={{0,2},{1,3},{2,0},{3,1},{4,6},{5,7},{6,4},{7,5},{8,10},{9,11},{10,... | collective-permute-start | bytes 393224 | tf_op jit(solution)/shard_map/ppermute | solution.py:72

commit v16 on v15

--- a/solution.py
+++ b/solution.py
@@ -242,21 +242,40 @@
         attended = weighted / jnp.transpose(row_mass, (0, 2, 1))[:, :, :, None]
         attended_parts.append(attended.astype(jnp.bfloat16).reshape(-1, local_width))
     attended = jnp.concatenate(attended_parts, axis=0) if not split_last else None
-    outputs = []
-    for chunk in range(chunk_count):
-        rows = slice(chunk * chunk_rows, (chunk + 1) * chunk_rows)
-        attended_rows = attended_parts[chunk] if split_last else attended[rows]
-        partial_out = jnp.dot(attended_rows, out_weight, preferred_element_type=jnp.float32)
-        out_sum = scatter_heads(partial_out, head_id, head_total)
-        stream_two = (stream[rows].astype(jnp.float32) + out_sum).astype(jnp.bfloat16)
-        stream_two_full = gather_heads(stream_two, head_id, head_total)
-        normed_two = layer_norm(stream_two_full, gain_two).astype(jnp.bfloat16)
-        hidden = jax.nn.gelu(
-            jnp.dot(normed_two, up_weight, preferred_element_type=jnp.float32), approximate=True
-        ).astype(jnp.bfloat16)
-        lowered = jnp.dot(hidden, down_weight, preferred_element_type=jnp.float32)
-        mixed = scatter_heads(lowered, head_id, head_total)
-        outputs.append((stream_two.astype(jnp.float32) + mixed).astype(jnp.bfloat16))
+    held = [{} for _ in range(chunk_count)]
+    for slot in range(chunk_count + 3):
+        made = []
+        for chunk in range(chunk_count):
+            stage = slot - chunk
+            rows = slice(chunk * chunk_rows, (chunk + 1) * chunk_rows)
+            box = held[chunk]
+            if stage == 0:
+                attended_rows = attended_parts[chunk] if split_last else attended[rows]
+                partial_out = jnp.dot(
+                    attended_rows, out_weight, preferred_element_type=jnp.float32
+                )
+                out_sum = scatter_heads(partial_out, head_id, head_total)
+                box["two"] = (stream[rows].astype(jnp.float32) + out_sum).astype(jnp.bfloat16)
+                made.append((box, "two"))
+            elif stage == 1:
+                box["full"] = gather_heads(box["two"], head_id, head_total)
+                made.append((box, "full"))
+            elif stage == 2:
+                normed_two = layer_norm(box["full"], gain_two).astype(jnp.bfloat16)
+                hidden = jax.nn.gelu(
+                    jnp.dot(normed_two, up_weight, preferred_element_type=jnp.float32),
+                    approximate=True,
+                ).astype(jnp.bfloat16)
+                box["low"] = jnp.dot(hidden, down_weight, preferred_element_type=jnp.float32)
+                made.append((box, "low"))
+            elif stage == 3:
+                mixed = scatter_heads(box["low"], head_id, head_total)
+                box["out"] = (box["two"].astype(jnp.float32) + mixed).astype(jnp.bfloat16)
+        if made and slot < chunk_count + 2:
+            packed = lax.optimization_barrier([table[key] for table, key in made])
+            for (table, key), value in zip(made, packed):
+                table[key] = value
+    outputs = [box["out"] for box in held]
     return jnp.concatenate(outputs, axis=0)
 
 def solution(mesh):

time: 120 us -> 152 us (1.27)
  local copies, waits for them, and re-layouts: 12.7 us -> 32 us
  other arithmetic: 17.2 us -> 27.4 us
  waiting for transfers between devices: 40.5 us -> 43.7 us
  starting transfers between devices: 22.2 us -> 20.1 us
    dynamic_slice x0 -> x6, local copies, waits for them, and re-layouts: none -> 7.25 us  [the longest x4 5.79 us: scatter_heads(): keep = lax.dynamic_index_in_dim(current, mine, axis, keepdims=False)]
    another operation x16, other arithmetic: 3.99 us -> 10.4 us  [gather_levels(): current = jnp.stack([low, high], axis=current.ndim - 1)]
    another operation x4, local copies, waits for them, and re-layouts: 0.28 us -> 6.22 us  [gather_levels(): current = jnp.stack([low, high], axis=current.ndim - 1)]
    unnamed x17 -> x54, local copies, waits for them, and re-layouts: 1.54 us -> 6.58 us
    ppermute x4, waiting for transfers between devices: 6.85 us -> 11.2 us  [gather_heads(): lax.ppermute(current, 'heads', [(i, i ^ bit) for i in range(head_total)])]
    optimization_barrier x0 -> x2, local copies, waits for them, and re-layouts: none -> 3.11 us  [shards(): packed = lax.optimization_barrier([table[key] for table, key in made])]
    convert_element_type x8 -> x6, local copies, waits for them, and re-layouts: 3.34 us -> 1.46 us  [scatter_heads(): give.astype(jnp.bfloat16)]
    add x2, other arithmetic: 0.21 us -> 1.83 us  [absorb_block(): weighted * jnp.transpose(factor, (0, 2, 1))[..., None]]
  transfers between devices with their start and end apart: 25 -> 25, of which waited for: 18 -> 14; matrix products, arithmetic and copies ran while one was open for 24% -> 31% of each run, Pallas kernels for 0% -> 0%
where the time goes in v16:
time: 152 us; the launch traced here: 151 us
  waiting for transfers between devices  43.7 us (29%)
  local copies, waits for them, and re-layouts  32 us (21%)
  other arithmetic  27.4 us (18%)
  matrix products  23 us (15%)
  starting transfers between devices  20.1 us (13%)
  between operations  4.48 us (3%)
    ppermute x8, waiting for transfers between devices, scatter_heads(): lax.ppermute(give.astype(jnp.bfloat16), 'heads', [(i, i ^ bit) for i in r...  12.3 us
    ppermute x8, waiting for transfers between devices, gather_levels(): lax.ppermute(current, 'heads', [(i, i ^ bit) for i in range(head_total)])  11.9 us
    ppermute x4, waiting for transfers between devices, gather_heads(): lax.ppermute(current, 'heads', [(i, i ^ bit) for i in range(head_total)])  11.2 us
    another operation x16, other arithmetic, gather_levels(): current = jnp.stack([low, high], axis=current.ndim - 1)  10.4 us
    dot_general x2, matrix products, shards(): jnp.dot(hidden, down_weight, preferred_element_type=jnp.float32)  8.35 us
    ppermute x3, waiting for transfers between devices, shards(): ringed[slot + 1] = lax.ppermute(ringed[slot], 'bricks', ring)  8.22 us
    unnamed x54, local copies, waits for them, and re-layouts  6.58 us
    another operation x4, local copies, waits for them, and re-layouts, gather_levels(): current = jnp.stack([low, high], axis=current.ndim - 1)  6.22 us
  transfers between devices with their start and end apart: 25, of which 14 were waited for; matrix products, arithmetic and copies ran while one was open for 31% of the time, Pallas kernels for 0%

profile of v16, /device:TPU:0, one launch (start us, length us, event | category | flops | bytes accessed | tf_op | source)
XLA Modules:
  0.0 150.7 jit_solution(17177784537216405011)
XLA Ops:
  0.0 0.9 fusion.224
  0.9 1.3 collective-permute-start.1
  2.2 5.6 %collective-permute-start = (bf16[64,256]{1,0:T(8,128)(2,1)S(1)}, bf16[64,256]{1,0:T(8,128)(2,1)S(1)}, u32[]{:S(2)}, u32[]{:S(2)}) collective-permute-start(bf16[64,256]{1,0:T(8,128)(2,1)S(1)} %get-tuple-element.252), channel_id=1, source_target_pairs={{0,4},{4,8},{8,12},{1,5},{5,9},{9,13},{2,6},{6,10},{10,14},{3,7},{... | collective-permute-start | bytes 98312 | tf_op jit(solution)/shard_map/ppermute | solution.py:20
  7.8 1.0 fusion.225
  8.8 0.9 fusion.226
  9.7 1.4 fusion.228
  11.7 1.0 convert
  14.3 1.6 %fusion.122 = f32[1,8,8,8,256]{4,3,2,1,0:T(8,128)S(1)} fusion(f32[1,10,10,10,256]{4,3,2,1,0:T(8,128)S(1)} %select_maximum_fusion, f32[1,1,8,8,256]{4,3,2,1,0:T(8,128)S(1)} %multiply_bitcast_fusion, f32[1,8,8,8,256]{4,3,2,1,0:T(8,128)S(1)} %convert, f32[1,1,8,8,256]{4,3,2,1,0:T(8,128)S(1)} %multiply_bitcast_fusion.1, f32[256]{0:T(256)S(1)} %bitcast.581, ...), kind=kLoop, calls=%fused_computation.148 | loop fusion | flops 7208960 | bytes 13790208 | tf_op jit(solution)/shard_map/add | solution.py:51
  16.1 2.0 %collective-permute-start.3 = (bf16[512,256]{1,0:T(8,128)(2,1)S(1)}, bf16[512,256]{1,0:T(8,128)(2,1)S(1)}, u32[]{:S(2)}, u32[]{:S(2)}) collective-permute-start(bf16[512,256]{1,0:T(8,128)(2,1)S(1)} %fusion.151), channel_id=1, source_target_pairs={{0,2},{1,3},{2,0},{3,1},{4,6},{5,7},{6,4},{7,5},{8,10},{9,11},{10,... | collective-permute-start | bytes 786440 | tf_op jit(solution)/shard_map/ppermute | solution.py:97
  18.1 1.6 %collective-permute-start.2 = (bf16[512,256]{1,0:T(8,128)(2,1)S(1)}, bf16[512,256]{1,0:T(8,128)(2,1)}, u32[]{:S(2)}, u32[]{:S(2)}) collective-permute-start(bf16[512,256]{1,0:T(8,128)(2,1)S(1)} %fusion.151), channel_id=1, source_target_pairs={{0,4},{4,8},{8,12},{12,0},{1,5},{5,9},{9,13},{13,1},{2,6},{6,10},{... | collective-permute-start | bytes 786440 | tf_op jit(solution)/shard_map/ppermute | solution.py:192
  19.6 4.3 %collective-permute-done.3 = bf16[512,256]{1,0:T(8,128)(2,1)S(1)} collective-permute-done((bf16[512,256]{1,0:T(8,128)(2,1)S(1)}, bf16[512,256]{1,0:T(8,128)(2,1)S(1)}, u32[]{:S(2)}, u32[]{:S(2)}) %collective-permute-start.3) | collective-permute-done | bytes 262176 | tf_op jit(solution)/shard_map/ppermute | solution.py:97
  24.0 3.2 %collective-permute-done.2 = bf16[512,256]{1,0:T(8,128)(2,1)} collective-permute-done((bf16[512,256]{1,0:T(8,128)(2,1)S(1)}, bf16[512,256]{1,0:T(8,128)(2,1)}, u32[]{:S(2)}, u32[]{:S(2)}) %collective-permute-start.2) | collective-permute-done | bytes 262176 | tf_op jit(solution)/shard_map/ppermute | solution.py:192
  30.6 2.1 %copy.55 = bf16[1024,256]{1,0:T(8,128)(2,1)} copy(bf16[1024,256]{0,1:T(8,128)(2,1)} %bitcast.541) | data formatting | bytes 1048576 | tf_op jit(solution)/shard_map/dot_general | solution.py:254
  32.7 1.2 collective-permute-done.5
  33.9 1.1 select_bitcast_fusion.17
  34.9 0.8 pad_maximum_fusion.7
  35.9 1.1 pad_maximum_fusion
  36.9 1.5 copy.24
  38.5 5.0 %collective-permute-done.4 = bf16[512,256]{1,0:T(8,128)(2,1)} collective-permute-done((bf16[512,256]{1,0:T(8,128)(2,1)}, bf16[512,256]{1,0:T(8,128)(2,1)}, u32[]{:S(2)}, u32[]{:S(2)}) %collective-permute-start.4) | collective-permute-done | bytes 262176 | tf_op jit(solution)/shard_map/ppermute | solution.py:192
  43.5 1.6 %collective-permute-start.8 = (bf16[512,256]{1,0:T(8,128)(2,1)}, bf16[512,256]{1,0:T(8,128)(2,1)S(1)}, u32[]{:S(2)}, u32[]{:S(2)}) collective-permute-start(bf16[512,256]{1,0:T(8,128)(2,1)} %collective-permute-done.4), channel_id=1, source_target_pairs={{0,2},{1,3},{2,0},{3,1},{4,6},{5,7},{6,4},{7,5},{8,10},{9,11},{10,... | collective-permute-start | bytes 786440 | tf_op jit(solution)/shard_map/ppermute | solution.py:97
  48.9 0.8 fusion.4
  49.8 1.0 fusion.60
  50.9 0.9 multiply_add_fusion.1
  51.8 1.0 select_bitcast_fusion.15
  52.9 0.8 pad_maximum_fusion.8
  53.8 1.1 pad_maximum_fusion.1
  54.9 1.5 copy.26
  59.6 0.8 fusion.6
  60.4 1.0 fusion.57
  61.4 1.5 %collective-permute-start.10 = (bf16[512,256]{1,0:T(8,128)(2,1)}, bf16[512,256]{1,0:T(8,128)(2,1)S(1)}, u32[]{:S(2)}, u32[]{:S(2)}) collective-permute-start(bf16[512,256]{1,0:T(8,128)(2,1)} %collective-permute-done.7), channel_id=1, source_target_pairs={{0,2},{1,3},{2,0},{3,1},{4,6},{5,7},{6,4},{7,5},{8,10},{9,11},{10,... | collective-permute-start | bytes 786440 | tf_op jit(solution)/shard_map/ppermute | solution.py:97
  63.0 0.9 multiply_add_fusion
  63.9 6.5 %collective-permute-done.10 = bf16[512,256]{1,0:T(8,128)(2,1)S(1)} collective-permute-done((bf16[512,256]{1,0:T(8,128)(2,1)}, bf16[512,256]{1,0:T(8,128)(2,1)S(1)}, u32[]{:S(2)}, u32[]{:S(2)}) %collective-permute-start.10) | collective-permute-done | bytes 262176 | tf_op jit(solution)/shard_map/ppermute | solution.py:97
  70.4 1.0 select_bitcast_fusion.13
  71.4 0.8 pad_maximum_fusion.9
  72.4 1.1 pad_maximum_fusion.2
  73.4 1.5 copy.28
  77.7 0.8 bitcast_reduce_fusion
  78.5 0.8 fusion.8
  79.5 1.8 %fusion.63 = f32[1,512,4,64]{1,3,2,0:T(8,128)} fusion(bf16[512,4,64]{0,2,1:T(8,128)(2,1)S(1)} %bitcast.584, f32[4,512,512]{2,1,0:T(8,128)S(1)} %get-tuple-element.298, f32[4,512]{1,0:T(4,128)S(1)} %bitcast.552, pred[]{:T(512)} %bitcast.89, f32[1,512,4,64]{1,3,2,0:T(8,128)S(1)} %copy-done.11, f32[512,4]{0,1:T(4,128)S(1)} %get-tuple-element.220), kind=kOutput, calls=%fused_computation.89 | convolution fusion | flops 138674176 | bytes 5521409 | tf_op jit(solution)/shard_map/bhqk,khd->bqhd/dot_general | solution.py:118
  81.4 1.1 pad_maximum_fusion.3
  82.5 1.7 %copy.30 = bf16[512,2,2,256]{0,3,2,1:T(8,128)(2,1)S(1)} copy(bf16[512,2,2,256]{3,0,1,2:T(8,128)(2,1)} %pad_maximum_fusion.3) | data formatting | bytes 2097152 | tf_op jit(solution)/shard_map/stack | solution.py:100
  87.6 0.8 fusion.46
  93.8 1.4 collective-permute-start.14
  95.2 3.8 %collective-permute-done.18 = bf16[256,256]{1,0:T(8,128)(2,1)S(1)} collective-permute-done((bf16[256,256]{1,0:T(8,128)(2,1)}, bf16[256,256]{1,0:T(8,128)(2,1)S(1)}, u32[]{:S(2)}, u32[]{:S(2)}) %collective-permute-start.18) | collective-permute-done | bytes 131104 | tf_op jit(solution)/shard_map/ppermute | solution.py:72
  99.6 1.7 %collective-permute-done.14 = bf16[256,256]{1,0:T(8,128)(2,1)} collective-permute-done((bf16[256,256]{1,0:T(8,128)(2,1)}, bf16[256,256]{1,0:T(8,128)(2,1)}, u32[]{:S(2)}, u32[]{:S(2)}) %collective-permute-start.14) | collective-permute-done | bytes 131104 | tf_op jit(solution)/shard_map/ppermute | solution.py:72
  101.3 1.7 %fusion.179 = (bf16[256,256]{1,0:T(8,128)(2,1)}, bf16[256,256]{1,0:T(8,128)(2,1)S(1)}) fusion(bf16[256,256]{1,0:T(8,128)(2,1)} %copy-done.12, f32[256,2,256]{2,0,1:T(8,128)S(1)} %bitcast_add_fusion.2, s32[]{:T(128)S(6)} %select_n.301, bf16[512,256]{1,0:T(8,128)(2,1)S(1)} %copy-done.3, bf16[256,256]{1,0:T(8,128)(2,1)} %collective-permute-done.14, ...), kind=kLoop, calls=%fused_computation.253 | loop fusion | flops 655360 | bytes 1310724 | tf_op jit(solution)/shard_map/convert_element_type | solution.py:258
  103.4 4.6 %collective-permute-done.15 = bf16[256,256]{1,0:T(8,128)(2,1)S(1)} collective-permute-done((bf16[256,256]{1,0:T(8,128)(2,1)S(1)}, bf16[256,256]{1,0:T(8,128)(2,1)S(1)}, u32[]{:S(2)}, u32[]{:S(2)}) %collective-permute-start.15) | collective-permute-done | bytes 131104 | tf_op jit(solution)/shard_map/ppermute | solution.py:86
  108.2 1.5 collective-permute-done.16
  110.8 5.2 %collective-permute-done.19 = bf16[256,256]{1,0:T(8,128)(2,1)S(1)} collective-permute-done((bf16[256,256]{1,0:T(8,128)(2,1)S(1)}, bf16[256,256]{1,0:T(8,128)(2,1)S(1)}, u32[]{:S(2)}, u32[]{:S(2)}) %collective-permute-start.19) | collective-permute-done | bytes 131104 | tf_op jit(solution)/shard_map/ppermute | solution.py:86
  116.1 4.2 %fusion.108 = f32[256,1024]{1,0:T(8,128)} fusion(bf16[1024,1024]{1,0:T(8,128)(2,1)S(1)} %copy-done, bf16[1024,1024]{1,0:T(8,128)(2,1)} %param.46, bf16[256,1024]{0,1:T(8,128)(2,1)S(1)} %bitcast.525, f32[1024]{0:T(1024)S(1)} %convert_element_type.274, f32[256]{0:T(256)S(1)} %add_rsqrt_fusion.5, f32[256]{0:T(256)S(1)} %broadcast_multiply_fusion.5), kind=kOutput, calls=%fused_computation.144 | convolution fusion | flops 1077411840 | bytes 5773312 | tf_op jit(solution)/shard_map/dot_general | solution.py:269
  120.3 1.0 select_bitcast_fusion.9
  121.9 4.2 %fusion.106 = f32[256,1024]{1,0:T(8,128)} fusion(bf16[1024,1024]{1,0:T(8,128)(2,1)S(1)} %copy-done, bf16[1024,1024]{1,0:T(8,128)(2,1)} %param.46, bf16[256,1024]{0,1:T(8,128)(2,1)S(1)} %bitcast.528, f32[256]{0:T(256)S(1)} %add_rsqrt_fusion.4, f32[256]{0:T(256)S(1)} %broadcast_multiply_fusion.4, f32[1024]{0:T(1024)S(1)} %convert_element_type.274), kind=kOutput, calls=%fused_computation.143 | convolution fusion | flops 1077411840 | bytes 5773312 | tf_op jit(solution)/shard_map/dot_general | solution.py:269
  126.1 1.6 %copy.43 = f32[256,1024]{0,1:T(8,128)S(1)} copy(f32[256,1024]{1,0:T(8,128)} %fusion.106) | data formatting | bytes 2097152 | tf_op jit(solution)/shard_map/optimization_barrier | solution.py:275
  128.4 1.8 %copy.58 = bf16[256,2,1,256]{3,0,1,2:T(8,128)(2,1)} copy(bf16[256,2,1,256]{0,3,2,1:T(8,128)(2,1)} %constant_dynamic-slice_fusion) | data formatting | bytes 524288
  130.7 0.8 constant_dynamic-slice_fusion.1
  131.5 2.1 %copy.44 = f32[256,2,1,256]{3,0,1,2:T(8,128)} copy(f32[256,2,1,256]{0,3,2,1:T(8,128)} %constant_dynamic-slice_fusion.1) | data formatting | bytes 1048576 | tf_op jit(solution)/shard_map/jit(dynamic_index_in_dim)/dynamic_slice | solution.py:70
  133.6 1.6 %copy.40 = f32[256,1024]{0,1:T(8,128)S(1)} copy(f32[256,1024]{1,0:T(8,128)} %fusion.108) | data formatting | bytes 2097152 | tf_op jit(solution)/shard_map/optimization_barrier | solution.py:275
  135.1 0.8 constant_dynamic-slice_fusion.3
  136.0 2.0 %copy.41 = f32[256,2,1,256]{3,0,1,2:T(8,128)} copy(f32[256,2,1,256]{0,3,2,1:T(8,128)} %constant_dynamic-slice_fusion.3) | data formatting | bytes 1048576 | tf_op jit(solution)/shard_map/jit(dynamic_index_in_dim)/dynamic_slice | solution.py:70
  138.7 1.1 copy.57
  140.0 1.2 bitcast_add_fusion
  141.7 1.7 %collective-permute-start.22 = (bf16[256,256]{1,0:T(8,128)(2,1)S(1)}, bf16[256,256]{1,0:T(8,128)(2,1)S(1)}, u32[]{:S(2)}, u32[]{:S(2)}) collective-permute-start(bf16[256,256]{1,0:T(8,128)(2,1)S(1)} %fusion.190), channel_id=1, source_target_pairs={{0,2},{1,3},{2,0},{3,1},{4,6},{5,7},{6,4},{7,5},{8,10},{9,11},{10,... | collective-permute-start | bytes 393224 | tf_op jit(solution)/shard_map/ppermute | solution.py:72
  143.4 4.1 %collective-permute-done.24 = bf16[256,256]{1,0:T(8,128)(2,1)S(1)} collective-permute-done((bf16[256,256]{1,0:T(8,128)(2,1)S(1)}, bf16[256,256]{1,0:T(8,128)(2,1)S(1)}, u32[]{:S(2)}, u32[]{:S(2)}) %collective-permute-start.24) | collective-permute-done | bytes 131104 | tf_op jit(solution)/shard_map/ppermute | solution.py:72
  147.6 2.4 %collective-permute-done.22 = bf16[256,256]{1,0:T(8,128)(2,1)S(1)} collective-permute-done((bf16[256,256]{1,0:T(8,128)(2,1)S(1)}, bf16[256,256]{1,0:T(8,128)(2,1)S(1)}, u32[]{:S(2)}, u32[]{:S(2)}) %collective-permute-start.22) | collective-permute-done | bytes 131104 | tf_op jit(solution)/shard_map/ppermute | solution.py:72
  (171 shorter events, 27.5 us)
Async XLA Ops:
  0.0 116.1 %copy-start = (bf16[1024,1024]{1,0:T(8,128)(2,1)S(1)}, bf16[1024,1024]{1,0:T(8,128)(2,1)}, u32[]{:S(2)}) copy-start(bf16[1024,1024]{1,0:T(8,128)(2,1)} %param.47) | copy-start | bytes 6291460
  0.9 13.1 %collective-permute-start.1 = (bf16[64,256]{1,0:T(8,128)(2,1)S(1)}, bf16[64,256]{1,0:T(8,128)(2,1)S(1)}, u32[]{:S(2)}, u32[]{:S(2)}) collective-permute-start(bf16[64,256]{1,0:T(8,128)(2,1)S(1)} %get-tuple-element.253), channel_id=1, source_target_pairs={{4,0},{8,4},{12,8},{5,1},{9,5},{13,9},{6,2},{10,6},{14,10},{7,3},{... | collective-permute-start | bytes 98312 | tf_op jit(solution)/shard_map/ppermute | solution.py:21
  2.2 11.8 %collective-permute-start = (bf16[64,256]{1,0:T(8,128)(2,1)S(1)}, bf16[64,256]{1,0:T(8,128)(2,1)S(1)}, u32[]{:S(2)}, u32[]{:S(2)}) collective-permute-start(bf16[64,256]{1,0:T(8,128)(2,1)S(1)} %get-tuple-element.252), channel_id=1, source_target_pairs={{0,4},{4,8},{8,12},{1,5},{5,9},{9,13},{2,6},{6,10},{10,14},{3,7},{... | collective-permute-start | bytes 98312 | tf_op jit(solution)/shard_map/ppermute | solution.py:20
  14.3 1.6 %copy-start.9 = (bf16[512,256]{1,0:T(8,128)(2,1)S(1)}, bf16[512,256]{1,0:T(8,128)(2,1)}, u32[]{:S(2)}) copy-start(bf16[512,256]{1,0:T(8,128)(2,1)} %param.35) | copy-start | bytes 786436
  16.0 11.6 %copy-start.13 = (bf16[1024]{0:T(1024)(128)(2,1)S(1)}, bf16[1024]{0:T(1024)(128)(2,1)}, u32[]{:S(2)}) copy-start(bf16[1024]{0:T(1024)(128)(2,1)} %param.40) | copy-start | bytes 6148
  16.0 11.6 %copy-start.15 = (s32[4,4]{1,0:T(4,128)S(1)}, s32[4,4]{1,0:T(4,128)}, u32[]{:S(2)}) copy-start(s32[4,4]{1,0:T(4,128)} %param.37) | copy-start | bytes 196
  16.1 18.9 %copy-start.2 = (bf16[512,256]{1,0:T(8,128)(2,1)}, bf16[512,256]{1,0:T(8,128)(2,1)S(1)}, u32[]{:S(2)}) copy-start(bf16[512,256]{1,0:T(8,128)(2,1)S(1)} %fusion.151) | copy-start | bytes 786436
  16.1 7.8 %collective-permute-start.3 = (bf16[512,256]{1,0:T(8,128)(2,1)S(1)}, bf16[512,256]{1,0:T(8,128)(2,1)S(1)}, u32[]{:S(2)}, u32[]{:S(2)}) collective-permute-start(bf16[512,256]{1,0:T(8,128)(2,1)S(1)} %fusion.151), channel_id=1, source_target_pairs={{0,2},{1,3},{2,0},{3,1},{4,6},{5,7},{6,4},{7,5},{8,10},{9,11},{10,... | collective-permute-start | bytes 786440 | tf_op jit(solution)/shard_map/ppermute | solution.py:97
  18.1 9.1 %collective-permute-start.2 = (bf16[512,256]{1,0:T(8,128)(2,1)S(1)}, bf16[512,256]{1,0:T(8,128)(2,1)}, u32[]{:S(2)}, u32[]{:S(2)}) collective-permute-start(bf16[512,256]{1,0:T(8,128)(2,1)S(1)} %fusion.151), channel_id=1, source_target_pairs={{0,4},{4,8},{8,12},{12,0},{1,5},{5,9},{9,13},{13,1},{2,6},{6,10},{... | collective-permute-start | bytes 786440 | tf_op jit(solution)/shard_map/ppermute | solution.py:192
  27.2 6.7 %collective-permute-start.5 = (bf16[512,256]{1,0:T(8,128)(2,1)}, bf16[512,256]{1,0:T(8,128)(2,1)}, u32[]{:S(2)}, u32[]{:S(2)}) collective-permute-start(bf16[512,256]{1,0:T(8,128)(2,1)} %collective-permute-done.2), channel_id=1, source_target_pairs={{0,2},{1,3},{2,0},{3,1},{4,6},{5,7},{6,4},{7,5},{8,10},{9,11},{10,... | collective-permute-start | bytes 786440 | tf_op jit(solution)/shard_map/ppermute | solution.py:97
  27.5 8.2 %collective-permute-start.6 = (bf16[512,2,256]{2,0,1:T(8,128)(2,1)S(1)}, bf16[512,2,256]{2,0,1:T(8,128)(2,1)S(1)}, u32[]{:S(2)}, u32[]{:S(2)}) collective-permute-start(bf16[512,2,256]{2,0,1:T(8,128)(2,1)S(1)} %pad_maximum_fusion.6), channel_id=1, source_target_pairs={{0,1},{1,0},{2,3},{3,2},{4,5},{5,4},{6,7},{7,6},{8,9},{9,8},{10,11... | collective-permute-start | bytes 1572872 | tf_op jit(solution)/shard_map/ppermute | solution.py:97
  32.7 10.8 %collective-permute-start.4 = (bf16[512,256]{1,0:T(8,128)(2,1)}, bf16[512,256]{1,0:T(8,128)(2,1)}, u32[]{:S(2)}, u32[]{:S(2)}) collective-permute-start(bf16[512,256]{1,0:T(8,128)(2,1)} %collective-permute-done.2), channel_id=1, source_target_pairs={{0,4},{4,8},{8,12},{12,0},{1,5},{5,9},{9,13},{13,1},{2,6},{6,10},{... | collective-permute-start | bytes 786440 | tf_op jit(solution)/shard_map/ppermute | solution.py:192
  38.4 7.3 %copy-start.21 = (bf16[1024,256]{1,0:T(8,128)(2,1)S(1)}, bf16[1024,256]{1,0:T(8,128)(2,1)}, u32[]{:S(2)}) copy-start(bf16[1024,256]{1,0:T(8,128)(2,1)} %param.42) | copy-start | bytes 1572868
  43.5 12.9 %collective-permute-start.7 = (bf16[512,256]{1,0:T(8,128)(2,1)}, bf16[512,256]{1,0:T(8,128)(2,1)}, u32[]{:S(2)}, u32[]{:S(2)}) collective-permute-start(bf16[512,256]{1,0:T(8,128)(2,1)} %collective-permute-done.4), channel_id=1, source_target_pairs={{0,4},{4,8},{8,12},{12,0},{1,5},{5,9},{9,13},{13,1},{2,6},{6,10},{... | collective-permute-start | bytes 786440 | tf_op jit(solution)/shard_map/ppermute | solution.py:192
  43.5 8.3 %collective-permute-start.8 = (bf16[512,256]{1,0:T(8,128)(2,1)}, bf16[512,256]{1,0:T(8,128)(2,1)S(1)}, u32[]{:S(2)}, u32[]{:S(2)}) collective-permute-start(bf16[512,256]{1,0:T(8,128)(2,1)} %collective-permute-done.4), channel_id=1, source_target_pairs={{0,2},{1,3},{2,0},{3,1},{4,6},{5,7},{6,4},{7,5},{8,10},{9,11},{10,... | collective-permute-start | bytes 786440 | tf_op jit(solution)/shard_map/ppermute | solution.py:97
  45.4 1.0 copy-start.16
  46.4 1.0 copy-start.17
  49.8 1.0 copy-start.5
  50.8 2.9 %collective-permute-start.9 = (bf16[512,2,256]{2,0,1:T(8,128)(2,1)S(1)}, bf16[512,2,256]{2,0,1:T(8,128)(2,1)S(1)}, u32[]{:S(2)}, u32[]{:S(2)}) collective-permute-start(bf16[512,2,256]{2,0,1:T(8,128)(2,1)S(1)} %copy-done.5), channel_id=1, source_target_pairs={{0,1},{1,0},{2,3},{3,2},{4,5},{5,4},{6,7},{7,6},{8,9},{9,8},{10,11... | collective-permute-start | bytes 1572872 | tf_op jit(solution)/shard_map/ppermute | solution.py:97
  56.4 1.0 copy-start.22
  56.7 1.5 copy-start.18
  60.4 2.5 %copy-start.6 = (bf16[512,2,256]{2,0,1:T(8,128)(2,1)S(1)}, bf16[512,2,256]{2,0,1:T(8,128)(2,1)}, u32[]{:S(2)}) copy-start(bf16[512,2,256]{2,0,1:T(8,128)(2,1)} %pad_maximum_fusion.8) | copy-start | bytes 1572868
  60.4 2.5 %copy-start.4 = (f32[1,512,4,64]{1,3,2,0:T(8,128)S(1)}, f32[1,512,4,64]{1,3,2,0:T(8,128)}, u32[]{:S(2)}) copy-start(f32[1,512,4,64]{1,3,2,0:T(8,128)} %multiply_add_fusion.1) | copy-start | bytes 1572868
  61.4 9.0 %collective-permute-start.10 = (bf16[512,256]{1,0:T(8,128)(2,1)}, bf16[512,256]{1,0:T(8,128)(2,1)S(1)}, u32[]{:S(2)}, u32[]{:S(2)}) collective-permute-start(bf16[512,256]{1,0:T(8,128)(2,1)} %collective-permute-done.7), channel_id=1, source_target_pairs={{0,2},{1,3},{2,0},{3,1},{4,6},{5,7},{6,4},{7,5},{8,10},{9,11},{10,... | collective-permute-start | bytes 786440 | tf_op jit(solution)/shard_map/ppermute | solution.py:97
  62.9 9.3 %collective-permute-start.11 = (bf16[512,2,256]{2,0,1:T(8,128)(2,1)S(1)}, bf16[512,2,256]{2,0,1:T(8,128)(2,1)S(1)}, u32[]{:S(2)}, u32[]{:S(2)}) collective-permute-start(bf16[512,2,256]{2,0,1:T(8,128)(2,1)S(1)} %copy-done.6), channel_id=1, source_target_pairs={{0,1},{1,0},{2,3},{3,2},{4,5},{5,4},{6,7},{7,6},{8,9},{9,8},{10,11... | collective-permute-start | bytes 1572872 | tf_op jit(solution)/shard_map/ppermute | solution.py:97
  74.9 1.0 copy-start.23
  75.2 1.5 copy-start.19
  76.6 1.0 copy-start.7
  77.7 3.6 %collective-permute-start.12 = (bf16[512,2,256]{2,0,1:T(8,128)(2,1)S(1)}, bf16[512,2,256]{2,0,1:T(8,128)(2,1)S(1)}, u32[]{:S(2)}, u32[]{:S(2)}) collective-permute-start(bf16[512,2,256]{2,0,1:T(8,128)(2,1)S(1)} %copy-done.7), channel_id=1, source_target_pairs={{0,1},{1,0},{2,3},{3,2},{4,5},{5,4},{6,7},{7,6},{8,9},{9,8},{10,11... | collective-permute-start | bytes 1572872 | tf_op jit(solution)/shard_map/ppermute | solution.py:97
  78.5 1.0 copy-start.11
  84.2 1.0 copy-start.20
  84.4 1.5 copy-start.24
  87.6 1.0 copy-start.25
  88.4 1.1 copy-start.1
  89.9 1.7 %collective-permute-start.17 = (bf16[256,2,256]{2,0,1:T(8,128)(2,1)S(1)}, bf16[256,2,256]{2,0,1:T(8,128)(2,1)S(1)}, u32[]{:S(2)}, u32[]{:S(2)}) collective-permute-start(bf16[256,2,256]{2,0,1:T(8,128)(2,1)S(1)} %fusion.173), channel_id=1, source_target_pairs={{0,1},{1,0},{2,3},{3,2},{4,5},{5,4},{6,7},{7,6},{8,9},{9,8},{10,11... | collective-permute-start | bytes 786440 | tf_op jit(solution)/shard_map/ppermute | solution.py:72
  91.4 9.9 %copy-start.3 = (bf16[512,256]{1,0:T(8,128)(2,1)S(1)}, bf16[512,256]{1,0:T(8,128)(2,1)}, u32[]{:S(2)}) copy-start(bf16[512,256]{1,0:T(8,128)(2,1)} %copy-done.2) | copy-start | bytes 786436
  91.5 1.6 %collective-permute-start.13 = (bf16[256,2,256]{2,0,1:T(8,128)(2,1)S(1)}, bf16[256,2,256]{2,0,1:T(8,128)(2,1)S(1)}, u32[]{:S(2)}, u32[]{:S(2)}) collective-permute-start(bf16[256,2,256]{2,0,1:T(8,128)(2,1)S(1)} %fusion.172), channel_id=1, source_target_pairs={{0,1},{1,0},{2,3},{3,2},{4,5},{5,4},{6,7},{7,6},{8,9},{9,8},{10,11... | collective-permute-start | bytes 786440 | tf_op jit(solution)/shard_map/ppermute | solution.py:72
  91.7 16.4 %copy-start.14 = (bf16[1024]{0:T(1024)(128)(2,1)S(1)}, bf16[1024]{0:T(1024)(128)(2,1)}, u32[]{:S(2)}) copy-start(bf16[1024]{0:T(1024)(128)(2,1)} %param.45) | copy-start | bytes 6148
  92.4 6.5 %collective-permute-start.18 = (bf16[256,256]{1,0:T(8,128)(2,1)}, bf16[256,256]{1,0:T(8,128)(2,1)S(1)}, u32[]{:S(2)}, u32[]{:S(2)}) collective-permute-start(bf16[256,256]{1,0:T(8,128)(2,1)} %fusion.189), channel_id=1, source_target_pairs={{0,2},{1,3},{2,0},{3,1},{4,6},{5,7},{6,4},{7,5},{8,10},{9,11},{10,... | collective-permute-start | bytes 393224 | tf_op jit(solution)/shard_map/ppermute | solution.py:72
  93.8 7.5 %collective-permute-start.14 = (bf16[256,256]{1,0:T(8,128)(2,1)}, bf16[256,256]{1,0:T(8,128)(2,1)}, u32[]{:S(2)}, u32[]{:S(2)}) collective-permute-start(bf16[256,256]{1,0:T(8,128)(2,1)} %fusion.188), channel_id=1, source_target_pairs={{0,2},{1,3},{2,0},{3,1},{4,6},{5,7},{6,4},{7,5},{8,10},{9,11},{10,... | collective-permute-start | bytes 393224 | tf_op jit(solution)/shard_map/ppermute | solution.py:72
  98.9 0.7 copy-start.12
  103.0 5.0 %collective-permute-start.15 = (bf16[256,256]{1,0:T(8,128)(2,1)S(1)}, bf16[256,256]{1,0:T(8,128)(2,1)S(1)}, u32[]{:S(2)}, u32[]{:S(2)}) collective-permute-start(bf16[256,256]{1,0:T(8,128)(2,1)S(1)} %get-tuple-element.249), channel_id=1, source_target_pairs={{0,2},{1,3},{2,0},{3,1},{4,6},{5,7},{6,4},{7,5},{8,10},{9,11},{10,... | collective-permute-start | bytes 393224 | tf_op jit(solution)/shard_map/ppermute | solution.py:86
  108.0 1.6 %collective-permute-start.16 = (bf16[256,2,256]{2,0,1:T(8,128)(2,1)S(1)}, bf16[256,2,256]{2,0,1:T(8,128)(2,1)S(1)}, u32[]{:S(2)}, u32[]{:S(2)}) collective-permute-start(bf16[256,2,256]{2,0,1:T(8,128)(2,1)S(1)} %pad_maximum_fusion.12), channel_id=1, source_target_pairs={{0,1},{1,0},{2,3},{3,2},{4,5},{5,4},{6,7},{7,6},{8,9},{9,8},{10,11... | collective-permute-start | bytes 786440 | tf_op jit(solution)/shard_map/ppermute | solution.py:86
  108.1 2.2 %copy-start.10 = (bf16[256,256]{1,0:T(8,128)(2,1)S(1)}, bf16[256,256]{1,0:T(8,128)(2,1)}, u32[]{:S(2)}) copy-start(bf16[256,256]{1,0:T(8,128)(2,1)} %get-tuple-element.151) | copy-start | bytes 393220
  110.3 5.6 %collective-permute-start.19 = (bf16[256,256]{1,0:T(8,128)(2,1)S(1)}, bf16[256,256]{1,0:T(8,128)(2,1)S(1)}, u32[]{:S(2)}, u32[]{:S(2)}) collective-permute-start(bf16[256,256]{1,0:T(8,128)(2,1)S(1)} %copy-done.10), channel_id=1, source_target_pairs={{0,2},{1,3},{2,0},{3,1},{4,6},{5,7},{6,4},{7,5},{8,10},{9,11},{10,... | collective-permute-start | bytes 393224 | tf_op jit(solution)/shard_map/ppermute | solution.py:86
  116.0 4.3 %collective-permute-start.20 = (bf16[256,2,256]{2,0,1:T(8,128)(2,1)S(1)}, bf16[256,2,256]{2,0,1:T(8,128)(2,1)}, u32[]{:S(2)}, u32[]{:S(2)}) collective-permute-start(bf16[256,2,256]{2,0,1:T(8,128)(2,1)S(1)} %pad_maximum_fusion.13), channel_id=1, source_target_pairs={{0,1},{1,0},{2,3},{3,2},{4,5},{5,4},{6,7},{7,6},{8,9},{9,8},{10,11... | collective-permute-start | bytes 786440 | tf_op jit(solution)/shard_map/ppermute | solution.py:86
  130.2 9.8 %collective-permute-start.23 = (bf16[256,2,256]{2,0,1:T(8,128)(2,1)}, bf16[256,2,256]{2,0,1:T(8,128)(2,1)}, u32[]{:S(2)}, u32[]{:S(2)}) collective-permute-start(bf16[256,2,256]{2,0,1:T(8,128)(2,1)} %bitcast.545), channel_id=1, source_target_pairs={{0,1},{1,0},{2,3},{3,2},{4,5},{5,4},{6,7},{7,6},{8,9},{9,8},{10,11... | collective-permute-start | bytes 786440 | tf_op jit(solution)/shard_map/ppermute | solution.py:72
  138.7 2.9 %copy-start.8 = (f32[256,2,1,256]{3,0,1,2:T(8,128)S(1)}, f32[256,2,1,256]{3,0,1,2:T(8,128)}, u32[]{:S(2)}) copy-start(f32[256,2,1,256]{3,0,1,2:T(8,128)} %copy.41) | copy-start | bytes 1572868
  139.9 1.7 %collective-permute-start.21 = (bf16[256,2,256]{2,0,1:T(8,128)(2,1)S(1)}, bf16[256,2,256]{2,0,1:T(8,128)(2,1)S(1)}, u32[]{:S(2)}, u32[]{:S(2)}) collective-permute-start(bf16[256,2,256]{2,0,1:T(8,128)(2,1)S(1)} %bitcast.546), channel_id=1, source_target_pairs={{0,1},{1,0},{2,3},{3,2},{4,5},{5,4},{6,7},{7,6},{8,9},{9,8},{10,11... | collective-permute-start | bytes 786440 | tf_op jit(solution)/shard_map/ppermute | solution.py:72
  141.2 6.4 %collective-permute-start.24 = (bf16[256,256]{1,0:T(8,128)(2,1)S(1)}, bf16[256,256]{1,0:T(8,128)(2,1)S(1)}, u32[]{:S(2)}, u32[]{:S(2)}) collective-permute-start(bf16[256,256]{1,0:T(8,128)(2,1)S(1)} %fusion.191), channel_id=1, source_target_pairs={{0,2},{1,3},{2,0},{3,1},{4,6},{5,7},{6,4},{7,5},{8,10},{9,11},{10,... | collective-permute-start | bytes 393224 | tf_op jit(solution)/shard_map/ppermute | solution.py:72
  141.7 8.2 %collective-permute-start.22 = (bf16[256,256]{1,0:T(8,128)(2,1)S(1)}, bf16[256,256]{1,0:T(8,128)(2,1)S(1)}, u32[]{:S(2)}, u32[]{:S(2)}) collective-permute-start(bf16[256,256]{1,0:T(8,128)(2,1)S(1)} %fusion.190), channel_id=1, source_target_pairs={{0,2},{1,3},{2,0},{3,1},{4,6},{5,7},{6,4},{7,5},{8,10},{9,11},{10,... | collective-permute-start | bytes 393224 | tf_op jit(solution)/shard_map/ppermute | solution.py:72

commit v17 on v15

--- a/solution.py
+++ b/solution.py
@@ -254,6 +254,7 @@
         hidden = jax.nn.gelu(
             jnp.dot(normed_two, up_weight, preferred_element_type=jnp.float32), approximate=True
         ).astype(jnp.bfloat16)
+        hidden = lax.optimization_barrier(hidden)
         lowered = jnp.dot(hidden, down_weight, preferred_element_type=jnp.float32)
         mixed = scatter_heads(lowered, head_id, head_total)
         outputs.append((stream_two.astype(jnp.float32) + mixed).astype(jnp.bfloat16))

time: 120 us -> 113 us (0.942)
  matrix products: 22.4 us -> 17.8 us
  local copies, waits for them, and re-layouts: 12.7 us -> 11.2 us
    dot_general x2, matrix products: 8.42 us -> 1.9 us  [shards(): lowered = jnp.dot(hidden, down_weight, preferred_element_type=jnp.float32)]
    convert_element_type x8, local copies, waits for them, and re-layouts: 3.34 us -> 1.19 us  [scatter_heads(): give.astype(jnp.bfloat16)]
    dot_general x0 -> x2, matrix products: none -> 1.84 us  [shards(): jnp.dot(normed_two, up_weight, preferred_element_type=jnp.float32)]
  transfers between devices with their start and end apart: 25 -> 25, of which waited for: 18 -> 19; matrix products, arithmetic and copies ran while one was open for 24% -> 21% of each run, Pallas kernels for 0% -> 0%
where the time goes in v17:
time: 113 us; the launch traced here: 112 us
  waiting for transfers between devices  40.8 us (36%)
  starting transfers between devices  21.9 us (19%)
  matrix products  17.8 us (16%)
  other arithmetic  16.2 us (14%)
  local copies, waits for them, and re-layouts  11.2 us (10%)
  between operations  4.58 us (4%)
    ppermute x8, waiting for transfers between devices, gather_levels(): lax.ppermute(current, 'heads', [(i, i ^ bit) for i in range(head_total)])  13.3 us
    ppermute x8, waiting for transfers between devices, scatter_heads(): lax.ppermute(give.astype(jnp.bfloat16), 'heads', [(i, i ^ bit) for i in r...  11.8 us
    ppermute x3, waiting for transfers between devices, shards(): ringed[slot + 1] = lax.ppermute(ringed[slot], 'bricks', ring)  8.81 us
    ppermute x4, waiting for transfers between devices, gather_heads(): lax.ppermute(current, 'heads', [(i, i ^ bit) for i in range(head_total)])  6.85 us
    ppermute x8, starting transfers between devices, gather_levels(): lax.ppermute(current, 'heads', [(i, i ^ bit) for i in range(head_total)])  5.88 us
    ppermute x1, starting transfers between devices, extended_2(): before = lax.ppermute(last, axis, up)  5.56 us
    ppermute x8, starting transfers between devices, scatter_heads(): lax.ppermute(give.astype(jnp.bfloat16), 'heads', [(i, i ^ bit) for i in r...  4.76 us
    dot_general x5, matrix products, absorb_block(): jnp.einsum('bhqk,khd->bqhd', weights.astype(jnp.bfloat16), value_rows, pr...  4.05 us
  transfers between devices with their start and end apart: 25, of which 19 were waited for; matrix products, arithmetic and copies ran while one was open for 21% of the time, Pallas kernels for 0%

profile of v17, /device:TPU:0, one launch (start us, length us, event | category | flops | bytes accessed | tf_op | source)
XLA Modules:
  0.0 112.4 jit_solution(6159938960314966302)
XLA Ops:
  0.0 0.9 fusion.178
  0.9 1.3 %collective-permute-start.1 = (bf16[64,256]{1,0:T(8,128)(2,1)S(1)}, bf16[64,256]{1,0:T(8,128)(2,1)S(1)}, u32[]{:S(2)}, u32[]{:S(2)}) collective-permute-start(bf16[64,256]{1,0:T(8,128)(2,1)S(1)} %get-tuple-element.245), channel_id=1, source_target_pairs={{4,0},{8,4},{12,8},{5,1},{9,5},{13,9},{6,2},{10,6},{14,10},{7,3},{... | collective-permute-start | bytes 98312 | tf_op jit(solution)/shard_map/ppermute | solution.py:21
  2.2 5.6 %collective-permute-start = (bf16[64,256]{1,0:T(8,128)(2,1)S(1)}, bf16[64,256]{1,0:T(8,128)(2,1)S(1)}, u32[]{:S(2)}, u32[]{:S(2)}) collective-permute-start(bf16[64,256]{1,0:T(8,128)(2,1)S(1)} %get-tuple-element.244), channel_id=1, source_target_pairs={{0,4},{4,8},{8,12},{1,5},{5,9},{9,13},{2,6},{6,10},{10,14},{3,7},{... | collective-permute-start | bytes 98312 | tf_op jit(solution)/shard_map/ppermute | solution.py:20
  7.8 1.0 fusion.179
  8.8 0.9 fusion.180
  9.7 1.1 copy.30
  10.8 1.4 %fusion.182 = (s32[1]{0:T(128)}, s32[1]{0:T(128)}) fusion(s32[4]{0:T(128)} %param.36, s32[]{:T(128)} %bitcast.2, s32[]{:T(128)} %bitcast.6), kind=kLoop, calls=%fused_computation.319 | loop fusion | bytes 24 | tf_op jit(solution)/shard_map/jit(_take)/gather | solution.py:157
  13.7 0.7 convert_element_type.243
  14.7 1.7 %fusion.102 = f32[1,8,8,8,256]{4,3,2,1,0:T(8,128)S(1)} fusion(f32[1,10,10,10,256]{4,3,2,1,0:T(8,128)S(1)} %select_maximum_fusion, f32[1,1,8,8,256]{4,3,2,1,0:T(8,128)S(1)} %multiply_bitcast_fusion, f32[1,8,8,8,256]{4,3,2,1,0:T(8,128)S(1)} %bitcast.542, f32[1,1,8,8,256]{4,3,2,1,0:T(8,128)S(1)} %multiply_bitcast_fusion.1, f32[256]{0:T(256)S(1)} %bitcast.593, ...), kind=kLoop, calls=%fused_computation.140 | loop fusion | flops 7208960 | bytes 13790208 | tf_op jit(solution)/shard_map/add | solution.py:51
  16.7 2.0 %collective-permute-start.3 = (bf16[512,256]{0,1:T(8,128)(2,1)S(1)}, bf16[512,256]{0,1:T(8,128)(2,1)S(1)}, u32[]{:S(2)}, u32[]{:S(2)}) collective-permute-start(bf16[512,256]{0,1:T(8,128)(2,1)S(1)} %add_convert_fusion), channel_id=1, source_target_pairs={{0,2},{1,3},{2,0},{3,1},{4,6},{5,7},{6,4},{7,5},{8,10},{9,11},{10,... | collective-permute-start | bytes 786440 | tf_op jit(solution)/shard_map/ppermute | solution.py:97
  18.7 1.6 %collective-permute-start.2 = (bf16[512,256]{0,1:T(8,128)(2,1)S(1)}, bf16[512,256]{0,1:T(8,128)(2,1)S(1)}, u32[]{:S(2)}, u32[]{:S(2)}) collective-permute-start(bf16[512,256]{0,1:T(8,128)(2,1)S(1)} %add_convert_fusion), channel_id=1, source_target_pairs={{0,4},{4,8},{8,12},{12,0},{1,5},{5,9},{9,13},{13,1},{2,6},{6,10},{... | collective-permute-start | bytes 786440 | tf_op jit(solution)/shard_map/ppermute | solution.py:192
  20.3 4.3 %collective-permute-done.3 = bf16[512,256]{0,1:T(8,128)(2,1)S(1)} collective-permute-done((bf16[512,256]{0,1:T(8,128)(2,1)S(1)}, bf16[512,256]{0,1:T(8,128)(2,1)S(1)}, u32[]{:S(2)}, u32[]{:S(2)}) %collective-permute-start.3) | collective-permute-done | bytes 262176 | tf_op jit(solution)/shard_map/ppermute | solution.py:97
  24.6 0.8 pad_maximum_fusion.6
  25.4 2.3 %collective-permute-done.2 = bf16[512,256]{0,1:T(8,128)(2,1)S(1)} collective-permute-done((bf16[512,256]{0,1:T(8,128)(2,1)S(1)}, bf16[512,256]{0,1:T(8,128)(2,1)S(1)}, u32[]{:S(2)}, u32[]{:S(2)}) %collective-permute-start.2) | collective-permute-done | bytes 262176 | tf_op jit(solution)/shard_map/ppermute | solution.py:192
  28.1 0.6 fusion.181
  31.2 1.2 %copy.65 = bf16[1024,256]{1,0:T(8,128)(2,1)S(1)} copy(bf16[1024,256]{0,1:T(8,128)(2,1)} %bitcast.555) | data formatting | bytes 1048576 | tf_op jit(solution)/shard_map/dot_general | solution.py:249
  33.0 1.1 %collective-permute-done.5 = bf16[512,256]{0,1:T(8,128)(2,1)} collective-permute-done((bf16[512,256]{0,1:T(8,128)(2,1)S(1)}, bf16[512,256]{0,1:T(8,128)(2,1)}, u32[]{:S(2)}, u32[]{:S(2)}) %collective-permute-start.5) | collective-permute-done | bytes 262176 | tf_op jit(solution)/shard_map/ppermute | solution.py:97
  34.2 1.0 select_bitcast_fusion.17
  35.2 1.3 %select_bitcast_fusion.7 = (bf16[512,2,1,256]{0,3,1,2:T(8,128)(2,1)S(1)}, bf16[512,2,1,256]{0,3,1,2:T(8,128)(2,1)S(1)}) fusion(bf16[512,2,256]{0,2,1:T(8,128)(2,1)} %pad_maximum_fusion.6, bf16[512,2,256]{0,2,1:T(8,128)(2,1)} %collective-permute-done.6, pred[]{:T(512)S(6)} %eq.9), kind=kLoop, calls=%fused_computation.216 | loop fusion | flops 524288 | bytes 2097153 | tf_op jit(solution)/shard_map/stack | solution.py:100
  36.7 6.3 %collective-permute-done.4 = bf16[512,256]{0,1:T(8,128)(2,1)S(1)} collective-permute-done((bf16[512,256]{0,1:T(8,128)(2,1)S(1)}, bf16[512,256]{0,1:T(8,128)(2,1)S(1)}, u32[]{:S(2)}, u32[]{:S(2)}) %collective-permute-start.4) | collective-permute-done | bytes 262176 | tf_op jit(solution)/shard_map/ppermute | solution.py:192
  43.0 1.6 %collective-permute-start.8 = (bf16[512,256]{0,1:T(8,128)(2,1)S(1)}, bf16[512,256]{0,1:T(8,128)(2,1)S(1)}, u32[]{:S(2)}, u32[]{:S(2)}) collective-permute-start(bf16[512,256]{0,1:T(8,128)(2,1)S(1)} %collective-permute-done.4), channel_id=1, source_target_pairs={{0,2},{1,3},{2,0},{3,1},{4,6},{5,7},{6,4},{7,5},{8,10},{9,11},{10,... | collective-permute-start | bytes 786440 | tf_op jit(solution)/shard_map/ppermute | solution.py:97
  45.2 0.6 convolution_convert_fusion.8
  45.9 0.6 convolution_convert_fusion.7
  46.9 0.6 convolution_convert_fusion.6
  47.6 0.8 bitcast_reduce_fusion.2
  48.4 0.8 fusion.4
  49.2 1.0 fusion.56
  51.0 1.2 %collective-permute-done.9 = bf16[512,2,256]{0,2,1:T(8,128)(2,1)S(1)} collective-permute-done((bf16[512,2,256]{0,2,1:T(8,128)(2,1)S(1)}, bf16[512,2,256]{0,2,1:T(8,128)(2,1)S(1)}, u32[]{:S(2)}, u32[]{:S(2)}) %collective-permute-start.9) | collective-permute-done | bytes 524320 | tf_op jit(solution)/shard_map/ppermute | solution.py:97
  53.3 0.6 convolution_convert_fusion.5
  53.9 0.6 convolution_convert_fusion.4
  54.6 0.8 bitcast_reduce_fusion.1
  55.4 0.8 fusion.6
  56.2 1.0 fusion.53
  57.2 1.7 %collective-permute-start.10 = (bf16[512,256]{0,1:T(8,128)(2,1)S(1)}, bf16[512,256]{0,1:T(8,128)(2,1)S(1)}, u32[]{:S(2)}, u32[]{:S(2)}) collective-permute-start(bf16[512,256]{0,1:T(8,128)(2,1)S(1)} %collective-permute-done.7), channel_id=1, source_target_pairs={{0,2},{1,3},{2,0},{3,1},{4,6},{5,7},{6,4},{7,5},{8,10},{9,11},{10,... | collective-permute-start | bytes 786440 | tf_op jit(solution)/shard_map/ppermute | solution.py:97
  59.0 6.3 %collective-permute-done.10 = bf16[512,256]{0,1:T(8,128)(2,1)S(1)} collective-permute-done((bf16[512,256]{0,1:T(8,128)(2,1)S(1)}, bf16[512,256]{0,1:T(8,128)(2,1)S(1)}, u32[]{:S(2)}, u32[]{:S(2)}) %collective-permute-start.10) | collective-permute-done | bytes 262176 | tf_op jit(solution)/shard_map/ppermute | solution.py:97
  66.3 0.6 convolution_convert_fusion.3
  66.9 0.6 convolution_convert_fusion.2
  67.7 1.0 bitcast_reduce_fusion
  68.7 0.8 fusion.8
  69.6 1.0 fusion.59
  71.4 0.6 convolution_convert_fusion
  72.1 0.6 convolution_convert_fusion.1
  77.3 0.7 collective-permute-start.14
  78.6 0.8 bitcast_add_fusion.1
  79.4 1.0 fusion.152
  80.4 0.9 collective-permute-start.20
  81.3 1.8 %collective-permute-done.14 = bf16[256,256]{0,1:T(8,128)(2,1)S(1)} collective-permute-done((bf16[256,256]{0,1:T(8,128)(2,1)S(1)}, bf16[256,256]{0,1:T(8,128)(2,1)S(1)}, u32[]{:S(2)}, u32[]{:S(2)}) %collective-permute-start.14) | collective-permute-done | bytes 131104 | tf_op jit(solution)/shard_map/ppermute | solution.py:72
  83.2 2.8 %collective-permute-done.20 = bf16[256,256]{0,1:T(8,128)(2,1)S(1)} collective-permute-done((bf16[256,256]{0,1:T(8,128)(2,1)S(1)}, bf16[256,256]{0,1:T(8,128)(2,1)S(1)}, u32[]{:S(2)}, u32[]{:S(2)}) %collective-permute-start.20) | collective-permute-done | bytes 131104 | tf_op jit(solution)/shard_map/ppermute | solution.py:72
  86.0 1.0 fusion.141
  87.1 0.9 collective-permute-start.21
  87.9 1.2 %collective-permute-start.15 = (bf16[256,256]{0,1:T(8,128)(2,1)S(1)}, bf16[256,256]{0,1:T(8,128)(2,1)S(1)}, u32[]{:S(2)}, u32[]{:S(2)}) collective-permute-start(bf16[256,256]{0,1:T(8,128)(2,1)S(1)} %get-tuple-element.240), channel_id=1, source_target_pairs={{0,2},{1,3},{2,0},{3,1},{4,6},{5,7},{6,4},{7,5},{8,10},{9,11},{10,... | collective-permute-start | bytes 393224 | tf_op jit(solution)/shard_map/ppermute | solution.py:86
  89.1 4.1 %collective-permute-done.21 = bf16[256,256]{0,1:T(8,128)(2,1)S(1)} collective-permute-done((bf16[256,256]{0,1:T(8,128)(2,1)S(1)}, bf16[256,256]{0,1:T(8,128)(2,1)S(1)}, u32[]{:S(2)}, u32[]{:S(2)}) %collective-permute-start.21) | collective-permute-done | bytes 131104 | tf_op jit(solution)/shard_map/ppermute | solution.py:86
  93.4 1.3 %collective-permute-done.15 = bf16[256,256]{0,1:T(8,128)(2,1)S(1)} collective-permute-done((bf16[256,256]{0,1:T(8,128)(2,1)S(1)}, bf16[256,256]{0,1:T(8,128)(2,1)S(1)}, u32[]{:S(2)}, u32[]{:S(2)}) %collective-permute-start.15) | collective-permute-done | bytes 131104 | tf_op jit(solution)/shard_map/ppermute | solution.py:86
  94.9 1.4 %collective-permute-done.16 = bf16[256,2,256]{0,2,1:T(8,128)(2,1)S(1)} collective-permute-done((bf16[256,2,256]{0,2,1:T(8,128)(2,1)S(1)}, bf16[256,2,256]{0,2,1:T(8,128)(2,1)S(1)}, u32[]{:S(2)}, u32[]{:S(2)}) %collective-permute-start.16) | collective-permute-done | bytes 262176 | tf_op jit(solution)/shard_map/ppermute | solution.py:86
  97.8 0.9 fusion.83
  98.7 0.6 copy-done.1
  99.4 1.0 fusion.186
  100.6 0.9 fusion.75
  101.5 1.0 fusion.184
  103.0 0.8 collective-permute-start.24
  104.2 1.1 collective-permute-start.18
  105.3 4.2 %collective-permute-done.24 = bf16[256,256]{0,1:T(8,128)(2,1)S(1)} collective-permute-done((bf16[256,256]{0,1:T(8,128)(2,1)S(1)}, bf16[256,256]{0,1:T(8,128)(2,1)S(1)}, u32[]{:S(2)}, u32[]{:S(2)}) %collective-permute-start.24) | collective-permute-done | bytes 131104 | tf_op jit(solution)/shard_map/ppermute | solution.py:72
  109.5 1.9 %collective-permute-done.18 = bf16[256,256]{0,1:T(8,128)(2,1)S(1)} collective-permute-done((bf16[256,256]{0,1:T(8,128)(2,1)S(1)}, bf16[256,256]{0,1:T(8,128)(2,1)S(1)}, u32[]{:S(2)}, u32[]{:S(2)}) %collective-permute-start.18) | collective-permute-done | bytes 131104 | tf_op jit(solution)/shard_map/ppermute | solution.py:72
  111.5 0.8 copy.53
  (133 shorter events, 15.0 us)
Async XLA Ops:
  0.0 97.8 %copy-start = (bf16[1024,1024]{1,0:T(8,128)(2,1)S(1)}, bf16[1024,1024]{1,0:T(8,128)(2,1)}, u32[]{:S(2)}) copy-start(bf16[1024,1024]{1,0:T(8,128)(2,1)} %param.46) | copy-start | bytes 6291460
  0.9 13.4 %collective-permute-start.1 = (bf16[64,256]{1,0:T(8,128)(2,1)S(1)}, bf16[64,256]{1,0:T(8,128)(2,1)S(1)}, u32[]{:S(2)}, u32[]{:S(2)}) collective-permute-start(bf16[64,256]{1,0:T(8,128)(2,1)S(1)} %get-tuple-element.245), channel_id=1, source_target_pairs={{4,0},{8,4},{12,8},{5,1},{9,5},{13,9},{6,2},{10,6},{14,10},{7,3},{... | collective-permute-start | bytes 98312 | tf_op jit(solution)/shard_map/ppermute | solution.py:21
  2.2 12.2 %collective-permute-start = (bf16[64,256]{1,0:T(8,128)(2,1)S(1)}, bf16[64,256]{1,0:T(8,128)(2,1)S(1)}, u32[]{:S(2)}, u32[]{:S(2)}) collective-permute-start(bf16[64,256]{1,0:T(8,128)(2,1)S(1)} %get-tuple-element.244), channel_id=1, source_target_pairs={{0,4},{4,8},{8,12},{1,5},{5,9},{9,13},{2,6},{6,10},{10,14},{3,7},{... | collective-permute-start | bytes 98312 | tf_op jit(solution)/shard_map/ppermute | solution.py:20
  16.3 11.7 %copy-start.2 = (bf16[1024]{0:T(1024)(128)(2,1)S(1)}, bf16[1024]{0:T(1024)(128)(2,1)}, u32[]{:S(2)}) copy-start(bf16[1024]{0:T(1024)(128)(2,1)} %param.40) | copy-start | bytes 6148
  16.3 11.7 %copy-start.4 = (s32[4,4]{1,0:T(4,128)S(1)}, s32[4,4]{1,0:T(4,128)}, u32[]{:S(2)}) copy-start(s32[4,4]{1,0:T(4,128)} %param.37) | copy-start | bytes 196
  16.7 7.8 %collective-permute-start.3 = (bf16[512,256]{0,1:T(8,128)(2,1)S(1)}, bf16[512,256]{0,1:T(8,128)(2,1)S(1)}, u32[]{:S(2)}, u32[]{:S(2)}) collective-permute-start(bf16[512,256]{0,1:T(8,128)(2,1)S(1)} %add_convert_fusion), channel_id=1, source_target_pairs={{0,2},{1,3},{2,0},{3,1},{4,6},{5,7},{6,4},{7,5},{8,10},{9,11},{10,... | collective-permute-start | bytes 786440 | tf_op jit(solution)/shard_map/ppermute | solution.py:97
  18.7 9.0 %collective-permute-start.2 = (bf16[512,256]{0,1:T(8,128)(2,1)S(1)}, bf16[512,256]{0,1:T(8,128)(2,1)S(1)}, u32[]{:S(2)}, u32[]{:S(2)}) collective-permute-start(bf16[512,256]{0,1:T(8,128)(2,1)S(1)} %add_convert_fusion), channel_id=1, source_target_pairs={{0,4},{4,8},{8,12},{12,0},{1,5},{5,9},{9,13},{13,1},{2,6},{6,10},{... | collective-permute-start | bytes 786440 | tf_op jit(solution)/shard_map/ppermute | solution.py:192
  27.7 6.5 %collective-permute-start.5 = (bf16[512,256]{0,1:T(8,128)(2,1)S(1)}, bf16[512,256]{0,1:T(8,128)(2,1)}, u32[]{:S(2)}, u32[]{:S(2)}) collective-permute-start(bf16[512,256]{0,1:T(8,128)(2,1)S(1)} %collective-permute-done.2), channel_id=1, source_target_pairs={{0,2},{1,3},{2,0},{3,1},{4,6},{5,7},{6,4},{7,5},{8,10},{9,11},{10,... | collective-permute-start | bytes 786440 | tf_op jit(solution)/shard_map/ppermute | solution.py:97
  28.1 7.2 %collective-permute-start.6 = (bf16[512,2,256]{0,2,1:T(8,128)(2,1)}, bf16[512,2,256]{0,2,1:T(8,128)(2,1)}, u32[]{:S(2)}, u32[]{:S(2)}) collective-permute-start(bf16[512,2,256]{0,2,1:T(8,128)(2,1)} %pad_maximum_fusion.6), channel_id=1, source_target_pairs={{0,1},{1,0},{2,3},{3,2},{4,5},{5,4},{6,7},{7,6},{8,9},{9,8},{10,11... | collective-permute-start | bytes 1572872 | tf_op jit(solution)/shard_map/ppermute | solution.py:97
  32.4 10.5 %collective-permute-start.4 = (bf16[512,256]{0,1:T(8,128)(2,1)S(1)}, bf16[512,256]{0,1:T(8,128)(2,1)S(1)}, u32[]{:S(2)}, u32[]{:S(2)}) collective-permute-start(bf16[512,256]{0,1:T(8,128)(2,1)S(1)} %collective-permute-done.2), channel_id=1, source_target_pairs={{0,4},{4,8},{8,12},{12,0},{1,5},{5,9},{9,13},{13,1},{2,6},{6,10},{... | collective-permute-start | bytes 786440 | tf_op jit(solution)/shard_map/ppermute | solution.py:192
  36.6 8.6 %copy-start.7 = (bf16[1024,256]{1,0:T(8,128)(2,1)S(1)}, bf16[1024,256]{1,0:T(8,128)(2,1)}, u32[]{:S(2)}) copy-start(bf16[1024,256]{1,0:T(8,128)(2,1)} %param.42) | copy-start | bytes 1572868
  43.0 9.7 %collective-permute-start.7 = (bf16[512,256]{0,1:T(8,128)(2,1)S(1)}, bf16[512,256]{0,1:T(8,128)(2,1)S(1)}, u32[]{:S(2)}, u32[]{:S(2)}) collective-permute-start(bf16[512,256]{0,1:T(8,128)(2,1)S(1)} %collective-permute-done.4), channel_id=1, source_target_pairs={{0,4},{4,8},{8,12},{12,0},{1,5},{5,9},{9,13},{13,1},{2,6},{6,10},{... | collective-permute-start | bytes 786440 | tf_op jit(solution)/shard_map/ppermute | solution.py:192
  43.0 7.9 %collective-permute-start.8 = (bf16[512,256]{0,1:T(8,128)(2,1)S(1)}, bf16[512,256]{0,1:T(8,128)(2,1)S(1)}, u32[]{:S(2)}, u32[]{:S(2)}) collective-permute-start(bf16[512,256]{0,1:T(8,128)(2,1)S(1)} %collective-permute-done.4), channel_id=1, source_target_pairs={{0,2},{1,3},{2,0},{3,1},{4,6},{5,7},{6,4},{7,5},{8,10},{9,11},{10,... | collective-permute-start | bytes 786440 | tf_op jit(solution)/shard_map/ppermute | solution.py:97
  44.8 1.0 copy-start.5
  45.9 1.0 copy-start.6
  50.2 2.0 %collective-permute-start.9 = (bf16[512,2,256]{0,2,1:T(8,128)(2,1)S(1)}, bf16[512,2,256]{0,2,1:T(8,128)(2,1)S(1)}, u32[]{:S(2)}, u32[]{:S(2)}) collective-permute-start(bf16[512,2,256]{0,2,1:T(8,128)(2,1)S(1)} %pad_maximum_fusion.7), channel_id=1, source_target_pairs={{0,1},{1,0},{2,3},{3,2},{4,5},{5,4},{6,7},{7,6},{8,9},{9,8},{10,11... | collective-permute-start | bytes 1572872 | tf_op jit(solution)/shard_map/ppermute | solution.py:97
  57.2 8.2 %collective-permute-start.10 = (bf16[512,256]{0,1:T(8,128)(2,1)S(1)}, bf16[512,256]{0,1:T(8,128)(2,1)S(1)}, u32[]{:S(2)}, u32[]{:S(2)}) collective-permute-start(bf16[512,256]{0,1:T(8,128)(2,1)S(1)} %collective-permute-done.7), channel_id=1, source_target_pairs={{0,2},{1,3},{2,0},{3,1},{4,6},{5,7},{6,4},{7,5},{8,10},{9,11},{10,... | collective-permute-start | bytes 786440 | tf_op jit(solution)/shard_map/ppermute | solution.py:97
  58.9 6.6 %collective-permute-start.11 = (bf16[512,2,256]{0,2,1:T(8,128)(2,1)S(1)}, bf16[512,2,256]{0,2,1:T(8,128)(2,1)S(1)}, u32[]{:S(2)}, u32[]{:S(2)}) collective-permute-start(bf16[512,2,256]{0,2,1:T(8,128)(2,1)S(1)} %pad_maximum_fusion.8), channel_id=1, source_target_pairs={{0,1},{1,0},{2,3},{3,2},{4,5},{5,4},{6,7},{7,6},{8,9},{9,8},{10,11... | collective-permute-start | bytes 1572872 | tf_op jit(solution)/shard_map/ppermute | solution.py:97
  67.6 3.0 %collective-permute-start.12 = (bf16[512,2,256]{0,2,1:T(8,128)(2,1)S(1)}, bf16[512,2,256]{0,2,1:T(8,128)(2,1)S(1)}, u32[]{:S(2)}, u32[]{:S(2)}) collective-permute-start(bf16[512,2,256]{0,2,1:T(8,128)(2,1)S(1)} %pad_maximum_fusion.9), channel_id=1, source_target_pairs={{0,1},{1,0},{2,3},{3,2},{4,5},{5,4},{6,7},{7,6},{8,9},{9,8},{10,11... | collective-permute-start | bytes 1572872 | tf_op jit(solution)/shard_map/ppermute | solution.py:97
  75.5 1.7 %collective-permute-start.13 = (bf16[256,2,256]{0,2,1:T(8,128)(2,1)S(1)}, bf16[256,2,256]{0,2,1:T(8,128)(2,1)S(1)}, u32[]{:S(2)}, u32[]{:S(2)}) collective-permute-start(bf16[256,2,256]{0,2,1:T(8,128)(2,1)S(1)} %fusion.130), channel_id=1, source_target_pairs={{0,1},{1,0},{2,3},{3,2},{4,5},{5,4},{6,7},{7,6},{8,9},{9,8},{10,11... | collective-permute-start | bytes 786440 | tf_op jit(solution)/shard_map/ppermute | solution.py:72
  77.0 1.6 %collective-permute-start.19 = (bf16[256,2,256]{0,2,1:T(8,128)(2,1)S(1)}, bf16[256,2,256]{0,2,1:T(8,128)(2,1)S(1)}, u32[]{:S(2)}, u32[]{:S(2)}) collective-permute-start(bf16[256,2,256]{0,2,1:T(8,128)(2,1)S(1)} %fusion.131), channel_id=1, source_target_pairs={{0,1},{1,0},{2,3},{3,2},{4,5},{5,4},{6,7},{7,6},{8,9},{9,8},{10,11... | collective-permute-start | bytes 786440 | tf_op jit(solution)/shard_map/ppermute | solution.py:72
  77.3 5.8 %collective-permute-start.14 = (bf16[256,256]{0,1:T(8,128)(2,1)S(1)}, bf16[256,256]{0,1:T(8,128)(2,1)S(1)}, u32[]{:S(2)}, u32[]{:S(2)}) collective-permute-start(bf16[256,256]{0,1:T(8,128)(2,1)S(1)} %fusion.150), channel_id=1, source_target_pairs={{0,2},{1,3},{2,0},{3,1},{4,6},{5,7},{6,4},{7,5},{8,10},{9,11},{10,... | collective-permute-start | bytes 393224 | tf_op jit(solution)/shard_map/ppermute | solution.py:72
  79.4 15.4 %copy-start.3 = (bf16[1024]{0:T(1024)(128)(2,1)S(1)}, bf16[1024]{0:T(1024)(128)(2,1)}, u32[]{:S(2)}) copy-start(bf16[1024]{0:T(1024)(128)(2,1)} %param.45) | copy-start | bytes 6148
  80.4 5.6 %collective-permute-start.20 = (bf16[256,256]{0,1:T(8,128)(2,1)S(1)}, bf16[256,256]{0,1:T(8,128)(2,1)S(1)}, u32[]{:S(2)}, u32[]{:S(2)}) collective-permute-start(bf16[256,256]{0,1:T(8,128)(2,1)S(1)} %fusion.152), channel_id=1, source_target_pairs={{0,2},{1,3},{2,0},{3,1},{4,6},{5,7},{6,4},{7,5},{8,10},{9,11},{10,... | collective-permute-start | bytes 393224 | tf_op jit(solution)/shard_map/ppermute | solution.py:72
  87.1 6.2 %collective-permute-start.21 = (bf16[256,256]{0,1:T(8,128)(2,1)S(1)}, bf16[256,256]{0,1:T(8,128)(2,1)S(1)}, u32[]{:S(2)}, u32[]{:S(2)}) collective-permute-start(bf16[256,256]{0,1:T(8,128)(2,1)S(1)} %get-tuple-element.241), channel_id=1, source_target_pairs={{0,2},{1,3},{2,0},{3,1},{4,6},{5,7},{6,4},{7,5},{8,10},{9,11},{10,... | collective-permute-start | bytes 393224 | tf_op jit(solution)/shard_map/ppermute | solution.py:86
  87.9 6.7 %collective-permute-start.15 = (bf16[256,256]{0,1:T(8,128)(2,1)S(1)}, bf16[256,256]{0,1:T(8,128)(2,1)S(1)}, u32[]{:S(2)}, u32[]{:S(2)}) collective-permute-start(bf16[256,256]{0,1:T(8,128)(2,1)S(1)} %get-tuple-element.240), channel_id=1, source_target_pairs={{0,2},{1,3},{2,0},{3,1},{4,6},{5,7},{6,4},{7,5},{8,10},{9,11},{10,... | collective-permute-start | bytes 393224 | tf_op jit(solution)/shard_map/ppermute | solution.py:86
  93.3 1.6 %collective-permute-start.22 = (bf16[256,2,256]{0,2,1:T(8,128)(2,1)S(1)}, bf16[256,2,256]{0,2,1:T(8,128)(2,1)S(1)}, u32[]{:S(2)}, u32[]{:S(2)}) collective-permute-start(bf16[256,2,256]{0,2,1:T(8,128)(2,1)S(1)} %pad_maximum_fusion.11), channel_id=1, source_target_pairs={{0,1},{1,0},{2,3},{3,2},{4,5},{5,4},{6,7},{7,6},{8,9},{9,8},{10,11... | collective-permute-start | bytes 786440 | tf_op jit(solution)/shard_map/ppermute | solution.py:86
  94.7 1.6 %collective-permute-start.16 = (bf16[256,2,256]{0,2,1:T(8,128)(2,1)S(1)}, bf16[256,2,256]{0,2,1:T(8,128)(2,1)S(1)}, u32[]{:S(2)}, u32[]{:S(2)}) collective-permute-start(bf16[256,2,256]{0,2,1:T(8,128)(2,1)S(1)} %pad_maximum_fusion.10), channel_id=1, source_target_pairs={{0,1},{1,0},{2,3},{3,2},{4,5},{5,4},{6,7},{7,6},{8,9},{9,8},{10,11... | collective-permute-start | bytes 786440 | tf_op jit(solution)/shard_map/ppermute | solution.py:86
  97.8 1.6 %copy-start.1 = (bf16[1024,1024]{1,0:T(8,128)(2,1)S(1)}, bf16[1024,1024]{1,0:T(8,128)(2,1)}, u32[]{:S(2)}) copy-start(bf16[1024,1024]{1,0:T(8,128)(2,1)} %param.47) | copy-start | bytes 6291460
  100.4 2.6 %collective-permute-start.23 = (bf16[256,2,256]{0,2,1:T(8,128)(2,1)S(1)}, bf16[256,2,256]{0,2,1:T(8,128)(2,1)S(1)}, u32[]{:S(2)}, u32[]{:S(2)}) collective-permute-start(bf16[256,2,256]{0,2,1:T(8,128)(2,1)S(1)} %fusion.133), channel_id=1, source_target_pairs={{0,1},{1,0},{2,3},{3,2},{4,5},{5,4},{6,7},{7,6},{8,9},{9,8},{10,11... | collective-permute-start | bytes 786440 | tf_op jit(solution)/shard_map/ppermute | solution.py:72
  102.5 1.6 %collective-permute-start.17 = (bf16[256,2,256]{0,2,1:T(8,128)(2,1)S(1)}, bf16[256,2,256]{0,2,1:T(8,128)(2,1)S(1)}, u32[]{:S(2)}, u32[]{:S(2)}) collective-permute-start(bf16[256,2,256]{0,2,1:T(8,128)(2,1)S(1)} %fusion.132), channel_id=1, source_target_pairs={{0,1},{1,0},{2,3},{3,2},{4,5},{5,4},{6,7},{7,6},{8,9},{9,8},{10,11... | collective-permute-start | bytes 786440 | tf_op jit(solution)/shard_map/ppermute | solution.py:72
  103.0 6.4 %collective-permute-start.24 = (bf16[256,256]{0,1:T(8,128)(2,1)S(1)}, bf16[256,256]{0,1:T(8,128)(2,1)S(1)}, u32[]{:S(2)}, u32[]{:S(2)}) collective-permute-start(bf16[256,256]{0,1:T(8,128)(2,1)S(1)} %fusion.153), channel_id=1, source_target_pairs={{0,2},{1,3},{2,0},{3,1},{4,6},{5,7},{6,4},{7,5},{8,10},{9,11},{10,... | collective-permute-start | bytes 393224 | tf_op jit(solution)/shard_map/ppermute | solution.py:72
  104.2 7.2 %collective-permute-start.18 = (bf16[256,256]{0,1:T(8,128)(2,1)S(1)}, bf16[256,256]{0,1:T(8,128)(2,1)S(1)}, u32[]{:S(2)}, u32[]{:S(2)}) collective-permute-start(bf16[256,256]{0,1:T(8,128)(2,1)S(1)} %fusion.151), channel_id=1, source_target_pairs={{0,2},{1,3},{2,0},{3,1},{4,6},{5,7},{6,4},{7,5},{8,10},{9,11},{10,... | collective-permute-start | bytes 393224 | tf_op jit(solution)/shard_map/ppermute | solution.py:72

commit v18 on v17

--- a/solution.py
+++ b/solution.py
@@ -201,7 +201,9 @@
             made.append((gathered, slot - 1))
         step = slot - 2
         if 0 <= step < dev_total:
-            normed_now = layer_norm(gathered[step], gain_one).astype(jnp.bfloat16)
+            normed_now = lax.optimization_barrier(
+                layer_norm(gathered[step], gain_one).astype(jnp.bfloat16)
+            )
             if step == 0:
                 queries = jnp.dot(
                     normed_now, query_weight, preferred_element_type=jnp.float32

time: 113 us -> 113 us (level)
  matrix products: 17.8 us -> 16.3 us
  other arithmetic: 16.2 us -> 17.5 us
    convert_element_type x0 -> x4, other arithmetic: none -> 1.33 us  [shards(): layer_norm(gathered[step], gain_one).astype(jnp.bfloat16)]
where the time goes in v18:
time: 113 us; the launch traced here: 112 us
  waiting for transfers between devices  40.2 us (36%)
  starting transfers between devices  22.5 us (20%)
  other arithmetic  17.5 us (15%)
  matrix products  16.3 us (14%)
  local copies, waits for them, and re-layouts  10.9 us (10%)
  between operations  4.62 us (4%)
    ppermute x8, waiting for transfers between devices, gather_levels(): lax.ppermute(current, 'heads', [(i, i ^ bit) for i in range(head_total)])  13 us
    ppermute x8, waiting for transfers between devices, scatter_heads(): lax.ppermute(give.astype(jnp.bfloat16), 'heads', [(i, i ^ bit) for i in r...  11.2 us
    ppermute x3, waiting for transfers between devices, shards(): ringed[slot + 1] = lax.ppermute(ringed[slot], 'bricks', ring)  9.17 us
    ppermute x4, waiting for transfers between devices, gather_heads(): lax.ppermute(current, 'heads', [(i, i ^ bit) for i in range(head_total)])  6.85 us
    ppermute x8, starting transfers between devices, gather_levels(): lax.ppermute(current, 'heads', [(i, i ^ bit) for i in range(head_total)])  5.88 us
    ppermute x1, starting transfers between devices, extended_2(): before = lax.ppermute(last, axis, up)  5.56 us
    ppermute x8, starting transfers between devices, scatter_heads(): lax.ppermute(give.astype(jnp.bfloat16), 'heads', [(i, i ^ bit) for i in r...  5.38 us
    dot_general x5, matrix products, absorb_block(): jnp.einsum('bhqk,khd->bqhd', weights.astype(jnp.bfloat16), value_rows, pr...  4.06 us
  transfers between devices with their start and end apart: 25, of which 19 were waited for; matrix products, arithmetic and copies ran while one was open for 21% of the time, Pallas kernels for 0%

profile of v18, /device:TPU:0, one launch (start us, length us, event | category | flops | bytes accessed | tf_op | source)
XLA Modules:
  0.0 112.1 jit_solution(3651079271637154681)
XLA Ops:
  0.0 0.9 fusion.169
  0.9 1.3 %collective-permute-start.1 = (bf16[64,256]{1,0:T(8,128)(2,1)S(1)}, bf16[64,256]{1,0:T(8,128)(2,1)S(1)}, u32[]{:S(2)}, u32[]{:S(2)}) collective-permute-start(bf16[64,256]{1,0:T(8,128)(2,1)S(1)} %get-tuple-element.245), channel_id=1, source_target_pairs={{4,0},{8,4},{12,8},{5,1},{9,5},{13,9},{6,2},{10,6},{14,10},{7,3},{... | collective-permute-start | bytes 98312 | tf_op jit(solution)/shard_map/ppermute | solution.py:21
  2.2 5.6 %collective-permute-start = (bf16[64,256]{1,0:T(8,128)(2,1)S(1)}, bf16[64,256]{1,0:T(8,128)(2,1)S(1)}, u32[]{:S(2)}, u32[]{:S(2)}) collective-permute-start(bf16[64,256]{1,0:T(8,128)(2,1)S(1)} %get-tuple-element.244), channel_id=1, source_target_pairs={{0,4},{4,8},{8,12},{1,5},{5,9},{9,13},{2,6},{6,10},{10,14},{3,7},{... | collective-permute-start | bytes 98312 | tf_op jit(solution)/shard_map/ppermute | solution.py:20
  7.8 1.0 fusion.170
  8.8 0.9 fusion.171
  9.7 1.1 copy.30
  10.8 1.4 %fusion.173 = (s32[1]{0:T(128)}, s32[1]{0:T(128)}) fusion(s32[4]{0:T(128)} %param.36, s32[]{:T(128)} %bitcast.2, s32[]{:T(128)} %bitcast.6), kind=kLoop, calls=%fused_computation.319 | loop fusion | bytes 24 | tf_op jit(solution)/shard_map/jit(_take)/gather | solution.py:157
  13.7 0.7 convert_element_type.243
  14.7 1.7 %fusion.102 = f32[1,8,8,8,256]{4,3,2,1,0:T(8,128)S(1)} fusion(f32[1,10,10,10,256]{4,3,2,1,0:T(8,128)S(1)} %select_maximum_fusion, f32[1,1,8,8,256]{4,3,2,1,0:T(8,128)S(1)} %multiply_bitcast_fusion, f32[1,8,8,8,256]{4,3,2,1,0:T(8,128)S(1)} %bitcast.546, f32[1,1,8,8,256]{4,3,2,1,0:T(8,128)S(1)} %multiply_bitcast_fusion.1, f32[256]{0:T(256)S(1)} %bitcast.597, ...), kind=kLoop, calls=%fused_computation.140 | loop fusion | flops 7208960 | bytes 13790208 | tf_op jit(solution)/shard_map/add | solution.py:51
  16.7 2.0 %collective-permute-start.3 = (bf16[512,256]{0,1:T(8,128)(2,1)S(1)}, bf16[512,256]{0,1:T(8,128)(2,1)S(1)}, u32[]{:S(2)}, u32[]{:S(2)}) collective-permute-start(bf16[512,256]{0,1:T(8,128)(2,1)S(1)} %add_convert_fusion), channel_id=1, source_target_pairs={{0,2},{1,3},{2,0},{3,1},{4,6},{5,7},{6,4},{7,5},{8,10},{9,11},{10,... | collective-permute-start | bytes 786440 | tf_op jit(solution)/shard_map/ppermute | solution.py:97
  18.7 1.6 %collective-permute-start.2 = (bf16[512,256]{0,1:T(8,128)(2,1)S(1)}, bf16[512,256]{0,1:T(8,128)(2,1)S(1)}, u32[]{:S(2)}, u32[]{:S(2)}) collective-permute-start(bf16[512,256]{0,1:T(8,128)(2,1)S(1)} %add_convert_fusion), channel_id=1, source_target_pairs={{0,4},{4,8},{8,12},{12,0},{1,5},{5,9},{9,13},{13,1},{2,6},{6,10},{... | collective-permute-start | bytes 786440 | tf_op jit(solution)/shard_map/ppermute | solution.py:192
  20.3 4.3 %collective-permute-done.3 = bf16[512,256]{0,1:T(8,128)(2,1)S(1)} collective-permute-done((bf16[512,256]{0,1:T(8,128)(2,1)S(1)}, bf16[512,256]{0,1:T(8,128)(2,1)S(1)}, u32[]{:S(2)}, u32[]{:S(2)}) %collective-permute-start.3) | collective-permute-done | bytes 262176 | tf_op jit(solution)/shard_map/ppermute | solution.py:97
  24.6 0.8 pad_maximum_fusion.6
  25.4 2.3 %collective-permute-done.2 = bf16[512,256]{0,1:T(8,128)(2,1)S(1)} collective-permute-done((bf16[512,256]{0,1:T(8,128)(2,1)S(1)}, bf16[512,256]{0,1:T(8,128)(2,1)S(1)}, u32[]{:S(2)}, u32[]{:S(2)}) %collective-permute-start.2) | collective-permute-done | bytes 262176 | tf_op jit(solution)/shard_map/ppermute | solution.py:192
  28.1 0.6 fusion.172
  31.2 1.2 %copy.65 = bf16[1024,256]{1,0:T(8,128)(2,1)S(1)} copy(bf16[1024,256]{0,1:T(8,128)(2,1)} %bitcast.559) | data formatting | bytes 1048576 | tf_op jit(solution)/shard_map/dot_general | solution.py:251
  32.4 0.6 collective-permute-start.4
  33.0 1.1 %collective-permute-done.5 = bf16[512,256]{0,1:T(8,128)(2,1)} collective-permute-done((bf16[512,256]{0,1:T(8,128)(2,1)S(1)}, bf16[512,256]{0,1:T(8,128)(2,1)}, u32[]{:S(2)}, u32[]{:S(2)}) %collective-permute-start.5) | collective-permute-done | bytes 262176 | tf_op jit(solution)/shard_map/ppermute | solution.py:97
  34.2 1.0 select_bitcast_fusion.17
  35.2 1.3 %select_bitcast_fusion.7 = (bf16[512,2,1,256]{0,3,1,2:T(8,128)(2,1)S(1)}, bf16[512,2,1,256]{0,3,1,2:T(8,128)(2,1)S(1)}) fusion(bf16[512,2,256]{0,2,1:T(8,128)(2,1)} %pad_maximum_fusion.6, bf16[512,2,256]{0,2,1:T(8,128)(2,1)} %collective-permute-done.6, pred[]{:T(512)S(6)} %eq.9), kind=kLoop, calls=%fused_computation.216 | loop fusion | flops 524288 | bytes 2097153 | tf_op jit(solution)/shard_map/stack | solution.py:100
  36.7 6.3 %collective-permute-done.4 = bf16[512,256]{0,1:T(8,128)(2,1)S(1)} collective-permute-done((bf16[512,256]{0,1:T(8,128)(2,1)S(1)}, bf16[512,256]{0,1:T(8,128)(2,1)S(1)}, u32[]{:S(2)}, u32[]{:S(2)}) %collective-permute-start.4) | collective-permute-done | bytes 262176 | tf_op jit(solution)/shard_map/ppermute | solution.py:192
  43.0 1.6 %collective-permute-start.8 = (bf16[512,256]{0,1:T(8,128)(2,1)S(1)}, bf16[512,256]{0,1:T(8,128)(2,1)S(1)}, u32[]{:S(2)}, u32[]{:S(2)}) collective-permute-start(bf16[512,256]{0,1:T(8,128)(2,1)S(1)} %collective-permute-done.4), channel_id=1, source_target_pairs={{0,2},{1,3},{2,0},{3,1},{4,6},{5,7},{6,4},{7,5},{8,10},{9,11},{10,... | collective-permute-start | bytes 786440 | tf_op jit(solution)/shard_map/ppermute | solution.py:97
  45.6 0.5 convolution_convert_fusion.8
  47.2 0.8 bitcast_reduce_fusion.2
  48.0 0.8 fusion.4
  48.9 1.0 fusion.56
  50.1 0.8 collective-permute-done.8
  51.0 0.8 collective-permute-done.9
  52.1 0.6 collective-permute-done.7
  54.6 0.8 bitcast_reduce_fusion.1
  55.4 0.8 fusion.6
  56.2 1.0 fusion.53
  57.2 1.7 %collective-permute-start.10 = (bf16[512,256]{0,1:T(8,128)(2,1)S(1)}, bf16[512,256]{0,1:T(8,128)(2,1)S(1)}, u32[]{:S(2)}, u32[]{:S(2)}) collective-permute-start(bf16[512,256]{0,1:T(8,128)(2,1)S(1)} %collective-permute-done.7), channel_id=1, source_target_pairs={{0,2},{1,3},{2,0},{3,1},{4,6},{5,7},{6,4},{7,5},{8,10},{9,11},{10,... | collective-permute-start | bytes 786440 | tf_op jit(solution)/shard_map/ppermute | solution.py:97
  59.0 6.0 %collective-permute-done.10 = bf16[512,256]{0,1:T(8,128)(2,1)S(1)} collective-permute-done((bf16[512,256]{0,1:T(8,128)(2,1)S(1)}, bf16[512,256]{0,1:T(8,128)(2,1)S(1)}, u32[]{:S(2)}, u32[]{:S(2)}) %collective-permute-start.10) | collective-permute-done | bytes 262176 | tf_op jit(solution)/shard_map/ppermute | solution.py:97
  67.4 1.0 bitcast_reduce_fusion
  68.4 0.8 fusion.8
  69.2 1.0 fusion.59
  72.4 0.5 bitcast_reduce_fusion.4
  72.9 0.5 bitcast_reduce_fusion.3
  74.3 0.6 fusion.66
  75.2 0.6 collective-permute-start.13
  75.8 0.6 fusion.67
  77.0 1.0 collective-permute-start.14
  78.3 0.8 bitcast_add_fusion.1
  79.1 1.0 fusion.146
  80.1 1.0 collective-permute-start.20
  81.1 1.8 %collective-permute-done.14 = bf16[256,256]{0,1:T(8,128)(2,1)S(1)} collective-permute-done((bf16[256,256]{0,1:T(8,128)(2,1)S(1)}, bf16[256,256]{0,1:T(8,128)(2,1)S(1)}, u32[]{:S(2)}, u32[]{:S(2)}) %collective-permute-start.14) | collective-permute-done | bytes 131104 | tf_op jit(solution)/shard_map/ppermute | solution.py:72
  82.9 2.8 %collective-permute-done.20 = bf16[256,256]{0,1:T(8,128)(2,1)S(1)} collective-permute-done((bf16[256,256]{0,1:T(8,128)(2,1)S(1)}, bf16[256,256]{0,1:T(8,128)(2,1)S(1)}, u32[]{:S(2)}, u32[]{:S(2)}) %collective-permute-start.20) | collective-permute-done | bytes 131104 | tf_op jit(solution)/shard_map/ppermute | solution.py:72
  85.7 1.0 fusion.141
  86.8 1.0 collective-permute-start.21
  87.8 1.1 collective-permute-start.15
  88.9 4.1 %collective-permute-done.21 = bf16[256,256]{0,1:T(8,128)(2,1)S(1)} collective-permute-done((bf16[256,256]{0,1:T(8,128)(2,1)S(1)}, bf16[256,256]{0,1:T(8,128)(2,1)S(1)}, u32[]{:S(2)}, u32[]{:S(2)}) %collective-permute-start.21) | collective-permute-done | bytes 131104 | tf_op jit(solution)/shard_map/ppermute | solution.py:86
  93.1 1.3 %collective-permute-done.15 = bf16[256,256]{0,1:T(8,128)(2,1)S(1)} collective-permute-done((bf16[256,256]{0,1:T(8,128)(2,1)S(1)}, bf16[256,256]{0,1:T(8,128)(2,1)S(1)}, u32[]{:S(2)}, u32[]{:S(2)}) %collective-permute-start.15) | collective-permute-done | bytes 131104 | tf_op jit(solution)/shard_map/ppermute | solution.py:86
  94.6 1.4 %collective-permute-done.16 = bf16[256,2,256]{0,2,1:T(8,128)(2,1)S(1)} collective-permute-done((bf16[256,2,256]{0,2,1:T(8,128)(2,1)S(1)}, bf16[256,2,256]{0,2,1:T(8,128)(2,1)S(1)}, u32[]{:S(2)}, u32[]{:S(2)}) %collective-permute-start.16) | collective-permute-done | bytes 262176 | tf_op jit(solution)/shard_map/ppermute | solution.py:86
  97.5 0.9 fusion.83
  98.4 0.6 copy-done.1
  99.1 1.0 fusion.177
  100.3 0.9 fusion.75
  101.2 1.0 fusion.175
  102.7 1.0 collective-permute-start.24
  103.9 1.1 collective-permute-start.18
  105.0 4.2 %collective-permute-done.24 = bf16[256,256]{0,1:T(8,128)(2,1)S(1)} collective-permute-done((bf16[256,256]{0,1:T(8,128)(2,1)S(1)}, bf16[256,256]{0,1:T(8,128)(2,1)S(1)}, u32[]{:S(2)}, u32[]{:S(2)}) %collective-permute-start.24) | collective-permute-done | bytes 131104 | tf_op jit(solution)/shard_map/ppermute | solution.py:72
  109.2 1.9 %collective-permute-done.18 = bf16[256,256]{0,1:T(8,128)(2,1)S(1)} collective-permute-done((bf16[256,256]{0,1:T(8,128)(2,1)S(1)}, bf16[256,256]{0,1:T(8,128)(2,1)S(1)}, u32[]{:S(2)}, u32[]{:S(2)}) %collective-permute-start.18) | collective-permute-done | bytes 131104 | tf_op jit(solution)/shard_map/ppermute | solution.py:72
  111.2 0.8 copy.53
  (137 shorter events, 15.4 us)
Async XLA Ops:
  0.0 97.5 %copy-start = (bf16[1024,1024]{1,0:T(8,128)(2,1)S(1)}, bf16[1024,1024]{1,0:T(8,128)(2,1)}, u32[]{:S(2)}) copy-start(bf16[1024,1024]{1,0:T(8,128)(2,1)} %param.46) | copy-start | bytes 6291460
  0.9 13.4 %collective-permute-start.1 = (bf16[64,256]{1,0:T(8,128)(2,1)S(1)}, bf16[64,256]{1,0:T(8,128)(2,1)S(1)}, u32[]{:S(2)}, u32[]{:S(2)}) collective-permute-start(bf16[64,256]{1,0:T(8,128)(2,1)S(1)} %get-tuple-element.245), channel_id=1, source_target_pairs={{4,0},{8,4},{12,8},{5,1},{9,5},{13,9},{6,2},{10,6},{14,10},{7,3},{... | collective-permute-start | bytes 98312 | tf_op jit(solution)/shard_map/ppermute | solution.py:21
  2.2 12.2 %collective-permute-start = (bf16[64,256]{1,0:T(8,128)(2,1)S(1)}, bf16[64,256]{1,0:T(8,128)(2,1)S(1)}, u32[]{:S(2)}, u32[]{:S(2)}) collective-permute-start(bf16[64,256]{1,0:T(8,128)(2,1)S(1)} %get-tuple-element.244), channel_id=1, source_target_pairs={{0,4},{4,8},{8,12},{1,5},{5,9},{9,13},{2,6},{6,10},{10,14},{3,7},{... | collective-permute-start | bytes 98312 | tf_op jit(solution)/shard_map/ppermute | solution.py:20
  16.3 11.7 %copy-start.2 = (bf16[1024]{0:T(1024)(128)(2,1)S(1)}, bf16[1024]{0:T(1024)(128)(2,1)}, u32[]{:S(2)}) copy-start(bf16[1024]{0:T(1024)(128)(2,1)} %param.40) | copy-start | bytes 6148
  16.3 11.7 %copy-start.4 = (s32[4,4]{1,0:T(4,128)S(1)}, s32[4,4]{1,0:T(4,128)}, u32[]{:S(2)}) copy-start(s32[4,4]{1,0:T(4,128)} %param.37) | copy-start | bytes 196
  16.7 7.8 %collective-permute-start.3 = (bf16[512,256]{0,1:T(8,128)(2,1)S(1)}, bf16[512,256]{0,1:T(8,128)(2,1)S(1)}, u32[]{:S(2)}, u32[]{:S(2)}) collective-permute-start(bf16[512,256]{0,1:T(8,128)(2,1)S(1)} %add_convert_fusion), channel_id=1, source_target_pairs={{0,2},{1,3},{2,0},{3,1},{4,6},{5,7},{6,4},{7,5},{8,10},{9,11},{10,... | collective-permute-start | bytes 786440 | tf_op jit(solution)/shard_map/ppermute | solution.py:97
  18.7 9.0 %collective-permute-start.2 = (bf16[512,256]{0,1:T(8,128)(2,1)S(1)}, bf16[512,256]{0,1:T(8,128)(2,1)S(1)}, u32[]{:S(2)}, u32[]{:S(2)}) collective-permute-start(bf16[512,256]{0,1:T(8,128)(2,1)S(1)} %add_convert_fusion), channel_id=1, source_target_pairs={{0,4},{4,8},{8,12},{12,0},{1,5},{5,9},{9,13},{13,1},{2,6},{6,10},{... | collective-permute-start | bytes 786440 | tf_op jit(solution)/shard_map/ppermute | solution.py:192
  27.7 6.5 %collective-permute-start.5 = (bf16[512,256]{0,1:T(8,128)(2,1)S(1)}, bf16[512,256]{0,1:T(8,128)(2,1)}, u32[]{:S(2)}, u32[]{:S(2)}) collective-permute-start(bf16[512,256]{0,1:T(8,128)(2,1)S(1)} %collective-permute-done.2), channel_id=1, source_target_pairs={{0,2},{1,3},{2,0},{3,1},{4,6},{5,7},{6,4},{7,5},{8,10},{9,11},{10,... | collective-permute-start | bytes 786440 | tf_op jit(solution)/shard_map/ppermute | solution.py:97
  28.1 7.2 %collective-permute-start.6 = (bf16[512,2,256]{0,2,1:T(8,128)(2,1)}, bf16[512,2,256]{0,2,1:T(8,128)(2,1)}, u32[]{:S(2)}, u32[]{:S(2)}) collective-permute-start(bf16[512,2,256]{0,2,1:T(8,128)(2,1)} %pad_maximum_fusion.6), channel_id=1, source_target_pairs={{0,1},{1,0},{2,3},{3,2},{4,5},{5,4},{6,7},{7,6},{8,9},{9,8},{10,11... | collective-permute-start | bytes 1572872 | tf_op jit(solution)/shard_map/ppermute | solution.py:97
  32.4 10.5 %collective-permute-start.4 = (bf16[512,256]{0,1:T(8,128)(2,1)S(1)}, bf16[512,256]{0,1:T(8,128)(2,1)S(1)}, u32[]{:S(2)}, u32[]{:S(2)}) collective-permute-start(bf16[512,256]{0,1:T(8,128)(2,1)S(1)} %collective-permute-done.2), channel_id=1, source_target_pairs={{0,4},{4,8},{8,12},{12,0},{1,5},{5,9},{9,13},{13,1},{2,6},{6,10},{... | collective-permute-start | bytes 786440 | tf_op jit(solution)/shard_map/ppermute | solution.py:192
  43.0 2.6 %copy-start.7 = (bf16[1024,256]{1,0:T(8,128)(2,1)S(1)}, bf16[1024,256]{1,0:T(8,128)(2,1)}, u32[]{:S(2)}) copy-start(bf16[1024,256]{1,0:T(8,128)(2,1)} %param.42) | copy-start | bytes 1572868
  43.0 9.7 %collective-permute-start.7 = (bf16[512,256]{0,1:T(8,128)(2,1)S(1)}, bf16[512,256]{0,1:T(8,128)(2,1)S(1)}, u32[]{:S(2)}, u32[]{:S(2)}) collective-permute-start(bf16[512,256]{0,1:T(8,128)(2,1)S(1)} %collective-permute-done.4), channel_id=1, source_target_pairs={{0,4},{4,8},{8,12},{12,0},{1,5},{5,9},{9,13},{13,1},{2,6},{6,10},{... | collective-permute-start | bytes 786440 | tf_op jit(solution)/shard_map/ppermute | solution.py:192
  43.0 7.9 %collective-permute-start.8 = (bf16[512,256]{0,1:T(8,128)(2,1)S(1)}, bf16[512,256]{0,1:T(8,128)(2,1)S(1)}, u32[]{:S(2)}, u32[]{:S(2)}) collective-permute-start(bf16[512,256]{0,1:T(8,128)(2,1)S(1)} %collective-permute-done.4), channel_id=1, source_target_pairs={{0,2},{1,3},{2,0},{3,1},{4,6},{5,7},{6,4},{7,5},{8,10},{9,11},{10,... | collective-permute-start | bytes 786440 | tf_op jit(solution)/shard_map/ppermute | solution.py:97
  45.2 1.0 copy-start.5
  45.5 1.2 %copy-start.6 = (bf16[1024,256]{1,0:T(8,128)(2,1)S(1)}, bf16[1024,256]{1,0:T(8,128)(2,1)}, u32[]{:S(2)}) copy-start(bf16[1024,256]{1,0:T(8,128)(2,1)} %param.43) | copy-start | bytes 1572868
  49.8 2.0 %collective-permute-start.9 = (bf16[512,2,256]{0,2,1:T(8,128)(2,1)S(1)}, bf16[512,2,256]{0,2,1:T(8,128)(2,1)S(1)}, u32[]{:S(2)}, u32[]{:S(2)}) collective-permute-start(bf16[512,2,256]{0,2,1:T(8,128)(2,1)S(1)} %pad_maximum_fusion.7), channel_id=1, source_target_pairs={{0,1},{1,0},{2,3},{3,2},{4,5},{5,4},{6,7},{7,6},{8,9},{9,8},{10,11... | collective-permute-start | bytes 1572872 | tf_op jit(solution)/shard_map/ppermute | solution.py:97
  57.2 7.8 %collective-permute-start.10 = (bf16[512,256]{0,1:T(8,128)(2,1)S(1)}, bf16[512,256]{0,1:T(8,128)(2,1)S(1)}, u32[]{:S(2)}, u32[]{:S(2)}) collective-permute-start(bf16[512,256]{0,1:T(8,128)(2,1)S(1)} %collective-permute-done.7), channel_id=1, source_target_pairs={{0,2},{1,3},{2,0},{3,1},{4,6},{5,7},{6,4},{7,5},{8,10},{9,11},{10,... | collective-permute-start | bytes 786440 | tf_op jit(solution)/shard_map/ppermute | solution.py:97
  58.9 6.2 %collective-permute-start.11 = (bf16[512,2,256]{0,2,1:T(8,128)(2,1)S(1)}, bf16[512,2,256]{0,2,1:T(8,128)(2,1)S(1)}, u32[]{:S(2)}, u32[]{:S(2)}) collective-permute-start(bf16[512,2,256]{0,2,1:T(8,128)(2,1)S(1)} %pad_maximum_fusion.8), channel_id=1, source_target_pairs={{0,1},{1,0},{2,3},{3,2},{4,5},{5,4},{6,7},{7,6},{8,9},{9,8},{10,11... | collective-permute-start | bytes 1572872 | tf_op jit(solution)/shard_map/ppermute | solution.py:97
  67.3 3.0 %collective-permute-start.12 = (bf16[512,2,256]{0,2,1:T(8,128)(2,1)S(1)}, bf16[512,2,256]{0,2,1:T(8,128)(2,1)S(1)}, u32[]{:S(2)}, u32[]{:S(2)}) collective-permute-start(bf16[512,2,256]{0,2,1:T(8,128)(2,1)S(1)} %pad_maximum_fusion.9), channel_id=1, source_target_pairs={{0,1},{1,0},{2,3},{3,2},{4,5},{5,4},{6,7},{7,6},{8,9},{9,8},{10,11... | collective-permute-start | bytes 1572872 | tf_op jit(solution)/shard_map/ppermute | solution.py:97
  75.2 1.7 %collective-permute-start.13 = (bf16[256,2,256]{0,2,1:T(8,128)(2,1)S(1)}, bf16[256,2,256]{0,2,1:T(8,128)(2,1)S(1)}, u32[]{:S(2)}, u32[]{:S(2)}) collective-permute-start(bf16[256,2,256]{0,2,1:T(8,128)(2,1)S(1)} %fusion.130), channel_id=1, source_target_pairs={{0,1},{1,0},{2,3},{3,2},{4,5},{5,4},{6,7},{7,6},{8,9},{9,8},{10,11... | collective-permute-start | bytes 786440 | tf_op jit(solution)/shard_map/ppermute | solution.py:72
  76.7 1.6 %collective-permute-start.19 = (bf16[256,2,256]{0,2,1:T(8,128)(2,1)S(1)}, bf16[256,2,256]{0,2,1:T(8,128)(2,1)S(1)}, u32[]{:S(2)}, u32[]{:S(2)}) collective-permute-start(bf16[256,2,256]{0,2,1:T(8,128)(2,1)S(1)} %fusion.131), channel_id=1, source_target_pairs={{0,1},{1,0},{2,3},{3,2},{4,5},{5,4},{6,7},{7,6},{8,9},{9,8},{10,11... | collective-permute-start | bytes 786440 | tf_op jit(solution)/shard_map/ppermute | solution.py:72
  77.0 5.8 %collective-permute-start.14 = (bf16[256,256]{0,1:T(8,128)(2,1)S(1)}, bf16[256,256]{0,1:T(8,128)(2,1)S(1)}, u32[]{:S(2)}, u32[]{:S(2)}) collective-permute-start(bf16[256,256]{0,1:T(8,128)(2,1)S(1)} %fusion.144), channel_id=1, source_target_pairs={{0,2},{1,3},{2,0},{3,1},{4,6},{5,7},{6,4},{7,5},{8,10},{9,11},{10,... | collective-permute-start | bytes 393224 | tf_op jit(solution)/shard_map/ppermute | solution.py:72
  79.1 15.4 %copy-start.3 = (bf16[1024]{0:T(1024)(128)(2,1)S(1)}, bf16[1024]{0:T(1024)(128)(2,1)}, u32[]{:S(2)}) copy-start(bf16[1024]{0:T(1024)(128)(2,1)} %param.45) | copy-start | bytes 6148
  80.1 5.6 %collective-permute-start.20 = (bf16[256,256]{0,1:T(8,128)(2,1)S(1)}, bf16[256,256]{0,1:T(8,128)(2,1)S(1)}, u32[]{:S(2)}, u32[]{:S(2)}) collective-permute-start(bf16[256,256]{0,1:T(8,128)(2,1)S(1)} %fusion.146), channel_id=1, source_target_pairs={{0,2},{1,3},{2,0},{3,1},{4,6},{5,7},{6,4},{7,5},{8,10},{9,11},{10,... | collective-permute-start | bytes 393224 | tf_op jit(solution)/shard_map/ppermute | solution.py:72
  86.8 6.2 %collective-permute-start.21 = (bf16[256,256]{0,1:T(8,128)(2,1)S(1)}, bf16[256,256]{0,1:T(8,128)(2,1)S(1)}, u32[]{:S(2)}, u32[]{:S(2)}) collective-permute-start(bf16[256,256]{0,1:T(8,128)(2,1)S(1)} %get-tuple-element.241), channel_id=1, source_target_pairs={{0,2},{1,3},{2,0},{3,1},{4,6},{5,7},{6,4},{7,5},{8,10},{9,11},{10,... | collective-permute-start | bytes 393224 | tf_op jit(solution)/shard_map/ppermute | solution.py:86
  87.8 6.6 %collective-permute-start.15 = (bf16[256,256]{0,1:T(8,128)(2,1)S(1)}, bf16[256,256]{0,1:T(8,128)(2,1)S(1)}, u32[]{:S(2)}, u32[]{:S(2)}) collective-permute-start(bf16[256,256]{0,1:T(8,128)(2,1)S(1)} %get-tuple-element.240), channel_id=1, source_target_pairs={{0,2},{1,3},{2,0},{3,1},{4,6},{5,7},{6,4},{7,5},{8,10},{9,11},{10,... | collective-permute-start | bytes 393224 | tf_op jit(solution)/shard_map/ppermute | solution.py:86
  93.0 1.6 %collective-permute-start.22 = (bf16[256,2,256]{0,2,1:T(8,128)(2,1)S(1)}, bf16[256,2,256]{0,2,1:T(8,128)(2,1)S(1)}, u32[]{:S(2)}, u32[]{:S(2)}) collective-permute-start(bf16[256,2,256]{0,2,1:T(8,128)(2,1)S(1)} %pad_maximum_fusion.11), channel_id=1, source_target_pairs={{0,1},{1,0},{2,3},{3,2},{4,5},{5,4},{6,7},{7,6},{8,9},{9,8},{10,11... | collective-permute-start | bytes 786440 | tf_op jit(solution)/shard_map/ppermute | solution.py:86
  94.4 1.6 %collective-permute-start.16 = (bf16[256,2,256]{0,2,1:T(8,128)(2,1)S(1)}, bf16[256,2,256]{0,2,1:T(8,128)(2,1)S(1)}, u32[]{:S(2)}, u32[]{:S(2)}) collective-permute-start(bf16[256,2,256]{0,2,1:T(8,128)(2,1)S(1)} %pad_maximum_fusion.10), channel_id=1, source_target_pairs={{0,1},{1,0},{2,3},{3,2},{4,5},{5,4},{6,7},{7,6},{8,9},{9,8},{10,11... | collective-permute-start | bytes 786440 | tf_op jit(solution)/shard_map/ppermute | solution.py:86
  97.5 1.6 %copy-start.1 = (bf16[1024,1024]{1,0:T(8,128)(2,1)S(1)}, bf16[1024,1024]{1,0:T(8,128)(2,1)}, u32[]{:S(2)}) copy-start(bf16[1024,1024]{1,0:T(8,128)(2,1)} %param.47) | copy-start | bytes 6291460
  100.1 2.6 %collective-permute-start.23 = (bf16[256,2,256]{0,2,1:T(8,128)(2,1)S(1)}, bf16[256,2,256]{0,2,1:T(8,128)(2,1)S(1)}, u32[]{:S(2)}, u32[]{:S(2)}) collective-permute-start(bf16[256,2,256]{0,2,1:T(8,128)(2,1)S(1)} %fusion.133), channel_id=1, source_target_pairs={{0,1},{1,0},{2,3},{3,2},{4,5},{5,4},{6,7},{7,6},{8,9},{9,8},{10,11... | collective-permute-start | bytes 786440 | tf_op jit(solution)/shard_map/ppermute | solution.py:72
  102.2 1.6 %collective-permute-start.17 = (bf16[256,2,256]{0,2,1:T(8,128)(2,1)S(1)}, bf16[256,2,256]{0,2,1:T(8,128)(2,1)S(1)}, u32[]{:S(2)}, u32[]{:S(2)}) collective-permute-start(bf16[256,2,256]{0,2,1:T(8,128)(2,1)S(1)} %fusion.132), channel_id=1, source_target_pairs={{0,1},{1,0},{2,3},{3,2},{4,5},{5,4},{6,7},{7,6},{8,9},{9,8},{10,11... | collective-permute-start | bytes 786440 | tf_op jit(solution)/shard_map/ppermute | solution.py:72
  102.7 6.4 %collective-permute-start.24 = (bf16[256,256]{0,1:T(8,128)(2,1)S(1)}, bf16[256,256]{0,1:T(8,128)(2,1)S(1)}, u32[]{:S(2)}, u32[]{:S(2)}) collective-permute-start(bf16[256,256]{0,1:T(8,128)(2,1)S(1)} %fusion.147), channel_id=1, source_target_pairs={{0,2},{1,3},{2,0},{3,1},{4,6},{5,7},{6,4},{7,5},{8,10},{9,11},{10,... | collective-permute-start | bytes 393224 | tf_op jit(solution)/shard_map/ppermute | solution.py:72
  103.9 7.2 %collective-permute-start.18 = (bf16[256,256]{0,1:T(8,128)(2,1)S(1)}, bf16[256,256]{0,1:T(8,128)(2,1)S(1)}, u32[]{:S(2)}, u32[]{:S(2)}) collective-permute-start(bf16[256,256]{0,1:T(8,128)(2,1)S(1)} %fusion.145), channel_id=1, source_target_pairs={{0,2},{1,3},{2,0},{3,1},{4,6},{5,7},{6,4},{7,5},{8,10},{9,11},{10,... | collective-permute-start | bytes 393224 | tf_op jit(solution)/shard_map/ppermute | solution.py:72

commit v19 on v17

--- a/solution.py
+++ b/solution.py
@@ -250,7 +250,9 @@
         out_sum = scatter_heads(partial_out, head_id, head_total)
         stream_two = (stream[rows].astype(jnp.float32) + out_sum).astype(jnp.bfloat16)
         stream_two_full = gather_heads(stream_two, head_id, head_total)
-        normed_two = layer_norm(stream_two_full, gain_two).astype(jnp.bfloat16)
+        normed_two = lax.optimization_barrier(
+            layer_norm(stream_two_full, gain_two).astype(jnp.bfloat16)
+        )
         hidden = jax.nn.gelu(
             jnp.dot(normed_two, up_weight, preferred_element_type=jnp.float32), approximate=True
         ).astype(jnp.bfloat16)

time: 113 us -> 113 us (level)
  no operation moved by 1% of the time
where the time goes in v19:
time: 113 us; the launch traced here: 112 us
  waiting for transfers between devices  40.8 us (36%)
  starting transfers between devices  21.9 us (19%)
  matrix products  17.8 us (16%)
  other arithmetic  16.2 us (14%)
  local copies, waits for them, and re-layouts  11.2 us (10%)
  between operations  4.58 us (4%)
    ppermute x8, waiting for transfers between devices, gather_levels(): lax.ppermute(current, 'heads', [(i, i ^ bit) for i in range(head_total)])  13.3 us
    ppermute x8, waiting for transfers between devices, scatter_heads(): lax.ppermute(give.astype(jnp.bfloat16), 'heads', [(i, i ^ bit) for i in r...  11.8 us
    ppermute x3, waiting for transfers between devices, shards(): ringed[slot + 1] = lax.ppermute(ringed[slot], 'bricks', ring)  8.81 us
    ppermute x4, waiting for transfers between devices, gather_heads(): lax.ppermute(current, 'heads', [(i, i ^ bit) for i in range(head_total)])  6.85 us
    ppermute x8, starting transfers between devices, gather_levels(): lax.ppermute(current, 'heads', [(i, i ^ bit) for i in range(head_total)])  5.88 us
    ppermute x1, starting transfers between devices, extended_2(): before = lax.ppermute(last, axis, up)  5.56 us
    ppermute x8, starting transfers between devices, scatter_heads(): lax.ppermute(give.astype(jnp.bfloat16), 'heads', [(i, i ^ bit) for i in r...  4.76 us
    dot_general x5, matrix products, absorb_block(): jnp.einsum('bhqk,khd->bqhd', weights.astype(jnp.bfloat16), value_rows, pr...  4.05 us
  transfers between devices with their start and end apart: 25, of which 19 were waited for; matrix products, arithmetic and copies ran while one was open for 21% of the time, Pallas kernels for 0%

profile of v19, /device:TPU:0, one launch (start us, length us, event | category | flops | bytes accessed | tf_op | source)
XLA Modules:
  0.0 112.4 jit_solution(6159938960314966302)
XLA Ops:
  0.0 0.9 fusion.178
  0.9 1.3 %collective-permute-start.1 = (bf16[64,256]{1,0:T(8,128)(2,1)S(1)}, bf16[64,256]{1,0:T(8,128)(2,1)S(1)}, u32[]{:S(2)}, u32[]{:S(2)}) collective-permute-start(bf16[64,256]{1,0:T(8,128)(2,1)S(1)} %get-tuple-element.245), channel_id=1, source_target_pairs={{4,0},{8,4},{12,8},{5,1},{9,5},{13,9},{6,2},{10,6},{14,10},{7,3},{... | collective-permute-start | bytes 98312 | tf_op jit(solution)/shard_map/ppermute | solution.py:21
  2.2 5.6 %collective-permute-start = (bf16[64,256]{1,0:T(8,128)(2,1)S(1)}, bf16[64,256]{1,0:T(8,128)(2,1)S(1)}, u32[]{:S(2)}, u32[]{:S(2)}) collective-permute-start(bf16[64,256]{1,0:T(8,128)(2,1)S(1)} %get-tuple-element.244), channel_id=1, source_target_pairs={{0,4},{4,8},{8,12},{1,5},{5,9},{9,13},{2,6},{6,10},{10,14},{3,7},{... | collective-permute-start | bytes 98312 | tf_op jit(solution)/shard_map/ppermute | solution.py:20
  7.8 1.0 fusion.179
  8.8 0.9 fusion.180
  9.7 1.1 copy.30
  10.8 1.4 %fusion.182 = (s32[1]{0:T(128)}, s32[1]{0:T(128)}) fusion(s32[4]{0:T(128)} %param.36, s32[]{:T(128)} %bitcast.2, s32[]{:T(128)} %bitcast.6), kind=kLoop, calls=%fused_computation.319 | loop fusion | bytes 24 | tf_op jit(solution)/shard_map/jit(_take)/gather | solution.py:157
  13.7 0.7 convert_element_type.243
  14.7 1.7 %fusion.102 = f32[1,8,8,8,256]{4,3,2,1,0:T(8,128)S(1)} fusion(f32[1,10,10,10,256]{4,3,2,1,0:T(8,128)S(1)} %select_maximum_fusion, f32[1,1,8,8,256]{4,3,2,1,0:T(8,128)S(1)} %multiply_bitcast_fusion, f32[1,8,8,8,256]{4,3,2,1,0:T(8,128)S(1)} %bitcast.542, f32[1,1,8,8,256]{4,3,2,1,0:T(8,128)S(1)} %multiply_bitcast_fusion.1, f32[256]{0:T(256)S(1)} %bitcast.593, ...), kind=kLoop, calls=%fused_computation.140 | loop fusion | flops 7208960 | bytes 13790208 | tf_op jit(solution)/shard_map/add | solution.py:51
  16.7 2.0 %collective-permute-start.3 = (bf16[512,256]{0,1:T(8,128)(2,1)S(1)}, bf16[512,256]{0,1:T(8,128)(2,1)S(1)}, u32[]{:S(2)}, u32[]{:S(2)}) collective-permute-start(bf16[512,256]{0,1:T(8,128)(2,1)S(1)} %add_convert_fusion), channel_id=1, source_target_pairs={{0,2},{1,3},{2,0},{3,1},{4,6},{5,7},{6,4},{7,5},{8,10},{9,11},{10,... | collective-permute-start | bytes 786440 | tf_op jit(solution)/shard_map/ppermute | solution.py:97
  18.7 1.6 %collective-permute-start.2 = (bf16[512,256]{0,1:T(8,128)(2,1)S(1)}, bf16[512,256]{0,1:T(8,128)(2,1)S(1)}, u32[]{:S(2)}, u32[]{:S(2)}) collective-permute-start(bf16[512,256]{0,1:T(8,128)(2,1)S(1)} %add_convert_fusion), channel_id=1, source_target_pairs={{0,4},{4,8},{8,12},{12,0},{1,5},{5,9},{9,13},{13,1},{2,6},{6,10},{... | collective-permute-start | bytes 786440 | tf_op jit(solution)/shard_map/ppermute | solution.py:192
  20.3 4.3 %collective-permute-done.3 = bf16[512,256]{0,1:T(8,128)(2,1)S(1)} collective-permute-done((bf16[512,256]{0,1:T(8,128)(2,1)S(1)}, bf16[512,256]{0,1:T(8,128)(2,1)S(1)}, u32[]{:S(2)}, u32[]{:S(2)}) %collective-permute-start.3) | collective-permute-done | bytes 262176 | tf_op jit(solution)/shard_map/ppermute | solution.py:97
  24.6 0.8 pad_maximum_fusion.6
  25.4 2.3 %collective-permute-done.2 = bf16[512,256]{0,1:T(8,128)(2,1)S(1)} collective-permute-done((bf16[512,256]{0,1:T(8,128)(2,1)S(1)}, bf16[512,256]{0,1:T(8,128)(2,1)S(1)}, u32[]{:S(2)}, u32[]{:S(2)}) %collective-permute-start.2) | collective-permute-done | bytes 262176 | tf_op jit(solution)/shard_map/ppermute | solution.py:192
  28.1 0.6 fusion.181
  31.2 1.2 %copy.65 = bf16[1024,256]{1,0:T(8,128)(2,1)S(1)} copy(bf16[1024,256]{0,1:T(8,128)(2,1)} %bitcast.555) | data formatting | bytes 1048576 | tf_op jit(solution)/shard_map/dot_general | solution.py:249
  33.0 1.1 %collective-permute-done.5 = bf16[512,256]{0,1:T(8,128)(2,1)} collective-permute-done((bf16[512,256]{0,1:T(8,128)(2,1)S(1)}, bf16[512,256]{0,1:T(8,128)(2,1)}, u32[]{:S(2)}, u32[]{:S(2)}) %collective-permute-start.5) | collective-permute-done | bytes 262176 | tf_op jit(solution)/shard_map/ppermute | solution.py:97
  34.2 1.0 select_bitcast_fusion.17
  35.2 1.3 %select_bitcast_fusion.7 = (bf16[512,2,1,256]{0,3,1,2:T(8,128)(2,1)S(1)}, bf16[512,2,1,256]{0,3,1,2:T(8,128)(2,1)S(1)}) fusion(bf16[512,2,256]{0,2,1:T(8,128)(2,1)} %pad_maximum_fusion.6, bf16[512,2,256]{0,2,1:T(8,128)(2,1)} %collective-permute-done.6, pred[]{:T(512)S(6)} %eq.9), kind=kLoop, calls=%fused_computation.216 | loop fusion | flops 524288 | bytes 2097153 | tf_op jit(solution)/shard_map/stack | solution.py:100
  36.7 6.3 %collective-permute-done.4 = bf16[512,256]{0,1:T(8,128)(2,1)S(1)} collective-permute-done((bf16[512,256]{0,1:T(8,128)(2,1)S(1)}, bf16[512,256]{0,1:T(8,128)(2,1)S(1)}, u32[]{:S(2)}, u32[]{:S(2)}) %collective-permute-start.4) | collective-permute-done | bytes 262176 | tf_op jit(solution)/shard_map/ppermute | solution.py:192
  43.0 1.6 %collective-permute-start.8 = (bf16[512,256]{0,1:T(8,128)(2,1)S(1)}, bf16[512,256]{0,1:T(8,128)(2,1)S(1)}, u32[]{:S(2)}, u32[]{:S(2)}) collective-permute-start(bf16[512,256]{0,1:T(8,128)(2,1)S(1)} %collective-permute-done.4), channel_id=1, source_target_pairs={{0,2},{1,3},{2,0},{3,1},{4,6},{5,7},{6,4},{7,5},{8,10},{9,11},{10,... | collective-permute-start | bytes 786440 | tf_op jit(solution)/shard_map/ppermute | solution.py:97
  45.2 0.6 convolution_convert_fusion.8
  45.9 0.6 convolution_convert_fusion.7
  46.9 0.6 convolution_convert_fusion.6
  47.6 0.8 bitcast_reduce_fusion.2
  48.4 0.8 fusion.4
  49.2 1.0 fusion.56
  51.0 1.2 %collective-permute-done.9 = bf16[512,2,256]{0,2,1:T(8,128)(2,1)S(1)} collective-permute-done((bf16[512,2,256]{0,2,1:T(8,128)(2,1)S(1)}, bf16[512,2,256]{0,2,1:T(8,128)(2,1)S(1)}, u32[]{:S(2)}, u32[]{:S(2)}) %collective-permute-start.9) | collective-permute-done | bytes 524320 | tf_op jit(solution)/shard_map/ppermute | solution.py:97
  53.3 0.6 convolution_convert_fusion.5
  53.9 0.6 convolution_convert_fusion.4
  54.6 0.8 bitcast_reduce_fusion.1
  55.4 0.8 fusion.6
  56.2 1.0 fusion.53
  57.2 1.7 %collective-permute-start.10 = (bf16[512,256]{0,1:T(8,128)(2,1)S(1)}, bf16[512,256]{0,1:T(8,128)(2,1)S(1)}, u32[]{:S(2)}, u32[]{:S(2)}) collective-permute-start(bf16[512,256]{0,1:T(8,128)(2,1)S(1)} %collective-permute-done.7), channel_id=1, source_target_pairs={{0,2},{1,3},{2,0},{3,1},{4,6},{5,7},{6,4},{7,5},{8,10},{9,11},{10,... | collective-permute-start | bytes 786440 | tf_op jit(solution)/shard_map/ppermute | solution.py:97
  59.0 6.3 %collective-permute-done.10 = bf16[512,256]{0,1:T(8,128)(2,1)S(1)} collective-permute-done((bf16[512,256]{0,1:T(8,128)(2,1)S(1)}, bf16[512,256]{0,1:T(8,128)(2,1)S(1)}, u32[]{:S(2)}, u32[]{:S(2)}) %collective-permute-start.10) | collective-permute-done | bytes 262176 | tf_op jit(solution)/shard_map/ppermute | solution.py:97
  66.3 0.6 convolution_convert_fusion.3
  66.9 0.6 convolution_convert_fusion.2
  67.7 1.0 bitcast_reduce_fusion
  68.7 0.8 fusion.8
  69.6 1.0 fusion.59
  71.4 0.6 convolution_convert_fusion
  72.1 0.6 convolution_convert_fusion.1
  77.3 0.7 collective-permute-start.14
  78.6 0.8 bitcast_add_fusion.1
  79.4 1.0 fusion.152
  80.4 0.9 collective-permute-start.20
  81.3 1.8 %collective-permute-done.14 = bf16[256,256]{0,1:T(8,128)(2,1)S(1)} collective-permute-done((bf16[256,256]{0,1:T(8,128)(2,1)S(1)}, bf16[256,256]{0,1:T(8,128)(2,1)S(1)}, u32[]{:S(2)}, u32[]{:S(2)}) %collective-permute-start.14) | collective-permute-done | bytes 131104 | tf_op jit(solution)/shard_map/ppermute | solution.py:72
  83.2 2.8 %collective-permute-done.20 = bf16[256,256]{0,1:T(8,128)(2,1)S(1)} collective-permute-done((bf16[256,256]{0,1:T(8,128)(2,1)S(1)}, bf16[256,256]{0,1:T(8,128)(2,1)S(1)}, u32[]{:S(2)}, u32[]{:S(2)}) %collective-permute-start.20) | collective-permute-done | bytes 131104 | tf_op jit(solution)/shard_map/ppermute | solution.py:72
  86.0 1.0 fusion.141
  87.1 0.9 collective-permute-start.21
  87.9 1.2 %collective-permute-start.15 = (bf16[256,256]{0,1:T(8,128)(2,1)S(1)}, bf16[256,256]{0,1:T(8,128)(2,1)S(1)}, u32[]{:S(2)}, u32[]{:S(2)}) collective-permute-start(bf16[256,256]{0,1:T(8,128)(2,1)S(1)} %get-tuple-element.240), channel_id=1, source_target_pairs={{0,2},{1,3},{2,0},{3,1},{4,6},{5,7},{6,4},{7,5},{8,10},{9,11},{10,... | collective-permute-start | bytes 393224 | tf_op jit(solution)/shard_map/ppermute | solution.py:86
  89.1 4.1 %collective-permute-done.21 = bf16[256,256]{0,1:T(8,128)(2,1)S(1)} collective-permute-done((bf16[256,256]{0,1:T(8,128)(2,1)S(1)}, bf16[256,256]{0,1:T(8,128)(2,1)S(1)}, u32[]{:S(2)}, u32[]{:S(2)}) %collective-permute-start.21) | collective-permute-done | bytes 131104 | tf_op jit(solution)/shard_map/ppermute | solution.py:86
  93.4 1.3 %collective-permute-done.15 = bf16[256,256]{0,1:T(8,128)(2,1)S(1)} collective-permute-done((bf16[256,256]{0,1:T(8,128)(2,1)S(1)}, bf16[256,256]{0,1:T(8,128)(2,1)S(1)}, u32[]{:S(2)}, u32[]{:S(2)}) %collective-permute-start.15) | collective-permute-done | bytes 131104 | tf_op jit(solution)/shard_map/ppermute | solution.py:86
  94.9 1.4 %collective-permute-done.16 = bf16[256,2,256]{0,2,1:T(8,128)(2,1)S(1)} collective-permute-done((bf16[256,2,256]{0,2,1:T(8,128)(2,1)S(1)}, bf16[256,2,256]{0,2,1:T(8,128)(2,1)S(1)}, u32[]{:S(2)}, u32[]{:S(2)}) %collective-permute-start.16) | collective-permute-done | bytes 262176 | tf_op jit(solution)/shard_map/ppermute | solution.py:86
  97.8 0.9 fusion.83
  98.7 0.6 copy-done.1
  99.4 1.0 fusion.186
  100.6 0.9 fusion.75
  101.5 1.0 fusion.184
  103.0 0.8 collective-permute-start.24
  104.2 1.1 collective-permute-start.18
  105.3 4.2 %collective-permute-done.24 = bf16[256,256]{0,1:T(8,128)(2,1)S(1)} collective-permute-done((bf16[256,256]{0,1:T(8,128)(2,1)S(1)}, bf16[256,256]{0,1:T(8,128)(2,1)S(1)}, u32[]{:S(2)}, u32[]{:S(2)}) %collective-permute-start.24) | collective-permute-done | bytes 131104 | tf_op jit(solution)/shard_map/ppermute | solution.py:72
  109.5 1.9 %collective-permute-done.18 = bf16[256,256]{0,1:T(8,128)(2,1)S(1)} collective-permute-done((bf16[256,256]{0,1:T(8,128)(2,1)S(1)}, bf16[256,256]{0,1:T(8,128)(2,1)S(1)}, u32[]{:S(2)}, u32[]{:S(2)}) %collective-permute-start.18) | collective-permute-done | bytes 131104 | tf_op jit(solution)/shard_map/ppermute | solution.py:72
  111.5 0.8 copy.53
  (133 shorter events, 15.0 us)
Async XLA Ops:
  0.0 97.8 %copy-start = (bf16[1024,1024]{1,0:T(8,128)(2,1)S(1)}, bf16[1024,1024]{1,0:T(8,128)(2,1)}, u32[]{:S(2)}) copy-start(bf16[1024,1024]{1,0:T(8,128)(2,1)} %param.46) | copy-start | bytes 6291460
  0.9 13.4 %collective-permute-start.1 = (bf16[64,256]{1,0:T(8,128)(2,1)S(1)}, bf16[64,256]{1,0:T(8,128)(2,1)S(1)}, u32[]{:S(2)}, u32[]{:S(2)}) collective-permute-start(bf16[64,256]{1,0:T(8,128)(2,1)S(1)} %get-tuple-element.245), channel_id=1, source_target_pairs={{4,0},{8,4},{12,8},{5,1},{9,5},{13,9},{6,2},{10,6},{14,10},{7,3},{... | collective-permute-start | bytes 98312 | tf_op jit(solution)/shard_map/ppermute | solution.py:21
  2.2 12.2 %collective-permute-start = (bf16[64,256]{1,0:T(8,128)(2,1)S(1)}, bf16[64,256]{1,0:T(8,128)(2,1)S(1)}, u32[]{:S(2)}, u32[]{:S(2)}) collective-permute-start(bf16[64,256]{1,0:T(8,128)(2,1)S(1)} %get-tuple-element.244), channel_id=1, source_target_pairs={{0,4},{4,8},{8,12},{1,5},{5,9},{9,13},{2,6},{6,10},{10,14},{3,7},{... | collective-permute-start | bytes 98312 | tf_op jit(solution)/shard_map/ppermute | solution.py:20
  16.3 11.7 %copy-start.2 = (bf16[1024]{0:T(1024)(128)(2,1)S(1)}, bf16[1024]{0:T(1024)(128)(2,1)}, u32[]{:S(2)}) copy-start(bf16[1024]{0:T(1024)(128)(2,1)} %param.40) | copy-start | bytes 6148
  16.3 11.7 %copy-start.4 = (s32[4,4]{1,0:T(4,128)S(1)}, s32[4,4]{1,0:T(4,128)}, u32[]{:S(2)}) copy-start(s32[4,4]{1,0:T(4,128)} %param.37) | copy-start | bytes 196
  16.7 7.8 %collective-permute-start.3 = (bf16[512,256]{0,1:T(8,128)(2,1)S(1)}, bf16[512,256]{0,1:T(8,128)(2,1)S(1)}, u32[]{:S(2)}, u32[]{:S(2)}) collective-permute-start(bf16[512,256]{0,1:T(8,128)(2,1)S(1)} %add_convert_fusion), channel_id=1, source_target_pairs={{0,2},{1,3},{2,0},{3,1},{4,6},{5,7},{6,4},{7,5},{8,10},{9,11},{10,... | collective-permute-start | bytes 786440 | tf_op jit(solution)/shard_map/ppermute | solution.py:97
  18.7 9.0 %collective-permute-start.2 = (bf16[512,256]{0,1:T(8,128)(2,1)S(1)}, bf16[512,256]{0,1:T(8,128)(2,1)S(1)}, u32[]{:S(2)}, u32[]{:S(2)}) collective-permute-start(bf16[512,256]{0,1:T(8,128)(2,1)S(1)} %add_convert_fusion), channel_id=1, source_target_pairs={{0,4},{4,8},{8,12},{12,0},{1,5},{5,9},{9,13},{13,1},{2,6},{6,10},{... | collective-permute-start | bytes 786440 | tf_op jit(solution)/shard_map/ppermute | solution.py:192
  27.7 6.5 %collective-permute-start.5 = (bf16[512,256]{0,1:T(8,128)(2,1)S(1)}, bf16[512,256]{0,1:T(8,128)(2,1)}, u32[]{:S(2)}, u32[]{:S(2)}) collective-permute-start(bf16[512,256]{0,1:T(8,128)(2,1)S(1)} %collective-permute-done.2), channel_id=1, source_target_pairs={{0,2},{1,3},{2,0},{3,1},{4,6},{5,7},{6,4},{7,5},{8,10},{9,11},{10,... | collective-permute-start | bytes 786440 | tf_op jit(solution)/shard_map/ppermute | solution.py:97
  28.1 7.2 %collective-permute-start.6 = (bf16[512,2,256]{0,2,1:T(8,128)(2,1)}, bf16[512,2,256]{0,2,1:T(8,128)(2,1)}, u32[]{:S(2)}, u32[]{:S(2)}) collective-permute-start(bf16[512,2,256]{0,2,1:T(8,128)(2,1)} %pad_maximum_fusion.6), channel_id=1, source_target_pairs={{0,1},{1,0},{2,3},{3,2},{4,5},{5,4},{6,7},{7,6},{8,9},{9,8},{10,11... | collective-permute-start | bytes 1572872 | tf_op jit(solution)/shard_map/ppermute | solution.py:97
  32.4 10.5 %collective-permute-start.4 = (bf16[512,256]{0,1:T(8,128)(2,1)S(1)}, bf16[512,256]{0,1:T(8,128)(2,1)S(1)}, u32[]{:S(2)}, u32[]{:S(2)}) collective-permute-start(bf16[512,256]{0,1:T(8,128)(2,1)S(1)} %collective-permute-done.2), channel_id=1, source_target_pairs={{0,4},{4,8},{8,12},{12,0},{1,5},{5,9},{9,13},{13,1},{2,6},{6,10},{... | collective-permute-start | bytes 786440 | tf_op jit(solution)/shard_map/ppermute | solution.py:192
  36.6 8.6 %copy-start.7 = (bf16[1024,256]{1,0:T(8,128)(2,1)S(1)}, bf16[1024,256]{1,0:T(8,128)(2,1)}, u32[]{:S(2)}) copy-start(bf16[1024,256]{1,0:T(8,128)(2,1)} %param.42) | copy-start | bytes 1572868
  43.0 9.7 %collective-permute-start.7 = (bf16[512,256]{0,1:T(8,128)(2,1)S(1)}, bf16[512,256]{0,1:T(8,128)(2,1)S(1)}, u32[]{:S(2)}, u32[]{:S(2)}) collective-permute-start(bf16[512,256]{0,1:T(8,128)(2,1)S(1)} %collective-permute-done.4), channel_id=1, source_target_pairs={{0,4},{4,8},{8,12},{12,0},{1,5},{5,9},{9,13},{13,1},{2,6},{6,10},{... | collective-permute-start | bytes 786440 | tf_op jit(solution)/shard_map/ppermute | solution.py:192
  43.0 7.9 %collective-permute-start.8 = (bf16[512,256]{0,1:T(8,128)(2,1)S(1)}, bf16[512,256]{0,1:T(8,128)(2,1)S(1)}, u32[]{:S(2)}, u32[]{:S(2)}) collective-permute-start(bf16[512,256]{0,1:T(8,128)(2,1)S(1)} %collective-permute-done.4), channel_id=1, source_target_pairs={{0,2},{1,3},{2,0},{3,1},{4,6},{5,7},{6,4},{7,5},{8,10},{9,11},{10,... | collective-permute-start | bytes 786440 | tf_op jit(solution)/shard_map/ppermute | solution.py:97
  44.8 1.0 copy-start.5
  45.9 1.0 copy-start.6
  50.2 2.0 %collective-permute-start.9 = (bf16[512,2,256]{0,2,1:T(8,128)(2,1)S(1)}, bf16[512,2,256]{0,2,1:T(8,128)(2,1)S(1)}, u32[]{:S(2)}, u32[]{:S(2)}) collective-permute-start(bf16[512,2,256]{0,2,1:T(8,128)(2,1)S(1)} %pad_maximum_fusion.7), channel_id=1, source_target_pairs={{0,1},{1,0},{2,3},{3,2},{4,5},{5,4},{6,7},{7,6},{8,9},{9,8},{10,11... | collective-permute-start | bytes 1572872 | tf_op jit(solution)/shard_map/ppermute | solution.py:97
  57.2 8.2 %collective-permute-start.10 = (bf16[512,256]{0,1:T(8,128)(2,1)S(1)}, bf16[512,256]{0,1:T(8,128)(2,1)S(1)}, u32[]{:S(2)}, u32[]{:S(2)}) collective-permute-start(bf16[512,256]{0,1:T(8,128)(2,1)S(1)} %collective-permute-done.7), channel_id=1, source_target_pairs={{0,2},{1,3},{2,0},{3,1},{4,6},{5,7},{6,4},{7,5},{8,10},{9,11},{10,... | collective-permute-start | bytes 786440 | tf_op jit(solution)/shard_map/ppermute | solution.py:97
  58.9 6.6 %collective-permute-start.11 = (bf16[512,2,256]{0,2,1:T(8,128)(2,1)S(1)}, bf16[512,2,256]{0,2,1:T(8,128)(2,1)S(1)}, u32[]{:S(2)}, u32[]{:S(2)}) collective-permute-start(bf16[512,2,256]{0,2,1:T(8,128)(2,1)S(1)} %pad_maximum_fusion.8), channel_id=1, source_target_pairs={{0,1},{1,0},{2,3},{3,2},{4,5},{5,4},{6,7},{7,6},{8,9},{9,8},{10,11... | collective-permute-start | bytes 1572872 | tf_op jit(solution)/shard_map/ppermute | solution.py:97
  67.6 3.0 %collective-permute-start.12 = (bf16[512,2,256]{0,2,1:T(8,128)(2,1)S(1)}, bf16[512,2,256]{0,2,1:T(8,128)(2,1)S(1)}, u32[]{:S(2)}, u32[]{:S(2)}) collective-permute-start(bf16[512,2,256]{0,2,1:T(8,128)(2,1)S(1)} %pad_maximum_fusion.9), channel_id=1, source_target_pairs={{0,1},{1,0},{2,3},{3,2},{4,5},{5,4},{6,7},{7,6},{8,9},{9,8},{10,11... | collective-permute-start | bytes 1572872 | tf_op jit(solution)/shard_map/ppermute | solution.py:97
  75.5 1.7 %collective-permute-start.13 = (bf16[256,2,256]{0,2,1:T(8,128)(2,1)S(1)}, bf16[256,2,256]{0,2,1:T(8,128)(2,1)S(1)}, u32[]{:S(2)}, u32[]{:S(2)}) collective-permute-start(bf16[256,2,256]{0,2,1:T(8,128)(2,1)S(1)} %fusion.130), channel_id=1, source_target_pairs={{0,1},{1,0},{2,3},{3,2},{4,5},{5,4},{6,7},{7,6},{8,9},{9,8},{10,11... | collective-permute-start | bytes 786440 | tf_op jit(solution)/shard_map/ppermute | solution.py:72
  77.0 1.6 %collective-permute-start.19 = (bf16[256,2,256]{0,2,1:T(8,128)(2,1)S(1)}, bf16[256,2,256]{0,2,1:T(8,128)(2,1)S(1)}, u32[]{:S(2)}, u32[]{:S(2)}) collective-permute-start(bf16[256,2,256]{0,2,1:T(8,128)(2,1)S(1)} %fusion.131), channel_id=1, source_target_pairs={{0,1},{1,0},{2,3},{3,2},{4,5},{5,4},{6,7},{7,6},{8,9},{9,8},{10,11... | collective-permute-start | bytes 786440 | tf_op jit(solution)/shard_map/ppermute | solution.py:72
  77.3 5.8 %collective-permute-start.14 = (bf16[256,256]{0,1:T(8,128)(2,1)S(1)}, bf16[256,256]{0,1:T(8,128)(2,1)S(1)}, u32[]{:S(2)}, u32[]{:S(2)}) collective-permute-start(bf16[256,256]{0,1:T(8,128)(2,1)S(1)} %fusion.150), channel_id=1, source_target_pairs={{0,2},{1,3},{2,0},{3,1},{4,6},{5,7},{6,4},{7,5},{8,10},{9,11},{10,... | collective-permute-start | bytes 393224 | tf_op jit(solution)/shard_map/ppermute | solution.py:72
  79.4 15.4 %copy-start.3 = (bf16[1024]{0:T(1024)(128)(2,1)S(1)}, bf16[1024]{0:T(1024)(128)(2,1)}, u32[]{:S(2)}) copy-start(bf16[1024]{0:T(1024)(128)(2,1)} %param.45) | copy-start | bytes 6148
  80.4 5.6 %collective-permute-start.20 = (bf16[256,256]{0,1:T(8,128)(2,1)S(1)}, bf16[256,256]{0,1:T(8,128)(2,1)S(1)}, u32[]{:S(2)}, u32[]{:S(2)}) collective-permute-start(bf16[256,256]{0,1:T(8,128)(2,1)S(1)} %fusion.152), channel_id=1, source_target_pairs={{0,2},{1,3},{2,0},{3,1},{4,6},{5,7},{6,4},{7,5},{8,10},{9,11},{10,... | collective-permute-start | bytes 393224 | tf_op jit(solution)/shard_map/ppermute | solution.py:72
  87.1 6.2 %collective-permute-start.21 = (bf16[256,256]{0,1:T(8,128)(2,1)S(1)}, bf16[256,256]{0,1:T(8,128)(2,1)S(1)}, u32[]{:S(2)}, u32[]{:S(2)}) collective-permute-start(bf16[256,256]{0,1:T(8,128)(2,1)S(1)} %get-tuple-element.241), channel_id=1, source_target_pairs={{0,2},{1,3},{2,0},{3,1},{4,6},{5,7},{6,4},{7,5},{8,10},{9,11},{10,... | collective-permute-start | bytes 393224 | tf_op jit(solution)/shard_map/ppermute | solution.py:86
  87.9 6.7 %collective-permute-start.15 = (bf16[256,256]{0,1:T(8,128)(2,1)S(1)}, bf16[256,256]{0,1:T(8,128)(2,1)S(1)}, u32[]{:S(2)}, u32[]{:S(2)}) collective-permute-start(bf16[256,256]{0,1:T(8,128)(2,1)S(1)} %get-tuple-element.240), channel_id=1, source_target_pairs={{0,2},{1,3},{2,0},{3,1},{4,6},{5,7},{6,4},{7,5},{8,10},{9,11},{10,... | collective-permute-start | bytes 393224 | tf_op jit(solution)/shard_map/ppermute | solution.py:86
  93.3 1.6 %collective-permute-start.22 = (bf16[256,2,256]{0,2,1:T(8,128)(2,1)S(1)}, bf16[256,2,256]{0,2,1:T(8,128)(2,1)S(1)}, u32[]{:S(2)}, u32[]{:S(2)}) collective-permute-start(bf16[256,2,256]{0,2,1:T(8,128)(2,1)S(1)} %pad_maximum_fusion.11), channel_id=1, source_target_pairs={{0,1},{1,0},{2,3},{3,2},{4,5},{5,4},{6,7},{7,6},{8,9},{9,8},{10,11... | collective-permute-start | bytes 786440 | tf_op jit(solution)/shard_map/ppermute | solution.py:86
  94.7 1.6 %collective-permute-start.16 = (bf16[256,2,256]{0,2,1:T(8,128)(2,1)S(1)}, bf16[256,2,256]{0,2,1:T(8,128)(2,1)S(1)}, u32[]{:S(2)}, u32[]{:S(2)}) collective-permute-start(bf16[256,2,256]{0,2,1:T(8,128)(2,1)S(1)} %pad_maximum_fusion.10), channel_id=1, source_target_pairs={{0,1},{1,0},{2,3},{3,2},{4,5},{5,4},{6,7},{7,6},{8,9},{9,8},{10,11... | collective-permute-start | bytes 786440 | tf_op jit(solution)/shard_map/ppermute | solution.py:86
  97.8 1.6 %copy-start.1 = (bf16[1024,1024]{1,0:T(8,128)(2,1)S(1)}, bf16[1024,1024]{1,0:T(8,128)(2,1)}, u32[]{:S(2)}) copy-start(bf16[1024,1024]{1,0:T(8,128)(2,1)} %param.47) | copy-start | bytes 6291460
  100.4 2.6 %collective-permute-start.23 = (bf16[256,2,256]{0,2,1:T(8,128)(2,1)S(1)}, bf16[256,2,256]{0,2,1:T(8,128)(2,1)S(1)}, u32[]{:S(2)}, u32[]{:S(2)}) collective-permute-start(bf16[256,2,256]{0,2,1:T(8,128)(2,1)S(1)} %fusion.133), channel_id=1, source_target_pairs={{0,1},{1,0},{2,3},{3,2},{4,5},{5,4},{6,7},{7,6},{8,9},{9,8},{10,11... | collective-permute-start | bytes 786440 | tf_op jit(solution)/shard_map/ppermute | solution.py:72
  102.5 1.6 %collective-permute-start.17 = (bf16[256,2,256]{0,2,1:T(8,128)(2,1)S(1)}, bf16[256,2,256]{0,2,1:T(8,128)(2,1)S(1)}, u32[]{:S(2)}, u32[]{:S(2)}) collective-permute-start(bf16[256,2,256]{0,2,1:T(8,128)(2,1)S(1)} %fusion.132), channel_id=1, source_target_pairs={{0,1},{1,0},{2,3},{3,2},{4,5},{5,4},{6,7},{7,6},{8,9},{9,8},{10,11... | collective-permute-start | bytes 786440 | tf_op jit(solution)/shard_map/ppermute | solution.py:72
  103.0 6.4 %collective-permute-start.24 = (bf16[256,256]{0,1:T(8,128)(2,1)S(1)}, bf16[256,256]{0,1:T(8,128)(2,1)S(1)}, u32[]{:S(2)}, u32[]{:S(2)}) collective-permute-start(bf16[256,256]{0,1:T(8,128)(2,1)S(1)} %fusion.153), channel_id=1, source_target_pairs={{0,2},{1,3},{2,0},{3,1},{4,6},{5,7},{6,4},{7,5},{8,10},{9,11},{10,... | collective-permute-start | bytes 393224 | tf_op jit(solution)/shard_map/ppermute | solution.py:72
  104.2 7.2 %collective-permute-start.18 = (bf16[256,256]{0,1:T(8,128)(2,1)S(1)}, bf16[256,256]{0,1:T(8,128)(2,1)S(1)}, u32[]{:S(2)}, u32[]{:S(2)}) collective-permute-start(bf16[256,256]{0,1:T(8,128)(2,1)S(1)} %fusion.151), channel_id=1, source_target_pairs={{0,2},{1,3},{2,0},{3,1},{4,6},{5,7},{6,4},{7,5},{8,10},{9,11},{10,... | collective-permute-start | bytes 393224 | tf_op jit(solution)/shard_map/ppermute | solution.py:72

commit v20 on v17

--- a/solution.py
+++ b/solution.py
@@ -257,8 +257,10 @@
         hidden = lax.optimization_barrier(hidden)
         lowered = jnp.dot(hidden, down_weight, preferred_element_type=jnp.float32)
         mixed = scatter_heads(lowered, head_id, head_total)
-        outputs.append((stream_two.astype(jnp.float32) + mixed).astype(jnp.bfloat16))
-    return jnp.concatenate(outputs, axis=0)
+        outputs.append((stream_two, mixed))
+    two_rows = jnp.concatenate([two for two, _ in outputs], axis=0)
+    mixed_rows = jnp.concatenate([mix for _, mix in outputs], axis=0)
+    return (two_rows.astype(jnp.float32) + mixed_rows).astype(jnp.bfloat16)
 
 def solution(mesh):
     return jax.shard_map(

time: 113 us -> 113 us (level)
  no operation moved by 1% of the time
where the time goes in v20:
time: 113 us; the launch traced here: 112 us
  waiting for transfers between devices  40.8 us (36%)
  starting transfers between devices  21.9 us (19%)
  matrix products  17.8 us (16%)
  other arithmetic  16.1 us (14%)
  local copies, waits for them, and re-layouts  11.2 us (10%)
  between operations  4.59 us (4%)
    ppermute x8, waiting for transfers between devices, gather_levels(): lax.ppermute(current, 'heads', [(i, i ^ bit) for i in range(head_total)])  13.3 us
    ppermute x8, waiting for transfers between devices, scatter_heads(): lax.ppermute(give.astype(jnp.bfloat16), 'heads', [(i, i ^ bit) for i in r...  11.8 us
    ppermute x3, waiting for transfers between devices, shards(): ringed[slot + 1] = lax.ppermute(ringed[slot], 'bricks', ring)  8.81 us
    ppermute x4, waiting for transfers between devices, gather_heads(): lax.ppermute(current, 'heads', [(i, i ^ bit) for i in range(head_total)])  6.85 us
    ppermute x8, starting transfers between devices, gather_levels(): lax.ppermute(current, 'heads', [(i, i ^ bit) for i in range(head_total)])  5.88 us
    ppermute x1, starting transfers between devices, extended_2(): before = lax.ppermute(last, axis, up)  5.56 us
    ppermute x8, starting transfers between devices, scatter_heads(): lax.ppermute(give.astype(jnp.bfloat16), 'heads', [(i, i ^ bit) for i in r...  4.76 us
    dot_general x5, matrix products, absorb_block(): jnp.einsum('bhqk,khd->bqhd', weights.astype(jnp.bfloat16), value_rows, pr...  4.05 us
  transfers between devices with their start and end apart: 25, of which 19 were waited for; matrix products, arithmetic and copies ran while one was open for 21% of the time, Pallas kernels for 0%

profile of v20, /device:TPU:0, one launch (start us, length us, event | category | flops | bytes accessed | tf_op | source)
XLA Modules:
  0.0 112.4 jit_solution(3328037113649274101)
XLA Ops:
  0.0 0.9 fusion.175
  0.9 1.3 %collective-permute-start.1 = (bf16[64,256]{1,0:T(8,128)(2,1)S(1)}, bf16[64,256]{1,0:T(8,128)(2,1)S(1)}, u32[]{:S(2)}, u32[]{:S(2)}) collective-permute-start(bf16[64,256]{1,0:T(8,128)(2,1)S(1)} %get-tuple-element.245), channel_id=1, source_target_pairs={{4,0},{8,4},{12,8},{5,1},{9,5},{13,9},{6,2},{10,6},{14,10},{7,3},{... | collective-permute-start | bytes 98312 | tf_op jit(solution)/shard_map/ppermute | solution.py:21
  2.2 5.6 %collective-permute-start = (bf16[64,256]{1,0:T(8,128)(2,1)S(1)}, bf16[64,256]{1,0:T(8,128)(2,1)S(1)}, u32[]{:S(2)}, u32[]{:S(2)}) collective-permute-start(bf16[64,256]{1,0:T(8,128)(2,1)S(1)} %get-tuple-element.244), channel_id=1, source_target_pairs={{0,4},{4,8},{8,12},{1,5},{5,9},{9,13},{2,6},{6,10},{10,14},{3,7},{... | collective-permute-start | bytes 98312 | tf_op jit(solution)/shard_map/ppermute | solution.py:20
  7.8 1.0 fusion.176
  8.8 0.9 fusion.177
  9.7 1.1 copy.30
  10.8 1.4 %fusion.179 = (s32[1]{0:T(128)}, s32[1]{0:T(128)}) fusion(s32[4]{0:T(128)} %param.36, s32[]{:T(128)} %bitcast.2, s32[]{:T(128)} %bitcast.6), kind=kLoop, calls=%fused_computation.316 | loop fusion | bytes 24 | tf_op jit(solution)/shard_map/jit(_take)/gather | solution.py:157
  13.7 0.7 convert_element_type.237
  14.7 1.7 %fusion.102 = f32[1,8,8,8,256]{4,3,2,1,0:T(8,128)S(1)} fusion(f32[1,10,10,10,256]{4,3,2,1,0:T(8,128)S(1)} %select_maximum_fusion, f32[1,1,8,8,256]{4,3,2,1,0:T(8,128)S(1)} %multiply_bitcast_fusion, f32[1,8,8,8,256]{4,3,2,1,0:T(8,128)S(1)} %bitcast.534, f32[1,1,8,8,256]{4,3,2,1,0:T(8,128)S(1)} %multiply_bitcast_fusion.1, f32[256]{0:T(256)S(1)} %bitcast.585, ...), kind=kLoop, calls=%fused_computation.140 | loop fusion | flops 7208960 | bytes 13790208 | tf_op jit(solution)/shard_map/add | solution.py:51
  16.7 2.0 %collective-permute-start.3 = (bf16[512,256]{0,1:T(8,128)(2,1)S(1)}, bf16[512,256]{0,1:T(8,128)(2,1)S(1)}, u32[]{:S(2)}, u32[]{:S(2)}) collective-permute-start(bf16[512,256]{0,1:T(8,128)(2,1)S(1)} %add_convert_fusion), channel_id=1, source_target_pairs={{0,2},{1,3},{2,0},{3,1},{4,6},{5,7},{6,4},{7,5},{8,10},{9,11},{10,... | collective-permute-start | bytes 786440 | tf_op jit(solution)/shard_map/ppermute | solution.py:97
  18.7 1.6 %collective-permute-start.2 = (bf16[512,256]{0,1:T(8,128)(2,1)S(1)}, bf16[512,256]{0,1:T(8,128)(2,1)S(1)}, u32[]{:S(2)}, u32[]{:S(2)}) collective-permute-start(bf16[512,256]{0,1:T(8,128)(2,1)S(1)} %add_convert_fusion), channel_id=1, source_target_pairs={{0,4},{4,8},{8,12},{12,0},{1,5},{5,9},{9,13},{13,1},{2,6},{6,10},{... | collective-permute-start | bytes 786440 | tf_op jit(solution)/shard_map/ppermute | solution.py:192
  20.3 4.3 %collective-permute-done.3 = bf16[512,256]{0,1:T(8,128)(2,1)S(1)} collective-permute-done((bf16[512,256]{0,1:T(8,128)(2,1)S(1)}, bf16[512,256]{0,1:T(8,128)(2,1)S(1)}, u32[]{:S(2)}, u32[]{:S(2)}) %collective-permute-start.3) | collective-permute-done | bytes 262176 | tf_op jit(solution)/shard_map/ppermute | solution.py:97
  24.6 0.8 pad_maximum_fusion.6
  25.4 2.3 %collective-permute-done.2 = bf16[512,256]{0,1:T(8,128)(2,1)S(1)} collective-permute-done((bf16[512,256]{0,1:T(8,128)(2,1)S(1)}, bf16[512,256]{0,1:T(8,128)(2,1)S(1)}, u32[]{:S(2)}, u32[]{:S(2)}) %collective-permute-start.2) | collective-permute-done | bytes 262176 | tf_op jit(solution)/shard_map/ppermute | solution.py:192
  28.1 0.6 fusion.178
  31.2 1.2 %copy.65 = bf16[1024,256]{1,0:T(8,128)(2,1)S(1)} copy(bf16[1024,256]{0,1:T(8,128)(2,1)} %bitcast.547) | data formatting | bytes 1048576 | tf_op jit(solution)/shard_map/dot_general | solution.py:249
  33.0 1.1 %collective-permute-done.5 = bf16[512,256]{0,1:T(8,128)(2,1)} collective-permute-done((bf16[512,256]{0,1:T(8,128)(2,1)S(1)}, bf16[512,256]{0,1:T(8,128)(2,1)}, u32[]{:S(2)}, u32[]{:S(2)}) %collective-permute-start.5) | collective-permute-done | bytes 262176 | tf_op jit(solution)/shard_map/ppermute | solution.py:97
  34.2 1.0 select_bitcast_fusion.17
  35.2 1.3 %select_bitcast_fusion.7 = (bf16[512,2,1,256]{0,3,1,2:T(8,128)(2,1)S(1)}, bf16[512,2,1,256]{0,3,1,2:T(8,128)(2,1)S(1)}) fusion(bf16[512,2,256]{0,2,1:T(8,128)(2,1)} %pad_maximum_fusion.6, bf16[512,2,256]{0,2,1:T(8,128)(2,1)} %collective-permute-done.6, pred[]{:T(512)S(6)} %eq.9), kind=kLoop, calls=%fused_computation.218 | loop fusion | flops 524288 | bytes 2097153 | tf_op jit(solution)/shard_map/stack | solution.py:100
  36.7 6.3 %collective-permute-done.4 = bf16[512,256]{0,1:T(8,128)(2,1)S(1)} collective-permute-done((bf16[512,256]{0,1:T(8,128)(2,1)S(1)}, bf16[512,256]{0,1:T(8,128)(2,1)S(1)}, u32[]{:S(2)}, u32[]{:S(2)}) %collective-permute-start.4) | collective-permute-done | bytes 262176 | tf_op jit(solution)/shard_map/ppermute | solution.py:192
  43.0 1.6 %collective-permute-start.8 = (bf16[512,256]{0,1:T(8,128)(2,1)S(1)}, bf16[512,256]{0,1:T(8,128)(2,1)S(1)}, u32[]{:S(2)}, u32[]{:S(2)}) collective-permute-start(bf16[512,256]{0,1:T(8,128)(2,1)S(1)} %collective-permute-done.4), channel_id=1, source_target_pairs={{0,2},{1,3},{2,0},{3,1},{4,6},{5,7},{6,4},{7,5},{8,10},{9,11},{10,... | collective-permute-start | bytes 786440 | tf_op jit(solution)/shard_map/ppermute | solution.py:97
  45.2 0.6 convolution_convert_fusion.8
  45.9 0.6 convolution_convert_fusion.7
  46.9 0.6 convolution_convert_fusion.6
  47.6 0.8 bitcast_reduce_fusion.2
  48.4 0.8 fusion.4
  49.2 1.0 fusion.56
  51.0 1.2 %collective-permute-done.9 = bf16[512,2,256]{0,2,1:T(8,128)(2,1)S(1)} collective-permute-done((bf16[512,2,256]{0,2,1:T(8,128)(2,1)S(1)}, bf16[512,2,256]{0,2,1:T(8,128)(2,1)S(1)}, u32[]{:S(2)}, u32[]{:S(2)}) %collective-permute-start.9) | collective-permute-done | bytes 524320 | tf_op jit(solution)/shard_map/ppermute | solution.py:97
  53.3 0.6 convolution_convert_fusion.5
  53.9 0.6 convolution_convert_fusion.4
  54.6 0.8 bitcast_reduce_fusion.1
  55.4 0.8 fusion.6
  56.2 1.0 fusion.53
  57.2 1.7 %collective-permute-start.10 = (bf16[512,256]{0,1:T(8,128)(2,1)S(1)}, bf16[512,256]{0,1:T(8,128)(2,1)S(1)}, u32[]{:S(2)}, u32[]{:S(2)}) collective-permute-start(bf16[512,256]{0,1:T(8,128)(2,1)S(1)} %collective-permute-done.7), channel_id=1, source_target_pairs={{0,2},{1,3},{2,0},{3,1},{4,6},{5,7},{6,4},{7,5},{8,10},{9,11},{10,... | collective-permute-start | bytes 786440 | tf_op jit(solution)/shard_map/ppermute | solution.py:97
  59.0 6.3 %collective-permute-done.10 = bf16[512,256]{0,1:T(8,128)(2,1)S(1)} collective-permute-done((bf16[512,256]{0,1:T(8,128)(2,1)S(1)}, bf16[512,256]{0,1:T(8,128)(2,1)S(1)}, u32[]{:S(2)}, u32[]{:S(2)}) %collective-permute-start.10) | collective-permute-done | bytes 262176 | tf_op jit(solution)/shard_map/ppermute | solution.py:97
  66.3 0.6 convolution_convert_fusion.3
  66.9 0.6 convolution_convert_fusion.2
  67.7 1.0 bitcast_reduce_fusion
  68.7 0.8 fusion.8
  69.6 1.0 fusion.59
  71.4 0.6 convolution_convert_fusion
  72.1 0.6 convolution_convert_fusion.1
  77.3 0.7 collective-permute-start.14
  78.6 0.8 bitcast_add_fusion.2
  79.4 1.0 fusion.148
  80.4 0.9 collective-permute-start.16
  81.3 1.8 %collective-permute-done.14 = bf16[256,256]{0,1:T(8,128)(2,1)S(1)} collective-permute-done((bf16[256,256]{0,1:T(8,128)(2,1)S(1)}, bf16[256,256]{0,1:T(8,128)(2,1)S(1)}, u32[]{:S(2)}, u32[]{:S(2)}) %collective-permute-start.14) | collective-permute-done | bytes 131104 | tf_op jit(solution)/shard_map/ppermute | solution.py:72
  83.2 2.8 %collective-permute-done.16 = bf16[256,256]{0,1:T(8,128)(2,1)S(1)} collective-permute-done((bf16[256,256]{0,1:T(8,128)(2,1)S(1)}, bf16[256,256]{0,1:T(8,128)(2,1)S(1)}, u32[]{:S(2)}, u32[]{:S(2)}) %collective-permute-start.16) | collective-permute-done | bytes 131104 | tf_op jit(solution)/shard_map/ppermute | solution.py:72
  86.0 1.0 fusion.138
  87.1 0.9 collective-permute-start.21
  87.9 1.2 %collective-permute-start.17 = (bf16[256,256]{0,1:T(8,128)(2,1)S(1)}, bf16[256,256]{0,1:T(8,128)(2,1)S(1)}, u32[]{:S(2)}, u32[]{:S(2)}) collective-permute-start(bf16[256,256]{0,1:T(8,128)(2,1)S(1)} %get-tuple-element.240), channel_id=1, source_target_pairs={{0,2},{1,3},{2,0},{3,1},{4,6},{5,7},{6,4},{7,5},{8,10},{9,11},{10,... | collective-permute-start | bytes 393224 | tf_op jit(solution)/shard_map/ppermute | solution.py:86
  89.1 4.1 %collective-permute-done.21 = bf16[256,256]{0,1:T(8,128)(2,1)S(1)} collective-permute-done((bf16[256,256]{0,1:T(8,128)(2,1)S(1)}, bf16[256,256]{0,1:T(8,128)(2,1)S(1)}, u32[]{:S(2)}, u32[]{:S(2)}) %collective-permute-start.21) | collective-permute-done | bytes 131104 | tf_op jit(solution)/shard_map/ppermute | solution.py:86
  93.4 1.3 %collective-permute-done.17 = bf16[256,256]{0,1:T(8,128)(2,1)S(1)} collective-permute-done((bf16[256,256]{0,1:T(8,128)(2,1)S(1)}, bf16[256,256]{0,1:T(8,128)(2,1)S(1)}, u32[]{:S(2)}, u32[]{:S(2)}) %collective-permute-start.17) | collective-permute-done | bytes 131104 | tf_op jit(solution)/shard_map/ppermute | solution.py:86
  94.9 1.4 %collective-permute-done.18 = bf16[256,2,256]{0,2,1:T(8,128)(2,1)S(1)} collective-permute-done((bf16[256,2,256]{0,2,1:T(8,128)(2,1)S(1)}, bf16[256,2,256]{0,2,1:T(8,128)(2,1)S(1)}, u32[]{:S(2)}, u32[]{:S(2)}) %collective-permute-start.18) | collective-permute-done | bytes 262176 | tf_op jit(solution)/shard_map/ppermute | solution.py:86
  97.8 0.9 fusion.83
  98.7 0.7 copy-done.1
  99.4 1.0 fusion.183
  100.6 0.9 fusion.75
  101.5 1.0 fusion.182
  103.0 0.8 collective-permute-start.24
  104.2 1.1 collective-permute-start.20
  105.3 4.2 %collective-permute-done.24 = bf16[256,256]{0,1:T(8,128)(2,1)S(1)} collective-permute-done((bf16[256,256]{0,1:T(8,128)(2,1)S(1)}, bf16[256,256]{0,1:T(8,128)(2,1)S(1)}, u32[]{:S(2)}, u32[]{:S(2)}) %collective-permute-start.24) | collective-permute-done | bytes 131104 | tf_op jit(solution)/shard_map/ppermute | solution.py:72
  109.5 2.0 %collective-permute-done.20 = bf16[256,256]{0,1:T(8,128)(2,1)S(1)} collective-permute-done((bf16[256,256]{0,1:T(8,128)(2,1)S(1)}, bf16[256,256]{0,1:T(8,128)(2,1)S(1)}, u32[]{:S(2)}, u32[]{:S(2)}) %collective-permute-start.20) | collective-permute-done | bytes 131104 | tf_op jit(solution)/shard_map/ppermute | solution.py:72
  111.5 0.8 copy.53
  (133 shorter events, 14.9 us)
Async XLA Ops:
  0.0 97.8 %copy-start = (bf16[1024,1024]{1,0:T(8,128)(2,1)S(1)}, bf16[1024,1024]{1,0:T(8,128)(2,1)}, u32[]{:S(2)}) copy-start(bf16[1024,1024]{1,0:T(8,128)(2,1)} %param.46) | copy-start | bytes 6291460
  0.9 13.4 %collective-permute-start.1 = (bf16[64,256]{1,0:T(8,128)(2,1)S(1)}, bf16[64,256]{1,0:T(8,128)(2,1)S(1)}, u32[]{:S(2)}, u32[]{:S(2)}) collective-permute-start(bf16[64,256]{1,0:T(8,128)(2,1)S(1)} %get-tuple-element.245), channel_id=1, source_target_pairs={{4,0},{8,4},{12,8},{5,1},{9,5},{13,9},{6,2},{10,6},{14,10},{7,3},{... | collective-permute-start | bytes 98312 | tf_op jit(solution)/shard_map/ppermute | solution.py:21
  2.2 12.2 %collective-permute-start = (bf16[64,256]{1,0:T(8,128)(2,1)S(1)}, bf16[64,256]{1,0:T(8,128)(2,1)S(1)}, u32[]{:S(2)}, u32[]{:S(2)}) collective-permute-start(bf16[64,256]{1,0:T(8,128)(2,1)S(1)} %get-tuple-element.244), channel_id=1, source_target_pairs={{0,4},{4,8},{8,12},{1,5},{5,9},{9,13},{2,6},{6,10},{10,14},{3,7},{... | collective-permute-start | bytes 98312 | tf_op jit(solution)/shard_map/ppermute | solution.py:20
  16.3 11.7 %copy-start.2 = (bf16[1024]{0:T(1024)(128)(2,1)S(1)}, bf16[1024]{0:T(1024)(128)(2,1)}, u32[]{:S(2)}) copy-start(bf16[1024]{0:T(1024)(128)(2,1)} %param.40) | copy-start | bytes 6148
  16.3 11.7 %copy-start.4 = (s32[4,4]{1,0:T(4,128)S(1)}, s32[4,4]{1,0:T(4,128)}, u32[]{:S(2)}) copy-start(s32[4,4]{1,0:T(4,128)} %param.37) | copy-start | bytes 196
  16.7 7.8 %collective-permute-start.3 = (bf16[512,256]{0,1:T(8,128)(2,1)S(1)}, bf16[512,256]{0,1:T(8,128)(2,1)S(1)}, u32[]{:S(2)}, u32[]{:S(2)}) collective-permute-start(bf16[512,256]{0,1:T(8,128)(2,1)S(1)} %add_convert_fusion), channel_id=1, source_target_pairs={{0,2},{1,3},{2,0},{3,1},{4,6},{5,7},{6,4},{7,5},{8,10},{9,11},{10,... | collective-permute-start | bytes 786440 | tf_op jit(solution)/shard_map/ppermute | solution.py:97
  18.7 9.0 %collective-permute-start.2 = (bf16[512,256]{0,1:T(8,128)(2,1)S(1)}, bf16[512,256]{0,1:T(8,128)(2,1)S(1)}, u32[]{:S(2)}, u32[]{:S(2)}) collective-permute-start(bf16[512,256]{0,1:T(8,128)(2,1)S(1)} %add_convert_fusion), channel_id=1, source_target_pairs={{0,4},{4,8},{8,12},{12,0},{1,5},{5,9},{9,13},{13,1},{2,6},{6,10},{... | collective-permute-start | bytes 786440 | tf_op jit(solution)/shard_map/ppermute | solution.py:192
  27.7 6.5 %collective-permute-start.5 = (bf16[512,256]{0,1:T(8,128)(2,1)S(1)}, bf16[512,256]{0,1:T(8,128)(2,1)}, u32[]{:S(2)}, u32[]{:S(2)}) collective-permute-start(bf16[512,256]{0,1:T(8,128)(2,1)S(1)} %collective-permute-done.2), channel_id=1, source_target_pairs={{0,2},{1,3},{2,0},{3,1},{4,6},{5,7},{6,4},{7,5},{8,10},{9,11},{10,... | collective-permute-start | bytes 786440 | tf_op jit(solution)/shard_map/ppermute | solution.py:97
  28.1 7.2 %collective-permute-start.6 = (bf16[512,2,256]{0,2,1:T(8,128)(2,1)}, bf16[512,2,256]{0,2,1:T(8,128)(2,1)}, u32[]{:S(2)}, u32[]{:S(2)}) collective-permute-start(bf16[512,2,256]{0,2,1:T(8,128)(2,1)} %pad_maximum_fusion.6), channel_id=1, source_target_pairs={{0,1},{1,0},{2,3},{3,2},{4,5},{5,4},{6,7},{7,6},{8,9},{9,8},{10,11... | collective-permute-start | bytes 1572872 | tf_op jit(solution)/shard_map/ppermute | solution.py:97
  32.4 10.5 %collective-permute-start.4 = (bf16[512,256]{0,1:T(8,128)(2,1)S(1)}, bf16[512,256]{0,1:T(8,128)(2,1)S(1)}, u32[]{:S(2)}, u32[]{:S(2)}) collective-permute-start(bf16[512,256]{0,1:T(8,128)(2,1)S(1)} %collective-permute-done.2), channel_id=1, source_target_pairs={{0,4},{4,8},{8,12},{12,0},{1,5},{5,9},{9,13},{13,1},{2,6},{6,10},{... | collective-permute-start | bytes 786440 | tf_op jit(solution)/shard_map/ppermute | solution.py:192
  36.6 8.6 %copy-start.7 = (bf16[1024,256]{1,0:T(8,128)(2,1)S(1)}, bf16[1024,256]{1,0:T(8,128)(2,1)}, u32[]{:S(2)}) copy-start(bf16[1024,256]{1,0:T(8,128)(2,1)} %param.42) | copy-start | bytes 1572868
  43.0 9.7 %collective-permute-start.7 = (bf16[512,256]{0,1:T(8,128)(2,1)S(1)}, bf16[512,256]{0,1:T(8,128)(2,1)S(1)}, u32[]{:S(2)}, u32[]{:S(2)}) collective-permute-start(bf16[512,256]{0,1:T(8,128)(2,1)S(1)} %collective-permute-done.4), channel_id=1, source_target_pairs={{0,4},{4,8},{8,12},{12,0},{1,5},{5,9},{9,13},{13,1},{2,6},{6,10},{... | collective-permute-start | bytes 786440 | tf_op jit(solution)/shard_map/ppermute | solution.py:192
  43.0 7.9 %collective-permute-start.8 = (bf16[512,256]{0,1:T(8,128)(2,1)S(1)}, bf16[512,256]{0,1:T(8,128)(2,1)S(1)}, u32[]{:S(2)}, u32[]{:S(2)}) collective-permute-start(bf16[512,256]{0,1:T(8,128)(2,1)S(1)} %collective-permute-done.4), channel_id=1, source_target_pairs={{0,2},{1,3},{2,0},{3,1},{4,6},{5,7},{6,4},{7,5},{8,10},{9,11},{10,... | collective-permute-start | bytes 786440 | tf_op jit(solution)/shard_map/ppermute | solution.py:97
  44.8 1.0 copy-start.5
  45.9 1.0 copy-start.6
  50.2 2.0 %collective-permute-start.9 = (bf16[512,2,256]{0,2,1:T(8,128)(2,1)S(1)}, bf16[512,2,256]{0,2,1:T(8,128)(2,1)S(1)}, u32[]{:S(2)}, u32[]{:S(2)}) collective-permute-start(bf16[512,2,256]{0,2,1:T(8,128)(2,1)S(1)} %pad_maximum_fusion.7), channel_id=1, source_target_pairs={{0,1},{1,0},{2,3},{3,2},{4,5},{5,4},{6,7},{7,6},{8,9},{9,8},{10,11... | collective-permute-start | bytes 1572872 | tf_op jit(solution)/shard_map/ppermute | solution.py:97
  57.2 8.2 %collective-permute-start.10 = (bf16[512,256]{0,1:T(8,128)(2,1)S(1)}, bf16[512,256]{0,1:T(8,128)(2,1)S(1)}, u32[]{:S(2)}, u32[]{:S(2)}) collective-permute-start(bf16[512,256]{0,1:T(8,128)(2,1)S(1)} %collective-permute-done.7), channel_id=1, source_target_pairs={{0,2},{1,3},{2,0},{3,1},{4,6},{5,7},{6,4},{7,5},{8,10},{9,11},{10,... | collective-permute-start | bytes 786440 | tf_op jit(solution)/shard_map/ppermute | solution.py:97
  58.9 6.6 %collective-permute-start.11 = (bf16[512,2,256]{0,2,1:T(8,128)(2,1)S(1)}, bf16[512,2,256]{0,2,1:T(8,128)(2,1)S(1)}, u32[]{:S(2)}, u32[]{:S(2)}) collective-permute-start(bf16[512,2,256]{0,2,1:T(8,128)(2,1)S(1)} %pad_maximum_fusion.8), channel_id=1, source_target_pairs={{0,1},{1,0},{2,3},{3,2},{4,5},{5,4},{6,7},{7,6},{8,9},{9,8},{10,11... | collective-permute-start | bytes 1572872 | tf_op jit(solution)/shard_map/ppermute | solution.py:97
  67.6 3.0 %collective-permute-start.12 = (bf16[512,2,256]{0,2,1:T(8,128)(2,1)S(1)}, bf16[512,2,256]{0,2,1:T(8,128)(2,1)S(1)}, u32[]{:S(2)}, u32[]{:S(2)}) collective-permute-start(bf16[512,2,256]{0,2,1:T(8,128)(2,1)S(1)} %pad_maximum_fusion.9), channel_id=1, source_target_pairs={{0,1},{1,0},{2,3},{3,2},{4,5},{5,4},{6,7},{7,6},{8,9},{9,8},{10,11... | collective-permute-start | bytes 1572872 | tf_op jit(solution)/shard_map/ppermute | solution.py:97
  75.5 1.7 %collective-permute-start.13 = (bf16[256,2,256]{0,2,1:T(8,128)(2,1)S(1)}, bf16[256,2,256]{0,2,1:T(8,128)(2,1)S(1)}, u32[]{:S(2)}, u32[]{:S(2)}) collective-permute-start(bf16[256,2,256]{0,2,1:T(8,128)(2,1)S(1)} %fusion.131), channel_id=1, source_target_pairs={{0,1},{1,0},{2,3},{3,2},{4,5},{5,4},{6,7},{7,6},{8,9},{9,8},{10,11... | collective-permute-start | bytes 786440 | tf_op jit(solution)/shard_map/ppermute | solution.py:72
  77.0 1.6 %collective-permute-start.15 = (bf16[256,2,256]{0,2,1:T(8,128)(2,1)S(1)}, bf16[256,2,256]{0,2,1:T(8,128)(2,1)S(1)}, u32[]{:S(2)}, u32[]{:S(2)}) collective-permute-start(bf16[256,2,256]{0,2,1:T(8,128)(2,1)S(1)} %fusion.132), channel_id=1, source_target_pairs={{0,1},{1,0},{2,3},{3,2},{4,5},{5,4},{6,7},{7,6},{8,9},{9,8},{10,11... | collective-permute-start | bytes 786440 | tf_op jit(solution)/shard_map/ppermute | solution.py:72
  77.3 5.8 %collective-permute-start.14 = (bf16[256,256]{0,1:T(8,128)(2,1)S(1)}, bf16[256,256]{0,1:T(8,128)(2,1)S(1)}, u32[]{:S(2)}, u32[]{:S(2)}) collective-permute-start(bf16[256,256]{0,1:T(8,128)(2,1)S(1)} %fusion.147), channel_id=1, source_target_pairs={{0,2},{1,3},{2,0},{3,1},{4,6},{5,7},{6,4},{7,5},{8,10},{9,11},{10,... | collective-permute-start | bytes 393224 | tf_op jit(solution)/shard_map/ppermute | solution.py:72
  79.4 15.3 %copy-start.3 = (bf16[1024]{0:T(1024)(128)(2,1)S(1)}, bf16[1024]{0:T(1024)(128)(2,1)}, u32[]{:S(2)}) copy-start(bf16[1024]{0:T(1024)(128)(2,1)} %param.45) | copy-start | bytes 6148
  80.4 5.6 %collective-permute-start.16 = (bf16[256,256]{0,1:T(8,128)(2,1)S(1)}, bf16[256,256]{0,1:T(8,128)(2,1)S(1)}, u32[]{:S(2)}, u32[]{:S(2)}) collective-permute-start(bf16[256,256]{0,1:T(8,128)(2,1)S(1)} %fusion.148), channel_id=1, source_target_pairs={{0,2},{1,3},{2,0},{3,1},{4,6},{5,7},{6,4},{7,5},{8,10},{9,11},{10,... | collective-permute-start | bytes 393224 | tf_op jit(solution)/shard_map/ppermute | solution.py:72
  87.1 6.2 %collective-permute-start.21 = (bf16[256,256]{0,1:T(8,128)(2,1)S(1)}, bf16[256,256]{0,1:T(8,128)(2,1)S(1)}, u32[]{:S(2)}, u32[]{:S(2)}) collective-permute-start(bf16[256,256]{0,1:T(8,128)(2,1)S(1)} %get-tuple-element.241), channel_id=1, source_target_pairs={{0,2},{1,3},{2,0},{3,1},{4,6},{5,7},{6,4},{7,5},{8,10},{9,11},{10,... | collective-permute-start | bytes 393224 | tf_op jit(solution)/shard_map/ppermute | solution.py:86
  87.9 6.7 %collective-permute-start.17 = (bf16[256,256]{0,1:T(8,128)(2,1)S(1)}, bf16[256,256]{0,1:T(8,128)(2,1)S(1)}, u32[]{:S(2)}, u32[]{:S(2)}) collective-permute-start(bf16[256,256]{0,1:T(8,128)(2,1)S(1)} %get-tuple-element.240), channel_id=1, source_target_pairs={{0,2},{1,3},{2,0},{3,1},{4,6},{5,7},{6,4},{7,5},{8,10},{9,11},{10,... | collective-permute-start | bytes 393224 | tf_op jit(solution)/shard_map/ppermute | solution.py:86
  93.3 1.6 %collective-permute-start.22 = (bf16[256,2,256]{0,2,1:T(8,128)(2,1)S(1)}, bf16[256,2,256]{0,2,1:T(8,128)(2,1)S(1)}, u32[]{:S(2)}, u32[]{:S(2)}) collective-permute-start(bf16[256,2,256]{0,2,1:T(8,128)(2,1)S(1)} %pad_maximum_fusion.11), channel_id=1, source_target_pairs={{0,1},{1,0},{2,3},{3,2},{4,5},{5,4},{6,7},{7,6},{8,9},{9,8},{10,11... | collective-permute-start | bytes 786440 | tf_op jit(solution)/shard_map/ppermute | solution.py:86
  94.7 1.6 %collective-permute-start.18 = (bf16[256,2,256]{0,2,1:T(8,128)(2,1)S(1)}, bf16[256,2,256]{0,2,1:T(8,128)(2,1)S(1)}, u32[]{:S(2)}, u32[]{:S(2)}) collective-permute-start(bf16[256,2,256]{0,2,1:T(8,128)(2,1)S(1)} %pad_maximum_fusion.10), channel_id=1, source_target_pairs={{0,1},{1,0},{2,3},{3,2},{4,5},{5,4},{6,7},{7,6},{8,9},{9,8},{10,11... | collective-permute-start | bytes 786440 | tf_op jit(solution)/shard_map/ppermute | solution.py:86
  97.8 1.6 %copy-start.1 = (bf16[1024,1024]{1,0:T(8,128)(2,1)S(1)}, bf16[1024,1024]{1,0:T(8,128)(2,1)}, u32[]{:S(2)}) copy-start(bf16[1024,1024]{1,0:T(8,128)(2,1)} %param.47) | copy-start | bytes 6291460
  100.4 2.6 %collective-permute-start.23 = (bf16[256,2,256]{0,2,1:T(8,128)(2,1)S(1)}, bf16[256,2,256]{0,2,1:T(8,128)(2,1)S(1)}, u32[]{:S(2)}, u32[]{:S(2)}) collective-permute-start(bf16[256,2,256]{0,2,1:T(8,128)(2,1)S(1)} %fusion.134), channel_id=1, source_target_pairs={{0,1},{1,0},{2,3},{3,2},{4,5},{5,4},{6,7},{7,6},{8,9},{9,8},{10,11... | collective-permute-start | bytes 786440 | tf_op jit(solution)/shard_map/ppermute | solution.py:72
  102.5 1.6 %collective-permute-start.19 = (bf16[256,2,256]{0,2,1:T(8,128)(2,1)S(1)}, bf16[256,2,256]{0,2,1:T(8,128)(2,1)S(1)}, u32[]{:S(2)}, u32[]{:S(2)}) collective-permute-start(bf16[256,2,256]{0,2,1:T(8,128)(2,1)S(1)} %fusion.133), channel_id=1, source_target_pairs={{0,1},{1,0},{2,3},{3,2},{4,5},{5,4},{6,7},{7,6},{8,9},{9,8},{10,11... | collective-permute-start | bytes 786440 | tf_op jit(solution)/shard_map/ppermute | solution.py:72
  103.0 6.4 %collective-permute-start.24 = (bf16[256,256]{0,1:T(8,128)(2,1)S(1)}, bf16[256,256]{0,1:T(8,128)(2,1)S(1)}, u32[]{:S(2)}, u32[]{:S(2)}) collective-permute-start(bf16[256,256]{0,1:T(8,128)(2,1)S(1)} %fusion.150), channel_id=1, source_target_pairs={{0,2},{1,3},{2,0},{3,1},{4,6},{5,7},{6,4},{7,5},{8,10},{9,11},{10,... | collective-permute-start | bytes 393224 | tf_op jit(solution)/shard_map/ppermute | solution.py:72
  104.2 7.2 %collective-permute-start.20 = (bf16[256,256]{0,1:T(8,128)(2,1)S(1)}, bf16[256,256]{0,1:T(8,128)(2,1)S(1)}, u32[]{:S(2)}, u32[]{:S(2)}) collective-permute-start(bf16[256,256]{0,1:T(8,128)(2,1)S(1)} %fusion.149), channel_id=1, source_target_pairs={{0,2},{1,3},{2,0},{3,1},{4,6},{5,7},{6,4},{7,5},{8,10},{9,11},{10,... | collective-permute-start | bytes 393224 | tf_op jit(solution)/shard_map/ppermute | solution.py:72

commit v21 on v17

--- a/solution.py
+++ b/solution.py
@@ -176,7 +176,7 @@
         jnp.zeros((local_bricks, head_count, brick_rows), jnp.float32),
         jnp.zeros((local_bricks, brick_rows, head_count, HEAD_DIM), jnp.float32),
     )
-    chunk_count = 2 if row_count % 16 == 0 else 1
+    chunk_count = 1
     chunk_rows = row_count // chunk_count
     split_last = local_bricks == 1 and chunk_count == 2
     levels = level_count(head_total)

time: 113 us -> 120 us (1.062)
  waiting for transfers between devices: 40.8 us -> 52.6 us
  starting transfers between devices: 21.9 us -> 17 us
  matrix products: 17.8 us -> 16.5 us
  local copies, waits for them, and re-layouts: 11.2 us -> 12.5 us
    ppermute x8 -> x4, waiting for transfers between devices: 11.8 us -> 19.6 us  [scatter_heads(): lax.ppermute(give.astype(jnp.bfloat16), 'heads', [(i, i ^ bit) for i in r...]
    ppermute x8 -> x4, starting transfers between devices: 4.76 us -> 1.96 us  [scatter_heads(): lax.ppermute(give.astype(jnp.bfloat16), 'heads', [(i, i ^ bit) for i in r...]
    ppermute x4 -> x2, waiting for transfers between devices: 6.85 us -> 9.08 us  [gather_heads(): lax.ppermute(current, 'heads', [(i, i ^ bit) for i in range(head_total)])]
    ppermute x3, waiting for transfers between devices: 8.81 us -> 11 us  [shards(): ringed[slot + 1] = lax.ppermute(ringed[slot], 'bricks', ring)]
    ppermute x4 -> x2, starting transfers between devices: 2.23 us -> 0.7 us  [gather_heads(): lax.ppermute(current, 'heads', [(i, i ^ bit) for i in range(head_total)])]
    unnamed x17 -> x21, local copies, waits for them, and re-layouts: 2.19 us -> 2.9 us
    dot_general x5 -> x4, matrix products: 3.57 us -> 3.34 us  [absorb_block(): jnp.einsum('bqhd,khd->bhqk', query_heads, key_rows, preferred_element_typ...]
    dot_general x5 -> x4, matrix products: 4.05 us -> 3.95 us  [absorb_block(): jnp.einsum('bhqk,khd->bqhd', weights.astype(jnp.bfloat16), value_rows, pr...]
  transfers between devices with their start and end apart: 25 -> 19, of which waited for: 19 -> 14; matrix products, arithmetic and copies ran while one was open for 21% -> 16% of each run, Pallas kernels for 0% -> 0%
where the time goes in v21:
time: 120 us; the launch traced here: 119 us
  waiting for transfers between devices  52.6 us (44%)
  starting transfers between devices  17 us (14%)
  matrix products  16.5 us (14%)
  other arithmetic  15.8 us (13%)
  local copies, waits for them, and re-layouts  12.5 us (10%)
  between operations  4.72 us (4%)
    ppermute x4, waiting for transfers between devices, scatter_heads(): lax.ppermute(give.astype(jnp.bfloat16), 'heads', [(i, i ^ bit) for i in r...  19.6 us
    ppermute x8, waiting for transfers between devices, gather_levels(): lax.ppermute(current, 'heads', [(i, i ^ bit) for i in range(head_total)])  13 us
    ppermute x3, waiting for transfers between devices, shards(): ringed[slot + 1] = lax.ppermute(ringed[slot], 'bricks', ring)  11 us
    ppermute x2, waiting for transfers between devices, gather_heads(): lax.ppermute(current, 'heads', [(i, i ^ bit) for i in range(head_total)])  9.08 us
    ppermute x8, starting transfers between devices, gather_levels(): lax.ppermute(current, 'heads', [(i, i ^ bit) for i in range(head_total)])  5.88 us
    ppermute x1, starting transfers between devices, extended_2(): before = lax.ppermute(last, axis, up)  5.56 us
    dot_general x4, matrix products, absorb_block(): jnp.einsum('bhqk,khd->bqhd', weights.astype(jnp.bfloat16), value_rows, pr...  3.95 us
    reduce_sum x4, other arithmetic, absorb_block(): mass_new = row_mass * factor + jnp.sum(weights, axis=-1)  3.36 us
  transfers between devices with their start and end apart: 19, of which 14 were waited for; matrix products, arithmetic and copies ran while one was open for 16% of the time, Pallas kernels for 0%

profile of v21, /device:TPU:0, one launch (start us, length us, event | category | flops | bytes accessed | tf_op | source)
XLA Modules:
  0.0 119.0 jit_solution(7713471424505047349)
XLA Ops:
  0.0 0.9 fusion.146
  0.9 1.3 %collective-permute-start.1 = (bf16[64,256]{1,0:T(8,128)(2,1)S(1)}, bf16[64,256]{1,0:T(8,128)(2,1)S(1)}, u32[]{:S(2)}, u32[]{:S(2)}) collective-permute-start(bf16[64,256]{1,0:T(8,128)(2,1)S(1)} %get-tuple-element.223), channel_id=1, source_target_pairs={{4,0},{8,4},{12,8},{5,1},{9,5},{13,9},{6,2},{10,6},{14,10},{7,3},{... | collective-permute-start | bytes 98312 | tf_op jit(solution)/shard_map/ppermute | solution.py:21
  2.2 5.6 %collective-permute-start = (bf16[64,256]{1,0:T(8,128)(2,1)S(1)}, bf16[64,256]{1,0:T(8,128)(2,1)S(1)}, u32[]{:S(2)}, u32[]{:S(2)}) collective-permute-start(bf16[64,256]{1,0:T(8,128)(2,1)S(1)} %get-tuple-element.222), channel_id=1, source_target_pairs={{0,4},{4,8},{8,12},{1,5},{5,9},{9,13},{2,6},{6,10},{10,14},{3,7},{... | collective-permute-start | bytes 98312 | tf_op jit(solution)/shard_map/ppermute | solution.py:20
  7.8 1.0 fusion.147
  8.8 0.9 fusion.148
  9.7 1.1 copy.26
  10.8 1.4 %fusion.150 = (s32[1]{0:T(128)}, s32[1]{0:T(128)}) fusion(s32[4]{0:T(128)} %param.32, s32[]{:T(128)} %bitcast.2, s32[]{:T(128)} %bitcast.6), kind=kLoop, calls=%fused_computation.250 | loop fusion | bytes 24 | tf_op jit(solution)/shard_map/jit(_take)/gather | solution.py:157
  13.7 0.7 convert_element_type.172
  14.7 1.7 %fusion.88 = f32[1,8,8,8,256]{4,3,2,1,0:T(8,128)S(1)} fusion(f32[1,10,10,10,256]{4,3,2,1,0:T(8,128)S(1)} %select_maximum_fusion, f32[1,1,8,8,256]{4,3,2,1,0:T(8,128)S(1)} %multiply_bitcast_fusion, f32[1,8,8,8,256]{4,3,2,1,0:T(8,128)S(1)} %bitcast.432, f32[1,1,8,8,256]{4,3,2,1,0:T(8,128)S(1)} %multiply_bitcast_fusion.1, f32[256]{0:T(256)S(1)} %bitcast.479, ...), kind=kLoop, calls=%fused_computation.116 | loop fusion | flops 7208960 | bytes 13790208 | tf_op jit(solution)/shard_map/add | solution.py:51
  16.7 2.0 %collective-permute-start.3 = (bf16[512,256]{0,1:T(8,128)(2,1)S(1)}, bf16[512,256]{0,1:T(8,128)(2,1)S(1)}, u32[]{:S(2)}, u32[]{:S(2)}) collective-permute-start(bf16[512,256]{0,1:T(8,128)(2,1)S(1)} %add_convert_fusion), channel_id=1, source_target_pairs={{0,2},{1,3},{2,0},{3,1},{4,6},{5,7},{6,4},{7,5},{8,10},{9,11},{10,... | collective-permute-start | bytes 786440 | tf_op jit(solution)/shard_map/ppermute | solution.py:97
  18.7 1.6 %collective-permute-start.2 = (bf16[512,256]{0,1:T(8,128)(2,1)S(1)}, bf16[512,256]{0,1:T(8,128)(2,1)}, u32[]{:S(2)}, u32[]{:S(2)}) collective-permute-start(bf16[512,256]{0,1:T(8,128)(2,1)S(1)} %add_convert_fusion), channel_id=1, source_target_pairs={{0,4},{4,8},{8,12},{12,0},{1,5},{5,9},{9,13},{13,1},{2,6},{6,10},{... | collective-permute-start | bytes 786440 | tf_op jit(solution)/shard_map/ppermute | solution.py:192
  20.3 4.3 %collective-permute-done.3 = bf16[512,256]{0,1:T(8,128)(2,1)S(1)} collective-permute-done((bf16[512,256]{0,1:T(8,128)(2,1)S(1)}, bf16[512,256]{0,1:T(8,128)(2,1)S(1)}, u32[]{:S(2)}, u32[]{:S(2)}) %collective-permute-start.3) | collective-permute-done | bytes 262176 | tf_op jit(solution)/shard_map/ppermute | solution.py:97
  24.6 3.2 %collective-permute-done.2 = bf16[512,256]{0,1:T(8,128)(2,1)} collective-permute-done((bf16[512,256]{0,1:T(8,128)(2,1)S(1)}, bf16[512,256]{0,1:T(8,128)(2,1)}, u32[]{:S(2)}, u32[]{:S(2)}) %collective-permute-start.2) | collective-permute-done | bytes 262176 | tf_op jit(solution)/shard_map/ppermute | solution.py:192
  28.2 0.7 fusion.149
  31.5 2.1 %copy.50 = bf16[1024,256]{1,0:T(8,128)(2,1)} copy(bf16[1024,256]{0,1:T(8,128)(2,1)} %bitcast.441) | data formatting | bytes 1048576 | tf_op jit(solution)/shard_map/dot_general | solution.py:249
  33.6 0.8 collective-permute-done.5
  34.4 1.0 select_bitcast_fusion.17
  35.4 1.1 select_bitcast_fusion.9
  36.8 7.6 %collective-permute-done.4 = bf16[512,256]{0,1:T(8,128)(2,1)S(1)} collective-permute-done((bf16[512,256]{0,1:T(8,128)(2,1)}, bf16[512,256]{0,1:T(8,128)(2,1)S(1)}, u32[]{:S(2)}, u32[]{:S(2)}) %collective-permute-start.4) | collective-permute-done | bytes 262176 | tf_op jit(solution)/shard_map/ppermute | solution.py:192
  44.3 1.6 %collective-permute-start.8 = (bf16[512,256]{0,1:T(8,128)(2,1)S(1)}, bf16[512,256]{0,1:T(8,128)(2,1)S(1)}, u32[]{:S(2)}, u32[]{:S(2)}) collective-permute-start(bf16[512,256]{0,1:T(8,128)(2,1)S(1)} %collective-permute-done.4), channel_id=1, source_target_pairs={{0,2},{1,3},{2,0},{3,1},{4,6},{5,7},{6,4},{7,5},{8,10},{9,11},{10,... | collective-permute-start | bytes 786440 | tf_op jit(solution)/shard_map/ppermute | solution.py:97
  46.5 0.6 convolution_convert_fusion.8
  47.2 0.6 convolution_convert_fusion.7
  47.9 0.4 copy-done.8
  48.3 0.6 convolution_convert_fusion.6
  48.9 0.8 bitcast_reduce_fusion.3
  49.7 0.8 fusion.5
  50.6 1.0 fusion.71
  51.8 0.4 collective-permute-done.8
  52.3 1.2 collective-permute-done.9
  54.6 0.6 convolution_convert_fusion.5
  55.3 0.6 convolution_convert_fusion.4
  55.9 0.8 bitcast_reduce_fusion.2
  56.7 0.8 fusion.7
  57.6 1.0 fusion.68
  58.5 1.7 %collective-permute-start.10 = (bf16[512,256]{0,1:T(8,128)(2,1)S(1)}, bf16[512,256]{0,1:T(8,128)(2,1)S(1)}, u32[]{:S(2)}, u32[]{:S(2)}) collective-permute-start(bf16[512,256]{0,1:T(8,128)(2,1)S(1)} %collective-permute-done.7), channel_id=1, source_target_pairs={{0,2},{1,3},{2,0},{3,1},{4,6},{5,7},{6,4},{7,5},{8,10},{9,11},{10,... | collective-permute-start | bytes 786440 | tf_op jit(solution)/shard_map/ppermute | solution.py:97
  60.4 6.3 %collective-permute-done.10 = bf16[512,256]{0,1:T(8,128)(2,1)S(1)} collective-permute-done((bf16[512,256]{0,1:T(8,128)(2,1)S(1)}, bf16[512,256]{0,1:T(8,128)(2,1)S(1)}, u32[]{:S(2)}, u32[]{:S(2)}) %collective-permute-start.10) | collective-permute-done | bytes 262176 | tf_op jit(solution)/shard_map/ppermute | solution.py:97
  67.7 0.7 convolution_convert_fusion.3
  68.3 0.6 convolution_convert_fusion.2
  69.0 1.0 bitcast_reduce_fusion.1
  70.1 0.8 fusion.9
  70.9 1.0 fusion.74
  72.8 0.6 convolution_convert_fusion
  73.4 0.6 convolution_convert_fusion.1
  74.1 0.8 bitcast_reduce_fusion
  74.9 0.8 fusion.10
  75.8 1.0 fusion.83
  76.8 0.4 fusion.151
  77.2 1.3 %copy-done.1 = f32[512,2,2,256]{0,3,2,1:T(8,128)} copy-done((f32[512,2,2,256]{0,3,2,1:T(8,128)}, f32[512,2,2,256]{0,3,2,1:T(8,128)S(1)}, u32[]{:S(2)}) %copy-start.1) | copy-done | bytes 2097176
  78.6 0.6 collective-permute-start.13
  79.2 1.7 %collective-permute-done.13 = bf16[512,2,256]{0,2,1:T(8,128)(2,1)} collective-permute-done((bf16[512,2,256]{0,2,1:T(8,128)(2,1)S(1)}, bf16[512,2,256]{0,2,1:T(8,128)(2,1)}, u32[]{:S(2)}, u32[]{:S(2)}) %collective-permute-start.13) | collective-permute-done | bytes 524320 | tf_op jit(solution)/shard_map/ppermute | solution.py:72
  80.9 1.6 %bitcast_add_fusion.1 = f32[512,2,256]{0,2,1:T(8,128)S(1)} fusion(bf16[512,2,256]{0,2,1:T(8,128)(2,1)} %collective-permute-done.13, f32[512,2,2,256]{0,3,2,1:T(8,128)} %copy-done.1, s32[]{:T(128)S(6)} %select_n.259), kind=kLoop, calls=%fused_computation.109 | loop fusion | flops 524288 | bytes 2621444 | tf_op jit(solution)/shard_map/add | solution.py:75
  82.5 0.7 fusion.121
  83.2 0.6 collective-permute-start.14
  83.8 8.3 %collective-permute-done.14 = bf16[512,256]{0,1:T(8,128)(2,1)} collective-permute-done((bf16[512,256]{0,1:T(8,128)(2,1)}, bf16[512,256]{0,1:T(8,128)(2,1)}, u32[]{:S(2)}, u32[]{:S(2)}) %collective-permute-start.14) | collective-permute-done | bytes 262176 | tf_op jit(solution)/shard_map/ppermute | solution.py:72
  92.1 1.1 fusion.119
  93.2 0.6 collective-permute-start.15
  93.8 7.2 %collective-permute-done.15 = bf16[512,256]{0,1:T(8,128)(2,1)S(1)} collective-permute-done((bf16[512,256]{0,1:T(8,128)(2,1)S(1)}, bf16[512,256]{0,1:T(8,128)(2,1)S(1)}, u32[]{:S(2)}, u32[]{:S(2)}) %collective-permute-start.15) | collective-permute-done | bytes 262176 | tf_op jit(solution)/shard_map/ppermute | solution.py:86
  101.2 1.9 %collective-permute-done.16 = bf16[512,2,256]{0,2,1:T(8,128)(2,1)S(1)} collective-permute-done((bf16[512,2,256]{0,2,1:T(8,128)(2,1)S(1)}, bf16[512,2,256]{0,2,1:T(8,128)(2,1)S(1)}, u32[]{:S(2)}, u32[]{:S(2)}) %collective-permute-start.16) | collective-permute-done | bytes 524320 | tf_op jit(solution)/shard_map/ppermute | solution.py:86
  104.4 1.7 %fusion.39 = bf16[512,1024]{1,0:T(8,128)(2,1)S(1)} fusion(bf16[512,1024]{0,1:T(8,128)(2,1)S(1)} %fusion.46, bf16[1024,1024]{1,0:T(8,128)(2,1)S(1)} %copy-done), kind=kOutput, calls=%fused_computation.64 | convolution fusion | flops 1078460416 | bytes 4194304 | tf_op jit(solution)/shard_map/dot_general | solution.py:255
  106.1 1.3 %fusion.152 = f32[512,1024]{0,1:T(8,128)S(1)} fusion(bf16[512,1024]{1,0:T(8,128)(2,1)S(1)} %fusion.39, bf16[1024,1024]{1,0:T(8,128)(2,1)S(1)} %copy-done.6), kind=kOutput, calls=%fused_computation.252 | convolution fusion | flops 1073741824 | bytes 5242880 | tf_op jit(solution)/shard_map/dot_general | solution.py:258
  107.6 1.8 %collective-permute-done.17 = bf16[512,2,256]{0,2,1:T(8,128)(2,1)S(1)} collective-permute-done((bf16[512,2,256]{0,2,1:T(8,128)(2,1)S(1)}, bf16[512,2,256]{0,2,1:T(8,128)(2,1)S(1)}, u32[]{:S(2)}, u32[]{:S(2)}) %collective-permute-start.17) | collective-permute-done | bytes 524320 | tf_op jit(solution)/shard_map/ppermute | solution.py:72
  109.7 0.6 collective-permute-start.18
  110.3 7.8 %collective-permute-done.18 = bf16[512,256]{0,1:T(8,128)(2,1)S(1)} collective-permute-done((bf16[512,256]{0,1:T(8,128)(2,1)S(1)}, bf16[512,256]{0,1:T(8,128)(2,1)S(1)}, u32[]{:S(2)}, u32[]{:S(2)}) %collective-permute-start.18) | collective-permute-done | bytes 262176 | tf_op jit(solution)/shard_map/ppermute | solution.py:72
  118.2 0.8 copy.42
  (103 shorter events, 7.5 us)
Async XLA Ops:
  0.0 104.3 %copy-start = (bf16[1024,1024]{1,0:T(8,128)(2,1)S(1)}, bf16[1024,1024]{1,0:T(8,128)(2,1)}, u32[]{:S(2)}) copy-start(bf16[1024,1024]{1,0:T(8,128)(2,1)} %param.42) | copy-start | bytes 6291460
  0.9 13.4 %collective-permute-start.1 = (bf16[64,256]{1,0:T(8,128)(2,1)S(1)}, bf16[64,256]{1,0:T(8,128)(2,1)S(1)}, u32[]{:S(2)}, u32[]{:S(2)}) collective-permute-start(bf16[64,256]{1,0:T(8,128)(2,1)S(1)} %get-tuple-element.223), channel_id=1, source_target_pairs={{4,0},{8,4},{12,8},{5,1},{9,5},{13,9},{6,2},{10,6},{14,10},{7,3},{... | collective-permute-start | bytes 98312 | tf_op jit(solution)/shard_map/ppermute | solution.py:21
  2.2 12.2 %collective-permute-start = (bf16[64,256]{1,0:T(8,128)(2,1)S(1)}, bf16[64,256]{1,0:T(8,128)(2,1)S(1)}, u32[]{:S(2)}, u32[]{:S(2)}) collective-permute-start(bf16[64,256]{1,0:T(8,128)(2,1)S(1)} %get-tuple-element.222), channel_id=1, source_target_pairs={{0,4},{4,8},{8,12},{1,5},{5,9},{9,13},{2,6},{6,10},{10,14},{3,7},{... | collective-permute-start | bytes 98312 | tf_op jit(solution)/shard_map/ppermute | solution.py:20
  16.3 11.9 %copy-start.3 = (bf16[1024]{0:T(1024)(128)(2,1)S(1)}, bf16[1024]{0:T(1024)(128)(2,1)}, u32[]{:S(2)}) copy-start(bf16[1024]{0:T(1024)(128)(2,1)} %param.36) | copy-start | bytes 6148
  16.3 11.9 %copy-start.5 = (s32[4,4]{1,0:T(4,128)S(1)}, s32[4,4]{1,0:T(4,128)}, u32[]{:S(2)}) copy-start(s32[4,4]{1,0:T(4,128)} %param.33) | copy-start | bytes 196
  16.7 7.8 %collective-permute-start.3 = (bf16[512,256]{0,1:T(8,128)(2,1)S(1)}, bf16[512,256]{0,1:T(8,128)(2,1)S(1)}, u32[]{:S(2)}, u32[]{:S(2)}) collective-permute-start(bf16[512,256]{0,1:T(8,128)(2,1)S(1)} %add_convert_fusion), channel_id=1, source_target_pairs={{0,2},{1,3},{2,0},{3,1},{4,6},{5,7},{6,4},{7,5},{8,10},{9,11},{10,... | collective-permute-start | bytes 786440 | tf_op jit(solution)/shard_map/ppermute | solution.py:97
  18.7 9.1 %collective-permute-start.2 = (bf16[512,256]{0,1:T(8,128)(2,1)S(1)}, bf16[512,256]{0,1:T(8,128)(2,1)}, u32[]{:S(2)}, u32[]{:S(2)}) collective-permute-start(bf16[512,256]{0,1:T(8,128)(2,1)S(1)} %add_convert_fusion), channel_id=1, source_target_pairs={{0,4},{4,8},{8,12},{12,0},{1,5},{5,9},{9,13},{13,1},{2,6},{6,10},{... | collective-permute-start | bytes 786440 | tf_op jit(solution)/shard_map/ppermute | solution.py:192
  27.8 6.6 %collective-permute-start.5 = (bf16[512,256]{0,1:T(8,128)(2,1)}, bf16[512,256]{0,1:T(8,128)(2,1)S(1)}, u32[]{:S(2)}, u32[]{:S(2)}) collective-permute-start(bf16[512,256]{0,1:T(8,128)(2,1)} %collective-permute-done.2), channel_id=1, source_target_pairs={{0,2},{1,3},{2,0},{3,1},{4,6},{5,7},{6,4},{7,5},{8,10},{9,11},{10,... | collective-permute-start | bytes 786440 | tf_op jit(solution)/shard_map/ppermute | solution.py:97
  28.2 7.3 %collective-permute-start.6 = (bf16[512,2,256]{0,2,1:T(8,128)(2,1)S(1)}, bf16[512,2,256]{0,2,1:T(8,128)(2,1)}, u32[]{:S(2)}, u32[]{:S(2)}) collective-permute-start(bf16[512,2,256]{0,2,1:T(8,128)(2,1)S(1)} %pad_maximum_fusion.6), channel_id=1, source_target_pairs={{0,1},{1,0},{2,3},{3,2},{4,5},{5,4},{6,7},{7,6},{8,9},{9,8},{10,11... | collective-permute-start | bytes 1572872 | tf_op jit(solution)/shard_map/ppermute | solution.py:97
  33.6 10.7 %collective-permute-start.4 = (bf16[512,256]{0,1:T(8,128)(2,1)}, bf16[512,256]{0,1:T(8,128)(2,1)S(1)}, u32[]{:S(2)}, u32[]{:S(2)}) collective-permute-start(bf16[512,256]{0,1:T(8,128)(2,1)} %collective-permute-done.2), channel_id=1, source_target_pairs={{0,4},{4,8},{8,12},{12,0},{1,5},{5,9},{9,13},{13,1},{2,6},{6,10},{... | collective-permute-start | bytes 786440 | tf_op jit(solution)/shard_map/ppermute | solution.py:192
  36.7 9.9 %copy-start.9 = (bf16[1024,256]{1,0:T(8,128)(2,1)S(1)}, bf16[1024,256]{1,0:T(8,128)(2,1)}, u32[]{:S(2)}) copy-start(bf16[1024,256]{1,0:T(8,128)(2,1)} %param.38) | copy-start | bytes 1572868
  44.3 9.7 %collective-permute-start.7 = (bf16[512,256]{0,1:T(8,128)(2,1)S(1)}, bf16[512,256]{0,1:T(8,128)(2,1)S(1)}, u32[]{:S(2)}, u32[]{:S(2)}) collective-permute-start(bf16[512,256]{0,1:T(8,128)(2,1)S(1)} %collective-permute-done.4), channel_id=1, source_target_pairs={{0,4},{4,8},{8,12},{12,0},{1,5},{5,9},{9,13},{13,1},{2,6},{6,10},{... | collective-permute-start | bytes 786440 | tf_op jit(solution)/shard_map/ppermute | solution.py:192
  44.3 7.9 %collective-permute-start.8 = (bf16[512,256]{0,1:T(8,128)(2,1)S(1)}, bf16[512,256]{0,1:T(8,128)(2,1)S(1)}, u32[]{:S(2)}, u32[]{:S(2)}) collective-permute-start(bf16[512,256]{0,1:T(8,128)(2,1)S(1)} %collective-permute-done.4), channel_id=1, source_target_pairs={{0,2},{1,3},{2,0},{3,1},{4,6},{5,7},{6,4},{7,5},{8,10},{9,11},{10,... | collective-permute-start | bytes 786440 | tf_op jit(solution)/shard_map/ppermute | solution.py:97
  46.2 1.0 copy-start.7
  47.2 1.0 copy-start.8
  51.5 2.0 %collective-permute-start.9 = (bf16[512,2,256]{0,2,1:T(8,128)(2,1)S(1)}, bf16[512,2,256]{0,2,1:T(8,128)(2,1)S(1)}, u32[]{:S(2)}, u32[]{:S(2)}) collective-permute-start(bf16[512,2,256]{0,2,1:T(8,128)(2,1)S(1)} %pad_maximum_fusion.7), channel_id=1, source_target_pairs={{0,1},{1,0},{2,3},{3,2},{4,5},{5,4},{6,7},{7,6},{8,9},{9,8},{10,11... | collective-permute-start | bytes 1572872 | tf_op jit(solution)/shard_map/ppermute | solution.py:97
  58.5 8.2 %collective-permute-start.10 = (bf16[512,256]{0,1:T(8,128)(2,1)S(1)}, bf16[512,256]{0,1:T(8,128)(2,1)S(1)}, u32[]{:S(2)}, u32[]{:S(2)}) collective-permute-start(bf16[512,256]{0,1:T(8,128)(2,1)S(1)} %collective-permute-done.7), channel_id=1, source_target_pairs={{0,2},{1,3},{2,0},{3,1},{4,6},{5,7},{6,4},{7,5},{8,10},{9,11},{10,... | collective-permute-start | bytes 786440 | tf_op jit(solution)/shard_map/ppermute | solution.py:97
  60.2 6.6 %collective-permute-start.11 = (bf16[512,2,256]{0,2,1:T(8,128)(2,1)S(1)}, bf16[512,2,256]{0,2,1:T(8,128)(2,1)S(1)}, u32[]{:S(2)}, u32[]{:S(2)}) collective-permute-start(bf16[512,2,256]{0,2,1:T(8,128)(2,1)S(1)} %pad_maximum_fusion.8), channel_id=1, source_target_pairs={{0,1},{1,0},{2,3},{3,2},{4,5},{5,4},{6,7},{7,6},{8,9},{9,8},{10,11... | collective-permute-start | bytes 1572872 | tf_op jit(solution)/shard_map/ppermute | solution.py:97
  69.0 3.0 %collective-permute-start.12 = (bf16[512,2,256]{0,2,1:T(8,128)(2,1)S(1)}, bf16[512,2,256]{0,2,1:T(8,128)(2,1)S(1)}, u32[]{:S(2)}, u32[]{:S(2)}) collective-permute-start(bf16[512,2,256]{0,2,1:T(8,128)(2,1)S(1)} %pad_maximum_fusion.9), channel_id=1, source_target_pairs={{0,1},{1,0},{2,3},{3,2},{4,5},{5,4},{6,7},{7,6},{8,9},{9,8},{10,11... | collective-permute-start | bytes 1572872 | tf_op jit(solution)/shard_map/ppermute | solution.py:97
  75.7 1.0 copy-start.2
  77.2 1.4 %copy-start.1 = (f32[512,2,2,256]{0,3,2,1:T(8,128)}, f32[512,2,2,256]{0,3,2,1:T(8,128)S(1)}, u32[]{:S(2)}) copy-start(f32[512,2,2,256]{0,3,2,1:T(8,128)S(1)} %fusion.151) | copy-start | bytes 6291460
  78.6 2.2 %collective-permute-start.13 = (bf16[512,2,256]{0,2,1:T(8,128)(2,1)S(1)}, bf16[512,2,256]{0,2,1:T(8,128)(2,1)}, u32[]{:S(2)}, u32[]{:S(2)}) collective-permute-start(bf16[512,2,256]{0,2,1:T(8,128)(2,1)S(1)} %fusion.86), channel_id=1, source_target_pairs={{0,1},{1,0},{2,3},{3,2},{4,5},{5,4},{6,7},{7,6},{8,9},{9,8},{10,11... | collective-permute-start | bytes 1572872 | tf_op jit(solution)/shard_map/ppermute | solution.py:72
  82.4 18.7 %copy-start.4 = (bf16[1024]{0:T(1024)(128)(2,1)S(1)}, bf16[1024]{0:T(1024)(128)(2,1)}, u32[]{:S(2)}) copy-start(bf16[1024]{0:T(1024)(128)(2,1)} %param.41) | copy-start | bytes 6148
  83.2 8.9 %collective-permute-start.14 = (bf16[512,256]{0,1:T(8,128)(2,1)}, bf16[512,256]{0,1:T(8,128)(2,1)}, u32[]{:S(2)}, u32[]{:S(2)}) collective-permute-start(bf16[512,256]{0,1:T(8,128)(2,1)} %fusion.121), channel_id=1, source_target_pairs={{0,2},{1,3},{2,0},{3,1},{4,6},{5,7},{6,4},{7,5},{8,10},{9,11},{10,... | collective-permute-start | bytes 786440 | tf_op jit(solution)/shard_map/ppermute | solution.py:72
  93.2 7.8 %collective-permute-start.15 = (bf16[512,256]{0,1:T(8,128)(2,1)S(1)}, bf16[512,256]{0,1:T(8,128)(2,1)S(1)}, u32[]{:S(2)}, u32[]{:S(2)}) collective-permute-start(bf16[512,256]{0,1:T(8,128)(2,1)S(1)} %fusion.119), channel_id=1, source_target_pairs={{0,2},{1,3},{2,0},{3,1},{4,6},{5,7},{6,4},{7,5},{8,10},{9,11},{10,... | collective-permute-start | bytes 786440 | tf_op jit(solution)/shard_map/ppermute | solution.py:86
  101.1 2.0 %collective-permute-start.16 = (bf16[512,2,256]{0,2,1:T(8,128)(2,1)S(1)}, bf16[512,2,256]{0,2,1:T(8,128)(2,1)S(1)}, u32[]{:S(2)}, u32[]{:S(2)}) collective-permute-start(bf16[512,2,256]{0,2,1:T(8,128)(2,1)S(1)} %pad_maximum_fusion.10), channel_id=1, source_target_pairs={{0,1},{1,0},{2,3},{3,2},{4,5},{5,4},{6,7},{7,6},{8,9},{9,8},{10,11... | collective-permute-start | bytes 1572872 | tf_op jit(solution)/shard_map/ppermute | solution.py:86
  104.3 1.7 %copy-start.6 = (bf16[1024,1024]{1,0:T(8,128)(2,1)S(1)}, bf16[1024,1024]{1,0:T(8,128)(2,1)}, u32[]{:S(2)}) copy-start(bf16[1024,1024]{1,0:T(8,128)(2,1)} %param.43) | copy-start | bytes 6291460
  107.4 2.0 %collective-permute-start.17 = (bf16[512,2,256]{0,2,1:T(8,128)(2,1)S(1)}, bf16[512,2,256]{0,2,1:T(8,128)(2,1)S(1)}, u32[]{:S(2)}, u32[]{:S(2)}) collective-permute-start(bf16[512,2,256]{0,2,1:T(8,128)(2,1)S(1)} %fusion.87), channel_id=1, source_target_pairs={{0,1},{1,0},{2,3},{3,2},{4,5},{5,4},{6,7},{7,6},{8,9},{9,8},{10,11... | collective-permute-start | bytes 1572872 | tf_op jit(solution)/shard_map/ppermute | solution.py:72
  109.7 8.4 %collective-permute-start.18 = (bf16[512,256]{0,1:T(8,128)(2,1)S(1)}, bf16[512,256]{0,1:T(8,128)(2,1)S(1)}, u32[]{:S(2)}, u32[]{:S(2)}) collective-permute-start(bf16[512,256]{0,1:T(8,128)(2,1)S(1)} %fusion.122), channel_id=1, source_target_pairs={{0,2},{1,3},{2,0},{3,1},{4,6},{5,7},{6,4},{7,5},{8,10},{9,11},{10,... | collective-permute-start | bytes 786440 | tf_op jit(solution)/shard_map/ppermute | solution.py:72
